TPU v7x, 32 devices: a whole 2x2x4 slice. The times are simulated.
32 devices in a mesh: dom: 8 (over z, y), rep: 4 (over x, core).
Axes of the slice: x: 2, y: 2, z: 4, core: 2. Of those that a mesh axis runs over, the one named last changes fastest.
Arguments:
- rhs: float32 [256, 32, 128], P(('dom', 'rep')), may hold values from -15 to 15
- precond: float32 [256, 128], P(('dom', 'rep')), may hold values from 0.25 to 1
- diag_tiles: bfloat16 [256, 128, 128], P(('dom', 'rep')), may hold values from -0.08 to 6.08
- off_tiles: bfloat16 [256, 2, 128, 128], P(('dom', 'rep')), may hold values from -0.119628906 to 0.119628906
- off_cols: int32 [256, 2], P(('dom', 'rep')), may hold values from 0 to 7
- link_tiles: bfloat16 [32, 128, 128], P(('dom', 'rep')), may hold values from -0.19921875 to 0.19921875
- contact_tiles: bfloat16 [512, 128, 128], P(('dom', 'rep')), may hold values from -0.29882812 to 0.29882812
- contact_owner: int32 [512, 1], P(('dom', 'rep')), may hold values from 0 to 3; in each aligned block of 16 rows (0 to 15, 16 to 31, ...) at most 8 rows name the same one
- contact_anode: int32 [512], P(('dom', 'rep')), may hold values from 0 to 7
- contact_bnode: int32 [512], P(('dom', 'rep')), may hold values from 0 to 7
Outputs:
- solution: float32 [256, 32, 128], P(('dom', 'rep'))
- residual: float32 [256, 32, 128], P(('dom', 'rep'))
Inputs may be any that keep to these rules, and one draw needn't show every extreme that they name: `contact_owner`: among the rows of one device no rep index is named by more than 8 rows.
All inputs are finite; a program needn't handle non-finite values.
Results may differ from a plain program's by a relative error of at most 0.03.
Values may be sent and summed in bfloat16 or wider, within the bound.
No kernel may reach another device: no remote copies, remote signals or barrier semaphores. Data moves between devices by JAX's collectives and lax.ppermute only.
A program may use at most 64 MiB of HBM per device.

v0:
```python
import jax
import jax.numpy as jnp
from jax import lax
from jax.sharding import PartitionSpec as P

B = 128
ITERS = 4
CAP = 8


def from_behind(value, axis, steps):
    count = lax.axis_size(axis)
    pairs = [(source, (source + steps) % count) for source in range(count)]
    return lax.ppermute(value, axis, pairs)


def partner(value, axis, distance):
    return lax.ppermute(value, axis, [(i, i ^ 1 << distance) for i in range(lax.axis_size(axis))])


def local_stiffness(rounded, diag_tiles, off_tiles, off_cols):
    nodes = rounded.shape[0]
    result = jnp.einsum("nrk,nkj->nrj", rounded, diag_tiles, preferred_element_type=jnp.float32)
    picked = rounded[off_cols]
    result = result + jnp.einsum(
        "nmrk,nmkj->nrj", picked, off_tiles, preferred_element_type=jnp.float32
    )
    mirror = jnp.einsum("nrk,nmjk->nmrj", rounded, off_tiles, preferred_element_type=jnp.float32)
    flat_cols = off_cols.reshape(-1)
    onehot = (flat_cols[:, None] == jnp.arange(nodes, dtype=jnp.int32)[None, :]).astype(jnp.float32)
    mirror = mirror.reshape(flat_cols.shape[0], rounded.shape[1], rounded.shape[2])
    return result + jnp.einsum("pn,prj->nrj", onehot, mirror, precision=lax.Precision.HIGHEST)


def contact_pairs(vector, other, near_index, far_index, contact_set):
    difference = (vector[near_index] - other[far_index]).astype(jnp.bfloat16)
    multiplier = jnp.einsum(
        "srk,skj->srj", difference, contact_set, preferred_element_type=jnp.float32
    ).astype(jnp.bfloat16)
    return jnp.einsum("srj,skj->srk", multiplier, contact_set, preferred_element_type=jnp.float32)


def collect(values, index, nodes):
    onehot = (index[:, None] == jnp.arange(nodes, dtype=jnp.int32)[None, :]).astype(jnp.float32)
    return jnp.einsum("sn,srk->nrk", onehot, values, precision=lax.Precision.HIGHEST)


def apply_operator(
    vector, diag_tiles, off_tiles, off_cols, link_tile, contact_set, near_index, far_index
):
    nodes = vector.shape[0]
    rounded = vector.astype(jnp.bfloat16)
    result = local_stiffness(rounded, diag_tiles, off_tiles, off_cols)
    before = from_behind(rounded[nodes - 1], "rep", 1)
    first_add = jnp.dot(before, link_tile, preferred_element_type=jnp.float32)
    back_term = lax.dot_general(
        rounded[0], link_tile, (((1,), (1,)), ((), ())), preferred_element_type=jnp.float32
    )
    after = from_behind(back_term, "rep", -1)
    result = result.at[0].add(first_add)
    result = result.at[nodes - 1].add(after)
    other = partner(vector.astype(jnp.bfloat16), "dom", 0).astype(vector.dtype)
    terms = contact_pairs(vector, other, near_index, far_index, contact_set)
    result = result + collect(terms, near_index, nodes)
    far_terms = partner(collect(terms, far_index, nodes).astype(jnp.bfloat16), "dom", 0).astype(
        jnp.float32
    )
    result = result - far_terms
    return result


def body(
    rhs,
    precond,
    diag_tiles,
    off_tiles,
    off_cols,
    link_tiles,
    contact_tiles,
    contact_owner,
    contact_anode,
    contact_bnode,
):
    groups = lax.axis_size("rep")
    target = contact_owner[:, 0]
    choose = (target[:, None] == jnp.arange(groups, dtype=jnp.int32)[None, :]).astype(jnp.int32)
    rank = jnp.sum((jnp.cumsum(choose, axis=0) - choose) * choose, axis=1)
    send_set = jnp.zeros((groups, CAP, B, B), jnp.bfloat16).at[target, rank].set(contact_tiles)
    labels = jnp.stack([contact_anode, contact_bnode], axis=1)
    send_labels = jnp.zeros((groups, CAP, 2), jnp.int32).at[target, rank].set(labels)
    got_set, got_labels = (
        lax.all_to_all(send_set, "rep", split_axis=0, concat_axis=0, tiled=True),
        lax.all_to_all(send_labels, "rep", split_axis=0, concat_axis=0, tiled=True),
    )
    slots = groups * CAP
    contact_set = got_set.reshape(slots, B, B)
    got_labels = got_labels.reshape(slots, 2)
    near_index = got_labels[:, 0]
    far_index = got_labels[:, 1]
    link_tile = link_tiles[0]
    scale = precond[:, None, :]
    solution = jnp.zeros_like(rhs)
    residual = rhs
    preconditioned = scale * residual
    direction = preconditioned
    res_dot = lax.psum(jnp.sum(residual * preconditioned, axis=(0, 2)), ("dom", "rep"))
    for step in range(ITERS):
        image = apply_operator(
            direction,
            diag_tiles,
            off_tiles,
            off_cols,
            link_tile,
            contact_set,
            near_index,
            far_index,
        )
        curve = lax.psum(jnp.sum(direction * image, axis=(0, 2)), ("dom", "rep"))
        alpha = res_dot / curve
        solution = solution + alpha[None, :, None] * direction
        residual = residual - alpha[None, :, None] * image
        preconditioned = scale * residual
        next_dot = lax.psum(jnp.sum(residual * preconditioned, axis=(0, 2)), ("dom", "rep"))
        direction = preconditioned + (next_dot / res_dot)[None, :, None] * direction
        res_dot = next_dot
    return (solution, residual)


def solution(mesh):
    in_specs = (
        P(("dom", "rep"), None, None),
        P(("dom", "rep"), None),
        P(("dom", "rep"), None, None),
        P(("dom", "rep"), None, None, None),
        P(("dom", "rep"), None),
        P(("dom", "rep"), None, None),
        P(("dom", "rep"), None, None),
        P(("dom", "rep"), None),
        P(("dom", "rep")),
        P(("dom", "rep")),
    )
    out_specs = (P(("dom", "rep"), None, None), P(("dom", "rep"), None, None))
    return jax.shard_map(body, mesh=mesh, in_specs=in_specs, out_specs=out_specs, check_vma=False)
```

profile of v0, /device:TPU:0, one launch (start us, length us, event | category | flops | bytes accessed | tf_op | source)
XLA Modules:
  0.0 372.2 jit_solution(10462506235294913822)
XLA Ops:
  4.4 4.2 %all-to-all-start = ((s32[4,8,2]{1,2,0:T(2,128)}), s32[4,8,2]{1,2,0:T(2,128)S(1)}, u32[]{:S(2)}, u32[]{:S(2)}) async-start(s32[4,8,2]{1,2,0:T(2,128)} %copy.71), calls=%async_computation | async-start | bytes 8192 | tf_op jit(solution)/shard_map/all_to_all | solution.py:93
  8.7 2.1 collective-permute-start.2
  15.9 2.8 scatter_fusion.1
  18.7 3.5 all-to-all-start.1
  24.5 12.1 %all-to-all-done.1 = bf16[4,8,128,128]{3,2,1,0:T(8,128)(2,1)S(1)} async-done(((bf16[4,8,128,128]{3,2,1,0:T(8,128)(2,1)}), bf16[4,8,128,128]{3,2,1,0:T(8,128)(2,1)S(1)}, u32[]{:S(2)}, u32[]{:S(2)}) %all-to-all-start.1) | async-done | bytes 1048608 | tf_op jit(solution)/shard_map/all_to_all | solution.py:92
  36.6 2.0 fusion
  40.5 3.1 collective-permute-done.3
  43.7 39.5 %all-reduce = (f32[32]{0:T(128)S(1)}, f32[32]{0:T(128)S(1)}) all-reduce(f32[32]{0:T(128)S(1)} %get-tuple-element.99, f32[32]{0:T(128)S(1)} %get-tuple-element.98), channel_id=1, replica_groups=mesh['dom'=8,'rep'=4] {'dom','rep'}, use_global_device_ids=true, to_apply=%region_1.2 | all-reduce | flops 64 | bytes 512 | tf_op jit(solution)/shard_map/psum | solution.py:106
  83.4 40.3 %psum.58 = f32[32]{0:T(128)S(1)} all-reduce(f32[32]{0:T(128)S(1)} %get-tuple-element.112), channel_id=1, replica_groups=mesh['dom'=8,'rep'=4] {'dom','rep'}, use_global_device_ids=true, to_apply=%region_9.10 | all-reduce | flops 32 | bytes 256 | tf_op jit(solution)/shard_map/psum | solution.py:123
  123.9 2.3 collective-permute-start.6
  129.1 1.7 collective-permute-start.5
  133.7 2.0 fusion.1
  136.9 3.9 %collective-permute-done.7 = bf16[8,32,128]{2,1,0:T(8,128)(2,1)S(1)} collective-permute-done((bf16[8,32,128]{2,1,0:T(8,128)(2,1)S(1)}, bf16[8,32,128]{2,1,0:T(8,128)(2,1)S(1)}, u32[]{:S(2)}, u32[]{:S(2)}) %collective-permute-start.7) | collective-permute-done | bytes 65568 | tf_op jit(solution)/shard_map/ppermute | solution.py:18
  141.0 38.3 %psum.59 = f32[32]{0:T(128)S(1)} all-reduce(f32[32]{0:T(128)S(1)} %multiply_reduce_fusion.2), channel_id=1, replica_groups=mesh['dom'=8,'rep'=4] {'dom','rep'}, use_global_device_ids=true, to_apply=%region_11.12 | all-reduce | flops 32 | bytes 256 | tf_op jit(solution)/shard_map/psum | solution.py:118
  179.5 41.0 %psum.60 = f32[32]{0:T(128)S(1)} all-reduce(f32[32]{0:T(128)S(1)} %get-tuple-element.108), channel_id=1, replica_groups=mesh['dom'=8,'rep'=4] {'dom','rep'}, use_global_device_ids=true, to_apply=%region_13.14 | all-reduce | flops 32 | bytes 256 | tf_op jit(solution)/shard_map/psum | solution.py:123
  220.7 2.3 collective-permute-start.10
  230.7 2.0 fusion.2
  233.9 4.0 %collective-permute-done.11 = bf16[8,32,128]{2,1,0:T(8,128)(2,1)S(1)} collective-permute-done((bf16[8,32,128]{2,1,0:T(8,128)(2,1)S(1)}, bf16[8,32,128]{2,1,0:T(8,128)(2,1)S(1)}, u32[]{:S(2)}, u32[]{:S(2)}) %collective-permute-start.11) | collective-permute-done | bytes 65568 | tf_op jit(solution)/shard_map/ppermute | solution.py:18
  238.0 38.4 %psum.61 = f32[32]{0:T(128)S(1)} all-reduce(f32[32]{0:T(128)S(1)} %multiply_reduce_fusion.1), channel_id=1, replica_groups=mesh['dom'=8,'rep'=4] {'dom','rep'}, use_global_device_ids=true, to_apply=%region_15.16 | all-reduce | flops 32 | bytes 256 | tf_op jit(solution)/shard_map/psum | solution.py:118
  276.6 39.8 %psum.62 = f32[32]{0:T(128)S(1)} all-reduce(f32[32]{0:T(128)S(1)} %get-tuple-element.104), channel_id=1, replica_groups=mesh['dom'=8,'rep'=4] {'dom','rep'}, use_global_device_ids=true, to_apply=%region_17.18 | all-reduce | flops 32 | bytes 256 | tf_op jit(solution)/shard_map/psum | solution.py:123
  316.6 2.3 collective-permute-start.14
  325.7 2.0 fusion.3
  329.0 3.7 collective-permute-done.15
  332.8 38.5 %psum.63 = f32[32]{0:T(128)S(1)} all-reduce(f32[32]{0:T(128)S(1)} %multiply_reduce_fusion), channel_id=1, replica_groups=mesh['dom'=8,'rep'=4] {'dom','rep'}, use_global_device_ids=true, to_apply=%region_19.20 | all-reduce | flops 32 | bytes 256 | tf_op jit(solution)/shard_map/psum | solution.py:118
  (151 shorter events, 39.2 us)
Async XLA Ops:
  0.6 13.1 %copy-start = (bf16[8,2,128,128]{3,2,1,0:T(8,128)(2,1)S(1)}, bf16[8,2,128,128]{3,2,1,0:T(8,128)(2,1)}, u32[]{:S(2)}) copy-start(bf16[8,2,128,128]{3,2,1,0:T(8,128)(2,1)} %param.29) | copy-start | bytes 1572868
  2.4 10.4 %copy-start.1 = (bf16[8,128,128]{2,1,0:T(8,128)(2,1)S(1)}, bf16[8,128,128]{2,1,0:T(8,128)(2,1)}, u32[]{:S(2)}) copy-start(bf16[8,128,128]{2,1,0:T(8,128)(2,1)} %param.28) | copy-start | bytes 786436
  4.4 14.2 %all-to-all-start = ((s32[4,8,2]{1,2,0:T(2,128)}), s32[4,8,2]{1,2,0:T(2,128)S(1)}, u32[]{:S(2)}, u32[]{:S(2)}) async-start(s32[4,8,2]{1,2,0:T(2,128)} %copy.71), calls=%async_computation | async-start | bytes 8192 | tf_op jit(solution)/shard_map/all_to_all | solution.py:93
  8.7 14.4 %collective-permute-start.2 = (bf16[8,32,128]{2,1,0:T(8,128)(2,1)S(1)}, bf16[8,32,128]{2,1,0:T(8,128)(2,1)S(1)}, u32[]{:S(2)}, u32[]{:S(2)}) collective-permute-start(bf16[8,32,128]{2,1,0:T(8,128)(2,1)S(1)} %get-tuple-element.114), channel_id=1, source_target_pairs={{0,4},{4,0},{8,12},{12,8},{16,20},{20,16},{24,28},{28,24},{1,5},{5... | collective-permute-start | bytes 196616 | tf_op jit(solution)/shard_map/ppermute | solution.py:18
  10.8 12.1 %collective-permute-start = (bf16[32,128]{1,0:T(8,128)(2,1)S(1)}, bf16[32,128]{1,0:T(8,128)(2,1)S(1)}, u32[]{:S(2)}, u32[]{:S(2)}) collective-permute-start(bf16[32,128]{1,0:T(8,128)(2,1)S(1)} %slice_bitcast_fusion.11), channel_id=1, source_target_pairs={{0,1},{1,2},{2,3},{3,0},{4,5},{5,6},{6,7},{7,4},{8,9},{9,10},{10,1... | collective-permute-start | bytes 24584 | tf_op jit(solution)/shard_map/ppermute | solution.py:14
  11.1 12.0 %collective-permute-start.1 = (f32[32,128]{1,0:T(8,128)S(1)}, f32[32,128]{1,0:T(8,128)S(1)}, u32[]{:S(2)}, u32[]{:S(2)}) collective-permute-start(f32[32,128]{1,0:T(8,128)S(1)} %fusion.68), channel_id=1, source_target_pairs={{0,3},{1,0},{2,1},{3,2},{4,7},{5,4},{6,5},{7,6},{8,11},{9,8},{10,9... | collective-permute-start | bytes 49160 | tf_op jit(solution)/shard_map/ppermute | solution.py:14
  18.7 18.0 %all-to-all-start.1 = ((bf16[4,8,128,128]{3,2,1,0:T(8,128)(2,1)}), bf16[4,8,128,128]{3,2,1,0:T(8,128)(2,1)S(1)}, u32[]{:S(2)}, u32[]{:S(2)}) async-start(bf16[4,8,128,128]{3,2,1,0:T(8,128)(2,1)} %scatter_fusion.1), calls=%async_computation.1 | async-start | bytes 2097152 | tf_op jit(solution)/shard_map/all_to_all | solution.py:92
  39.2 4.3 %collective-permute-start.3 = (bf16[8,32,128]{2,1,0:T(8,128)(2,1)S(1)}, bf16[8,32,128]{2,1,0:T(8,128)(2,1)S(1)}, u32[]{:S(2)}, u32[]{:S(2)}) collective-permute-start(bf16[8,32,128]{2,1,0:T(8,128)(2,1)S(1)} %copy.166), channel_id=1, source_target_pairs={{0,4},{4,0},{8,12},{12,8},{16,20},{20,16},{24,28},{28,24},{1,5},{5... | collective-permute-start | bytes 196616 | tf_op jit(solution)/shard_map/ppermute | solution.py:18
  123.9 8.4 %collective-permute-start.6 = (bf16[8,32,128]{2,1,0:T(8,128)(2,1)S(1)}, bf16[8,32,128]{2,1,0:T(8,128)(2,1)S(1)}, u32[]{:S(2)}, u32[]{:S(2)}) collective-permute-start(bf16[8,32,128]{2,1,0:T(8,128)(2,1)S(1)} %get-tuple-element.110), channel_id=1, source_target_pairs={{0,4},{4,0},{8,12},{12,8},{16,20},{20,16},{24,28},{28,24},{1,5},{5... | collective-permute-start | bytes 196616 | tf_op jit(solution)/shard_map/ppermute | solution.py:18
  129.0 3.1 collective-permute-start.4
  129.1 3.2 collective-permute-start.5
  136.3 4.6 %collective-permute-start.7 = (bf16[8,32,128]{2,1,0:T(8,128)(2,1)S(1)}, bf16[8,32,128]{2,1,0:T(8,128)(2,1)S(1)}, u32[]{:S(2)}, u32[]{:S(2)}) collective-permute-start(bf16[8,32,128]{2,1,0:T(8,128)(2,1)S(1)} %copy.165), channel_id=1, source_target_pairs={{0,4},{4,0},{8,12},{12,8},{16,20},{20,16},{24,28},{28,24},{1,5},{5... | collective-permute-start | bytes 196616 | tf_op jit(solution)/shard_map/ppermute | solution.py:18
  179.5 41.1 %copy-start.6 = (f32[8,32,128]{2,1,0:T(8,128)}, f32[8,32,128]{2,1,0:T(8,128)S(1)}, u32[]{:S(2)}) copy-start(f32[8,32,128]{2,1,0:T(8,128)S(1)} %get-tuple-element.109) | copy-start | bytes 393220
  220.7 8.6 %collective-permute-start.10 = (bf16[8,32,128]{2,1,0:T(8,128)(2,1)S(1)}, bf16[8,32,128]{2,1,0:T(8,128)(2,1)S(1)}, u32[]{:S(2)}, u32[]{:S(2)}) collective-permute-start(bf16[8,32,128]{2,1,0:T(8,128)(2,1)S(1)} %get-tuple-element.106), channel_id=1, source_target_pairs={{0,4},{4,0},{8,12},{12,8},{16,20},{20,16},{24,28},{28,24},{1,5},{5... | collective-permute-start | bytes 196616 | tf_op jit(solution)/shard_map/ppermute | solution.py:18
  225.8 3.3 collective-permute-start.8
  226.1 3.2 collective-permute-start.9
  233.3 4.6 %collective-permute-start.11 = (bf16[8,32,128]{2,1,0:T(8,128)(2,1)S(1)}, bf16[8,32,128]{2,1,0:T(8,128)(2,1)S(1)}, u32[]{:S(2)}, u32[]{:S(2)}) collective-permute-start(bf16[8,32,128]{2,1,0:T(8,128)(2,1)S(1)} %copy.164), channel_id=1, source_target_pairs={{0,4},{4,0},{8,12},{12,8},{16,20},{20,16},{24,28},{28,24},{1,5},{5... | collective-permute-start | bytes 196616 | tf_op jit(solution)/shard_map/ppermute | solution.py:18
  233.9 42.5 %copy-start.7 = (f32[8,32,128]{2,1,0:T(8,128)S(1)}, f32[8,32,128]{2,1,0:T(8,128)}, u32[]{:S(2)}) copy-start(f32[8,32,128]{2,1,0:T(8,128)} %copy-done.6) | copy-start | bytes 393220
  276.6 39.9 %copy-start.4 = (f32[8,32,128]{2,1,0:T(8,128)}, f32[8,32,128]{2,1,0:T(8,128)S(1)}, u32[]{:S(2)}) copy-start(f32[8,32,128]{2,1,0:T(8,128)S(1)} %get-tuple-element.105) | copy-start | bytes 393220
  316.6 7.8 %collective-permute-start.14 = (bf16[8,32,128]{2,1,0:T(8,128)(2,1)S(1)}, bf16[8,32,128]{2,1,0:T(8,128)(2,1)S(1)}, u32[]{:S(2)}, u32[]{:S(2)}) collective-permute-start(bf16[8,32,128]{2,1,0:T(8,128)(2,1)S(1)} %get-tuple-element.102), channel_id=1, source_target_pairs={{0,4},{4,0},{8,12},{12,8},{16,20},{20,16},{24,28},{28,24},{1,5},{5... | collective-permute-start | bytes 196616 | tf_op jit(solution)/shard_map/ppermute | solution.py:18
  321.1 3.1 collective-permute-start.12
  321.1 3.2 collective-permute-start.13
  328.3 4.3 %collective-permute-start.15 = (bf16[8,32,128]{2,1,0:T(8,128)(2,1)S(1)}, bf16[8,32,128]{2,1,0:T(8,128)(2,1)S(1)}, u32[]{:S(2)}, u32[]{:S(2)}) collective-permute-start(bf16[8,32,128]{2,1,0:T(8,128)(2,1)S(1)} %copy.163), channel_id=1, source_target_pairs={{0,4},{4,0},{8,12},{12,8},{16,20},{20,16},{24,28},{28,24},{1,5},{5... | collective-permute-start | bytes 196616 | tf_op jit(solution)/shard_map/ppermute | solution.py:18
  329.0 42.4 %copy-start.5 = (f32[8,32,128]{2,1,0:T(8,128)S(1)}, f32[8,32,128]{2,1,0:T(8,128)}, u32[]{:S(2)}) copy-start(f32[8,32,128]{2,1,0:T(8,128)} %copy-done.4) | copy-start | bytes 393220
  (8 other events, 24.9 us)
where the time goes:
time: 373 us; the launch traced here: 372 us
  blocking collectives  276 us (74%)
  waiting for transfers between devices  30.1 us (8%)
  starting transfers between devices  25.1 us (7%)
  local copies, waits for them, and re-layouts  18.9 us (5%)
  matrix products  17.6 us (5%)
    psum x4, blocking collectives, body(): lax.psum(jnp.sum(residual * preconditioned, axis=(0, 2)), ('dom', 'rep'))  161 us
    psum x3, blocking collectives, body(): curve = lax.psum(jnp.sum(direction * image, axis=(0, 2)), ('dom', 'rep'))  115 us
    ppermute x8, waiting for transfers between devices, partner(): lax.ppermute(value, axis, [(i, i ^ 1 << distance) for i in range(lax.axis...  14.6 us
    all_to_all x1, waiting for transfers between devices, body(): lax.all_to_all(send_set, 'rep', split_axis=0, concat_axis=0, tiled=True)  12.1 us
    ppermute x8, starting transfers between devices, partner(): lax.ppermute(value, axis, [(i, i ^ 1 << distance) for i in range(lax.axis...  10 us
    gather x8, local copies, waits for them, and re-layouts, contact_pairs(): difference = (vector[near_index] - other[far_index]).astype(jnp.bfloat16)  7.96 us
    dot_general x4, matrix products, contact_pairs(): jnp.einsum('srj,skj->srk', multiplier, contact_set, preferred_element_typ...  7.84 us
  transfers between devices with their start and end apart: 18, of which 8 were waited for; matrix products, arithmetic and copies ran while one was open for 5% of the time, Pallas kernels for 0%

commit v1 on v0

--- a/solution.py
+++ b/solution.py
@@ -16,6 +16,13 @@
 
 def partner(value, axis, distance):
     return lax.ppermute(value, axis, [(i, i ^ 1 << distance) for i in range(lax.axis_size(axis))])
+
+
+def total(value):
+    count = lax.axis_size("dom") * lax.axis_size("rep")
+    spread = jnp.broadcast_to(value[None], (count,) + value.shape)
+    gathered = lax.all_to_all(spread, ("dom", "rep"), 0, 0, tiled=True)
+    return jnp.sum(gathered, axis=0)
 
 
 def local_stiffness(rounded, diag_tiles, off_tiles, off_cols):
@@ -103,7 +110,7 @@
     residual = rhs
     preconditioned = scale * residual
     direction = preconditioned
-    res_dot = lax.psum(jnp.sum(residual * preconditioned, axis=(0, 2)), ("dom", "rep"))
+    res_dot = total(jnp.sum(residual * preconditioned, axis=(0, 2)))
     for step in range(ITERS):
         image = apply_operator(
             direction,
@@ -115,12 +122,12 @@
             near_index,
             far_index,
         )
-        curve = lax.psum(jnp.sum(direction * image, axis=(0, 2)), ("dom", "rep"))
+        curve = total(jnp.sum(direction * image, axis=(0, 2)))
         alpha = res_dot / curve
         solution = solution + alpha[None, :, None] * direction
         residual = residual - alpha[None, :, None] * image
         preconditioned = scale * residual
-        next_dot = lax.psum(jnp.sum(residual * preconditioned, axis=(0, 2)), ("dom", "rep"))
+        next_dot = total(jnp.sum(residual * preconditioned, axis=(0, 2)))
         direction = preconditioned + (next_dot / res_dot)[None, :, None] * direction
         res_dot = next_dot
     return (solution, residual)

time: 373 us -> 166 us (0.45)
  blocking collectives: 276 us -> 64.1 us
    psum x7 -> x0, blocking collectives: 276 us -> none  [the longest x4 161 us: body(): lax.psum(jnp.sum(residual * preconditioned, axis=(0, 2)), ('dom', 'rep'))]
    all_to_all x0 -> x7, blocking collectives: none -> 64.1 us  [total(): gathered = lax.all_to_all(spread, ('dom', 'rep'), 0, 0, tiled=True)]
    all_to_all x0 -> x1, waiting for transfers between devices: none -> 7.05 us  [total(): gathered = lax.all_to_all(spread, ('dom', 'rep'), 0, 0, tiled=True)]
  transfers between devices with their start and end apart: 18 -> 19, of which waited for: 8 -> 9; matrix products, arithmetic and copies ran while one was open for 5% -> 11% of each run, Pallas kernels for 0% -> 0%
where the time goes in v1:
time: 166 us
  blocking collectives  64.1 us (39%)
  waiting for transfers between devices  33.4 us (20%)
  starting transfers between devices  26.7 us (16%)
  local copies, waits for them, and re-layouts  18.9 us (11%)
  matrix products  17.6 us (11%)
  other arithmetic  3.64 us (2%)
    all_to_all x7, blocking collectives, total(): gathered = lax.all_to_all(spread, ('dom', 'rep'), 0, 0, tiled=True)  64.1 us
    all_to_all x1, waiting for transfers between devices, body(): lax.all_to_all(send_set, 'rep', split_axis=0, concat_axis=0, tiled=True)  12.1 us
    ppermute x8, waiting for transfers between devices, partner(): lax.ppermute(value, axis, [(i, i ^ 1 << distance) for i in range(lax.axis...  10.9 us
    ppermute x8, starting transfers between devices, partner(): lax.ppermute(value, axis, [(i, i ^ 1 << distance) for i in range(lax.axis...  9.26 us
    gather x8, local copies, waits for them, and re-layouts, contact_pairs(): difference = (vector[near_index] - other[far_index]).astype(jnp.bfloat16)  7.96 us
    dot_general x4, matrix products, contact_pairs(): jnp.einsum('srj,skj->srk', multiplier, contact_set, preferred_element_typ...  7.84 us
    ppermute x8, starting transfers between devices, from_behind(): return lax.ppermute(value, axis, pairs)  7.14 us
    all_to_all x1, waiting for transfers between devices, total(): gathered = lax.all_to_all(spread, ('dom', 'rep'), 0, 0, tiled=True)  7.05 us
  transfers between devices with their start and end apart: 19, of which 9 were waited for; matrix products, arithmetic and copies ran while one was open for 11% of the time, Pallas kernels for 0%

profile of v1, /device:TPU:0, one launch (start us, length us, event | category | flops | bytes accessed | tf_op | source)
XLA Modules:
  0.0 165.6 jit_solution(12527866987354021008)
XLA Ops:
  4.4 4.2 %all-to-all-start.1 = ((s32[4,8,2]{1,2,0:T(2,128)}), s32[4,8,2]{1,2,0:T(2,128)S(1)}, u32[]{:S(2)}, u32[]{:S(2)}) async-start(s32[4,8,2]{1,2,0:T(2,128)} %copy.130), calls=%async_computation.1 | async-start | bytes 8192 | tf_op jit(solution)/shard_map/all_to_all | solution.py:100
  8.7 2.1 %collective-permute-start.2 = (bf16[8,32,128]{2,1,0:T(8,128)(2,1)S(1)}, bf16[8,32,128]{2,1,0:T(8,128)(2,1)S(1)}, u32[]{:S(2)}, u32[]{:S(2)}) collective-permute-start(bf16[8,32,128]{2,1,0:T(8,128)(2,1)S(1)} %get-tuple-element.112), channel_id=1, source_target_pairs={{0,4},{4,0},{8,12},{12,8},{16,20},{20,16},{24,28},{28,24},{1,5},{5... | collective-permute-start | bytes 196616 | tf_op jit(solution)/shard_map/ppermute | solution.py:18
  15.9 2.8 %scatter_fusion.1 = bf16[4,8,128,128]{3,2,1,0:T(8,128)(2,1)} fusion(bf16[4,8,128,128]{3,2,1,0:T(8,128)(2,1)} %broadcast_in_dim.25, s32[16]{0:T(128)S(1)} %fusion.107, bf16[16,128,128]{2,1,0:T(8,128)(2,1)S(1)} %copy-done.10), kind=kCustom, calls=%fused_computation.13 | custom fusion | bytes 1572992 | tf_op jit(solution)/shard_map/scatter | solution.py:95
  18.7 3.5 %all-to-all-start.2 = ((bf16[4,8,128,128]{3,2,1,0:T(8,128)(2,1)}), bf16[4,8,128,128]{3,2,1,0:T(8,128)(2,1)S(1)}, u32[]{:S(2)}, u32[]{:S(2)}) async-start(bf16[4,8,128,128]{3,2,1,0:T(8,128)(2,1)} %scatter_fusion.1), calls=%async_computation.2 | async-start | bytes 2097152 | tf_op jit(solution)/shard_map/all_to_all | solution.py:99
  24.5 12.1 %all-to-all-done.2 = bf16[4,8,128,128]{3,2,1,0:T(8,128)(2,1)S(1)} async-done(((bf16[4,8,128,128]{3,2,1,0:T(8,128)(2,1)}), bf16[4,8,128,128]{3,2,1,0:T(8,128)(2,1)S(1)}, u32[]{:S(2)}, u32[]{:S(2)}) %all-to-all-start.2) | async-done | bytes 1048608 | tf_op jit(solution)/shard_map/all_to_all | solution.py:99
  36.6 2.0 %fusion = f32[32,32,128]{2,1,0:T(8,128)S(1)} fusion(bf16[32,128,128]{2,1,0:T(8,128)(2,1)S(1)} %bitcast.211, f32[32,32,128]{2,1,0:T(8,128)S(1)} %gather_fusion.1, f32[32,32,128]{2,1,0:T(8,128)} %gather_fusion.2), kind=kOutput, calls=%fused_computation.18 | convolution fusion | flops 67502080 | bytes 2621440 | tf_op jit(solution)/shard_map/srj,skj->srk/dot_general | solution.py:47
  40.5 3.1 %collective-permute-done.3 = bf16[8,32,128]{2,1,0:T(8,128)(2,1)S(1)} collective-permute-done((bf16[8,32,128]{2,1,0:T(8,128)(2,1)S(1)}, bf16[8,32,128]{2,1,0:T(8,128)(2,1)S(1)}, u32[]{:S(2)}, u32[]{:S(2)}) %collective-permute-start.3) | collective-permute-done | bytes 65568 | tf_op jit(solution)/shard_map/ppermute | solution.py:18
  43.7 11.0 %all_to_all.58 = f32[32,1,32]{2,1,0:T(1,128)S(1)} all-to-all(f32[32,1,32]{2,1,0:T(1,128)S(1)} %broadcast_in_dim.22), channel_id=1, replica_groups=mesh['dom'=8,'rep'=4] {'dom','rep'}, dimensions={0} | all-to-all | bytes 8192 | tf_op jit(solution)/shard_map/all_to_all | solution.py:24
  55.3 2.5 %all-to-all-start.3 = ((f32[32,1,32]{2,1,0:T(1,128)}), f32[32,1,32]{2,1,0:T(1,128)S(1)}, u32[]{:S(2)}, u32[]{:S(2)}) async-start(f32[32,1,32]{2,1,0:T(1,128)} %broadcast_in_dim.26), calls=%async_computation.3 | async-start | bytes 32768 | tf_op jit(solution)/shard_map/all_to_all | solution.py:24
  57.9 7.0 %all-to-all-done.3 = f32[32,1,32]{2,1,0:T(1,128)S(1)} async-done(((f32[32,1,32]{2,1,0:T(1,128)}), f32[32,1,32]{2,1,0:T(1,128)S(1)}, u32[]{:S(2)}, u32[]{:S(2)}) %all-to-all-start.3) | async-done | bytes 4128 | tf_op jit(solution)/shard_map/all_to_all | solution.py:24
  65.2 8.8 %all_to_all.59 = f32[32,1,32]{2,1,0:T(1,128)S(1)} all-to-all(f32[32,1,32]{2,1,0:T(1,128)S(1)} %broadcast_in_dim.27), channel_id=1, replica_groups=mesh['dom'=8,'rep'=4] {'dom','rep'}, dimensions={0} | all-to-all | bytes 8192 | tf_op jit(solution)/shard_map/all_to_all | solution.py:24
  77.0 1.7 %collective-permute-start.5 = (f32[32,128]{1,0:T(8,128)S(1)}, f32[32,128]{1,0:T(8,128)S(1)}, u32[]{:S(2)}, u32[]{:S(2)}) collective-permute-start(f32[32,128]{1,0:T(8,128)S(1)} %fusion.65), channel_id=1, source_target_pairs={{0,3},{1,0},{2,1},{3,2},{4,7},{5,4},{6,5},{7,6},{8,11},{9,8},{10,9... | collective-permute-start | bytes 49160 | tf_op jit(solution)/shard_map/ppermute | solution.py:14
  81.6 2.0 %fusion.1 = f32[32,32,128]{2,1,0:T(8,128)S(1)} fusion(bf16[32,128,128]{2,1,0:T(8,128)(2,1)S(1)} %bitcast.212, f32[32,32,128]{2,1,0:T(8,128)S(1)} %gather_fusion.4, f32[32,32,128]{2,1,0:T(8,128)} %gather_fusion.5), kind=kOutput, calls=%fused_computation.19 | convolution fusion | flops 67502080 | bytes 2621440 | tf_op jit(solution)/shard_map/srj,skj->srk/dot_general | solution.py:47
  86.4 2.6 %collective-permute-done.7 = bf16[8,32,128]{2,1,0:T(8,128)(2,1)S(1)} collective-permute-done((bf16[8,32,128]{2,1,0:T(8,128)(2,1)S(1)}, bf16[8,32,128]{2,1,0:T(8,128)(2,1)S(1)}, u32[]{:S(2)}, u32[]{:S(2)}) %collective-permute-start.7) | collective-permute-done | bytes 65568 | tf_op jit(solution)/shard_map/ppermute | solution.py:18
  89.1 8.8 %all_to_all.60 = f32[32,1,32]{2,1,0:T(1,128)S(1)} all-to-all(f32[32,1,32]{2,1,0:T(1,128)S(1)} %broadcast_in_dim.28), channel_id=1, replica_groups=mesh['dom'=8,'rep'=4] {'dom','rep'}, dimensions={0} | all-to-all | bytes 8192 | tf_op jit(solution)/shard_map/all_to_all | solution.py:24
  98.2 8.8 %all_to_all.61 = f32[32,1,32]{2,1,0:T(1,128)S(1)} all-to-all(f32[32,1,32]{2,1,0:T(1,128)S(1)} %broadcast_in_dim.29), channel_id=1, replica_groups=mesh['dom'=8,'rep'=4] {'dom','rep'}, dimensions={0} | all-to-all | bytes 8192 | tf_op jit(solution)/shard_map/all_to_all | solution.py:24
  110.7 1.7 %collective-permute-start.9 = (f32[32,128]{1,0:T(8,128)S(1)}, f32[32,128]{1,0:T(8,128)S(1)}, u32[]{:S(2)}, u32[]{:S(2)}) collective-permute-start(f32[32,128]{1,0:T(8,128)S(1)} %fusion.62), channel_id=1, source_target_pairs={{0,3},{1,0},{2,1},{3,2},{4,7},{5,4},{6,5},{7,6},{8,11},{9,8},{10,9... | collective-permute-start | bytes 49160 | tf_op jit(solution)/shard_map/ppermute | solution.py:14
  115.3 2.0 %fusion.2 = f32[32,32,128]{2,1,0:T(8,128)S(1)} fusion(bf16[32,128,128]{2,1,0:T(8,128)(2,1)S(1)} %bitcast.213, f32[32,32,128]{2,1,0:T(8,128)S(1)} %gather_fusion.7, f32[32,32,128]{2,1,0:T(8,128)} %gather_fusion.8), kind=kOutput, calls=%fused_computation.20 | convolution fusion | flops 67502080 | bytes 2621440 | tf_op jit(solution)/shard_map/srj,skj->srk/dot_general | solution.py:47
  120.0 2.6 %collective-permute-done.11 = bf16[8,32,128]{2,1,0:T(8,128)(2,1)S(1)} collective-permute-done((bf16[8,32,128]{2,1,0:T(8,128)(2,1)S(1)}, bf16[8,32,128]{2,1,0:T(8,128)(2,1)S(1)}, u32[]{:S(2)}, u32[]{:S(2)}) %collective-permute-start.11) | collective-permute-done | bytes 65568 | tf_op jit(solution)/shard_map/ppermute | solution.py:18
  122.8 8.8 %all_to_all.62 = f32[32,1,32]{2,1,0:T(1,128)S(1)} all-to-all(f32[32,1,32]{2,1,0:T(1,128)S(1)} %broadcast_in_dim.30), channel_id=1, replica_groups=mesh['dom'=8,'rep'=4] {'dom','rep'}, dimensions={0} | all-to-all | bytes 8192 | tf_op jit(solution)/shard_map/all_to_all | solution.py:24
  131.9 8.8 %all_to_all.63 = f32[32,1,32]{2,1,0:T(1,128)S(1)} all-to-all(f32[32,1,32]{2,1,0:T(1,128)S(1)} %broadcast_in_dim.31), channel_id=1, replica_groups=mesh['dom'=8,'rep'=4] {'dom','rep'}, dimensions={0} | all-to-all | bytes 8192 | tf_op jit(solution)/shard_map/all_to_all | solution.py:24
  148.4 2.0 %fusion.3 = f32[32,32,128]{2,1,0:T(8,128)S(1)} fusion(bf16[32,128,128]{2,1,0:T(8,128)(2,1)S(1)} %bitcast.214, f32[32,32,128]{2,1,0:T(8,128)S(1)} %gather_fusion.10, f32[32,32,128]{2,1,0:T(8,128)} %gather_fusion.11), kind=kOutput, calls=%fused_computation.21 | convolution fusion | flops 67502080 | bytes 2621440 | tf_op jit(solution)/shard_map/srj,skj->srk/dot_general | solution.py:47
  153.1 2.6 %collective-permute-done.15 = bf16[8,32,128]{2,1,0:T(8,128)(2,1)S(1)} collective-permute-done((bf16[8,32,128]{2,1,0:T(8,128)(2,1)S(1)}, bf16[8,32,128]{2,1,0:T(8,128)(2,1)S(1)}, u32[]{:S(2)}, u32[]{:S(2)}) %collective-permute-start.15) | collective-permute-done | bytes 65568 | tf_op jit(solution)/shard_map/ppermute | solution.py:18
  155.9 8.8 %all_to_all.64 = f32[32,1,32]{2,1,0:T(1,128)S(1)} all-to-all(f32[32,1,32]{2,1,0:T(1,128)S(1)} %broadcast_in_dim.32), channel_id=1, replica_groups=mesh['dom'=8,'rep'=4] {'dom','rep'}, dimensions={0} | all-to-all | bytes 8192 | tf_op jit(solution)/shard_map/all_to_all | solution.py:24
  (171 shorter events, 43.8 us)
Async XLA Ops:
  0.6 13.1 %copy-start = (bf16[8,2,128,128]{3,2,1,0:T(8,128)(2,1)S(1)}, bf16[8,2,128,128]{3,2,1,0:T(8,128)(2,1)}, u32[]{:S(2)}) copy-start(bf16[8,2,128,128]{3,2,1,0:T(8,128)(2,1)} %param.29) | copy-start | bytes 1572868
  2.4 10.4 %copy-start.1 = (bf16[8,128,128]{2,1,0:T(8,128)(2,1)S(1)}, bf16[8,128,128]{2,1,0:T(8,128)(2,1)}, u32[]{:S(2)}) copy-start(bf16[8,128,128]{2,1,0:T(8,128)(2,1)} %param.28) | copy-start | bytes 786436
  4.4 14.2 %all-to-all-start.1 = ((s32[4,8,2]{1,2,0:T(2,128)}), s32[4,8,2]{1,2,0:T(2,128)S(1)}, u32[]{:S(2)}, u32[]{:S(2)}) async-start(s32[4,8,2]{1,2,0:T(2,128)} %copy.130), calls=%async_computation.1 | async-start | bytes 8192 | tf_op jit(solution)/shard_map/all_to_all | solution.py:100
  8.7 14.4 %collective-permute-start.2 = (bf16[8,32,128]{2,1,0:T(8,128)(2,1)S(1)}, bf16[8,32,128]{2,1,0:T(8,128)(2,1)S(1)}, u32[]{:S(2)}, u32[]{:S(2)}) collective-permute-start(bf16[8,32,128]{2,1,0:T(8,128)(2,1)S(1)} %get-tuple-element.112), channel_id=1, source_target_pairs={{0,4},{4,0},{8,12},{12,8},{16,20},{20,16},{24,28},{28,24},{1,5},{5... | collective-permute-start | bytes 196616 | tf_op jit(solution)/shard_map/ppermute | solution.py:18
  10.8 12.1 %collective-permute-start = (bf16[32,128]{1,0:T(8,128)(2,1)S(1)}, bf16[32,128]{1,0:T(8,128)(2,1)S(1)}, u32[]{:S(2)}, u32[]{:S(2)}) collective-permute-start(bf16[32,128]{1,0:T(8,128)(2,1)S(1)} %slice_bitcast_fusion.11), channel_id=1, source_target_pairs={{0,1},{1,2},{2,3},{3,0},{4,5},{5,6},{6,7},{7,4},{8,9},{9,10},{10,1... | collective-permute-start | bytes 24584 | tf_op jit(solution)/shard_map/ppermute | solution.py:14
  11.1 12.0 %collective-permute-start.1 = (f32[32,128]{1,0:T(8,128)S(1)}, f32[32,128]{1,0:T(8,128)S(1)}, u32[]{:S(2)}, u32[]{:S(2)}) collective-permute-start(f32[32,128]{1,0:T(8,128)S(1)} %fusion.68), channel_id=1, source_target_pairs={{0,3},{1,0},{2,1},{3,2},{4,7},{5,4},{6,5},{7,6},{8,11},{9,8},{10,9... | collective-permute-start | bytes 49160 | tf_op jit(solution)/shard_map/ppermute | solution.py:14
  18.7 18.0 %all-to-all-start.2 = ((bf16[4,8,128,128]{3,2,1,0:T(8,128)(2,1)}), bf16[4,8,128,128]{3,2,1,0:T(8,128)(2,1)S(1)}, u32[]{:S(2)}, u32[]{:S(2)}) async-start(bf16[4,8,128,128]{3,2,1,0:T(8,128)(2,1)} %scatter_fusion.1), calls=%async_computation.2 | async-start | bytes 2097152 | tf_op jit(solution)/shard_map/all_to_all | solution.py:99
  39.2 4.3 %collective-permute-start.3 = (bf16[8,32,128]{2,1,0:T(8,128)(2,1)S(1)}, bf16[8,32,128]{2,1,0:T(8,128)(2,1)S(1)}, u32[]{:S(2)}, u32[]{:S(2)}) collective-permute-start(bf16[8,32,128]{2,1,0:T(8,128)(2,1)S(1)} %copy.232), channel_id=1, source_target_pairs={{0,4},{4,0},{8,12},{12,8},{16,20},{20,16},{24,28},{28,24},{1,5},{5... | collective-permute-start | bytes 196616 | tf_op jit(solution)/shard_map/ppermute | solution.py:18
  55.3 9.6 %all-to-all-start.3 = ((f32[32,1,32]{2,1,0:T(1,128)}), f32[32,1,32]{2,1,0:T(1,128)S(1)}, u32[]{:S(2)}, u32[]{:S(2)}) async-start(f32[32,1,32]{2,1,0:T(1,128)} %broadcast_in_dim.26), calls=%async_computation.3 | async-start | bytes 32768 | tf_op jit(solution)/shard_map/all_to_all | solution.py:24
  74.2 6.0 %collective-permute-start.6 = (bf16[8,32,128]{2,1,0:T(8,128)(2,1)S(1)}, bf16[8,32,128]{2,1,0:T(8,128)(2,1)S(1)}, u32[]{:S(2)}, u32[]{:S(2)}) collective-permute-start(bf16[8,32,128]{2,1,0:T(8,128)(2,1)S(1)} %get-tuple-element.108), channel_id=1, source_target_pairs={{0,4},{4,0},{8,12},{12,8},{16,20},{20,16},{24,28},{28,24},{1,5},{5... | collective-permute-start | bytes 196616 | tf_op jit(solution)/shard_map/ppermute | solution.py:18
  77.0 3.1 %collective-permute-start.4 = (bf16[32,128]{1,0:T(8,128)(2,1)S(1)}, bf16[32,128]{1,0:T(8,128)(2,1)S(1)}, u32[]{:S(2)}, u32[]{:S(2)}) collective-permute-start(bf16[32,128]{1,0:T(8,128)(2,1)S(1)} %slice_bitcast_fusion.8), channel_id=1, source_target_pairs={{0,1},{1,2},{2,3},{3,0},{4,5},{5,6},{6,7},{7,4},{8,9},{9,10},{10,1... | collective-permute-start | bytes 24584 | tf_op jit(solution)/shard_map/ppermute | solution.py:14
  77.0 3.2 %collective-permute-start.5 = (f32[32,128]{1,0:T(8,128)S(1)}, f32[32,128]{1,0:T(8,128)S(1)}, u32[]{:S(2)}, u32[]{:S(2)}) collective-permute-start(f32[32,128]{1,0:T(8,128)S(1)} %fusion.65), channel_id=1, source_target_pairs={{0,3},{1,0},{2,1},{3,2},{4,7},{5,4},{6,5},{7,6},{8,11},{9,8},{10,9... | collective-permute-start | bytes 49160 | tf_op jit(solution)/shard_map/ppermute | solution.py:14
  84.2 4.7 %collective-permute-start.7 = (bf16[8,32,128]{2,1,0:T(8,128)(2,1)S(1)}, bf16[8,32,128]{2,1,0:T(8,128)(2,1)S(1)}, u32[]{:S(2)}, u32[]{:S(2)}) collective-permute-start(bf16[8,32,128]{2,1,0:T(8,128)(2,1)S(1)} %copy.231), channel_id=1, source_target_pairs={{0,4},{4,0},{8,12},{12,8},{16,20},{20,16},{24,28},{28,24},{1,5},{5... | collective-permute-start | bytes 196616 | tf_op jit(solution)/shard_map/ppermute | solution.py:18
  89.0 9.0 %copy-start.9 = (f32[8,32,128]{2,1,0:T(8,128)S(1)}, f32[8,32,128]{2,1,0:T(8,128)}, u32[]{:S(2)}) copy-start(f32[8,32,128]{2,1,0:T(8,128)} %copy-done.8) | copy-start | bytes 393220
  107.2 6.7 %collective-permute-start.10 = (bf16[8,32,128]{2,1,0:T(8,128)(2,1)S(1)}, bf16[8,32,128]{2,1,0:T(8,128)(2,1)S(1)}, u32[]{:S(2)}, u32[]{:S(2)}) collective-permute-start(bf16[8,32,128]{2,1,0:T(8,128)(2,1)S(1)} %get-tuple-element.104), channel_id=1, source_target_pairs={{0,4},{4,0},{8,12},{12,8},{16,20},{20,16},{24,28},{28,24},{1,5},{5... | collective-permute-start | bytes 196616 | tf_op jit(solution)/shard_map/ppermute | solution.py:18
  110.7 3.1 %collective-permute-start.8 = (bf16[32,128]{1,0:T(8,128)(2,1)S(1)}, bf16[32,128]{1,0:T(8,128)(2,1)S(1)}, u32[]{:S(2)}, u32[]{:S(2)}) collective-permute-start(bf16[32,128]{1,0:T(8,128)(2,1)S(1)} %slice_bitcast_fusion.5), channel_id=1, source_target_pairs={{0,1},{1,2},{2,3},{3,0},{4,5},{5,6},{6,7},{7,4},{8,9},{9,10},{10,1... | collective-permute-start | bytes 24584 | tf_op jit(solution)/shard_map/ppermute | solution.py:14
  110.7 3.2 %collective-permute-start.9 = (f32[32,128]{1,0:T(8,128)S(1)}, f32[32,128]{1,0:T(8,128)S(1)}, u32[]{:S(2)}, u32[]{:S(2)}) collective-permute-start(f32[32,128]{1,0:T(8,128)S(1)} %fusion.62), channel_id=1, source_target_pairs={{0,3},{1,0},{2,1},{3,2},{4,7},{5,4},{6,5},{7,6},{8,11},{9,8},{10,9... | collective-permute-start | bytes 49160 | tf_op jit(solution)/shard_map/ppermute | solution.py:14
  117.9 4.7 %collective-permute-start.11 = (bf16[8,32,128]{2,1,0:T(8,128)(2,1)S(1)}, bf16[8,32,128]{2,1,0:T(8,128)(2,1)S(1)}, u32[]{:S(2)}, u32[]{:S(2)}) collective-permute-start(bf16[8,32,128]{2,1,0:T(8,128)(2,1)S(1)} %copy.230), channel_id=1, source_target_pairs={{0,4},{4,0},{8,12},{12,8},{16,20},{20,16},{24,28},{28,24},{1,5},{5... | collective-permute-start | bytes 196616 | tf_op jit(solution)/shard_map/ppermute | solution.py:18
  122.7 9.0 %copy-start.7 = (f32[8,32,128]{2,1,0:T(8,128)S(1)}, f32[8,32,128]{2,1,0:T(8,128)}, u32[]{:S(2)}) copy-start(f32[8,32,128]{2,1,0:T(8,128)} %copy-done.6) | copy-start | bytes 393220
  140.9 6.0 %collective-permute-start.14 = (bf16[8,32,128]{2,1,0:T(8,128)(2,1)S(1)}, bf16[8,32,128]{2,1,0:T(8,128)(2,1)S(1)}, u32[]{:S(2)}, u32[]{:S(2)}) collective-permute-start(bf16[8,32,128]{2,1,0:T(8,128)(2,1)S(1)} %get-tuple-element.100), channel_id=1, source_target_pairs={{0,4},{4,0},{8,12},{12,8},{16,20},{20,16},{24,28},{28,24},{1,5},{5... | collective-permute-start | bytes 196616 | tf_op jit(solution)/shard_map/ppermute | solution.py:18
  143.7 3.1 %collective-permute-start.12 = (bf16[32,128]{1,0:T(8,128)(2,1)S(1)}, bf16[32,128]{1,0:T(8,128)(2,1)S(1)}, u32[]{:S(2)}, u32[]{:S(2)}) collective-permute-start(bf16[32,128]{1,0:T(8,128)(2,1)S(1)} %slice_bitcast_fusion.2), channel_id=1, source_target_pairs={{0,1},{1,2},{2,3},{3,0},{4,5},{5,6},{6,7},{7,4},{8,9},{9,10},{10,1... | collective-permute-start | bytes 24584 | tf_op jit(solution)/shard_map/ppermute | solution.py:14
  143.7 3.2 %collective-permute-start.13 = (f32[32,128]{1,0:T(8,128)S(1)}, f32[32,128]{1,0:T(8,128)S(1)}, u32[]{:S(2)}, u32[]{:S(2)}) collective-permute-start(f32[32,128]{1,0:T(8,128)S(1)} %fusion.59), channel_id=1, source_target_pairs={{0,3},{1,0},{2,1},{3,2},{4,7},{5,4},{6,5},{7,6},{8,11},{9,8},{10,9... | collective-permute-start | bytes 49160 | tf_op jit(solution)/shard_map/ppermute | solution.py:14
  150.9 4.7 %collective-permute-start.15 = (bf16[8,32,128]{2,1,0:T(8,128)(2,1)S(1)}, bf16[8,32,128]{2,1,0:T(8,128)(2,1)S(1)}, u32[]{:S(2)}, u32[]{:S(2)}) collective-permute-start(bf16[8,32,128]{2,1,0:T(8,128)(2,1)S(1)} %copy.229), channel_id=1, source_target_pairs={{0,4},{4,0},{8,12},{12,8},{16,20},{20,16},{24,28},{28,24},{1,5},{5... | collective-permute-start | bytes 196616 | tf_op jit(solution)/shard_map/ppermute | solution.py:18
  155.7 9.0 %copy-start.5 = (f32[8,32,128]{2,1,0:T(8,128)S(1)}, f32[8,32,128]{2,1,0:T(8,128)}, u32[]{:S(2)}) copy-start(f32[8,32,128]{2,1,0:T(8,128)} %copy-done.4) | copy-start | bytes 393220
  (10 other events, 49.6 us)

commit v2 on v1

--- a/solution.py
+++ b/solution.py
@@ -89,19 +89,27 @@
     contact_bnode,
 ):
     groups = lax.axis_size("rep")
+    tiles = contact_tiles.shape[0]
+    slots = groups * CAP
     target = contact_owner[:, 0]
     choose = (target[:, None] == jnp.arange(groups, dtype=jnp.int32)[None, :]).astype(jnp.int32)
     rank = jnp.sum((jnp.cumsum(choose, axis=0) - choose) * choose, axis=1)
-    send_set = jnp.zeros((groups, CAP, B, B), jnp.bfloat16).at[target, rank].set(contact_tiles)
+    slot_of = target * CAP + rank
+    pick = (slot_of[None, :] == jnp.arange(slots, dtype=jnp.int32)[:, None]).astype(jnp.bfloat16)
+    send_set = jnp.einsum(
+        "sc,cij->sij", pick, contact_tiles, preferred_element_type=jnp.float32
+    ).astype(jnp.bfloat16)
     labels = jnp.stack([contact_anode, contact_bnode], axis=1)
-    send_labels = jnp.zeros((groups, CAP, 2), jnp.int32).at[target, rank].set(labels)
-    got_set, got_labels = (
-        lax.all_to_all(send_set, "rep", split_axis=0, concat_axis=0, tiled=True),
-        lax.all_to_all(send_labels, "rep", split_axis=0, concat_axis=0, tiled=True),
-    )
-    slots = groups * CAP
-    contact_set = got_set.reshape(slots, B, B)
-    got_labels = got_labels.reshape(slots, 2)
+    wide = jnp.concatenate([labels // 256, labels % 256], axis=1).astype(jnp.bfloat16)
+    send_labels = jnp.einsum("sc,cl->sl", pick, wide, preferred_element_type=jnp.float32)
+    extra = jnp.zeros((slots, 16, B), jnp.float32).at[:, 0, :4].set(send_labels)
+    payload = jnp.concatenate([send_set, extra.astype(jnp.bfloat16)], axis=1)
+    got = lax.all_to_all(
+        payload.reshape(groups, CAP, B + 16, B), "rep", split_axis=0, concat_axis=0, tiled=True
+    ).reshape(slots, B + 16, B)
+    contact_set = got[:, :B]
+    got_labels = got[:, B, :4].astype(jnp.int32)
+    got_labels = got_labels[:, :2] * 256 + got_labels[:, 2:]
     near_index = got_labels[:, 0]
     far_index = got_labels[:, 1]
     link_tile = link_tiles[0]
@@ -110,7 +118,7 @@
     residual = rhs
     preconditioned = scale * residual
     direction = preconditioned
-    res_dot = total(jnp.sum(residual * preconditioned, axis=(0, 2)))
+    res_dot = jnp.sum(residual * preconditioned, axis=(0, 2))
     for step in range(ITERS):
         image = apply_operator(
             direction,
@@ -122,7 +130,12 @@
             near_index,
             far_index,
         )
-        curve = total(jnp.sum(direction * image, axis=(0, 2)))
+        curve = jnp.sum(direction * image, axis=(0, 2))
+        if step == 0:
+            both = total(jnp.stack([res_dot, curve]))
+            res_dot, curve = both[0], both[1]
+        else:
+            curve = total(curve)
         alpha = res_dot / curve
         solution = solution + alpha[None, :, None] * direction
         residual = residual - alpha[None, :, None] * image

time: 166 us -> 173 us (1.042)
  waiting for transfers between devices: 33.4 us -> 18.8 us
  other arithmetic: 3.64 us -> 14.7 us
  matrix products: 17.6 us -> 25.7 us
  local copies, waits for them, and re-layouts: 18.9 us -> 22.7 us
  starting transfers between devices: 26.7 us -> 22.9 us
    all_to_all x3 -> x1, waiting for transfers between devices: 19.2 us -> 0.01 us  [body(): lax.all_to_all(payload.reshape(groups, CAP, B + 16, B), 'rep', split_axis...]
    ppermute x8, waiting for transfers between devices: 3.36 us -> 9.59 us  [from_behind(): return lax.ppermute(value, axis, pairs)]
    all_to_all x3 -> x1, starting transfers between devices: 10.3 us -> 4.35 us  [body(): lax.all_to_all(payload.reshape(groups, CAP, B + 16, B), 'rep', split_axis...]
    scatter x3 -> x0, local copies, waits for them, and re-layouts: 4.75 us -> none  [the longest x1 2.75 us: body(): jnp.zeros((groups, CAP, B, B), jnp.bfloat16).at[target, rank]]
    gather x8, local copies, waits for them, and re-layouts: 7.96 us -> 12.1 us  [contact_pairs(): difference = (vector[near_index] - other[far_index]).astype(jnp.bfloat16)]
    convert_element_type x4, other arithmetic: 0.05 us -> 3.23 us  [apply_operator(): other = partner(vector.astype(jnp.bfloat16), 'dom', 0).astype(vector.dtype)]
    dot_general x4, matrix products: 0.82 us -> 3.65 us  [local_stiffness(): jnp.einsum('nmrk,nmkj->nrj', picked, off_tiles, preferred_element_type=jn...]
    ppermute x8, starting transfers between devices: 9.26 us -> 11.4 us  [partner(): lax.ppermute(value, axis, [(i, i ^ 1 << distance) for i in range(lax.axis...]
  transfers between devices with their start and end apart: 19 -> 17, of which waited for: 9 -> 8; matrix products, arithmetic and copies ran while one was open for 11% -> 14% of each run, Pallas kernels for 0% -> 0%
where the time goes in v2:
time: 173 us; the launch traced here: 172 us
  blocking collectives  65.8 us (38%)
  matrix products  25.7 us (15%)
  starting transfers between devices  22.9 us (13%)
  local copies, waits for them, and re-layouts  22.7 us (13%)
  waiting for transfers between devices  18.8 us (11%)
  other arithmetic  14.7 us (8%)
    all_to_all x7, blocking collectives, total(): gathered = lax.all_to_all(spread, ('dom', 'rep'), 0, 0, tiled=True)  65.8 us
    gather x8, local copies, waits for them, and re-layouts, contact_pairs(): difference = (vector[near_index] - other[far_index]).astype(jnp.bfloat16)  12.1 us
    ppermute x8, starting transfers between devices, partner(): lax.ppermute(value, axis, [(i, i ^ 1 << distance) for i in range(lax.axis...  11.4 us
    ppermute x8, waiting for transfers between devices, from_behind(): return lax.ppermute(value, axis, pairs)  9.59 us
    ppermute x8, waiting for transfers between devices, partner(): lax.ppermute(value, axis, [(i, i ^ 1 << distance) for i in range(lax.axis...  9.17 us
    dot_general x4, matrix products, contact_pairs(): jnp.einsum('srj,skj->srk', multiplier, contact_set, preferred_element_typ...  8.16 us
    ppermute x8, starting transfers between devices, from_behind(): return lax.ppermute(value, axis, pairs)  7.14 us
    dot_general x8, matrix products, collect(): jnp.einsum('sn,srk->nrk', onehot, values, precision=lax.Precision.HIGHEST)  5.95 us
  transfers between devices with their start and end apart: 17, of which 8 were waited for; matrix products, arithmetic and copies ran while one was open for 14% of the time, Pallas kernels for 0%

profile of v2, /device:TPU:0, one launch (start us, length us, event | category | flops | bytes accessed | tf_op | source)
XLA Modules:
  0.0 171.8 jit_solution(6354477979059569939)
XLA Ops:
  6.0 4.4 %all-to-all-start = ((bf16[4,8,144,128]{3,1,2,0:T(8,128)(2,1)}), bf16[4,8,144,128]{3,1,2,0:T(8,128)(2,1)S(1)}, u32[]{:S(2)}, u32[]{:S(2)}) async-start(bf16[4,8,144,128]{3,1,2,0:T(8,128)(2,1)} %copy.223), calls=%async_computation | async-start | bytes 2359296 | tf_op jit(solution)/shard_map/all_to_all | solution.py:107
  11.1 2.3 %collective-permute-start.2 = (bf16[8,32,128]{2,1,0:T(8,128)(2,1)S(1)}, bf16[8,32,128]{2,1,0:T(8,128)(2,1)S(1)}, u32[]{:S(2)}, u32[]{:S(2)}) collective-permute-start(bf16[8,32,128]{2,1,0:T(8,128)(2,1)S(1)} %get-tuple-element.124), channel_id=1, source_target_pairs={{0,4},{4,0},{8,12},{12,8},{16,20},{20,16},{24,28},{28,24},{1,5},{5... | collective-permute-start | bytes 196616 | tf_op jit(solution)/shard_map/ppermute | solution.py:18
  13.7 1.6 collective-permute-start.1
  17.3 8.4 %collective-permute-done = bf16[32,128]{1,0:T(8,128)(2,1)S(1)} collective-permute-done((bf16[32,128]{1,0:T(8,128)(2,1)S(1)}, bf16[32,128]{1,0:T(8,128)(2,1)S(1)}, u32[]{:S(2)}, u32[]{:S(2)}) %collective-permute-start) | collective-permute-done | bytes 8224 | tf_op jit(solution)/shard_map/ppermute | solution.py:14
  28.9 2.3 %gather_fusion.1 = f32[32,32,128]{2,1,0:T(8,128)} fusion(f32[8,32,128]{2,1,0:T(8,128)} %get-tuple-element.125, s32[1024]{0:T(1024)S(1)} %get-tuple-element.135), kind=kCustom, calls=%fused_computation.1 | custom fusion | bytes 1048704 | tf_op jit(solution)/shard_map/gather | solution.py:43
  31.2 2.0 %fusion.3 = f32[32,32,128]{2,1,0:T(8,128)S(1)} fusion(bf16[32,144,128]{2,1,0:T(8,128)(2,1)S(1)} %bitcast.212, f32[32,32,128]{2,1,0:T(8,128)} %gather_fusion.1, f32[32,32,128]{2,1,0:T(8,128)S(1)} %gather_fusion.2), kind=kOutput, calls=%fused_computation.21 | convolution fusion | flops 67502080 | bytes 3670016 | tf_op jit(solution)/shard_map/srj,skj->srk/dot_general | solution.py:47
  34.4 2.6 %collective-permute-start.3 = (bf16[8,32,128]{2,1,0:T(8,128)(2,1)S(1)}, bf16[8,32,128]{2,1,0:T(8,128)(2,1)S(1)}, u32[]{:S(2)}, u32[]{:S(2)}) collective-permute-start(bf16[8,32,128]{2,1,0:T(8,128)(2,1)S(1)} %copy.332), channel_id=1, source_target_pairs={{0,4},{4,0},{8,12},{12,8},{16,20},{20,16},{24,28},{28,24},{1,5},{5... | collective-permute-start | bytes 196616 | tf_op jit(solution)/shard_map/ppermute | solution.py:18
  37.6 2.0 %collective-permute-done.3 = bf16[8,32,128]{2,1,0:T(8,128)(2,1)S(1)} collective-permute-done((bf16[8,32,128]{2,1,0:T(8,128)(2,1)S(1)}, bf16[8,32,128]{2,1,0:T(8,128)(2,1)S(1)}, u32[]{:S(2)}, u32[]{:S(2)}) %collective-permute-start.3) | collective-permute-done | bytes 65568 | tf_op jit(solution)/shard_map/ppermute | solution.py:18
  39.8 12.2 %all_to_all.46 = f32[32,2,32]{2,1,0:T(2,128)S(1)} all-to-all(f32[32,2,32]{2,1,0:T(2,128)S(1)} %broadcast_in_dim.17), channel_id=1, replica_groups=mesh['dom'=8,'rep'=4] {'dom','rep'}, dimensions={0} | all-to-all | bytes 16384 | tf_op jit(solution)/shard_map/all_to_all | solution.py:24
  52.3 8.8 %all_to_all.47 = f32[32,1,32]{2,1,0:T(1,128)S(1)} all-to-all(f32[32,1,32]{2,1,0:T(1,128)S(1)} %broadcast_in_dim.18), channel_id=1, replica_groups=mesh['dom'=8,'rep'=4] {'dom','rep'}, dimensions={0} | all-to-all | bytes 8192 | tf_op jit(solution)/shard_map/all_to_all | solution.py:24
  66.8 1.7 %collective-permute-start.5 = (f32[32,128]{1,0:T(8,128)S(1)}, f32[32,128]{1,0:T(8,128)S(1)}, u32[]{:S(2)}, u32[]{:S(2)}) collective-permute-start(f32[32,128]{1,0:T(8,128)S(1)} %fusion.78), channel_id=1, source_target_pairs={{0,3},{1,0},{2,1},{3,2},{4,7},{5,4},{6,5},{7,6},{8,11},{9,8},{10,9... | collective-permute-start | bytes 49160 | tf_op jit(solution)/shard_map/ppermute | solution.py:14
  73.2 2.1 %fusion.4 = f32[32,32,128]{2,1,0:T(8,128)S(1)} fusion(bf16[32,144,128]{2,1,0:T(8,128)(2,1)S(1)} %bitcast.213, f32[32,32,128]{2,1,0:T(8,128)} %gather_fusion.4, f32[32,32,128]{2,1,0:T(8,128)} %gather_fusion.5), kind=kOutput, calls=%fused_computation.22 | convolution fusion | flops 67502080 | bytes 3670016 | tf_op jit(solution)/shard_map/srj,skj->srk/dot_general | solution.py:47
  78.1 2.4 %collective-permute-done.7 = bf16[8,32,128]{2,1,0:T(8,128)(2,1)S(1)} collective-permute-done((bf16[8,32,128]{2,1,0:T(8,128)(2,1)S(1)}, bf16[8,32,128]{2,1,0:T(8,128)(2,1)S(1)}, u32[]{:S(2)}, u32[]{:S(2)}) %collective-permute-start.7) | collective-permute-done | bytes 65568 | tf_op jit(solution)/shard_map/ppermute | solution.py:18
  80.7 9.0 %all_to_all.48 = f32[32,1,32]{2,1,0:T(1,128)S(1)} all-to-all(f32[32,1,32]{2,1,0:T(1,128)S(1)} %broadcast_in_dim.19), channel_id=1, replica_groups=mesh['dom'=8,'rep'=4] {'dom','rep'}, dimensions={0} | all-to-all | bytes 8192 | tf_op jit(solution)/shard_map/all_to_all | solution.py:24
  91.6 8.8 %all_to_all.49 = f32[32,1,32]{2,1,0:T(1,128)S(1)} all-to-all(f32[32,1,32]{2,1,0:T(1,128)S(1)} %broadcast_in_dim.20), channel_id=1, replica_groups=mesh['dom'=8,'rep'=4] {'dom','rep'}, dimensions={0} | all-to-all | bytes 8192 | tf_op jit(solution)/shard_map/all_to_all | solution.py:24
  106.9 1.7 %collective-permute-start.9 = (f32[32,128]{1,0:T(8,128)S(1)}, f32[32,128]{1,0:T(8,128)S(1)}, u32[]{:S(2)}, u32[]{:S(2)}) collective-permute-start(f32[32,128]{1,0:T(8,128)S(1)} %fusion.75), channel_id=1, source_target_pairs={{0,3},{1,0},{2,1},{3,2},{4,7},{5,4},{6,5},{7,6},{8,11},{9,8},{10,9... | collective-permute-start | bytes 49160 | tf_op jit(solution)/shard_map/ppermute | solution.py:14
  113.3 2.1 %fusion.5 = f32[32,32,128]{2,1,0:T(8,128)S(1)} fusion(bf16[32,144,128]{2,1,0:T(8,128)(2,1)S(1)} %bitcast.214, f32[32,32,128]{2,1,0:T(8,128)} %gather_fusion.7, f32[32,32,128]{2,1,0:T(8,128)} %gather_fusion.8), kind=kOutput, calls=%fused_computation.23 | convolution fusion | flops 67502080 | bytes 3670016 | tf_op jit(solution)/shard_map/srj,skj->srk/dot_general | solution.py:47
  118.9 2.4 %collective-permute-done.11 = bf16[8,32,128]{2,1,0:T(8,128)(2,1)S(1)} collective-permute-done((bf16[8,32,128]{2,1,0:T(8,128)(2,1)S(1)}, bf16[8,32,128]{2,1,0:T(8,128)(2,1)S(1)}, u32[]{:S(2)}, u32[]{:S(2)}) %collective-permute-start.11) | collective-permute-done | bytes 65568 | tf_op jit(solution)/shard_map/ppermute | solution.py:18
  121.9 9.0 %all_to_all.50 = f32[32,1,32]{2,1,0:T(1,128)S(1)} all-to-all(f32[32,1,32]{2,1,0:T(1,128)S(1)} %broadcast_in_dim.21), channel_id=1, replica_groups=mesh['dom'=8,'rep'=4] {'dom','rep'}, dimensions={0} | all-to-all | bytes 8192 | tf_op jit(solution)/shard_map/all_to_all | solution.py:24
  132.8 8.8 %all_to_all.51 = f32[32,1,32]{2,1,0:T(1,128)S(1)} all-to-all(f32[32,1,32]{2,1,0:T(1,128)S(1)} %broadcast_in_dim.22), channel_id=1, replica_groups=mesh['dom'=8,'rep'=4] {'dom','rep'}, dimensions={0} | all-to-all | bytes 8192 | tf_op jit(solution)/shard_map/all_to_all | solution.py:24
  148.8 1.7 %collective-permute-start.13 = (f32[32,128]{1,0:T(8,128)S(1)}, f32[32,128]{1,0:T(8,128)S(1)}, u32[]{:S(2)}, u32[]{:S(2)}) collective-permute-start(f32[32,128]{1,0:T(8,128)S(1)} %fusion.72), channel_id=1, source_target_pairs={{0,3},{1,0},{2,1},{3,2},{4,7},{5,4},{6,5},{7,6},{8,11},{9,8},{10,9... | collective-permute-start | bytes 49160 | tf_op jit(solution)/shard_map/ppermute | solution.py:14
  154.6 2.0 %fusion.6 = f32[32,32,128]{2,1,0:T(8,128)S(1)} fusion(bf16[32,144,128]{2,1,0:T(8,128)(2,1)S(1)} %bitcast.215, f32[32,32,128]{2,1,0:T(8,128)S(1)} %gather_fusion.10, f32[32,32,128]{2,1,0:T(8,128)} %gather_fusion.11), kind=kOutput, calls=%fused_computation.24 | convolution fusion | flops 67502080 | bytes 3670016 | tf_op jit(solution)/shard_map/srj,skj->srk/dot_general | solution.py:47
  159.4 2.4 %collective-permute-done.15 = bf16[8,32,128]{2,1,0:T(8,128)(2,1)S(1)} collective-permute-done((bf16[8,32,128]{2,1,0:T(8,128)(2,1)S(1)}, bf16[8,32,128]{2,1,0:T(8,128)(2,1)S(1)}, u32[]{:S(2)}, u32[]{:S(2)}) %collective-permute-start.15) | collective-permute-done | bytes 65568 | tf_op jit(solution)/shard_map/ppermute | solution.py:18
  161.9 9.0 %all_to_all.52 = f32[32,1,32]{2,1,0:T(1,128)S(1)} all-to-all(f32[32,1,32]{2,1,0:T(1,128)S(1)} %broadcast_in_dim.23), channel_id=1, replica_groups=mesh['dom'=8,'rep'=4] {'dom','rep'}, dimensions={0} | all-to-all | bytes 8192 | tf_op jit(solution)/shard_map/all_to_all | solution.py:24
  (212 shorter events, 60.7 us)
Async XLA Ops:
  6.0 20.5 %all-to-all-start = ((bf16[4,8,144,128]{3,1,2,0:T(8,128)(2,1)}), bf16[4,8,144,128]{3,1,2,0:T(8,128)(2,1)S(1)}, u32[]{:S(2)}, u32[]{:S(2)}) async-start(bf16[4,8,144,128]{3,1,2,0:T(8,128)(2,1)} %copy.223), calls=%async_computation | async-start | bytes 2359296 | tf_op jit(solution)/shard_map/all_to_all | solution.py:107
  11.1 14.8 %collective-permute-start.2 = (bf16[8,32,128]{2,1,0:T(8,128)(2,1)S(1)}, bf16[8,32,128]{2,1,0:T(8,128)(2,1)S(1)}, u32[]{:S(2)}, u32[]{:S(2)}) collective-permute-start(bf16[8,32,128]{2,1,0:T(8,128)(2,1)S(1)} %get-tuple-element.124), channel_id=1, source_target_pairs={{0,4},{4,0},{8,12},{12,8},{16,20},{20,16},{24,28},{28,24},{1,5},{5... | collective-permute-start | bytes 196616 | tf_op jit(solution)/shard_map/ppermute | solution.py:18
  13.4 12.3 %collective-permute-start = (bf16[32,128]{1,0:T(8,128)(2,1)S(1)}, bf16[32,128]{1,0:T(8,128)(2,1)S(1)}, u32[]{:S(2)}, u32[]{:S(2)}) collective-permute-start(bf16[32,128]{1,0:T(8,128)(2,1)S(1)} %slice_bitcast_fusion.11), channel_id=1, source_target_pairs={{0,1},{1,2},{2,3},{3,0},{4,5},{5,6},{6,7},{7,4},{8,9},{9,10},{10,1... | collective-permute-start | bytes 24584 | tf_op jit(solution)/shard_map/ppermute | solution.py:14
  13.7 12.1 %collective-permute-start.1 = (f32[32,128]{1,0:T(8,128)S(1)}, f32[32,128]{1,0:T(8,128)S(1)}, u32[]{:S(2)}, u32[]{:S(2)}) collective-permute-start(f32[32,128]{1,0:T(8,128)S(1)} %fusion.81), channel_id=1, source_target_pairs={{0,3},{1,0},{2,1},{3,2},{4,7},{5,4},{6,5},{7,6},{8,11},{9,8},{10,9... | collective-permute-start | bytes 49160 | tf_op jit(solution)/shard_map/ppermute | solution.py:14
  34.4 5.2 %collective-permute-start.3 = (bf16[8,32,128]{2,1,0:T(8,128)(2,1)S(1)}, bf16[8,32,128]{2,1,0:T(8,128)(2,1)S(1)}, u32[]{:S(2)}, u32[]{:S(2)}) collective-permute-start(bf16[8,32,128]{2,1,0:T(8,128)(2,1)S(1)} %copy.332), channel_id=1, source_target_pairs={{0,4},{4,0},{8,12},{12,8},{16,20},{20,16},{24,28},{28,24},{1,5},{5... | collective-permute-start | bytes 196616 | tf_op jit(solution)/shard_map/ppermute | solution.py:18
  39.8 24.2 %copy-start.3 = (bf16[8,128,128]{2,1,0:T(8,128)(2,1)S(1)}, bf16[8,128,128]{2,1,0:T(8,128)(2,1)}, u32[]{:S(2)}) copy-start(bf16[8,128,128]{2,1,0:T(8,128)(2,1)} %param.30) | copy-start | bytes 786436
  61.8 9.1 %collective-permute-start.6 = (bf16[8,32,128]{2,1,0:T(8,128)(2,1)S(1)}, bf16[8,32,128]{2,1,0:T(8,128)(2,1)}, u32[]{:S(2)}, u32[]{:S(2)}) collective-permute-start(bf16[8,32,128]{2,1,0:T(8,128)(2,1)S(1)} %get-tuple-element.120), channel_id=1, source_target_pairs={{0,4},{4,0},{8,12},{12,8},{16,20},{20,16},{24,28},{28,24},{1,5},{5... | collective-permute-start | bytes 196616 | tf_op jit(solution)/shard_map/ppermute | solution.py:18
  66.7 3.3 %collective-permute-start.4 = (bf16[32,128]{1,0:T(8,128)(2,1)}, bf16[32,128]{1,0:T(8,128)(2,1)S(1)}, u32[]{:S(2)}, u32[]{:S(2)}) collective-permute-start(bf16[32,128]{1,0:T(8,128)(2,1)} %slice_bitcast_fusion.8), channel_id=1, source_target_pairs={{0,1},{1,2},{2,3},{3,0},{4,5},{5,6},{6,7},{7,4},{8,9},{9,10},{10,1... | collective-permute-start | bytes 24584 | tf_op jit(solution)/shard_map/ppermute | solution.py:14
  66.8 3.4 %collective-permute-start.5 = (f32[32,128]{1,0:T(8,128)S(1)}, f32[32,128]{1,0:T(8,128)S(1)}, u32[]{:S(2)}, u32[]{:S(2)}) collective-permute-start(f32[32,128]{1,0:T(8,128)S(1)} %fusion.78), channel_id=1, source_target_pairs={{0,3},{1,0},{2,1},{3,2},{4,7},{5,4},{6,5},{7,6},{8,11},{9,8},{10,9... | collective-permute-start | bytes 49160 | tf_op jit(solution)/shard_map/ppermute | solution.py:14
  76.0 4.5 %collective-permute-start.7 = (bf16[8,32,128]{2,1,0:T(8,128)(2,1)S(1)}, bf16[8,32,128]{2,1,0:T(8,128)(2,1)S(1)}, u32[]{:S(2)}, u32[]{:S(2)}) collective-permute-start(bf16[8,32,128]{2,1,0:T(8,128)(2,1)S(1)} %copy.331), channel_id=1, source_target_pairs={{0,4},{4,0},{8,12},{12,8},{16,20},{20,16},{24,28},{28,24},{1,5},{5... | collective-permute-start | bytes 196616 | tf_op jit(solution)/shard_map/ppermute | solution.py:18
  91.6 14.9 %copy-start.16 = (f32[8,32,128]{2,1,0:T(8,128)}, f32[8,32,128]{2,1,0:T(8,128)S(1)}, u32[]{:S(2)}) copy-start(f32[8,32,128]{2,1,0:T(8,128)S(1)} %get-tuple-element.119) | copy-start | bytes 393220
  101.2 9.7 %collective-permute-start.10 = (bf16[8,32,128]{2,1,0:T(8,128)(2,1)S(1)}, bf16[8,32,128]{2,1,0:T(8,128)(2,1)}, u32[]{:S(2)}, u32[]{:S(2)}) collective-permute-start(bf16[8,32,128]{2,1,0:T(8,128)(2,1)S(1)} %get-tuple-element.116), channel_id=1, source_target_pairs={{0,4},{4,0},{8,12},{12,8},{16,20},{20,16},{24,28},{28,24},{1,5},{5... | collective-permute-start | bytes 196616 | tf_op jit(solution)/shard_map/ppermute | solution.py:18
  106.8 3.3 %collective-permute-start.8 = (bf16[32,128]{1,0:T(8,128)(2,1)}, bf16[32,128]{1,0:T(8,128)(2,1)S(1)}, u32[]{:S(2)}, u32[]{:S(2)}) collective-permute-start(bf16[32,128]{1,0:T(8,128)(2,1)} %slice_bitcast_fusion.5), channel_id=1, source_target_pairs={{0,1},{1,2},{2,3},{3,0},{4,5},{5,6},{6,7},{7,4},{8,9},{9,10},{10,1... | collective-permute-start | bytes 24584 | tf_op jit(solution)/shard_map/ppermute | solution.py:14
  106.9 3.4 %collective-permute-start.9 = (f32[32,128]{1,0:T(8,128)S(1)}, f32[32,128]{1,0:T(8,128)S(1)}, u32[]{:S(2)}, u32[]{:S(2)}) collective-permute-start(f32[32,128]{1,0:T(8,128)S(1)} %fusion.75), channel_id=1, source_target_pairs={{0,3},{1,0},{2,1},{3,2},{4,7},{5,4},{6,5},{7,6},{8,11},{9,8},{10,9... | collective-permute-start | bytes 49160 | tf_op jit(solution)/shard_map/ppermute | solution.py:14
  116.7 4.5 %collective-permute-start.11 = (bf16[8,32,128]{2,1,0:T(8,128)(2,1)S(1)}, bf16[8,32,128]{2,1,0:T(8,128)(2,1)S(1)}, u32[]{:S(2)}, u32[]{:S(2)}) collective-permute-start(bf16[8,32,128]{2,1,0:T(8,128)(2,1)S(1)} %copy.330), channel_id=1, source_target_pairs={{0,4},{4,0},{8,12},{12,8},{16,20},{20,16},{24,28},{28,24},{1,5},{5... | collective-permute-start | bytes 196616 | tf_op jit(solution)/shard_map/ppermute | solution.py:18
  142.3 9.9 %collective-permute-start.14 = (bf16[8,32,128]{2,1,0:T(8,128)(2,1)S(1)}, bf16[8,32,128]{2,1,0:T(8,128)(2,1)}, u32[]{:S(2)}, u32[]{:S(2)}) collective-permute-start(bf16[8,32,128]{2,1,0:T(8,128)(2,1)S(1)} %get-tuple-element.112), channel_id=1, source_target_pairs={{0,4},{4,0},{8,12},{12,8},{16,20},{20,16},{24,28},{28,24},{1,5},{5... | collective-permute-start | bytes 196616 | tf_op jit(solution)/shard_map/ppermute | solution.py:18
  148.7 3.3 %collective-permute-start.12 = (bf16[32,128]{1,0:T(8,128)(2,1)}, bf16[32,128]{1,0:T(8,128)(2,1)S(1)}, u32[]{:S(2)}, u32[]{:S(2)}) collective-permute-start(bf16[32,128]{1,0:T(8,128)(2,1)} %slice_bitcast_fusion.2), channel_id=1, source_target_pairs={{0,1},{1,2},{2,3},{3,0},{4,5},{5,6},{6,7},{7,4},{8,9},{9,10},{10,1... | collective-permute-start | bytes 24584 | tf_op jit(solution)/shard_map/ppermute | solution.py:14
  148.8 3.4 %collective-permute-start.13 = (f32[32,128]{1,0:T(8,128)S(1)}, f32[32,128]{1,0:T(8,128)S(1)}, u32[]{:S(2)}, u32[]{:S(2)}) collective-permute-start(f32[32,128]{1,0:T(8,128)S(1)} %fusion.72), channel_id=1, source_target_pairs={{0,3},{1,0},{2,1},{3,2},{4,7},{5,4},{6,5},{7,6},{8,11},{9,8},{10,9... | collective-permute-start | bytes 49160 | tf_op jit(solution)/shard_map/ppermute | solution.py:14
  156.6 14.4 %copy-start.36 = (f32[32]{0:T(128)S(1)}, f32[32]{0:T(128)}, u32[]{:S(2)}) copy-start(f32[32]{0:T(128)} %copy-done.35) | copy-start | bytes 388
  156.6 14.4 %copy-start.15 = (f32[8,32,128]{2,1,0:T(8,128)S(1)}, f32[8,32,128]{2,1,0:T(8,128)}, u32[]{:S(2)}) copy-start(f32[8,32,128]{2,1,0:T(8,128)} %copy-done.14) | copy-start | bytes 393220
  156.6 14.4 %copy-start.28 = (f32[32]{0:T(128)S(1)}, f32[32]{0:T(128)}, u32[]{:S(2)}) copy-start(f32[32]{0:T(128)} %copy-done.27) | copy-start | bytes 388
  156.6 14.4 %copy-start.30 = (f32[32]{0:T(128)S(1)}, f32[32]{0:T(128)}, u32[]{:S(2)}) copy-start(f32[32]{0:T(128)} %copy-done.29) | copy-start | bytes 388
  156.6 14.4 %copy-start.32 = (f32[32]{0:T(128)S(1)}, f32[32]{0:T(128)}, u32[]{:S(2)}) copy-start(f32[32]{0:T(128)} %copy-done.31) | copy-start | bytes 388
  157.2 4.5 %collective-permute-start.15 = (bf16[8,32,128]{2,1,0:T(8,128)(2,1)S(1)}, bf16[8,32,128]{2,1,0:T(8,128)(2,1)S(1)}, u32[]{:S(2)}, u32[]{:S(2)}) collective-permute-start(bf16[8,32,128]{2,1,0:T(8,128)(2,1)S(1)} %copy.329), channel_id=1, source_target_pairs={{0,4},{4,0},{8,12},{12,8},{16,20},{20,16},{24,28},{28,24},{1,5},{5... | collective-permute-start | bytes 196616 | tf_op jit(solution)/shard_map/ppermute | solution.py:18
  (30 other events, 170.7 us)

commit v3 on v1

--- a/solution.py
+++ b/solution.py
@@ -110,7 +110,7 @@
     residual = rhs
     preconditioned = scale * residual
     direction = preconditioned
-    res_dot = total(jnp.sum(residual * preconditioned, axis=(0, 2)))
+    res_dot = jnp.sum(residual * preconditioned, axis=(0, 2))
     for step in range(ITERS):
         image = apply_operator(
             direction,
@@ -122,7 +122,12 @@
             near_index,
             far_index,
         )
-        curve = total(jnp.sum(direction * image, axis=(0, 2)))
+        curve = jnp.sum(direction * image, axis=(0, 2))
+        if step == 0:
+            both = total(jnp.stack([res_dot, curve]))
+            res_dot, curve = both[0], both[1]
+        else:
+            curve = total(curve)
         alpha = res_dot / curve
         solution = solution + alpha[None, :, None] * direction
         residual = residual - alpha[None, :, None] * image

time: 166 us -> 157 us (0.946)
  waiting for transfers between devices: 33.4 us -> 26.4 us
  starting transfers between devices: 26.7 us -> 24.1 us
    all_to_all x1 -> x0, waiting for transfers between devices: 7.05 us -> none  [total(): gathered = lax.all_to_all(spread, ('dom', 'rep'), 0, 0, tiled=True)]
    all_to_all x1 -> x0, starting transfers between devices: 2.54 us -> none  [total(): gathered = lax.all_to_all(spread, ('dom', 'rep'), 0, 0, tiled=True)]
  transfers between devices with their start and end apart: 19 -> 18, of which waited for: 9 -> 8; matrix products, arithmetic and copies ran while one was open for 11% -> 12% of each run, Pallas kernels for 0% -> 0%
where the time goes in v3:
time: 157 us; the launch traced here: 156 us
  blocking collectives  64.1 us (41%)
  waiting for transfers between devices  26.4 us (17%)
  starting transfers between devices  24.1 us (15%)
  local copies, waits for them, and re-layouts  19 us (12%)
  matrix products  17.6 us (11%)
  other arithmetic  3.66 us (2%)
    all_to_all x7, blocking collectives, total(): gathered = lax.all_to_all(spread, ('dom', 'rep'), 0, 0, tiled=True)  64.1 us
    all_to_all x1, waiting for transfers between devices, body(): lax.all_to_all(send_set, 'rep', split_axis=0, concat_axis=0, tiled=True)  12.1 us
    ppermute x8, waiting for transfers between devices, partner(): lax.ppermute(value, axis, [(i, i ^ 1 << distance) for i in range(lax.axis...  10.9 us
    ppermute x8, starting transfers between devices, partner(): lax.ppermute(value, axis, [(i, i ^ 1 << distance) for i in range(lax.axis...  9.27 us
    gather x8, local copies, waits for them, and re-layouts, contact_pairs(): difference = (vector[near_index] - other[far_index]).astype(jnp.bfloat16)  7.96 us
    dot_general x4, matrix products, contact_pairs(): jnp.einsum('srj,skj->srk', multiplier, contact_set, preferred_element_typ...  7.84 us
    ppermute x8, starting transfers between devices, from_behind(): return lax.ppermute(value, axis, pairs)  7.14 us
    dot_general x8, matrix products, collect(): jnp.einsum('sn,srk->nrk', onehot, values, precision=lax.Precision.HIGHEST)  4.68 us
  transfers between devices with their start and end apart: 18, of which 8 were waited for; matrix products, arithmetic and copies ran while one was open for 12% of the time, Pallas kernels for 0%

profile of v3, /device:TPU:0, one launch (start us, length us, event | category | flops | bytes accessed | tf_op | source)
XLA Modules:
  0.0 156.1 jit_solution(12840186666000069758)
XLA Ops:
  4.4 4.2 %all-to-all-start = ((s32[4,8,2]{1,2,0:T(2,128)}), s32[4,8,2]{1,2,0:T(2,128)S(1)}, u32[]{:S(2)}, u32[]{:S(2)}) async-start(s32[4,8,2]{1,2,0:T(2,128)} %copy.129), calls=%async_computation | async-start | bytes 8192 | tf_op jit(solution)/shard_map/all_to_all | solution.py:100
  8.7 2.1 %collective-permute-start.2 = (bf16[8,32,128]{2,1,0:T(8,128)(2,1)S(1)}, bf16[8,32,128]{2,1,0:T(8,128)(2,1)S(1)}, u32[]{:S(2)}, u32[]{:S(2)}) collective-permute-start(bf16[8,32,128]{2,1,0:T(8,128)(2,1)S(1)} %get-tuple-element.112), channel_id=1, source_target_pairs={{0,4},{4,0},{8,12},{12,8},{16,20},{20,16},{24,28},{28,24},{1,5},{5... | collective-permute-start | bytes 196616 | tf_op jit(solution)/shard_map/ppermute | solution.py:18
  11.1 1.6 %collective-permute-start.1 = (f32[32,128]{1,0:T(8,128)S(1)}, f32[32,128]{1,0:T(8,128)S(1)}, u32[]{:S(2)}, u32[]{:S(2)}) collective-permute-start(f32[32,128]{1,0:T(8,128)S(1)} %fusion.68), channel_id=1, source_target_pairs={{0,3},{1,0},{2,1},{3,2},{4,7},{5,4},{6,5},{7,6},{8,11},{9,8},{10,9... | collective-permute-start | bytes 49160 | tf_op jit(solution)/shard_map/ppermute | solution.py:14
  15.9 2.8 %scatter_fusion.1 = bf16[4,8,128,128]{3,2,1,0:T(8,128)(2,1)} fusion(bf16[4,8,128,128]{3,2,1,0:T(8,128)(2,1)} %broadcast_in_dim.22, s32[16]{0:T(128)S(1)} %fusion.107, bf16[16,128,128]{2,1,0:T(8,128)(2,1)S(1)} %copy-done.8), kind=kCustom, calls=%fused_computation.13 | custom fusion | bytes 1572992 | tf_op jit(solution)/shard_map/scatter | solution.py:95
  18.7 3.5 %all-to-all-start.1 = ((bf16[4,8,128,128]{3,2,1,0:T(8,128)(2,1)}), bf16[4,8,128,128]{3,2,1,0:T(8,128)(2,1)S(1)}, u32[]{:S(2)}, u32[]{:S(2)}) async-start(bf16[4,8,128,128]{3,2,1,0:T(8,128)(2,1)} %scatter_fusion.1), calls=%async_computation.1 | async-start | bytes 2097152 | tf_op jit(solution)/shard_map/all_to_all | solution.py:99
  24.5 12.1 %all-to-all-done.1 = bf16[4,8,128,128]{3,2,1,0:T(8,128)(2,1)S(1)} async-done(((bf16[4,8,128,128]{3,2,1,0:T(8,128)(2,1)}), bf16[4,8,128,128]{3,2,1,0:T(8,128)(2,1)S(1)}, u32[]{:S(2)}, u32[]{:S(2)}) %all-to-all-start.1) | async-done | bytes 1048608 | tf_op jit(solution)/shard_map/all_to_all | solution.py:99
  36.6 2.0 %fusion = f32[32,32,128]{2,1,0:T(8,128)S(1)} fusion(bf16[32,128,128]{2,1,0:T(8,128)(2,1)S(1)} %bitcast.216, f32[32,32,128]{2,1,0:T(8,128)S(1)} %gather_fusion.1, f32[32,32,128]{2,1,0:T(8,128)} %gather_fusion.2), kind=kOutput, calls=%fused_computation.18 | convolution fusion | flops 67502080 | bytes 2621440 | tf_op jit(solution)/shard_map/srj,skj->srk/dot_general | solution.py:47
  40.5 3.0 %collective-permute-done.3 = bf16[8,32,128]{2,1,0:T(8,128)(2,1)S(1)} collective-permute-done((bf16[8,32,128]{2,1,0:T(8,128)(2,1)S(1)}, bf16[8,32,128]{2,1,0:T(8,128)(2,1)S(1)}, u32[]{:S(2)}, u32[]{:S(2)}) %collective-permute-start.3) | collective-permute-done | bytes 65568 | tf_op jit(solution)/shard_map/ppermute | solution.py:18
  43.7 11.1 %all_to_all.51 = f32[32,2,32]{2,1,0:T(2,128)S(1)} all-to-all(f32[32,2,32]{2,1,0:T(2,128)S(1)} %broadcast_in_dim.23), channel_id=1, replica_groups=mesh['dom'=8,'rep'=4] {'dom','rep'}, dimensions={0} | all-to-all | bytes 16384 | tf_op jit(solution)/shard_map/all_to_all | solution.py:24
  55.1 8.8 %all_to_all.52 = f32[32,1,32]{2,1,0:T(1,128)S(1)} all-to-all(f32[32,1,32]{2,1,0:T(1,128)S(1)} %broadcast_in_dim.24), channel_id=1, replica_groups=mesh['dom'=8,'rep'=4] {'dom','rep'}, dimensions={0} | all-to-all | bytes 8192 | tf_op jit(solution)/shard_map/all_to_all | solution.py:24
  67.6 1.7 %collective-permute-start.5 = (f32[32,128]{1,0:T(8,128)S(1)}, f32[32,128]{1,0:T(8,128)S(1)}, u32[]{:S(2)}, u32[]{:S(2)}) collective-permute-start(f32[32,128]{1,0:T(8,128)S(1)} %fusion.65), channel_id=1, source_target_pairs={{0,3},{1,0},{2,1},{3,2},{4,7},{5,4},{6,5},{7,6},{8,11},{9,8},{10,9... | collective-permute-start | bytes 49160 | tf_op jit(solution)/shard_map/ppermute | solution.py:14
  72.2 2.0 %fusion.1 = f32[32,32,128]{2,1,0:T(8,128)S(1)} fusion(bf16[32,128,128]{2,1,0:T(8,128)(2,1)S(1)} %bitcast.217, f32[32,32,128]{2,1,0:T(8,128)S(1)} %gather_fusion.4, f32[32,32,128]{2,1,0:T(8,128)} %gather_fusion.5), kind=kOutput, calls=%fused_computation.19 | convolution fusion | flops 67502080 | bytes 2621440 | tf_op jit(solution)/shard_map/srj,skj->srk/dot_general | solution.py:47
  76.9 2.6 %collective-permute-done.7 = bf16[8,32,128]{2,1,0:T(8,128)(2,1)S(1)} collective-permute-done((bf16[8,32,128]{2,1,0:T(8,128)(2,1)S(1)}, bf16[8,32,128]{2,1,0:T(8,128)(2,1)S(1)}, u32[]{:S(2)}, u32[]{:S(2)}) %collective-permute-start.7) | collective-permute-done | bytes 65568 | tf_op jit(solution)/shard_map/ppermute | solution.py:18
  79.7 8.8 %all_to_all.53 = f32[32,1,32]{2,1,0:T(1,128)S(1)} all-to-all(f32[32,1,32]{2,1,0:T(1,128)S(1)} %broadcast_in_dim.25), channel_id=1, replica_groups=mesh['dom'=8,'rep'=4] {'dom','rep'}, dimensions={0} | all-to-all | bytes 8192 | tf_op jit(solution)/shard_map/all_to_all | solution.py:24
  88.8 8.8 %all_to_all.54 = f32[32,1,32]{2,1,0:T(1,128)S(1)} all-to-all(f32[32,1,32]{2,1,0:T(1,128)S(1)} %broadcast_in_dim.26), channel_id=1, replica_groups=mesh['dom'=8,'rep'=4] {'dom','rep'}, dimensions={0} | all-to-all | bytes 8192 | tf_op jit(solution)/shard_map/all_to_all | solution.py:24
  101.2 1.7 %collective-permute-start.9 = (f32[32,128]{1,0:T(8,128)S(1)}, f32[32,128]{1,0:T(8,128)S(1)}, u32[]{:S(2)}, u32[]{:S(2)}) collective-permute-start(f32[32,128]{1,0:T(8,128)S(1)} %fusion.62), channel_id=1, source_target_pairs={{0,3},{1,0},{2,1},{3,2},{4,7},{5,4},{6,5},{7,6},{8,11},{9,8},{10,9... | collective-permute-start | bytes 49160 | tf_op jit(solution)/shard_map/ppermute | solution.py:14
  105.9 2.0 %fusion.2 = f32[32,32,128]{2,1,0:T(8,128)S(1)} fusion(bf16[32,128,128]{2,1,0:T(8,128)(2,1)S(1)} %bitcast.218, f32[32,32,128]{2,1,0:T(8,128)S(1)} %gather_fusion.7, f32[32,32,128]{2,1,0:T(8,128)} %gather_fusion.8), kind=kOutput, calls=%fused_computation.20 | convolution fusion | flops 67502080 | bytes 2621440 | tf_op jit(solution)/shard_map/srj,skj->srk/dot_general | solution.py:47
  110.6 2.6 %collective-permute-done.11 = bf16[8,32,128]{2,1,0:T(8,128)(2,1)S(1)} collective-permute-done((bf16[8,32,128]{2,1,0:T(8,128)(2,1)S(1)}, bf16[8,32,128]{2,1,0:T(8,128)(2,1)S(1)}, u32[]{:S(2)}, u32[]{:S(2)}) %collective-permute-start.11) | collective-permute-done | bytes 65568 | tf_op jit(solution)/shard_map/ppermute | solution.py:18
  113.3 8.8 %all_to_all.55 = f32[32,1,32]{2,1,0:T(1,128)S(1)} all-to-all(f32[32,1,32]{2,1,0:T(1,128)S(1)} %broadcast_in_dim.27), channel_id=1, replica_groups=mesh['dom'=8,'rep'=4] {'dom','rep'}, dimensions={0} | all-to-all | bytes 8192 | tf_op jit(solution)/shard_map/all_to_all | solution.py:24
  122.4 8.8 %all_to_all.56 = f32[32,1,32]{2,1,0:T(1,128)S(1)} all-to-all(f32[32,1,32]{2,1,0:T(1,128)S(1)} %broadcast_in_dim.28), channel_id=1, replica_groups=mesh['dom'=8,'rep'=4] {'dom','rep'}, dimensions={0} | all-to-all | bytes 8192 | tf_op jit(solution)/shard_map/all_to_all | solution.py:24
  134.3 1.7 %collective-permute-start.13 = (f32[32,128]{1,0:T(8,128)S(1)}, f32[32,128]{1,0:T(8,128)S(1)}, u32[]{:S(2)}, u32[]{:S(2)}) collective-permute-start(f32[32,128]{1,0:T(8,128)S(1)} %fusion.59), channel_id=1, source_target_pairs={{0,3},{1,0},{2,1},{3,2},{4,7},{5,4},{6,5},{7,6},{8,11},{9,8},{10,9... | collective-permute-start | bytes 49160 | tf_op jit(solution)/shard_map/ppermute | solution.py:14
  138.9 2.0 %fusion.3 = f32[32,32,128]{2,1,0:T(8,128)S(1)} fusion(bf16[32,128,128]{2,1,0:T(8,128)(2,1)S(1)} %bitcast.219, f32[32,32,128]{2,1,0:T(8,128)S(1)} %gather_fusion.10, f32[32,32,128]{2,1,0:T(8,128)} %gather_fusion.11), kind=kOutput, calls=%fused_computation.21 | convolution fusion | flops 67502080 | bytes 2621440 | tf_op jit(solution)/shard_map/srj,skj->srk/dot_general | solution.py:47
  143.6 2.6 %collective-permute-done.15 = bf16[8,32,128]{2,1,0:T(8,128)(2,1)S(1)} collective-permute-done((bf16[8,32,128]{2,1,0:T(8,128)(2,1)S(1)}, bf16[8,32,128]{2,1,0:T(8,128)(2,1)S(1)}, u32[]{:S(2)}, u32[]{:S(2)}) %collective-permute-start.15) | collective-permute-done | bytes 65568 | tf_op jit(solution)/shard_map/ppermute | solution.py:18
  146.4 8.8 %all_to_all.57 = f32[32,1,32]{2,1,0:T(1,128)S(1)} all-to-all(f32[32,1,32]{2,1,0:T(1,128)S(1)} %broadcast_in_dim.29), channel_id=1, replica_groups=mesh['dom'=8,'rep'=4] {'dom','rep'}, dimensions={0} | all-to-all | bytes 8192 | tf_op jit(solution)/shard_map/all_to_all | solution.py:24
  (166 shorter events, 40.5 us)
Async XLA Ops:
  0.6 13.1 %copy-start = (bf16[8,2,128,128]{3,2,1,0:T(8,128)(2,1)S(1)}, bf16[8,2,128,128]{3,2,1,0:T(8,128)(2,1)}, u32[]{:S(2)}) copy-start(bf16[8,2,128,128]{3,2,1,0:T(8,128)(2,1)} %param.29) | copy-start | bytes 1572868
  2.4 10.4 %copy-start.1 = (bf16[8,128,128]{2,1,0:T(8,128)(2,1)S(1)}, bf16[8,128,128]{2,1,0:T(8,128)(2,1)}, u32[]{:S(2)}) copy-start(bf16[8,128,128]{2,1,0:T(8,128)(2,1)} %param.28) | copy-start | bytes 786436
  4.4 14.2 %all-to-all-start = ((s32[4,8,2]{1,2,0:T(2,128)}), s32[4,8,2]{1,2,0:T(2,128)S(1)}, u32[]{:S(2)}, u32[]{:S(2)}) async-start(s32[4,8,2]{1,2,0:T(2,128)} %copy.129), calls=%async_computation | async-start | bytes 8192 | tf_op jit(solution)/shard_map/all_to_all | solution.py:100
  8.7 14.4 %collective-permute-start.2 = (bf16[8,32,128]{2,1,0:T(8,128)(2,1)S(1)}, bf16[8,32,128]{2,1,0:T(8,128)(2,1)S(1)}, u32[]{:S(2)}, u32[]{:S(2)}) collective-permute-start(bf16[8,32,128]{2,1,0:T(8,128)(2,1)S(1)} %get-tuple-element.112), channel_id=1, source_target_pairs={{0,4},{4,0},{8,12},{12,8},{16,20},{20,16},{24,28},{28,24},{1,5},{5... | collective-permute-start | bytes 196616 | tf_op jit(solution)/shard_map/ppermute | solution.py:18
  10.8 12.1 %collective-permute-start = (bf16[32,128]{1,0:T(8,128)(2,1)S(1)}, bf16[32,128]{1,0:T(8,128)(2,1)S(1)}, u32[]{:S(2)}, u32[]{:S(2)}) collective-permute-start(bf16[32,128]{1,0:T(8,128)(2,1)S(1)} %slice_bitcast_fusion.11), channel_id=1, source_target_pairs={{0,1},{1,2},{2,3},{3,0},{4,5},{5,6},{6,7},{7,4},{8,9},{9,10},{10,1... | collective-permute-start | bytes 24584 | tf_op jit(solution)/shard_map/ppermute | solution.py:14
  11.1 12.0 %collective-permute-start.1 = (f32[32,128]{1,0:T(8,128)S(1)}, f32[32,128]{1,0:T(8,128)S(1)}, u32[]{:S(2)}, u32[]{:S(2)}) collective-permute-start(f32[32,128]{1,0:T(8,128)S(1)} %fusion.68), channel_id=1, source_target_pairs={{0,3},{1,0},{2,1},{3,2},{4,7},{5,4},{6,5},{7,6},{8,11},{9,8},{10,9... | collective-permute-start | bytes 49160 | tf_op jit(solution)/shard_map/ppermute | solution.py:14
  18.7 18.0 %all-to-all-start.1 = ((bf16[4,8,128,128]{3,2,1,0:T(8,128)(2,1)}), bf16[4,8,128,128]{3,2,1,0:T(8,128)(2,1)S(1)}, u32[]{:S(2)}, u32[]{:S(2)}) async-start(bf16[4,8,128,128]{3,2,1,0:T(8,128)(2,1)} %scatter_fusion.1), calls=%async_computation.1 | async-start | bytes 2097152 | tf_op jit(solution)/shard_map/all_to_all | solution.py:99
  39.2 4.3 %collective-permute-start.3 = (bf16[8,32,128]{2,1,0:T(8,128)(2,1)S(1)}, bf16[8,32,128]{2,1,0:T(8,128)(2,1)S(1)}, u32[]{:S(2)}, u32[]{:S(2)}) collective-permute-start(bf16[8,32,128]{2,1,0:T(8,128)(2,1)S(1)} %copy.234), channel_id=1, source_target_pairs={{0,4},{4,0},{8,12},{12,8},{16,20},{20,16},{24,28},{28,24},{1,5},{5... | collective-permute-start | bytes 196616 | tf_op jit(solution)/shard_map/ppermute | solution.py:18
  64.1 6.7 %collective-permute-start.6 = (bf16[8,32,128]{2,1,0:T(8,128)(2,1)S(1)}, bf16[8,32,128]{2,1,0:T(8,128)(2,1)S(1)}, u32[]{:S(2)}, u32[]{:S(2)}) collective-permute-start(bf16[8,32,128]{2,1,0:T(8,128)(2,1)S(1)} %get-tuple-element.108), channel_id=1, source_target_pairs={{0,4},{4,0},{8,12},{12,8},{16,20},{20,16},{24,28},{28,24},{1,5},{5... | collective-permute-start | bytes 196616 | tf_op jit(solution)/shard_map/ppermute | solution.py:18
  67.5 3.1 %collective-permute-start.4 = (bf16[32,128]{1,0:T(8,128)(2,1)S(1)}, bf16[32,128]{1,0:T(8,128)(2,1)S(1)}, u32[]{:S(2)}, u32[]{:S(2)}) collective-permute-start(bf16[32,128]{1,0:T(8,128)(2,1)S(1)} %slice_bitcast_fusion.8), channel_id=1, source_target_pairs={{0,1},{1,2},{2,3},{3,0},{4,5},{5,6},{6,7},{7,4},{8,9},{9,10},{10,1... | collective-permute-start | bytes 24584 | tf_op jit(solution)/shard_map/ppermute | solution.py:14
  67.6 3.2 %collective-permute-start.5 = (f32[32,128]{1,0:T(8,128)S(1)}, f32[32,128]{1,0:T(8,128)S(1)}, u32[]{:S(2)}, u32[]{:S(2)}) collective-permute-start(f32[32,128]{1,0:T(8,128)S(1)} %fusion.65), channel_id=1, source_target_pairs={{0,3},{1,0},{2,1},{3,2},{4,7},{5,4},{6,5},{7,6},{8,11},{9,8},{10,9... | collective-permute-start | bytes 49160 | tf_op jit(solution)/shard_map/ppermute | solution.py:14
  74.8 4.7 %collective-permute-start.7 = (bf16[8,32,128]{2,1,0:T(8,128)(2,1)S(1)}, bf16[8,32,128]{2,1,0:T(8,128)(2,1)S(1)}, u32[]{:S(2)}, u32[]{:S(2)}) collective-permute-start(bf16[8,32,128]{2,1,0:T(8,128)(2,1)S(1)} %copy.233), channel_id=1, source_target_pairs={{0,4},{4,0},{8,12},{12,8},{16,20},{20,16},{24,28},{28,24},{1,5},{5... | collective-permute-start | bytes 196616 | tf_op jit(solution)/shard_map/ppermute | solution.py:18
  88.7 9.0 %copy-start.6 = (f32[8,32,128]{2,1,0:T(8,128)}, f32[8,32,128]{2,1,0:T(8,128)S(1)}, u32[]{:S(2)}) copy-start(f32[8,32,128]{2,1,0:T(8,128)S(1)} %get-tuple-element.107) | copy-start | bytes 393220
  97.8 6.7 %collective-permute-start.10 = (bf16[8,32,128]{2,1,0:T(8,128)(2,1)S(1)}, bf16[8,32,128]{2,1,0:T(8,128)(2,1)S(1)}, u32[]{:S(2)}, u32[]{:S(2)}) collective-permute-start(bf16[8,32,128]{2,1,0:T(8,128)(2,1)S(1)} %get-tuple-element.104), channel_id=1, source_target_pairs={{0,4},{4,0},{8,12},{12,8},{16,20},{20,16},{24,28},{28,24},{1,5},{5... | collective-permute-start | bytes 196616 | tf_op jit(solution)/shard_map/ppermute | solution.py:18
  101.2 3.1 %collective-permute-start.8 = (bf16[32,128]{1,0:T(8,128)(2,1)S(1)}, bf16[32,128]{1,0:T(8,128)(2,1)S(1)}, u32[]{:S(2)}, u32[]{:S(2)}) collective-permute-start(bf16[32,128]{1,0:T(8,128)(2,1)S(1)} %slice_bitcast_fusion.5), channel_id=1, source_target_pairs={{0,1},{1,2},{2,3},{3,0},{4,5},{5,6},{6,7},{7,4},{8,9},{9,10},{10,1... | collective-permute-start | bytes 24584 | tf_op jit(solution)/shard_map/ppermute | solution.py:14
  101.2 3.2 %collective-permute-start.9 = (f32[32,128]{1,0:T(8,128)S(1)}, f32[32,128]{1,0:T(8,128)S(1)}, u32[]{:S(2)}, u32[]{:S(2)}) collective-permute-start(f32[32,128]{1,0:T(8,128)S(1)} %fusion.62), channel_id=1, source_target_pairs={{0,3},{1,0},{2,1},{3,2},{4,7},{5,4},{6,5},{7,6},{8,11},{9,8},{10,9... | collective-permute-start | bytes 49160 | tf_op jit(solution)/shard_map/ppermute | solution.py:14
  108.4 4.7 %collective-permute-start.11 = (bf16[8,32,128]{2,1,0:T(8,128)(2,1)S(1)}, bf16[8,32,128]{2,1,0:T(8,128)(2,1)S(1)}, u32[]{:S(2)}, u32[]{:S(2)}) collective-permute-start(bf16[8,32,128]{2,1,0:T(8,128)(2,1)S(1)} %copy.232), channel_id=1, source_target_pairs={{0,4},{4,0},{8,12},{12,8},{16,20},{20,16},{24,28},{28,24},{1,5},{5... | collective-permute-start | bytes 196616 | tf_op jit(solution)/shard_map/ppermute | solution.py:18
  113.2 9.0 %copy-start.7 = (f32[8,32,128]{2,1,0:T(8,128)S(1)}, f32[8,32,128]{2,1,0:T(8,128)}, u32[]{:S(2)}) copy-start(f32[8,32,128]{2,1,0:T(8,128)} %copy-done.6) | copy-start | bytes 393220
  122.4 9.0 %copy-start.4 = (f32[8,32,128]{2,1,0:T(8,128)}, f32[8,32,128]{2,1,0:T(8,128)S(1)}, u32[]{:S(2)}) copy-start(f32[8,32,128]{2,1,0:T(8,128)S(1)} %get-tuple-element.103) | copy-start | bytes 393220
  131.4 6.0 %collective-permute-start.14 = (bf16[8,32,128]{2,1,0:T(8,128)(2,1)S(1)}, bf16[8,32,128]{2,1,0:T(8,128)(2,1)S(1)}, u32[]{:S(2)}, u32[]{:S(2)}) collective-permute-start(bf16[8,32,128]{2,1,0:T(8,128)(2,1)S(1)} %get-tuple-element.100), channel_id=1, source_target_pairs={{0,4},{4,0},{8,12},{12,8},{16,20},{20,16},{24,28},{28,24},{1,5},{5... | collective-permute-start | bytes 196616 | tf_op jit(solution)/shard_map/ppermute | solution.py:18
  134.2 3.1 %collective-permute-start.12 = (bf16[32,128]{1,0:T(8,128)(2,1)S(1)}, bf16[32,128]{1,0:T(8,128)(2,1)S(1)}, u32[]{:S(2)}, u32[]{:S(2)}) collective-permute-start(bf16[32,128]{1,0:T(8,128)(2,1)S(1)} %slice_bitcast_fusion.2), channel_id=1, source_target_pairs={{0,1},{1,2},{2,3},{3,0},{4,5},{5,6},{6,7},{7,4},{8,9},{9,10},{10,1... | collective-permute-start | bytes 24584 | tf_op jit(solution)/shard_map/ppermute | solution.py:14
  134.3 3.2 %collective-permute-start.13 = (f32[32,128]{1,0:T(8,128)S(1)}, f32[32,128]{1,0:T(8,128)S(1)}, u32[]{:S(2)}, u32[]{:S(2)}) collective-permute-start(f32[32,128]{1,0:T(8,128)S(1)} %fusion.59), channel_id=1, source_target_pairs={{0,3},{1,0},{2,1},{3,2},{4,7},{5,4},{6,5},{7,6},{8,11},{9,8},{10,9... | collective-permute-start | bytes 49160 | tf_op jit(solution)/shard_map/ppermute | solution.py:14
  141.5 4.7 %collective-permute-start.15 = (bf16[8,32,128]{2,1,0:T(8,128)(2,1)S(1)}, bf16[8,32,128]{2,1,0:T(8,128)(2,1)S(1)}, u32[]{:S(2)}, u32[]{:S(2)}) collective-permute-start(bf16[8,32,128]{2,1,0:T(8,128)(2,1)S(1)} %copy.231), channel_id=1, source_target_pairs={{0,4},{4,0},{8,12},{12,8},{16,20},{20,16},{24,28},{28,24},{1,5},{5... | collective-permute-start | bytes 196616 | tf_op jit(solution)/shard_map/ppermute | solution.py:18
  146.2 9.0 %copy-start.5 = (f32[8,32,128]{2,1,0:T(8,128)S(1)}, f32[8,32,128]{2,1,0:T(8,128)}, u32[]{:S(2)}) copy-start(f32[8,32,128]{2,1,0:T(8,128)} %copy-done.4) | copy-start | bytes 393220
  (8 other events, 24.8 us)

commit v4 on v1

--- a/solution.py
+++ b/solution.py
@@ -110,7 +110,6 @@
     residual = rhs
     preconditioned = scale * residual
     direction = preconditioned
-    res_dot = total(jnp.sum(residual * preconditioned, axis=(0, 2)))
     for step in range(ITERS):
         image = apply_operator(
             direction,
@@ -122,14 +121,22 @@
             near_index,
             far_index,
         )
-        curve = total(jnp.sum(direction * image, axis=(0, 2)))
+        parts = [
+            jnp.sum(direction * image, axis=(0, 2)),
+            jnp.sum(residual * preconditioned, axis=(0, 2)),
+        ]
+        if step < ITERS - 1:
+            parts.append(jnp.sum(preconditioned * image, axis=(0, 2)))
+            parts.append(jnp.sum(image * (scale * image), axis=(0, 2)))
+        sums = total(jnp.stack(parts))
+        curve, res_dot = sums[0], sums[1]
         alpha = res_dot / curve
         solution = solution + alpha[None, :, None] * direction
         residual = residual - alpha[None, :, None] * image
-        preconditioned = scale * residual
-        next_dot = total(jnp.sum(residual * preconditioned, axis=(0, 2)))
-        direction = preconditioned + (next_dot / res_dot)[None, :, None] * direction
-        res_dot = next_dot
+        if step < ITERS - 1:
+            preconditioned = scale * residual
+            next_dot = res_dot - 2.0 * alpha * sums[2] + alpha * alpha * sums[3]
+            direction = preconditioned + (next_dot / res_dot)[None, :, None] * direction
     return (solution, residual)
 
 

time: 166 us -> 134 us (0.81)
  blocking collectives: 64.1 us -> 37.8 us
  waiting for transfers between devices: 33.4 us -> 26.4 us
  starting transfers between devices: 26.7 us -> 24.1 us
  other arithmetic: 3.64 us -> 5.43 us
  local copies, waits for them, and re-layouts: 18.9 us -> 20.6 us
    all_to_all x7 -> x4, blocking collectives: 64.1 us -> 37.8 us  [total(): gathered = lax.all_to_all(spread, ('dom', 'rep'), 0, 0, tiled=True)]
    all_to_all x1 -> x0, waiting for transfers between devices: 7.05 us -> none  [total(): gathered = lax.all_to_all(spread, ('dom', 'rep'), 0, 0, tiled=True)]
    all_to_all x1 -> x0, starting transfers between devices: 2.54 us -> none  [total(): gathered = lax.all_to_all(spread, ('dom', 'rep'), 0, 0, tiled=True)]
    all_to_all x0 -> x3, other arithmetic: none -> 2.05 us  [total(): gathered = lax.all_to_all(spread, ('dom', 'rep'), 0, 0, tiled=True)]
  transfers between devices with their start and end apart: 19 -> 18, of which waited for: 9 -> 8; matrix products, arithmetic and copies ran while one was open for 11% -> 15% of each run, Pallas kernels for 0% -> 0%
where the time goes in v4:
time: 134 us; the launch traced here: 133 us
  blocking collectives  37.8 us (28%)
  waiting for transfers between devices  26.4 us (20%)
  starting transfers between devices  24.1 us (18%)
  local copies, waits for them, and re-layouts  20.6 us (15%)
  matrix products  17.6 us (13%)
  other arithmetic  5.43 us (4%)
    all_to_all x4, blocking collectives, total(): gathered = lax.all_to_all(spread, ('dom', 'rep'), 0, 0, tiled=True)  37.8 us
    all_to_all x1, waiting for transfers between devices, body(): lax.all_to_all(send_set, 'rep', split_axis=0, concat_axis=0, tiled=True)  12.1 us
    ppermute x8, waiting for transfers between devices, partner(): lax.ppermute(value, axis, [(i, i ^ 1 << distance) for i in range(lax.axis...  10.9 us
    ppermute x8, starting transfers between devices, partner(): lax.ppermute(value, axis, [(i, i ^ 1 << distance) for i in range(lax.axis...  9.26 us
    gather x8, local copies, waits for them, and re-layouts, contact_pairs(): difference = (vector[near_index] - other[far_index]).astype(jnp.bfloat16)  7.93 us
    dot_general x4, matrix products, contact_pairs(): jnp.einsum('srj,skj->srk', multiplier, contact_set, preferred_element_typ...  7.84 us
    ppermute x8, starting transfers between devices, from_behind(): return lax.ppermute(value, axis, pairs)  7.14 us
    dot_general x8, matrix products, collect(): jnp.einsum('sn,srk->nrk', onehot, values, precision=lax.Precision.HIGHEST)  4.68 us
  transfers between devices with their start and end apart: 18, of which 8 were waited for; matrix products, arithmetic and copies ran while one was open for 15% of the time, Pallas kernels for 0%

profile of v4, /device:TPU:0, one launch (start us, length us, event | category | flops | bytes accessed | tf_op | source)
XLA Modules:
  0.0 133.2 jit_solution(5963400787484995404)
XLA Ops:
  4.4 4.2 %all-to-all-start = ((s32[4,8,2]{1,2,0:T(2,128)}), s32[4,8,2]{1,2,0:T(2,128)S(1)}, u32[]{:S(2)}, u32[]{:S(2)}) async-start(s32[4,8,2]{1,2,0:T(2,128)} %copy.129), calls=%async_computation | async-start | bytes 8192 | tf_op jit(solution)/shard_map/all_to_all | solution.py:100
  8.7 2.1 %collective-permute-start.2 = (bf16[8,32,128]{2,1,0:T(8,128)(2,1)S(1)}, bf16[8,32,128]{2,1,0:T(8,128)(2,1)S(1)}, u32[]{:S(2)}, u32[]{:S(2)}) collective-permute-start(bf16[8,32,128]{2,1,0:T(8,128)(2,1)S(1)} %get-tuple-element.127), channel_id=1, source_target_pairs={{0,4},{4,0},{8,12},{12,8},{16,20},{20,16},{24,28},{28,24},{1,5},{5... | collective-permute-start | bytes 196616 | tf_op jit(solution)/shard_map/ppermute | solution.py:18
  11.1 1.6 %collective-permute-start.1 = (f32[32,128]{1,0:T(8,128)S(1)}, f32[32,128]{1,0:T(8,128)S(1)}, u32[]{:S(2)}, u32[]{:S(2)}) collective-permute-start(f32[32,128]{1,0:T(8,128)S(1)} %fusion.73), channel_id=1, source_target_pairs={{0,3},{1,0},{2,1},{3,2},{4,7},{5,4},{6,5},{7,6},{8,11},{9,8},{10,9... | collective-permute-start | bytes 49160 | tf_op jit(solution)/shard_map/ppermute | solution.py:14
  15.9 2.7 %scatter_fusion.1 = bf16[4,8,128,128]{3,2,1,0:T(8,128)(2,1)} fusion(bf16[4,8,128,128]{3,2,1,0:T(8,128)(2,1)} %broadcast_in_dim.16, s32[16]{0:T(128)S(1)} %fusion.122, bf16[16,128,128]{2,1,0:T(8,128)(2,1)S(1)} %copy-done.8), kind=kCustom, calls=%fused_computation.13 | custom fusion | bytes 1572992 | tf_op jit(solution)/shard_map/scatter | solution.py:95
  18.7 3.5 %all-to-all-start.1 = ((bf16[4,8,128,128]{3,2,1,0:T(8,128)(2,1)}), bf16[4,8,128,128]{3,2,1,0:T(8,128)(2,1)S(1)}, u32[]{:S(2)}, u32[]{:S(2)}) async-start(bf16[4,8,128,128]{3,2,1,0:T(8,128)(2,1)} %scatter_fusion.1), calls=%async_computation.1 | async-start | bytes 2097152 | tf_op jit(solution)/shard_map/all_to_all | solution.py:99
  24.5 12.1 %all-to-all-done.1 = bf16[4,8,128,128]{3,2,1,0:T(8,128)(2,1)S(1)} async-done(((bf16[4,8,128,128]{3,2,1,0:T(8,128)(2,1)}), bf16[4,8,128,128]{3,2,1,0:T(8,128)(2,1)S(1)}, u32[]{:S(2)}, u32[]{:S(2)}) %all-to-all-start.1) | async-done | bytes 1048608 | tf_op jit(solution)/shard_map/all_to_all | solution.py:99
  36.6 2.0 %fusion = f32[32,32,128]{2,1,0:T(8,128)S(1)} fusion(bf16[32,128,128]{2,1,0:T(8,128)(2,1)S(1)} %bitcast.275, f32[32,32,128]{2,1,0:T(8,128)S(1)} %gather_fusion.1, f32[32,32,128]{2,1,0:T(8,128)} %gather_fusion.2), kind=kOutput, calls=%fused_computation.18 | convolution fusion | flops 67502080 | bytes 2621440 | tf_op jit(solution)/shard_map/srj,skj->srk/dot_general | solution.py:47
  40.5 3.1 %collective-permute-done.3 = bf16[8,32,128]{2,1,0:T(8,128)(2,1)S(1)} collective-permute-done((bf16[8,32,128]{2,1,0:T(8,128)(2,1)S(1)}, bf16[8,32,128]{2,1,0:T(8,128)(2,1)S(1)}, u32[]{:S(2)}, u32[]{:S(2)}) %collective-permute-start.3) | collective-permute-done | bytes 65568 | tf_op jit(solution)/shard_map/ppermute | solution.py:18
  43.9 11.0 %all_to_all.30 = f32[32,1,128]{2,1,0:T(1,128)S(1)} all-to-all(f32[32,1,128]{2,1,0:T(1,128)S(1)} %reshape.536), channel_id=1, replica_groups=mesh['dom'=8,'rep'=4] {'dom','rep'}, dimensions={0} | all-to-all | bytes 32768 | tf_op jit(solution)/shard_map/all_to_all | solution.py:24
  59.8 1.7 %collective-permute-start.5 = (f32[32,128]{1,0:T(8,128)S(1)}, f32[32,128]{1,0:T(8,128)S(1)}, u32[]{:S(2)}, u32[]{:S(2)}) collective-permute-start(f32[32,128]{1,0:T(8,128)S(1)} %fusion.70), channel_id=1, source_target_pairs={{0,3},{1,0},{2,1},{3,2},{4,7},{5,4},{6,5},{7,6},{8,11},{9,8},{10,9... | collective-permute-start | bytes 49160 | tf_op jit(solution)/shard_map/ppermute | solution.py:14
  64.4 2.0 %fusion.1 = f32[32,32,128]{2,1,0:T(8,128)S(1)} fusion(bf16[32,128,128]{2,1,0:T(8,128)(2,1)S(1)} %bitcast.276, f32[32,32,128]{2,1,0:T(8,128)S(1)} %gather_fusion.4, f32[32,32,128]{2,1,0:T(8,128)} %gather_fusion.5), kind=kOutput, calls=%fused_computation.19 | convolution fusion | flops 67502080 | bytes 2621440 | tf_op jit(solution)/shard_map/srj,skj->srk/dot_general | solution.py:47
  67.0 1.5 %collective-permute-start.7 = (bf16[8,32,128]{2,1,0:T(8,128)(2,1)S(1)}, bf16[8,32,128]{2,1,0:T(8,128)(2,1)S(1)}, u32[]{:S(2)}, u32[]{:S(2)}) collective-permute-start(bf16[8,32,128]{2,1,0:T(8,128)(2,1)S(1)} %copy.233), channel_id=1, source_target_pairs={{0,4},{4,0},{8,12},{12,8},{16,20},{20,16},{24,28},{28,24},{1,5},{5... | collective-permute-start | bytes 196616 | tf_op jit(solution)/shard_map/ppermute | solution.py:18
  69.2 2.6 %collective-permute-done.7 = bf16[8,32,128]{2,1,0:T(8,128)(2,1)S(1)} collective-permute-done((bf16[8,32,128]{2,1,0:T(8,128)(2,1)S(1)}, bf16[8,32,128]{2,1,0:T(8,128)(2,1)S(1)}, u32[]{:S(2)}, u32[]{:S(2)}) %collective-permute-start.7) | collective-permute-done | bytes 65568 | tf_op jit(solution)/shard_map/ppermute | solution.py:18
  72.1 8.8 %all_to_all.31 = f32[32,1,128]{2,1,0:T(1,128)S(1)} all-to-all(f32[32,1,128]{2,1,0:T(1,128)S(1)} %reshape.538), channel_id=1, replica_groups=mesh['dom'=8,'rep'=4] {'dom','rep'}, dimensions={0} | all-to-all | bytes 32768 | tf_op jit(solution)/shard_map/all_to_all | solution.py:24
  85.4 1.7 %collective-permute-start.9 = (f32[32,128]{1,0:T(8,128)S(1)}, f32[32,128]{1,0:T(8,128)S(1)}, u32[]{:S(2)}, u32[]{:S(2)}) collective-permute-start(f32[32,128]{1,0:T(8,128)S(1)} %fusion.67), channel_id=1, source_target_pairs={{0,3},{1,0},{2,1},{3,2},{4,7},{5,4},{6,5},{7,6},{8,11},{9,8},{10,9... | collective-permute-start | bytes 49160 | tf_op jit(solution)/shard_map/ppermute | solution.py:14
  90.7 2.0 %fusion.2 = f32[32,32,128]{2,1,0:T(8,128)S(1)} fusion(bf16[32,128,128]{2,1,0:T(8,128)(2,1)S(1)} %bitcast.277, f32[32,32,128]{2,1,0:T(8,128)S(1)} %gather_fusion.7, f32[32,32,128]{2,1,0:T(8,128)} %gather_fusion.8), kind=kOutput, calls=%fused_computation.20 | convolution fusion | flops 67502080 | bytes 2621440 | tf_op jit(solution)/shard_map/srj,skj->srk/dot_general | solution.py:47
  93.3 1.5 %collective-permute-start.11 = (bf16[8,32,128]{2,1,0:T(8,128)(2,1)S(1)}, bf16[8,32,128]{2,1,0:T(8,128)(2,1)S(1)}, u32[]{:S(2)}, u32[]{:S(2)}) collective-permute-start(bf16[8,32,128]{2,1,0:T(8,128)(2,1)S(1)} %copy.232), channel_id=1, source_target_pairs={{0,4},{4,0},{8,12},{12,8},{16,20},{20,16},{24,28},{28,24},{1,5},{5... | collective-permute-start | bytes 196616 | tf_op jit(solution)/shard_map/ppermute | solution.py:18
  95.4 2.6 %collective-permute-done.11 = bf16[8,32,128]{2,1,0:T(8,128)(2,1)S(1)} collective-permute-done((bf16[8,32,128]{2,1,0:T(8,128)(2,1)S(1)}, bf16[8,32,128]{2,1,0:T(8,128)(2,1)S(1)}, u32[]{:S(2)}, u32[]{:S(2)}) %collective-permute-start.11) | collective-permute-done | bytes 65568 | tf_op jit(solution)/shard_map/ppermute | solution.py:18
  98.3 8.8 %all_to_all.32 = f32[32,1,128]{2,1,0:T(1,128)S(1)} all-to-all(f32[32,1,128]{2,1,0:T(1,128)S(1)} %reshape.540), channel_id=1, replica_groups=mesh['dom'=8,'rep'=4] {'dom','rep'}, dimensions={0} | all-to-all | bytes 32768 | tf_op jit(solution)/shard_map/all_to_all | solution.py:24
  111.1 1.7 %collective-permute-start.13 = (f32[32,128]{1,0:T(8,128)S(1)}, f32[32,128]{1,0:T(8,128)S(1)}, u32[]{:S(2)}, u32[]{:S(2)}) collective-permute-start(f32[32,128]{1,0:T(8,128)S(1)} %fusion.64), channel_id=1, source_target_pairs={{0,3},{1,0},{2,1},{3,2},{4,7},{5,4},{6,5},{7,6},{8,11},{9,8},{10,9... | collective-permute-start | bytes 49160 | tf_op jit(solution)/shard_map/ppermute | solution.py:14
  115.8 2.0 %fusion.3 = f32[32,32,128]{2,1,0:T(8,128)S(1)} fusion(bf16[32,128,128]{2,1,0:T(8,128)(2,1)S(1)} %bitcast.278, f32[32,32,128]{2,1,0:T(8,128)S(1)} %gather_fusion.10, f32[32,32,128]{2,1,0:T(8,128)} %gather_fusion.11), kind=kOutput, calls=%fused_computation.21 | convolution fusion | flops 67502080 | bytes 2621440 | tf_op jit(solution)/shard_map/srj,skj->srk/dot_general | solution.py:47
  118.3 1.5 %collective-permute-start.15 = (bf16[8,32,128]{2,1,0:T(8,128)(2,1)S(1)}, bf16[8,32,128]{2,1,0:T(8,128)(2,1)S(1)}, u32[]{:S(2)}, u32[]{:S(2)}) collective-permute-start(bf16[8,32,128]{2,1,0:T(8,128)(2,1)S(1)} %copy.231), channel_id=1, source_target_pairs={{0,4},{4,0},{8,12},{12,8},{16,20},{20,16},{24,28},{28,24},{1,5},{5... | collective-permute-start | bytes 196616 | tf_op jit(solution)/shard_map/ppermute | solution.py:18
  120.5 2.6 %collective-permute-done.15 = bf16[8,32,128]{2,1,0:T(8,128)(2,1)S(1)} collective-permute-done((bf16[8,32,128]{2,1,0:T(8,128)(2,1)S(1)}, bf16[8,32,128]{2,1,0:T(8,128)(2,1)S(1)}, u32[]{:S(2)}, u32[]{:S(2)}) %collective-permute-start.15) | collective-permute-done | bytes 65568 | tf_op jit(solution)/shard_map/ppermute | solution.py:18
  123.3 9.1 %all_to_all.33 = f32[32,2,32]{2,1,0:T(2,128)S(1)} all-to-all(f32[32,2,32]{2,1,0:T(2,128)S(1)} %broadcast_in_dim.20), channel_id=1, replica_groups=mesh['dom'=8,'rep'=4] {'dom','rep'}, dimensions={0} | all-to-all | bytes 16384 | tf_op jit(solution)/shard_map/all_to_all | solution.py:24
  (165 shorter events, 39.3 us)
Async XLA Ops:
  0.6 13.1 %copy-start = (bf16[8,2,128,128]{3,2,1,0:T(8,128)(2,1)S(1)}, bf16[8,2,128,128]{3,2,1,0:T(8,128)(2,1)}, u32[]{:S(2)}) copy-start(bf16[8,2,128,128]{3,2,1,0:T(8,128)(2,1)} %param.29) | copy-start | bytes 1572868
  0.7 8.0 %copy-start.3 = (f32[8,32,128]{2,1,0:T(8,128)S(1)}, f32[8,32,128]{2,1,0:T(8,128)}, u32[]{:S(2)}) copy-start(f32[8,32,128]{2,1,0:T(8,128)} %param.26) | copy-start | bytes 393220
  2.4 6.2 %copy-start.11 = (f32[8,128]{1,0:T(8,128)S(1)}, f32[8,128]{1,0:T(8,128)}, u32[]{:S(2)}) copy-start(f32[8,128]{1,0:T(8,128)} %param.27) | copy-start | bytes 12292
  2.4 10.4 %copy-start.1 = (bf16[8,128,128]{2,1,0:T(8,128)(2,1)S(1)}, bf16[8,128,128]{2,1,0:T(8,128)(2,1)}, u32[]{:S(2)}) copy-start(bf16[8,128,128]{2,1,0:T(8,128)(2,1)} %param.28) | copy-start | bytes 786436
  4.4 14.2 %all-to-all-start = ((s32[4,8,2]{1,2,0:T(2,128)}), s32[4,8,2]{1,2,0:T(2,128)S(1)}, u32[]{:S(2)}, u32[]{:S(2)}) async-start(s32[4,8,2]{1,2,0:T(2,128)} %copy.129), calls=%async_computation | async-start | bytes 8192 | tf_op jit(solution)/shard_map/all_to_all | solution.py:100
  8.7 14.4 %collective-permute-start.2 = (bf16[8,32,128]{2,1,0:T(8,128)(2,1)S(1)}, bf16[8,32,128]{2,1,0:T(8,128)(2,1)S(1)}, u32[]{:S(2)}, u32[]{:S(2)}) collective-permute-start(bf16[8,32,128]{2,1,0:T(8,128)(2,1)S(1)} %get-tuple-element.127), channel_id=1, source_target_pairs={{0,4},{4,0},{8,12},{12,8},{16,20},{20,16},{24,28},{28,24},{1,5},{5... | collective-permute-start | bytes 196616 | tf_op jit(solution)/shard_map/ppermute | solution.py:18
  10.8 12.1 %collective-permute-start = (bf16[32,128]{1,0:T(8,128)(2,1)S(1)}, bf16[32,128]{1,0:T(8,128)(2,1)S(1)}, u32[]{:S(2)}, u32[]{:S(2)}) collective-permute-start(bf16[32,128]{1,0:T(8,128)(2,1)S(1)} %slice_bitcast_fusion.11), channel_id=1, source_target_pairs={{0,1},{1,2},{2,3},{3,0},{4,5},{5,6},{6,7},{7,4},{8,9},{9,10},{10,1... | collective-permute-start | bytes 24584 | tf_op jit(solution)/shard_map/ppermute | solution.py:14
  11.1 12.0 %collective-permute-start.1 = (f32[32,128]{1,0:T(8,128)S(1)}, f32[32,128]{1,0:T(8,128)S(1)}, u32[]{:S(2)}, u32[]{:S(2)}) collective-permute-start(f32[32,128]{1,0:T(8,128)S(1)} %fusion.73), channel_id=1, source_target_pairs={{0,3},{1,0},{2,1},{3,2},{4,7},{5,4},{6,5},{7,6},{8,11},{9,8},{10,9... | collective-permute-start | bytes 49160 | tf_op jit(solution)/shard_map/ppermute | solution.py:14
  18.7 18.0 %all-to-all-start.1 = ((bf16[4,8,128,128]{3,2,1,0:T(8,128)(2,1)}), bf16[4,8,128,128]{3,2,1,0:T(8,128)(2,1)S(1)}, u32[]{:S(2)}, u32[]{:S(2)}) async-start(bf16[4,8,128,128]{3,2,1,0:T(8,128)(2,1)} %scatter_fusion.1), calls=%async_computation.1 | async-start | bytes 2097152 | tf_op jit(solution)/shard_map/all_to_all | solution.py:99
  39.2 4.3 %collective-permute-start.3 = (bf16[8,32,128]{2,1,0:T(8,128)(2,1)S(1)}, bf16[8,32,128]{2,1,0:T(8,128)(2,1)S(1)}, u32[]{:S(2)}, u32[]{:S(2)}) collective-permute-start(bf16[8,32,128]{2,1,0:T(8,128)(2,1)S(1)} %copy.234), channel_id=1, source_target_pairs={{0,4},{4,0},{8,12},{12,8},{16,20},{20,16},{24,28},{28,24},{1,5},{5... | collective-permute-start | bytes 196616 | tf_op jit(solution)/shard_map/ppermute | solution.py:18
  56.3 6.7 %collective-permute-start.6 = (bf16[8,32,128]{2,1,0:T(8,128)(2,1)S(1)}, bf16[8,32,128]{2,1,0:T(8,128)(2,1)S(1)}, u32[]{:S(2)}, u32[]{:S(2)}) collective-permute-start(bf16[8,32,128]{2,1,0:T(8,128)(2,1)S(1)} %get-tuple-element.121), channel_id=1, source_target_pairs={{0,4},{4,0},{8,12},{12,8},{16,20},{20,16},{24,28},{28,24},{1,5},{5... | collective-permute-start | bytes 196616 | tf_op jit(solution)/shard_map/ppermute | solution.py:18
  59.8 3.1 %collective-permute-start.4 = (bf16[32,128]{1,0:T(8,128)(2,1)S(1)}, bf16[32,128]{1,0:T(8,128)(2,1)S(1)}, u32[]{:S(2)}, u32[]{:S(2)}) collective-permute-start(bf16[32,128]{1,0:T(8,128)(2,1)S(1)} %slice_bitcast_fusion.8), channel_id=1, source_target_pairs={{0,1},{1,2},{2,3},{3,0},{4,5},{5,6},{6,7},{7,4},{8,9},{9,10},{10,1... | collective-permute-start | bytes 24584 | tf_op jit(solution)/shard_map/ppermute | solution.py:14
  59.8 3.2 %collective-permute-start.5 = (f32[32,128]{1,0:T(8,128)S(1)}, f32[32,128]{1,0:T(8,128)S(1)}, u32[]{:S(2)}, u32[]{:S(2)}) collective-permute-start(f32[32,128]{1,0:T(8,128)S(1)} %fusion.70), channel_id=1, source_target_pairs={{0,3},{1,0},{2,1},{3,2},{4,7},{5,4},{6,5},{7,6},{8,11},{9,8},{10,9... | collective-permute-start | bytes 49160 | tf_op jit(solution)/shard_map/ppermute | solution.py:14
  67.0 4.7 %collective-permute-start.7 = (bf16[8,32,128]{2,1,0:T(8,128)(2,1)S(1)}, bf16[8,32,128]{2,1,0:T(8,128)(2,1)S(1)}, u32[]{:S(2)}, u32[]{:S(2)}) collective-permute-start(bf16[8,32,128]{2,1,0:T(8,128)(2,1)S(1)} %copy.233), channel_id=1, source_target_pairs={{0,4},{4,0},{8,12},{12,8},{16,20},{20,16},{24,28},{28,24},{1,5},{5... | collective-permute-start | bytes 196616 | tf_op jit(solution)/shard_map/ppermute | solution.py:18
  81.9 7.4 %collective-permute-start.10 = (bf16[8,32,128]{2,1,0:T(8,128)(2,1)S(1)}, bf16[8,32,128]{2,1,0:T(8,128)(2,1)S(1)}, u32[]{:S(2)}, u32[]{:S(2)}) collective-permute-start(bf16[8,32,128]{2,1,0:T(8,128)(2,1)S(1)} %get-tuple-element.115), channel_id=1, source_target_pairs={{0,4},{4,0},{8,12},{12,8},{16,20},{20,16},{24,28},{28,24},{1,5},{5... | collective-permute-start | bytes 196616 | tf_op jit(solution)/shard_map/ppermute | solution.py:18
  85.3 3.1 %collective-permute-start.8 = (bf16[32,128]{1,0:T(8,128)(2,1)S(1)}, bf16[32,128]{1,0:T(8,128)(2,1)S(1)}, u32[]{:S(2)}, u32[]{:S(2)}) collective-permute-start(bf16[32,128]{1,0:T(8,128)(2,1)S(1)} %slice_bitcast_fusion.5), channel_id=1, source_target_pairs={{0,1},{1,2},{2,3},{3,0},{4,5},{5,6},{6,7},{7,4},{8,9},{9,10},{10,1... | collective-permute-start | bytes 24584 | tf_op jit(solution)/shard_map/ppermute | solution.py:14
  85.4 3.2 %collective-permute-start.9 = (f32[32,128]{1,0:T(8,128)S(1)}, f32[32,128]{1,0:T(8,128)S(1)}, u32[]{:S(2)}, u32[]{:S(2)}) collective-permute-start(f32[32,128]{1,0:T(8,128)S(1)} %fusion.67), channel_id=1, source_target_pairs={{0,3},{1,0},{2,1},{3,2},{4,7},{5,4},{6,5},{7,6},{8,11},{9,8},{10,9... | collective-permute-start | bytes 49160 | tf_op jit(solution)/shard_map/ppermute | solution.py:14
  93.2 4.8 %copy-start.7 = (f32[8,32,128]{2,1,0:T(8,128)S(1)}, f32[8,32,128]{2,1,0:T(8,128)}, u32[]{:S(2)}) copy-start(f32[8,32,128]{2,1,0:T(8,128)} %copy-done.6) | copy-start | bytes 393220
  93.3 4.7 %collective-permute-start.11 = (bf16[8,32,128]{2,1,0:T(8,128)(2,1)S(1)}, bf16[8,32,128]{2,1,0:T(8,128)(2,1)S(1)}, u32[]{:S(2)}, u32[]{:S(2)}) collective-permute-start(bf16[8,32,128]{2,1,0:T(8,128)(2,1)S(1)} %copy.232), channel_id=1, source_target_pairs={{0,4},{4,0},{8,12},{12,8},{16,20},{20,16},{24,28},{28,24},{1,5},{5... | collective-permute-start | bytes 196616 | tf_op jit(solution)/shard_map/ppermute | solution.py:18
  108.2 6.2 %collective-permute-start.14 = (bf16[8,32,128]{2,1,0:T(8,128)(2,1)S(1)}, bf16[8,32,128]{2,1,0:T(8,128)(2,1)S(1)}, u32[]{:S(2)}, u32[]{:S(2)}) collective-permute-start(bf16[8,32,128]{2,1,0:T(8,128)(2,1)S(1)} %get-tuple-element.109), channel_id=1, source_target_pairs={{0,4},{4,0},{8,12},{12,8},{16,20},{20,16},{24,28},{28,24},{1,5},{5... | collective-permute-start | bytes 196616 | tf_op jit(solution)/shard_map/ppermute | solution.py:18
  111.1 3.1 %collective-permute-start.12 = (bf16[32,128]{1,0:T(8,128)(2,1)S(1)}, bf16[32,128]{1,0:T(8,128)(2,1)S(1)}, u32[]{:S(2)}, u32[]{:S(2)}) collective-permute-start(bf16[32,128]{1,0:T(8,128)(2,1)S(1)} %slice_bitcast_fusion.2), channel_id=1, source_target_pairs={{0,1},{1,2},{2,3},{3,0},{4,5},{5,6},{6,7},{7,4},{8,9},{9,10},{10,1... | collective-permute-start | bytes 24584 | tf_op jit(solution)/shard_map/ppermute | solution.py:14
  111.1 3.2 %collective-permute-start.13 = (f32[32,128]{1,0:T(8,128)S(1)}, f32[32,128]{1,0:T(8,128)S(1)}, u32[]{:S(2)}, u32[]{:S(2)}) collective-permute-start(f32[32,128]{1,0:T(8,128)S(1)} %fusion.64), channel_id=1, source_target_pairs={{0,3},{1,0},{2,1},{3,2},{4,7},{5,4},{6,5},{7,6},{8,11},{9,8},{10,9... | collective-permute-start | bytes 49160 | tf_op jit(solution)/shard_map/ppermute | solution.py:14
  118.3 4.7 %collective-permute-start.15 = (bf16[8,32,128]{2,1,0:T(8,128)(2,1)S(1)}, bf16[8,32,128]{2,1,0:T(8,128)(2,1)S(1)}, u32[]{:S(2)}, u32[]{:S(2)}) collective-permute-start(bf16[8,32,128]{2,1,0:T(8,128)(2,1)S(1)} %copy.231), channel_id=1, source_target_pairs={{0,4},{4,0},{8,12},{12,8},{16,20},{20,16},{24,28},{28,24},{1,5},{5... | collective-permute-start | bytes 196616 | tf_op jit(solution)/shard_map/ppermute | solution.py:18
  123.2 9.2 %copy-start.5 = (f32[8,32,128]{2,1,0:T(8,128)S(1)}, f32[8,32,128]{2,1,0:T(8,128)}, u32[]{:S(2)}) copy-start(f32[8,32,128]{2,1,0:T(8,128)} %copy-done.4) | copy-start | bytes 393220
  (8 other events, 13.0 us)

commit v5 on v4

--- a/solution.py
+++ b/solution.py
@@ -92,9 +92,15 @@
     target = contact_owner[:, 0]
     choose = (target[:, None] == jnp.arange(groups, dtype=jnp.int32)[None, :]).astype(jnp.int32)
     rank = jnp.sum((jnp.cumsum(choose, axis=0) - choose) * choose, axis=1)
-    send_set = jnp.zeros((groups, CAP, B, B), jnp.bfloat16).at[target, rank].set(contact_tiles)
+    slot_of = target * CAP + rank
+    pick = slot_of[None, :] == jnp.arange(groups * CAP, dtype=jnp.int32)[:, None]
+    send_set = jnp.einsum(
+        "sc,cij->sij", pick.astype(jnp.bfloat16), contact_tiles, preferred_element_type=jnp.float32
+    ).astype(jnp.bfloat16).reshape(groups, CAP, B, B)
     labels = jnp.stack([contact_anode, contact_bnode], axis=1)
-    send_labels = jnp.zeros((groups, CAP, 2), jnp.int32).at[target, rank].set(labels)
+    send_labels = jnp.sum(
+        jnp.where(pick[:, :, None], labels[None, :, :], 0), axis=1
+    ).reshape(groups, CAP, 2)
     got_set, got_labels = (
         lax.all_to_all(send_set, "rep", split_axis=0, concat_axis=0, tiled=True),
         lax.all_to_all(send_labels, "rep", split_axis=0, concat_axis=0, tiled=True),

time: 134 us -> 140 us (1.045)
  other arithmetic: 5.43 us -> 10.6 us
  matrix products: 17.6 us -> 22.5 us
  waiting for transfers between devices: 26.4 us -> 23.7 us
    scatter x3 -> x0, local copies, waits for them, and re-layouts: 4.75 us -> none  [the longest x1 2.75 us: body(): jnp.zeros((groups, CAP, B, B), jnp.bfloat16).at[target, rank]]
    all_to_all x1, waiting for transfers between devices: 12.1 us -> 9.76 us  [body(): lax.all_to_all(send_set, 'rep', split_axis=0, concat_axis=0, tiled=True)]
    gather x8, local copies, waits for them, and re-layouts: 7.93 us -> 10.3 us  [contact_pairs(): difference = (vector[near_index] - other[far_index]).astype(jnp.bfloat16)]
    reshape x0 -> x3, local copies, waits for them, and re-layouts: none -> 1.86 us  [the longest x1 1.17 us: body(): send_set = jnp.einsum('sc,cij->sij', pick.astype(jnp.bfloat16), contact_t...]
  transfers between devices with their start and end apart: 18 -> 18, of which waited for: 8 -> 8; matrix products, arithmetic and copies ran while one was open for 15% -> 21% of each run, Pallas kernels for 0% -> 0%
where the time goes in v5:
time: 140 us; the launch traced here: 139 us
  blocking collectives  37.6 us (27%)
  waiting for transfers between devices  23.7 us (17%)
  starting transfers between devices  23.5 us (17%)
  matrix products  22.5 us (16%)
  local copies, waits for them, and re-layouts  19.6 us (14%)
  other arithmetic  10.6 us (8%)
    all_to_all x4, blocking collectives, total(): gathered = lax.all_to_all(spread, ('dom', 'rep'), 0, 0, tiled=True)  37.6 us
    ppermute x8, waiting for transfers between devices, partner(): lax.ppermute(value, axis, [(i, i ^ 1 << distance) for i in range(lax.axis...  11.5 us
    gather x8, local copies, waits for them, and re-layouts, contact_pairs(): difference = (vector[near_index] - other[far_index]).astype(jnp.bfloat16)  10.3 us
    all_to_all x1, waiting for transfers between devices, body(): lax.all_to_all(send_set, 'rep', split_axis=0, concat_axis=0, tiled=True)  9.76 us
    ppermute x8, starting transfers between devices, partner(): lax.ppermute(value, axis, [(i, i ^ 1 << distance) for i in range(lax.axis...  8.63 us
    dot_general x4, matrix products, contact_pairs(): jnp.einsum('srj,skj->srk', multiplier, contact_set, preferred_element_typ...  7.28 us
    ppermute x8, starting transfers between devices, from_behind(): return lax.ppermute(value, axis, pairs)  7.14 us
    dot_general x8, matrix products, collect(): jnp.einsum('sn,srk->nrk', onehot, values, precision=lax.Precision.HIGHEST)  4.66 us
  transfers between devices with their start and end apart: 18, of which 8 were waited for; matrix products, arithmetic and copies ran while one was open for 21% of the time, Pallas kernels for 0%

profile of v5, /device:TPU:0, one launch (start us, length us, event | category | flops | bytes accessed | tf_op | source)
XLA Modules:
  0.0 138.9 jit_solution(2134042694250570311)
XLA Ops:
  4.5 4.2 %all-to-all-start = ((s32[4,8,2]{1,2,0:T(2,128)}), s32[4,8,2]{1,2,0:T(2,128)S(1)}, u32[]{:S(2)}, u32[]{:S(2)}) async-start(s32[4,8,2]{1,2,0:T(2,128)} %copy.140), calls=%async_computation | async-start | bytes 8192 | tf_op jit(solution)/shard_map/all_to_all | solution.py:106
  9.7 2.1 %collective-permute-start.2 = (bf16[8,32,128]{2,1,0:T(8,128)(2,1)S(1)}, bf16[8,32,128]{2,1,0:T(8,128)(2,1)}, u32[]{:S(2)}, u32[]{:S(2)}) collective-permute-start(bf16[8,32,128]{2,1,0:T(8,128)(2,1)S(1)} %get-tuple-element.127), channel_id=1, source_target_pairs={{0,4},{4,0},{8,12},{12,8},{16,20},{20,16},{24,28},{28,24},{1,5},{5... | collective-permute-start | bytes 196616 | tf_op jit(solution)/shard_map/ppermute | solution.py:18
  13.4 1.6 %collective-permute-start.1 = (f32[32,128]{1,0:T(8,128)S(1)}, f32[32,128]{1,0:T(8,128)S(1)}, u32[]{:S(2)}, u32[]{:S(2)}) collective-permute-start(f32[32,128]{1,0:T(8,128)S(1)} %fusion.75), channel_id=1, source_target_pairs={{0,3},{1,0},{2,1},{3,2},{4,7},{5,4},{6,5},{7,6},{8,11},{9,8},{10,9... | collective-permute-start | bytes 49160 | tf_op jit(solution)/shard_map/ppermute | solution.py:14
  21.1 3.5 %all-to-all-start.1 = ((bf16[4,8,128,128]{3,1,2,0:T(8,128)(2,1)}), bf16[4,8,128,128]{3,1,2,0:T(8,128)(2,1)S(1)}, u32[]{:S(2)}, u32[]{:S(2)}) async-start(bf16[4,8,128,128]{3,1,2,0:T(8,128)(2,1)} %copy.143), calls=%async_computation.1 | async-start | bytes 2097152 | tf_op jit(solution)/shard_map/all_to_all | solution.py:105
  29.3 9.8 %all-to-all-done.1 = bf16[4,8,128,128]{3,1,2,0:T(8,128)(2,1)S(1)} async-done(((bf16[4,8,128,128]{3,1,2,0:T(8,128)(2,1)}), bf16[4,8,128,128]{3,1,2,0:T(8,128)(2,1)S(1)}, u32[]{:S(2)}, u32[]{:S(2)}) %all-to-all-start.1) | async-done | bytes 1048608 | tf_op jit(solution)/shard_map/all_to_all | solution.py:105
  39.3 2.1 %fusion.1 = f32[32,32,128]{2,1,0:T(8,128)S(1)} fusion(bf16[32,128,128]{2,1,0:T(8,128)(2,1)S(1)} %bitcast.277, f32[32,32,128]{2,1,0:T(8,128)} %gather_fusion.1, f32[32,32,128]{2,1,0:T(8,128)} %gather_fusion.2), kind=kOutput, calls=%fused_computation.18 | convolution fusion | flops 67502080 | bytes 2621440 | tf_op jit(solution)/shard_map/srj,skj->srk/dot_general | solution.py:47
  42.7 3.7 %collective-permute-done.3 = bf16[8,32,128]{2,1,0:T(8,128)(2,1)S(1)} collective-permute-done((bf16[8,32,128]{2,1,0:T(8,128)(2,1)S(1)}, bf16[8,32,128]{2,1,0:T(8,128)(2,1)S(1)}, u32[]{:S(2)}, u32[]{:S(2)}) %collective-permute-start.3) | collective-permute-done | bytes 65568 | tf_op jit(solution)/shard_map/ppermute | solution.py:18
  46.7 10.9 %all_to_all.30 = f32[32,1,128]{2,1,0:T(1,128)S(1)} all-to-all(f32[32,1,128]{2,1,0:T(1,128)S(1)} %reshape.548), channel_id=1, replica_groups=mesh['dom'=8,'rep'=4] {'dom','rep'}, dimensions={0} | all-to-all | bytes 32768 | tf_op jit(solution)/shard_map/all_to_all | solution.py:24
  60.9 1.5 %gather_fusion.4 = f32[32,32,128]{2,1,0:T(8,128)} fusion(f32[8,32,128]{2,1,0:T(8,128)S(1)} %get-tuple-element.122, s32[1024]{0:T(1024)} %copy-done.14), kind=kCustom, calls=%fused_computation.4 | custom fusion | bytes 1048704 | tf_op jit(solution)/shard_map/gather | solution.py:43
  62.8 1.7 %collective-permute-start.5 = (f32[32,128]{1,0:T(8,128)S(1)}, f32[32,128]{1,0:T(8,128)S(1)}, u32[]{:S(2)}, u32[]{:S(2)}) collective-permute-start(f32[32,128]{1,0:T(8,128)S(1)} %fusion.72), channel_id=1, source_target_pairs={{0,3},{1,0},{2,1},{3,2},{4,7},{5,4},{6,5},{7,6},{8,11},{9,8},{10,9... | collective-permute-start | bytes 49160 | tf_op jit(solution)/shard_map/ppermute | solution.py:14
  67.6 2.1 %fusion.2 = f32[32,32,128]{2,1,0:T(8,128)S(1)} fusion(bf16[32,128,128]{2,1,0:T(8,128)(2,1)S(1)} %bitcast.278, f32[32,32,128]{2,1,0:T(8,128)} %gather_fusion.4, f32[32,32,128]{2,1,0:T(8,128)} %gather_fusion.5), kind=kOutput, calls=%fused_computation.19 | convolution fusion | flops 67502080 | bytes 2621440 | tf_op jit(solution)/shard_map/srj,skj->srk/dot_general | solution.py:47
  70.3 1.5 %collective-permute-start.7 = (bf16[8,32,128]{2,1,0:T(8,128)(2,1)S(1)}, bf16[8,32,128]{2,1,0:T(8,128)(2,1)S(1)}, u32[]{:S(2)}, u32[]{:S(2)}) collective-permute-start(bf16[8,32,128]{2,1,0:T(8,128)(2,1)S(1)} %copy.249), channel_id=1, source_target_pairs={{0,4},{4,0},{8,12},{12,8},{16,20},{20,16},{24,28},{28,24},{1,5},{5... | collective-permute-start | bytes 196616 | tf_op jit(solution)/shard_map/ppermute | solution.py:18
  72.4 2.6 %collective-permute-done.7 = bf16[8,32,128]{2,1,0:T(8,128)(2,1)S(1)} collective-permute-done((bf16[8,32,128]{2,1,0:T(8,128)(2,1)S(1)}, bf16[8,32,128]{2,1,0:T(8,128)(2,1)S(1)}, u32[]{:S(2)}, u32[]{:S(2)}) %collective-permute-start.7) | collective-permute-done | bytes 65568 | tf_op jit(solution)/shard_map/ppermute | solution.py:18
  75.4 8.8 %all_to_all.31 = f32[32,1,128]{2,1,0:T(1,128)S(1)} all-to-all(f32[32,1,128]{2,1,0:T(1,128)S(1)} %reshape.550), channel_id=1, replica_groups=mesh['dom'=8,'rep'=4] {'dom','rep'}, dimensions={0} | all-to-all | bytes 32768 | tf_op jit(solution)/shard_map/all_to_all | solution.py:24
  87.0 1.5 %gather_fusion.7 = f32[32,32,128]{2,1,0:T(8,128)} fusion(f32[8,32,128]{2,1,0:T(8,128)S(1)} %get-tuple-element.116, s32[1024]{0:T(1024)} %copy-done.14), kind=kCustom, calls=%fused_computation.7 | custom fusion | bytes 1048704 | tf_op jit(solution)/shard_map/gather | solution.py:43
  89.0 1.7 %collective-permute-start.9 = (f32[32,128]{1,0:T(8,128)S(1)}, f32[32,128]{1,0:T(8,128)S(1)}, u32[]{:S(2)}, u32[]{:S(2)}) collective-permute-start(f32[32,128]{1,0:T(8,128)S(1)} %fusion.69), channel_id=1, source_target_pairs={{0,3},{1,0},{2,1},{3,2},{4,7},{5,4},{6,5},{7,6},{8,11},{9,8},{10,9... | collective-permute-start | bytes 49160 | tf_op jit(solution)/shard_map/ppermute | solution.py:14
  94.4 2.1 %fusion.3 = f32[32,32,128]{2,1,0:T(8,128)S(1)} fusion(bf16[32,128,128]{2,1,0:T(8,128)(2,1)S(1)} %bitcast.279, f32[32,32,128]{2,1,0:T(8,128)} %gather_fusion.7, f32[32,32,128]{2,1,0:T(8,128)} %gather_fusion.8), kind=kOutput, calls=%fused_computation.20 | convolution fusion | flops 67502080 | bytes 2621440 | tf_op jit(solution)/shard_map/srj,skj->srk/dot_general | solution.py:47
  97.1 1.5 %collective-permute-start.11 = (bf16[8,32,128]{2,1,0:T(8,128)(2,1)S(1)}, bf16[8,32,128]{2,1,0:T(8,128)(2,1)S(1)}, u32[]{:S(2)}, u32[]{:S(2)}) collective-permute-start(bf16[8,32,128]{2,1,0:T(8,128)(2,1)S(1)} %copy.248), channel_id=1, source_target_pairs={{0,4},{4,0},{8,12},{12,8},{16,20},{20,16},{24,28},{28,24},{1,5},{5... | collective-permute-start | bytes 196616 | tf_op jit(solution)/shard_map/ppermute | solution.py:18
  99.2 2.6 %collective-permute-done.11 = bf16[8,32,128]{2,1,0:T(8,128)(2,1)S(1)} collective-permute-done((bf16[8,32,128]{2,1,0:T(8,128)(2,1)S(1)}, bf16[8,32,128]{2,1,0:T(8,128)(2,1)S(1)}, u32[]{:S(2)}, u32[]{:S(2)}) %collective-permute-start.11) | collective-permute-done | bytes 65568 | tf_op jit(solution)/shard_map/ppermute | solution.py:18
  102.2 8.8 %all_to_all.32 = f32[32,1,128]{2,1,0:T(1,128)S(1)} all-to-all(f32[32,1,128]{2,1,0:T(1,128)S(1)} %reshape.552), channel_id=1, replica_groups=mesh['dom'=8,'rep'=4] {'dom','rep'}, dimensions={0} | all-to-all | bytes 32768 | tf_op jit(solution)/shard_map/all_to_all | solution.py:24
  117.9 1.7 %collective-permute-start.13 = (f32[32,128]{1,0:T(8,128)S(1)}, f32[32,128]{1,0:T(8,128)S(1)}, u32[]{:S(2)}, u32[]{:S(2)}) collective-permute-start(f32[32,128]{1,0:T(8,128)S(1)} %fusion.66), channel_id=1, source_target_pairs={{0,3},{1,0},{2,1},{3,2},{4,7},{5,4},{6,5},{7,6},{8,11},{9,8},{10,9... | collective-permute-start | bytes 49160 | tf_op jit(solution)/shard_map/ppermute | solution.py:14
  124.1 1.5 %collective-permute-start.15 = (bf16[8,32,128]{2,1,0:T(8,128)(2,1)S(1)}, bf16[8,32,128]{2,1,0:T(8,128)(2,1)S(1)}, u32[]{:S(2)}, u32[]{:S(2)}) collective-permute-start(bf16[8,32,128]{2,1,0:T(8,128)(2,1)S(1)} %copy.247), channel_id=1, source_target_pairs={{0,4},{4,0},{8,12},{12,8},{16,20},{20,16},{24,28},{28,24},{1,5},{5... | collective-permute-start | bytes 196616 | tf_op jit(solution)/shard_map/ppermute | solution.py:18
  126.2 2.6 %collective-permute-done.15 = bf16[8,32,128]{2,1,0:T(8,128)(2,1)S(1)} collective-permute-done((bf16[8,32,128]{2,1,0:T(8,128)(2,1)S(1)}, bf16[8,32,128]{2,1,0:T(8,128)(2,1)S(1)}, u32[]{:S(2)}, u32[]{:S(2)}) %collective-permute-start.15) | collective-permute-done | bytes 65568 | tf_op jit(solution)/shard_map/ppermute | solution.py:18
  129.0 8.9 %all_to_all.33 = f32[32,2,32]{2,1,0:T(2,128)S(1)} all-to-all(f32[32,2,32]{2,1,0:T(2,128)S(1)} %broadcast_in_dim.37), channel_id=1, replica_groups=mesh['dom'=8,'rep'=4] {'dom','rep'}, dimensions={0} | all-to-all | bytes 16384 | tf_op jit(solution)/shard_map/all_to_all | solution.py:24
  (182 shorter events, 48.1 us)
Async XLA Ops:
  0.6 18.7 %copy-start = (bf16[16,128,128]{2,1,0:T(8,128)(2,1)S(1)}, bf16[16,128,128]{2,1,0:T(8,128)(2,1)}, u32[]{:S(2)}) copy-start(bf16[16,128,128]{2,1,0:T(8,128)(2,1)} %param.32) | copy-start | bytes 1572868
  0.6 17.7 %copy-start.1 = (bf16[8,2,128,128]{3,2,1,0:T(8,128)(2,1)S(1)}, bf16[8,2,128,128]{3,2,1,0:T(8,128)(2,1)}, u32[]{:S(2)}) copy-start(bf16[8,2,128,128]{3,2,1,0:T(8,128)(2,1)} %param.29) | copy-start | bytes 1572868
  4.5 16.5 %all-to-all-start = ((s32[4,8,2]{1,2,0:T(2,128)}), s32[4,8,2]{1,2,0:T(2,128)S(1)}, u32[]{:S(2)}, u32[]{:S(2)}) async-start(s32[4,8,2]{1,2,0:T(2,128)} %copy.140), calls=%async_computation | async-start | bytes 8192 | tf_op jit(solution)/shard_map/all_to_all | solution.py:106
  9.7 17.3 %collective-permute-start.2 = (bf16[8,32,128]{2,1,0:T(8,128)(2,1)S(1)}, bf16[8,32,128]{2,1,0:T(8,128)(2,1)}, u32[]{:S(2)}, u32[]{:S(2)}) collective-permute-start(bf16[8,32,128]{2,1,0:T(8,128)(2,1)S(1)} %get-tuple-element.127), channel_id=1, source_target_pairs={{0,4},{4,0},{8,12},{12,8},{16,20},{20,16},{24,28},{28,24},{1,5},{5... | collective-permute-start | bytes 196616 | tf_op jit(solution)/shard_map/ppermute | solution.py:18
  12.4 13.8 %collective-permute-start = (bf16[32,128]{1,0:T(8,128)(2,1)}, bf16[32,128]{1,0:T(8,128)(2,1)}, u32[]{:S(2)}, u32[]{:S(2)}) collective-permute-start(bf16[32,128]{1,0:T(8,128)(2,1)} %slice_bitcast_fusion.11), channel_id=1, source_target_pairs={{0,1},{1,2},{2,3},{3,0},{4,5},{5,6},{6,7},{7,4},{8,9},{9,10},{10,1... | collective-permute-start | bytes 24584 | tf_op jit(solution)/shard_map/ppermute | solution.py:14
  13.4 13.6 %collective-permute-start.1 = (f32[32,128]{1,0:T(8,128)S(1)}, f32[32,128]{1,0:T(8,128)S(1)}, u32[]{:S(2)}, u32[]{:S(2)}) collective-permute-start(f32[32,128]{1,0:T(8,128)S(1)} %fusion.75), channel_id=1, source_target_pairs={{0,3},{1,0},{2,1},{3,2},{4,7},{5,4},{6,5},{7,6},{8,11},{9,8},{10,9... | collective-permute-start | bytes 49160 | tf_op jit(solution)/shard_map/ppermute | solution.py:14
  21.1 18.0 %all-to-all-start.1 = ((bf16[4,8,128,128]{3,1,2,0:T(8,128)(2,1)}), bf16[4,8,128,128]{3,1,2,0:T(8,128)(2,1)S(1)}, u32[]{:S(2)}, u32[]{:S(2)}) async-start(bf16[4,8,128,128]{3,1,2,0:T(8,128)(2,1)} %copy.143), calls=%async_computation.1 | async-start | bytes 2097152 | tf_op jit(solution)/shard_map/all_to_all | solution.py:105
  42.0 4.3 %collective-permute-start.3 = (bf16[8,32,128]{2,1,0:T(8,128)(2,1)S(1)}, bf16[8,32,128]{2,1,0:T(8,128)(2,1)S(1)}, u32[]{:S(2)}, u32[]{:S(2)}) collective-permute-start(bf16[8,32,128]{2,1,0:T(8,128)(2,1)S(1)} %copy.250), channel_id=1, source_target_pairs={{0,4},{4,0},{8,12},{12,8},{16,20},{20,16},{24,28},{28,24},{1,5},{5... | collective-permute-start | bytes 196616 | tf_op jit(solution)/shard_map/ppermute | solution.py:18
  42.1 17.6 %copy-start.2 = (bf16[8,128,128]{2,1,0:T(8,128)(2,1)S(1)}, bf16[8,128,128]{2,1,0:T(8,128)(2,1)}, u32[]{:S(2)}) copy-start(bf16[8,128,128]{2,1,0:T(8,128)(2,1)} %param.28) | copy-start | bytes 786436
  59.1 7.0 %collective-permute-start.6 = (bf16[8,32,128]{2,1,0:T(8,128)(2,1)S(1)}, bf16[8,32,128]{2,1,0:T(8,128)(2,1)S(1)}, u32[]{:S(2)}, u32[]{:S(2)}) collective-permute-start(bf16[8,32,128]{2,1,0:T(8,128)(2,1)S(1)} %get-tuple-element.121), channel_id=1, source_target_pairs={{0,4},{4,0},{8,12},{12,8},{16,20},{20,16},{24,28},{28,24},{1,5},{5... | collective-permute-start | bytes 196616 | tf_op jit(solution)/shard_map/ppermute | solution.py:18
  62.8 3.1 %collective-permute-start.4 = (bf16[32,128]{1,0:T(8,128)(2,1)S(1)}, bf16[32,128]{1,0:T(8,128)(2,1)S(1)}, u32[]{:S(2)}, u32[]{:S(2)}) collective-permute-start(bf16[32,128]{1,0:T(8,128)(2,1)S(1)} %slice_bitcast_fusion.8), channel_id=1, source_target_pairs={{0,1},{1,2},{2,3},{3,0},{4,5},{5,6},{6,7},{7,4},{8,9},{9,10},{10,1... | collective-permute-start | bytes 24584 | tf_op jit(solution)/shard_map/ppermute | solution.py:14
  62.8 3.2 %collective-permute-start.5 = (f32[32,128]{1,0:T(8,128)S(1)}, f32[32,128]{1,0:T(8,128)S(1)}, u32[]{:S(2)}, u32[]{:S(2)}) collective-permute-start(f32[32,128]{1,0:T(8,128)S(1)} %fusion.72), channel_id=1, source_target_pairs={{0,3},{1,0},{2,1},{3,2},{4,7},{5,4},{6,5},{7,6},{8,11},{9,8},{10,9... | collective-permute-start | bytes 49160 | tf_op jit(solution)/shard_map/ppermute | solution.py:14
  70.3 4.7 %collective-permute-start.7 = (bf16[8,32,128]{2,1,0:T(8,128)(2,1)S(1)}, bf16[8,32,128]{2,1,0:T(8,128)(2,1)S(1)}, u32[]{:S(2)}, u32[]{:S(2)}) collective-permute-start(bf16[8,32,128]{2,1,0:T(8,128)(2,1)S(1)} %copy.249), channel_id=1, source_target_pairs={{0,4},{4,0},{8,12},{12,8},{16,20},{20,16},{24,28},{28,24},{1,5},{5... | collective-permute-start | bytes 196616 | tf_op jit(solution)/shard_map/ppermute | solution.py:18
  85.2 7.6 %collective-permute-start.10 = (bf16[8,32,128]{2,1,0:T(8,128)(2,1)S(1)}, bf16[8,32,128]{2,1,0:T(8,128)(2,1)S(1)}, u32[]{:S(2)}, u32[]{:S(2)}) collective-permute-start(bf16[8,32,128]{2,1,0:T(8,128)(2,1)S(1)} %get-tuple-element.115), channel_id=1, source_target_pairs={{0,4},{4,0},{8,12},{12,8},{16,20},{20,16},{24,28},{28,24},{1,5},{5... | collective-permute-start | bytes 196616 | tf_op jit(solution)/shard_map/ppermute | solution.py:18
  88.9 3.1 %collective-permute-start.8 = (bf16[32,128]{1,0:T(8,128)(2,1)S(1)}, bf16[32,128]{1,0:T(8,128)(2,1)S(1)}, u32[]{:S(2)}, u32[]{:S(2)}) collective-permute-start(bf16[32,128]{1,0:T(8,128)(2,1)S(1)} %slice_bitcast_fusion.5), channel_id=1, source_target_pairs={{0,1},{1,2},{2,3},{3,0},{4,5},{5,6},{6,7},{7,4},{8,9},{9,10},{10,1... | collective-permute-start | bytes 24584 | tf_op jit(solution)/shard_map/ppermute | solution.py:14
  89.0 3.2 %collective-permute-start.9 = (f32[32,128]{1,0:T(8,128)S(1)}, f32[32,128]{1,0:T(8,128)S(1)}, u32[]{:S(2)}, u32[]{:S(2)}) collective-permute-start(f32[32,128]{1,0:T(8,128)S(1)} %fusion.69), channel_id=1, source_target_pairs={{0,3},{1,0},{2,1},{3,2},{4,7},{5,4},{6,5},{7,6},{8,11},{9,8},{10,9... | collective-permute-start | bytes 49160 | tf_op jit(solution)/shard_map/ppermute | solution.py:14
  97.1 4.7 %collective-permute-start.11 = (bf16[8,32,128]{2,1,0:T(8,128)(2,1)S(1)}, bf16[8,32,128]{2,1,0:T(8,128)(2,1)S(1)}, u32[]{:S(2)}, u32[]{:S(2)}) collective-permute-start(bf16[8,32,128]{2,1,0:T(8,128)(2,1)S(1)} %copy.248), channel_id=1, source_target_pairs={{0,4},{4,0},{8,12},{12,8},{16,20},{20,16},{24,28},{28,24},{1,5},{5... | collective-permute-start | bytes 196616 | tf_op jit(solution)/shard_map/ppermute | solution.py:18
  112.0 9.1 %collective-permute-start.14 = (bf16[8,32,128]{2,1,0:T(8,128)(2,1)S(1)}, bf16[8,32,128]{2,1,0:T(8,128)(2,1)S(1)}, u32[]{:S(2)}, u32[]{:S(2)}) collective-permute-start(bf16[8,32,128]{2,1,0:T(8,128)(2,1)S(1)} %get-tuple-element.109), channel_id=1, source_target_pairs={{0,4},{4,0},{8,12},{12,8},{16,20},{20,16},{24,28},{28,24},{1,5},{5... | collective-permute-start | bytes 196616 | tf_op jit(solution)/shard_map/ppermute | solution.py:18
  117.8 3.1 %collective-permute-start.12 = (bf16[32,128]{1,0:T(8,128)(2,1)S(1)}, bf16[32,128]{1,0:T(8,128)(2,1)S(1)}, u32[]{:S(2)}, u32[]{:S(2)}) collective-permute-start(bf16[32,128]{1,0:T(8,128)(2,1)S(1)} %slice_bitcast_fusion.2), channel_id=1, source_target_pairs={{0,1},{1,2},{2,3},{3,0},{4,5},{5,6},{6,7},{7,4},{8,9},{9,10},{10,1... | collective-permute-start | bytes 24584 | tf_op jit(solution)/shard_map/ppermute | solution.py:14
  117.9 3.2 %collective-permute-start.13 = (f32[32,128]{1,0:T(8,128)S(1)}, f32[32,128]{1,0:T(8,128)S(1)}, u32[]{:S(2)}, u32[]{:S(2)}) collective-permute-start(f32[32,128]{1,0:T(8,128)S(1)} %fusion.66), channel_id=1, source_target_pairs={{0,3},{1,0},{2,1},{3,2},{4,7},{5,4},{6,5},{7,6},{8,11},{9,8},{10,9... | collective-permute-start | bytes 49160 | tf_op jit(solution)/shard_map/ppermute | solution.py:14
  123.4 14.6 %copy-start.5 = (f32[8,32,128]{2,1,0:T(8,128)S(1)}, f32[8,32,128]{2,1,0:T(8,128)}, u32[]{:S(2)}) copy-start(f32[8,32,128]{2,1,0:T(8,128)} %param.26) | copy-start | bytes 393220
  123.4 14.6 %copy-start.9 = (f32[8,32,128]{2,1,0:T(8,128)S(1)}, f32[8,32,128]{2,1,0:T(8,128)}, u32[]{:S(2)}) copy-start(f32[8,32,128]{2,1,0:T(8,128)} %copy-done.8) | copy-start | bytes 393220
  123.5 14.6 %copy-start.16 = (f32[32]{0:T(128)S(1)}, f32[32]{0:T(128)}, u32[]{:S(2)}) copy-start(f32[32]{0:T(128)} %copy-done.15) | copy-start | bytes 388
  124.1 4.7 %collective-permute-start.15 = (bf16[8,32,128]{2,1,0:T(8,128)(2,1)S(1)}, bf16[8,32,128]{2,1,0:T(8,128)(2,1)S(1)}, u32[]{:S(2)}, u32[]{:S(2)}) collective-permute-start(bf16[8,32,128]{2,1,0:T(8,128)(2,1)S(1)} %copy.247), channel_id=1, source_target_pairs={{0,4},{4,0},{8,12},{12,8},{16,20},{20,16},{24,28},{28,24},{1,5},{5... | collective-permute-start | bytes 196616 | tf_op jit(solution)/shard_map/ppermute | solution.py:18
  (16 other events, 75.6 us)

commit v6 on v5

--- a/solution.py
+++ b/solution.py
@@ -101,10 +101,15 @@
     send_labels = jnp.sum(
         jnp.where(pick[:, :, None], labels[None, :, :], 0), axis=1
     ).reshape(groups, CAP, 2)
-    got_set, got_labels = (
-        lax.all_to_all(send_set, "rep", split_axis=0, concat_axis=0, tiled=True),
-        lax.all_to_all(send_labels, "rep", split_axis=0, concat_axis=0, tiled=True),
-    )
+    lane = lax.axis_index("rep")
+    got_set = [jnp.take(send_set, lane, axis=0)]
+    got_labels = [jnp.take(send_labels, lane, axis=0)]
+    for shift in range(1, groups):
+        ahead = (lane + shift) % groups
+        got_set.append(from_behind(jnp.take(send_set, ahead, axis=0), "rep", shift))
+        got_labels.append(from_behind(jnp.take(send_labels, ahead, axis=0), "rep", shift))
+    got_set = jnp.stack(got_set)
+    got_labels = jnp.stack(got_labels)
     slots = groups * CAP
     contact_set = got_set.reshape(slots, B, B)
     got_labels = got_labels.reshape(slots, 2)

time: 140 us -> 130 us (0.929)
  local copies, waits for them, and re-layouts: 19.6 us -> 15.2 us
  waiting for transfers between devices: 23.7 us -> 20.5 us
  starting transfers between devices: 23.5 us -> 21.1 us
  blocking collectives: 37.6 us -> 39.6 us
  matrix products: 22.5 us -> 21 us
    all_to_all x2 -> x0, waiting for transfers between devices: 9.76 us -> none  [the longest x1 9.76 us: body(): lax.all_to_all(send_set, 'rep', split_axis=0, concat_axis=0, tiled=True)]
    ppermute x8 -> x14, waiting for transfers between devices: 2.47 us -> 10.3 us  [from_behind(): return lax.ppermute(value, axis, pairs)]
    all_to_all x2 -> x0, starting transfers between devices: 7.72 us -> none  [the longest x1 4.21 us: body(): lax.all_to_all(send_labels, 'rep', split_axis=0, concat_axis=0, tiled=True)]
    ppermute x8 -> x14, starting transfers between devices: 7.14 us -> 11.4 us  [from_behind(): return lax.ppermute(value, axis, pairs)]
    all_to_all x4, blocking collectives: 37.6 us -> 39.6 us  [total(): gathered = lax.all_to_all(spread, ('dom', 'rep'), 0, 0, tiled=True)]
    unnamed x51, local copies, waits for them, and re-layouts: 2.73 us -> 0.79 us
  transfers between devices with their start and end apart: 18 -> 22, of which waited for: 8 -> 11; matrix products, arithmetic and copies ran while one was open for 21% -> 16% of each run, Pallas kernels for 0% -> 0%
where the time goes in v6:
time: 130 us; the launch traced here: 129 us
  blocking collectives  39.6 us (30%)
  starting transfers between devices  21.1 us (16%)
  matrix products  21 us (16%)
  waiting for transfers between devices  20.5 us (16%)
  local copies, waits for them, and re-layouts  15.2 us (12%)
  other arithmetic  10.4 us (8%)
  between operations  1.38 us (1%)
    all_to_all x4, blocking collectives, total(): gathered = lax.all_to_all(spread, ('dom', 'rep'), 0, 0, tiled=True)  39.6 us
    ppermute x14, starting transfers between devices, from_behind(): return lax.ppermute(value, axis, pairs)  11.4 us
    ppermute x14, waiting for transfers between devices, from_behind(): return lax.ppermute(value, axis, pairs)  10.3 us
    ppermute x8, waiting for transfers between devices, partner(): lax.ppermute(value, axis, [(i, i ^ 1 << distance) for i in range(lax.axis...  10.2 us
    ppermute x8, starting transfers between devices, partner(): lax.ppermute(value, axis, [(i, i ^ 1 << distance) for i in range(lax.axis...  9.64 us
    gather x8, local copies, waits for them, and re-layouts, contact_pairs(): difference = (vector[near_index] - other[far_index]).astype(jnp.bfloat16)  9.51 us
    dot_general x4, matrix products, contact_pairs(): jnp.einsum('srj,skj->srk', multiplier, contact_set, preferred_element_typ...  8.16 us
    dot_general x8, matrix products, collect(): jnp.einsum('sn,srk->nrk', onehot, values, precision=lax.Precision.HIGHEST)  4.66 us
  transfers between devices with their start and end apart: 22, of which 11 were waited for; matrix products, arithmetic and copies ran while one was open for 16% of the time, Pallas kernels for 0%

profile of v6, /device:TPU:0, one launch (start us, length us, event | category | flops | bytes accessed | tf_op | source)
XLA Modules:
  0.0 129.2 jit_solution(2097704334308225753)
XLA Ops:
  3.7 2.4 %collective-permute-start.8 = (bf16[8,128,128]{2,0,1:T(8,128)(2,1)S(1)}, bf16[8,128,128]{2,0,1:T(8,128)(2,1)}, u32[]{:S(2)}, u32[]{:S(2)}) collective-permute-start(bf16[8,128,128]{2,0,1:T(8,128)(2,1)S(1)} %select_bitcast_fusion), channel_id=1, source_target_pairs={{0,3},{1,0},{2,1},{3,2},{4,7},{5,4},{6,5},{7,6},{8,11},{9,8},{10,9... | collective-permute-start | bytes 786440 | tf_op jit(solution)/shard_map/ppermute | solution.py:14
  8.1 1.8 %collective-permute-start.3 = (s32[8,2]{0,1:T(2,128)S(1)}, s32[8,2]{0,1:T(2,128)S(1)}, u32[]{:S(2)}, u32[]{:S(2)}) collective-permute-start(s32[8,2]{0,1:T(2,128)S(1)} %bitcast.335), channel_id=1, source_target_pairs={{0,2},{1,3},{2,0},{3,1},{4,6},{5,7},{6,4},{7,5},{8,10},{9,11},{10,... | collective-permute-start | bytes 200 | tf_op jit(solution)/shard_map/ppermute | solution.py:14
  9.9 1.6 %collective-permute-start.5 = (bf16[8,32,128]{2,1,0:T(8,128)(2,1)S(1)}, bf16[8,32,128]{2,1,0:T(8,128)(2,1)S(1)}, u32[]{:S(2)}, u32[]{:S(2)}) collective-permute-start(bf16[8,32,128]{2,1,0:T(8,128)(2,1)S(1)} %get-tuple-element.154), channel_id=1, source_target_pairs={{0,4},{4,0},{8,12},{12,8},{16,20},{20,16},{24,28},{28,24},{1,5},{5... | collective-permute-start | bytes 196616 | tf_op jit(solution)/shard_map/ppermute | solution.py:18
  13.6 2.2 %collective-permute-done.4 = s32[8,2]{0,1:T(2,128)S(1)} collective-permute-done((s32[8,2]{0,1:T(2,128)S(1)}, s32[8,2]{0,1:T(2,128)S(1)}, u32[]{:S(2)}, u32[]{:S(2)}) %collective-permute-start.4) | collective-permute-done | bytes 96 | tf_op jit(solution)/shard_map/ppermute | solution.py:14
  16.9 2.3 %collective-permute-done.2 = s32[8,2]{0,1:T(2,128)S(1)} collective-permute-done((s32[8,2]{0,1:T(2,128)S(1)}, s32[8,2]{0,1:T(2,128)S(1)}, u32[]{:S(2)}, u32[]{:S(2)}) %collective-permute-start.2) | collective-permute-done | bytes 96 | tf_op jit(solution)/shard_map/ppermute | solution.py:14
  19.9 3.1 %collective-permute-done = bf16[32,128]{1,0:T(8,128)(2,1)S(1)} collective-permute-done((bf16[32,128]{1,0:T(8,128)(2,1)S(1)}, bf16[32,128]{1,0:T(8,128)(2,1)S(1)}, u32[]{:S(2)}, u32[]{:S(2)}) %collective-permute-start) | collective-permute-done | bytes 8224 | tf_op jit(solution)/shard_map/ppermute | solution.py:14
  27.3 2.0 %fusion.1 = f32[32,32,128]{2,1,0:T(8,128)S(1)} fusion(bf16[32,128,128]{2,1,0:T(8,128)(2,1)S(1)} %bitcast.305, f32[32,32,128]{2,1,0:T(8,128)S(1)} %gather_fusion.1, f32[32,32,128]{2,1,0:T(8,128)} %gather_fusion.2), kind=kOutput, calls=%fused_computation.18 | convolution fusion | flops 67502080 | bytes 2621440 | tf_op jit(solution)/shard_map/srj,skj->srk/dot_general | solution.py:47
  29.9 1.6 %collective-permute-start.9 = (bf16[8,32,128]{2,1,0:T(8,128)(2,1)S(1)}, bf16[8,32,128]{2,1,0:T(8,128)(2,1)S(1)}, u32[]{:S(2)}, u32[]{:S(2)}) collective-permute-start(bf16[8,32,128]{2,1,0:T(8,128)(2,1)S(1)} %copy.230), channel_id=1, source_target_pairs={{0,4},{4,0},{8,12},{12,8},{16,20},{20,16},{24,28},{28,24},{1,5},{5... | collective-permute-start | bytes 196616 | tf_op jit(solution)/shard_map/ppermute | solution.py:18
  32.1 2.3 %collective-permute-done.9 = bf16[8,32,128]{2,1,0:T(8,128)(2,1)S(1)} collective-permute-done((bf16[8,32,128]{2,1,0:T(8,128)(2,1)S(1)}, bf16[8,32,128]{2,1,0:T(8,128)(2,1)S(1)}, u32[]{:S(2)}, u32[]{:S(2)}) %collective-permute-start.9) | collective-permute-done | bytes 65568 | tf_op jit(solution)/shard_map/ppermute | solution.py:18
  34.7 13.0 %all_to_all.20 = f32[32,1,128]{2,1,0:T(1,128)S(1)} all-to-all(f32[32,1,128]{2,1,0:T(1,128)S(1)} %reshape.702), channel_id=1, replica_groups=mesh['dom'=8,'rep'=4] {'dom','rep'}, dimensions={0} | all-to-all | bytes 32768 | tf_op jit(solution)/shard_map/all_to_all | solution.py:24
  52.8 1.7 %collective-permute-start.11 = (f32[32,128]{1,0:T(8,128)S(1)}, f32[32,128]{1,0:T(8,128)S(1)}, u32[]{:S(2)}, u32[]{:S(2)}) collective-permute-start(f32[32,128]{1,0:T(8,128)S(1)} %fusion.74), channel_id=1, source_target_pairs={{0,3},{1,0},{2,1},{3,2},{4,7},{5,4},{6,5},{7,6},{8,11},{9,8},{10,9... | collective-permute-start | bytes 49160 | tf_op jit(solution)/shard_map/ppermute | solution.py:14
  57.4 2.1 %fusion.2 = f32[32,32,128]{2,1,0:T(8,128)S(1)} fusion(bf16[32,128,128]{2,1,0:T(8,128)(2,1)S(1)} %bitcast.306, f32[32,32,128]{2,1,0:T(8,128)} %gather_fusion.4, f32[32,32,128]{2,1,0:T(8,128)} %gather_fusion.5), kind=kOutput, calls=%fused_computation.19 | convolution fusion | flops 67502080 | bytes 2621440 | tf_op jit(solution)/shard_map/srj,skj->srk/dot_general | solution.py:47
  62.3 2.6 %collective-permute-done.13 = bf16[8,32,128]{2,1,0:T(8,128)(2,1)S(1)} collective-permute-done((bf16[8,32,128]{2,1,0:T(8,128)(2,1)S(1)}, bf16[8,32,128]{2,1,0:T(8,128)(2,1)S(1)}, u32[]{:S(2)}, u32[]{:S(2)}) %collective-permute-start.13) | collective-permute-done | bytes 65568 | tf_op jit(solution)/shard_map/ppermute | solution.py:18
  65.3 8.8 %all_to_all.21 = f32[32,1,128]{2,1,0:T(1,128)S(1)} all-to-all(f32[32,1,128]{2,1,0:T(1,128)S(1)} %reshape.704), channel_id=1, replica_groups=mesh['dom'=8,'rep'=4] {'dom','rep'}, dimensions={0} | all-to-all | bytes 32768 | tf_op jit(solution)/shard_map/all_to_all | solution.py:24
  79.3 1.7 %collective-permute-start.15 = (f32[32,128]{1,0:T(8,128)S(1)}, f32[32,128]{1,0:T(8,128)S(1)}, u32[]{:S(2)}, u32[]{:S(2)}) collective-permute-start(f32[32,128]{1,0:T(8,128)S(1)} %fusion.71), channel_id=1, source_target_pairs={{0,3},{1,0},{2,1},{3,2},{4,7},{5,4},{6,5},{7,6},{8,11},{9,8},{10,9... | collective-permute-start | bytes 49160 | tf_op jit(solution)/shard_map/ppermute | solution.py:14
  84.0 2.1 %fusion.3 = f32[32,32,128]{2,1,0:T(8,128)S(1)} fusion(bf16[32,128,128]{2,1,0:T(8,128)(2,1)S(1)} %bitcast.307, f32[32,32,128]{2,1,0:T(8,128)} %gather_fusion.7, f32[32,32,128]{2,1,0:T(8,128)} %gather_fusion.8), kind=kOutput, calls=%fused_computation.20 | convolution fusion | flops 67502080 | bytes 2621440 | tf_op jit(solution)/shard_map/srj,skj->srk/dot_general | solution.py:47
  86.7 1.5 %collective-permute-start.17 = (bf16[8,32,128]{2,1,0:T(8,128)(2,1)S(1)}, bf16[8,32,128]{2,1,0:T(8,128)(2,1)S(1)}, u32[]{:S(2)}, u32[]{:S(2)}) collective-permute-start(bf16[8,32,128]{2,1,0:T(8,128)(2,1)S(1)} %copy.228), channel_id=1, source_target_pairs={{0,4},{4,0},{8,12},{12,8},{16,20},{20,16},{24,28},{28,24},{1,5},{5... | collective-permute-start | bytes 196616 | tf_op jit(solution)/shard_map/ppermute | solution.py:18
  88.8 2.6 %collective-permute-done.17 = bf16[8,32,128]{2,1,0:T(8,128)(2,1)S(1)} collective-permute-done((bf16[8,32,128]{2,1,0:T(8,128)(2,1)S(1)}, bf16[8,32,128]{2,1,0:T(8,128)(2,1)S(1)}, u32[]{:S(2)}, u32[]{:S(2)}) %collective-permute-start.17) | collective-permute-done | bytes 65568 | tf_op jit(solution)/shard_map/ppermute | solution.py:18
  91.8 8.8 %all_to_all.22 = f32[32,1,128]{2,1,0:T(1,128)S(1)} all-to-all(f32[32,1,128]{2,1,0:T(1,128)S(1)} %reshape.706), channel_id=1, replica_groups=mesh['dom'=8,'rep'=4] {'dom','rep'}, dimensions={0} | all-to-all | bytes 32768 | tf_op jit(solution)/shard_map/all_to_all | solution.py:24
  106.4 1.7 %collective-permute-start.19 = (f32[32,128]{1,0:T(8,128)S(1)}, f32[32,128]{1,0:T(8,128)S(1)}, u32[]{:S(2)}, u32[]{:S(2)}) collective-permute-start(f32[32,128]{1,0:T(8,128)S(1)} %fusion.68), channel_id=1, source_target_pairs={{0,3},{1,0},{2,1},{3,2},{4,7},{5,4},{6,5},{7,6},{8,11},{9,8},{10,9... | collective-permute-start | bytes 49160 | tf_op jit(solution)/shard_map/ppermute | solution.py:14
  111.8 2.0 %fusion.4 = f32[32,32,128]{2,1,0:T(8,128)S(1)} fusion(bf16[32,128,128]{2,1,0:T(8,128)(2,1)S(1)} %bitcast.308, f32[32,32,128]{2,1,0:T(8,128)S(1)} %gather_fusion.10, f32[32,32,128]{2,1,0:T(8,128)} %gather_fusion.11), kind=kOutput, calls=%fused_computation.21 | convolution fusion | flops 67502080 | bytes 2621440 | tf_op jit(solution)/shard_map/srj,skj->srk/dot_general | solution.py:47
  114.4 1.5 %collective-permute-start.21 = (bf16[8,32,128]{2,1,0:T(8,128)(2,1)S(1)}, bf16[8,32,128]{2,1,0:T(8,128)(2,1)S(1)}, u32[]{:S(2)}, u32[]{:S(2)}) collective-permute-start(bf16[8,32,128]{2,1,0:T(8,128)(2,1)S(1)} %copy.227), channel_id=1, source_target_pairs={{0,4},{4,0},{8,12},{12,8},{16,20},{20,16},{24,28},{28,24},{1,5},{5... | collective-permute-start | bytes 196616 | tf_op jit(solution)/shard_map/ppermute | solution.py:18
  116.6 2.6 %collective-permute-done.21 = bf16[8,32,128]{2,1,0:T(8,128)(2,1)S(1)} collective-permute-done((bf16[8,32,128]{2,1,0:T(8,128)(2,1)S(1)}, bf16[8,32,128]{2,1,0:T(8,128)(2,1)S(1)}, u32[]{:S(2)}, u32[]{:S(2)}) %collective-permute-start.21) | collective-permute-done | bytes 65568 | tf_op jit(solution)/shard_map/ppermute | solution.py:18
  119.4 8.9 %all_to_all.23 = f32[32,2,32]{2,1,0:T(2,128)S(1)} all-to-all(f32[32,2,32]{2,1,0:T(2,128)S(1)} %broadcast_in_dim.52), channel_id=1, replica_groups=mesh['dom'=8,'rep'=4] {'dom','rep'}, dimensions={0} | all-to-all | bytes 16384 | tf_op jit(solution)/shard_map/all_to_all | solution.py:24
  (193 shorter events, 46.7 us)
Async XLA Ops:
  3.7 22.2 %collective-permute-start.8 = (bf16[8,128,128]{2,0,1:T(8,128)(2,1)S(1)}, bf16[8,128,128]{2,0,1:T(8,128)(2,1)}, u32[]{:S(2)}, u32[]{:S(2)}) collective-permute-start(bf16[8,128,128]{2,0,1:T(8,128)(2,1)S(1)} %select_bitcast_fusion), channel_id=1, source_target_pairs={{0,3},{1,0},{2,1},{3,2},{4,7},{5,4},{6,5},{7,6},{8,11},{9,8},{10,9... | collective-permute-start | bytes 786440 | tf_op jit(solution)/shard_map/ppermute | solution.py:14
  7.1 18.8 %collective-permute-start.7 = (bf16[8,128,128]{2,0,1:T(8,128)(2,1)}, bf16[8,128,128]{2,0,1:T(8,128)(2,1)}, u32[]{:S(2)}, u32[]{:S(2)}) collective-permute-start(bf16[8,128,128]{2,0,1:T(8,128)(2,1)} %get-tuple-element.153), channel_id=1, source_target_pairs={{0,2},{1,3},{2,0},{3,1},{4,6},{5,7},{6,4},{7,5},{8,10},{9,11},{10,... | collective-permute-start | bytes 786440 | tf_op jit(solution)/shard_map/ppermute | solution.py:14
  8.0 7.8 %collective-permute-start.4 = (s32[8,2]{0,1:T(2,128)S(1)}, s32[8,2]{0,1:T(2,128)S(1)}, u32[]{:S(2)}, u32[]{:S(2)}) collective-permute-start(s32[8,2]{0,1:T(2,128)S(1)} %bitcast.336), channel_id=1, source_target_pairs={{0,3},{1,0},{2,1},{3,2},{4,7},{5,4},{6,5},{7,6},{8,11},{9,8},{10,9... | collective-permute-start | bytes 200 | tf_op jit(solution)/shard_map/ppermute | solution.py:14
  8.1 8.8 %collective-permute-start.3 = (s32[8,2]{0,1:T(2,128)S(1)}, s32[8,2]{0,1:T(2,128)S(1)}, u32[]{:S(2)}, u32[]{:S(2)}) collective-permute-start(s32[8,2]{0,1:T(2,128)S(1)} %bitcast.335), channel_id=1, source_target_pairs={{0,2},{1,3},{2,0},{3,1},{4,6},{5,7},{6,4},{7,5},{8,10},{9,11},{10,... | collective-permute-start | bytes 200 | tf_op jit(solution)/shard_map/ppermute | solution.py:14
  9.9 14.6 %collective-permute-start.5 = (bf16[8,32,128]{2,1,0:T(8,128)(2,1)S(1)}, bf16[8,32,128]{2,1,0:T(8,128)(2,1)S(1)}, u32[]{:S(2)}, u32[]{:S(2)}) collective-permute-start(bf16[8,32,128]{2,1,0:T(8,128)(2,1)S(1)} %get-tuple-element.154), channel_id=1, source_target_pairs={{0,4},{4,0},{8,12},{12,8},{16,20},{20,16},{24,28},{28,24},{1,5},{5... | collective-permute-start | bytes 196616 | tf_op jit(solution)/shard_map/ppermute | solution.py:18
  15.8 3.5 %collective-permute-start.2 = (s32[8,2]{0,1:T(2,128)S(1)}, s32[8,2]{0,1:T(2,128)S(1)}, u32[]{:S(2)}, u32[]{:S(2)}) collective-permute-start(s32[8,2]{0,1:T(2,128)S(1)} %bitcast.334), channel_id=1, source_target_pairs={{0,1},{1,2},{2,3},{3,0},{4,5},{5,6},{6,7},{7,4},{8,9},{9,10},{10,1... | collective-permute-start | bytes 200 | tf_op jit(solution)/shard_map/ppermute | solution.py:14
  16.9 9.0 %collective-permute-start.6 = (bf16[8,128,128]{2,0,1:T(8,128)(2,1)}, bf16[8,128,128]{2,0,1:T(8,128)(2,1)S(1)}, u32[]{:S(2)}, u32[]{:S(2)}) collective-permute-start(bf16[8,128,128]{2,0,1:T(8,128)(2,1)} %get-tuple-element.152), channel_id=1, source_target_pairs={{0,1},{1,2},{2,3},{3,0},{4,5},{5,6},{6,7},{7,4},{8,9},{9,10},{10,1... | collective-permute-start | bytes 786440 | tf_op jit(solution)/shard_map/ppermute | solution.py:14
  19.2 3.8 %collective-permute-start = (bf16[32,128]{1,0:T(8,128)(2,1)S(1)}, bf16[32,128]{1,0:T(8,128)(2,1)S(1)}, u32[]{:S(2)}, u32[]{:S(2)}) collective-permute-start(bf16[32,128]{1,0:T(8,128)(2,1)S(1)} %slice_bitcast_fusion.11), channel_id=1, source_target_pairs={{0,1},{1,2},{2,3},{3,0},{4,5},{5,6},{6,7},{7,4},{8,9},{9,10},{10,1... | collective-permute-start | bytes 24584 | tf_op jit(solution)/shard_map/ppermute | solution.py:14
  23.0 1.4 %collective-permute-start.1 = (f32[32,128]{1,0:T(8,128)S(1)}, f32[32,128]{1,0:T(8,128)S(1)}, u32[]{:S(2)}, u32[]{:S(2)}) collective-permute-start(f32[32,128]{1,0:T(8,128)S(1)} %fusion.77), channel_id=1, source_target_pairs={{0,3},{1,0},{2,1},{3,2},{4,7},{5,4},{6,5},{7,6},{8,11},{9,8},{10,9... | collective-permute-start | bytes 49160 | tf_op jit(solution)/shard_map/ppermute | solution.py:14
  29.9 4.5 %collective-permute-start.9 = (bf16[8,32,128]{2,1,0:T(8,128)(2,1)S(1)}, bf16[8,32,128]{2,1,0:T(8,128)(2,1)S(1)}, u32[]{:S(2)}, u32[]{:S(2)}) collective-permute-start(bf16[8,32,128]{2,1,0:T(8,128)(2,1)S(1)} %copy.230), channel_id=1, source_target_pairs={{0,4},{4,0},{8,12},{12,8},{16,20},{20,16},{24,28},{28,24},{1,5},{5... | collective-permute-start | bytes 196616 | tf_op jit(solution)/shard_map/ppermute | solution.py:18
  49.2 6.8 %collective-permute-start.12 = (bf16[8,32,128]{2,1,0:T(8,128)(2,1)S(1)}, bf16[8,32,128]{2,1,0:T(8,128)(2,1)S(1)}, u32[]{:S(2)}, u32[]{:S(2)}) collective-permute-start(bf16[8,32,128]{2,1,0:T(8,128)(2,1)S(1)} %get-tuple-element.145), channel_id=1, source_target_pairs={{0,4},{4,0},{8,12},{12,8},{16,20},{20,16},{24,28},{28,24},{1,5},{5... | collective-permute-start | bytes 196616 | tf_op jit(solution)/shard_map/ppermute | solution.py:18
  52.7 3.1 %collective-permute-start.10 = (bf16[32,128]{1,0:T(8,128)(2,1)S(1)}, bf16[32,128]{1,0:T(8,128)(2,1)S(1)}, u32[]{:S(2)}, u32[]{:S(2)}) collective-permute-start(bf16[32,128]{1,0:T(8,128)(2,1)S(1)} %slice_bitcast_fusion.8), channel_id=1, source_target_pairs={{0,1},{1,2},{2,3},{3,0},{4,5},{5,6},{6,7},{7,4},{8,9},{9,10},{10,1... | collective-permute-start | bytes 24584 | tf_op jit(solution)/shard_map/ppermute | solution.py:14
  52.8 3.2 %collective-permute-start.11 = (f32[32,128]{1,0:T(8,128)S(1)}, f32[32,128]{1,0:T(8,128)S(1)}, u32[]{:S(2)}, u32[]{:S(2)}) collective-permute-start(f32[32,128]{1,0:T(8,128)S(1)} %fusion.74), channel_id=1, source_target_pairs={{0,3},{1,0},{2,1},{3,2},{4,7},{5,4},{6,5},{7,6},{8,11},{9,8},{10,9... | collective-permute-start | bytes 49160 | tf_op jit(solution)/shard_map/ppermute | solution.py:14
  60.2 4.7 %collective-permute-start.13 = (bf16[8,32,128]{2,1,0:T(8,128)(2,1)S(1)}, bf16[8,32,128]{2,1,0:T(8,128)(2,1)S(1)}, u32[]{:S(2)}, u32[]{:S(2)}) collective-permute-start(bf16[8,32,128]{2,1,0:T(8,128)(2,1)S(1)} %copy.229), channel_id=1, source_target_pairs={{0,4},{4,0},{8,12},{12,8},{16,20},{20,16},{24,28},{28,24},{1,5},{5... | collective-permute-start | bytes 196616 | tf_op jit(solution)/shard_map/ppermute | solution.py:18
  75.1 7.5 %collective-permute-start.16 = (bf16[8,32,128]{2,1,0:T(8,128)(2,1)S(1)}, bf16[8,32,128]{2,1,0:T(8,128)(2,1)S(1)}, u32[]{:S(2)}, u32[]{:S(2)}) collective-permute-start(bf16[8,32,128]{2,1,0:T(8,128)(2,1)S(1)} %get-tuple-element.139), channel_id=1, source_target_pairs={{0,4},{4,0},{8,12},{12,8},{16,20},{20,16},{24,28},{28,24},{1,5},{5... | collective-permute-start | bytes 196616 | tf_op jit(solution)/shard_map/ppermute | solution.py:18
  79.3 3.1 %collective-permute-start.14 = (bf16[32,128]{1,0:T(8,128)(2,1)S(1)}, bf16[32,128]{1,0:T(8,128)(2,1)S(1)}, u32[]{:S(2)}, u32[]{:S(2)}) collective-permute-start(bf16[32,128]{1,0:T(8,128)(2,1)S(1)} %slice_bitcast_fusion.5), channel_id=1, source_target_pairs={{0,1},{1,2},{2,3},{3,0},{4,5},{5,6},{6,7},{7,4},{8,9},{9,10},{10,1... | collective-permute-start | bytes 24584 | tf_op jit(solution)/shard_map/ppermute | solution.py:14
  79.3 3.2 %collective-permute-start.15 = (f32[32,128]{1,0:T(8,128)S(1)}, f32[32,128]{1,0:T(8,128)S(1)}, u32[]{:S(2)}, u32[]{:S(2)}) collective-permute-start(f32[32,128]{1,0:T(8,128)S(1)} %fusion.71), channel_id=1, source_target_pairs={{0,3},{1,0},{2,1},{3,2},{4,7},{5,4},{6,5},{7,6},{8,11},{9,8},{10,9... | collective-permute-start | bytes 49160 | tf_op jit(solution)/shard_map/ppermute | solution.py:14
  86.7 4.7 %collective-permute-start.17 = (bf16[8,32,128]{2,1,0:T(8,128)(2,1)S(1)}, bf16[8,32,128]{2,1,0:T(8,128)(2,1)S(1)}, u32[]{:S(2)}, u32[]{:S(2)}) collective-permute-start(bf16[8,32,128]{2,1,0:T(8,128)(2,1)S(1)} %copy.228), channel_id=1, source_target_pairs={{0,4},{4,0},{8,12},{12,8},{16,20},{20,16},{24,28},{28,24},{1,5},{5... | collective-permute-start | bytes 196616 | tf_op jit(solution)/shard_map/ppermute | solution.py:18
  101.6 8.0 %collective-permute-start.20 = (bf16[8,32,128]{2,1,0:T(8,128)(2,1)S(1)}, bf16[8,32,128]{2,1,0:T(8,128)(2,1)}, u32[]{:S(2)}, u32[]{:S(2)}) collective-permute-start(bf16[8,32,128]{2,1,0:T(8,128)(2,1)S(1)} %get-tuple-element.133), channel_id=1, source_target_pairs={{0,4},{4,0},{8,12},{12,8},{16,20},{20,16},{24,28},{28,24},{1,5},{5... | collective-permute-start | bytes 196616 | tf_op jit(solution)/shard_map/ppermute | solution.py:18
  106.3 3.1 %collective-permute-start.18 = (bf16[32,128]{1,0:T(8,128)(2,1)S(1)}, bf16[32,128]{1,0:T(8,128)(2,1)S(1)}, u32[]{:S(2)}, u32[]{:S(2)}) collective-permute-start(bf16[32,128]{1,0:T(8,128)(2,1)S(1)} %slice_bitcast_fusion.2), channel_id=1, source_target_pairs={{0,1},{1,2},{2,3},{3,0},{4,5},{5,6},{6,7},{7,4},{8,9},{9,10},{10,1... | collective-permute-start | bytes 24584 | tf_op jit(solution)/shard_map/ppermute | solution.py:14
  106.4 3.2 %collective-permute-start.19 = (f32[32,128]{1,0:T(8,128)S(1)}, f32[32,128]{1,0:T(8,128)S(1)}, u32[]{:S(2)}, u32[]{:S(2)}) collective-permute-start(f32[32,128]{1,0:T(8,128)S(1)} %fusion.68), channel_id=1, source_target_pairs={{0,3},{1,0},{2,1},{3,2},{4,7},{5,4},{6,5},{7,6},{8,11},{9,8},{10,9... | collective-permute-start | bytes 49160 | tf_op jit(solution)/shard_map/ppermute | solution.py:14
  113.8 14.6 %copy-start.6 = (f32[8,32,128]{2,1,0:T(8,128)S(1)}, f32[8,32,128]{2,1,0:T(8,128)}, u32[]{:S(2)}) copy-start(f32[8,32,128]{2,1,0:T(8,128)} %param.30) | copy-start | bytes 393220
  113.8 14.6 %copy-start.8 = (f32[8,32,128]{2,1,0:T(8,128)S(1)}, f32[8,32,128]{2,1,0:T(8,128)}, u32[]{:S(2)}) copy-start(f32[8,32,128]{2,1,0:T(8,128)} %copy-done.7) | copy-start | bytes 393220
  114.4 4.7 %collective-permute-start.21 = (bf16[8,32,128]{2,1,0:T(8,128)(2,1)S(1)}, bf16[8,32,128]{2,1,0:T(8,128)(2,1)S(1)}, u32[]{:S(2)}, u32[]{:S(2)}) collective-permute-start(bf16[8,32,128]{2,1,0:T(8,128)(2,1)S(1)} %copy.227), channel_id=1, source_target_pairs={{0,4},{4,0},{8,12},{12,8},{16,20},{20,16},{24,28},{28,24},{1,5},{5... | collective-permute-start | bytes 196616 | tf_op jit(solution)/shard_map/ppermute | solution.py:18
  (20 other events, 122.9 us)

commit v7 on v6

--- a/solution.py
+++ b/solution.py
@@ -39,21 +39,8 @@
     return result + jnp.einsum("pn,prj->nrj", onehot, mirror, precision=lax.Precision.HIGHEST)
 
 
-def contact_pairs(vector, other, near_index, far_index, contact_set):
-    difference = (vector[near_index] - other[far_index]).astype(jnp.bfloat16)
-    multiplier = jnp.einsum(
-        "srk,skj->srj", difference, contact_set, preferred_element_type=jnp.float32
-    ).astype(jnp.bfloat16)
-    return jnp.einsum("srj,skj->srk", multiplier, contact_set, preferred_element_type=jnp.float32)
-
-
-def collect(values, index, nodes):
-    onehot = (index[:, None] == jnp.arange(nodes, dtype=jnp.int32)[None, :]).astype(jnp.float32)
-    return jnp.einsum("sn,srk->nrk", onehot, values, precision=lax.Precision.HIGHEST)
-
-
 def apply_operator(
-    vector, diag_tiles, off_tiles, off_cols, link_tile, contact_set, near_index, far_index
+    vector, diag_tiles, off_tiles, off_cols, link_tile, contact_set, near_index, far_index, signs
 ):
     nodes = vector.shape[0]
     rounded = vector.astype(jnp.bfloat16)
@@ -66,13 +53,14 @@
     after = from_behind(back_term, "rep", -1)
     result = result.at[0].add(first_add)
     result = result.at[nodes - 1].add(after)
-    other = partner(vector.astype(jnp.bfloat16), "dom", 0).astype(vector.dtype)
-    terms = contact_pairs(vector, other, near_index, far_index, contact_set)
-    result = result + collect(terms, near_index, nodes)
-    far_terms = partner(collect(terms, far_index, nodes).astype(jnp.bfloat16), "dom", 0).astype(
-        jnp.float32
-    )
-    result = result - far_terms
+    other = partner(vector, "dom", 0)
+    field = jnp.concatenate([vector, other], axis=0)
+    difference = (field[near_index] - field[far_index]).astype(jnp.bfloat16)
+    multiplier = jnp.einsum(
+        "srk,skj->srj", difference, contact_set, preferred_element_type=jnp.float32
+    ).astype(jnp.bfloat16)
+    terms = jnp.einsum("srj,skj->srk", multiplier, contact_set, preferred_element_type=jnp.float32)
+    return result + jnp.einsum("sn,srk->nrk", signs, terms, precision=lax.Precision.HIGHEST)
     return result
 
 
@@ -108,13 +96,29 @@
         ahead = (lane + shift) % groups
         got_set.append(from_behind(jnp.take(send_set, ahead, axis=0), "rep", shift))
         got_labels.append(from_behind(jnp.take(send_labels, ahead, axis=0), "rep", shift))
+    rows = lax.axis_size("dom")
+    for shift in range(groups):
+        ahead = (lane + shift) % groups
+        pairs = [
+            (d * groups + q, (d ^ 1) * groups + (q + shift) % groups)
+            for d in range(rows)
+            for q in range(groups)
+        ]
+        got_set.append(lax.ppermute(jnp.take(send_set, ahead, axis=0), ("dom", "rep"), pairs))
+        got_labels.append(lax.ppermute(jnp.take(send_labels, ahead, axis=0), ("dom", "rep"), pairs))
     got_set = jnp.stack(got_set)
     got_labels = jnp.stack(got_labels)
-    slots = groups * CAP
+    slots = 2 * groups * CAP
+    nodes = rhs.shape[0]
     contact_set = got_set.reshape(slots, B, B)
-    got_labels = got_labels.reshape(slots, 2)
-    near_index = got_labels[:, 0]
-    far_index = got_labels[:, 1]
+    got_labels = got_labels.reshape(2, groups * CAP, 2)
+    near_index = jnp.concatenate([got_labels[0, :, 0], nodes + got_labels[1, :, 0]])
+    far_index = jnp.concatenate([nodes + got_labels[0, :, 1], got_labels[1, :, 1]])
+    own = jnp.arange(slots) < groups * CAP
+    local = jnp.where(own, near_index, far_index)
+    signs = jnp.where(own, 1.0, -1.0)[:, None] * (
+        local[:, None] == jnp.arange(nodes, dtype=jnp.int32)[None, :]
+    ).astype(jnp.float32)
     link_tile = link_tiles[0]
     scale = precond[:, None, :]
     solution = jnp.zeros_like(rhs)
@@ -131,6 +135,7 @@
             contact_set,
             near_index,
             far_index,
+            signs,
         )
         parts = [
             jnp.sum(direction * image, axis=(0, 2)),

time: 130 us -> 233 us (1.79)
  local copies, waits for them, and re-layouts: 15.2 us -> 42.7 us
  other arithmetic: 10.4 us -> 35.6 us
  matrix products: 21 us -> 45.3 us
  waiting for transfers between devices: 20.5 us -> 32.8 us
  starting transfers between devices: 21.1 us -> 30 us
  blocking collectives: 39.6 us -> 43.3 us
    ppermute x0 -> x8, waiting for transfers between devices: none -> 15.1 us  [the longest x4 7.91 us: body(): lax.ppermute(jnp.take(send_labels, ahead, axis=0), ('dom', 'rep'), pairs)]
    unnamed x51 -> x92, local copies, waits for them, and re-layouts: 0.79 us -> 15.7 us
    ppermute x0 -> x8, starting transfers between devices: none -> 14.6 us  [the longest x4 7.59 us: body(): lax.ppermute(jnp.take(send_set, ahead, axis=0), ('dom', 'rep'), pairs)]
    dot_general x12 -> x8, matrix products: 12.8 us -> 26.8 us  [the longest x4 17.2 us: apply_operator(): jnp.einsum('srj,skj->srk', multiplier, contact_set, preferred_element_typ...]
    ppermute x8 -> x4, starting transfers between devices: 9.64 us -> 3.74 us  [partner(): lax.ppermute(value, axis, [(i, i ^ 1 << distance) for i in range(lax.axis...]
    convert_element_type x4 -> x3, other arithmetic: 0.34 us -> 5.4 us  [apply_operator(): rounded = vector.astype(jnp.bfloat16)]
    gather x8, local copies, waits for them, and re-layouts: 9.51 us -> 14 us  [apply_operator(): difference = (field[near_index] - field[far_index]).astype(jnp.bfloat16)]
    reduce_sum x4 -> x3, other arithmetic: 1.2 us -> 5.29 us  [body(): jnp.sum(residual * preconditioned, axis=(0, 2))]
  transfers between devices with their start and end apart: 22 -> 26, of which waited for: 11 -> 14; matrix products, arithmetic and copies ran while one was open for 16% -> 12% of each run, Pallas kernels for 0% -> 0%
where the time goes in v7:
time: 233 us; the launch traced here: 231 us
  matrix products  45.3 us (19%)
  blocking collectives  43.3 us (19%)
  local copies, waits for them, and re-layouts  42.7 us (18%)
  other arithmetic  35.6 us (15%)
  waiting for transfers between devices  32.8 us (14%)
  starting transfers between devices  30 us (13%)
    all_to_all x4, blocking collectives, total(): gathered = lax.all_to_all(spread, ('dom', 'rep'), 0, 0, tiled=True)  43.3 us
    dot_general x4, matrix products, apply_operator(): jnp.einsum('srj,skj->srk', multiplier, contact_set, preferred_element_typ...  17.2 us
    unnamed x92, local copies, waits for them, and re-layouts  15.7 us
    gather x8, local copies, waits for them, and re-layouts, apply_operator(): difference = (field[near_index] - field[far_index]).astype(jnp.bfloat16)  14 us
    ppermute x14, starting transfers between devices, from_behind(): return lax.ppermute(value, axis, pairs)  11.7 us
    ppermute x4, waiting for transfers between devices, partner(): lax.ppermute(value, axis, [(i, i ^ 1 << distance) for i in range(lax.axis...  10.5 us
    dot_general x4, matrix products, apply_operator(): jnp.einsum('sn,srk->nrk', signs, terms, precision=lax.Precision.HIGHEST)  9.58 us
    ppermute x4, waiting for transfers between devices, body(): lax.ppermute(jnp.take(send_labels, ahead, axis=0), ('dom', 'rep'), pairs)  7.91 us
  transfers between devices with their start and end apart: 26, of which 14 were waited for; matrix products, arithmetic and copies ran while one was open for 12% of the time, Pallas kernels for 0%

profile of v7, /device:TPU:0, one launch (start us, length us, event | category | flops | bytes accessed | tf_op | source)
XLA Modules:
  0.0 230.9 jit_solution(4494373162350655560)
XLA Ops:
  6.0 3.7 %collective-permute-start.14 = (bf16[8,128,128]{2,1,0:T(8,128)(2,1)}, bf16[8,128,128]{2,1,0:T(8,128)(2,1)}, u32[]{:S(2)}, u32[]{:S(2)}) collective-permute-start(bf16[8,128,128]{2,1,0:T(8,128)(2,1)} %fusion.33), channel_id=1, source_target_pairs={{0,5},{1,6},{2,7},{3,4},{4,1},{5,2},{6,3},{7,0},{8,13},{9,14},{10,... | collective-permute-start | bytes 786440 | tf_op jit(solution)/shard_map/ppermute | solution.py:107
  23.5 2.7 %collective-permute-done.2 = s32[8,2]{0,1:T(2,128)S(1)} collective-permute-done((s32[8,2]{0,1:T(2,128)S(1)}, s32[8,2]{0,1:T(2,128)S(1)}, u32[]{:S(2)}, u32[]{:S(2)}) %collective-permute-start.2) | collective-permute-done | bytes 96 | tf_op jit(solution)/shard_map/ppermute | solution.py:14
  26.3 2.3 collective-permute-start.3
  38.9 2.9 %collective-permute-start.7 = (s32[8,2]{0,1:T(2,128)S(1)}, s32[8,2]{0,1:T(2,128)S(1)}, u32[]{:S(2)}, u32[]{:S(2)}) collective-permute-start(s32[8,2]{0,1:T(2,128)S(1)} %bitcast.360), channel_id=1, source_target_pairs={{0,6},{1,7},{2,4},{3,5},{4,2},{5,3},{6,0},{7,1},{8,14},{9,15},{10,... | collective-permute-start | bytes 200 | tf_op jit(solution)/shard_map/ppermute | solution.py:108
  43.4 3.0 %collective-permute-done.8 = s32[8,2]{0,1:T(2,128)S(1)} collective-permute-done((s32[8,2]{0,1:T(2,128)S(1)}, s32[8,2]{0,1:T(2,128)S(1)}, u32[]{:S(2)}, u32[]{:S(2)}) %collective-permute-start.8) | collective-permute-done | bytes 96 | tf_op jit(solution)/shard_map/ppermute | solution.py:108
  53.0 3.6 %collective-permute-done.9 = f32[8,32,128]{2,1,0:T(8,128)S(1)} collective-permute-done((f32[8,32,128]{2,1,0:T(8,128)}, f32[8,32,128]{2,1,0:T(8,128)S(1)}, u32[]{:S(2)}, u32[]{:S(2)}) %collective-permute-start.9) | collective-permute-done | bytes 131104 | tf_op jit(solution)/shard_map/ppermute | solution.py:18
  62.6 2.1 collective-permute-start.16
  68.1 7.2 %collective-permute-done.13 = bf16[8,128,128]{2,1,0:T(8,128)(2,1)S(1)} collective-permute-done((bf16[8,128,128]{2,1,0:T(8,128)(2,1)}, bf16[8,128,128]{2,1,0:T(8,128)(2,1)S(1)}, u32[]{:S(2)}, u32[]{:S(2)}) %collective-permute-start.13) | collective-permute-done | bytes 262176 | tf_op jit(solution)/shard_map/ppermute | solution.py:107
  77.3 4.3 %fusion.1 = f32[64,32,128]{2,1,0:T(8,128)} fusion(bf16[64,128,128]{2,1,0:T(8,128)(2,1)S(1)} %bitcast.329, f32[64,32,128]{2,1,0:T(8,128)} %gather_fusion.1, f32[64,32,128]{2,1,0:T(8,128)} %gather_fusion.2), kind=kOutput, calls=%fused_computation.18 | convolution fusion | flops 135004160 | bytes 5242880 | tf_op jit(solution)/shard_map/srj,skj->srk/dot_general | solution.py:62
  81.6 2.4 %fusion.27 = f32[8,32,128]{2,0,1:T(8,128)S(1)} fusion(f32[64,32,128]{2,1,0:T(8,128)} %fusion.1, f32[64]{0:T(128)} %compare_select_fusion.3, s32[64]{0:T(128)S(1)} %compare_select_fusion.4), kind=kOutput, calls=%fused_computation.52 | convolution fusion | flops 25166848 | bytes 1180160 | tf_op jit(solution)/shard_map/sn,srk->nrk/dot_general | solution.py:63
  85.3 13.9 %all_to_all.20 = f32[32,1,128]{2,1,0:T(1,128)S(1)} all-to-all(f32[32,1,128]{2,1,0:T(1,128)S(1)} %reshape.927), channel_id=1, replica_groups=mesh['dom'=8,'rep'=4] {'dom','rep'}, dimensions={0} | all-to-all | bytes 32768 | tf_op jit(solution)/shard_map/all_to_all | solution.py:24
  119.9 4.3 %fusion.2 = f32[64,32,128]{2,1,0:T(8,128)} fusion(bf16[64,128,128]{2,1,0:T(8,128)(2,1)S(1)} %bitcast.330, f32[64,32,128]{2,1,0:T(8,128)} %gather_fusion.4, f32[64,32,128]{2,1,0:T(8,128)} %gather_fusion.5), kind=kOutput, calls=%fused_computation.19 | convolution fusion | flops 135004160 | bytes 5242880 | tf_op jit(solution)/shard_map/srj,skj->srk/dot_general | solution.py:62
  124.2 2.4 %fusion.25 = f32[8,32,128]{2,0,1:T(8,128)S(1)} fusion(f32[64,32,128]{2,1,0:T(8,128)} %fusion.2, f32[64]{0:T(128)} %compare_select_fusion.3, s32[64]{0:T(128)S(1)} %compare_select_fusion.4), kind=kOutput, calls=%fused_computation.50 | convolution fusion | flops 25166848 | bytes 1180160 | tf_op jit(solution)/shard_map/sn,srk->nrk/dot_general | solution.py:63
  130.6 10.2 %all_to_all.21 = f32[32,1,128]{2,1,0:T(1,128)} all-to-all(f32[32,1,128]{2,1,0:T(1,128)} %reshape.929), channel_id=1, replica_groups=mesh['dom'=8,'rep'=4] {'dom','rep'}, dimensions={0} | all-to-all | bytes 32768 | tf_op jit(solution)/shard_map/all_to_all | solution.py:24
  149.8 2.1 gather_fusion.6
  159.5 2.5 %collective-permute-done.22 = f32[8,32,128]{2,1,0:T(8,128)S(1)} collective-permute-done((f32[8,32,128]{2,1,0:T(8,128)}, f32[8,32,128]{2,1,0:T(8,128)S(1)}, u32[]{:S(2)}, u32[]{:S(2)}) %collective-permute-start.22) | collective-permute-done | bytes 131104 | tf_op jit(solution)/shard_map/ppermute | solution.py:18
  165.5 4.3 %fusion.3 = f32[64,32,128]{2,1,0:T(8,128)} fusion(bf16[64,128,128]{2,1,0:T(8,128)(2,1)S(1)} %bitcast.331, f32[64,32,128]{2,1,0:T(8,128)} %gather_fusion.7, f32[64,32,128]{2,1,0:T(8,128)} %gather_fusion.8), kind=kOutput, calls=%fused_computation.20 | convolution fusion | flops 135004160 | bytes 5242880 | tf_op jit(solution)/shard_map/srj,skj->srk/dot_general | solution.py:62
  169.8 2.4 %fusion.23 = f32[8,32,128]{2,0,1:T(8,128)S(1)} fusion(f32[64,32,128]{2,1,0:T(8,128)} %fusion.3, f32[64]{0:T(128)} %compare_select_fusion.3, s32[64]{0:T(128)S(1)} %compare_select_fusion.4), kind=kOutput, calls=%fused_computation.48 | convolution fusion | flops 25166848 | bytes 1180160 | tf_op jit(solution)/shard_map/sn,srk->nrk/dot_general | solution.py:63
  176.3 10.3 %all_to_all.22 = f32[32,1,128]{2,1,0:T(1,128)} all-to-all(f32[32,1,128]{2,1,0:T(1,128)} %reshape.931), channel_id=1, replica_groups=mesh['dom'=8,'rep'=4] {'dom','rep'}, dimensions={0} | all-to-all | bytes 32768 | tf_op jit(solution)/shard_map/all_to_all | solution.py:24
  195.7 2.1 gather_fusion.9
  206.7 2.7 %collective-permute-done.25 = f32[8,32,128]{2,1,0:T(8,128)S(1)} collective-permute-done((f32[8,32,128]{2,1,0:T(8,128)}, f32[8,32,128]{2,1,0:T(8,128)S(1)}, u32[]{:S(2)}, u32[]{:S(2)}) %collective-permute-start.25) | collective-permute-done | bytes 131104 | tf_op jit(solution)/shard_map/ppermute | solution.py:18
  213.0 4.3 %fusion.4 = f32[64,32,128]{2,1,0:T(8,128)} fusion(bf16[64,128,128]{2,1,0:T(8,128)(2,1)S(1)} %bitcast.332, f32[64,32,128]{2,1,0:T(8,128)} %gather_fusion.10, f32[64,32,128]{2,1,0:T(8,128)} %gather_fusion.11), kind=kOutput, calls=%fused_computation.21 | convolution fusion | flops 135004160 | bytes 5242880 | tf_op jit(solution)/shard_map/srj,skj->srk/dot_general | solution.py:62
  217.3 2.4 %fusion.21 = f32[8,32,128]{2,0,1:T(8,128)S(1)} fusion(f32[64,32,128]{2,1,0:T(8,128)} %fusion.4, f32[64]{0:T(128)S(1)} %copy-done.28, s32[64]{0:T(128)S(1)} %compare_select_fusion.4), kind=kOutput, calls=%fused_computation.46 | convolution fusion | flops 25166848 | bytes 1180160 | tf_op jit(solution)/shard_map/sn,srk->nrk/dot_general | solution.py:63
  220.5 8.9 %all_to_all.23 = f32[32,2,32]{2,1,0:T(2,128)S(1)} all-to-all(f32[32,2,32]{2,1,0:T(2,128)S(1)} %broadcast_in_dim.62), channel_id=1, replica_groups=mesh['dom'=8,'rep'=4] {'dom','rep'}, dimensions={0} | all-to-all | bytes 16384 | tf_op jit(solution)/shard_map/all_to_all | solution.py:24
  (241 shorter events, 122.7 us)
Async XLA Ops:
  5.5 57.1 %collective-permute-start.10 = (bf16[8,128,128]{2,1,0:T(8,128)(2,1)}, bf16[8,128,128]{2,1,0:T(8,128)(2,1)}, u32[]{:S(2)}, u32[]{:S(2)}) collective-permute-start(bf16[8,128,128]{2,1,0:T(8,128)(2,1)} %fusion.33), channel_id=1, source_target_pairs={{0,1},{1,2},{2,3},{3,0},{4,5},{5,6},{6,7},{7,4},{8,9},{9,10},{10,1... | collective-permute-start | bytes 786440 | tf_op jit(solution)/shard_map/ppermute | solution.py:14
  6.0 69.3 %collective-permute-start.14 = (bf16[8,128,128]{2,1,0:T(8,128)(2,1)}, bf16[8,128,128]{2,1,0:T(8,128)(2,1)}, u32[]{:S(2)}, u32[]{:S(2)}) collective-permute-start(bf16[8,128,128]{2,1,0:T(8,128)(2,1)} %fusion.33), channel_id=1, source_target_pairs={{0,5},{1,6},{2,7},{3,4},{4,1},{5,2},{6,3},{7,0},{8,13},{9,14},{10,... | collective-permute-start | bytes 786440 | tf_op jit(solution)/shard_map/ppermute | solution.py:107
  10.4 55.3 %collective-permute-start.11 = (bf16[8,128,128]{2,1,0:T(8,128)(2,1)}, bf16[8,128,128]{2,1,0:T(8,128)(2,1)}, u32[]{:S(2)}, u32[]{:S(2)}) collective-permute-start(bf16[8,128,128]{2,1,0:T(8,128)(2,1)} %fusion.32), channel_id=1, source_target_pairs={{0,2},{1,3},{2,0},{3,1},{4,6},{5,7},{6,4},{7,5},{8,10},{9,11},{10,... | collective-permute-start | bytes 786440 | tf_op jit(solution)/shard_map/ppermute | solution.py:14
  11.0 65.3 %collective-permute-start.15 = (bf16[8,128,128]{2,1,0:T(8,128)(2,1)}, bf16[8,128,128]{2,1,0:T(8,128)(2,1)}, u32[]{:S(2)}, u32[]{:S(2)}) collective-permute-start(bf16[8,128,128]{2,1,0:T(8,128)(2,1)} %fusion.32), channel_id=1, source_target_pairs={{0,6},{1,7},{2,4},{3,5},{4,2},{5,3},{6,0},{7,1},{8,14},{9,15},{10,... | collective-permute-start | bytes 786440 | tf_op jit(solution)/shard_map/ppermute | solution.py:107
  12.7 13.6 %collective-permute-start.2 = (s32[8,2]{0,1:T(2,128)S(1)}, s32[8,2]{0,1:T(2,128)S(1)}, u32[]{:S(2)}, u32[]{:S(2)}) collective-permute-start(s32[8,2]{0,1:T(2,128)S(1)} %bitcast.361), channel_id=1, source_target_pairs={{0,1},{1,2},{2,3},{3,0},{4,5},{5,6},{6,7},{7,4},{8,9},{9,10},{10,1... | collective-permute-start | bytes 200 | tf_op jit(solution)/shard_map/ppermute | solution.py:14
  26.3 3.8 %collective-permute-start.3 = (s32[8,2]{0,1:T(2,128)S(1)}, s32[8,2]{0,1:T(2,128)S(1)}, u32[]{:S(2)}, u32[]{:S(2)}) collective-permute-start(s32[8,2]{0,1:T(2,128)S(1)} %bitcast.359), channel_id=1, source_target_pairs={{0,2},{1,3},{2,0},{3,1},{4,6},{5,7},{6,4},{7,5},{8,10},{9,11},{10,... | collective-permute-start | bytes 200 | tf_op jit(solution)/shard_map/ppermute | solution.py:14
  31.4 3.6 %collective-permute-start.5 = (s32[8,2]{0,1:T(2,128)S(1)}, s32[8,2]{0,1:T(2,128)S(1)}, u32[]{:S(2)}, u32[]{:S(2)}) collective-permute-start(s32[8,2]{0,1:T(2,128)S(1)} %bitcast.363), channel_id=1, source_target_pairs={{0,4},{1,5},{2,6},{3,7},{4,0},{5,1},{6,2},{7,3},{8,12},{9,13},{10,... | collective-permute-start | bytes 200 | tf_op jit(solution)/shard_map/ppermute | solution.py:108
  35.0 3.9 %collective-permute-start.6 = (s32[8,2]{0,1:T(2,128)S(1)}, s32[8,2]{0,1:T(2,128)S(1)}, u32[]{:S(2)}, u32[]{:S(2)}) collective-permute-start(s32[8,2]{0,1:T(2,128)S(1)} %bitcast.362), channel_id=1, source_target_pairs={{0,5},{1,6},{2,7},{3,4},{4,1},{5,2},{6,3},{7,0},{8,13},{9,14},{10,... | collective-permute-start | bytes 200 | tf_op jit(solution)/shard_map/ppermute | solution.py:108
  38.9 4.5 %collective-permute-start.7 = (s32[8,2]{0,1:T(2,128)S(1)}, s32[8,2]{0,1:T(2,128)S(1)}, u32[]{:S(2)}, u32[]{:S(2)}) collective-permute-start(s32[8,2]{0,1:T(2,128)S(1)} %bitcast.360), channel_id=1, source_target_pairs={{0,6},{1,7},{2,4},{3,5},{4,2},{5,3},{6,0},{7,1},{8,14},{9,15},{10,... | collective-permute-start | bytes 200 | tf_op jit(solution)/shard_map/ppermute | solution.py:108
  43.4 3.0 %collective-permute-start.8 = (s32[8,2]{0,1:T(2,128)S(1)}, s32[8,2]{0,1:T(2,128)S(1)}, u32[]{:S(2)}, u32[]{:S(2)}) collective-permute-start(s32[8,2]{0,1:T(2,128)S(1)} %bitcast.358), channel_id=1, source_target_pairs={{0,7},{1,4},{2,5},{3,6},{4,3},{5,0},{6,1},{7,2},{8,15},{9,12},{10,... | collective-permute-start | bytes 200 | tf_op jit(solution)/shard_map/ppermute | solution.py:108
  46.4 3.1 %collective-permute-start = (bf16[32,128]{1,0:T(8,128)(2,1)S(1)}, bf16[32,128]{1,0:T(8,128)(2,1)S(1)}, u32[]{:S(2)}, u32[]{:S(2)}) collective-permute-start(bf16[32,128]{1,0:T(8,128)(2,1)S(1)} %slice_bitcast_fusion.11), channel_id=1, source_target_pairs={{0,1},{1,2},{2,3},{3,0},{4,5},{5,6},{6,7},{7,4},{8,9},{9,10},{10,1... | collective-permute-start | bytes 24584 | tf_op jit(solution)/shard_map/ppermute | solution.py:14
  51.0 5.6 %collective-permute-start.9 = (f32[8,32,128]{2,1,0:T(8,128)}, f32[8,32,128]{2,1,0:T(8,128)S(1)}, u32[]{:S(2)}, u32[]{:S(2)}) collective-permute-start(f32[8,32,128]{2,1,0:T(8,128)} %get-tuple-element.155), channel_id=1, source_target_pairs={{0,4},{4,0},{8,12},{12,8},{16,20},{20,16},{24,28},{28,24},{1,5},{5... | collective-permute-start | bytes 393224 | tf_op jit(solution)/shard_map/ppermute | solution.py:18
  56.7 10.4 %collective-permute-start.12 = (bf16[8,128,128]{2,1,0:T(8,128)(2,1)}, bf16[8,128,128]{2,1,0:T(8,128)(2,1)}, u32[]{:S(2)}, u32[]{:S(2)}) collective-permute-start(bf16[8,128,128]{2,1,0:T(8,128)(2,1)} %fusion.31), channel_id=1, source_target_pairs={{0,3},{1,0},{2,1},{3,2},{4,7},{5,4},{6,5},{7,6},{8,11},{9,8},{10,9... | collective-permute-start | bytes 786440 | tf_op jit(solution)/shard_map/ppermute | solution.py:14
  62.6 14.7 %collective-permute-start.16 = (bf16[8,128,128]{2,1,0:T(8,128)(2,1)}, bf16[8,128,128]{2,1,0:T(8,128)(2,1)S(1)}, u32[]{:S(2)}, u32[]{:S(2)}) collective-permute-start(bf16[8,128,128]{2,1,0:T(8,128)(2,1)} %fusion.31), channel_id=1, source_target_pairs={{0,7},{1,4},{2,5},{3,6},{4,3},{5,0},{6,1},{7,2},{8,15},{9,12},{10,... | collective-permute-start | bytes 786440 | tf_op jit(solution)/shard_map/ppermute | solution.py:107
  65.7 9.5 %collective-permute-start.13 = (bf16[8,128,128]{2,1,0:T(8,128)(2,1)}, bf16[8,128,128]{2,1,0:T(8,128)(2,1)S(1)}, u32[]{:S(2)}, u32[]{:S(2)}) collective-permute-start(bf16[8,128,128]{2,1,0:T(8,128)(2,1)} %fusion.30), channel_id=1, source_target_pairs={{0,4},{1,5},{2,6},{3,7},{4,0},{5,1},{6,2},{7,3},{8,12},{9,13},{10,... | collective-permute-start | bytes 786440 | tf_op jit(solution)/shard_map/ppermute | solution.py:107
  109.6 3.5 %collective-permute-start.17 = (bf16[32,128]{1,0:T(8,128)(2,1)S(1)}, bf16[32,128]{1,0:T(8,128)(2,1)S(1)}, u32[]{:S(2)}, u32[]{:S(2)}) collective-permute-start(bf16[32,128]{1,0:T(8,128)(2,1)S(1)} %slice_bitcast_fusion.8), channel_id=1, source_target_pairs={{0,1},{1,2},{2,3},{3,0},{4,5},{5,6},{6,7},{7,4},{8,9},{9,10},{10,1... | collective-permute-start | bytes 24584 | tf_op jit(solution)/shard_map/ppermute | solution.py:14
  109.7 4.4 %collective-permute-start.18 = (f32[32,128]{1,0:T(8,128)S(1)}, f32[32,128]{1,0:T(8,128)S(1)}, u32[]{:S(2)}, u32[]{:S(2)}) collective-permute-start(f32[32,128]{1,0:T(8,128)S(1)} %fusion.65), channel_id=1, source_target_pairs={{0,3},{1,0},{2,1},{3,2},{4,7},{5,4},{6,5},{7,6},{8,11},{9,8},{10,9... | collective-permute-start | bytes 49160 | tf_op jit(solution)/shard_map/ppermute | solution.py:14
  111.4 5.0 %collective-permute-start.19 = (f32[8,32,128]{2,1,0:T(8,128)S(1)}, f32[8,32,128]{2,1,0:T(8,128)S(1)}, u32[]{:S(2)}, u32[]{:S(2)}) collective-permute-start(f32[8,32,128]{2,1,0:T(8,128)S(1)} %get-tuple-element.146), channel_id=1, source_target_pairs={{0,4},{4,0},{8,12},{12,8},{16,20},{20,16},{24,28},{28,24},{1,5},{5... | collective-permute-start | bytes 393224 | tf_op jit(solution)/shard_map/ppermute | solution.py:18
  155.0 3.7 %collective-permute-start.20 = (bf16[32,128]{1,0:T(8,128)(2,1)S(1)}, bf16[32,128]{1,0:T(8,128)(2,1)S(1)}, u32[]{:S(2)}, u32[]{:S(2)}) collective-permute-start(bf16[32,128]{1,0:T(8,128)(2,1)S(1)} %slice_bitcast_fusion.5), channel_id=1, source_target_pairs={{0,1},{1,2},{2,3},{3,0},{4,5},{5,6},{6,7},{7,4},{8,9},{9,10},{10,1... | collective-permute-start | bytes 24584 | tf_op jit(solution)/shard_map/ppermute | solution.py:14
  155.1 3.7 %collective-permute-start.21 = (f32[32,128]{1,0:T(8,128)S(1)}, f32[32,128]{1,0:T(8,128)S(1)}, u32[]{:S(2)}, u32[]{:S(2)}) collective-permute-start(f32[32,128]{1,0:T(8,128)S(1)} %fusion.62), channel_id=1, source_target_pairs={{0,3},{1,0},{2,1},{3,2},{4,7},{5,4},{6,5},{7,6},{8,11},{9,8},{10,9... | collective-permute-start | bytes 49160 | tf_op jit(solution)/shard_map/ppermute | solution.py:14
  156.8 5.2 %collective-permute-start.22 = (f32[8,32,128]{2,1,0:T(8,128)}, f32[8,32,128]{2,1,0:T(8,128)S(1)}, u32[]{:S(2)}, u32[]{:S(2)}) collective-permute-start(f32[8,32,128]{2,1,0:T(8,128)} %get-tuple-element.140), channel_id=1, source_target_pairs={{0,4},{4,0},{8,12},{12,8},{16,20},{20,16},{24,28},{28,24},{1,5},{5... | collective-permute-start | bytes 393224 | tf_op jit(solution)/shard_map/ppermute | solution.py:18
  202.4 3.5 %collective-permute-start.23 = (bf16[32,128]{1,0:T(8,128)(2,1)S(1)}, bf16[32,128]{1,0:T(8,128)(2,1)S(1)}, u32[]{:S(2)}, u32[]{:S(2)}) collective-permute-start(bf16[32,128]{1,0:T(8,128)(2,1)S(1)} %slice_bitcast_fusion.2), channel_id=1, source_target_pairs={{0,1},{1,2},{2,3},{3,0},{4,5},{5,6},{6,7},{7,4},{8,9},{9,10},{10,1... | collective-permute-start | bytes 24584 | tf_op jit(solution)/shard_map/ppermute | solution.py:14
  202.5 3.6 %collective-permute-start.24 = (f32[32,128]{1,0:T(8,128)S(1)}, f32[32,128]{1,0:T(8,128)S(1)}, u32[]{:S(2)}, u32[]{:S(2)}) collective-permute-start(f32[32,128]{1,0:T(8,128)S(1)} %fusion.59), channel_id=1, source_target_pairs={{0,3},{1,0},{2,1},{3,2},{4,7},{5,4},{6,5},{7,6},{8,11},{9,8},{10,9... | collective-permute-start | bytes 49160 | tf_op jit(solution)/shard_map/ppermute | solution.py:14
  204.2 5.2 %collective-permute-start.25 = (f32[8,32,128]{2,1,0:T(8,128)}, f32[8,32,128]{2,1,0:T(8,128)S(1)}, u32[]{:S(2)}, u32[]{:S(2)}) collective-permute-start(f32[8,32,128]{2,1,0:T(8,128)} %get-tuple-element.134), channel_id=1, source_target_pairs={{0,4},{4,0},{8,12},{12,8},{16,20},{20,16},{24,28},{28,24},{1,5},{5... | collective-permute-start | bytes 393224 | tf_op jit(solution)/shard_map/ppermute | solution.py:18
  (38 other events, 308.0 us)

commit v8 on v6

--- a/solution.py
+++ b/solution.py
@@ -25,55 +25,46 @@
     return jnp.sum(gathered, axis=0)
 
 
-def local_stiffness(rounded, diag_tiles, off_tiles, off_cols):
-    nodes = rounded.shape[0]
+def local_stiffness(rounded, diag_tiles, off_tiles, cols_onehot, mirror_onehot):
     result = jnp.einsum("nrk,nkj->nrj", rounded, diag_tiles, preferred_element_type=jnp.float32)
-    picked = rounded[off_cols]
+    picked = jnp.einsum(
+        "pn,nrk->prk", cols_onehot, rounded, preferred_element_type=jnp.float32
+    ).astype(jnp.bfloat16)
+    picked = picked.reshape(off_tiles.shape[0], off_tiles.shape[1], rounded.shape[1], rounded.shape[2])
     result = result + jnp.einsum(
         "nmrk,nmkj->nrj", picked, off_tiles, preferred_element_type=jnp.float32
     )
     mirror = jnp.einsum("nrk,nmjk->nmrj", rounded, off_tiles, preferred_element_type=jnp.float32)
-    flat_cols = off_cols.reshape(-1)
-    onehot = (flat_cols[:, None] == jnp.arange(nodes, dtype=jnp.int32)[None, :]).astype(jnp.float32)
-    mirror = mirror.reshape(flat_cols.shape[0], rounded.shape[1], rounded.shape[2])
-    return result + jnp.einsum("pn,prj->nrj", onehot, mirror, precision=lax.Precision.HIGHEST)
+    mirror = mirror.reshape(-1, rounded.shape[1], rounded.shape[2])
+    return result + jnp.einsum("pn,prj->nrj", mirror_onehot, mirror, precision=lax.Precision.HIGHEST)
 
 
-def contact_pairs(vector, other, near_index, far_index, contact_set):
-    difference = (vector[near_index] - other[far_index]).astype(jnp.bfloat16)
-    multiplier = jnp.einsum(
-        "srk,skj->srj", difference, contact_set, preferred_element_type=jnp.float32
-    ).astype(jnp.bfloat16)
-    return jnp.einsum("srj,skj->srk", multiplier, contact_set, preferred_element_type=jnp.float32)
-
-
-def collect(values, index, nodes):
-    onehot = (index[:, None] == jnp.arange(nodes, dtype=jnp.int32)[None, :]).astype(jnp.float32)
-    return jnp.einsum("sn,srk->nrk", onehot, values, precision=lax.Precision.HIGHEST)
-
-
-def apply_operator(
-    vector, diag_tiles, off_tiles, off_cols, link_tile, contact_set, near_index, far_index
-):
+def apply_operator(vector, diag_tiles, off_tiles, link_tile, contact_set, tables):
+    cols_onehot, mirror_onehot, near_onehot, far_onehot, near_collect, far_collect = tables
     nodes = vector.shape[0]
     rounded = vector.astype(jnp.bfloat16)
-    result = local_stiffness(rounded, diag_tiles, off_tiles, off_cols)
     before = from_behind(rounded[nodes - 1], "rep", 1)
-    first_add = jnp.dot(before, link_tile, preferred_element_type=jnp.float32)
     back_term = lax.dot_general(
         rounded[0], link_tile, (((1,), (1,)), ((), ())), preferred_element_type=jnp.float32
     )
     after = from_behind(back_term, "rep", -1)
+    other = partner(rounded, "dom", 0).astype(vector.dtype)
+    near = jnp.einsum("sn,nrk->srk", near_onehot, vector, precision=lax.Precision.HIGHEST)
+    far = jnp.einsum("sn,nrk->srk", far_onehot, other, precision=lax.Precision.HIGHEST)
+    difference = (near - far).astype(jnp.bfloat16)
+    multiplier = jnp.einsum(
+        "srk,skj->srj", difference, contact_set, preferred_element_type=jnp.float32
+    ).astype(jnp.bfloat16)
+    terms = jnp.einsum("srj,skj->srk", multiplier, contact_set, preferred_element_type=jnp.float32)
+    far_sum = jnp.einsum("sn,srk->nrk", far_collect, terms, precision=lax.Precision.HIGHEST)
+    far_sum, rounded = lax.optimization_barrier((far_sum.astype(jnp.bfloat16), rounded))
+    far_terms = partner(far_sum, "dom", 0).astype(jnp.float32)
+    result = local_stiffness(rounded, diag_tiles, off_tiles, cols_onehot, mirror_onehot)
+    first_add = jnp.dot(before, link_tile, preferred_element_type=jnp.float32)
     result = result.at[0].add(first_add)
     result = result.at[nodes - 1].add(after)
-    other = partner(vector.astype(jnp.bfloat16), "dom", 0).astype(vector.dtype)
-    terms = contact_pairs(vector, other, near_index, far_index, contact_set)
-    result = result + collect(terms, near_index, nodes)
-    far_terms = partner(collect(terms, far_index, nodes).astype(jnp.bfloat16), "dom", 0).astype(
-        jnp.float32
-    )
-    result = result - far_terms
-    return result
+    result = result + jnp.einsum("sn,srk->nrk", near_collect, terms, precision=lax.Precision.HIGHEST)
+    return result - far_terms
 
 
 def body(
@@ -115,6 +106,19 @@
     got_labels = got_labels.reshape(slots, 2)
     near_index = got_labels[:, 0]
     far_index = got_labels[:, 1]
+    nodes = rhs.shape[0]
+    blocks = jnp.arange(nodes, dtype=jnp.int32)[None, :]
+    near_collect = (near_index[:, None] == blocks).astype(jnp.float32)
+    far_collect = (far_index[:, None] == blocks).astype(jnp.float32)
+    mirror_onehot = (off_cols.reshape(-1)[:, None] == blocks).astype(jnp.float32)
+    tables = (
+        mirror_onehot.astype(jnp.bfloat16),
+        mirror_onehot,
+        near_collect,
+        far_collect,
+        near_collect,
+        far_collect,
+    )
     link_tile = link_tiles[0]
     scale = precond[:, None, :]
     solution = jnp.zeros_like(rhs)
@@ -122,16 +126,7 @@
     preconditioned = scale * residual
     direction = preconditioned
     for step in range(ITERS):
-        image = apply_operator(
-            direction,
-            diag_tiles,
-            off_tiles,
-            off_cols,
-            link_tile,
-            contact_set,
-            near_index,
-            far_index,
-        )
+        image = apply_operator(direction, diag_tiles, off_tiles, link_tile, contact_set, tables)
         parts = [
             jnp.sum(direction * image, axis=(0, 2)),
             jnp.sum(residual * preconditioned, axis=(0, 2)),

time: 130 us -> 127 us (0.977)
  matrix products: 21 us -> 28.1 us
  local copies, waits for them, and re-layouts: 15.2 us -> 8.46 us
  waiting for transfers between devices: 20.5 us -> 17.9 us
  blocking collectives: 39.6 us -> 37.6 us
  other arithmetic: 10.4 us -> 12.3 us
    gather x12 -> x0, local copies, waits for them, and re-layouts: 13.1 us -> none  [the longest x8 9.51 us: contact_pairs(): difference = (vector[near_index] - other[far_index]).astype(jnp.bfloat16)]
    dot_general x16 -> x28, matrix products: 14.3 us -> 23.9 us  [the longest x4 6.53 us: apply_operator(): jnp.einsum('srj,skj->srk', multiplier, contact_set, preferred_element_typ...]
    ppermute x8, waiting for transfers between devices: 10.2 us -> 5.9 us  [partner(): lax.ppermute(value, axis, [(i, i ^ 1 << distance) for i in range(lax.axis...]
    scatter-add x0 -> x8, local copies, waits for them, and re-layouts: none -> 3.7 us  [the longest x4 1.85 us: apply_operator(): result = result.at[0].add(first_add)]
    convert_element_type x4, other arithmetic: 0.34 us -> 3.22 us  [apply_operator(): rounded = vector.astype(jnp.bfloat16)]
    unnamed x51 -> x47, local copies, waits for them, and re-layouts: 0.79 us -> 3.64 us
    add x0 -> x8, other arithmetic: none -> 2.52 us  [the longest x4 2.45 us: apply_operator(): result = result.at[nodes - 1].add(after)]
    all_to_all x4, blocking collectives: 39.6 us -> 37.6 us  [total(): gathered = lax.all_to_all(spread, ('dom', 'rep'), 0, 0, tiled=True)]
  transfers between devices with their start and end apart: 22 -> 22, of which waited for: 11 -> 11; matrix products, arithmetic and copies ran while one was open for 16% -> 24% of each run, Pallas kernels for 0% -> 0%
where the time goes in v8:
time: 127 us
  blocking collectives  37.6 us (30%)
  matrix products  28.1 us (22%)
  starting transfers between devices  20.9 us (16%)
  waiting for transfers between devices  17.9 us (14%)
  other arithmetic  12.3 us (10%)
  local copies, waits for them, and re-layouts  8.46 us (7%)
  between operations  1.38 us (1%)
    all_to_all x4, blocking collectives, total(): gathered = lax.all_to_all(spread, ('dom', 'rep'), 0, 0, tiled=True)  37.6 us
    ppermute x14, starting transfers between devices, from_behind(): return lax.ppermute(value, axis, pairs)  13.1 us
    ppermute x14, waiting for transfers between devices, from_behind(): return lax.ppermute(value, axis, pairs)  12 us
    ppermute x8, starting transfers between devices, partner(): lax.ppermute(value, axis, [(i, i ^ 1 << distance) for i in range(lax.axis...  7.84 us
    dot_general x4, matrix products, apply_operator(): jnp.einsum('srj,skj->srk', multiplier, contact_set, preferred_element_typ...  6.53 us
    dot_general x4, matrix products, apply_operator(): jnp.einsum('sn,srk->nrk', near_collect, terms, precision=lax.Precision.HI...  6.21 us
    ppermute x8, waiting for transfers between devices, partner(): lax.ppermute(value, axis, [(i, i ^ 1 << distance) for i in range(lax.axis...  5.9 us
    dot_general x4, matrix products, apply_operator(): jnp.einsum('sn,srk->nrk', far_collect, terms, precision=lax.Precision.HIG...  3.64 us
  transfers between devices with their start and end apart: 22, of which 11 were waited for; matrix products, arithmetic and copies ran while one was open for 24% of the time, Pallas kernels for 0%

profile of v8, /device:TPU:0, one launch (start us, length us, event | category | flops | bytes accessed | tf_op | source)
XLA Modules:
  0.0 126.6 jit_solution(3509251597005514361)
XLA Ops:
  4.0 2.4 %collective-permute-start.2 = (s32[8,2]{0,1:T(2,128)S(1)}, s32[8,2]{0,1:T(2,128)S(1)}, u32[]{:S(2)}, u32[]{:S(2)}) collective-permute-start(s32[8,2]{0,1:T(2,128)S(1)} %bitcast.320), channel_id=1, source_target_pairs={{0,3},{1,0},{2,1},{3,2},{4,7},{5,4},{6,5},{7,6},{8,11},{9,8},{10,9... | collective-permute-start | bytes 200 | tf_op jit(solution)/shard_map/ppermute | solution.py:14
  8.2 1.6 %collective-permute-start.3 = (bf16[8,32,128]{2,0,1:T(8,128)(2,1)S(1)}, bf16[8,32,128]{2,0,1:T(8,128)(2,1)S(1)}, u32[]{:S(2)}, u32[]{:S(2)}) collective-permute-start(bf16[8,32,128]{2,0,1:T(8,128)(2,1)S(1)} %multiply_convert_fusion), channel_id=1, source_target_pairs={{0,4},{4,0},{8,12},{12,8},{16,20},{20,16},{24,28},{28,24},{1,5},{5... | collective-permute-start | bytes 196616 | tf_op jit(solution)/shard_map/ppermute | solution.py:18
  13.3 1.3 %collective-permute-start.5 = (bf16[8,128,128]{2,0,1:T(8,128)(2,1)S(1)}, bf16[8,128,128]{2,0,1:T(8,128)(2,1)S(1)}, u32[]{:S(2)}, u32[]{:S(2)}) collective-permute-start(bf16[8,128,128]{2,0,1:T(8,128)(2,1)S(1)} %get-tuple-element.174), channel_id=1, source_target_pairs={{0,2},{1,3},{2,0},{3,1},{4,6},{5,7},{6,4},{7,5},{8,10},{9,11},{10,... | collective-permute-start | bytes 786440 | tf_op jit(solution)/shard_map/ppermute | solution.py:14
  15.1 1.4 %collective-permute-start.6 = (bf16[8,128,128]{2,0,1:T(8,128)(2,1)S(1)}, bf16[8,128,128]{2,0,1:T(8,128)(2,1)S(1)}, u32[]{:S(2)}, u32[]{:S(2)}) collective-permute-start(bf16[8,128,128]{2,0,1:T(8,128)(2,1)S(1)} %select_bitcast_fusion), channel_id=1, source_target_pairs={{0,3},{1,0},{2,1},{3,2},{4,7},{5,4},{6,5},{7,6},{8,11},{9,8},{10,9... | collective-permute-start | bytes 786440 | tf_op jit(solution)/shard_map/ppermute | solution.py:14
  17.0 4.3 %collective-permute-done.4 = bf16[8,128,128]{2,0,1:T(8,128)(2,1)S(1)} collective-permute-done((bf16[8,128,128]{2,0,1:T(8,128)(2,1)S(1)}, bf16[8,128,128]{2,0,1:T(8,128)(2,1)S(1)}, u32[]{:S(2)}, u32[]{:S(2)}) %collective-permute-start.4) | collective-permute-done | bytes 262176 | tf_op jit(solution)/shard_map/ppermute | solution.py:14
  22.5 3.8 %collective-permute-done.6 = bf16[8,128,128]{2,0,1:T(8,128)(2,1)S(1)} collective-permute-done((bf16[8,128,128]{2,0,1:T(8,128)(2,1)S(1)}, bf16[8,128,128]{2,0,1:T(8,128)(2,1)S(1)}, u32[]{:S(2)}, u32[]{:S(2)}) %collective-permute-start.6) | collective-permute-done | bytes 262176 | tf_op jit(solution)/shard_map/ppermute | solution.py:14
  30.4 2.7 %collective-permute-done.9 = bf16[8,32,128]{2,0,1:T(8,128)(2,1)S(1)} collective-permute-done((bf16[8,32,128]{2,0,1:T(8,128)(2,1)S(1)}, bf16[8,32,128]{2,0,1:T(8,128)(2,1)S(1)}, u32[]{:S(2)}, u32[]{:S(2)}) %collective-permute-start.9) | collective-permute-done | bytes 65568 | tf_op jit(solution)/shard_map/ppermute | solution.py:18
  34.1 10.9 %all_to_all.20 = f32[32,1,128]{2,1,0:T(1,128)S(1)} all-to-all(f32[32,1,128]{2,1,0:T(1,128)S(1)} %reshape.615), channel_id=1, replica_groups=mesh['dom'=8,'rep'=4] {'dom','rep'}, dimensions={0} | all-to-all | bytes 32768 | tf_op jit(solution)/shard_map/all_to_all | solution.py:24
  47.6 1.7 %collective-permute-start.12 = (f32[32,128]{1,0:T(8,128)S(1)}, f32[32,128]{1,0:T(8,128)}, u32[]{:S(2)}, u32[]{:S(2)}) collective-permute-start(f32[32,128]{1,0:T(8,128)S(1)} %fusion.81), channel_id=1, source_target_pairs={{0,3},{1,0},{2,1},{3,2},{4,7},{5,4},{6,5},{7,6},{8,11},{9,8},{10,9... | collective-permute-start | bytes 49160 | tf_op jit(solution)/shard_map/ppermute | solution.py:14
  52.1 1.9 %fusion.6 = f32[32,32,128]{2,1,0:T(8,128)S(1)} fusion(bf16[32,128,128]{2,1,0:T(8,128)(2,1)S(1)} %bitcast.275, bf16[32,32,128]{2,0,1:T(8,128)(2,1)} %fusion.2), kind=kOutput, calls=%fused_computation.15 | convolution fusion | flops 67239936 | bytes 1835008 | tf_op jit(solution)/shard_map/srj,skj->srk/dot_general | solution.py:58
  54.0 1.2 convolution_convert_fusion.11
  58.7 1.6 %collective-permute-done.13 = bf16[8,32,128]{2,0,1:T(8,128)(2,1)} collective-permute-done((bf16[8,32,128]{2,0,1:T(8,128)(2,1)}, bf16[8,32,128]{2,0,1:T(8,128)(2,1)}, u32[]{:S(2)}, u32[]{:S(2)}) %collective-permute-start.13) | collective-permute-done | bytes 65568 | tf_op jit(solution)/shard_map/ppermute | solution.py:18
  60.3 2.2 %fusion.43 = (f32[32]{0:T(128)S(1)}, f32[32]{0:T(128)S(1)}, f32[32]{0:T(128)S(1)}, f32[32]{0:T(128)S(1)}, f32[8,32,128]{2,0,1:T(8,128)}) fusion(f32[8,32,128]{2,0,1:T(8,128)S(1)} %get-tuple-element.169, f32[8,128]{1,0:T(8,128)S(1)} %copy-done.8, f32[8,32,128]{2,0,1:T(8,128)S(1)} %get-tuple-element.168, bf16[8,32,128]{2,0,1:T(8,128)(2,1)} %collective-permute-done.13, ...), kind=kOutput, calls=%fused_computation.89 | convolution fusion | flops 13009024 | bytes 1118848 | tf_op jit(solution)/shard_map/sn,srk->nrk/dot_general | solution.py:66
  62.6 8.8 %all_to_all.21 = f32[32,1,128]{2,1,0:T(1,128)S(1)} all-to-all(f32[32,1,128]{2,1,0:T(1,128)S(1)} %reshape.617), channel_id=1, replica_groups=mesh['dom'=8,'rep'=4] {'dom','rep'}, dimensions={0} | all-to-all | bytes 32768 | tf_op jit(solution)/shard_map/all_to_all | solution.py:24
  74.0 1.7 %collective-permute-start.16 = (f32[32,128]{1,0:T(8,128)S(1)}, f32[32,128]{1,0:T(8,128)}, u32[]{:S(2)}, u32[]{:S(2)}) collective-permute-start(f32[32,128]{1,0:T(8,128)S(1)} %fusion.77), channel_id=1, source_target_pairs={{0,3},{1,0},{2,1},{3,2},{4,7},{5,4},{6,5},{7,6},{8,11},{9,8},{10,9... | collective-permute-start | bytes 49160 | tf_op jit(solution)/shard_map/ppermute | solution.py:14
  78.6 1.9 %fusion.7 = f32[32,32,128]{2,1,0:T(8,128)S(1)} fusion(bf16[32,128,128]{2,1,0:T(8,128)(2,1)S(1)} %bitcast.276, bf16[32,32,128]{2,0,1:T(8,128)(2,1)} %fusion.3), kind=kOutput, calls=%fused_computation.16 | convolution fusion | flops 67239936 | bytes 1835008 | tf_op jit(solution)/shard_map/srj,skj->srk/dot_general | solution.py:58
  84.9 1.6 %scatter-add.34 = f32[8,32,128]{2,0,1:T(8,128)} dynamic-update-slice(f32[8,32,128]{2,0,1:T(8,128)} %copy-done.7, f32[1,32,128]{2,0,1:T(1,128)S(1)} %slice_add_fusion.3, s32[]{:T(128)} %constant.228.clone.1, s32[]{:T(128)} %constant.228.clone.1, s32[]{:T(128)} %constant.228.clone.1) | dynamic-update-slice | bytes 32772 | tf_op jit(solution)/shard_map/scatter-add | solution.py:64
  87.4 1.6 %scatter-add.35 = f32[8,32,128]{2,0,1:T(8,128)} dynamic-update-slice(f32[8,32,128]{2,0,1:T(8,128)} %scatter-add.34, f32[1,32,128]{2,0,1:T(1,128)S(1)} %slice_add_fusion.2, s32[]{:T(128)} %constant.234.clone.1, s32[]{:T(128)} %constant.228.clone.1, s32[]{:T(128)} %constant.228.clone.1) | dynamic-update-slice | bytes 32772 | tf_op jit(solution)/shard_map/scatter-add | solution.py:65
  89.0 2.3 %fusion.45 = (f32[32]{0:T(128)S(1)}, f32[32]{0:T(128)S(1)}, f32[32]{0:T(128)S(1)}, f32[32]{0:T(128)S(1)}, f32[8,32,128]{2,0,1:T(8,128)}) fusion(f32[8,32,128]{2,0,1:T(8,128)S(1)} %get-tuple-element.164, f32[8,128]{1,0:T(8,128)S(1)} %copy-done.8, f32[8,32,128]{2,0,1:T(8,128)S(1)} %get-tuple-element.163, bf16[8,32,128]{2,0,1:T(8,128)(2,1)} %collective-permute-done.17, ...), kind=kOutput, calls=%fused_computation.91 | convolution fusion | flops 13009024 | bytes 1118848 | tf_op jit(solution)/shard_map/sn,srk->nrk/dot_general | solution.py:66
  91.5 8.8 %all_to_all.22 = f32[32,1,128]{2,1,0:T(1,128)S(1)} all-to-all(f32[32,1,128]{2,1,0:T(1,128)S(1)} %reshape.619), channel_id=1, replica_groups=mesh['dom'=8,'rep'=4] {'dom','rep'}, dimensions={0} | all-to-all | bytes 32768 | tf_op jit(solution)/shard_map/all_to_all | solution.py:24
  103.8 1.7 %collective-permute-start.20 = (f32[32,128]{1,0:T(8,128)S(1)}, f32[32,128]{1,0:T(8,128)}, u32[]{:S(2)}, u32[]{:S(2)}) collective-permute-start(f32[32,128]{1,0:T(8,128)S(1)} %fusion.73), channel_id=1, source_target_pairs={{0,3},{1,0},{2,1},{3,2},{4,7},{5,4},{6,5},{7,6},{8,11},{9,8},{10,9... | collective-permute-start | bytes 49160 | tf_op jit(solution)/shard_map/ppermute | solution.py:14
  107.9 1.9 %fusion.8 = f32[32,32,128]{2,1,0:T(8,128)S(1)} fusion(bf16[32,128,128]{2,1,0:T(8,128)(2,1)S(1)} %bitcast.277, bf16[32,32,128]{2,0,1:T(8,128)(2,1)} %fusion.4), kind=kOutput, calls=%fused_computation.17 | convolution fusion | flops 67239936 | bytes 1835008 | tf_op jit(solution)/shard_map/srj,skj->srk/dot_general | solution.py:58
  110.8 1.5 %collective-permute-start.21 = (bf16[8,32,128]{2,0,1:T(8,128)(2,1)S(1)}, bf16[8,32,128]{2,0,1:T(8,128)(2,1)S(1)}, u32[]{:S(2)}, u32[]{:S(2)}) collective-permute-start(bf16[8,32,128]{2,0,1:T(8,128)(2,1)S(1)} %convolution_convert_fusion.9), channel_id=1, source_target_pairs={{0,4},{4,0},{8,12},{12,8},{16,20},{20,16},{24,28},{28,24},{1,5},{5... | collective-permute-start | bytes 196616 | tf_op jit(solution)/shard_map/ppermute | solution.py:18
  116.0 8.9 %all_to_all.23 = f32[32,2,32]{2,1,0:T(2,128)S(1)} all-to-all(f32[32,2,32]{2,1,0:T(2,128)S(1)} %broadcast_in_dim.49), channel_id=1, replica_groups=mesh['dom'=8,'rep'=4] {'dom','rep'}, dimensions={0} | all-to-all | bytes 16384 | tf_op jit(solution)/shard_map/all_to_all | solution.py:24
  (184 shorter events, 47.3 us)
Async XLA Ops:
  4.0 8.6 %collective-permute-start.2 = (s32[8,2]{0,1:T(2,128)S(1)}, s32[8,2]{0,1:T(2,128)S(1)}, u32[]{:S(2)}, u32[]{:S(2)}) collective-permute-start(s32[8,2]{0,1:T(2,128)S(1)} %bitcast.320), channel_id=1, source_target_pairs={{0,3},{1,0},{2,1},{3,2},{4,7},{5,4},{6,5},{7,6},{8,11},{9,8},{10,9... | collective-permute-start | bytes 200 | tf_op jit(solution)/shard_map/ppermute | solution.py:14
  6.4 6.9 %collective-permute-start.1 = (s32[8,2]{0,1:T(2,128)S(1)}, s32[8,2]{0,1:T(2,128)S(1)}, u32[]{:S(2)}, u32[]{:S(2)}) collective-permute-start(s32[8,2]{0,1:T(2,128)S(1)} %bitcast.319), channel_id=1, source_target_pairs={{0,2},{1,3},{2,0},{3,1},{4,6},{5,7},{6,4},{7,5},{8,10},{9,11},{10,... | collective-permute-start | bytes 200 | tf_op jit(solution)/shard_map/ppermute | solution.py:14
  7.0 6.3 %collective-permute-start = (s32[8,2]{0,1:T(2,128)S(1)}, s32[8,2]{0,1:T(2,128)S(1)}, u32[]{:S(2)}, u32[]{:S(2)}) collective-permute-start(s32[8,2]{0,1:T(2,128)S(1)} %bitcast.318), channel_id=1, source_target_pairs={{0,1},{1,2},{2,3},{3,0},{4,5},{5,6},{6,7},{7,4},{8,9},{9,10},{10,1... | collective-permute-start | bytes 200 | tf_op jit(solution)/shard_map/ppermute | solution.py:14
  8.2 8.5 %collective-permute-start.3 = (bf16[8,32,128]{2,0,1:T(8,128)(2,1)S(1)}, bf16[8,32,128]{2,0,1:T(8,128)(2,1)S(1)}, u32[]{:S(2)}, u32[]{:S(2)}) collective-permute-start(bf16[8,32,128]{2,0,1:T(8,128)(2,1)S(1)} %multiply_convert_fusion), channel_id=1, source_target_pairs={{0,4},{4,0},{8,12},{12,8},{16,20},{20,16},{24,28},{28,24},{1,5},{5... | collective-permute-start | bytes 196616 | tf_op jit(solution)/shard_map/ppermute | solution.py:18
  9.8 5.3 %collective-permute-start.7 = (bf16[32,128]{1,0:T(8,128)(2,1)S(1)}, bf16[32,128]{1,0:T(8,128)(2,1)S(1)}, u32[]{:S(2)}, u32[]{:S(2)}) collective-permute-start(bf16[32,128]{1,0:T(8,128)(2,1)S(1)} %bitcast.298), channel_id=1, source_target_pairs={{0,1},{1,2},{2,3},{3,0},{4,5},{5,6},{6,7},{7,4},{8,9},{9,10},{10,1... | collective-permute-start | bytes 24584 | tf_op jit(solution)/shard_map/ppermute | solution.py:14
  12.5 17.7 %collective-permute-start.8 = (f32[32,128]{1,0:T(8,128)S(1)}, f32[32,128]{1,0:T(8,128)S(1)}, u32[]{:S(2)}, u32[]{:S(2)}) collective-permute-start(f32[32,128]{1,0:T(8,128)S(1)} %fusion.85), channel_id=1, source_target_pairs={{0,3},{1,0},{2,1},{3,2},{4,7},{5,4},{6,5},{7,6},{8,11},{9,8},{10,9... | collective-permute-start | bytes 49160 | tf_op jit(solution)/shard_map/ppermute | solution.py:14
  13.3 8.0 %collective-permute-start.4 = (bf16[8,128,128]{2,0,1:T(8,128)(2,1)S(1)}, bf16[8,128,128]{2,0,1:T(8,128)(2,1)S(1)}, u32[]{:S(2)}, u32[]{:S(2)}) collective-permute-start(bf16[8,128,128]{2,0,1:T(8,128)(2,1)S(1)} %get-tuple-element.173), channel_id=1, source_target_pairs={{0,1},{1,2},{2,3},{3,0},{4,5},{5,6},{6,7},{7,4},{8,9},{9,10},{10,1... | collective-permute-start | bytes 786440 | tf_op jit(solution)/shard_map/ppermute | solution.py:14
  13.3 9.2 %collective-permute-start.5 = (bf16[8,128,128]{2,0,1:T(8,128)(2,1)S(1)}, bf16[8,128,128]{2,0,1:T(8,128)(2,1)S(1)}, u32[]{:S(2)}, u32[]{:S(2)}) collective-permute-start(bf16[8,128,128]{2,0,1:T(8,128)(2,1)S(1)} %get-tuple-element.174), channel_id=1, source_target_pairs={{0,2},{1,3},{2,0},{3,1},{4,6},{5,7},{6,4},{7,5},{8,10},{9,11},{10,... | collective-permute-start | bytes 786440 | tf_op jit(solution)/shard_map/ppermute | solution.py:14
  15.1 11.1 %collective-permute-start.6 = (bf16[8,128,128]{2,0,1:T(8,128)(2,1)S(1)}, bf16[8,128,128]{2,0,1:T(8,128)(2,1)S(1)}, u32[]{:S(2)}, u32[]{:S(2)}) collective-permute-start(bf16[8,128,128]{2,0,1:T(8,128)(2,1)S(1)} %select_bitcast_fusion), channel_id=1, source_target_pairs={{0,3},{1,0},{2,1},{3,2},{4,7},{5,4},{6,5},{7,6},{8,11},{9,8},{10,9... | collective-permute-start | bytes 786440 | tf_op jit(solution)/shard_map/ppermute | solution.py:14
  28.2 4.9 %collective-permute-start.9 = (bf16[8,32,128]{2,0,1:T(8,128)(2,1)S(1)}, bf16[8,32,128]{2,0,1:T(8,128)(2,1)S(1)}, u32[]{:S(2)}, u32[]{:S(2)}) collective-permute-start(bf16[8,32,128]{2,0,1:T(8,128)(2,1)S(1)} %convolution_convert_fusion.12), channel_id=1, source_target_pairs={{0,4},{4,0},{8,12},{12,8},{16,20},{20,16},{24,28},{28,24},{1,5},{5... | collective-permute-start | bytes 196616 | tf_op jit(solution)/shard_map/ppermute | solution.py:18
  46.8 4.3 %collective-permute-start.10 = (bf16[8,32,128]{2,0,1:T(8,128)(2,1)S(1)}, bf16[8,32,128]{2,0,1:T(8,128)(2,1)S(1)}, u32[]{:S(2)}, u32[]{:S(2)}) collective-permute-start(bf16[8,32,128]{2,0,1:T(8,128)(2,1)S(1)} %get-tuple-element.110), channel_id=1, source_target_pairs={{0,4},{4,0},{8,12},{12,8},{16,20},{20,16},{24,28},{28,24},{1,5},{5... | collective-permute-start | bytes 196616 | tf_op jit(solution)/shard_map/ppermute | solution.py:18
  47.6 3.1 %collective-permute-start.11 = (bf16[32,128]{1,0:T(8,128)(2,1)S(1)}, bf16[32,128]{1,0:T(8,128)(2,1)S(1)}, u32[]{:S(2)}, u32[]{:S(2)}) collective-permute-start(bf16[32,128]{1,0:T(8,128)(2,1)S(1)} %bitcast.300), channel_id=1, source_target_pairs={{0,1},{1,2},{2,3},{3,0},{4,5},{5,6},{6,7},{7,4},{8,9},{9,10},{10,1... | collective-permute-start | bytes 24584 | tf_op jit(solution)/shard_map/ppermute | solution.py:14
  47.6 10.2 %collective-permute-start.12 = (f32[32,128]{1,0:T(8,128)S(1)}, f32[32,128]{1,0:T(8,128)}, u32[]{:S(2)}, u32[]{:S(2)}) collective-permute-start(f32[32,128]{1,0:T(8,128)S(1)} %fusion.81), channel_id=1, source_target_pairs={{0,3},{1,0},{2,1},{3,2},{4,7},{5,4},{6,5},{7,6},{8,11},{9,8},{10,9... | collective-permute-start | bytes 49160 | tf_op jit(solution)/shard_map/ppermute | solution.py:14
  55.6 4.6 %collective-permute-start.13 = (bf16[8,32,128]{2,0,1:T(8,128)(2,1)}, bf16[8,32,128]{2,0,1:T(8,128)(2,1)}, u32[]{:S(2)}, u32[]{:S(2)}) collective-permute-start(bf16[8,32,128]{2,0,1:T(8,128)(2,1)} %convolution_convert_fusion.11), channel_id=1, source_target_pairs={{0,4},{4,0},{8,12},{12,8},{16,20},{20,16},{24,28},{28,24},{1,5},{5... | collective-permute-start | bytes 196616 | tf_op jit(solution)/shard_map/ppermute | solution.py:18
  73.3 4.3 %collective-permute-start.14 = (bf16[8,32,128]{2,0,1:T(8,128)(2,1)S(1)}, bf16[8,32,128]{2,0,1:T(8,128)(2,1)S(1)}, u32[]{:S(2)}, u32[]{:S(2)}) collective-permute-start(bf16[8,32,128]{2,0,1:T(8,128)(2,1)S(1)} %get-tuple-element.112), channel_id=1, source_target_pairs={{0,4},{4,0},{8,12},{12,8},{16,20},{20,16},{24,28},{28,24},{1,5},{5... | collective-permute-start | bytes 196616 | tf_op jit(solution)/shard_map/ppermute | solution.py:18
  74.0 3.1 %collective-permute-start.15 = (bf16[32,128]{1,0:T(8,128)(2,1)S(1)}, bf16[32,128]{1,0:T(8,128)(2,1)S(1)}, u32[]{:S(2)}, u32[]{:S(2)}) collective-permute-start(bf16[32,128]{1,0:T(8,128)(2,1)S(1)} %bitcast.301), channel_id=1, source_target_pairs={{0,1},{1,2},{2,3},{3,0},{4,5},{5,6},{6,7},{7,4},{8,9},{9,10},{10,1... | collective-permute-start | bytes 24584 | tf_op jit(solution)/shard_map/ppermute | solution.py:14
  74.0 12.4 %collective-permute-start.16 = (f32[32,128]{1,0:T(8,128)S(1)}, f32[32,128]{1,0:T(8,128)}, u32[]{:S(2)}, u32[]{:S(2)}) collective-permute-start(f32[32,128]{1,0:T(8,128)S(1)} %fusion.77), channel_id=1, source_target_pairs={{0,3},{1,0},{2,1},{3,2},{4,7},{5,4},{6,5},{7,6},{8,11},{9,8},{10,9... | collective-permute-start | bytes 49160 | tf_op jit(solution)/shard_map/ppermute | solution.py:14
  82.1 7.0 %collective-permute-start.17 = (bf16[8,32,128]{2,0,1:T(8,128)(2,1)}, bf16[8,32,128]{2,0,1:T(8,128)(2,1)}, u32[]{:S(2)}, u32[]{:S(2)}) collective-permute-start(bf16[8,32,128]{2,0,1:T(8,128)(2,1)} %convolution_convert_fusion.10), channel_id=1, source_target_pairs={{0,4},{4,0},{8,12},{12,8},{16,20},{20,16},{24,28},{28,24},{1,5},{5... | collective-permute-start | bytes 196616 | tf_op jit(solution)/shard_map/ppermute | solution.py:18
  102.2 4.8 %collective-permute-start.18 = (bf16[8,32,128]{2,0,1:T(8,128)(2,1)S(1)}, bf16[8,32,128]{2,0,1:T(8,128)(2,1)S(1)}, u32[]{:S(2)}, u32[]{:S(2)}) collective-permute-start(bf16[8,32,128]{2,0,1:T(8,128)(2,1)S(1)} %get-tuple-element.114), channel_id=1, source_target_pairs={{0,4},{4,0},{8,12},{12,8},{16,20},{20,16},{24,28},{28,24},{1,5},{5... | collective-permute-start | bytes 196616 | tf_op jit(solution)/shard_map/ppermute | solution.py:18
  103.7 3.1 %collective-permute-start.19 = (bf16[32,128]{1,0:T(8,128)(2,1)S(1)}, bf16[32,128]{1,0:T(8,128)(2,1)S(1)}, u32[]{:S(2)}, u32[]{:S(2)}) collective-permute-start(bf16[32,128]{1,0:T(8,128)(2,1)S(1)} %bitcast.299), channel_id=1, source_target_pairs={{0,1},{1,2},{2,3},{3,0},{4,5},{5,6},{6,7},{7,4},{8,9},{9,10},{10,1... | collective-permute-start | bytes 24584 | tf_op jit(solution)/shard_map/ppermute | solution.py:14
  103.8 9.7 %collective-permute-start.20 = (f32[32,128]{1,0:T(8,128)S(1)}, f32[32,128]{1,0:T(8,128)}, u32[]{:S(2)}, u32[]{:S(2)}) collective-permute-start(f32[32,128]{1,0:T(8,128)S(1)} %fusion.73), channel_id=1, source_target_pairs={{0,3},{1,0},{2,1},{3,2},{4,7},{5,4},{6,5},{7,6},{8,11},{9,8},{10,9... | collective-permute-start | bytes 49160 | tf_op jit(solution)/shard_map/ppermute | solution.py:14
  110.8 4.3 %collective-permute-start.21 = (bf16[8,32,128]{2,0,1:T(8,128)(2,1)S(1)}, bf16[8,32,128]{2,0,1:T(8,128)(2,1)S(1)}, u32[]{:S(2)}, u32[]{:S(2)}) collective-permute-start(bf16[8,32,128]{2,0,1:T(8,128)(2,1)S(1)} %convolution_convert_fusion.9), channel_id=1, source_target_pairs={{0,4},{4,0},{8,12},{12,8},{16,20},{20,16},{24,28},{28,24},{1,5},{5... | collective-permute-start | bytes 196616 | tf_op jit(solution)/shard_map/ppermute | solution.py:18
  112.8 12.2 %copy-start.6 = (f32[8,32,128]{2,0,1:T(8,128)S(1)}, f32[8,32,128]{2,0,1:T(8,128)}, u32[]{:S(2)}) copy-start(f32[8,32,128]{2,0,1:T(8,128)} %copy-done.5) | copy-start | bytes 393220
  112.8 12.2 %copy-start.10 = (f32[32]{0:T(128)S(1)}, f32[32]{0:T(128)}, u32[]{:S(2)}) copy-start(f32[32]{0:T(128)} %copy-done.9) | copy-start | bytes 388
  (15 other events, 56.2 us)

commit v9 on v8

--- a/solution.py
+++ b/solution.py
@@ -61,8 +61,10 @@
     far_terms = partner(far_sum, "dom", 0).astype(jnp.float32)
     result = local_stiffness(rounded, diag_tiles, off_tiles, cols_onehot, mirror_onehot)
     first_add = jnp.dot(before, link_tile, preferred_element_type=jnp.float32)
-    result = result.at[0].add(first_add)
-    result = result.at[nodes - 1].add(after)
+    ends = jnp.concatenate(
+        [first_add[None], jnp.zeros((nodes - 2,) + first_add.shape, jnp.float32), after[None]]
+    )
+    result = result + ends
     result = result + jnp.einsum("sn,srk->nrk", near_collect, terms, precision=lax.Precision.HIGHEST)
     return result - far_terms
 

time: 127 us -> 120 us (0.945)
  other arithmetic: 12.3 us -> 6.74 us
  waiting for transfers between devices: 17.9 us -> 22.2 us
  local copies, waits for them, and re-layouts: 8.46 us -> 4.59 us
  matrix products: 28.1 us -> 25.6 us
  blocking collectives: 37.6 us -> 40 us
  starting transfers between devices: 20.9 us -> 19.6 us
    dot_general x4, matrix products: 6.21 us -> 2.31 us  [apply_operator(): jnp.einsum('sn,srk->nrk', near_collect, terms, precision=lax.Precision.HI...]
    scatter-add x8 -> x0, local copies, waits for them, and re-layouts: 3.7 us -> none  [the longest x4 1.85 us: apply_operator(): result = result.at[0].add(first_add)]
    ppermute x8, waiting for transfers between devices: 5.9 us -> 8.88 us  [partner(): lax.ppermute(value, axis, [(i, i ^ 1 << distance) for i in range(lax.axis...]
    ppermute x14, starting transfers between devices: 13.1 us -> 10.2 us  [from_behind(): return lax.ppermute(value, axis, pairs)]
    convert_element_type x4, other arithmetic: 3.22 us -> 0.5 us  [apply_operator(): rounded = vector.astype(jnp.bfloat16)]
    add x8 -> x0, other arithmetic: 2.52 us -> none  [the longest x4 2.45 us: apply_operator(): result = result.at[nodes - 1].add(after)]
    all_to_all x4, blocking collectives: 37.6 us -> 40 us  [total(): gathered = lax.all_to_all(spread, ('dom', 'rep'), 0, 0, tiled=True)]
    ppermute x8, starting transfers between devices: 7.84 us -> 9.38 us  [partner(): lax.ppermute(value, axis, [(i, i ^ 1 << distance) for i in range(lax.axis...]
  transfers between devices with their start and end apart: 22 -> 22, of which waited for: 11 -> 10; matrix products, arithmetic and copies ran while one was open for 24% -> 20% of each run, Pallas kernels for 0% -> 0%
where the time goes in v9:
time: 120 us
  blocking collectives  40 us (33%)
  matrix products  25.6 us (21%)
  waiting for transfers between devices  22.2 us (18%)
  starting transfers between devices  19.6 us (16%)
  other arithmetic  6.74 us (6%)
  local copies, waits for them, and re-layouts  4.59 us (4%)
  between operations  1.34 us (1%)
    all_to_all x4, blocking collectives, total(): gathered = lax.all_to_all(spread, ('dom', 'rep'), 0, 0, tiled=True)  40 us
    ppermute x14, waiting for transfers between devices, from_behind(): return lax.ppermute(value, axis, pairs)  13.4 us
    ppermute x14, starting transfers between devices, from_behind(): return lax.ppermute(value, axis, pairs)  10.2 us
    ppermute x8, starting transfers between devices, partner(): lax.ppermute(value, axis, [(i, i ^ 1 << distance) for i in range(lax.axis...  9.38 us
    ppermute x8, waiting for transfers between devices, partner(): lax.ppermute(value, axis, [(i, i ^ 1 << distance) for i in range(lax.axis...  8.88 us
    dot_general x4, matrix products, apply_operator(): jnp.einsum('srj,skj->srk', multiplier, contact_set, preferred_element_typ...  6.53 us
    unnamed x55, local copies, waits for them, and re-layouts  3.35 us
    dot_general x4, matrix products, local_stiffness(): jnp.einsum('pn,prj->nrj', mirror_onehot, mirror, precision=lax.Precision....  3.2 us
  transfers between devices with their start and end apart: 22, of which 10 were waited for; matrix products, arithmetic and copies ran while one was open for 20% of the time, Pallas kernels for 0%

profile of v9, /device:TPU:0, one launch (start us, length us, event | category | flops | bytes accessed | tf_op | source)
XLA Modules:
  0.0 120.1 jit_solution(812649706833718826)
XLA Ops:
  3.7 2.4 %collective-permute-start.6 = (bf16[8,128,128]{2,0,1:T(8,128)(2,1)S(1)}, bf16[8,128,128]{2,0,1:T(8,128)(2,1)S(1)}, u32[]{:S(2)}, u32[]{:S(2)}) collective-permute-start(bf16[8,128,128]{2,0,1:T(8,128)(2,1)S(1)} %select_bitcast_fusion), channel_id=1, source_target_pairs={{0,3},{1,0},{2,1},{3,2},{4,7},{5,4},{6,5},{7,6},{8,11},{9,8},{10,9... | collective-permute-start | bytes 786440 | tf_op jit(solution)/shard_map/ppermute | solution.py:14
  7.4 1.7 %collective-permute-start.1 = (s32[8,2]{0,1:T(2,128)S(1)}, s32[8,2]{0,1:T(2,128)S(1)}, u32[]{:S(2)}, u32[]{:S(2)}) collective-permute-start(s32[8,2]{0,1:T(2,128)S(1)} %bitcast.330), channel_id=1, source_target_pairs={{0,2},{1,3},{2,0},{3,1},{4,6},{5,7},{6,4},{7,5},{8,10},{9,11},{10,... | collective-permute-start | bytes 200 | tf_op jit(solution)/shard_map/ppermute | solution.py:14
  9.2 1.6 %collective-permute-start.3 = (bf16[8,32,128]{2,0,1:T(8,128)(2,1)S(1)}, bf16[8,32,128]{2,0,1:T(8,128)(2,1)S(1)}, u32[]{:S(2)}, u32[]{:S(2)}) collective-permute-start(bf16[8,32,128]{2,0,1:T(8,128)(2,1)S(1)} %multiply_convert_fusion), channel_id=1, source_target_pairs={{0,4},{4,0},{8,12},{12,8},{16,20},{20,16},{24,28},{28,24},{1,5},{5... | collective-permute-start | bytes 196616 | tf_op jit(solution)/shard_map/ppermute | solution.py:18
  11.2 4.5 %collective-permute-done.2 = s32[8,2]{0,1:T(2,128)S(1)} collective-permute-done((s32[8,2]{0,1:T(2,128)S(1)}, s32[8,2]{0,1:T(2,128)S(1)}, u32[]{:S(2)}, u32[]{:S(2)}) %collective-permute-start.2) | collective-permute-done | bytes 96 | tf_op jit(solution)/shard_map/ppermute | solution.py:14
  16.8 2.3 %collective-permute-done = s32[8,2]{0,1:T(2,128)S(1)} collective-permute-done((s32[8,2]{0,1:T(2,128)S(1)}, s32[8,2]{0,1:T(2,128)S(1)}, u32[]{:S(2)}, u32[]{:S(2)}) %collective-permute-start) | collective-permute-done | bytes 96 | tf_op jit(solution)/shard_map/ppermute | solution.py:14
  19.7 3.0 %collective-permute-done.7 = bf16[32,128]{1,0:T(8,128)(2,1)S(1)} collective-permute-done((bf16[32,128]{1,0:T(8,128)(2,1)S(1)}, bf16[32,128]{1,0:T(8,128)(2,1)S(1)}, u32[]{:S(2)}, u32[]{:S(2)}) %collective-permute-start.7) | collective-permute-done | bytes 8224 | tf_op jit(solution)/shard_map/ppermute | solution.py:14
  25.6 1.6 %collective-permute-start.9 = (bf16[8,32,128]{2,0,1:T(8,128)(2,1)S(1)}, bf16[8,32,128]{2,0,1:T(8,128)(2,1)S(1)}, u32[]{:S(2)}, u32[]{:S(2)}) collective-permute-start(bf16[8,32,128]{2,0,1:T(8,128)(2,1)S(1)} %convolution_convert_fusion.12), channel_id=1, source_target_pairs={{0,4},{4,0},{8,12},{12,8},{16,20},{20,16},{24,28},{28,24},{1,5},{5... | collective-permute-start | bytes 196616 | tf_op jit(solution)/shard_map/ppermute | solution.py:18
  28.2 2.0 %collective-permute-done.9 = bf16[8,32,128]{2,0,1:T(8,128)(2,1)S(1)} collective-permute-done((bf16[8,32,128]{2,0,1:T(8,128)(2,1)S(1)}, bf16[8,32,128]{2,0,1:T(8,128)(2,1)S(1)}, u32[]{:S(2)}, u32[]{:S(2)}) %collective-permute-start.9) | collective-permute-done | bytes 65568 | tf_op jit(solution)/shard_map/ppermute | solution.py:18
  31.2 12.8 %all_to_all.20 = f32[32,1,128]{2,1,0:T(1,128)S(1)} all-to-all(f32[32,1,128]{2,1,0:T(1,128)S(1)} %reshape.371), channel_id=1, replica_groups=mesh['dom'=8,'rep'=4] {'dom','rep'}, dimensions={0} | all-to-all | bytes 32768 | tf_op jit(solution)/shard_map/all_to_all | solution.py:24
  47.1 1.8 %collective-permute-start.12 = (f32[32,128]{1,0:T(8,128)S(1)}, f32[32,128]{1,0:T(8,128)S(1)}, u32[]{:S(2)}, u32[]{:S(2)}) collective-permute-start(f32[32,128]{1,0:T(8,128)S(1)} %fusion.89), channel_id=1, source_target_pairs={{0,3},{1,0},{2,1},{3,2},{4,7},{5,4},{6,5},{7,6},{8,11},{9,8},{10,9... | collective-permute-start | bytes 49160 | tf_op jit(solution)/shard_map/ppermute | solution.py:14
  51.1 1.9 %fusion.6 = f32[32,32,128]{2,1,0:T(8,128)S(1)} fusion(bf16[32,128,128]{2,1,0:T(8,128)(2,1)S(1)} %bitcast.283, bf16[32,32,128]{2,0,1:T(8,128)(2,1)} %fusion.2), kind=kOutput, calls=%fused_computation.15 | convolution fusion | flops 67239936 | bytes 1835008 | tf_op jit(solution)/shard_map/srj,skj->srk/dot_general | solution.py:58
  54.6 1.5 %collective-permute-start.13 = (bf16[8,32,128]{2,0,1:T(8,128)(2,1)S(1)}, bf16[8,32,128]{2,0,1:T(8,128)(2,1)S(1)}, u32[]{:S(2)}, u32[]{:S(2)}) collective-permute-start(bf16[8,32,128]{2,0,1:T(8,128)(2,1)S(1)} %convolution_convert_fusion.11), channel_id=1, source_target_pairs={{0,4},{4,0},{8,12},{12,8},{16,20},{20,16},{24,28},{28,24},{1,5},{5... | collective-permute-start | bytes 196616 | tf_op jit(solution)/shard_map/ppermute | solution.py:18
  56.6 2.3 %collective-permute-done.13 = bf16[8,32,128]{2,0,1:T(8,128)(2,1)S(1)} collective-permute-done((bf16[8,32,128]{2,0,1:T(8,128)(2,1)S(1)}, bf16[8,32,128]{2,0,1:T(8,128)(2,1)S(1)}, u32[]{:S(2)}, u32[]{:S(2)}) %collective-permute-start.13) | collective-permute-done | bytes 65568 | tf_op jit(solution)/shard_map/ppermute | solution.py:18
  59.9 8.9 %all_to_all.21 = f32[32,1,128]{2,1,0:T(1,128)S(1)} all-to-all(f32[32,1,128]{2,1,0:T(1,128)S(1)} %reshape.373), channel_id=1, replica_groups=mesh['dom'=8,'rep'=4] {'dom','rep'}, dimensions={0} | all-to-all | bytes 32768 | tf_op jit(solution)/shard_map/all_to_all | solution.py:24
  71.9 1.7 %collective-permute-start.16 = (f32[32,128]{1,0:T(8,128)}, f32[32,128]{1,0:T(8,128)S(1)}, u32[]{:S(2)}, u32[]{:S(2)}) collective-permute-start(f32[32,128]{1,0:T(8,128)} %fusion.85), channel_id=1, source_target_pairs={{0,3},{1,0},{2,1},{3,2},{4,7},{5,4},{6,5},{7,6},{8,11},{9,8},{10,9... | collective-permute-start | bytes 49160 | tf_op jit(solution)/shard_map/ppermute | solution.py:14
  75.3 1.9 %fusion.7 = f32[32,32,128]{2,1,0:T(8,128)S(1)} fusion(bf16[32,128,128]{2,1,0:T(8,128)(2,1)S(1)} %bitcast.284, bf16[32,32,128]{2,0,1:T(8,128)(2,1)} %fusion.3), kind=kOutput, calls=%fused_computation.16 | convolution fusion | flops 67239936 | bytes 1835008 | tf_op jit(solution)/shard_map/srj,skj->srk/dot_general | solution.py:58
  78.8 1.5 %collective-permute-start.17 = (bf16[8,32,128]{2,0,1:T(8,128)(2,1)S(1)}, bf16[8,32,128]{2,0,1:T(8,128)(2,1)S(1)}, u32[]{:S(2)}, u32[]{:S(2)}) collective-permute-start(bf16[8,32,128]{2,0,1:T(8,128)(2,1)S(1)} %convolution_convert_fusion.10), channel_id=1, source_target_pairs={{0,4},{4,0},{8,12},{12,8},{16,20},{20,16},{24,28},{28,24},{1,5},{5... | collective-permute-start | bytes 196616 | tf_op jit(solution)/shard_map/ppermute | solution.py:18
  80.8 2.3 %collective-permute-done.17 = bf16[8,32,128]{2,0,1:T(8,128)(2,1)S(1)} collective-permute-done((bf16[8,32,128]{2,0,1:T(8,128)(2,1)S(1)}, bf16[8,32,128]{2,0,1:T(8,128)(2,1)S(1)}, u32[]{:S(2)}, u32[]{:S(2)}) %collective-permute-start.17) | collective-permute-done | bytes 65568 | tf_op jit(solution)/shard_map/ppermute | solution.py:18
  84.0 8.8 %all_to_all.22 = f32[32,1,128]{2,1,0:T(1,128)S(1)} all-to-all(f32[32,1,128]{2,1,0:T(1,128)S(1)} %reshape.375), channel_id=1, replica_groups=mesh['dom'=8,'rep'=4] {'dom','rep'}, dimensions={0} | all-to-all | bytes 32768 | tf_op jit(solution)/shard_map/all_to_all | solution.py:24
  97.5 1.7 %collective-permute-done.19 = bf16[32,128]{1,0:T(8,128)(2,1)S(1)} collective-permute-done((bf16[32,128]{1,0:T(8,128)(2,1)S(1)}, bf16[32,128]{1,0:T(8,128)(2,1)S(1)}, u32[]{:S(2)}, u32[]{:S(2)}) %collective-permute-start.19) | collective-permute-done | bytes 8224 | tf_op jit(solution)/shard_map/ppermute | solution.py:14
  100.4 1.9 %fusion.8 = f32[32,32,128]{2,1,0:T(8,128)S(1)} fusion(bf16[32,128,128]{2,1,0:T(8,128)(2,1)S(1)} %bitcast.285, bf16[32,32,128]{2,0,1:T(8,128)(2,1)} %fusion.4), kind=kOutput, calls=%fused_computation.17 | convolution fusion | flops 67239936 | bytes 1835008 | tf_op jit(solution)/shard_map/srj,skj->srk/dot_general | solution.py:58
  103.8 1.5 %collective-permute-start.21 = (bf16[8,32,128]{2,0,1:T(8,128)(2,1)S(1)}, bf16[8,32,128]{2,0,1:T(8,128)(2,1)S(1)}, u32[]{:S(2)}, u32[]{:S(2)}) collective-permute-start(bf16[8,32,128]{2,0,1:T(8,128)(2,1)S(1)} %convolution_convert_fusion.9), channel_id=1, source_target_pairs={{0,4},{4,0},{8,12},{12,8},{16,20},{20,16},{24,28},{28,24},{1,5},{5... | collective-permute-start | bytes 196616 | tf_op jit(solution)/shard_map/ppermute | solution.py:18
  105.9 2.2 %collective-permute-done.21 = bf16[8,32,128]{2,0,1:T(8,128)(2,1)S(1)} collective-permute-done((bf16[8,32,128]{2,0,1:T(8,128)(2,1)S(1)}, bf16[8,32,128]{2,0,1:T(8,128)(2,1)S(1)}, u32[]{:S(2)}, u32[]{:S(2)}) %collective-permute-start.21) | collective-permute-done | bytes 65568 | tf_op jit(solution)/shard_map/ppermute | solution.py:18
  108.9 9.5 %all_to_all.23 = f32[32,2,32]{2,1,0:T(2,128)S(1)} all-to-all(f32[32,2,32]{2,1,0:T(2,128)S(1)} %broadcast_in_dim.115), channel_id=1, replica_groups=mesh['dom'=8,'rep'=4] {'dom','rep'}, dimensions={0} | all-to-all | bytes 16384 | tf_op jit(solution)/shard_map/all_to_all | solution.py:24
  (178 shorter events, 37.3 us)
Async XLA Ops:
  3.7 19.4 %collective-permute-start.6 = (bf16[8,128,128]{2,0,1:T(8,128)(2,1)S(1)}, bf16[8,128,128]{2,0,1:T(8,128)(2,1)S(1)}, u32[]{:S(2)}, u32[]{:S(2)}) collective-permute-start(bf16[8,128,128]{2,0,1:T(8,128)(2,1)S(1)} %select_bitcast_fusion), channel_id=1, source_target_pairs={{0,3},{1,0},{2,1},{3,2},{4,7},{5,4},{6,5},{7,6},{8,11},{9,8},{10,9... | collective-permute-start | bytes 786440 | tf_op jit(solution)/shard_map/ppermute | solution.py:14
  6.3 16.9 %collective-permute-start.5 = (bf16[8,128,128]{2,0,1:T(8,128)(2,1)S(1)}, bf16[8,128,128]{2,0,1:T(8,128)(2,1)S(1)}, u32[]{:S(2)}, u32[]{:S(2)}) collective-permute-start(bf16[8,128,128]{2,0,1:T(8,128)(2,1)S(1)} %get-tuple-element.78), channel_id=1, source_target_pairs={{0,2},{1,3},{2,0},{3,1},{4,6},{5,7},{6,4},{7,5},{8,10},{9,11},{10,... | collective-permute-start | bytes 786440 | tf_op jit(solution)/shard_map/ppermute | solution.py:14
  7.2 8.5 %collective-permute-start.2 = (s32[8,2]{0,1:T(2,128)S(1)}, s32[8,2]{0,1:T(2,128)S(1)}, u32[]{:S(2)}, u32[]{:S(2)}) collective-permute-start(s32[8,2]{0,1:T(2,128)S(1)} %bitcast.331), channel_id=1, source_target_pairs={{0,3},{1,0},{2,1},{3,2},{4,7},{5,4},{6,5},{7,6},{8,11},{9,8},{10,9... | collective-permute-start | bytes 200 | tf_op jit(solution)/shard_map/ppermute | solution.py:14
  7.4 9.5 %collective-permute-start.1 = (s32[8,2]{0,1:T(2,128)S(1)}, s32[8,2]{0,1:T(2,128)S(1)}, u32[]{:S(2)}, u32[]{:S(2)}) collective-permute-start(s32[8,2]{0,1:T(2,128)S(1)} %bitcast.330), channel_id=1, source_target_pairs={{0,2},{1,3},{2,0},{3,1},{4,6},{5,7},{6,4},{7,5},{8,10},{9,11},{10,... | collective-permute-start | bytes 200 | tf_op jit(solution)/shard_map/ppermute | solution.py:14
  9.2 13.6 %collective-permute-start.3 = (bf16[8,32,128]{2,0,1:T(8,128)(2,1)S(1)}, bf16[8,32,128]{2,0,1:T(8,128)(2,1)S(1)}, u32[]{:S(2)}, u32[]{:S(2)}) collective-permute-start(bf16[8,32,128]{2,0,1:T(8,128)(2,1)S(1)} %multiply_convert_fusion), channel_id=1, source_target_pairs={{0,4},{4,0},{8,12},{12,8},{16,20},{20,16},{24,28},{28,24},{1,5},{5... | collective-permute-start | bytes 196616 | tf_op jit(solution)/shard_map/ppermute | solution.py:18
  11.2 47.7 %copy-start.8 = (f32[8]{0:T(128)}, f32[8]{0:T(128)S(1)}, u32[]{:S(2)}) copy-start(f32[8]{0:T(128)S(1)} %pad.28.clone) | copy-start | bytes 100
  15.7 3.4 %collective-permute-start = (s32[8,2]{0,1:T(2,128)S(1)}, s32[8,2]{0,1:T(2,128)S(1)}, u32[]{:S(2)}, u32[]{:S(2)}) collective-permute-start(s32[8,2]{0,1:T(2,128)S(1)} %bitcast.329), channel_id=1, source_target_pairs={{0,1},{1,2},{2,3},{3,0},{4,5},{5,6},{6,7},{7,4},{8,9},{9,10},{10,1... | collective-permute-start | bytes 200 | tf_op jit(solution)/shard_map/ppermute | solution.py:14
  16.8 6.3 %collective-permute-start.4 = (bf16[8,128,128]{2,0,1:T(8,128)(2,1)S(1)}, bf16[8,128,128]{2,0,1:T(8,128)(2,1)S(1)}, u32[]{:S(2)}, u32[]{:S(2)}) collective-permute-start(bf16[8,128,128]{2,0,1:T(8,128)(2,1)S(1)} %get-tuple-element.77), channel_id=1, source_target_pairs={{0,1},{1,2},{2,3},{3,0},{4,5},{5,6},{6,7},{7,4},{8,9},{9,10},{10,1... | collective-permute-start | bytes 786440 | tf_op jit(solution)/shard_map/ppermute | solution.py:14
  19.1 3.6 %collective-permute-start.7 = (bf16[32,128]{1,0:T(8,128)(2,1)S(1)}, bf16[32,128]{1,0:T(8,128)(2,1)S(1)}, u32[]{:S(2)}, u32[]{:S(2)}) collective-permute-start(bf16[32,128]{1,0:T(8,128)(2,1)S(1)} %bitcast.309), channel_id=1, source_target_pairs={{0,1},{1,2},{2,3},{3,0},{4,5},{5,6},{6,7},{7,4},{8,9},{9,10},{10,1... | collective-permute-start | bytes 24584 | tf_op jit(solution)/shard_map/ppermute | solution.py:14
  22.7 5.5 %collective-permute-start.8 = (f32[32,128]{1,0:T(8,128)S(1)}, f32[32,128]{1,0:T(8,128)S(1)}, u32[]{:S(2)}, u32[]{:S(2)}) collective-permute-start(f32[32,128]{1,0:T(8,128)S(1)} %fusion.93), channel_id=1, source_target_pairs={{0,3},{1,0},{2,1},{3,2},{4,7},{5,4},{6,5},{7,6},{8,11},{9,8},{10,9... | collective-permute-start | bytes 49160 | tf_op jit(solution)/shard_map/ppermute | solution.py:14
  25.6 4.6 %collective-permute-start.9 = (bf16[8,32,128]{2,0,1:T(8,128)(2,1)S(1)}, bf16[8,32,128]{2,0,1:T(8,128)(2,1)S(1)}, u32[]{:S(2)}, u32[]{:S(2)}) collective-permute-start(bf16[8,32,128]{2,0,1:T(8,128)(2,1)S(1)} %convolution_convert_fusion.12), channel_id=1, source_target_pairs={{0,4},{4,0},{8,12},{12,8},{16,20},{20,16},{24,28},{28,24},{1,5},{5... | collective-permute-start | bytes 196616 | tf_op jit(solution)/shard_map/ppermute | solution.py:18
  45.9 4.3 %collective-permute-start.10 = (bf16[8,32,128]{2,0,1:T(8,128)(2,1)S(1)}, bf16[8,32,128]{2,0,1:T(8,128)(2,1)S(1)}, u32[]{:S(2)}, u32[]{:S(2)}) collective-permute-start(bf16[8,32,128]{2,0,1:T(8,128)(2,1)S(1)} %get-tuple-element.14), channel_id=1, source_target_pairs={{0,4},{4,0},{8,12},{12,8},{16,20},{20,16},{24,28},{28,24},{1,5},{5... | collective-permute-start | bytes 196616 | tf_op jit(solution)/shard_map/ppermute | solution.py:18
  46.9 3.1 %collective-permute-start.11 = (bf16[32,128]{1,0:T(8,128)(2,1)S(1)}, bf16[32,128]{1,0:T(8,128)(2,1)S(1)}, u32[]{:S(2)}, u32[]{:S(2)}) collective-permute-start(bf16[32,128]{1,0:T(8,128)(2,1)S(1)} %bitcast.310), channel_id=1, source_target_pairs={{0,1},{1,2},{2,3},{3,0},{4,5},{5,6},{6,7},{7,4},{8,9},{9,10},{10,1... | collective-permute-start | bytes 24584 | tf_op jit(solution)/shard_map/ppermute | solution.py:14
  47.1 9.5 %collective-permute-start.12 = (f32[32,128]{1,0:T(8,128)S(1)}, f32[32,128]{1,0:T(8,128)S(1)}, u32[]{:S(2)}, u32[]{:S(2)}) collective-permute-start(f32[32,128]{1,0:T(8,128)S(1)} %fusion.89), channel_id=1, source_target_pairs={{0,3},{1,0},{2,1},{3,2},{4,7},{5,4},{6,5},{7,6},{8,11},{9,8},{10,9... | collective-permute-start | bytes 49160 | tf_op jit(solution)/shard_map/ppermute | solution.py:14
  54.6 4.3 %collective-permute-start.13 = (bf16[8,32,128]{2,0,1:T(8,128)(2,1)S(1)}, bf16[8,32,128]{2,0,1:T(8,128)(2,1)S(1)}, u32[]{:S(2)}, u32[]{:S(2)}) collective-permute-start(bf16[8,32,128]{2,0,1:T(8,128)(2,1)S(1)} %convolution_convert_fusion.11), channel_id=1, source_target_pairs={{0,4},{4,0},{8,12},{12,8},{16,20},{20,16},{24,28},{28,24},{1,5},{5... | collective-permute-start | bytes 196616 | tf_op jit(solution)/shard_map/ppermute | solution.py:18
  70.1 4.3 %collective-permute-start.14 = (bf16[8,32,128]{2,0,1:T(8,128)(2,1)S(1)}, bf16[8,32,128]{2,0,1:T(8,128)(2,1)S(1)}, u32[]{:S(2)}, u32[]{:S(2)}) collective-permute-start(bf16[8,32,128]{2,0,1:T(8,128)(2,1)S(1)} %get-tuple-element.16), channel_id=1, source_target_pairs={{0,4},{4,0},{8,12},{12,8},{16,20},{20,16},{24,28},{28,24},{1,5},{5... | collective-permute-start | bytes 196616 | tf_op jit(solution)/shard_map/ppermute | solution.py:18
  71.1 3.1 %collective-permute-start.15 = (bf16[32,128]{1,0:T(8,128)(2,1)S(1)}, bf16[32,128]{1,0:T(8,128)(2,1)S(1)}, u32[]{:S(2)}, u32[]{:S(2)}) collective-permute-start(bf16[32,128]{1,0:T(8,128)(2,1)S(1)} %bitcast.311), channel_id=1, source_target_pairs={{0,1},{1,2},{2,3},{3,0},{4,5},{5,6},{6,7},{7,4},{8,9},{9,10},{10,1... | collective-permute-start | bytes 24584 | tf_op jit(solution)/shard_map/ppermute | solution.py:14
  71.9 8.9 %collective-permute-start.16 = (f32[32,128]{1,0:T(8,128)}, f32[32,128]{1,0:T(8,128)S(1)}, u32[]{:S(2)}, u32[]{:S(2)}) collective-permute-start(f32[32,128]{1,0:T(8,128)} %fusion.85), channel_id=1, source_target_pairs={{0,3},{1,0},{2,1},{3,2},{4,7},{5,4},{6,5},{7,6},{8,11},{9,8},{10,9... | collective-permute-start | bytes 49160 | tf_op jit(solution)/shard_map/ppermute | solution.py:14
  78.8 4.3 %collective-permute-start.17 = (bf16[8,32,128]{2,0,1:T(8,128)(2,1)S(1)}, bf16[8,32,128]{2,0,1:T(8,128)(2,1)S(1)}, u32[]{:S(2)}, u32[]{:S(2)}) collective-permute-start(bf16[8,32,128]{2,0,1:T(8,128)(2,1)S(1)} %convolution_convert_fusion.10), channel_id=1, source_target_pairs={{0,4},{4,0},{8,12},{12,8},{16,20},{20,16},{24,28},{28,24},{1,5},{5... | collective-permute-start | bytes 196616 | tf_op jit(solution)/shard_map/ppermute | solution.py:18
  94.3 5.0 %collective-permute-start.18 = (bf16[8,32,128]{2,0,1:T(8,128)(2,1)S(1)}, bf16[8,32,128]{2,0,1:T(8,128)(2,1)S(1)}, u32[]{:S(2)}, u32[]{:S(2)}) collective-permute-start(bf16[8,32,128]{2,0,1:T(8,128)(2,1)S(1)} %get-tuple-element.18), channel_id=1, source_target_pairs={{0,4},{4,0},{8,12},{12,8},{16,20},{20,16},{24,28},{28,24},{1,5},{5... | collective-permute-start | bytes 196616 | tf_op jit(solution)/shard_map/ppermute | solution.py:18
  96.1 9.8 %collective-permute-start.20 = (f32[32,128]{1,0:T(8,128)}, f32[32,128]{1,0:T(8,128)S(1)}, u32[]{:S(2)}, u32[]{:S(2)}) collective-permute-start(f32[32,128]{1,0:T(8,128)} %fusion.81), channel_id=1, source_target_pairs={{0,3},{1,0},{2,1},{3,2},{4,7},{5,4},{6,5},{7,6},{8,11},{9,8},{10,9... | collective-permute-start | bytes 49160 | tf_op jit(solution)/shard_map/ppermute | solution.py:14
  96.1 3.2 %collective-permute-start.19 = (bf16[32,128]{1,0:T(8,128)(2,1)S(1)}, bf16[32,128]{1,0:T(8,128)(2,1)S(1)}, u32[]{:S(2)}, u32[]{:S(2)}) collective-permute-start(bf16[32,128]{1,0:T(8,128)(2,1)S(1)} %bitcast.312), channel_id=1, source_target_pairs={{0,1},{1,2},{2,3},{3,0},{4,5},{5,6},{6,7},{7,4},{8,9},{9,10},{10,1... | collective-permute-start | bytes 24584 | tf_op jit(solution)/shard_map/ppermute | solution.py:14
  103.8 4.3 %collective-permute-start.21 = (bf16[8,32,128]{2,0,1:T(8,128)(2,1)S(1)}, bf16[8,32,128]{2,0,1:T(8,128)(2,1)S(1)}, u32[]{:S(2)}, u32[]{:S(2)}) collective-permute-start(bf16[8,32,128]{2,0,1:T(8,128)(2,1)S(1)} %convolution_convert_fusion.9), channel_id=1, source_target_pairs={{0,4},{4,0},{8,12},{12,8},{16,20},{20,16},{24,28},{28,24},{1,5},{5... | collective-permute-start | bytes 196616 | tf_op jit(solution)/shard_map/ppermute | solution.py:18
  105.6 12.8 %copy-start.6 = (f32[8,32,128]{2,0,1:T(8,128)S(1)}, f32[8,32,128]{2,0,1:T(8,128)}, u32[]{:S(2)}) copy-start(f32[8,32,128]{2,0,1:T(8,128)} %copy-done.5) | copy-start | bytes 393220
  (19 other events, 98.6 us)

commit v10 on v9

--- a/solution.py
+++ b/solution.py
@@ -39,7 +39,7 @@
     return result + jnp.einsum("pn,prj->nrj", mirror_onehot, mirror, precision=lax.Precision.HIGHEST)
 
 
-def apply_operator(vector, diag_tiles, off_tiles, link_tile, contact_set, tables):
+def apply_operator(vector, diag_tiles, off_tiles, link_tile, contact_set, flipped_set, tables):
     cols_onehot, mirror_onehot, near_onehot, far_onehot, near_collect, far_collect = tables
     nodes = vector.shape[0]
     rounded = vector.astype(jnp.bfloat16)
@@ -55,7 +55,7 @@
     multiplier = jnp.einsum(
         "srk,skj->srj", difference, contact_set, preferred_element_type=jnp.float32
     ).astype(jnp.bfloat16)
-    terms = jnp.einsum("srj,skj->srk", multiplier, contact_set, preferred_element_type=jnp.float32)
+    terms = jnp.einsum("srj,sjk->srk", multiplier, flipped_set, preferred_element_type=jnp.float32)
     far_sum = jnp.einsum("sn,srk->nrk", far_collect, terms, precision=lax.Precision.HIGHEST)
     far_sum, rounded = lax.optimization_barrier((far_sum.astype(jnp.bfloat16), rounded))
     far_terms = partner(far_sum, "dom", 0).astype(jnp.float32)
@@ -122,13 +122,16 @@
         far_collect,
     )
     link_tile = link_tiles[0]
+    flipped_set = jnp.swapaxes(contact_set, 1, 2)
     scale = precond[:, None, :]
     solution = jnp.zeros_like(rhs)
     residual = rhs
     preconditioned = scale * residual
     direction = preconditioned
     for step in range(ITERS):
-        image = apply_operator(direction, diag_tiles, off_tiles, link_tile, contact_set, tables)
+        image = apply_operator(
+            direction, diag_tiles, off_tiles, link_tile, contact_set, flipped_set, tables
+        )
         parts = [
             jnp.sum(direction * image, axis=(0, 2)),
             jnp.sum(residual * preconditioned, axis=(0, 2)),

time: 120 us -> 120 us (level)
  no operation moved by 1% of the time
where the time goes in v10:
time: 120 us
  blocking collectives  40 us (33%)
  matrix products  25.6 us (21%)
  waiting for transfers between devices  22.2 us (18%)
  starting transfers between devices  19.6 us (16%)
  other arithmetic  6.74 us (6%)
  local copies, waits for them, and re-layouts  4.59 us (4%)
  between operations  1.34 us (1%)
    all_to_all x4, blocking collectives, total(): gathered = lax.all_to_all(spread, ('dom', 'rep'), 0, 0, tiled=True)  40 us
    ppermute x14, waiting for transfers between devices, from_behind(): return lax.ppermute(value, axis, pairs)  13.4 us
    ppermute x14, starting transfers between devices, from_behind(): return lax.ppermute(value, axis, pairs)  10.2 us
    ppermute x8, starting transfers between devices, partner(): lax.ppermute(value, axis, [(i, i ^ 1 << distance) for i in range(lax.axis...  9.38 us
    ppermute x8, waiting for transfers between devices, partner(): lax.ppermute(value, axis, [(i, i ^ 1 << distance) for i in range(lax.axis...  8.88 us
    dot_general x4, matrix products, apply_operator(): jnp.einsum('srj,sjk->srk', multiplier, flipped_set, preferred_element_typ...  6.53 us
    unnamed x55, local copies, waits for them, and re-layouts  3.35 us
    dot_general x4, matrix products, local_stiffness(): jnp.einsum('pn,prj->nrj', mirror_onehot, mirror, precision=lax.Precision....  3.2 us
  transfers between devices with their start and end apart: 22, of which 10 were waited for; matrix products, arithmetic and copies ran while one was open for 20% of the time, Pallas kernels for 0%

profile of v10, /device:TPU:0, one launch (start us, length us, event | category | flops | bytes accessed | tf_op | source)
XLA Modules:
  0.0 120.1 jit_solution(812649706833718826)
XLA Ops:
  3.7 2.4 %collective-permute-start.6 = (bf16[8,128,128]{2,0,1:T(8,128)(2,1)S(1)}, bf16[8,128,128]{2,0,1:T(8,128)(2,1)S(1)}, u32[]{:S(2)}, u32[]{:S(2)}) collective-permute-start(bf16[8,128,128]{2,0,1:T(8,128)(2,1)S(1)} %select_bitcast_fusion), channel_id=1, source_target_pairs={{0,3},{1,0},{2,1},{3,2},{4,7},{5,4},{6,5},{7,6},{8,11},{9,8},{10,9... | collective-permute-start | bytes 786440 | tf_op jit(solution)/shard_map/ppermute | solution.py:14
  7.4 1.7 %collective-permute-start.1 = (s32[8,2]{0,1:T(2,128)S(1)}, s32[8,2]{0,1:T(2,128)S(1)}, u32[]{:S(2)}, u32[]{:S(2)}) collective-permute-start(s32[8,2]{0,1:T(2,128)S(1)} %bitcast.330), channel_id=1, source_target_pairs={{0,2},{1,3},{2,0},{3,1},{4,6},{5,7},{6,4},{7,5},{8,10},{9,11},{10,... | collective-permute-start | bytes 200 | tf_op jit(solution)/shard_map/ppermute | solution.py:14
  9.2 1.6 %collective-permute-start.3 = (bf16[8,32,128]{2,0,1:T(8,128)(2,1)S(1)}, bf16[8,32,128]{2,0,1:T(8,128)(2,1)S(1)}, u32[]{:S(2)}, u32[]{:S(2)}) collective-permute-start(bf16[8,32,128]{2,0,1:T(8,128)(2,1)S(1)} %multiply_convert_fusion), channel_id=1, source_target_pairs={{0,4},{4,0},{8,12},{12,8},{16,20},{20,16},{24,28},{28,24},{1,5},{5... | collective-permute-start | bytes 196616 | tf_op jit(solution)/shard_map/ppermute | solution.py:18
  11.2 4.5 %collective-permute-done.2 = s32[8,2]{0,1:T(2,128)S(1)} collective-permute-done((s32[8,2]{0,1:T(2,128)S(1)}, s32[8,2]{0,1:T(2,128)S(1)}, u32[]{:S(2)}, u32[]{:S(2)}) %collective-permute-start.2) | collective-permute-done | bytes 96 | tf_op jit(solution)/shard_map/ppermute | solution.py:14
  16.8 2.3 %collective-permute-done = s32[8,2]{0,1:T(2,128)S(1)} collective-permute-done((s32[8,2]{0,1:T(2,128)S(1)}, s32[8,2]{0,1:T(2,128)S(1)}, u32[]{:S(2)}, u32[]{:S(2)}) %collective-permute-start) | collective-permute-done | bytes 96 | tf_op jit(solution)/shard_map/ppermute | solution.py:14
  19.7 3.0 %collective-permute-done.7 = bf16[32,128]{1,0:T(8,128)(2,1)S(1)} collective-permute-done((bf16[32,128]{1,0:T(8,128)(2,1)S(1)}, bf16[32,128]{1,0:T(8,128)(2,1)S(1)}, u32[]{:S(2)}, u32[]{:S(2)}) %collective-permute-start.7) | collective-permute-done | bytes 8224 | tf_op jit(solution)/shard_map/ppermute | solution.py:14
  25.6 1.6 %collective-permute-start.9 = (bf16[8,32,128]{2,0,1:T(8,128)(2,1)S(1)}, bf16[8,32,128]{2,0,1:T(8,128)(2,1)S(1)}, u32[]{:S(2)}, u32[]{:S(2)}) collective-permute-start(bf16[8,32,128]{2,0,1:T(8,128)(2,1)S(1)} %convolution_convert_fusion.12), channel_id=1, source_target_pairs={{0,4},{4,0},{8,12},{12,8},{16,20},{20,16},{24,28},{28,24},{1,5},{5... | collective-permute-start | bytes 196616 | tf_op jit(solution)/shard_map/ppermute | solution.py:18
  28.2 2.0 %collective-permute-done.9 = bf16[8,32,128]{2,0,1:T(8,128)(2,1)S(1)} collective-permute-done((bf16[8,32,128]{2,0,1:T(8,128)(2,1)S(1)}, bf16[8,32,128]{2,0,1:T(8,128)(2,1)S(1)}, u32[]{:S(2)}, u32[]{:S(2)}) %collective-permute-start.9) | collective-permute-done | bytes 65568 | tf_op jit(solution)/shard_map/ppermute | solution.py:18
  31.2 12.8 %all_to_all.20 = f32[32,1,128]{2,1,0:T(1,128)S(1)} all-to-all(f32[32,1,128]{2,1,0:T(1,128)S(1)} %reshape.371), channel_id=1, replica_groups=mesh['dom'=8,'rep'=4] {'dom','rep'}, dimensions={0} | all-to-all | bytes 32768 | tf_op jit(solution)/shard_map/all_to_all | solution.py:24
  47.1 1.8 %collective-permute-start.12 = (f32[32,128]{1,0:T(8,128)S(1)}, f32[32,128]{1,0:T(8,128)S(1)}, u32[]{:S(2)}, u32[]{:S(2)}) collective-permute-start(f32[32,128]{1,0:T(8,128)S(1)} %fusion.89), channel_id=1, source_target_pairs={{0,3},{1,0},{2,1},{3,2},{4,7},{5,4},{6,5},{7,6},{8,11},{9,8},{10,9... | collective-permute-start | bytes 49160 | tf_op jit(solution)/shard_map/ppermute | solution.py:14
  51.1 1.9 %fusion.6 = f32[32,32,128]{2,1,0:T(8,128)S(1)} fusion(bf16[32,128,128]{2,1,0:T(8,128)(2,1)S(1)} %bitcast.283, bf16[32,32,128]{2,0,1:T(8,128)(2,1)} %fusion.2), kind=kOutput, calls=%fused_computation.15 | convolution fusion | flops 67239936 | bytes 1835008 | tf_op jit(solution)/shard_map/srj,sjk->srk/dot_general | solution.py:58
  54.6 1.5 %collective-permute-start.13 = (bf16[8,32,128]{2,0,1:T(8,128)(2,1)S(1)}, bf16[8,32,128]{2,0,1:T(8,128)(2,1)S(1)}, u32[]{:S(2)}, u32[]{:S(2)}) collective-permute-start(bf16[8,32,128]{2,0,1:T(8,128)(2,1)S(1)} %convolution_convert_fusion.11), channel_id=1, source_target_pairs={{0,4},{4,0},{8,12},{12,8},{16,20},{20,16},{24,28},{28,24},{1,5},{5... | collective-permute-start | bytes 196616 | tf_op jit(solution)/shard_map/ppermute | solution.py:18
  56.6 2.3 %collective-permute-done.13 = bf16[8,32,128]{2,0,1:T(8,128)(2,1)S(1)} collective-permute-done((bf16[8,32,128]{2,0,1:T(8,128)(2,1)S(1)}, bf16[8,32,128]{2,0,1:T(8,128)(2,1)S(1)}, u32[]{:S(2)}, u32[]{:S(2)}) %collective-permute-start.13) | collective-permute-done | bytes 65568 | tf_op jit(solution)/shard_map/ppermute | solution.py:18
  59.9 8.9 %all_to_all.21 = f32[32,1,128]{2,1,0:T(1,128)S(1)} all-to-all(f32[32,1,128]{2,1,0:T(1,128)S(1)} %reshape.373), channel_id=1, replica_groups=mesh['dom'=8,'rep'=4] {'dom','rep'}, dimensions={0} | all-to-all | bytes 32768 | tf_op jit(solution)/shard_map/all_to_all | solution.py:24
  71.9 1.7 %collective-permute-start.16 = (f32[32,128]{1,0:T(8,128)}, f32[32,128]{1,0:T(8,128)S(1)}, u32[]{:S(2)}, u32[]{:S(2)}) collective-permute-start(f32[32,128]{1,0:T(8,128)} %fusion.85), channel_id=1, source_target_pairs={{0,3},{1,0},{2,1},{3,2},{4,7},{5,4},{6,5},{7,6},{8,11},{9,8},{10,9... | collective-permute-start | bytes 49160 | tf_op jit(solution)/shard_map/ppermute | solution.py:14
  75.3 1.9 %fusion.7 = f32[32,32,128]{2,1,0:T(8,128)S(1)} fusion(bf16[32,128,128]{2,1,0:T(8,128)(2,1)S(1)} %bitcast.284, bf16[32,32,128]{2,0,1:T(8,128)(2,1)} %fusion.3), kind=kOutput, calls=%fused_computation.16 | convolution fusion | flops 67239936 | bytes 1835008 | tf_op jit(solution)/shard_map/srj,sjk->srk/dot_general | solution.py:58
  78.8 1.5 %collective-permute-start.17 = (bf16[8,32,128]{2,0,1:T(8,128)(2,1)S(1)}, bf16[8,32,128]{2,0,1:T(8,128)(2,1)S(1)}, u32[]{:S(2)}, u32[]{:S(2)}) collective-permute-start(bf16[8,32,128]{2,0,1:T(8,128)(2,1)S(1)} %convolution_convert_fusion.10), channel_id=1, source_target_pairs={{0,4},{4,0},{8,12},{12,8},{16,20},{20,16},{24,28},{28,24},{1,5},{5... | collective-permute-start | bytes 196616 | tf_op jit(solution)/shard_map/ppermute | solution.py:18
  80.8 2.3 %collective-permute-done.17 = bf16[8,32,128]{2,0,1:T(8,128)(2,1)S(1)} collective-permute-done((bf16[8,32,128]{2,0,1:T(8,128)(2,1)S(1)}, bf16[8,32,128]{2,0,1:T(8,128)(2,1)S(1)}, u32[]{:S(2)}, u32[]{:S(2)}) %collective-permute-start.17) | collective-permute-done | bytes 65568 | tf_op jit(solution)/shard_map/ppermute | solution.py:18
  84.0 8.8 %all_to_all.22 = f32[32,1,128]{2,1,0:T(1,128)S(1)} all-to-all(f32[32,1,128]{2,1,0:T(1,128)S(1)} %reshape.375), channel_id=1, replica_groups=mesh['dom'=8,'rep'=4] {'dom','rep'}, dimensions={0} | all-to-all | bytes 32768 | tf_op jit(solution)/shard_map/all_to_all | solution.py:24
  97.5 1.7 %collective-permute-done.19 = bf16[32,128]{1,0:T(8,128)(2,1)S(1)} collective-permute-done((bf16[32,128]{1,0:T(8,128)(2,1)S(1)}, bf16[32,128]{1,0:T(8,128)(2,1)S(1)}, u32[]{:S(2)}, u32[]{:S(2)}) %collective-permute-start.19) | collective-permute-done | bytes 8224 | tf_op jit(solution)/shard_map/ppermute | solution.py:14
  100.4 1.9 %fusion.8 = f32[32,32,128]{2,1,0:T(8,128)S(1)} fusion(bf16[32,128,128]{2,1,0:T(8,128)(2,1)S(1)} %bitcast.285, bf16[32,32,128]{2,0,1:T(8,128)(2,1)} %fusion.4), kind=kOutput, calls=%fused_computation.17 | convolution fusion | flops 67239936 | bytes 1835008 | tf_op jit(solution)/shard_map/srj,sjk->srk/dot_general | solution.py:58
  103.8 1.5 %collective-permute-start.21 = (bf16[8,32,128]{2,0,1:T(8,128)(2,1)S(1)}, bf16[8,32,128]{2,0,1:T(8,128)(2,1)S(1)}, u32[]{:S(2)}, u32[]{:S(2)}) collective-permute-start(bf16[8,32,128]{2,0,1:T(8,128)(2,1)S(1)} %convolution_convert_fusion.9), channel_id=1, source_target_pairs={{0,4},{4,0},{8,12},{12,8},{16,20},{20,16},{24,28},{28,24},{1,5},{5... | collective-permute-start | bytes 196616 | tf_op jit(solution)/shard_map/ppermute | solution.py:18
  105.9 2.2 %collective-permute-done.21 = bf16[8,32,128]{2,0,1:T(8,128)(2,1)S(1)} collective-permute-done((bf16[8,32,128]{2,0,1:T(8,128)(2,1)S(1)}, bf16[8,32,128]{2,0,1:T(8,128)(2,1)S(1)}, u32[]{:S(2)}, u32[]{:S(2)}) %collective-permute-start.21) | collective-permute-done | bytes 65568 | tf_op jit(solution)/shard_map/ppermute | solution.py:18
  108.9 9.5 %all_to_all.23 = f32[32,2,32]{2,1,0:T(2,128)S(1)} all-to-all(f32[32,2,32]{2,1,0:T(2,128)S(1)} %broadcast_in_dim.115), channel_id=1, replica_groups=mesh['dom'=8,'rep'=4] {'dom','rep'}, dimensions={0} | all-to-all | bytes 16384 | tf_op jit(solution)/shard_map/all_to_all | solution.py:24
  (178 shorter events, 37.3 us)
Async XLA Ops:
  3.7 19.4 %collective-permute-start.6 = (bf16[8,128,128]{2,0,1:T(8,128)(2,1)S(1)}, bf16[8,128,128]{2,0,1:T(8,128)(2,1)S(1)}, u32[]{:S(2)}, u32[]{:S(2)}) collective-permute-start(bf16[8,128,128]{2,0,1:T(8,128)(2,1)S(1)} %select_bitcast_fusion), channel_id=1, source_target_pairs={{0,3},{1,0},{2,1},{3,2},{4,7},{5,4},{6,5},{7,6},{8,11},{9,8},{10,9... | collective-permute-start | bytes 786440 | tf_op jit(solution)/shard_map/ppermute | solution.py:14
  6.3 16.9 %collective-permute-start.5 = (bf16[8,128,128]{2,0,1:T(8,128)(2,1)S(1)}, bf16[8,128,128]{2,0,1:T(8,128)(2,1)S(1)}, u32[]{:S(2)}, u32[]{:S(2)}) collective-permute-start(bf16[8,128,128]{2,0,1:T(8,128)(2,1)S(1)} %get-tuple-element.78), channel_id=1, source_target_pairs={{0,2},{1,3},{2,0},{3,1},{4,6},{5,7},{6,4},{7,5},{8,10},{9,11},{10,... | collective-permute-start | bytes 786440 | tf_op jit(solution)/shard_map/ppermute | solution.py:14
  7.2 8.5 %collective-permute-start.2 = (s32[8,2]{0,1:T(2,128)S(1)}, s32[8,2]{0,1:T(2,128)S(1)}, u32[]{:S(2)}, u32[]{:S(2)}) collective-permute-start(s32[8,2]{0,1:T(2,128)S(1)} %bitcast.331), channel_id=1, source_target_pairs={{0,3},{1,0},{2,1},{3,2},{4,7},{5,4},{6,5},{7,6},{8,11},{9,8},{10,9... | collective-permute-start | bytes 200 | tf_op jit(solution)/shard_map/ppermute | solution.py:14
  7.4 9.5 %collective-permute-start.1 = (s32[8,2]{0,1:T(2,128)S(1)}, s32[8,2]{0,1:T(2,128)S(1)}, u32[]{:S(2)}, u32[]{:S(2)}) collective-permute-start(s32[8,2]{0,1:T(2,128)S(1)} %bitcast.330), channel_id=1, source_target_pairs={{0,2},{1,3},{2,0},{3,1},{4,6},{5,7},{6,4},{7,5},{8,10},{9,11},{10,... | collective-permute-start | bytes 200 | tf_op jit(solution)/shard_map/ppermute | solution.py:14
  9.2 13.6 %collective-permute-start.3 = (bf16[8,32,128]{2,0,1:T(8,128)(2,1)S(1)}, bf16[8,32,128]{2,0,1:T(8,128)(2,1)S(1)}, u32[]{:S(2)}, u32[]{:S(2)}) collective-permute-start(bf16[8,32,128]{2,0,1:T(8,128)(2,1)S(1)} %multiply_convert_fusion), channel_id=1, source_target_pairs={{0,4},{4,0},{8,12},{12,8},{16,20},{20,16},{24,28},{28,24},{1,5},{5... | collective-permute-start | bytes 196616 | tf_op jit(solution)/shard_map/ppermute | solution.py:18
  11.2 47.7 %copy-start.8 = (f32[8]{0:T(128)}, f32[8]{0:T(128)S(1)}, u32[]{:S(2)}) copy-start(f32[8]{0:T(128)S(1)} %pad.28.clone) | copy-start | bytes 100
  15.7 3.4 %collective-permute-start = (s32[8,2]{0,1:T(2,128)S(1)}, s32[8,2]{0,1:T(2,128)S(1)}, u32[]{:S(2)}, u32[]{:S(2)}) collective-permute-start(s32[8,2]{0,1:T(2,128)S(1)} %bitcast.329), channel_id=1, source_target_pairs={{0,1},{1,2},{2,3},{3,0},{4,5},{5,6},{6,7},{7,4},{8,9},{9,10},{10,1... | collective-permute-start | bytes 200 | tf_op jit(solution)/shard_map/ppermute | solution.py:14
  16.8 6.3 %collective-permute-start.4 = (bf16[8,128,128]{2,0,1:T(8,128)(2,1)S(1)}, bf16[8,128,128]{2,0,1:T(8,128)(2,1)S(1)}, u32[]{:S(2)}, u32[]{:S(2)}) collective-permute-start(bf16[8,128,128]{2,0,1:T(8,128)(2,1)S(1)} %get-tuple-element.77), channel_id=1, source_target_pairs={{0,1},{1,2},{2,3},{3,0},{4,5},{5,6},{6,7},{7,4},{8,9},{9,10},{10,1... | collective-permute-start | bytes 786440 | tf_op jit(solution)/shard_map/ppermute | solution.py:14
  19.1 3.6 %collective-permute-start.7 = (bf16[32,128]{1,0:T(8,128)(2,1)S(1)}, bf16[32,128]{1,0:T(8,128)(2,1)S(1)}, u32[]{:S(2)}, u32[]{:S(2)}) collective-permute-start(bf16[32,128]{1,0:T(8,128)(2,1)S(1)} %bitcast.309), channel_id=1, source_target_pairs={{0,1},{1,2},{2,3},{3,0},{4,5},{5,6},{6,7},{7,4},{8,9},{9,10},{10,1... | collective-permute-start | bytes 24584 | tf_op jit(solution)/shard_map/ppermute | solution.py:14
  22.7 5.5 %collective-permute-start.8 = (f32[32,128]{1,0:T(8,128)S(1)}, f32[32,128]{1,0:T(8,128)S(1)}, u32[]{:S(2)}, u32[]{:S(2)}) collective-permute-start(f32[32,128]{1,0:T(8,128)S(1)} %fusion.93), channel_id=1, source_target_pairs={{0,3},{1,0},{2,1},{3,2},{4,7},{5,4},{6,5},{7,6},{8,11},{9,8},{10,9... | collective-permute-start | bytes 49160 | tf_op jit(solution)/shard_map/ppermute | solution.py:14
  25.6 4.6 %collective-permute-start.9 = (bf16[8,32,128]{2,0,1:T(8,128)(2,1)S(1)}, bf16[8,32,128]{2,0,1:T(8,128)(2,1)S(1)}, u32[]{:S(2)}, u32[]{:S(2)}) collective-permute-start(bf16[8,32,128]{2,0,1:T(8,128)(2,1)S(1)} %convolution_convert_fusion.12), channel_id=1, source_target_pairs={{0,4},{4,0},{8,12},{12,8},{16,20},{20,16},{24,28},{28,24},{1,5},{5... | collective-permute-start | bytes 196616 | tf_op jit(solution)/shard_map/ppermute | solution.py:18
  45.9 4.3 %collective-permute-start.10 = (bf16[8,32,128]{2,0,1:T(8,128)(2,1)S(1)}, bf16[8,32,128]{2,0,1:T(8,128)(2,1)S(1)}, u32[]{:S(2)}, u32[]{:S(2)}) collective-permute-start(bf16[8,32,128]{2,0,1:T(8,128)(2,1)S(1)} %get-tuple-element.14), channel_id=1, source_target_pairs={{0,4},{4,0},{8,12},{12,8},{16,20},{20,16},{24,28},{28,24},{1,5},{5... | collective-permute-start | bytes 196616 | tf_op jit(solution)/shard_map/ppermute | solution.py:18
  46.9 3.1 %collective-permute-start.11 = (bf16[32,128]{1,0:T(8,128)(2,1)S(1)}, bf16[32,128]{1,0:T(8,128)(2,1)S(1)}, u32[]{:S(2)}, u32[]{:S(2)}) collective-permute-start(bf16[32,128]{1,0:T(8,128)(2,1)S(1)} %bitcast.310), channel_id=1, source_target_pairs={{0,1},{1,2},{2,3},{3,0},{4,5},{5,6},{6,7},{7,4},{8,9},{9,10},{10,1... | collective-permute-start | bytes 24584 | tf_op jit(solution)/shard_map/ppermute | solution.py:14
  47.1 9.5 %collective-permute-start.12 = (f32[32,128]{1,0:T(8,128)S(1)}, f32[32,128]{1,0:T(8,128)S(1)}, u32[]{:S(2)}, u32[]{:S(2)}) collective-permute-start(f32[32,128]{1,0:T(8,128)S(1)} %fusion.89), channel_id=1, source_target_pairs={{0,3},{1,0},{2,1},{3,2},{4,7},{5,4},{6,5},{7,6},{8,11},{9,8},{10,9... | collective-permute-start | bytes 49160 | tf_op jit(solution)/shard_map/ppermute | solution.py:14
  54.6 4.3 %collective-permute-start.13 = (bf16[8,32,128]{2,0,1:T(8,128)(2,1)S(1)}, bf16[8,32,128]{2,0,1:T(8,128)(2,1)S(1)}, u32[]{:S(2)}, u32[]{:S(2)}) collective-permute-start(bf16[8,32,128]{2,0,1:T(8,128)(2,1)S(1)} %convolution_convert_fusion.11), channel_id=1, source_target_pairs={{0,4},{4,0},{8,12},{12,8},{16,20},{20,16},{24,28},{28,24},{1,5},{5... | collective-permute-start | bytes 196616 | tf_op jit(solution)/shard_map/ppermute | solution.py:18
  70.1 4.3 %collective-permute-start.14 = (bf16[8,32,128]{2,0,1:T(8,128)(2,1)S(1)}, bf16[8,32,128]{2,0,1:T(8,128)(2,1)S(1)}, u32[]{:S(2)}, u32[]{:S(2)}) collective-permute-start(bf16[8,32,128]{2,0,1:T(8,128)(2,1)S(1)} %get-tuple-element.16), channel_id=1, source_target_pairs={{0,4},{4,0},{8,12},{12,8},{16,20},{20,16},{24,28},{28,24},{1,5},{5... | collective-permute-start | bytes 196616 | tf_op jit(solution)/shard_map/ppermute | solution.py:18
  71.1 3.1 %collective-permute-start.15 = (bf16[32,128]{1,0:T(8,128)(2,1)S(1)}, bf16[32,128]{1,0:T(8,128)(2,1)S(1)}, u32[]{:S(2)}, u32[]{:S(2)}) collective-permute-start(bf16[32,128]{1,0:T(8,128)(2,1)S(1)} %bitcast.311), channel_id=1, source_target_pairs={{0,1},{1,2},{2,3},{3,0},{4,5},{5,6},{6,7},{7,4},{8,9},{9,10},{10,1... | collective-permute-start | bytes 24584 | tf_op jit(solution)/shard_map/ppermute | solution.py:14
  71.9 8.9 %collective-permute-start.16 = (f32[32,128]{1,0:T(8,128)}, f32[32,128]{1,0:T(8,128)S(1)}, u32[]{:S(2)}, u32[]{:S(2)}) collective-permute-start(f32[32,128]{1,0:T(8,128)} %fusion.85), channel_id=1, source_target_pairs={{0,3},{1,0},{2,1},{3,2},{4,7},{5,4},{6,5},{7,6},{8,11},{9,8},{10,9... | collective-permute-start | bytes 49160 | tf_op jit(solution)/shard_map/ppermute | solution.py:14
  78.8 4.3 %collective-permute-start.17 = (bf16[8,32,128]{2,0,1:T(8,128)(2,1)S(1)}, bf16[8,32,128]{2,0,1:T(8,128)(2,1)S(1)}, u32[]{:S(2)}, u32[]{:S(2)}) collective-permute-start(bf16[8,32,128]{2,0,1:T(8,128)(2,1)S(1)} %convolution_convert_fusion.10), channel_id=1, source_target_pairs={{0,4},{4,0},{8,12},{12,8},{16,20},{20,16},{24,28},{28,24},{1,5},{5... | collective-permute-start | bytes 196616 | tf_op jit(solution)/shard_map/ppermute | solution.py:18
  94.3 5.0 %collective-permute-start.18 = (bf16[8,32,128]{2,0,1:T(8,128)(2,1)S(1)}, bf16[8,32,128]{2,0,1:T(8,128)(2,1)S(1)}, u32[]{:S(2)}, u32[]{:S(2)}) collective-permute-start(bf16[8,32,128]{2,0,1:T(8,128)(2,1)S(1)} %get-tuple-element.18), channel_id=1, source_target_pairs={{0,4},{4,0},{8,12},{12,8},{16,20},{20,16},{24,28},{28,24},{1,5},{5... | collective-permute-start | bytes 196616 | tf_op jit(solution)/shard_map/ppermute | solution.py:18
  96.1 9.8 %collective-permute-start.20 = (f32[32,128]{1,0:T(8,128)}, f32[32,128]{1,0:T(8,128)S(1)}, u32[]{:S(2)}, u32[]{:S(2)}) collective-permute-start(f32[32,128]{1,0:T(8,128)} %fusion.81), channel_id=1, source_target_pairs={{0,3},{1,0},{2,1},{3,2},{4,7},{5,4},{6,5},{7,6},{8,11},{9,8},{10,9... | collective-permute-start | bytes 49160 | tf_op jit(solution)/shard_map/ppermute | solution.py:14
  96.1 3.2 %collective-permute-start.19 = (bf16[32,128]{1,0:T(8,128)(2,1)S(1)}, bf16[32,128]{1,0:T(8,128)(2,1)S(1)}, u32[]{:S(2)}, u32[]{:S(2)}) collective-permute-start(bf16[32,128]{1,0:T(8,128)(2,1)S(1)} %bitcast.312), channel_id=1, source_target_pairs={{0,1},{1,2},{2,3},{3,0},{4,5},{5,6},{6,7},{7,4},{8,9},{9,10},{10,1... | collective-permute-start | bytes 24584 | tf_op jit(solution)/shard_map/ppermute | solution.py:14
  103.8 4.3 %collective-permute-start.21 = (bf16[8,32,128]{2,0,1:T(8,128)(2,1)S(1)}, bf16[8,32,128]{2,0,1:T(8,128)(2,1)S(1)}, u32[]{:S(2)}, u32[]{:S(2)}) collective-permute-start(bf16[8,32,128]{2,0,1:T(8,128)(2,1)S(1)} %convolution_convert_fusion.9), channel_id=1, source_target_pairs={{0,4},{4,0},{8,12},{12,8},{16,20},{20,16},{24,28},{28,24},{1,5},{5... | collective-permute-start | bytes 196616 | tf_op jit(solution)/shard_map/ppermute | solution.py:18
  105.6 12.8 %copy-start.6 = (f32[8,32,128]{2,0,1:T(8,128)S(1)}, f32[8,32,128]{2,0,1:T(8,128)}, u32[]{:S(2)}) copy-start(f32[8,32,128]{2,0,1:T(8,128)} %copy-done.5) | copy-start | bytes 393220
  (19 other events, 98.6 us)

commit v11 on v9

--- a/solution.py
+++ b/solution.py
@@ -57,7 +57,9 @@
     ).astype(jnp.bfloat16)
     terms = jnp.einsum("srj,skj->srk", multiplier, contact_set, preferred_element_type=jnp.float32)
     far_sum = jnp.einsum("sn,srk->nrk", far_collect, terms, precision=lax.Precision.HIGHEST)
-    far_sum, rounded = lax.optimization_barrier((far_sum.astype(jnp.bfloat16), rounded))
+    far_sum, rounded, terms = lax.optimization_barrier(
+        (far_sum.astype(jnp.bfloat16), rounded, terms)
+    )
     far_terms = partner(far_sum, "dom", 0).astype(jnp.float32)
     result = local_stiffness(rounded, diag_tiles, off_tiles, cols_onehot, mirror_onehot)
     first_add = jnp.dot(before, link_tile, preferred_element_type=jnp.float32)

time: 120 us -> 118 us (0.983)
  waiting for transfers between devices: 22.2 us -> 20 us
    ppermute x8, waiting for transfers between devices: 8.88 us -> 6.59 us  [partner(): lax.ppermute(value, axis, [(i, i ^ 1 << distance) for i in range(lax.axis...]
where the time goes in v11:
time: 118 us
  blocking collectives  39.9 us (34%)
  matrix products  25.7 us (22%)
  waiting for transfers between devices  20 us (17%)
  starting transfers between devices  19.5 us (17%)
  other arithmetic  6.74 us (6%)
  local copies, waits for them, and re-layouts  4.58 us (4%)
  between operations  1.32 us (1%)
    all_to_all x4, blocking collectives, total(): gathered = lax.all_to_all(spread, ('dom', 'rep'), 0, 0, tiled=True)  39.9 us
    ppermute x14, waiting for transfers between devices, from_behind(): return lax.ppermute(value, axis, pairs)  13.4 us
    ppermute x14, starting transfers between devices, from_behind(): return lax.ppermute(value, axis, pairs)  10.2 us
    ppermute x8, starting transfers between devices, partner(): lax.ppermute(value, axis, [(i, i ^ 1 << distance) for i in range(lax.axis...  9.36 us
    ppermute x8, waiting for transfers between devices, partner(): lax.ppermute(value, axis, [(i, i ^ 1 << distance) for i in range(lax.axis...  6.59 us
    dot_general x4, matrix products, apply_operator(): jnp.einsum('srj,skj->srk', multiplier, contact_set, preferred_element_typ...  6.53 us
    unnamed x55, local copies, waits for them, and re-layouts  3.34 us
    dot_general x4, matrix products, local_stiffness(): jnp.einsum('pn,prj->nrj', mirror_onehot, mirror, precision=lax.Precision....  3.2 us
  transfers between devices with their start and end apart: 22, of which 10 were waited for; matrix products, arithmetic and copies ran while one was open for 20% of the time, Pallas kernels for 0%

profile of v11, /device:TPU:0, one launch (start us, length us, event | category | flops | bytes accessed | tf_op | source)
XLA Modules:
  0.0 117.8 jit_solution(2431658342732879704)
XLA Ops:
  3.7 2.4 %collective-permute-start.6 = (bf16[8,128,128]{2,0,1:T(8,128)(2,1)S(1)}, bf16[8,128,128]{2,0,1:T(8,128)(2,1)S(1)}, u32[]{:S(2)}, u32[]{:S(2)}) collective-permute-start(bf16[8,128,128]{2,0,1:T(8,128)(2,1)S(1)} %select_bitcast_fusion), channel_id=1, source_target_pairs={{0,3},{1,0},{2,1},{3,2},{4,7},{5,4},{6,5},{7,6},{8,11},{9,8},{10,9... | collective-permute-start | bytes 786440 | tf_op jit(solution)/shard_map/ppermute | solution.py:14
  7.4 1.7 %collective-permute-start.1 = (s32[8,2]{0,1:T(2,128)S(1)}, s32[8,2]{0,1:T(2,128)S(1)}, u32[]{:S(2)}, u32[]{:S(2)}) collective-permute-start(s32[8,2]{0,1:T(2,128)S(1)} %bitcast.330), channel_id=1, source_target_pairs={{0,2},{1,3},{2,0},{3,1},{4,6},{5,7},{6,4},{7,5},{8,10},{9,11},{10,... | collective-permute-start | bytes 200 | tf_op jit(solution)/shard_map/ppermute | solution.py:14
  9.2 1.6 %collective-permute-start.3 = (bf16[8,32,128]{2,0,1:T(8,128)(2,1)S(1)}, bf16[8,32,128]{2,0,1:T(8,128)(2,1)S(1)}, u32[]{:S(2)}, u32[]{:S(2)}) collective-permute-start(bf16[8,32,128]{2,0,1:T(8,128)(2,1)S(1)} %multiply_convert_fusion), channel_id=1, source_target_pairs={{0,4},{4,0},{8,12},{12,8},{16,20},{20,16},{24,28},{28,24},{1,5},{5... | collective-permute-start | bytes 196616 | tf_op jit(solution)/shard_map/ppermute | solution.py:18
  11.2 4.5 %collective-permute-done.2 = s32[8,2]{0,1:T(2,128)S(1)} collective-permute-done((s32[8,2]{0,1:T(2,128)S(1)}, s32[8,2]{0,1:T(2,128)S(1)}, u32[]{:S(2)}, u32[]{:S(2)}) %collective-permute-start.2) | collective-permute-done | bytes 96 | tf_op jit(solution)/shard_map/ppermute | solution.py:14
  16.8 2.3 %collective-permute-done = s32[8,2]{0,1:T(2,128)S(1)} collective-permute-done((s32[8,2]{0,1:T(2,128)S(1)}, s32[8,2]{0,1:T(2,128)S(1)}, u32[]{:S(2)}, u32[]{:S(2)}) %collective-permute-start) | collective-permute-done | bytes 96 | tf_op jit(solution)/shard_map/ppermute | solution.py:14
  19.7 3.0 %collective-permute-done.7 = bf16[32,128]{1,0:T(8,128)(2,1)S(1)} collective-permute-done((bf16[32,128]{1,0:T(8,128)(2,1)S(1)}, bf16[32,128]{1,0:T(8,128)(2,1)S(1)}, u32[]{:S(2)}, u32[]{:S(2)}) %collective-permute-start.7) | collective-permute-done | bytes 8224 | tf_op jit(solution)/shard_map/ppermute | solution.py:14
  25.1 1.6 %collective-permute-start.9 = (bf16[8,32,128]{2,0,1:T(8,128)(2,1)S(1)}, bf16[8,32,128]{2,0,1:T(8,128)(2,1)S(1)}, u32[]{:S(2)}, u32[]{:S(2)}) collective-permute-start(bf16[8,32,128]{2,0,1:T(8,128)(2,1)S(1)} %convolution_convert_fusion.12), channel_id=1, source_target_pairs={{0,4},{4,0},{8,12},{12,8},{16,20},{20,16},{24,28},{28,24},{1,5},{5... | collective-permute-start | bytes 196616 | tf_op jit(solution)/shard_map/ppermute | solution.py:18
  28.2 1.5 %collective-permute-done.9 = bf16[8,32,128]{2,0,1:T(8,128)(2,1)S(1)} collective-permute-done((bf16[8,32,128]{2,0,1:T(8,128)(2,1)S(1)}, bf16[8,32,128]{2,0,1:T(8,128)(2,1)S(1)}, u32[]{:S(2)}, u32[]{:S(2)}) %collective-permute-start.9) | collective-permute-done | bytes 65568 | tf_op jit(solution)/shard_map/ppermute | solution.py:18
  30.6 12.8 %all_to_all.20 = f32[32,1,128]{2,1,0:T(1,128)S(1)} all-to-all(f32[32,1,128]{2,1,0:T(1,128)S(1)} %reshape.371), channel_id=1, replica_groups=mesh['dom'=8,'rep'=4] {'dom','rep'}, dimensions={0} | all-to-all | bytes 32768 | tf_op jit(solution)/shard_map/all_to_all | solution.py:24
  46.5 1.8 %collective-permute-start.12 = (f32[32,128]{1,0:T(8,128)S(1)}, f32[32,128]{1,0:T(8,128)S(1)}, u32[]{:S(2)}, u32[]{:S(2)}) collective-permute-start(f32[32,128]{1,0:T(8,128)S(1)} %fusion.89), channel_id=1, source_target_pairs={{0,3},{1,0},{2,1},{3,2},{4,7},{5,4},{6,5},{7,6},{8,11},{9,8},{10,9... | collective-permute-start | bytes 49160 | tf_op jit(solution)/shard_map/ppermute | solution.py:14
  50.5 1.9 %fusion.6 = f32[32,32,128]{2,1,0:T(8,128)S(1)} fusion(bf16[32,128,128]{2,1,0:T(8,128)(2,1)S(1)} %bitcast.283, bf16[32,32,128]{2,0,1:T(8,128)(2,1)} %fusion.2), kind=kOutput, calls=%fused_computation.15 | convolution fusion | flops 67239936 | bytes 1835008 | tf_op jit(solution)/shard_map/srj,skj->srk/dot_general | solution.py:58
  53.4 1.5 %collective-permute-start.13 = (bf16[8,32,128]{2,0,1:T(8,128)(2,1)S(1)}, bf16[8,32,128]{2,0,1:T(8,128)(2,1)S(1)}, u32[]{:S(2)}, u32[]{:S(2)}) collective-permute-start(bf16[8,32,128]{2,0,1:T(8,128)(2,1)S(1)} %convolution_convert_fusion.11), channel_id=1, source_target_pairs={{0,4},{4,0},{8,12},{12,8},{16,20},{20,16},{24,28},{28,24},{1,5},{5... | collective-permute-start | bytes 196616 | tf_op jit(solution)/shard_map/ppermute | solution.py:18
  56.0 1.7 %collective-permute-done.13 = bf16[8,32,128]{2,0,1:T(8,128)(2,1)S(1)} collective-permute-done((bf16[8,32,128]{2,0,1:T(8,128)(2,1)S(1)}, bf16[8,32,128]{2,0,1:T(8,128)(2,1)S(1)}, u32[]{:S(2)}, u32[]{:S(2)}) %collective-permute-start.13) | collective-permute-done | bytes 65568 | tf_op jit(solution)/shard_map/ppermute | solution.py:18
  58.7 8.8 %all_to_all.21 = f32[32,1,128]{2,1,0:T(1,128)S(1)} all-to-all(f32[32,1,128]{2,1,0:T(1,128)S(1)} %reshape.373), channel_id=1, replica_groups=mesh['dom'=8,'rep'=4] {'dom','rep'}, dimensions={0} | all-to-all | bytes 32768 | tf_op jit(solution)/shard_map/all_to_all | solution.py:24
  70.7 1.7 %collective-permute-start.16 = (f32[32,128]{1,0:T(8,128)}, f32[32,128]{1,0:T(8,128)S(1)}, u32[]{:S(2)}, u32[]{:S(2)}) collective-permute-start(f32[32,128]{1,0:T(8,128)} %fusion.85), channel_id=1, source_target_pairs={{0,3},{1,0},{2,1},{3,2},{4,7},{5,4},{6,5},{7,6},{8,11},{9,8},{10,9... | collective-permute-start | bytes 49160 | tf_op jit(solution)/shard_map/ppermute | solution.py:14
  74.1 1.9 %fusion.7 = f32[32,32,128]{2,1,0:T(8,128)S(1)} fusion(bf16[32,128,128]{2,1,0:T(8,128)(2,1)S(1)} %bitcast.284, bf16[32,32,128]{2,0,1:T(8,128)(2,1)} %fusion.3), kind=kOutput, calls=%fused_computation.16 | convolution fusion | flops 67239936 | bytes 1835008 | tf_op jit(solution)/shard_map/srj,skj->srk/dot_general | solution.py:58
  77.0 1.5 %collective-permute-start.17 = (bf16[8,32,128]{2,0,1:T(8,128)(2,1)S(1)}, bf16[8,32,128]{2,0,1:T(8,128)(2,1)S(1)}, u32[]{:S(2)}, u32[]{:S(2)}) collective-permute-start(bf16[8,32,128]{2,0,1:T(8,128)(2,1)S(1)} %convolution_convert_fusion.10), channel_id=1, source_target_pairs={{0,4},{4,0},{8,12},{12,8},{16,20},{20,16},{24,28},{28,24},{1,5},{5... | collective-permute-start | bytes 196616 | tf_op jit(solution)/shard_map/ppermute | solution.py:18
  79.6 1.7 %collective-permute-done.17 = bf16[8,32,128]{2,0,1:T(8,128)(2,1)S(1)} collective-permute-done((bf16[8,32,128]{2,0,1:T(8,128)(2,1)S(1)}, bf16[8,32,128]{2,0,1:T(8,128)(2,1)S(1)}, u32[]{:S(2)}, u32[]{:S(2)}) %collective-permute-start.17) | collective-permute-done | bytes 65568 | tf_op jit(solution)/shard_map/ppermute | solution.py:18
  82.3 8.8 %all_to_all.22 = f32[32,1,128]{2,1,0:T(1,128)S(1)} all-to-all(f32[32,1,128]{2,1,0:T(1,128)S(1)} %reshape.375), channel_id=1, replica_groups=mesh['dom'=8,'rep'=4] {'dom','rep'}, dimensions={0} | all-to-all | bytes 32768 | tf_op jit(solution)/shard_map/all_to_all | solution.py:24
  95.8 1.7 %collective-permute-done.19 = bf16[32,128]{1,0:T(8,128)(2,1)S(1)} collective-permute-done((bf16[32,128]{1,0:T(8,128)(2,1)S(1)}, bf16[32,128]{1,0:T(8,128)(2,1)S(1)}, u32[]{:S(2)}, u32[]{:S(2)}) %collective-permute-start.19) | collective-permute-done | bytes 8224 | tf_op jit(solution)/shard_map/ppermute | solution.py:14
  98.6 1.9 %fusion.8 = f32[32,32,128]{2,1,0:T(8,128)S(1)} fusion(bf16[32,128,128]{2,1,0:T(8,128)(2,1)S(1)} %bitcast.285, bf16[32,32,128]{2,0,1:T(8,128)(2,1)} %fusion.4), kind=kOutput, calls=%fused_computation.17 | convolution fusion | flops 67239936 | bytes 1835008 | tf_op jit(solution)/shard_map/srj,skj->srk/dot_general | solution.py:58
  101.5 1.5 %collective-permute-start.21 = (bf16[8,32,128]{2,0,1:T(8,128)(2,1)S(1)}, bf16[8,32,128]{2,0,1:T(8,128)(2,1)S(1)}, u32[]{:S(2)}, u32[]{:S(2)}) collective-permute-start(bf16[8,32,128]{2,0,1:T(8,128)(2,1)S(1)} %convolution_convert_fusion.9), channel_id=1, source_target_pairs={{0,4},{4,0},{8,12},{12,8},{16,20},{20,16},{24,28},{28,24},{1,5},{5... | collective-permute-start | bytes 196616 | tf_op jit(solution)/shard_map/ppermute | solution.py:18
  104.1 1.7 %collective-permute-done.21 = bf16[8,32,128]{2,0,1:T(8,128)(2,1)S(1)} collective-permute-done((bf16[8,32,128]{2,0,1:T(8,128)(2,1)S(1)}, bf16[8,32,128]{2,0,1:T(8,128)(2,1)S(1)}, u32[]{:S(2)}, u32[]{:S(2)}) %collective-permute-start.21) | collective-permute-done | bytes 65568 | tf_op jit(solution)/shard_map/ppermute | solution.py:18
  106.6 9.5 %all_to_all.23 = f32[32,2,32]{2,1,0:T(2,128)S(1)} all-to-all(f32[32,2,32]{2,1,0:T(2,128)S(1)} %broadcast_in_dim.115), channel_id=1, replica_groups=mesh['dom'=8,'rep'=4] {'dom','rep'}, dimensions={0} | all-to-all | bytes 16384 | tf_op jit(solution)/shard_map/all_to_all | solution.py:24
  (178 shorter events, 37.4 us)
Async XLA Ops:
  3.7 19.4 %collective-permute-start.6 = (bf16[8,128,128]{2,0,1:T(8,128)(2,1)S(1)}, bf16[8,128,128]{2,0,1:T(8,128)(2,1)S(1)}, u32[]{:S(2)}, u32[]{:S(2)}) collective-permute-start(bf16[8,128,128]{2,0,1:T(8,128)(2,1)S(1)} %select_bitcast_fusion), channel_id=1, source_target_pairs={{0,3},{1,0},{2,1},{3,2},{4,7},{5,4},{6,5},{7,6},{8,11},{9,8},{10,9... | collective-permute-start | bytes 786440 | tf_op jit(solution)/shard_map/ppermute | solution.py:14
  6.3 16.9 %collective-permute-start.5 = (bf16[8,128,128]{2,0,1:T(8,128)(2,1)S(1)}, bf16[8,128,128]{2,0,1:T(8,128)(2,1)S(1)}, u32[]{:S(2)}, u32[]{:S(2)}) collective-permute-start(bf16[8,128,128]{2,0,1:T(8,128)(2,1)S(1)} %get-tuple-element.86), channel_id=1, source_target_pairs={{0,2},{1,3},{2,0},{3,1},{4,6},{5,7},{6,4},{7,5},{8,10},{9,11},{10,... | collective-permute-start | bytes 786440 | tf_op jit(solution)/shard_map/ppermute | solution.py:14
  7.2 8.5 %collective-permute-start.2 = (s32[8,2]{0,1:T(2,128)S(1)}, s32[8,2]{0,1:T(2,128)S(1)}, u32[]{:S(2)}, u32[]{:S(2)}) collective-permute-start(s32[8,2]{0,1:T(2,128)S(1)} %bitcast.331), channel_id=1, source_target_pairs={{0,3},{1,0},{2,1},{3,2},{4,7},{5,4},{6,5},{7,6},{8,11},{9,8},{10,9... | collective-permute-start | bytes 200 | tf_op jit(solution)/shard_map/ppermute | solution.py:14
  7.4 9.5 %collective-permute-start.1 = (s32[8,2]{0,1:T(2,128)S(1)}, s32[8,2]{0,1:T(2,128)S(1)}, u32[]{:S(2)}, u32[]{:S(2)}) collective-permute-start(s32[8,2]{0,1:T(2,128)S(1)} %bitcast.330), channel_id=1, source_target_pairs={{0,2},{1,3},{2,0},{3,1},{4,6},{5,7},{6,4},{7,5},{8,10},{9,11},{10,... | collective-permute-start | bytes 200 | tf_op jit(solution)/shard_map/ppermute | solution.py:14
  9.2 13.6 %collective-permute-start.3 = (bf16[8,32,128]{2,0,1:T(8,128)(2,1)S(1)}, bf16[8,32,128]{2,0,1:T(8,128)(2,1)S(1)}, u32[]{:S(2)}, u32[]{:S(2)}) collective-permute-start(bf16[8,32,128]{2,0,1:T(8,128)(2,1)S(1)} %multiply_convert_fusion), channel_id=1, source_target_pairs={{0,4},{4,0},{8,12},{12,8},{16,20},{20,16},{24,28},{28,24},{1,5},{5... | collective-permute-start | bytes 196616 | tf_op jit(solution)/shard_map/ppermute | solution.py:18
  11.2 46.5 %copy-start.8 = (f32[8]{0:T(128)}, f32[8]{0:T(128)S(1)}, u32[]{:S(2)}) copy-start(f32[8]{0:T(128)S(1)} %pad.28.clone) | copy-start | bytes 100
  15.7 3.4 %collective-permute-start = (s32[8,2]{0,1:T(2,128)S(1)}, s32[8,2]{0,1:T(2,128)S(1)}, u32[]{:S(2)}, u32[]{:S(2)}) collective-permute-start(s32[8,2]{0,1:T(2,128)S(1)} %bitcast.329), channel_id=1, source_target_pairs={{0,1},{1,2},{2,3},{3,0},{4,5},{5,6},{6,7},{7,4},{8,9},{9,10},{10,1... | collective-permute-start | bytes 200 | tf_op jit(solution)/shard_map/ppermute | solution.py:14
  16.8 6.3 %collective-permute-start.4 = (bf16[8,128,128]{2,0,1:T(8,128)(2,1)S(1)}, bf16[8,128,128]{2,0,1:T(8,128)(2,1)S(1)}, u32[]{:S(2)}, u32[]{:S(2)}) collective-permute-start(bf16[8,128,128]{2,0,1:T(8,128)(2,1)S(1)} %get-tuple-element.85), channel_id=1, source_target_pairs={{0,1},{1,2},{2,3},{3,0},{4,5},{5,6},{6,7},{7,4},{8,9},{9,10},{10,1... | collective-permute-start | bytes 786440 | tf_op jit(solution)/shard_map/ppermute | solution.py:14
  19.1 3.6 %collective-permute-start.7 = (bf16[32,128]{1,0:T(8,128)(2,1)S(1)}, bf16[32,128]{1,0:T(8,128)(2,1)S(1)}, u32[]{:S(2)}, u32[]{:S(2)}) collective-permute-start(bf16[32,128]{1,0:T(8,128)(2,1)S(1)} %bitcast.309), channel_id=1, source_target_pairs={{0,1},{1,2},{2,3},{3,0},{4,5},{5,6},{6,7},{7,4},{8,9},{9,10},{10,1... | collective-permute-start | bytes 24584 | tf_op jit(solution)/shard_map/ppermute | solution.py:14
  22.7 5.5 %collective-permute-start.8 = (f32[32,128]{1,0:T(8,128)S(1)}, f32[32,128]{1,0:T(8,128)S(1)}, u32[]{:S(2)}, u32[]{:S(2)}) collective-permute-start(f32[32,128]{1,0:T(8,128)S(1)} %fusion.93), channel_id=1, source_target_pairs={{0,3},{1,0},{2,1},{3,2},{4,7},{5,4},{6,5},{7,6},{8,11},{9,8},{10,9... | collective-permute-start | bytes 49160 | tf_op jit(solution)/shard_map/ppermute | solution.py:14
  25.1 4.6 %collective-permute-start.9 = (bf16[8,32,128]{2,0,1:T(8,128)(2,1)S(1)}, bf16[8,32,128]{2,0,1:T(8,128)(2,1)S(1)}, u32[]{:S(2)}, u32[]{:S(2)}) collective-permute-start(bf16[8,32,128]{2,0,1:T(8,128)(2,1)S(1)} %convolution_convert_fusion.12), channel_id=1, source_target_pairs={{0,4},{4,0},{8,12},{12,8},{16,20},{20,16},{24,28},{28,24},{1,5},{5... | collective-permute-start | bytes 196616 | tf_op jit(solution)/shard_map/ppermute | solution.py:18
  45.3 4.3 %collective-permute-start.10 = (bf16[8,32,128]{2,0,1:T(8,128)(2,1)S(1)}, bf16[8,32,128]{2,0,1:T(8,128)(2,1)S(1)}, u32[]{:S(2)}, u32[]{:S(2)}) collective-permute-start(bf16[8,32,128]{2,0,1:T(8,128)(2,1)S(1)} %get-tuple-element.19), channel_id=1, source_target_pairs={{0,4},{4,0},{8,12},{12,8},{16,20},{20,16},{24,28},{28,24},{1,5},{5... | collective-permute-start | bytes 196616 | tf_op jit(solution)/shard_map/ppermute | solution.py:18
  46.3 3.1 %collective-permute-start.11 = (bf16[32,128]{1,0:T(8,128)(2,1)S(1)}, bf16[32,128]{1,0:T(8,128)(2,1)S(1)}, u32[]{:S(2)}, u32[]{:S(2)}) collective-permute-start(bf16[32,128]{1,0:T(8,128)(2,1)S(1)} %bitcast.310), channel_id=1, source_target_pairs={{0,1},{1,2},{2,3},{3,0},{4,5},{5,6},{6,7},{7,4},{8,9},{9,10},{10,1... | collective-permute-start | bytes 24584 | tf_op jit(solution)/shard_map/ppermute | solution.py:14
  46.5 9.5 %collective-permute-start.12 = (f32[32,128]{1,0:T(8,128)S(1)}, f32[32,128]{1,0:T(8,128)S(1)}, u32[]{:S(2)}, u32[]{:S(2)}) collective-permute-start(f32[32,128]{1,0:T(8,128)S(1)} %fusion.89), channel_id=1, source_target_pairs={{0,3},{1,0},{2,1},{3,2},{4,7},{5,4},{6,5},{7,6},{8,11},{9,8},{10,9... | collective-permute-start | bytes 49160 | tf_op jit(solution)/shard_map/ppermute | solution.py:14
  53.4 4.3 %collective-permute-start.13 = (bf16[8,32,128]{2,0,1:T(8,128)(2,1)S(1)}, bf16[8,32,128]{2,0,1:T(8,128)(2,1)S(1)}, u32[]{:S(2)}, u32[]{:S(2)}) collective-permute-start(bf16[8,32,128]{2,0,1:T(8,128)(2,1)S(1)} %convolution_convert_fusion.11), channel_id=1, source_target_pairs={{0,4},{4,0},{8,12},{12,8},{16,20},{20,16},{24,28},{28,24},{1,5},{5... | collective-permute-start | bytes 196616 | tf_op jit(solution)/shard_map/ppermute | solution.py:18
  68.9 4.3 %collective-permute-start.14 = (bf16[8,32,128]{2,0,1:T(8,128)(2,1)S(1)}, bf16[8,32,128]{2,0,1:T(8,128)(2,1)S(1)}, u32[]{:S(2)}, u32[]{:S(2)}) collective-permute-start(bf16[8,32,128]{2,0,1:T(8,128)(2,1)S(1)} %get-tuple-element.22), channel_id=1, source_target_pairs={{0,4},{4,0},{8,12},{12,8},{16,20},{20,16},{24,28},{28,24},{1,5},{5... | collective-permute-start | bytes 196616 | tf_op jit(solution)/shard_map/ppermute | solution.py:18
  69.9 3.1 %collective-permute-start.15 = (bf16[32,128]{1,0:T(8,128)(2,1)S(1)}, bf16[32,128]{1,0:T(8,128)(2,1)S(1)}, u32[]{:S(2)}, u32[]{:S(2)}) collective-permute-start(bf16[32,128]{1,0:T(8,128)(2,1)S(1)} %bitcast.311), channel_id=1, source_target_pairs={{0,1},{1,2},{2,3},{3,0},{4,5},{5,6},{6,7},{7,4},{8,9},{9,10},{10,1... | collective-permute-start | bytes 24584 | tf_op jit(solution)/shard_map/ppermute | solution.py:14
  70.7 8.9 %collective-permute-start.16 = (f32[32,128]{1,0:T(8,128)}, f32[32,128]{1,0:T(8,128)S(1)}, u32[]{:S(2)}, u32[]{:S(2)}) collective-permute-start(f32[32,128]{1,0:T(8,128)} %fusion.85), channel_id=1, source_target_pairs={{0,3},{1,0},{2,1},{3,2},{4,7},{5,4},{6,5},{7,6},{8,11},{9,8},{10,9... | collective-permute-start | bytes 49160 | tf_op jit(solution)/shard_map/ppermute | solution.py:14
  77.0 4.3 %collective-permute-start.17 = (bf16[8,32,128]{2,0,1:T(8,128)(2,1)S(1)}, bf16[8,32,128]{2,0,1:T(8,128)(2,1)S(1)}, u32[]{:S(2)}, u32[]{:S(2)}) collective-permute-start(bf16[8,32,128]{2,0,1:T(8,128)(2,1)S(1)} %convolution_convert_fusion.10), channel_id=1, source_target_pairs={{0,4},{4,0},{8,12},{12,8},{16,20},{20,16},{24,28},{28,24},{1,5},{5... | collective-permute-start | bytes 196616 | tf_op jit(solution)/shard_map/ppermute | solution.py:18
  92.6 5.1 %collective-permute-start.18 = (bf16[8,32,128]{2,0,1:T(8,128)(2,1)S(1)}, bf16[8,32,128]{2,0,1:T(8,128)(2,1)S(1)}, u32[]{:S(2)}, u32[]{:S(2)}) collective-permute-start(bf16[8,32,128]{2,0,1:T(8,128)(2,1)S(1)} %get-tuple-element.25), channel_id=1, source_target_pairs={{0,4},{4,0},{8,12},{12,8},{16,20},{20,16},{24,28},{28,24},{1,5},{5... | collective-permute-start | bytes 196616 | tf_op jit(solution)/shard_map/ppermute | solution.py:18
  94.4 9.8 %collective-permute-start.20 = (f32[32,128]{1,0:T(8,128)}, f32[32,128]{1,0:T(8,128)S(1)}, u32[]{:S(2)}, u32[]{:S(2)}) collective-permute-start(f32[32,128]{1,0:T(8,128)} %fusion.81), channel_id=1, source_target_pairs={{0,3},{1,0},{2,1},{3,2},{4,7},{5,4},{6,5},{7,6},{8,11},{9,8},{10,9... | collective-permute-start | bytes 49160 | tf_op jit(solution)/shard_map/ppermute | solution.py:14
  94.4 3.2 %collective-permute-start.19 = (bf16[32,128]{1,0:T(8,128)(2,1)S(1)}, bf16[32,128]{1,0:T(8,128)(2,1)S(1)}, u32[]{:S(2)}, u32[]{:S(2)}) collective-permute-start(bf16[32,128]{1,0:T(8,128)(2,1)S(1)} %bitcast.312), channel_id=1, source_target_pairs={{0,1},{1,2},{2,3},{3,0},{4,5},{5,6},{6,7},{7,4},{8,9},{9,10},{10,1... | collective-permute-start | bytes 24584 | tf_op jit(solution)/shard_map/ppermute | solution.py:14
  101.5 4.3 %collective-permute-start.21 = (bf16[8,32,128]{2,0,1:T(8,128)(2,1)S(1)}, bf16[8,32,128]{2,0,1:T(8,128)(2,1)S(1)}, u32[]{:S(2)}, u32[]{:S(2)}) collective-permute-start(bf16[8,32,128]{2,0,1:T(8,128)(2,1)S(1)} %convolution_convert_fusion.9), channel_id=1, source_target_pairs={{0,4},{4,0},{8,12},{12,8},{16,20},{20,16},{24,28},{28,24},{1,5},{5... | collective-permute-start | bytes 196616 | tf_op jit(solution)/shard_map/ppermute | solution.py:18
  103.9 12.3 %copy-start.6 = (f32[8,32,128]{2,0,1:T(8,128)S(1)}, f32[8,32,128]{2,0,1:T(8,128)}, u32[]{:S(2)}) copy-start(f32[8,32,128]{2,0,1:T(8,128)} %copy-done.5) | copy-start | bytes 393220
  (19 other events, 96.0 us)

commit v12 on v11

--- a/solution.py
+++ b/solution.py
@@ -44,10 +44,6 @@
     nodes = vector.shape[0]
     rounded = vector.astype(jnp.bfloat16)
     before = from_behind(rounded[nodes - 1], "rep", 1)
-    back_term = lax.dot_general(
-        rounded[0], link_tile, (((1,), (1,)), ((), ())), preferred_element_type=jnp.float32
-    )
-    after = from_behind(back_term, "rep", -1)
     other = partner(rounded, "dom", 0).astype(vector.dtype)
     near = jnp.einsum("sn,nrk->srk", near_onehot, vector, precision=lax.Precision.HIGHEST)
     far = jnp.einsum("sn,nrk->srk", far_onehot, other, precision=lax.Precision.HIGHEST)
@@ -61,6 +57,10 @@
         (far_sum.astype(jnp.bfloat16), rounded, terms)
     )
     far_terms = partner(far_sum, "dom", 0).astype(jnp.float32)
+    back_term = lax.dot_general(
+        rounded[0], link_tile, (((1,), (1,)), ((), ())), preferred_element_type=jnp.float32
+    )
+    after = from_behind(back_term, "rep", -1)
     result = local_stiffness(rounded, diag_tiles, off_tiles, cols_onehot, mirror_onehot)
     first_add = jnp.dot(before, link_tile, preferred_element_type=jnp.float32)
     ends = jnp.concatenate(

time: 118 us -> 116 us (0.983)
  waiting for transfers between devices: 20 us -> 24.6 us
  starting transfers between devices: 19.5 us -> 15.4 us
  matrix products: 25.7 us -> 24.4 us
  local copies, waits for them, and re-layouts: 4.58 us -> 3.38 us
    ppermute x14, waiting for transfers between devices: 13.4 us -> 20.9 us  [from_behind(): return lax.ppermute(value, axis, pairs)]
    ppermute x14, starting transfers between devices: 10.2 us -> 6.46 us  [from_behind(): return lax.ppermute(value, axis, pairs)]
    ppermute x8, waiting for transfers between devices: 6.59 us -> 3.69 us  [partner(): lax.ppermute(value, axis, [(i, i ^ 1 << distance) for i in range(lax.axis...]
    dot_general x4, matrix products: 1.77 us -> 0.52 us  [apply_operator(): lax.dot_general(rounded[0], link_tile, (((1,), (1,)), ((), ())), preferre...]
    unnamed x55 -> x37, local copies, waits for them, and re-layouts: 3.34 us -> 2.13 us
  transfers between devices with their start and end apart: 22 -> 22, of which waited for: 10 -> 16; matrix products, arithmetic and copies ran while one was open for 20% -> 8% of each run, Pallas kernels for 0% -> 0%
where the time goes in v12:
time: 116 us; the launch traced here: 115 us
  blocking collectives  39.4 us (34%)
  waiting for transfers between devices  24.6 us (21%)
  matrix products  24.4 us (21%)
  starting transfers between devices  15.4 us (13%)
  other arithmetic  6.67 us (6%)
  local copies, waits for them, and re-layouts  3.38 us (3%)
  between operations  1.29 us (1%)
    all_to_all x4, blocking collectives, total(): gathered = lax.all_to_all(spread, ('dom', 'rep'), 0, 0, tiled=True)  39.4 us
    ppermute x14, waiting for transfers between devices, from_behind(): return lax.ppermute(value, axis, pairs)  20.9 us
    ppermute x8, starting transfers between devices, partner(): lax.ppermute(value, axis, [(i, i ^ 1 << distance) for i in range(lax.axis...  8.92 us
    dot_general x4, matrix products, apply_operator(): jnp.einsum('srj,skj->srk', multiplier, contact_set, preferred_element_typ...  6.53 us
    ppermute x14, starting transfers between devices, from_behind(): return lax.ppermute(value, axis, pairs)  6.46 us
    ppermute x8, waiting for transfers between devices, partner(): lax.ppermute(value, axis, [(i, i ^ 1 << distance) for i in range(lax.axis...  3.69 us
    dot_general x4, matrix products, local_stiffness(): jnp.einsum('pn,prj->nrj', mirror_onehot, mirror, precision=lax.Precision....  3.2 us
    dot_general x4, matrix products, apply_operator(): jnp.einsum('sn,nrk->srk', far_onehot, other, precision=lax.Precision.HIGH...  3.16 us
  transfers between devices with their start and end apart: 22, of which 16 were waited for; matrix products, arithmetic and copies ran while one was open for 8% of the time, Pallas kernels for 0%

profile of v12, /device:TPU:0, one launch (start us, length us, event | category | flops | bytes accessed | tf_op | source)
XLA Modules:
  0.0 115.2 jit_solution(10139055316796089720)
XLA Ops:
  3.7 2.4 %collective-permute-start.6 = (bf16[8,128,128]{2,0,1:T(8,128)(2,1)S(1)}, bf16[8,128,128]{2,0,1:T(8,128)(2,1)S(1)}, u32[]{:S(2)}, u32[]{:S(2)}) collective-permute-start(bf16[8,128,128]{2,0,1:T(8,128)(2,1)S(1)} %select_bitcast_fusion), channel_id=1, source_target_pairs={{0,3},{1,0},{2,1},{3,2},{4,7},{5,4},{6,5},{7,6},{8,11},{9,8},{10,9... | collective-permute-start | bytes 786440 | tf_op jit(solution)/shard_map/ppermute | solution.py:14
  7.3 1.7 %collective-permute-start.1 = (s32[8,2]{0,1:T(2,128)S(1)}, s32[8,2]{0,1:T(2,128)S(1)}, u32[]{:S(2)}, u32[]{:S(2)}) collective-permute-start(s32[8,2]{0,1:T(2,128)S(1)} %bitcast.330), channel_id=1, source_target_pairs={{0,2},{1,3},{2,0},{3,1},{4,6},{5,7},{6,4},{7,5},{8,10},{9,11},{10,... | collective-permute-start | bytes 200 | tf_op jit(solution)/shard_map/ppermute | solution.py:14
  9.2 1.6 %collective-permute-start.3 = (bf16[8,32,128]{2,0,1:T(8,128)(2,1)S(1)}, bf16[8,32,128]{2,0,1:T(8,128)(2,1)S(1)}, u32[]{:S(2)}, u32[]{:S(2)}) collective-permute-start(bf16[8,32,128]{2,0,1:T(8,128)(2,1)S(1)} %multiply_convert_fusion), channel_id=1, source_target_pairs={{0,4},{4,0},{8,12},{12,8},{16,20},{20,16},{24,28},{28,24},{1,5},{5... | collective-permute-start | bytes 196616 | tf_op jit(solution)/shard_map/ppermute | solution.py:18
  11.1 4.6 %collective-permute-done.2 = s32[8,2]{0,1:T(2,128)S(1)} collective-permute-done((s32[8,2]{0,1:T(2,128)S(1)}, s32[8,2]{0,1:T(2,128)S(1)}, u32[]{:S(2)}, u32[]{:S(2)}) %collective-permute-start.2) | collective-permute-done | bytes 96 | tf_op jit(solution)/shard_map/ppermute | solution.py:14
  15.7 1.1 collective-permute-start
  16.8 2.3 %collective-permute-done = s32[8,2]{0,1:T(2,128)S(1)} collective-permute-done((s32[8,2]{0,1:T(2,128)S(1)}, s32[8,2]{0,1:T(2,128)S(1)}, u32[]{:S(2)}, u32[]{:S(2)}) %collective-permute-start) | collective-permute-done | bytes 96 | tf_op jit(solution)/shard_map/ppermute | solution.py:14
  19.6 3.0 %collective-permute-done.7 = bf16[32,128]{1,0:T(8,128)(2,1)S(1)} collective-permute-done((bf16[32,128]{1,0:T(8,128)(2,1)S(1)}, bf16[32,128]{1,0:T(8,128)(2,1)S(1)}, u32[]{:S(2)}, u32[]{:S(2)}) %collective-permute-start.7) | collective-permute-done | bytes 8224 | tf_op jit(solution)/shard_map/ppermute | solution.py:14
  25.0 1.6 %collective-permute-start.9 = (bf16[8,32,128]{2,0,1:T(8,128)(2,1)S(1)}, bf16[8,32,128]{2,0,1:T(8,128)(2,1)S(1)}, u32[]{:S(2)}, u32[]{:S(2)}) collective-permute-start(bf16[8,32,128]{2,0,1:T(8,128)(2,1)S(1)} %convolution_convert_fusion.12), channel_id=1, source_target_pairs={{0,4},{4,0},{8,12},{12,8},{16,20},{20,16},{24,28},{28,24},{1,5},{5... | collective-permute-start | bytes 196616 | tf_op jit(solution)/shard_map/ppermute | solution.py:18
  30.3 12.8 %all_to_all.20 = f32[32,1,128]{2,1,0:T(1,128)S(1)} all-to-all(f32[32,1,128]{2,1,0:T(1,128)S(1)} %reshape.371), channel_id=1, replica_groups=mesh['dom'=8,'rep'=4] {'dom','rep'}, dimensions={0} | all-to-all | bytes 32768 | tf_op jit(solution)/shard_map/all_to_all | solution.py:24
  45.8 2.6 %collective-permute-done.11 = bf16[32,128]{1,0:T(8,128)(2,1)S(1)} collective-permute-done((bf16[32,128]{1,0:T(8,128)(2,1)S(1)}, bf16[32,128]{1,0:T(8,128)(2,1)S(1)}, u32[]{:S(2)}, u32[]{:S(2)}) %collective-permute-start.11) | collective-permute-done | bytes 8224 | tf_op jit(solution)/shard_map/ppermute | solution.py:14
  49.9 1.9 %fusion.6 = f32[32,32,128]{2,1,0:T(8,128)S(1)} fusion(bf16[32,128,128]{2,1,0:T(8,128)(2,1)S(1)} %bitcast.283, bf16[32,32,128]{2,0,1:T(8,128)(2,1)} %fusion.2), kind=kOutput, calls=%fused_computation.15 | convolution fusion | flops 67239936 | bytes 1835008 | tf_op jit(solution)/shard_map/srj,skj->srk/dot_general | solution.py:54
  52.8 1.1 collective-permute-start.13
  56.1 1.0 collective-permute-done.13
  58.1 8.8 %all_to_all.21 = f32[32,1,128]{2,1,0:T(1,128)S(1)} all-to-all(f32[32,1,128]{2,1,0:T(1,128)S(1)} %reshape.373), channel_id=1, replica_groups=mesh['dom'=8,'rep'=4] {'dom','rep'}, dimensions={0} | all-to-all | bytes 32768 | tf_op jit(solution)/shard_map/all_to_all | solution.py:24
  69.3 2.6 %collective-permute-done.15 = bf16[32,128]{1,0:T(8,128)(2,1)S(1)} collective-permute-done((bf16[32,128]{1,0:T(8,128)(2,1)S(1)}, bf16[32,128]{1,0:T(8,128)(2,1)S(1)}, u32[]{:S(2)}, u32[]{:S(2)}) %collective-permute-start.15) | collective-permute-done | bytes 8224 | tf_op jit(solution)/shard_map/ppermute | solution.py:14
  72.3 1.0 fusion.3
  73.2 1.9 %fusion.7 = f32[32,32,128]{2,1,0:T(8,128)S(1)} fusion(bf16[32,128,128]{2,1,0:T(8,128)(2,1)S(1)} %bitcast.284, bf16[32,32,128]{2,0,1:T(8,128)(2,1)} %fusion.3), kind=kOutput, calls=%fused_computation.16 | convolution fusion | flops 67239936 | bytes 1835008 | tf_op jit(solution)/shard_map/srj,skj->srk/dot_general | solution.py:54
  76.1 1.3 %collective-permute-start.17 = (bf16[8,32,128]{2,0,1:T(8,128)(2,1)S(1)}, bf16[8,32,128]{2,0,1:T(8,128)(2,1)S(1)}, u32[]{:S(2)}, u32[]{:S(2)}) collective-permute-start(bf16[8,32,128]{2,0,1:T(8,128)(2,1)S(1)} %convolution_convert_fusion.10), channel_id=1, source_target_pairs={{0,4},{4,0},{8,12},{12,8},{16,20},{20,16},{24,28},{28,24},{1,5},{5... | collective-permute-start | bytes 196616 | tf_op jit(solution)/shard_map/ppermute | solution.py:18
  81.4 8.8 %all_to_all.22 = f32[32,1,128]{2,1,0:T(1,128)S(1)} all-to-all(f32[32,1,128]{2,1,0:T(1,128)S(1)} %reshape.375), channel_id=1, replica_groups=mesh['dom'=8,'rep'=4] {'dom','rep'}, dimensions={0} | all-to-all | bytes 32768 | tf_op jit(solution)/shard_map/all_to_all | solution.py:24
  93.2 2.2 %collective-permute-done.19 = bf16[32,128]{1,0:T(8,128)(2,1)S(1)} collective-permute-done((bf16[32,128]{1,0:T(8,128)(2,1)S(1)}, bf16[32,128]{1,0:T(8,128)(2,1)S(1)}, u32[]{:S(2)}, u32[]{:S(2)}) %collective-permute-start.19) | collective-permute-done | bytes 8224 | tf_op jit(solution)/shard_map/ppermute | solution.py:14
  95.6 1.0 fusion.4
  96.6 1.9 %fusion.8 = f32[32,32,128]{2,1,0:T(8,128)S(1)} fusion(bf16[32,128,128]{2,1,0:T(8,128)(2,1)S(1)} %bitcast.285, bf16[32,32,128]{2,0,1:T(8,128)(2,1)} %fusion.4), kind=kOutput, calls=%fused_computation.17 | convolution fusion | flops 67239936 | bytes 1835008 | tf_op jit(solution)/shard_map/srj,skj->srk/dot_general | solution.py:54
  99.5 1.5 %collective-permute-start.21 = (bf16[8,32,128]{2,0,1:T(8,128)(2,1)S(1)}, bf16[8,32,128]{2,0,1:T(8,128)(2,1)S(1)}, u32[]{:S(2)}, u32[]{:S(2)}) collective-permute-start(bf16[8,32,128]{2,0,1:T(8,128)(2,1)S(1)} %convolution_convert_fusion.9), channel_id=1, source_target_pairs={{0,4},{4,0},{8,12},{12,8},{16,20},{20,16},{24,28},{28,24},{1,5},{5... | collective-permute-start | bytes 196616 | tf_op jit(solution)/shard_map/ppermute | solution.py:18
  104.6 8.9 %all_to_all.23 = f32[32,2,32]{2,1,0:T(2,128)S(1)} all-to-all(f32[32,2,32]{2,1,0:T(2,128)S(1)} %broadcast_in_dim.115), channel_id=1, replica_groups=mesh['dom'=8,'rep'=4] {'dom','rep'}, dimensions={0} | all-to-all | bytes 16384 | tf_op jit(solution)/shard_map/all_to_all | solution.py:24
  (164 shorter events, 36.1 us)
Async XLA Ops:
  3.7 19.4 %collective-permute-start.6 = (bf16[8,128,128]{2,0,1:T(8,128)(2,1)S(1)}, bf16[8,128,128]{2,0,1:T(8,128)(2,1)S(1)}, u32[]{:S(2)}, u32[]{:S(2)}) collective-permute-start(bf16[8,128,128]{2,0,1:T(8,128)(2,1)S(1)} %select_bitcast_fusion), channel_id=1, source_target_pairs={{0,3},{1,0},{2,1},{3,2},{4,7},{5,4},{6,5},{7,6},{8,11},{9,8},{10,9... | collective-permute-start | bytes 786440 | tf_op jit(solution)/shard_map/ppermute | solution.py:14
  6.1 16.5 %copy-start.4 = (bf16[1,128,128]{2,1,0:T(8,128)(2,1)S(1)}, bf16[1,128,128]{2,1,0:T(8,128)(2,1)}, u32[]{:S(2)}) copy-start(bf16[1,128,128]{2,1,0:T(8,128)(2,1)} %param.19) | copy-start | bytes 98308
  6.2 16.9 %collective-permute-start.5 = (bf16[8,128,128]{2,0,1:T(8,128)(2,1)S(1)}, bf16[8,128,128]{2,0,1:T(8,128)(2,1)S(1)}, u32[]{:S(2)}, u32[]{:S(2)}) collective-permute-start(bf16[8,128,128]{2,0,1:T(8,128)(2,1)S(1)} %get-tuple-element.86), channel_id=1, source_target_pairs={{0,2},{1,3},{2,0},{3,1},{4,6},{5,7},{6,4},{7,5},{8,10},{9,11},{10,... | collective-permute-start | bytes 786440 | tf_op jit(solution)/shard_map/ppermute | solution.py:14
  7.2 8.4 %collective-permute-start.2 = (s32[8,2]{0,1:T(2,128)S(1)}, s32[8,2]{0,1:T(2,128)S(1)}, u32[]{:S(2)}, u32[]{:S(2)}) collective-permute-start(s32[8,2]{0,1:T(2,128)S(1)} %bitcast.331), channel_id=1, source_target_pairs={{0,3},{1,0},{2,1},{3,2},{4,7},{5,4},{6,5},{7,6},{8,11},{9,8},{10,9... | collective-permute-start | bytes 200 | tf_op jit(solution)/shard_map/ppermute | solution.py:14
  7.3 9.5 %collective-permute-start.1 = (s32[8,2]{0,1:T(2,128)S(1)}, s32[8,2]{0,1:T(2,128)S(1)}, u32[]{:S(2)}, u32[]{:S(2)}) collective-permute-start(s32[8,2]{0,1:T(2,128)S(1)} %bitcast.330), channel_id=1, source_target_pairs={{0,2},{1,3},{2,0},{3,1},{4,6},{5,7},{6,4},{7,5},{8,10},{9,11},{10,... | collective-permute-start | bytes 200 | tf_op jit(solution)/shard_map/ppermute | solution.py:14
  9.2 13.6 %collective-permute-start.3 = (bf16[8,32,128]{2,0,1:T(8,128)(2,1)S(1)}, bf16[8,32,128]{2,0,1:T(8,128)(2,1)S(1)}, u32[]{:S(2)}, u32[]{:S(2)}) collective-permute-start(bf16[8,32,128]{2,0,1:T(8,128)(2,1)S(1)} %multiply_convert_fusion), channel_id=1, source_target_pairs={{0,4},{4,0},{8,12},{12,8},{16,20},{20,16},{24,28},{28,24},{1,5},{5... | collective-permute-start | bytes 196616 | tf_op jit(solution)/shard_map/ppermute | solution.py:18
  15.7 3.4 %collective-permute-start = (s32[8,2]{0,1:T(2,128)S(1)}, s32[8,2]{0,1:T(2,128)S(1)}, u32[]{:S(2)}, u32[]{:S(2)}) collective-permute-start(s32[8,2]{0,1:T(2,128)S(1)} %bitcast.329), channel_id=1, source_target_pairs={{0,1},{1,2},{2,3},{3,0},{4,5},{5,6},{6,7},{7,4},{8,9},{9,10},{10,1... | collective-permute-start | bytes 200 | tf_op jit(solution)/shard_map/ppermute | solution.py:14
  16.8 6.3 %collective-permute-start.4 = (bf16[8,128,128]{2,0,1:T(8,128)(2,1)S(1)}, bf16[8,128,128]{2,0,1:T(8,128)(2,1)S(1)}, u32[]{:S(2)}, u32[]{:S(2)}) collective-permute-start(bf16[8,128,128]{2,0,1:T(8,128)(2,1)S(1)} %get-tuple-element.85), channel_id=1, source_target_pairs={{0,1},{1,2},{2,3},{3,0},{4,5},{5,6},{6,7},{7,4},{8,9},{9,10},{10,1... | collective-permute-start | bytes 786440 | tf_op jit(solution)/shard_map/ppermute | solution.py:14
  19.1 3.6 %collective-permute-start.7 = (bf16[32,128]{1,0:T(8,128)(2,1)S(1)}, bf16[32,128]{1,0:T(8,128)(2,1)S(1)}, u32[]{:S(2)}, u32[]{:S(2)}) collective-permute-start(bf16[32,128]{1,0:T(8,128)(2,1)S(1)} %bitcast.309), channel_id=1, source_target_pairs={{0,1},{1,2},{2,3},{3,0},{4,5},{5,6},{6,7},{7,4},{8,9},{9,10},{10,1... | collective-permute-start | bytes 24584 | tf_op jit(solution)/shard_map/ppermute | solution.py:14
  25.0 4.3 %collective-permute-start.9 = (bf16[8,32,128]{2,0,1:T(8,128)(2,1)S(1)}, bf16[8,32,128]{2,0,1:T(8,128)(2,1)S(1)}, u32[]{:S(2)}, u32[]{:S(2)}) collective-permute-start(bf16[8,32,128]{2,0,1:T(8,128)(2,1)S(1)} %convolution_convert_fusion.12), channel_id=1, source_target_pairs={{0,4},{4,0},{8,12},{12,8},{16,20},{20,16},{24,28},{28,24},{1,5},{5... | collective-permute-start | bytes 196616 | tf_op jit(solution)/shard_map/ppermute | solution.py:18
  27.4 1.5 %collective-permute-start.8 = (f32[32,128]{1,0:T(8,128)S(1)}, f32[32,128]{1,0:T(8,128)S(1)}, u32[]{:S(2)}, u32[]{:S(2)}) collective-permute-start(f32[32,128]{1,0:T(8,128)S(1)} %fusion.93), channel_id=1, source_target_pairs={{0,3},{1,0},{2,1},{3,2},{4,7},{5,4},{6,5},{7,6},{8,11},{9,8},{10,9... | collective-permute-start | bytes 49160 | tf_op jit(solution)/shard_map/ppermute | solution.py:14
  44.6 4.3 %collective-permute-start.10 = (bf16[8,32,128]{2,0,1:T(8,128)(2,1)S(1)}, bf16[8,32,128]{2,0,1:T(8,128)(2,1)S(1)}, u32[]{:S(2)}, u32[]{:S(2)}) collective-permute-start(bf16[8,32,128]{2,0,1:T(8,128)(2,1)S(1)} %get-tuple-element.19), channel_id=1, source_target_pairs={{0,4},{4,0},{8,12},{12,8},{16,20},{20,16},{24,28},{28,24},{1,5},{5... | collective-permute-start | bytes 196616 | tf_op jit(solution)/shard_map/ppermute | solution.py:18
  45.3 3.1 %collective-permute-start.11 = (bf16[32,128]{1,0:T(8,128)(2,1)S(1)}, bf16[32,128]{1,0:T(8,128)(2,1)S(1)}, u32[]{:S(2)}, u32[]{:S(2)}) collective-permute-start(bf16[32,128]{1,0:T(8,128)(2,1)S(1)} %bitcast.311), channel_id=1, source_target_pairs={{0,1},{1,2},{2,3},{3,0},{4,5},{5,6},{6,7},{7,4},{8,9},{9,10},{10,1... | collective-permute-start | bytes 24584 | tf_op jit(solution)/shard_map/ppermute | solution.py:14
  52.8 4.3 %collective-permute-start.13 = (bf16[8,32,128]{2,0,1:T(8,128)(2,1)S(1)}, bf16[8,32,128]{2,0,1:T(8,128)(2,1)S(1)}, u32[]{:S(2)}, u32[]{:S(2)}) collective-permute-start(bf16[8,32,128]{2,0,1:T(8,128)(2,1)S(1)} %convolution_convert_fusion.11), channel_id=1, source_target_pairs={{0,4},{4,0},{8,12},{12,8},{16,20},{20,16},{24,28},{28,24},{1,5},{5... | collective-permute-start | bytes 196616 | tf_op jit(solution)/shard_map/ppermute | solution.py:18
  54.7 1.5 %collective-permute-start.12 = (f32[32,128]{1,0:T(8,128)S(1)}, f32[32,128]{1,0:T(8,128)S(1)}, u32[]{:S(2)}, u32[]{:S(2)}) collective-permute-start(f32[32,128]{1,0:T(8,128)S(1)} %fusion.89), channel_id=1, source_target_pairs={{0,3},{1,0},{2,1},{3,2},{4,7},{5,4},{6,5},{7,6},{8,11},{9,8},{10,9... | collective-permute-start | bytes 49160 | tf_op jit(solution)/shard_map/ppermute | solution.py:14
  67.9 4.3 %collective-permute-start.14 = (bf16[8,32,128]{2,0,1:T(8,128)(2,1)S(1)}, bf16[8,32,128]{2,0,1:T(8,128)(2,1)S(1)}, u32[]{:S(2)}, u32[]{:S(2)}) collective-permute-start(bf16[8,32,128]{2,0,1:T(8,128)(2,1)S(1)} %get-tuple-element.22), channel_id=1, source_target_pairs={{0,4},{4,0},{8,12},{12,8},{16,20},{20,16},{24,28},{28,24},{1,5},{5... | collective-permute-start | bytes 196616 | tf_op jit(solution)/shard_map/ppermute | solution.py:18
  68.6 3.3 %collective-permute-start.15 = (bf16[32,128]{1,0:T(8,128)(2,1)S(1)}, bf16[32,128]{1,0:T(8,128)(2,1)S(1)}, u32[]{:S(2)}, u32[]{:S(2)}) collective-permute-start(bf16[32,128]{1,0:T(8,128)(2,1)S(1)} %bitcast.312), channel_id=1, source_target_pairs={{0,1},{1,2},{2,3},{3,0},{4,5},{5,6},{6,7},{7,4},{8,9},{9,10},{10,1... | collective-permute-start | bytes 24584 | tf_op jit(solution)/shard_map/ppermute | solution.py:14
  76.1 4.3 %collective-permute-start.17 = (bf16[8,32,128]{2,0,1:T(8,128)(2,1)S(1)}, bf16[8,32,128]{2,0,1:T(8,128)(2,1)S(1)}, u32[]{:S(2)}, u32[]{:S(2)}) collective-permute-start(bf16[8,32,128]{2,0,1:T(8,128)(2,1)S(1)} %convolution_convert_fusion.10), channel_id=1, source_target_pairs={{0,4},{4,0},{8,12},{12,8},{16,20},{20,16},{24,28},{28,24},{1,5},{5... | collective-permute-start | bytes 196616 | tf_op jit(solution)/shard_map/ppermute | solution.py:18
  78.1 1.5 %collective-permute-start.16 = (f32[32,128]{1,0:T(8,128)S(1)}, f32[32,128]{1,0:T(8,128)S(1)}, u32[]{:S(2)}, u32[]{:S(2)}) collective-permute-start(f32[32,128]{1,0:T(8,128)S(1)} %fusion.85), channel_id=1, source_target_pairs={{0,3},{1,0},{2,1},{3,2},{4,7},{5,4},{6,5},{7,6},{8,11},{9,8},{10,9... | collective-permute-start | bytes 49160 | tf_op jit(solution)/shard_map/ppermute | solution.py:14
  91.3 4.3 %collective-permute-start.18 = (bf16[8,32,128]{2,0,1:T(8,128)(2,1)S(1)}, bf16[8,32,128]{2,0,1:T(8,128)(2,1)S(1)}, u32[]{:S(2)}, u32[]{:S(2)}) collective-permute-start(bf16[8,32,128]{2,0,1:T(8,128)(2,1)S(1)} %get-tuple-element.25), channel_id=1, source_target_pairs={{0,4},{4,0},{8,12},{12,8},{16,20},{20,16},{24,28},{28,24},{1,5},{5... | collective-permute-start | bytes 196616 | tf_op jit(solution)/shard_map/ppermute | solution.py:18
  92.3 3.1 %collective-permute-start.19 = (bf16[32,128]{1,0:T(8,128)(2,1)S(1)}, bf16[32,128]{1,0:T(8,128)(2,1)S(1)}, u32[]{:S(2)}, u32[]{:S(2)}) collective-permute-start(bf16[32,128]{1,0:T(8,128)(2,1)S(1)} %bitcast.310), channel_id=1, source_target_pairs={{0,1},{1,2},{2,3},{3,0},{4,5},{5,6},{6,7},{7,4},{8,9},{9,10},{10,1... | collective-permute-start | bytes 24584 | tf_op jit(solution)/shard_map/ppermute | solution.py:14
  99.5 4.3 %collective-permute-start.21 = (bf16[8,32,128]{2,0,1:T(8,128)(2,1)S(1)}, bf16[8,32,128]{2,0,1:T(8,128)(2,1)S(1)}, u32[]{:S(2)}, u32[]{:S(2)}) collective-permute-start(bf16[8,32,128]{2,0,1:T(8,128)(2,1)S(1)} %convolution_convert_fusion.9), channel_id=1, source_target_pairs={{0,4},{4,0},{8,12},{12,8},{16,20},{20,16},{24,28},{28,24},{1,5},{5... | collective-permute-start | bytes 196616 | tf_op jit(solution)/shard_map/ppermute | solution.py:18
  101.7 1.5 %collective-permute-start.20 = (f32[32,128]{1,0:T(8,128)S(1)}, f32[32,128]{1,0:T(8,128)S(1)}, u32[]{:S(2)}, u32[]{:S(2)}) collective-permute-start(f32[32,128]{1,0:T(8,128)S(1)} %fusion.81), channel_id=1, source_target_pairs={{0,3},{1,0},{2,1},{3,2},{4,7},{5,4},{6,5},{7,6},{8,11},{9,8},{10,9... | collective-permute-start | bytes 49160 | tf_op jit(solution)/shard_map/ppermute | solution.py:14
  102.0 11.6 %copy-start.6 = (f32[8,32,128]{2,0,1:T(8,128)S(1)}, f32[8,32,128]{2,0,1:T(8,128)}, u32[]{:S(2)}) copy-start(f32[8,32,128]{2,0,1:T(8,128)} %copy-done.5) | copy-start | bytes 393220
  (10 other events, 40.7 us)

commit v13 on v12

--- a/solution.py
+++ b/solution.py
@@ -91,23 +91,24 @@
     pick = slot_of[None, :] == jnp.arange(groups * CAP, dtype=jnp.int32)[:, None]
     send_set = jnp.einsum(
         "sc,cij->sij", pick.astype(jnp.bfloat16), contact_tiles, preferred_element_type=jnp.float32
-    ).astype(jnp.bfloat16).reshape(groups, CAP, B, B)
+    ).astype(jnp.bfloat16)
     labels = jnp.stack([contact_anode, contact_bnode], axis=1)
-    send_labels = jnp.sum(
-        jnp.where(pick[:, :, None], labels[None, :, :], 0), axis=1
-    ).reshape(groups, CAP, 2)
+    digits = jnp.concatenate([labels // 256, labels % 256], axis=1).astype(jnp.float32)
+    send_labels = jnp.einsum(
+        "sc,cl->sl", pick.astype(jnp.float32), digits, precision=lax.Precision.HIGHEST
+    )
+    extra = jnp.pad(send_labels[:, None, :], ((0, 0), (0, 15), (0, B - 4))).astype(jnp.bfloat16)
+    payload = jnp.concatenate([send_set, extra], axis=1).reshape(groups, CAP, B + 16, B)
     lane = lax.axis_index("rep")
-    got_set = [jnp.take(send_set, lane, axis=0)]
-    got_labels = [jnp.take(send_labels, lane, axis=0)]
+    got = [jnp.take(payload, lane, axis=0)]
     for shift in range(1, groups):
         ahead = (lane + shift) % groups
-        got_set.append(from_behind(jnp.take(send_set, ahead, axis=0), "rep", shift))
-        got_labels.append(from_behind(jnp.take(send_labels, ahead, axis=0), "rep", shift))
-    got_set = jnp.stack(got_set)
-    got_labels = jnp.stack(got_labels)
+        got.append(from_behind(jnp.take(payload, ahead, axis=0), "rep", shift))
     slots = groups * CAP
-    contact_set = got_set.reshape(slots, B, B)
-    got_labels = got_labels.reshape(slots, 2)
+    got = jnp.stack(got).reshape(slots, B + 16, B)
+    contact_set = lax.optimization_barrier(got[:, :B, :])
+    digits = got[:, B, :4].astype(jnp.int32)
+    got_labels = digits[:, :2] * 256 + digits[:, 2:]
     near_index = got_labels[:, 0]
     far_index = got_labels[:, 1]
     nodes = rhs.shape[0]

time: 116 us -> 120 us (1.034)
  other arithmetic: 6.67 us -> 10.9 us
  starting transfers between devices: 15.4 us -> 14.1 us
    convert_element_type x4, other arithmetic: 0.51 us -> 2.31 us  [apply_operator(): rounded = vector.astype(jnp.bfloat16)]
    ppermute x14 -> x11, starting transfers between devices: 6.46 us -> 4.77 us  [from_behind(): return lax.ppermute(value, axis, pairs)]
    select_n x3 -> x5, other arithmetic: 0.16 us -> 1.57 us  [the longest x3 0.84 us: body(): got.append(from_behind(jnp.take(payload, ahead, axis=0), 'rep', shift))]
    unnamed x37 -> x40, local copies, waits for them, and re-layouts: 2.13 us -> 2.92 us
    ppermute x14 -> x11, waiting for transfers between devices: 20.9 us -> 21.4 us  [from_behind(): return lax.ppermute(value, axis, pairs)]
  transfers between devices with their start and end apart: 22 -> 19, of which waited for: 16 -> 15; matrix products, arithmetic and copies ran while one was open for 8% -> 8% of each run, Pallas kernels for 0% -> 0%
where the time goes in v13:
time: 120 us
  blocking collectives  39.8 us (33%)
  matrix products  24.7 us (21%)
  waiting for transfers between devices  24.7 us (21%)
  starting transfers between devices  14.1 us (12%)
  other arithmetic  10.9 us (9%)
  local copies, waits for them, and re-layouts  4.22 us (4%)
  between operations  1.29 us (1%)
    all_to_all x4, blocking collectives, total(): gathered = lax.all_to_all(spread, ('dom', 'rep'), 0, 0, tiled=True)  39.8 us
    ppermute x11, waiting for transfers between devices, from_behind(): return lax.ppermute(value, axis, pairs)  21.4 us
    ppermute x8, starting transfers between devices, partner(): lax.ppermute(value, axis, [(i, i ^ 1 << distance) for i in range(lax.axis...  9.3 us
    dot_general x4, matrix products, apply_operator(): jnp.einsum('srj,skj->srk', multiplier, contact_set, preferred_element_typ...  6.53 us
    ppermute x11, starting transfers between devices, from_behind(): return lax.ppermute(value, axis, pairs)  4.77 us
    ppermute x8, waiting for transfers between devices, partner(): lax.ppermute(value, axis, [(i, i ^ 1 << distance) for i in range(lax.axis...  3.31 us
    dot_general x4, matrix products, local_stiffness(): jnp.einsum('pn,prj->nrj', mirror_onehot, mirror, precision=lax.Precision....  3.19 us
    dot_general x4, matrix products, apply_operator(): jnp.einsum('sn,nrk->srk', far_onehot, other, precision=lax.Precision.HIGH...  3.16 us
  transfers between devices with their start and end apart: 19, of which 15 were waited for; matrix products, arithmetic and copies ran while one was open for 8% of the time, Pallas kernels for 0%

profile of v13, /device:TPU:0, one launch (start us, length us, event | category | flops | bytes accessed | tf_op | source)
XLA Modules:
  0.0 119.7 jit_solution(12616955237850802578)
XLA Ops:
  5.8 2.4 %collective-permute-start.2 = (bf16[8,144,128]{2,1,0:T(8,128)(2,1)}, bf16[8,144,128]{2,1,0:T(8,128)(2,1)S(1)}, u32[]{:S(2)}, u32[]{:S(2)}) collective-permute-start(bf16[8,144,128]{2,1,0:T(8,128)(2,1)} %fusion.25), channel_id=1, source_target_pairs={{0,3},{1,0},{2,1},{3,2},{4,7},{5,4},{6,5},{7,6},{8,11},{9,8},{10,9... | collective-permute-start | bytes 884744 | tf_op jit(solution)/shard_map/ppermute | solution.py:14
  9.3 1.6 %collective-permute-start.3 = (bf16[8,32,128]{2,0,1:T(8,128)(2,1)S(1)}, bf16[8,32,128]{2,0,1:T(8,128)(2,1)S(1)}, u32[]{:S(2)}, u32[]{:S(2)}) collective-permute-start(bf16[8,32,128]{2,0,1:T(8,128)(2,1)S(1)} %multiply_convert_fusion), channel_id=1, source_target_pairs={{0,4},{4,0},{8,12},{12,8},{16,20},{20,16},{24,28},{28,24},{1,5},{5... | collective-permute-start | bytes 196616 | tf_op jit(solution)/shard_map/ppermute | solution.py:18
  10.9 1.1 collective-permute-start.4
  12.3 10.4 %collective-permute-done.4 = bf16[32,128]{1,0:T(8,128)(2,1)S(1)} collective-permute-done((bf16[32,128]{1,0:T(8,128)(2,1)S(1)}, bf16[32,128]{1,0:T(8,128)(2,1)S(1)}, u32[]{:S(2)}, u32[]{:S(2)}) %collective-permute-start.4) | collective-permute-done | bytes 8224 | tf_op jit(solution)/shard_map/ppermute | solution.py:14
  23.7 1.1 pad_maximum_fusion
  27.3 2.0 %collective-permute-start.6 = (bf16[8,32,128]{2,0,1:T(8,128)(2,1)S(1)}, bf16[8,32,128]{2,0,1:T(8,128)(2,1)S(1)}, u32[]{:S(2)}, u32[]{:S(2)}) collective-permute-start(bf16[8,32,128]{2,0,1:T(8,128)(2,1)S(1)} %convolution_convert_fusion.12), channel_id=1, source_target_pairs={{0,4},{4,0},{8,12},{12,8},{16,20},{20,16},{24,28},{28,24},{1,5},{5... | collective-permute-start | bytes 196616 | tf_op jit(solution)/shard_map/ppermute | solution.py:18
  32.6 13.2 %all_to_all.20 = f32[32,1,128]{2,1,0:T(1,128)S(1)} all-to-all(f32[32,1,128]{2,1,0:T(1,128)S(1)} %reshape.270), channel_id=1, replica_groups=mesh['dom'=8,'rep'=4] {'dom','rep'}, dimensions={0} | all-to-all | bytes 32768 | tf_op jit(solution)/shard_map/all_to_all | solution.py:24
  48.5 2.6 %collective-permute-done.8 = bf16[32,128]{1,0:T(8,128)(2,1)S(1)} collective-permute-done((bf16[32,128]{1,0:T(8,128)(2,1)S(1)}, bf16[32,128]{1,0:T(8,128)(2,1)S(1)}, u32[]{:S(2)}, u32[]{:S(2)}) %collective-permute-start.8) | collective-permute-done | bytes 8224 | tf_op jit(solution)/shard_map/ppermute | solution.py:14
  52.6 1.9 %fusion.8 = f32[32,32,128]{2,1,0:T(8,128)S(1)} fusion(bf16[32,128,128]{2,1,0:T(8,128)(2,1)S(1)} %slice.124, bf16[32,32,128]{2,0,1:T(8,128)(2,1)} %fusion.2), kind=kOutput, calls=%fused_computation.19 | convolution fusion | flops 67239936 | bytes 1835008 | tf_op jit(solution)/shard_map/srj,skj->srk/dot_general | solution.py:54
  55.5 1.1 collective-permute-start.10
  58.8 1.0 collective-permute-done.10
  60.8 8.8 %all_to_all.21 = f32[32,1,128]{2,1,0:T(1,128)S(1)} all-to-all(f32[32,1,128]{2,1,0:T(1,128)S(1)} %reshape.272), channel_id=1, replica_groups=mesh['dom'=8,'rep'=4] {'dom','rep'}, dimensions={0} | all-to-all | bytes 32768 | tf_op jit(solution)/shard_map/all_to_all | solution.py:24
  70.5 1.0 fusion.199
  72.9 2.6 %collective-permute-done.12 = bf16[32,128]{1,0:T(8,128)(2,1)S(1)} collective-permute-done((bf16[32,128]{1,0:T(8,128)(2,1)S(1)}, bf16[32,128]{1,0:T(8,128)(2,1)S(1)}, u32[]{:S(2)}, u32[]{:S(2)}) %collective-permute-start.12) | collective-permute-done | bytes 8224 | tf_op jit(solution)/shard_map/ppermute | solution.py:14
  75.9 1.0 fusion.3
  76.8 1.9 %fusion.9 = f32[32,32,128]{2,1,0:T(8,128)S(1)} fusion(bf16[32,128,128]{2,1,0:T(8,128)(2,1)S(1)} %slice.124, bf16[32,32,128]{2,0,1:T(8,128)(2,1)} %fusion.3), kind=kOutput, calls=%fused_computation.20 | convolution fusion | flops 67239936 | bytes 1835008 | tf_op jit(solution)/shard_map/srj,skj->srk/dot_general | solution.py:54
  79.8 1.3 %collective-permute-start.14 = (bf16[8,32,128]{2,0,1:T(8,128)(2,1)S(1)}, bf16[8,32,128]{2,0,1:T(8,128)(2,1)S(1)}, u32[]{:S(2)}, u32[]{:S(2)}) collective-permute-start(bf16[8,32,128]{2,0,1:T(8,128)(2,1)S(1)} %convolution_convert_fusion.10), channel_id=1, source_target_pairs={{0,4},{4,0},{8,12},{12,8},{16,20},{20,16},{24,28},{28,24},{1,5},{5... | collective-permute-start | bytes 196616 | tf_op jit(solution)/shard_map/ppermute | solution.py:18
  85.0 8.8 %all_to_all.22 = f32[32,1,128]{2,1,0:T(1,128)S(1)} all-to-all(f32[32,1,128]{2,1,0:T(1,128)S(1)} %reshape.274), channel_id=1, replica_groups=mesh['dom'=8,'rep'=4] {'dom','rep'}, dimensions={0} | all-to-all | bytes 32768 | tf_op jit(solution)/shard_map/all_to_all | solution.py:24
  94.7 1.0 fusion.198
  97.7 2.2 %collective-permute-done.16 = bf16[32,128]{1,0:T(8,128)(2,1)S(1)} collective-permute-done((bf16[32,128]{1,0:T(8,128)(2,1)S(1)}, bf16[32,128]{1,0:T(8,128)(2,1)S(1)}, u32[]{:S(2)}, u32[]{:S(2)}) %collective-permute-start.16) | collective-permute-done | bytes 8224 | tf_op jit(solution)/shard_map/ppermute | solution.py:14
  100.1 1.0 fusion.4
  101.1 1.9 %fusion.10 = f32[32,32,128]{2,1,0:T(8,128)S(1)} fusion(bf16[32,128,128]{2,1,0:T(8,128)(2,1)S(1)} %slice.124, bf16[32,32,128]{2,0,1:T(8,128)(2,1)} %fusion.4), kind=kOutput, calls=%fused_computation.21 | convolution fusion | flops 67239936 | bytes 1835008 | tf_op jit(solution)/shard_map/srj,skj->srk/dot_general | solution.py:54
  104.0 1.5 %collective-permute-start.18 = (bf16[8,32,128]{2,0,1:T(8,128)(2,1)S(1)}, bf16[8,32,128]{2,0,1:T(8,128)(2,1)S(1)}, u32[]{:S(2)}, u32[]{:S(2)}) collective-permute-start(bf16[8,32,128]{2,0,1:T(8,128)(2,1)S(1)} %convolution_convert_fusion.9), channel_id=1, source_target_pairs={{0,4},{4,0},{8,12},{12,8},{16,20},{20,16},{24,28},{28,24},{1,5},{5... | collective-permute-start | bytes 196616 | tf_op jit(solution)/shard_map/ppermute | solution.py:18
  109.1 8.9 %all_to_all.23 = f32[32,2,32]{2,1,0:T(2,128)S(1)} all-to-all(f32[32,2,32]{2,1,0:T(2,128)S(1)} %broadcast_in_dim.89), channel_id=1, replica_groups=mesh['dom'=8,'rep'=4] {'dom','rep'}, dimensions={0} | all-to-all | bytes 16384 | tf_op jit(solution)/shard_map/all_to_all | solution.py:24
  (163 shorter events, 37.9 us)
Async XLA Ops:
  5.1 7.0 %copy-start.12 = (s32[8,2]{0,1:T(2,128)S(1)}, s32[8,2]{0,1:T(2,128)}, u32[]{:S(2)}) copy-start(s32[8,2]{0,1:T(2,128)} %param.16) | copy-start | bytes 196
  5.8 17.0 %copy-start.4 = (bf16[1,128,128]{2,1,0:T(8,128)(2,1)S(1)}, bf16[1,128,128]{2,1,0:T(8,128)(2,1)}, u32[]{:S(2)}) copy-start(bf16[1,128,128]{2,1,0:T(8,128)(2,1)} %param.17) | copy-start | bytes 98308
  5.8 17.1 %collective-permute-start.2 = (bf16[8,144,128]{2,1,0:T(8,128)(2,1)}, bf16[8,144,128]{2,1,0:T(8,128)(2,1)S(1)}, u32[]{:S(2)}, u32[]{:S(2)}) collective-permute-start(bf16[8,144,128]{2,1,0:T(8,128)(2,1)} %fusion.25), channel_id=1, source_target_pairs={{0,3},{1,0},{2,1},{3,2},{4,7},{5,4},{6,5},{7,6},{8,11},{9,8},{10,9... | collective-permute-start | bytes 884744 | tf_op jit(solution)/shard_map/ppermute | solution.py:14
  8.3 14.7 %collective-permute-start.1 = (bf16[8,144,128]{2,1,0:T(8,128)(2,1)S(1)}, bf16[8,144,128]{2,1,0:T(8,128)(2,1)S(1)}, u32[]{:S(2)}, u32[]{:S(2)}) collective-permute-start(bf16[8,144,128]{2,1,0:T(8,128)(2,1)S(1)} %fusion.26), channel_id=1, source_target_pairs={{0,2},{1,3},{2,0},{3,1},{4,6},{5,7},{6,4},{7,5},{8,10},{9,11},{10,... | collective-permute-start | bytes 884744 | tf_op jit(solution)/shard_map/ppermute | solution.py:14
  8.9 14.0 %collective-permute-start = (bf16[8,144,128]{2,1,0:T(8,128)(2,1)S(1)}, bf16[8,144,128]{2,1,0:T(8,128)(2,1)S(1)}, u32[]{:S(2)}, u32[]{:S(2)}) collective-permute-start(bf16[8,144,128]{2,1,0:T(8,128)(2,1)S(1)} %fusion.27), channel_id=1, source_target_pairs={{0,1},{1,2},{2,3},{3,0},{4,5},{5,6},{6,7},{7,4},{8,9},{9,10},{10,1... | collective-permute-start | bytes 884744 | tf_op jit(solution)/shard_map/ppermute | solution.py:14
  9.3 16.2 %collective-permute-start.3 = (bf16[8,32,128]{2,0,1:T(8,128)(2,1)S(1)}, bf16[8,32,128]{2,0,1:T(8,128)(2,1)S(1)}, u32[]{:S(2)}, u32[]{:S(2)}) collective-permute-start(bf16[8,32,128]{2,0,1:T(8,128)(2,1)S(1)} %multiply_convert_fusion), channel_id=1, source_target_pairs={{0,4},{4,0},{8,12},{12,8},{16,20},{20,16},{24,28},{28,24},{1,5},{5... | collective-permute-start | bytes 196616 | tf_op jit(solution)/shard_map/ppermute | solution.py:18
  10.9 11.9 %collective-permute-start.4 = (bf16[32,128]{1,0:T(8,128)(2,1)S(1)}, bf16[32,128]{1,0:T(8,128)(2,1)S(1)}, u32[]{:S(2)}, u32[]{:S(2)}) collective-permute-start(bf16[32,128]{1,0:T(8,128)(2,1)S(1)} %bitcast.290), channel_id=1, source_target_pairs={{0,1},{1,2},{2,3},{3,0},{4,5},{5,6},{6,7},{7,4},{8,9},{9,10},{10,1... | collective-permute-start | bytes 24584 | tf_op jit(solution)/shard_map/ppermute | solution.py:14
  27.3 4.3 %collective-permute-start.6 = (bf16[8,32,128]{2,0,1:T(8,128)(2,1)S(1)}, bf16[8,32,128]{2,0,1:T(8,128)(2,1)S(1)}, u32[]{:S(2)}, u32[]{:S(2)}) collective-permute-start(bf16[8,32,128]{2,0,1:T(8,128)(2,1)S(1)} %convolution_convert_fusion.12), channel_id=1, source_target_pairs={{0,4},{4,0},{8,12},{12,8},{16,20},{20,16},{24,28},{28,24},{1,5},{5... | collective-permute-start | bytes 196616 | tf_op jit(solution)/shard_map/ppermute | solution.py:18
  30.0 1.5 %collective-permute-start.5 = (f32[32,128]{1,0:T(8,128)S(1)}, f32[32,128]{1,0:T(8,128)S(1)}, u32[]{:S(2)}, u32[]{:S(2)}) collective-permute-start(f32[32,128]{1,0:T(8,128)S(1)} %fusion.97), channel_id=1, source_target_pairs={{0,3},{1,0},{2,1},{3,2},{4,7},{5,4},{6,5},{7,6},{8,11},{9,8},{10,9... | collective-permute-start | bytes 49160 | tf_op jit(solution)/shard_map/ppermute | solution.py:14
  47.3 12.5 %copy-start.8 = (f32[8,32,128]{2,0,1:T(8,128)}, f32[8,32,128]{2,0,1:T(8,128)S(1)}, u32[]{:S(2)}) copy-start(f32[8,32,128]{2,0,1:T(8,128)S(1)} %get-tuple-element.71) | copy-start | bytes 393220
  47.3 4.3 %collective-permute-start.7 = (bf16[8,32,128]{2,0,1:T(8,128)(2,1)S(1)}, bf16[8,32,128]{2,0,1:T(8,128)(2,1)S(1)}, u32[]{:S(2)}, u32[]{:S(2)}) collective-permute-start(bf16[8,32,128]{2,0,1:T(8,128)(2,1)S(1)} %get-tuple-element.18), channel_id=1, source_target_pairs={{0,4},{4,0},{8,12},{12,8},{16,20},{20,16},{24,28},{28,24},{1,5},{5... | collective-permute-start | bytes 196616 | tf_op jit(solution)/shard_map/ppermute | solution.py:18
  48.0 3.1 %collective-permute-start.8 = (bf16[32,128]{1,0:T(8,128)(2,1)S(1)}, bf16[32,128]{1,0:T(8,128)(2,1)S(1)}, u32[]{:S(2)}, u32[]{:S(2)}) collective-permute-start(bf16[32,128]{1,0:T(8,128)(2,1)S(1)} %bitcast.292), channel_id=1, source_target_pairs={{0,1},{1,2},{2,3},{3,0},{4,5},{5,6},{6,7},{7,4},{8,9},{9,10},{10,1... | collective-permute-start | bytes 24584 | tf_op jit(solution)/shard_map/ppermute | solution.py:14
  55.5 4.3 %collective-permute-start.10 = (bf16[8,32,128]{2,0,1:T(8,128)(2,1)S(1)}, bf16[8,32,128]{2,0,1:T(8,128)(2,1)S(1)}, u32[]{:S(2)}, u32[]{:S(2)}) collective-permute-start(bf16[8,32,128]{2,0,1:T(8,128)(2,1)S(1)} %convolution_convert_fusion.11), channel_id=1, source_target_pairs={{0,4},{4,0},{8,12},{12,8},{16,20},{20,16},{24,28},{28,24},{1,5},{5... | collective-permute-start | bytes 196616 | tf_op jit(solution)/shard_map/ppermute | solution.py:18
  57.3 1.5 %collective-permute-start.9 = (f32[32,128]{1,0:T(8,128)S(1)}, f32[32,128]{1,0:T(8,128)S(1)}, u32[]{:S(2)}, u32[]{:S(2)}) collective-permute-start(f32[32,128]{1,0:T(8,128)S(1)} %fusion.93), channel_id=1, source_target_pairs={{0,3},{1,0},{2,1},{3,2},{4,7},{5,4},{6,5},{7,6},{8,11},{9,8},{10,9... | collective-permute-start | bytes 49160 | tf_op jit(solution)/shard_map/ppermute | solution.py:14
  71.5 12.5 %copy-start.7 = (f32[8,32,128]{2,0,1:T(8,128)}, f32[8,32,128]{2,0,1:T(8,128)S(1)}, u32[]{:S(2)}) copy-start(f32[8,32,128]{2,0,1:T(8,128)S(1)} %get-tuple-element.66) | copy-start | bytes 393220
  71.6 4.3 %collective-permute-start.11 = (bf16[8,32,128]{2,0,1:T(8,128)(2,1)S(1)}, bf16[8,32,128]{2,0,1:T(8,128)(2,1)S(1)}, u32[]{:S(2)}, u32[]{:S(2)}) collective-permute-start(bf16[8,32,128]{2,0,1:T(8,128)(2,1)S(1)} %get-tuple-element.21), channel_id=1, source_target_pairs={{0,4},{4,0},{8,12},{12,8},{16,20},{20,16},{24,28},{28,24},{1,5},{5... | collective-permute-start | bytes 196616 | tf_op jit(solution)/shard_map/ppermute | solution.py:18
  72.2 3.3 %collective-permute-start.12 = (bf16[32,128]{1,0:T(8,128)(2,1)S(1)}, bf16[32,128]{1,0:T(8,128)(2,1)S(1)}, u32[]{:S(2)}, u32[]{:S(2)}) collective-permute-start(bf16[32,128]{1,0:T(8,128)(2,1)S(1)} %bitcast.293), channel_id=1, source_target_pairs={{0,1},{1,2},{2,3},{3,0},{4,5},{5,6},{6,7},{7,4},{8,9},{9,10},{10,1... | collective-permute-start | bytes 24584 | tf_op jit(solution)/shard_map/ppermute | solution.py:14
  79.8 4.3 %collective-permute-start.14 = (bf16[8,32,128]{2,0,1:T(8,128)(2,1)S(1)}, bf16[8,32,128]{2,0,1:T(8,128)(2,1)S(1)}, u32[]{:S(2)}, u32[]{:S(2)}) collective-permute-start(bf16[8,32,128]{2,0,1:T(8,128)(2,1)S(1)} %convolution_convert_fusion.10), channel_id=1, source_target_pairs={{0,4},{4,0},{8,12},{12,8},{16,20},{20,16},{24,28},{28,24},{1,5},{5... | collective-permute-start | bytes 196616 | tf_op jit(solution)/shard_map/ppermute | solution.py:18
  81.7 1.5 %collective-permute-start.13 = (f32[32,128]{1,0:T(8,128)S(1)}, f32[32,128]{1,0:T(8,128)S(1)}, u32[]{:S(2)}, u32[]{:S(2)}) collective-permute-start(f32[32,128]{1,0:T(8,128)S(1)} %fusion.89), channel_id=1, source_target_pairs={{0,3},{1,0},{2,1},{3,2},{4,7},{5,4},{6,5},{7,6},{8,11},{9,8},{10,9... | collective-permute-start | bytes 49160 | tf_op jit(solution)/shard_map/ppermute | solution.py:14
  95.8 4.3 %collective-permute-start.15 = (bf16[8,32,128]{2,0,1:T(8,128)(2,1)S(1)}, bf16[8,32,128]{2,0,1:T(8,128)(2,1)S(1)}, u32[]{:S(2)}, u32[]{:S(2)}) collective-permute-start(bf16[8,32,128]{2,0,1:T(8,128)(2,1)S(1)} %get-tuple-element.24), channel_id=1, source_target_pairs={{0,4},{4,0},{8,12},{12,8},{16,20},{20,16},{24,28},{28,24},{1,5},{5... | collective-permute-start | bytes 196616 | tf_op jit(solution)/shard_map/ppermute | solution.py:18
  96.8 3.1 %collective-permute-start.16 = (bf16[32,128]{1,0:T(8,128)(2,1)S(1)}, bf16[32,128]{1,0:T(8,128)(2,1)S(1)}, u32[]{:S(2)}, u32[]{:S(2)}) collective-permute-start(bf16[32,128]{1,0:T(8,128)(2,1)S(1)} %bitcast.291), channel_id=1, source_target_pairs={{0,1},{1,2},{2,3},{3,0},{4,5},{5,6},{6,7},{7,4},{8,9},{9,10},{10,1... | collective-permute-start | bytes 24584 | tf_op jit(solution)/shard_map/ppermute | solution.py:14
  104.0 4.3 %collective-permute-start.18 = (bf16[8,32,128]{2,0,1:T(8,128)(2,1)S(1)}, bf16[8,32,128]{2,0,1:T(8,128)(2,1)S(1)}, u32[]{:S(2)}, u32[]{:S(2)}) collective-permute-start(bf16[8,32,128]{2,0,1:T(8,128)(2,1)S(1)} %convolution_convert_fusion.9), channel_id=1, source_target_pairs={{0,4},{4,0},{8,12},{12,8},{16,20},{20,16},{24,28},{28,24},{1,5},{5... | collective-permute-start | bytes 196616 | tf_op jit(solution)/shard_map/ppermute | solution.py:18
  106.2 1.5 %collective-permute-start.17 = (f32[32,128]{1,0:T(8,128)S(1)}, f32[32,128]{1,0:T(8,128)S(1)}, u32[]{:S(2)}, u32[]{:S(2)}) collective-permute-start(f32[32,128]{1,0:T(8,128)S(1)} %fusion.85), channel_id=1, source_target_pairs={{0,3},{1,0},{2,1},{3,2},{4,7},{5,4},{6,5},{7,6},{8,11},{9,8},{10,9... | collective-permute-start | bytes 49160 | tf_op jit(solution)/shard_map/ppermute | solution.py:14
  106.5 11.6 %copy-start.6 = (f32[8,32,128]{2,0,1:T(8,128)S(1)}, f32[8,32,128]{2,0,1:T(8,128)}, u32[]{:S(2)}) copy-start(f32[8,32,128]{2,0,1:T(8,128)} %copy-done.5) | copy-start | bytes 393220
  (8 other events, 26.9 us)

commit v14 on v12

--- a/solution.py
+++ b/solution.py
@@ -39,12 +39,11 @@
     return result + jnp.einsum("pn,prj->nrj", mirror_onehot, mirror, precision=lax.Precision.HIGHEST)
 
 
-def apply_operator(vector, diag_tiles, off_tiles, link_tile, contact_set, tables):
+def apply_operator(vector, other, diag_tiles, off_tiles, link_tile, contact_set, tables):
     cols_onehot, mirror_onehot, near_onehot, far_onehot, near_collect, far_collect = tables
     nodes = vector.shape[0]
     rounded = vector.astype(jnp.bfloat16)
     before = from_behind(rounded[nodes - 1], "rep", 1)
-    other = partner(rounded, "dom", 0).astype(vector.dtype)
     near = jnp.einsum("sn,nrk->srk", near_onehot, vector, precision=lax.Precision.HIGHEST)
     far = jnp.einsum("sn,nrk->srk", far_onehot, other, precision=lax.Precision.HIGHEST)
     difference = (near - far).astype(jnp.bfloat16)
@@ -129,13 +128,19 @@
     residual = rhs
     preconditioned = scale * residual
     direction = preconditioned
+    mate_scale = partner(precond, "dom", 0)[:, None, :]
+    mate_residual = partner(rhs, "dom", 0)
+    mate_direction = mate_scale * mate_residual
     for step in range(ITERS):
-        image = apply_operator(direction, diag_tiles, off_tiles, link_tile, contact_set, tables)
+        image = apply_operator(
+            direction, mate_direction, diag_tiles, off_tiles, link_tile, contact_set, tables
+        )
         parts = [
             jnp.sum(direction * image, axis=(0, 2)),
             jnp.sum(residual * preconditioned, axis=(0, 2)),
         ]
         if step < ITERS - 1:
+            mate_image = partner(image, "dom", 0)
             parts.append(jnp.sum(preconditioned * image, axis=(0, 2)))
             parts.append(jnp.sum(image * (scale * image), axis=(0, 2)))
         sums = total(jnp.stack(parts))
@@ -144,9 +149,12 @@
         solution = solution + alpha[None, :, None] * direction
         residual = residual - alpha[None, :, None] * image
         if step < ITERS - 1:
+            next_dot = res_dot - 2.0 * alpha * sums[2] + alpha * alpha * sums[3]
+            beta = (next_dot / res_dot)[None, :, None]
             preconditioned = scale * residual
-            next_dot = res_dot - 2.0 * alpha * sums[2] + alpha * alpha * sums[3]
-            direction = preconditioned + (next_dot / res_dot)[None, :, None] * direction
+            direction = preconditioned + beta * direction
+            mate_residual = mate_residual - alpha[None, :, None] * mate_image
+            mate_direction = mate_scale * mate_residual + beta * mate_direction
     return (solution, residual)
 
 

time: 116 us -> 125 us (1.078)
  blocking collectives: 39.4 us -> 8.95 us
  starting transfers between devices: 15.4 us -> 31.9 us
  waiting for transfers between devices: 24.6 us -> 39.2 us
  other arithmetic: 6.67 us -> 10.6 us
  matrix products: 24.4 us -> 26.9 us
  local copies, waits for them, and re-layouts: 3.38 us -> 5.54 us
    all_to_all x4 -> x1, blocking collectives: 39.4 us -> 8.95 us  [total(): gathered = lax.all_to_all(spread, ('dom', 'rep'), 0, 0, tiled=True)]
    all_to_all x0 -> x3, waiting for transfers between devices: none -> 15.8 us  [total(): gathered = lax.all_to_all(spread, ('dom', 'rep'), 0, 0, tiled=True)]
    all_to_all x0 -> x3, starting transfers between devices: none -> 12.9 us  [total(): gathered = lax.all_to_all(spread, ('dom', 'rep'), 0, 0, tiled=True)]
    convert_element_type x4, other arithmetic: 0.51 us -> 3.69 us  [apply_operator(): rounded = vector.astype(jnp.bfloat16)]
    ppermute x14, waiting for transfers between devices: 20.9 us -> 18 us  [from_behind(): return lax.ppermute(value, axis, pairs)]
    ppermute x8 -> x9, starting transfers between devices: 8.92 us -> 11.7 us  [partner(): lax.ppermute(value, axis, [(i, i ^ 1 << distance) for i in range(lax.axis...]
    unnamed x37 -> x63, local copies, waits for them, and re-layouts: 2.13 us -> 4.28 us
    ppermute x8 -> x9, waiting for transfers between devices: 3.69 us -> 5.39 us  [partner(): lax.ppermute(value, axis, [(i, i ^ 1 << distance) for i in range(lax.axis...]
  transfers between devices with their start and end apart: 22 -> 26, of which waited for: 16 -> 14; matrix products, arithmetic and copies ran while one was open for 8% -> 10% of each run, Pallas kernels for 0% -> 0%
where the time goes in v14:
time: 125 us; the launch traced here: 124 us
  waiting for transfers between devices  39.2 us (31%)
  starting transfers between devices  31.9 us (26%)
  matrix products  26.9 us (22%)
  other arithmetic  10.6 us (8%)
  blocking collectives  8.95 us (7%)
  local copies, waits for them, and re-layouts  5.54 us (4%)
  between operations  1.39 us (1%)
    ppermute x14, waiting for transfers between devices, from_behind(): return lax.ppermute(value, axis, pairs)  18 us
    all_to_all x3, waiting for transfers between devices, total(): gathered = lax.all_to_all(spread, ('dom', 'rep'), 0, 0, tiled=True)  15.8 us
    all_to_all x3, starting transfers between devices, total(): gathered = lax.all_to_all(spread, ('dom', 'rep'), 0, 0, tiled=True)  12.9 us
    ppermute x9, starting transfers between devices, partner(): lax.ppermute(value, axis, [(i, i ^ 1 << distance) for i in range(lax.axis...  11.7 us
    all_to_all x1, blocking collectives, total(): gathered = lax.all_to_all(spread, ('dom', 'rep'), 0, 0, tiled=True)  8.95 us
    ppermute x14, starting transfers between devices, from_behind(): return lax.ppermute(value, axis, pairs)  7.18 us
    dot_general x4, matrix products, apply_operator(): jnp.einsum('srj,skj->srk', multiplier, contact_set, preferred_element_typ...  6.53 us
    ppermute x9, waiting for transfers between devices, partner(): lax.ppermute(value, axis, [(i, i ^ 1 << distance) for i in range(lax.axis...  5.39 us
  transfers between devices with their start and end apart: 26, of which 14 were waited for; matrix products, arithmetic and copies ran while one was open for 10% of the time, Pallas kernels for 0%

profile of v14, /device:TPU:0, one launch (start us, length us, event | category | flops | bytes accessed | tf_op | source)
XLA Modules:
  0.0 124.4 jit_solution(12804848264141867746)
XLA Ops:
  3.7 2.4 %collective-permute-start.7 = (bf16[8,128,128]{2,0,1:T(8,128)(2,1)S(1)}, bf16[8,128,128]{2,0,1:T(8,128)(2,1)}, u32[]{:S(2)}, u32[]{:S(2)}) collective-permute-start(bf16[8,128,128]{2,0,1:T(8,128)(2,1)S(1)} %select_bitcast_fusion), channel_id=1, source_target_pairs={{0,3},{1,0},{2,1},{3,2},{4,7},{5,4},{6,5},{7,6},{8,11},{9,8},{10,9... | collective-permute-start | bytes 786440 | tf_op jit(solution)/shard_map/ppermute | solution.py:14
  7.3 1.7 %collective-permute-start.1 = (s32[8,2]{0,1:T(2,128)S(1)}, s32[8,2]{0,1:T(2,128)S(1)}, u32[]{:S(2)}, u32[]{:S(2)}) collective-permute-start(s32[8,2]{0,1:T(2,128)S(1)} %bitcast.326), channel_id=1, source_target_pairs={{0,2},{1,3},{2,0},{3,1},{4,6},{5,7},{6,4},{7,5},{8,10},{9,11},{10,... | collective-permute-start | bytes 200 | tf_op jit(solution)/shard_map/ppermute | solution.py:14
  11.0 4.7 %collective-permute-done.2 = s32[8,2]{0,1:T(2,128)S(1)} collective-permute-done((s32[8,2]{0,1:T(2,128)S(1)}, s32[8,2]{0,1:T(2,128)S(1)}, u32[]{:S(2)}, u32[]{:S(2)}) %collective-permute-start.2) | collective-permute-done | bytes 96 | tf_op jit(solution)/shard_map/ppermute | solution.py:14
  16.8 2.3 %collective-permute-done = s32[8,2]{0,1:T(2,128)S(1)} collective-permute-done((s32[8,2]{0,1:T(2,128)S(1)}, s32[8,2]{0,1:T(2,128)S(1)}, u32[]{:S(2)}, u32[]{:S(2)}) %collective-permute-start) | collective-permute-done | bytes 96 | tf_op jit(solution)/shard_map/ppermute | solution.py:14
  19.6 3.0 %collective-permute-done.8 = bf16[32,128]{1,0:T(8,128)(2,1)S(1)} collective-permute-done((bf16[32,128]{1,0:T(8,128)(2,1)S(1)}, bf16[32,128]{1,0:T(8,128)(2,1)S(1)}, u32[]{:S(2)}, u32[]{:S(2)}) %collective-permute-start.8) | collective-permute-done | bytes 8224 | tf_op jit(solution)/shard_map/ppermute | solution.py:14
  24.3 3.3 %collective-permute-done.4 = f32[8,32,128]{2,0,1:T(8,128)S(1)} collective-permute-done((f32[8,32,128]{2,0,1:T(8,128)S(1)}, f32[8,32,128]{2,0,1:T(8,128)S(1)}, u32[]{:S(2)}, u32[]{:S(2)}) %collective-permute-start.4) | collective-permute-done | bytes 131104 | tf_op jit(solution)/shard_map/ppermute | solution.py:18
  36.9 5.8 %all-to-all-start = ((f32[32,1,128]{2,1,0:T(1,128)}), f32[32,1,128]{2,1,0:T(1,128)S(1)}, u32[]{:S(2)}, u32[]{:S(2)}) async-start(f32[32,1,128]{2,1,0:T(1,128)} %reshape.372), calls=%async_computation | async-start | bytes 32768 | tf_op jit(solution)/shard_map/all_to_all | solution.py:24
  42.7 1.8 %collective-permute-start.11 = (f32[8,32,128]{2,0,1:T(8,128)S(1)}, f32[8,32,128]{2,0,1:T(8,128)S(1)}, u32[]{:S(2)}, u32[]{:S(2)}) collective-permute-start(f32[8,32,128]{2,0,1:T(8,128)S(1)} %get-tuple-element.99), channel_id=1, source_target_pairs={{0,4},{4,0},{8,12},{12,8},{16,20},{20,16},{24,28},{28,24},{1,5},{5... | collective-permute-start | bytes 393224 | tf_op jit(solution)/shard_map/ppermute | solution.py:18
  44.5 5.2 %all-to-all-done = f32[32,1,128]{2,1,0:T(1,128)S(1)} async-done(((f32[32,1,128]{2,1,0:T(1,128)}), f32[32,1,128]{2,1,0:T(1,128)S(1)}, u32[]{:S(2)}, u32[]{:S(2)}) %all-to-all-start) | async-done | bytes 16416 | tf_op jit(solution)/shard_map/all_to_all | solution.py:24
  53.4 1.9 %fusion.6 = f32[32,32,128]{2,1,0:T(8,128)S(1)} fusion(bf16[32,128,128]{2,1,0:T(8,128)(2,1)S(1)} %bitcast.280, bf16[32,32,128]{2,0,1:T(8,128)(2,1)} %fusion.2), kind=kOutput, calls=%fused_computation.15 | convolution fusion | flops 67239936 | bytes 1835008 | tf_op jit(solution)/shard_map/srj,skj->srk/dot_general | solution.py:53
  58.7 2.1 %collective-permute-done.12 = bf16[32,128]{1,0:T(8,128)(2,1)S(1)} collective-permute-done((bf16[32,128]{1,0:T(8,128)(2,1)S(1)}, bf16[32,128]{1,0:T(8,128)(2,1)S(1)}, u32[]{:S(2)}, u32[]{:S(2)}) %collective-permute-start.12) | collective-permute-done | bytes 8224 | tf_op jit(solution)/shard_map/ppermute | solution.py:14
  63.0 3.3 %all-to-all-start.1 = ((f32[32,1,128]{2,1,0:T(1,128)}), f32[32,1,128]{2,1,0:T(1,128)S(1)}, u32[]{:S(2)}, u32[]{:S(2)}) async-start(f32[32,1,128]{2,1,0:T(1,128)} %reshape.374), calls=%async_computation.1 | async-start | bytes 32768 | tf_op jit(solution)/shard_map/all_to_all | solution.py:24
  66.3 1.7 %collective-permute-start.15 = (f32[8,32,128]{2,0,1:T(8,128)}, f32[8,32,128]{2,0,1:T(8,128)S(1)}, u32[]{:S(2)}, u32[]{:S(2)}) collective-permute-start(f32[8,32,128]{2,0,1:T(8,128)} %get-tuple-element.100), channel_id=1, source_target_pairs={{0,4},{4,0},{8,12},{12,8},{16,20},{20,16},{24,28},{28,24},{1,5},{5... | collective-permute-start | bytes 393224 | tf_op jit(solution)/shard_map/ppermute | solution.py:18
  68.0 5.3 %all-to-all-done.1 = f32[32,1,128]{2,1,0:T(1,128)S(1)} async-done(((f32[32,1,128]{2,1,0:T(1,128)}), f32[32,1,128]{2,1,0:T(1,128)S(1)}, u32[]{:S(2)}, u32[]{:S(2)}) %all-to-all-start.1) | async-done | bytes 16416 | tf_op jit(solution)/shard_map/all_to_all | solution.py:24
  74.1 1.8 %fusion.202 = (bf16[8,32,128]{2,0,1:T(8,128)(2,1)S(1)}, f32[8,32,128]{2,0,1:T(8,128)S(1)}, f32[8,32,128]{2,0,1:T(8,128)}, f32[8,32,128]{2,0,1:T(8,128)S(1)}) fusion(f32[8,32,128]{2,0,1:T(8,128)S(1)} %get-tuple-element.80, f32[32]{0:T(128)S(1)} %get-tuple-element.77, f32[8,128]{1,0:T(8,128)S(1)} %copy-done.16, f32[8,32,128]{2,0,1:T(8,128)S(1)} %copy-done.13, ...), kind=kLoop, calls=%fused_computation.262 | loop fusion | flops 327680 | bytes 1249664 | tf_op jit(solution)/shard_map/convert_element_type | solution.py:45
  77.6 1.9 %fusion.7 = f32[32,32,128]{2,1,0:T(8,128)S(1)} fusion(bf16[32,128,128]{2,1,0:T(8,128)(2,1)S(1)} %bitcast.281, bf16[32,32,128]{2,0,1:T(8,128)(2,1)} %fusion.3), kind=kOutput, calls=%fused_computation.16 | convolution fusion | flops 67239936 | bytes 1835008 | tf_op jit(solution)/shard_map/srj,skj->srk/dot_general | solution.py:53
  82.9 2.1 %collective-permute-done.16 = bf16[32,128]{1,0:T(8,128)(2,1)S(1)} collective-permute-done((bf16[32,128]{1,0:T(8,128)(2,1)S(1)}, bf16[32,128]{1,0:T(8,128)(2,1)S(1)}, u32[]{:S(2)}, u32[]{:S(2)}) %collective-permute-start.16) | collective-permute-done | bytes 8224 | tf_op jit(solution)/shard_map/ppermute | solution.py:14
  87.2 3.8 %all-to-all-start.2 = ((f32[32,1,128]{2,1,0:T(1,128)}), f32[32,1,128]{2,1,0:T(1,128)S(1)}, u32[]{:S(2)}, u32[]{:S(2)}) async-start(f32[32,1,128]{2,1,0:T(1,128)} %reshape.376), calls=%async_computation.2 | async-start | bytes 32768 | tf_op jit(solution)/shard_map/all_to_all | solution.py:24
  91.0 1.8 %collective-permute-start.19 = (f32[8,32,128]{2,0,1:T(8,128)}, f32[8,32,128]{2,0,1:T(8,128)}, u32[]{:S(2)}, u32[]{:S(2)}) collective-permute-start(f32[8,32,128]{2,0,1:T(8,128)} %get-tuple-element.101), channel_id=1, source_target_pairs={{0,4},{4,0},{8,12},{12,8},{16,20},{20,16},{24,28},{28,24},{1,5},{5... | collective-permute-start | bytes 393224 | tf_op jit(solution)/shard_map/ppermute | solution.py:18
  92.8 5.2 %all-to-all-done.2 = f32[32,1,128]{2,1,0:T(1,128)S(1)} async-done(((f32[32,1,128]{2,1,0:T(1,128)}), f32[32,1,128]{2,1,0:T(1,128)S(1)}, u32[]{:S(2)}, u32[]{:S(2)}) %all-to-all-start.2) | async-done | bytes 16416 | tf_op jit(solution)/shard_map/all_to_all | solution.py:24
  101.2 2.2 %collective-permute-done.20 = bf16[32,128]{1,0:T(8,128)(2,1)S(1)} collective-permute-done((bf16[32,128]{1,0:T(8,128)(2,1)S(1)}, bf16[32,128]{1,0:T(8,128)(2,1)S(1)}, u32[]{:S(2)}, u32[]{:S(2)}) %collective-permute-start.20) | collective-permute-done | bytes 8224 | tf_op jit(solution)/shard_map/ppermute | solution.py:14
  103.6 2.1 %fusion.4 = bf16[32,32,128]{2,0,1:T(8,128)(2,1)} fusion(f32[32,32,128]{2,0,1:T(8,128)S(1)} %fusion.151, f32[8,32,128]{2,0,1:T(8,128)} %copy-done.10, f32[8,32,128]{2,0,1:T(8,128)} %collective-permute-done.19, f32[8,32,128]{2,0,1:T(8,128)S(1)} %get-tuple-element.93, f32[32]{0:T(128)S(1)} %get-tuple-element.72, f32[32]{0:T(128)S(1)} %get-tuple-element.73, ...), kind=kOutput, calls=%fused_computation.9 | convolution fusion | flops 13107456 | bytes 1184256 | tf_op jit(solution)/shard_map/sn,nrk->srk/dot_general | solution.py:48
  105.8 1.9 %fusion.8 = f32[32,32,128]{2,1,0:T(8,128)S(1)} fusion(bf16[32,128,128]{2,1,0:T(8,128)(2,1)S(1)} %bitcast.282, bf16[32,32,128]{2,0,1:T(8,128)(2,1)} %fusion.4), kind=kOutput, calls=%fused_computation.17 | convolution fusion | flops 67239936 | bytes 1835008 | tf_op jit(solution)/shard_map/srj,skj->srk/dot_general | solution.py:53
  113.8 8.9 %all_to_all.20 = f32[32,2,32]{2,1,0:T(2,128)S(1)} all-to-all(f32[32,2,32]{2,1,0:T(2,128)S(1)} %broadcast_in_dim.119), channel_id=1, replica_groups=mesh['dom'=8,'rep'=4] {'dom','rep'}, dimensions={0} | all-to-all | bytes 16384 | tf_op jit(solution)/shard_map/all_to_all | solution.py:24
  (195 shorter events, 46.5 us)
Async XLA Ops:
  3.7 24.4 %collective-permute-start.7 = (bf16[8,128,128]{2,0,1:T(8,128)(2,1)S(1)}, bf16[8,128,128]{2,0,1:T(8,128)(2,1)}, u32[]{:S(2)}, u32[]{:S(2)}) collective-permute-start(bf16[8,128,128]{2,0,1:T(8,128)(2,1)S(1)} %select_bitcast_fusion), channel_id=1, source_target_pairs={{0,3},{1,0},{2,1},{3,2},{4,7},{5,4},{6,5},{7,6},{8,11},{9,8},{10,9... | collective-permute-start | bytes 786440 | tf_op jit(solution)/shard_map/ppermute | solution.py:14
  6.2 21.8 %collective-permute-start.6 = (bf16[8,128,128]{2,0,1:T(8,128)(2,1)S(1)}, bf16[8,128,128]{2,0,1:T(8,128)(2,1)S(1)}, u32[]{:S(2)}, u32[]{:S(2)}) collective-permute-start(bf16[8,128,128]{2,0,1:T(8,128)(2,1)S(1)} %get-tuple-element.86), channel_id=1, source_target_pairs={{0,2},{1,3},{2,0},{3,1},{4,6},{5,7},{6,4},{7,5},{8,10},{9,11},{10,... | collective-permute-start | bytes 786440 | tf_op jit(solution)/shard_map/ppermute | solution.py:14
  7.2 8.4 %collective-permute-start.2 = (s32[8,2]{0,1:T(2,128)S(1)}, s32[8,2]{0,1:T(2,128)S(1)}, u32[]{:S(2)}, u32[]{:S(2)}) collective-permute-start(s32[8,2]{0,1:T(2,128)S(1)} %bitcast.327), channel_id=1, source_target_pairs={{0,3},{1,0},{2,1},{3,2},{4,7},{5,4},{6,5},{7,6},{8,11},{9,8},{10,9... | collective-permute-start | bytes 200 | tf_op jit(solution)/shard_map/ppermute | solution.py:14
  7.3 9.5 %collective-permute-start.1 = (s32[8,2]{0,1:T(2,128)S(1)}, s32[8,2]{0,1:T(2,128)S(1)}, u32[]{:S(2)}, u32[]{:S(2)}) collective-permute-start(s32[8,2]{0,1:T(2,128)S(1)} %bitcast.326), channel_id=1, source_target_pairs={{0,2},{1,3},{2,0},{3,1},{4,6},{5,7},{6,4},{7,5},{8,10},{9,11},{10,... | collective-permute-start | bytes 200 | tf_op jit(solution)/shard_map/ppermute | solution.py:14
  9.1 15.2 %collective-permute-start.3 = (f32[8,128]{1,0:T(8,128)S(1)}, f32[8,128]{1,0:T(8,128)S(1)}, u32[]{:S(2)}, u32[]{:S(2)}) collective-permute-start(f32[8,128]{1,0:T(8,128)S(1)} %copy-done.16), channel_id=1, source_target_pairs={{0,4},{4,0},{8,12},{12,8},{16,20},{20,16},{24,28},{28,24},{1,5},{5... | collective-permute-start | bytes 12296 | tf_op jit(solution)/shard_map/ppermute | solution.py:18
  15.7 3.4 %collective-permute-start = (s32[8,2]{0,1:T(2,128)S(1)}, s32[8,2]{0,1:T(2,128)S(1)}, u32[]{:S(2)}, u32[]{:S(2)}) collective-permute-start(s32[8,2]{0,1:T(2,128)S(1)} %bitcast.325), channel_id=1, source_target_pairs={{0,1},{1,2},{2,3},{3,0},{4,5},{5,6},{6,7},{7,4},{8,9},{9,10},{10,1... | collective-permute-start | bytes 200 | tf_op jit(solution)/shard_map/ppermute | solution.py:14
  16.8 11.3 %collective-permute-start.5 = (bf16[8,128,128]{2,0,1:T(8,128)(2,1)S(1)}, bf16[8,128,128]{2,0,1:T(8,128)(2,1)S(1)}, u32[]{:S(2)}, u32[]{:S(2)}) collective-permute-start(bf16[8,128,128]{2,0,1:T(8,128)(2,1)S(1)} %get-tuple-element.85), channel_id=1, source_target_pairs={{0,1},{1,2},{2,3},{3,0},{4,5},{5,6},{6,7},{7,4},{8,9},{9,10},{10,1... | collective-permute-start | bytes 786440 | tf_op jit(solution)/shard_map/ppermute | solution.py:14
  19.1 3.6 %collective-permute-start.8 = (bf16[32,128]{1,0:T(8,128)(2,1)S(1)}, bf16[32,128]{1,0:T(8,128)(2,1)S(1)}, u32[]{:S(2)}, u32[]{:S(2)}) collective-permute-start(bf16[32,128]{1,0:T(8,128)(2,1)S(1)} %bitcast.305), channel_id=1, source_target_pairs={{0,1},{1,2},{2,3},{3,0},{4,5},{5,6},{6,7},{7,4},{8,9},{9,10},{10,1... | collective-permute-start | bytes 24584 | tf_op jit(solution)/shard_map/ppermute | solution.py:14
  22.7 5.0 %collective-permute-start.4 = (f32[8,32,128]{2,0,1:T(8,128)S(1)}, f32[8,32,128]{2,0,1:T(8,128)S(1)}, u32[]{:S(2)}, u32[]{:S(2)}) collective-permute-start(f32[8,32,128]{2,0,1:T(8,128)S(1)} %get-tuple-element.88), channel_id=1, source_target_pairs={{0,4},{4,0},{8,12},{12,8},{16,20},{20,16},{24,28},{28,24},{1,5},{5... | collective-permute-start | bytes 393224 | tf_op jit(solution)/shard_map/ppermute | solution.py:18
  31.0 4.3 %collective-permute-start.10 = (bf16[8,32,128]{2,0,1:T(8,128)(2,1)S(1)}, bf16[8,32,128]{2,0,1:T(8,128)(2,1)S(1)}, u32[]{:S(2)}, u32[]{:S(2)}) collective-permute-start(bf16[8,32,128]{2,0,1:T(8,128)(2,1)S(1)} %convolution_convert_fusion.12), channel_id=1, source_target_pairs={{0,4},{4,0},{8,12},{12,8},{16,20},{20,16},{24,28},{28,24},{1,5},{5... | collective-permute-start | bytes 196616 | tf_op jit(solution)/shard_map/ppermute | solution.py:18
  36.9 12.9 %all-to-all-start = ((f32[32,1,128]{2,1,0:T(1,128)}), f32[32,1,128]{2,1,0:T(1,128)S(1)}, u32[]{:S(2)}, u32[]{:S(2)}) async-start(f32[32,1,128]{2,1,0:T(1,128)} %reshape.372), calls=%async_computation | async-start | bytes 32768 | tf_op jit(solution)/shard_map/all_to_all | solution.py:24
  42.7 8.4 %collective-permute-start.11 = (f32[8,32,128]{2,0,1:T(8,128)S(1)}, f32[8,32,128]{2,0,1:T(8,128)S(1)}, u32[]{:S(2)}, u32[]{:S(2)}) collective-permute-start(f32[8,32,128]{2,0,1:T(8,128)S(1)} %get-tuple-element.99), channel_id=1, source_target_pairs={{0,4},{4,0},{8,12},{12,8},{16,20},{20,16},{24,28},{28,24},{1,5},{5... | collective-permute-start | bytes 393224 | tf_op jit(solution)/shard_map/ppermute | solution.py:18
  56.3 4.6 %collective-permute-start.14 = (bf16[8,32,128]{2,0,1:T(8,128)(2,1)S(1)}, bf16[8,32,128]{2,0,1:T(8,128)(2,1)S(1)}, u32[]{:S(2)}, u32[]{:S(2)}) collective-permute-start(bf16[8,32,128]{2,0,1:T(8,128)(2,1)S(1)} %convolution_convert_fusion.11), channel_id=1, source_target_pairs={{0,4},{4,0},{8,12},{12,8},{16,20},{20,16},{24,28},{28,24},{1,5},{5... | collective-permute-start | bytes 196616 | tf_op jit(solution)/shard_map/ppermute | solution.py:18
  57.6 3.3 %collective-permute-start.13 = (f32[32,128]{1,0:T(8,128)S(1)}, f32[32,128]{1,0:T(8,128)S(1)}, u32[]{:S(2)}, u32[]{:S(2)}) collective-permute-start(f32[32,128]{1,0:T(8,128)S(1)} %fusion.101), channel_id=1, source_target_pairs={{0,3},{1,0},{2,1},{3,2},{4,7},{5,4},{6,5},{7,6},{8,11},{9,8},{10,9... | collective-permute-start | bytes 49160 | tf_op jit(solution)/shard_map/ppermute | solution.py:14
  57.7 3.1 %collective-permute-start.12 = (bf16[32,128]{1,0:T(8,128)(2,1)S(1)}, bf16[32,128]{1,0:T(8,128)(2,1)S(1)}, u32[]{:S(2)}, u32[]{:S(2)}) collective-permute-start(bf16[32,128]{1,0:T(8,128)(2,1)S(1)} %bitcast.306), channel_id=1, source_target_pairs={{0,1},{1,2},{2,3},{3,0},{4,5},{5,6},{6,7},{7,4},{8,9},{9,10},{10,1... | collective-permute-start | bytes 24584 | tf_op jit(solution)/shard_map/ppermute | solution.py:14
  63.0 10.3 %all-to-all-start.1 = ((f32[32,1,128]{2,1,0:T(1,128)}), f32[32,1,128]{2,1,0:T(1,128)S(1)}, u32[]{:S(2)}, u32[]{:S(2)}) async-start(f32[32,1,128]{2,1,0:T(1,128)} %reshape.374), calls=%async_computation.1 | async-start | bytes 32768 | tf_op jit(solution)/shard_map/all_to_all | solution.py:24
  66.3 7.7 %collective-permute-start.15 = (f32[8,32,128]{2,0,1:T(8,128)}, f32[8,32,128]{2,0,1:T(8,128)S(1)}, u32[]{:S(2)}, u32[]{:S(2)}) collective-permute-start(f32[8,32,128]{2,0,1:T(8,128)} %get-tuple-element.100), channel_id=1, source_target_pairs={{0,4},{4,0},{8,12},{12,8},{16,20},{20,16},{24,28},{28,24},{1,5},{5... | collective-permute-start | bytes 393224 | tf_op jit(solution)/shard_map/ppermute | solution.py:18
  80.6 4.6 %collective-permute-start.18 = (bf16[8,32,128]{2,0,1:T(8,128)(2,1)S(1)}, bf16[8,32,128]{2,0,1:T(8,128)(2,1)S(1)}, u32[]{:S(2)}, u32[]{:S(2)}) collective-permute-start(bf16[8,32,128]{2,0,1:T(8,128)(2,1)S(1)} %convolution_convert_fusion.10), channel_id=1, source_target_pairs={{0,4},{4,0},{8,12},{12,8},{16,20},{20,16},{24,28},{28,24},{1,5},{5... | collective-permute-start | bytes 196616 | tf_op jit(solution)/shard_map/ppermute | solution.py:18
  81.9 3.3 %collective-permute-start.17 = (f32[32,128]{1,0:T(8,128)S(1)}, f32[32,128]{1,0:T(8,128)S(1)}, u32[]{:S(2)}, u32[]{:S(2)}) collective-permute-start(f32[32,128]{1,0:T(8,128)S(1)} %fusion.97), channel_id=1, source_target_pairs={{0,3},{1,0},{2,1},{3,2},{4,7},{5,4},{6,5},{7,6},{8,11},{9,8},{10,9... | collective-permute-start | bytes 49160 | tf_op jit(solution)/shard_map/ppermute | solution.py:14
  81.9 3.1 %collective-permute-start.16 = (bf16[32,128]{1,0:T(8,128)(2,1)S(1)}, bf16[32,128]{1,0:T(8,128)(2,1)S(1)}, u32[]{:S(2)}, u32[]{:S(2)}) collective-permute-start(bf16[32,128]{1,0:T(8,128)(2,1)S(1)} %bitcast.307), channel_id=1, source_target_pairs={{0,1},{1,2},{2,3},{3,0},{4,5},{5,6},{6,7},{7,4},{8,9},{9,10},{10,1... | collective-permute-start | bytes 24584 | tf_op jit(solution)/shard_map/ppermute | solution.py:14
  87.2 10.9 %all-to-all-start.2 = ((f32[32,1,128]{2,1,0:T(1,128)}), f32[32,1,128]{2,1,0:T(1,128)S(1)}, u32[]{:S(2)}, u32[]{:S(2)}) async-start(f32[32,1,128]{2,1,0:T(1,128)} %reshape.376), calls=%async_computation.2 | async-start | bytes 32768 | tf_op jit(solution)/shard_map/all_to_all | solution.py:24
  91.0 12.6 %collective-permute-start.19 = (f32[8,32,128]{2,0,1:T(8,128)}, f32[8,32,128]{2,0,1:T(8,128)}, u32[]{:S(2)}, u32[]{:S(2)}) collective-permute-start(f32[8,32,128]{2,0,1:T(8,128)} %get-tuple-element.101), channel_id=1, source_target_pairs={{0,4},{4,0},{8,12},{12,8},{16,20},{20,16},{24,28},{28,24},{1,5},{5... | collective-permute-start | bytes 393224 | tf_op jit(solution)/shard_map/ppermute | solution.py:18
  100.3 3.1 %collective-permute-start.20 = (bf16[32,128]{1,0:T(8,128)(2,1)S(1)}, bf16[32,128]{1,0:T(8,128)(2,1)S(1)}, u32[]{:S(2)}, u32[]{:S(2)}) collective-permute-start(bf16[32,128]{1,0:T(8,128)(2,1)S(1)} %bitcast.308), channel_id=1, source_target_pairs={{0,1},{1,2},{2,3},{3,0},{4,5},{5,6},{6,7},{7,4},{8,9},{9,10},{10,1... | collective-permute-start | bytes 24584 | tf_op jit(solution)/shard_map/ppermute | solution.py:14
  108.7 4.3 %collective-permute-start.22 = (bf16[8,32,128]{2,0,1:T(8,128)(2,1)S(1)}, bf16[8,32,128]{2,0,1:T(8,128)(2,1)S(1)}, u32[]{:S(2)}, u32[]{:S(2)}) collective-permute-start(bf16[8,32,128]{2,0,1:T(8,128)(2,1)S(1)} %convolution_convert_fusion.9), channel_id=1, source_target_pairs={{0,4},{4,0},{8,12},{12,8},{16,20},{20,16},{24,28},{28,24},{1,5},{5... | collective-permute-start | bytes 196616 | tf_op jit(solution)/shard_map/ppermute | solution.py:18
  (27 other events, 160.0 us)

commit v15 on v12

--- a/solution.py
+++ b/solution.py
@@ -45,6 +45,7 @@
     rounded = vector.astype(jnp.bfloat16)
     before = from_behind(rounded[nodes - 1], "rep", 1)
     other = partner(rounded, "dom", 0).astype(vector.dtype)
+    result = local_stiffness(rounded, diag_tiles, off_tiles, cols_onehot, mirror_onehot)
     near = jnp.einsum("sn,nrk->srk", near_onehot, vector, precision=lax.Precision.HIGHEST)
     far = jnp.einsum("sn,nrk->srk", far_onehot, other, precision=lax.Precision.HIGHEST)
     difference = (near - far).astype(jnp.bfloat16)
@@ -61,7 +62,6 @@
         rounded[0], link_tile, (((1,), (1,)), ((), ())), preferred_element_type=jnp.float32
     )
     after = from_behind(back_term, "rep", -1)
-    result = local_stiffness(rounded, diag_tiles, off_tiles, cols_onehot, mirror_onehot)
     first_add = jnp.dot(before, link_tile, preferred_element_type=jnp.float32)
     ends = jnp.concatenate(
         [first_add[None], jnp.zeros((nodes - 2,) + first_add.shape, jnp.float32), after[None]]

time: 116 us -> 124 us (1.069)
  other arithmetic: 6.67 us -> 13.4 us
  matrix products: 24.4 us -> 30.3 us
  waiting for transfers between devices: 24.6 us -> 21.7 us
  local copies, waits for them, and re-layouts: 3.38 us -> 2.08 us
    ppermute x14, waiting for transfers between devices: 20.9 us -> 16.8 us  [from_behind(): return lax.ppermute(value, axis, pairs)]
    convert_element_type x4, other arithmetic: 0.51 us -> 3.46 us  [apply_operator(): rounded = vector.astype(jnp.bfloat16)]
    dot_general x4, matrix products: 0.71 us -> 3.38 us  [local_stiffness(): jnp.einsum('nrk,nkj->nrj', rounded, diag_tiles, preferred_element_type=jn...]
    dot_general x4, matrix products: 0.93 us -> 3.54 us  [local_stiffness(): jnp.einsum('pn,nrk->prk', cols_onehot, rounded, preferred_element_type=jn...]
    ppermute x14, starting transfers between devices: 6.46 us -> 8.06 us  [from_behind(): return lax.ppermute(value, axis, pairs)]
    unnamed x37 -> x59, local copies, waits for them, and re-layouts: 2.13 us -> 0.82 us
  transfers between devices with their start and end apart: 22 -> 22, of which waited for: 16 -> 13; matrix products, arithmetic and copies ran while one was open for 8% -> 19% of each run, Pallas kernels for 0% -> 0%
where the time goes in v15:
time: 124 us
  blocking collectives  38.6 us (31%)
  matrix products  30.3 us (24%)
  waiting for transfers between devices  21.7 us (18%)
  starting transfers between devices  16.3 us (13%)
  other arithmetic  13.4 us (11%)
  local copies, waits for them, and re-layouts  2.08 us (2%)
  between operations  1.25 us (1%)
    all_to_all x4, blocking collectives, total(): gathered = lax.all_to_all(spread, ('dom', 'rep'), 0, 0, tiled=True)  38.6 us
    ppermute x14, waiting for transfers between devices, from_behind(): return lax.ppermute(value, axis, pairs)  16.8 us
    ppermute x8, starting transfers between devices, partner(): lax.ppermute(value, axis, [(i, i ^ 1 << distance) for i in range(lax.axis...  8.26 us
    ppermute x14, starting transfers between devices, from_behind(): return lax.ppermute(value, axis, pairs)  8.06 us
    dot_general x4, matrix products, apply_operator(): jnp.einsum('srj,skj->srk', multiplier, contact_set, preferred_element_typ...  5.58 us
    ppermute x8, waiting for transfers between devices, partner(): lax.ppermute(value, axis, [(i, i ^ 1 << distance) for i in range(lax.axis...  4.85 us
    dot_general x4, matrix products, local_stiffness(): jnp.einsum('pn,prj->nrj', mirror_onehot, mirror, precision=lax.Precision....  4.06 us
    dot_general x4, matrix products, local_stiffness(): jnp.einsum('pn,nrk->prk', cols_onehot, rounded, preferred_element_type=jn...  3.54 us
  transfers between devices with their start and end apart: 22, of which 13 were waited for; matrix products, arithmetic and copies ran while one was open for 19% of the time, Pallas kernels for 0%

profile of v15, /device:TPU:0, one launch (start us, length us, event | category | flops | bytes accessed | tf_op | source)
XLA Modules:
  0.0 123.6 jit_solution(10369711178022999572)
XLA Ops:
  4.5 2.6 %collective-permute-start.2 = (s32[8,2]{0,1:T(2,128)S(1)}, s32[8,2]{0,1:T(2,128)S(1)}, u32[]{:S(2)}, u32[]{:S(2)}) collective-permute-start(s32[8,2]{0,1:T(2,128)S(1)} %bitcast.327), channel_id=1, source_target_pairs={{0,2},{1,3},{2,0},{3,1},{4,6},{5,7},{6,4},{7,5},{8,10},{9,11},{10,... | collective-permute-start | bytes 200 | tf_op jit(solution)/shard_map/ppermute | solution.py:14
  7.0 1.4 %collective-permute-start.3 = (s32[8,2]{0,1:T(2,128)S(1)}, s32[8,2]{0,1:T(2,128)S(1)}, u32[]{:S(2)}, u32[]{:S(2)}) collective-permute-start(s32[8,2]{0,1:T(2,128)S(1)} %bitcast.326), channel_id=1, source_target_pairs={{0,3},{1,0},{2,1},{3,2},{4,7},{5,4},{6,5},{7,6},{8,11},{9,8},{10,9... | collective-permute-start | bytes 200 | tf_op jit(solution)/shard_map/ppermute | solution.py:14
  8.4 1.6 %fusion.108 = (bf16[8,32,128]{2,1,0:T(8,128)(2,1)S(1)}, f32[8,32,128]{2,1,0:T(8,128)}) fusion(f32[8,32,128]{2,1,0:T(8,128)} %param.14, f32[8,128]{1,0:T(8,128)} %param.15), kind=kLoop, calls=%fused_computation.160 | loop fusion | flops 65536 | bytes 331776 | tf_op jit(solution)/shard_map/convert_element_type | solution.py:45
  10.0 1.5 %collective-permute-start.4 = (bf16[8,32,128]{2,1,0:T(8,128)(2,1)S(1)}, bf16[8,32,128]{2,1,0:T(8,128)(2,1)}, u32[]{:S(2)}, u32[]{:S(2)}) collective-permute-start(bf16[8,32,128]{2,1,0:T(8,128)(2,1)S(1)} %get-tuple-element.16), channel_id=1, source_target_pairs={{0,4},{4,0},{8,12},{12,8},{16,20},{20,16},{24,28},{28,24},{1,5},{5... | collective-permute-start | bytes 196616 | tf_op jit(solution)/shard_map/ppermute | solution.py:18
  17.6 1.5 %collective-permute-start.7 = (bf16[8,128,128]{2,0,1:T(8,128)(2,1)}, bf16[8,128,128]{2,0,1:T(8,128)(2,1)S(1)}, u32[]{:S(2)}, u32[]{:S(2)}) collective-permute-start(bf16[8,128,128]{2,0,1:T(8,128)(2,1)} %select_bitcast_fusion), channel_id=1, source_target_pairs={{0,3},{1,0},{2,1},{3,2},{4,7},{5,4},{6,5},{7,6},{8,11},{9,8},{10,9... | collective-permute-start | bytes 786440 | tf_op jit(solution)/shard_map/ppermute | solution.py:14
  19.6 6.4 %collective-permute-done = bf16[32,128]{1,0:T(8,128)(2,1)S(1)} collective-permute-done((bf16[32,128]{1,0:T(8,128)(2,1)S(1)}, bf16[32,128]{1,0:T(8,128)(2,1)S(1)}, u32[]{:S(2)}, u32[]{:S(2)}) %collective-permute-start) | collective-permute-done | bytes 8224 | tf_op jit(solution)/shard_map/ppermute | solution.py:14
  30.9 1.6 %collective-permute-start.8 = (f32[32,128]{1,0:T(8,128)S(1)}, f32[32,128]{1,0:T(8,128)S(1)}, u32[]{:S(2)}, u32[]{:S(2)}) collective-permute-start(f32[32,128]{1,0:T(8,128)S(1)} %fusion.105), channel_id=1, source_target_pairs={{0,3},{1,0},{2,1},{3,2},{4,7},{5,4},{6,5},{7,6},{8,11},{9,8},{10,9... | collective-permute-start | bytes 49160 | tf_op jit(solution)/shard_map/ppermute | solution.py:14
  33.9 1.3 %collective-permute-done.9 = bf16[8,32,128]{2,1,0:T(8,128)(2,1)S(1)} collective-permute-done((bf16[8,32,128]{2,1,0:T(8,128)(2,1)S(1)}, bf16[8,32,128]{2,1,0:T(8,128)(2,1)S(1)}, u32[]{:S(2)}, u32[]{:S(2)}) %collective-permute-start.9) | collective-permute-done | bytes 65568 | tf_op jit(solution)/shard_map/ppermute | solution.py:18
  35.7 12.0 %all_to_all.20 = f32[32,1,128]{2,1,0:T(1,128)S(1)} all-to-all(f32[32,1,128]{2,1,0:T(1,128)S(1)} %reshape.371), channel_id=1, replica_groups=mesh['dom'=8,'rep'=4] {'dom','rep'}, dimensions={0} | all-to-all | bytes 32768 | tf_op jit(solution)/shard_map/all_to_all | solution.py:24
  53.4 2.2 %collective-permute-done.10 = bf16[32,128]{1,0:T(8,128)(2,1)S(1)} collective-permute-done((bf16[32,128]{1,0:T(8,128)(2,1)S(1)}, bf16[32,128]{1,0:T(8,128)(2,1)S(1)}, u32[]{:S(2)}, u32[]{:S(2)}) %collective-permute-start.10) | collective-permute-done | bytes 8224 | tf_op jit(solution)/shard_map/ppermute | solution.py:14
  56.7 1.9 %fusion.6 = f32[32,32,128]{2,1,0:T(8,128)S(1)} fusion(bf16[32,128,128]{2,1,0:T(8,128)(2,1)S(1)} %bitcast.292, bf16[32,32,128]{2,0,1:T(8,128)(2,1)} %fusion.2), kind=kOutput, calls=%fused_computation.15 | convolution fusion | flops 67239936 | bytes 1835008 | tf_op jit(solution)/shard_map/srj,skj->srk/dot_general | solution.py:55
  59.2 1.5 %collective-permute-start.13 = (bf16[8,32,128]{2,1,0:T(8,128)(2,1)S(1)}, bf16[8,32,128]{2,1,0:T(8,128)(2,1)S(1)}, u32[]{:S(2)}, u32[]{:S(2)}) collective-permute-start(bf16[8,32,128]{2,1,0:T(8,128)(2,1)S(1)} %copy.317), channel_id=1, source_target_pairs={{0,4},{4,0},{8,12},{12,8},{16,20},{20,16},{24,28},{28,24},{1,5},{5... | collective-permute-start | bytes 196616 | tf_op jit(solution)/shard_map/ppermute | solution.py:18
  62.3 1.2 collective-permute-done.13
  64.0 8.8 %all_to_all.21 = f32[32,1,128]{2,1,0:T(1,128)S(1)} all-to-all(f32[32,1,128]{2,1,0:T(1,128)S(1)} %reshape.373), channel_id=1, replica_groups=mesh['dom'=8,'rep'=4] {'dom','rep'}, dimensions={0} | all-to-all | bytes 32768 | tf_op jit(solution)/shard_map/all_to_all | solution.py:24
  73.8 1.7 %fusion.183 = (bf16[8,32,128]{2,1,0:T(8,128)(2,1)S(1)}, f32[8,32,128]{2,1,0:T(8,128)S(1)}, f32[8,32,128]{2,1,0:T(8,128)}) fusion(f32[8,32,128]{2,1,0:T(8,128)S(1)} %get-tuple-element.74, f32[32]{0:T(128)S(1)} %get-tuple-element.70, f32[8,128]{1,0:T(8,128)S(1)} %copy-done.23, f32[8,32,128]{2,1,0:T(8,128)} %copy-done.9, ...), kind=kLoop, calls=%fused_computation.249 | loop fusion | flops 196608 | bytes 725248 | tf_op jit(solution)/shard_map/convert_element_type | solution.py:45
  79.4 2.2 %collective-permute-done.14 = bf16[32,128]{1,0:T(8,128)(2,1)S(1)} collective-permute-done((bf16[32,128]{1,0:T(8,128)(2,1)S(1)}, bf16[32,128]{1,0:T(8,128)(2,1)S(1)}, u32[]{:S(2)}, u32[]{:S(2)}) %collective-permute-start.14) | collective-permute-done | bytes 8224 | tf_op jit(solution)/shard_map/ppermute | solution.py:14
  82.7 1.9 %fusion.7 = f32[32,32,128]{2,1,0:T(8,128)S(1)} fusion(bf16[32,128,128]{2,1,0:T(8,128)(2,1)S(1)} %bitcast.293, bf16[32,32,128]{2,0,1:T(8,128)(2,1)} %fusion.3), kind=kOutput, calls=%fused_computation.16 | convolution fusion | flops 67239936 | bytes 1835008 | tf_op jit(solution)/shard_map/srj,skj->srk/dot_general | solution.py:55
  85.2 1.5 %collective-permute-start.17 = (bf16[8,32,128]{2,1,0:T(8,128)(2,1)S(1)}, bf16[8,32,128]{2,1,0:T(8,128)(2,1)S(1)}, u32[]{:S(2)}, u32[]{:S(2)}) collective-permute-start(bf16[8,32,128]{2,1,0:T(8,128)(2,1)S(1)} %copy.316), channel_id=1, source_target_pairs={{0,4},{4,0},{8,12},{12,8},{16,20},{20,16},{24,28},{28,24},{1,5},{5... | collective-permute-start | bytes 196616 | tf_op jit(solution)/shard_map/ppermute | solution.py:18
  88.4 1.2 collective-permute-done.17
  90.1 8.8 %all_to_all.22 = f32[32,1,128]{2,1,0:T(1,128)S(1)} all-to-all(f32[32,1,128]{2,1,0:T(1,128)S(1)} %reshape.375), channel_id=1, replica_groups=mesh['dom'=8,'rep'=4] {'dom','rep'}, dimensions={0} | all-to-all | bytes 32768 | tf_op jit(solution)/shard_map/all_to_all | solution.py:24
  104.7 2.4 %collective-permute-done.18 = bf16[32,128]{1,0:T(8,128)(2,1)S(1)} collective-permute-done((bf16[32,128]{1,0:T(8,128)(2,1)S(1)}, bf16[32,128]{1,0:T(8,128)(2,1)S(1)}, u32[]{:S(2)}, u32[]{:S(2)}) %collective-permute-start.18) | collective-permute-done | bytes 8224 | tf_op jit(solution)/shard_map/ppermute | solution.py:14
  109.1 1.5 %collective-permute-start.21 = (bf16[8,32,128]{2,1,0:T(8,128)(2,1)S(1)}, bf16[8,32,128]{2,1,0:T(8,128)(2,1)S(1)}, u32[]{:S(2)}, u32[]{:S(2)}) collective-permute-start(bf16[8,32,128]{2,1,0:T(8,128)(2,1)S(1)} %copy.315), channel_id=1, source_target_pairs={{0,4},{4,0},{8,12},{12,8},{16,20},{20,16},{24,28},{28,24},{1,5},{5... | collective-permute-start | bytes 196616 | tf_op jit(solution)/shard_map/ppermute | solution.py:18
  112.2 1.2 collective-permute-done.21
  113.8 8.9 %all_to_all.23 = f32[32,2,32]{2,1,0:T(2,128)S(1)} all-to-all(f32[32,2,32]{2,1,0:T(2,128)S(1)} %broadcast_in_dim.115), channel_id=1, replica_groups=mesh['dom'=8,'rep'=4] {'dom','rep'}, dimensions={0} | all-to-all | bytes 16384 | tf_op jit(solution)/shard_map/all_to_all | solution.py:24
  (186 shorter events, 45.7 us)
Async XLA Ops:
  4.0 13.1 %collective-permute-start.1 = (s32[8,2]{0,1:T(2,128)S(1)}, s32[8,2]{0,1:T(2,128)S(1)}, u32[]{:S(2)}, u32[]{:S(2)}) collective-permute-start(s32[8,2]{0,1:T(2,128)S(1)} %bitcast.328), channel_id=1, source_target_pairs={{0,1},{1,2},{2,3},{3,0},{4,5},{5,6},{6,7},{7,4},{8,9},{9,10},{10,1... | collective-permute-start | bytes 200 | tf_op jit(solution)/shard_map/ppermute | solution.py:14
  4.5 13.2 %collective-permute-start.2 = (s32[8,2]{0,1:T(2,128)S(1)}, s32[8,2]{0,1:T(2,128)S(1)}, u32[]{:S(2)}, u32[]{:S(2)}) collective-permute-start(s32[8,2]{0,1:T(2,128)S(1)} %bitcast.327), channel_id=1, source_target_pairs={{0,2},{1,3},{2,0},{3,1},{4,6},{5,7},{6,4},{7,5},{8,10},{9,11},{10,... | collective-permute-start | bytes 200 | tf_op jit(solution)/shard_map/ppermute | solution.py:14
  7.0 12.1 %collective-permute-start.3 = (s32[8,2]{0,1:T(2,128)S(1)}, s32[8,2]{0,1:T(2,128)S(1)}, u32[]{:S(2)}, u32[]{:S(2)}) collective-permute-start(s32[8,2]{0,1:T(2,128)S(1)} %bitcast.326), channel_id=1, source_target_pairs={{0,3},{1,0},{2,1},{3,2},{4,7},{5,4},{6,5},{7,6},{8,11},{9,8},{10,9... | collective-permute-start | bytes 200 | tf_op jit(solution)/shard_map/ppermute | solution.py:14
  10.0 16.1 %collective-permute-start.4 = (bf16[8,32,128]{2,1,0:T(8,128)(2,1)S(1)}, bf16[8,32,128]{2,1,0:T(8,128)(2,1)}, u32[]{:S(2)}, u32[]{:S(2)}) collective-permute-start(bf16[8,32,128]{2,1,0:T(8,128)(2,1)S(1)} %get-tuple-element.16), channel_id=1, source_target_pairs={{0,4},{4,0},{8,12},{12,8},{16,20},{20,16},{24,28},{28,24},{1,5},{5... | collective-permute-start | bytes 196616 | tf_op jit(solution)/shard_map/ppermute | solution.py:18
  13.1 14.2 %collective-permute-start.5 = (bf16[8,128,128]{2,0,1:T(8,128)(2,1)}, bf16[8,128,128]{2,0,1:T(8,128)(2,1)}, u32[]{:S(2)}, u32[]{:S(2)}) collective-permute-start(bf16[8,128,128]{2,0,1:T(8,128)(2,1)} %get-tuple-element.80), channel_id=1, source_target_pairs={{0,1},{1,2},{2,3},{3,0},{4,5},{5,6},{6,7},{7,4},{8,9},{9,10},{10,1... | collective-permute-start | bytes 786440 | tf_op jit(solution)/shard_map/ppermute | solution.py:14
  17.1 10.2 %collective-permute-start.6 = (bf16[8,128,128]{2,0,1:T(8,128)(2,1)}, bf16[8,128,128]{2,0,1:T(8,128)(2,1)S(1)}, u32[]{:S(2)}, u32[]{:S(2)}) collective-permute-start(bf16[8,128,128]{2,0,1:T(8,128)(2,1)} %get-tuple-element.81), channel_id=1, source_target_pairs={{0,2},{1,3},{2,0},{3,1},{4,6},{5,7},{6,4},{7,5},{8,10},{9,11},{10,... | collective-permute-start | bytes 786440 | tf_op jit(solution)/shard_map/ppermute | solution.py:14
  17.6 9.9 %collective-permute-start.7 = (bf16[8,128,128]{2,0,1:T(8,128)(2,1)}, bf16[8,128,128]{2,0,1:T(8,128)(2,1)S(1)}, u32[]{:S(2)}, u32[]{:S(2)}) collective-permute-start(bf16[8,128,128]{2,0,1:T(8,128)(2,1)} %select_bitcast_fusion), channel_id=1, source_target_pairs={{0,3},{1,0},{2,1},{3,2},{4,7},{5,4},{6,5},{7,6},{8,11},{9,8},{10,9... | collective-permute-start | bytes 786440 | tf_op jit(solution)/shard_map/ppermute | solution.py:14
  19.1 6.9 %collective-permute-start = (bf16[32,128]{1,0:T(8,128)(2,1)S(1)}, bf16[32,128]{1,0:T(8,128)(2,1)S(1)}, u32[]{:S(2)}, u32[]{:S(2)}) collective-permute-start(bf16[32,128]{1,0:T(8,128)(2,1)S(1)} %slice_bitcast_fusion.3), channel_id=1, source_target_pairs={{0,1},{1,2},{2,3},{3,0},{4,5},{5,6},{6,7},{7,4},{8,9},{9,10},{10,1... | collective-permute-start | bytes 24584 | tf_op jit(solution)/shard_map/ppermute | solution.py:14
  30.4 4.8 %collective-permute-start.9 = (bf16[8,32,128]{2,1,0:T(8,128)(2,1)S(1)}, bf16[8,32,128]{2,1,0:T(8,128)(2,1)S(1)}, u32[]{:S(2)}, u32[]{:S(2)}) collective-permute-start(bf16[8,32,128]{2,1,0:T(8,128)(2,1)S(1)} %copy.318), channel_id=1, source_target_pairs={{0,4},{4,0},{8,12},{12,8},{16,20},{20,16},{24,28},{28,24},{1,5},{5... | collective-permute-start | bytes 196616 | tf_op jit(solution)/shard_map/ppermute | solution.py:18
  30.9 3.0 %collective-permute-start.8 = (f32[32,128]{1,0:T(8,128)S(1)}, f32[32,128]{1,0:T(8,128)S(1)}, u32[]{:S(2)}, u32[]{:S(2)}) collective-permute-start(f32[32,128]{1,0:T(8,128)S(1)} %fusion.105), channel_id=1, source_target_pairs={{0,3},{1,0},{2,1},{3,2},{4,7},{5,4},{6,5},{7,6},{8,11},{9,8},{10,9... | collective-permute-start | bytes 49160 | tf_op jit(solution)/shard_map/ppermute | solution.py:14
  49.3 14.2 %copy-start.9 = (f32[8,32,128]{2,1,0:T(8,128)}, f32[8,32,128]{2,1,0:T(8,128)S(1)}, u32[]{:S(2)}) copy-start(f32[8,32,128]{2,1,0:T(8,128)S(1)} %get-tuple-element.75) | copy-start | bytes 393220
  49.3 6.4 %collective-permute-start.11 = (bf16[8,32,128]{2,1,0:T(8,128)(2,1)S(1)}, bf16[8,32,128]{2,1,0:T(8,128)(2,1)S(1)}, u32[]{:S(2)}, u32[]{:S(2)}) collective-permute-start(bf16[8,32,128]{2,1,0:T(8,128)(2,1)S(1)} %get-tuple-element.19), channel_id=1, source_target_pairs={{0,4},{4,0},{8,12},{12,8},{16,20},{20,16},{24,28},{28,24},{1,5},{5... | collective-permute-start | bytes 196616 | tf_op jit(solution)/shard_map/ppermute | solution.py:18
  52.5 3.1 %collective-permute-start.10 = (bf16[32,128]{1,0:T(8,128)(2,1)S(1)}, bf16[32,128]{1,0:T(8,128)(2,1)S(1)}, u32[]{:S(2)}, u32[]{:S(2)}) collective-permute-start(bf16[32,128]{1,0:T(8,128)(2,1)S(1)} %slice_bitcast_fusion.2), channel_id=1, source_target_pairs={{0,1},{1,2},{2,3},{3,0},{4,5},{5,6},{6,7},{7,4},{8,9},{9,10},{10,1... | collective-permute-start | bytes 24584 | tf_op jit(solution)/shard_map/ppermute | solution.py:14
  59.2 4.3 %collective-permute-start.13 = (bf16[8,32,128]{2,1,0:T(8,128)(2,1)S(1)}, bf16[8,32,128]{2,1,0:T(8,128)(2,1)S(1)}, u32[]{:S(2)}, u32[]{:S(2)}) collective-permute-start(bf16[8,32,128]{2,1,0:T(8,128)(2,1)S(1)} %copy.317), channel_id=1, source_target_pairs={{0,4},{4,0},{8,12},{12,8},{16,20},{20,16},{24,28},{28,24},{1,5},{5... | collective-permute-start | bytes 196616 | tf_op jit(solution)/shard_map/ppermute | solution.py:18
  60.8 1.5 %collective-permute-start.12 = (f32[32,128]{1,0:T(8,128)S(1)}, f32[32,128]{1,0:T(8,128)S(1)}, u32[]{:S(2)}, u32[]{:S(2)}) collective-permute-start(f32[32,128]{1,0:T(8,128)S(1)} %fusion.102), channel_id=1, source_target_pairs={{0,3},{1,0},{2,1},{3,2},{4,7},{5,4},{6,5},{7,6},{8,11},{9,8},{10,9... | collective-permute-start | bytes 49160 | tf_op jit(solution)/shard_map/ppermute | solution.py:14
  75.4 6.3 %collective-permute-start.15 = (bf16[8,32,128]{2,1,0:T(8,128)(2,1)S(1)}, bf16[8,32,128]{2,1,0:T(8,128)(2,1)S(1)}, u32[]{:S(2)}, u32[]{:S(2)}) collective-permute-start(bf16[8,32,128]{2,1,0:T(8,128)(2,1)S(1)} %get-tuple-element.22), channel_id=1, source_target_pairs={{0,4},{4,0},{8,12},{12,8},{16,20},{20,16},{24,28},{28,24},{1,5},{5... | collective-permute-start | bytes 196616 | tf_op jit(solution)/shard_map/ppermute | solution.py:18
  78.5 3.1 %collective-permute-start.14 = (bf16[32,128]{1,0:T(8,128)(2,1)S(1)}, bf16[32,128]{1,0:T(8,128)(2,1)S(1)}, u32[]{:S(2)}, u32[]{:S(2)}) collective-permute-start(bf16[32,128]{1,0:T(8,128)(2,1)S(1)} %slice_bitcast_fusion.1), channel_id=1, source_target_pairs={{0,1},{1,2},{2,3},{3,0},{4,5},{5,6},{6,7},{7,4},{8,9},{9,10},{10,1... | collective-permute-start | bytes 24584 | tf_op jit(solution)/shard_map/ppermute | solution.py:14
  85.2 4.3 %collective-permute-start.17 = (bf16[8,32,128]{2,1,0:T(8,128)(2,1)S(1)}, bf16[8,32,128]{2,1,0:T(8,128)(2,1)S(1)}, u32[]{:S(2)}, u32[]{:S(2)}) collective-permute-start(bf16[8,32,128]{2,1,0:T(8,128)(2,1)S(1)} %copy.316), channel_id=1, source_target_pairs={{0,4},{4,0},{8,12},{12,8},{16,20},{20,16},{24,28},{28,24},{1,5},{5... | collective-permute-start | bytes 196616 | tf_op jit(solution)/shard_map/ppermute | solution.py:18
  86.9 1.5 %collective-permute-start.16 = (f32[32,128]{1,0:T(8,128)S(1)}, f32[32,128]{1,0:T(8,128)S(1)}, u32[]{:S(2)}, u32[]{:S(2)}) collective-permute-start(f32[32,128]{1,0:T(8,128)S(1)} %fusion.99), channel_id=1, source_target_pairs={{0,3},{1,0},{2,1},{3,2},{4,7},{5,4},{6,5},{7,6},{8,11},{9,8},{10,9... | collective-permute-start | bytes 49160 | tf_op jit(solution)/shard_map/ppermute | solution.py:14
  87.5 12.3 %copy-start.8 = (f32[8,32,128]{2,1,0:T(8,128)S(1)}, f32[8,32,128]{2,1,0:T(8,128)}, u32[]{:S(2)}) copy-start(f32[8,32,128]{2,1,0:T(8,128)} %get-tuple-element.69) | copy-start | bytes 393220
  100.0 7.2 %collective-permute-start.19 = (bf16[8,32,128]{2,1,0:T(8,128)(2,1)S(1)}, bf16[8,32,128]{2,1,0:T(8,128)(2,1)S(1)}, u32[]{:S(2)}, u32[]{:S(2)}) collective-permute-start(bf16[8,32,128]{2,1,0:T(8,128)(2,1)S(1)} %get-tuple-element.25), channel_id=1, source_target_pairs={{0,4},{4,0},{8,12},{12,8},{16,20},{20,16},{24,28},{28,24},{1,5},{5... | collective-permute-start | bytes 196616 | tf_op jit(solution)/shard_map/ppermute | solution.py:18
  104.0 3.1 %collective-permute-start.18 = (bf16[32,128]{1,0:T(8,128)(2,1)S(1)}, bf16[32,128]{1,0:T(8,128)(2,1)S(1)}, u32[]{:S(2)}, u32[]{:S(2)}) collective-permute-start(bf16[32,128]{1,0:T(8,128)(2,1)S(1)} %slice_bitcast_fusion), channel_id=1, source_target_pairs={{0,1},{1,2},{2,3},{3,0},{4,5},{5,6},{6,7},{7,4},{8,9},{9,10},{10,1... | collective-permute-start | bytes 24584 | tf_op jit(solution)/shard_map/ppermute | solution.py:14
  109.1 4.3 %collective-permute-start.21 = (bf16[8,32,128]{2,1,0:T(8,128)(2,1)S(1)}, bf16[8,32,128]{2,1,0:T(8,128)(2,1)S(1)}, u32[]{:S(2)}, u32[]{:S(2)}) collective-permute-start(bf16[8,32,128]{2,1,0:T(8,128)(2,1)S(1)} %copy.315), channel_id=1, source_target_pairs={{0,4},{4,0},{8,12},{12,8},{16,20},{20,16},{24,28},{28,24},{1,5},{5... | collective-permute-start | bytes 196616 | tf_op jit(solution)/shard_map/ppermute | solution.py:18
  110.7 1.5 %collective-permute-start.20 = (f32[32,128]{1,0:T(8,128)S(1)}, f32[32,128]{1,0:T(8,128)S(1)}, u32[]{:S(2)}, u32[]{:S(2)}) collective-permute-start(f32[32,128]{1,0:T(8,128)S(1)} %fusion.96), channel_id=1, source_target_pairs={{0,3},{1,0},{2,1},{3,2},{4,7},{5,4},{6,5},{7,6},{8,11},{9,8},{10,9... | collective-permute-start | bytes 49160 | tf_op jit(solution)/shard_map/ppermute | solution.py:14
  (24 other events, 130.4 us)

commit v16 on v12

--- a/solution.py
+++ b/solution.py
@@ -20,9 +20,10 @@
 
 def total(value):
     count = lax.axis_size("dom") * lax.axis_size("rep")
-    spread = jnp.broadcast_to(value[None], (count,) + value.shape)
+    flat = value.reshape(-1)
+    spread = jnp.broadcast_to(flat[None, None], (count, 8, flat.shape[0]))
     gathered = lax.all_to_all(spread, ("dom", "rep"), 0, 0, tiled=True)
-    return jnp.sum(gathered, axis=0)
+    return jnp.sum(gathered[:, 0], axis=0).reshape(value.shape)
 
 
 def local_stiffness(rounded, diag_tiles, off_tiles, cols_onehot, mirror_onehot):

time: 116 us -> 119 us (1.026)
  blocking collectives: 39.4 us -> 44.3 us
    all_to_all x4, blocking collectives: 39.4 us -> 44.3 us  [total(): gathered = lax.all_to_all(spread, ('dom', 'rep'), 0, 0, tiled=True)]
    all_to_all x3 -> x1, other arithmetic: 2.05 us -> 0.8 us  [total(): gathered = lax.all_to_all(spread, ('dom', 'rep'), 0, 0, tiled=True)]
where the time goes in v16:
time: 119 us
  blocking collectives  44.3 us (37%)
  matrix products  24.5 us (21%)
  waiting for transfers between devices  24.5 us (21%)
  starting transfers between devices  15.6 us (13%)
  other arithmetic  5.58 us (5%)
  local copies, waits for them, and re-layouts  3.37 us (3%)
  between operations  1.23 us (1%)
    all_to_all x4, blocking collectives, total(): gathered = lax.all_to_all(spread, ('dom', 'rep'), 0, 0, tiled=True)  44.3 us
    ppermute x14, waiting for transfers between devices, from_behind(): return lax.ppermute(value, axis, pairs)  20.9 us
    ppermute x8, starting transfers between devices, partner(): lax.ppermute(value, axis, [(i, i ^ 1 << distance) for i in range(lax.axis...  9.14 us
    dot_general x4, matrix products, apply_operator(): jnp.einsum('srj,skj->srk', multiplier, contact_set, preferred_element_typ...  6.53 us
    ppermute x14, starting transfers between devices, from_behind(): return lax.ppermute(value, axis, pairs)  6.46 us
    ppermute x8, waiting for transfers between devices, partner(): lax.ppermute(value, axis, [(i, i ^ 1 << distance) for i in range(lax.axis...  3.58 us
    dot_general x4, matrix products, local_stiffness(): jnp.einsum('pn,prj->nrj', mirror_onehot, mirror, precision=lax.Precision....  3.2 us
    dot_general x4, matrix products, apply_operator(): jnp.einsum('sn,nrk->srk', far_onehot, other, precision=lax.Precision.HIGH...  3.17 us
  transfers between devices with their start and end apart: 22, of which 16 were waited for; matrix products, arithmetic and copies ran while one was open for 8% of the time, Pallas kernels for 0%

profile of v16, /device:TPU:0, one launch (start us, length us, event | category | flops | bytes accessed | tf_op | source)
XLA Modules:
  0.0 119.0 jit_solution(16775694178165307402)
XLA Ops:
  3.7 2.4 %collective-permute-start.6 = (bf16[8,128,128]{2,0,1:T(8,128)(2,1)S(1)}, bf16[8,128,128]{2,0,1:T(8,128)(2,1)S(1)}, u32[]{:S(2)}, u32[]{:S(2)}) collective-permute-start(bf16[8,128,128]{2,0,1:T(8,128)(2,1)S(1)} %select_bitcast_fusion), channel_id=1, source_target_pairs={{0,3},{1,0},{2,1},{3,2},{4,7},{5,4},{6,5},{7,6},{8,11},{9,8},{10,9... | collective-permute-start | bytes 786440 | tf_op jit(solution)/shard_map/ppermute | solution.py:14
  7.3 1.7 %collective-permute-start.1 = (s32[8,2]{0,1:T(2,128)S(1)}, s32[8,2]{0,1:T(2,128)S(1)}, u32[]{:S(2)}, u32[]{:S(2)}) collective-permute-start(s32[8,2]{0,1:T(2,128)S(1)} %bitcast.279), channel_id=1, source_target_pairs={{0,2},{1,3},{2,0},{3,1},{4,6},{5,7},{6,4},{7,5},{8,10},{9,11},{10,... | collective-permute-start | bytes 200 | tf_op jit(solution)/shard_map/ppermute | solution.py:14
  9.2 1.6 %collective-permute-start.3 = (bf16[8,32,128]{2,0,1:T(8,128)(2,1)S(1)}, bf16[8,32,128]{2,0,1:T(8,128)(2,1)S(1)}, u32[]{:S(2)}, u32[]{:S(2)}) collective-permute-start(bf16[8,32,128]{2,0,1:T(8,128)(2,1)S(1)} %multiply_convert_fusion), channel_id=1, source_target_pairs={{0,4},{4,0},{8,12},{12,8},{16,20},{20,16},{24,28},{28,24},{1,5},{5... | collective-permute-start | bytes 196616 | tf_op jit(solution)/shard_map/ppermute | solution.py:18
  11.1 4.6 %collective-permute-done.2 = s32[8,2]{0,1:T(2,128)S(1)} collective-permute-done((s32[8,2]{0,1:T(2,128)S(1)}, s32[8,2]{0,1:T(2,128)S(1)}, u32[]{:S(2)}, u32[]{:S(2)}) %collective-permute-start.2) | collective-permute-done | bytes 96 | tf_op jit(solution)/shard_map/ppermute | solution.py:14
  15.7 1.1 collective-permute-start
  16.8 2.3 %collective-permute-done = s32[8,2]{0,1:T(2,128)S(1)} collective-permute-done((s32[8,2]{0,1:T(2,128)S(1)}, s32[8,2]{0,1:T(2,128)S(1)}, u32[]{:S(2)}, u32[]{:S(2)}) %collective-permute-start) | collective-permute-done | bytes 96 | tf_op jit(solution)/shard_map/ppermute | solution.py:14
  19.6 3.0 %collective-permute-done.7 = bf16[32,128]{1,0:T(8,128)(2,1)S(1)} collective-permute-done((bf16[32,128]{1,0:T(8,128)(2,1)S(1)}, bf16[32,128]{1,0:T(8,128)(2,1)S(1)}, u32[]{:S(2)}, u32[]{:S(2)}) %collective-permute-start.7) | collective-permute-done | bytes 8224 | tf_op jit(solution)/shard_map/ppermute | solution.py:14
  25.0 1.6 %collective-permute-start.9 = (bf16[8,32,128]{2,0,1:T(8,128)(2,1)S(1)}, bf16[8,32,128]{2,0,1:T(8,128)(2,1)S(1)}, u32[]{:S(2)}, u32[]{:S(2)}) collective-permute-start(bf16[8,32,128]{2,0,1:T(8,128)(2,1)S(1)} %convolution_convert_fusion.12), channel_id=1, source_target_pairs={{0,4},{4,0},{8,12},{12,8},{16,20},{20,16},{24,28},{28,24},{1,5},{5... | collective-permute-start | bytes 196616 | tf_op jit(solution)/shard_map/ppermute | solution.py:18
  30.3 13.9 %all_to_all.20 = f32[32,8,128]{2,1,0:T(8,128)S(1)} all-to-all(f32[32,8,128]{2,1,0:T(8,128)S(1)} %broadcast_in_dim.111), channel_id=1, replica_groups=mesh['dom'=8,'rep'=4] {'dom','rep'}, dimensions={0} | all-to-all | bytes 262144 | tf_op jit(solution)/shard_map/all_to_all | solution.py:25
  45.7 2.6 %collective-permute-done.11 = bf16[32,128]{1,0:T(8,128)(2,1)S(1)} collective-permute-done((bf16[32,128]{1,0:T(8,128)(2,1)S(1)}, bf16[32,128]{1,0:T(8,128)(2,1)S(1)}, u32[]{:S(2)}, u32[]{:S(2)}) %collective-permute-start.11) | collective-permute-done | bytes 8224 | tf_op jit(solution)/shard_map/ppermute | solution.py:14
  49.7 1.9 %fusion.6 = f32[32,32,128]{2,1,0:T(8,128)S(1)} fusion(bf16[32,128,128]{2,1,0:T(8,128)(2,1)S(1)} %bitcast.228, bf16[32,32,128]{2,0,1:T(8,128)(2,1)} %fusion.2), kind=kOutput, calls=%fused_computation.15 | convolution fusion | flops 67239936 | bytes 1835008 | tf_op jit(solution)/shard_map/srj,skj->srk/dot_general | solution.py:55
  52.6 1.1 collective-permute-start.13
  55.9 1.0 collective-permute-done.13
  57.9 10.3 %all_to_all.21 = f32[32,8,128]{2,1,0:T(8,128)S(1)} all-to-all(f32[32,8,128]{2,1,0:T(8,128)S(1)} %broadcast_in_dim.115), channel_id=1, replica_groups=mesh['dom'=8,'rep'=4] {'dom','rep'}, dimensions={0} | all-to-all | bytes 262144 | tf_op jit(solution)/shard_map/all_to_all | solution.py:25
  69.8 2.6 %collective-permute-done.15 = bf16[32,128]{1,0:T(8,128)(2,1)S(1)} collective-permute-done((bf16[32,128]{1,0:T(8,128)(2,1)S(1)}, bf16[32,128]{1,0:T(8,128)(2,1)S(1)}, u32[]{:S(2)}, u32[]{:S(2)}) %collective-permute-start.15) | collective-permute-done | bytes 8224 | tf_op jit(solution)/shard_map/ppermute | solution.py:14
  72.7 1.0 fusion.3
  73.7 1.9 %fusion.7 = f32[32,32,128]{2,1,0:T(8,128)S(1)} fusion(bf16[32,128,128]{2,1,0:T(8,128)(2,1)S(1)} %bitcast.229, bf16[32,32,128]{2,0,1:T(8,128)(2,1)} %fusion.3), kind=kOutput, calls=%fused_computation.16 | convolution fusion | flops 67239936 | bytes 1835008 | tf_op jit(solution)/shard_map/srj,skj->srk/dot_general | solution.py:55
  76.6 1.3 %collective-permute-start.17 = (bf16[8,32,128]{2,0,1:T(8,128)(2,1)S(1)}, bf16[8,32,128]{2,0,1:T(8,128)(2,1)S(1)}, u32[]{:S(2)}, u32[]{:S(2)}) collective-permute-start(bf16[8,32,128]{2,0,1:T(8,128)(2,1)S(1)} %convolution_convert_fusion.10), channel_id=1, source_target_pairs={{0,4},{4,0},{8,12},{12,8},{16,20},{20,16},{24,28},{28,24},{1,5},{5... | collective-permute-start | bytes 196616 | tf_op jit(solution)/shard_map/ppermute | solution.py:18
  81.8 10.4 %all_to_all.22 = f32[32,8,128]{2,1,0:T(8,128)S(1)} all-to-all(f32[32,8,128]{2,1,0:T(8,128)S(1)} %broadcast_in_dim.119), channel_id=1, replica_groups=mesh['dom'=8,'rep'=4] {'dom','rep'}, dimensions={0} | all-to-all | bytes 262144 | tf_op jit(solution)/shard_map/all_to_all | solution.py:25
  94.6 2.2 %collective-permute-done.19 = bf16[32,128]{1,0:T(8,128)(2,1)S(1)} collective-permute-done((bf16[32,128]{1,0:T(8,128)(2,1)S(1)}, bf16[32,128]{1,0:T(8,128)(2,1)S(1)}, u32[]{:S(2)}, u32[]{:S(2)}) %collective-permute-start.19) | collective-permute-done | bytes 8224 | tf_op jit(solution)/shard_map/ppermute | solution.py:14
  97.0 1.0 fusion.4
  98.0 1.9 %fusion.8 = f32[32,32,128]{2,1,0:T(8,128)S(1)} fusion(bf16[32,128,128]{2,1,0:T(8,128)(2,1)S(1)} %bitcast.230, bf16[32,32,128]{2,0,1:T(8,128)(2,1)} %fusion.4), kind=kOutput, calls=%fused_computation.17 | convolution fusion | flops 67239936 | bytes 1835008 | tf_op jit(solution)/shard_map/srj,skj->srk/dot_general | solution.py:55
  100.9 1.4 %collective-permute-start.21 = (bf16[8,32,128]{2,0,1:T(8,128)(2,1)S(1)}, bf16[8,32,128]{2,0,1:T(8,128)(2,1)S(1)}, u32[]{:S(2)}, u32[]{:S(2)}) collective-permute-start(bf16[8,32,128]{2,0,1:T(8,128)(2,1)S(1)} %convolution_convert_fusion.9), channel_id=1, source_target_pairs={{0,4},{4,0},{8,12},{12,8},{16,20},{20,16},{24,28},{28,24},{1,5},{5... | collective-permute-start | bytes 196616 | tf_op jit(solution)/shard_map/ppermute | solution.py:18
  106.2 9.7 %all_to_all.23 = f32[32,1,512]{2,1,0:T(1,128)S(1)} all-to-all(f32[32,1,512]{2,1,0:T(1,128)S(1)} %reshape.295), channel_id=1, replica_groups=mesh['dom'=8,'rep'=4] {'dom','rep'}, dimensions={0} | all-to-all | bytes 131072 | tf_op jit(solution)/shard_map/all_to_all | solution.py:25
  (166 shorter events, 35.2 us)
Async XLA Ops:
  3.7 19.4 %collective-permute-start.6 = (bf16[8,128,128]{2,0,1:T(8,128)(2,1)S(1)}, bf16[8,128,128]{2,0,1:T(8,128)(2,1)S(1)}, u32[]{:S(2)}, u32[]{:S(2)}) collective-permute-start(bf16[8,128,128]{2,0,1:T(8,128)(2,1)S(1)} %select_bitcast_fusion), channel_id=1, source_target_pairs={{0,3},{1,0},{2,1},{3,2},{4,7},{5,4},{6,5},{7,6},{8,11},{9,8},{10,9... | collective-permute-start | bytes 786440 | tf_op jit(solution)/shard_map/ppermute | solution.py:14
  6.1 16.5 %copy-start.4 = (bf16[1,128,128]{2,1,0:T(8,128)(2,1)S(1)}, bf16[1,128,128]{2,1,0:T(8,128)(2,1)}, u32[]{:S(2)}) copy-start(bf16[1,128,128]{2,1,0:T(8,128)(2,1)} %param.19) | copy-start | bytes 98308
  6.2 16.9 %collective-permute-start.5 = (bf16[8,128,128]{2,0,1:T(8,128)(2,1)S(1)}, bf16[8,128,128]{2,0,1:T(8,128)(2,1)S(1)}, u32[]{:S(2)}, u32[]{:S(2)}) collective-permute-start(bf16[8,128,128]{2,0,1:T(8,128)(2,1)S(1)} %get-tuple-element.86), channel_id=1, source_target_pairs={{0,2},{1,3},{2,0},{3,1},{4,6},{5,7},{6,4},{7,5},{8,10},{9,11},{10,... | collective-permute-start | bytes 786440 | tf_op jit(solution)/shard_map/ppermute | solution.py:14
  7.2 8.4 %collective-permute-start.2 = (s32[8,2]{0,1:T(2,128)S(1)}, s32[8,2]{0,1:T(2,128)S(1)}, u32[]{:S(2)}, u32[]{:S(2)}) collective-permute-start(s32[8,2]{0,1:T(2,128)S(1)} %bitcast.280), channel_id=1, source_target_pairs={{0,3},{1,0},{2,1},{3,2},{4,7},{5,4},{6,5},{7,6},{8,11},{9,8},{10,9... | collective-permute-start | bytes 200 | tf_op jit(solution)/shard_map/ppermute | solution.py:14
  7.3 9.5 %collective-permute-start.1 = (s32[8,2]{0,1:T(2,128)S(1)}, s32[8,2]{0,1:T(2,128)S(1)}, u32[]{:S(2)}, u32[]{:S(2)}) collective-permute-start(s32[8,2]{0,1:T(2,128)S(1)} %bitcast.279), channel_id=1, source_target_pairs={{0,2},{1,3},{2,0},{3,1},{4,6},{5,7},{6,4},{7,5},{8,10},{9,11},{10,... | collective-permute-start | bytes 200 | tf_op jit(solution)/shard_map/ppermute | solution.py:14
  9.2 13.6 %collective-permute-start.3 = (bf16[8,32,128]{2,0,1:T(8,128)(2,1)S(1)}, bf16[8,32,128]{2,0,1:T(8,128)(2,1)S(1)}, u32[]{:S(2)}, u32[]{:S(2)}) collective-permute-start(bf16[8,32,128]{2,0,1:T(8,128)(2,1)S(1)} %multiply_convert_fusion), channel_id=1, source_target_pairs={{0,4},{4,0},{8,12},{12,8},{16,20},{20,16},{24,28},{28,24},{1,5},{5... | collective-permute-start | bytes 196616 | tf_op jit(solution)/shard_map/ppermute | solution.py:18
  15.7 3.4 %collective-permute-start = (s32[8,2]{0,1:T(2,128)S(1)}, s32[8,2]{0,1:T(2,128)S(1)}, u32[]{:S(2)}, u32[]{:S(2)}) collective-permute-start(s32[8,2]{0,1:T(2,128)S(1)} %bitcast.278), channel_id=1, source_target_pairs={{0,1},{1,2},{2,3},{3,0},{4,5},{5,6},{6,7},{7,4},{8,9},{9,10},{10,1... | collective-permute-start | bytes 200 | tf_op jit(solution)/shard_map/ppermute | solution.py:14
  16.8 6.3 %collective-permute-start.4 = (bf16[8,128,128]{2,0,1:T(8,128)(2,1)S(1)}, bf16[8,128,128]{2,0,1:T(8,128)(2,1)S(1)}, u32[]{:S(2)}, u32[]{:S(2)}) collective-permute-start(bf16[8,128,128]{2,0,1:T(8,128)(2,1)S(1)} %get-tuple-element.85), channel_id=1, source_target_pairs={{0,1},{1,2},{2,3},{3,0},{4,5},{5,6},{6,7},{7,4},{8,9},{9,10},{10,1... | collective-permute-start | bytes 786440 | tf_op jit(solution)/shard_map/ppermute | solution.py:14
  19.1 3.6 %collective-permute-start.7 = (bf16[32,128]{1,0:T(8,128)(2,1)S(1)}, bf16[32,128]{1,0:T(8,128)(2,1)S(1)}, u32[]{:S(2)}, u32[]{:S(2)}) collective-permute-start(bf16[32,128]{1,0:T(8,128)(2,1)S(1)} %bitcast.258), channel_id=1, source_target_pairs={{0,1},{1,2},{2,3},{3,0},{4,5},{5,6},{6,7},{7,4},{8,9},{9,10},{10,1... | collective-permute-start | bytes 24584 | tf_op jit(solution)/shard_map/ppermute | solution.py:14
  25.0 4.3 %collective-permute-start.9 = (bf16[8,32,128]{2,0,1:T(8,128)(2,1)S(1)}, bf16[8,32,128]{2,0,1:T(8,128)(2,1)S(1)}, u32[]{:S(2)}, u32[]{:S(2)}) collective-permute-start(bf16[8,32,128]{2,0,1:T(8,128)(2,1)S(1)} %convolution_convert_fusion.12), channel_id=1, source_target_pairs={{0,4},{4,0},{8,12},{12,8},{16,20},{20,16},{24,28},{28,24},{1,5},{5... | collective-permute-start | bytes 196616 | tf_op jit(solution)/shard_map/ppermute | solution.py:18
  27.4 1.5 %collective-permute-start.8 = (f32[32,128]{1,0:T(8,128)S(1)}, f32[32,128]{1,0:T(8,128)S(1)}, u32[]{:S(2)}, u32[]{:S(2)}) collective-permute-start(f32[32,128]{1,0:T(8,128)S(1)} %fusion.93), channel_id=1, source_target_pairs={{0,3},{1,0},{2,1},{3,2},{4,7},{5,4},{6,5},{7,6},{8,11},{9,8},{10,9... | collective-permute-start | bytes 49160 | tf_op jit(solution)/shard_map/ppermute | solution.py:14
  44.4 4.3 %collective-permute-start.10 = (bf16[8,32,128]{2,0,1:T(8,128)(2,1)S(1)}, bf16[8,32,128]{2,0,1:T(8,128)(2,1)S(1)}, u32[]{:S(2)}, u32[]{:S(2)}) collective-permute-start(bf16[8,32,128]{2,0,1:T(8,128)(2,1)S(1)} %get-tuple-element.19), channel_id=1, source_target_pairs={{0,4},{4,0},{8,12},{12,8},{16,20},{20,16},{24,28},{28,24},{1,5},{5... | collective-permute-start | bytes 196616 | tf_op jit(solution)/shard_map/ppermute | solution.py:18
  45.2 3.1 %collective-permute-start.11 = (bf16[32,128]{1,0:T(8,128)(2,1)S(1)}, bf16[32,128]{1,0:T(8,128)(2,1)S(1)}, u32[]{:S(2)}, u32[]{:S(2)}) collective-permute-start(bf16[32,128]{1,0:T(8,128)(2,1)S(1)} %bitcast.260), channel_id=1, source_target_pairs={{0,1},{1,2},{2,3},{3,0},{4,5},{5,6},{6,7},{7,4},{8,9},{9,10},{10,1... | collective-permute-start | bytes 24584 | tf_op jit(solution)/shard_map/ppermute | solution.py:14
  52.6 4.3 %collective-permute-start.13 = (bf16[8,32,128]{2,0,1:T(8,128)(2,1)S(1)}, bf16[8,32,128]{2,0,1:T(8,128)(2,1)S(1)}, u32[]{:S(2)}, u32[]{:S(2)}) collective-permute-start(bf16[8,32,128]{2,0,1:T(8,128)(2,1)S(1)} %convolution_convert_fusion.11), channel_id=1, source_target_pairs={{0,4},{4,0},{8,12},{12,8},{16,20},{20,16},{24,28},{28,24},{1,5},{5... | collective-permute-start | bytes 196616 | tf_op jit(solution)/shard_map/ppermute | solution.py:18
  54.5 1.5 %collective-permute-start.12 = (f32[32,128]{1,0:T(8,128)S(1)}, f32[32,128]{1,0:T(8,128)S(1)}, u32[]{:S(2)}, u32[]{:S(2)}) collective-permute-start(f32[32,128]{1,0:T(8,128)S(1)} %fusion.89), channel_id=1, source_target_pairs={{0,3},{1,0},{2,1},{3,2},{4,7},{5,4},{6,5},{7,6},{8,11},{9,8},{10,9... | collective-permute-start | bytes 49160 | tf_op jit(solution)/shard_map/ppermute | solution.py:14
  68.4 4.3 %collective-permute-start.14 = (bf16[8,32,128]{2,0,1:T(8,128)(2,1)S(1)}, bf16[8,32,128]{2,0,1:T(8,128)(2,1)S(1)}, u32[]{:S(2)}, u32[]{:S(2)}) collective-permute-start(bf16[8,32,128]{2,0,1:T(8,128)(2,1)S(1)} %get-tuple-element.22), channel_id=1, source_target_pairs={{0,4},{4,0},{8,12},{12,8},{16,20},{20,16},{24,28},{28,24},{1,5},{5... | collective-permute-start | bytes 196616 | tf_op jit(solution)/shard_map/ppermute | solution.py:18
  69.2 3.3 %collective-permute-start.15 = (bf16[32,128]{1,0:T(8,128)(2,1)S(1)}, bf16[32,128]{1,0:T(8,128)(2,1)S(1)}, u32[]{:S(2)}, u32[]{:S(2)}) collective-permute-start(bf16[32,128]{1,0:T(8,128)(2,1)S(1)} %bitcast.261), channel_id=1, source_target_pairs={{0,1},{1,2},{2,3},{3,0},{4,5},{5,6},{6,7},{7,4},{8,9},{9,10},{10,1... | collective-permute-start | bytes 24584 | tf_op jit(solution)/shard_map/ppermute | solution.py:14
  76.6 4.3 %collective-permute-start.17 = (bf16[8,32,128]{2,0,1:T(8,128)(2,1)S(1)}, bf16[8,32,128]{2,0,1:T(8,128)(2,1)S(1)}, u32[]{:S(2)}, u32[]{:S(2)}) collective-permute-start(bf16[8,32,128]{2,0,1:T(8,128)(2,1)S(1)} %convolution_convert_fusion.10), channel_id=1, source_target_pairs={{0,4},{4,0},{8,12},{12,8},{16,20},{20,16},{24,28},{28,24},{1,5},{5... | collective-permute-start | bytes 196616 | tf_op jit(solution)/shard_map/ppermute | solution.py:18
  78.6 1.5 %collective-permute-start.16 = (f32[32,128]{1,0:T(8,128)S(1)}, f32[32,128]{1,0:T(8,128)S(1)}, u32[]{:S(2)}, u32[]{:S(2)}) collective-permute-start(f32[32,128]{1,0:T(8,128)S(1)} %fusion.85), channel_id=1, source_target_pairs={{0,3},{1,0},{2,1},{3,2},{4,7},{5,4},{6,5},{7,6},{8,11},{9,8},{10,9... | collective-permute-start | bytes 49160 | tf_op jit(solution)/shard_map/ppermute | solution.py:14
  92.5 4.4 %collective-permute-start.18 = (bf16[8,32,128]{2,0,1:T(8,128)(2,1)S(1)}, bf16[8,32,128]{2,0,1:T(8,128)(2,1)S(1)}, u32[]{:S(2)}, u32[]{:S(2)}) collective-permute-start(bf16[8,32,128]{2,0,1:T(8,128)(2,1)S(1)} %get-tuple-element.25), channel_id=1, source_target_pairs={{0,4},{4,0},{8,12},{12,8},{16,20},{20,16},{24,28},{28,24},{1,5},{5... | collective-permute-start | bytes 196616 | tf_op jit(solution)/shard_map/ppermute | solution.py:18
  93.7 3.1 %collective-permute-start.19 = (bf16[32,128]{1,0:T(8,128)(2,1)S(1)}, bf16[32,128]{1,0:T(8,128)(2,1)S(1)}, u32[]{:S(2)}, u32[]{:S(2)}) collective-permute-start(bf16[32,128]{1,0:T(8,128)(2,1)S(1)} %bitcast.259), channel_id=1, source_target_pairs={{0,1},{1,2},{2,3},{3,0},{4,5},{5,6},{6,7},{7,4},{8,9},{9,10},{10,1... | collective-permute-start | bytes 24584 | tf_op jit(solution)/shard_map/ppermute | solution.py:14
  100.9 4.3 %collective-permute-start.21 = (bf16[8,32,128]{2,0,1:T(8,128)(2,1)S(1)}, bf16[8,32,128]{2,0,1:T(8,128)(2,1)S(1)}, u32[]{:S(2)}, u32[]{:S(2)}) collective-permute-start(bf16[8,32,128]{2,0,1:T(8,128)(2,1)S(1)} %convolution_convert_fusion.9), channel_id=1, source_target_pairs={{0,4},{4,0},{8,12},{12,8},{16,20},{20,16},{24,28},{28,24},{1,5},{5... | collective-permute-start | bytes 196616 | tf_op jit(solution)/shard_map/ppermute | solution.py:18
  103.0 1.5 %collective-permute-start.20 = (f32[32,128]{1,0:T(8,128)S(1)}, f32[32,128]{1,0:T(8,128)S(1)}, u32[]{:S(2)}, u32[]{:S(2)}) collective-permute-start(f32[32,128]{1,0:T(8,128)S(1)} %fusion.81), channel_id=1, source_target_pairs={{0,3},{1,0},{2,1},{3,2},{4,7},{5,4},{6,5},{7,6},{8,11},{9,8},{10,9... | collective-permute-start | bytes 49160 | tf_op jit(solution)/shard_map/ppermute | solution.py:14
  103.5 13.9 %copy-start.6 = (f32[8,32,128]{2,0,1:T(8,128)S(1)}, f32[8,32,128]{2,0,1:T(8,128)}, u32[]{:S(2)}) copy-start(f32[8,32,128]{2,0,1:T(8,128)} %copy-done.5) | copy-start | bytes 393220
  (10 other events, 41.0 us)

commit v17 on v12

--- a/solution.py
+++ b/solution.py
@@ -21,7 +21,7 @@
 def total(value):
     count = lax.axis_size("dom") * lax.axis_size("rep")
     spread = jnp.broadcast_to(value[None], (count,) + value.shape)
-    gathered = lax.all_to_all(spread, ("dom", "rep"), 0, 0, tiled=True)
+    gathered = lax.all_to_all(spread, ("rep", "dom"), 0, 0, tiled=True)
     return jnp.sum(gathered, axis=0)
 
 

time: 116 us -> 115 us (level)
  no operation moved by 1% of the time
where the time goes in v17:
time: 115 us
  blocking collectives  39.3 us (34%)
  waiting for transfers between devices  24.5 us (21%)
  matrix products  24.4 us (21%)
  starting transfers between devices  15.5 us (13%)
  other arithmetic  6.67 us (6%)
  local copies, waits for them, and re-layouts  3.38 us (3%)
  between operations  1.28 us (1%)
    all_to_all x4, blocking collectives, total(): gathered = lax.all_to_all(spread, ('rep', 'dom'), 0, 0, tiled=True)  39.3 us
    ppermute x14, waiting for transfers between devices, from_behind(): return lax.ppermute(value, axis, pairs)  20.9 us
    ppermute x8, starting transfers between devices, partner(): lax.ppermute(value, axis, [(i, i ^ 1 << distance) for i in range(lax.axis...  9.07 us
    dot_general x4, matrix products, apply_operator(): jnp.einsum('srj,skj->srk', multiplier, contact_set, preferred_element_typ...  6.53 us
    ppermute x14, starting transfers between devices, from_behind(): return lax.ppermute(value, axis, pairs)  6.46 us
    ppermute x8, waiting for transfers between devices, partner(): lax.ppermute(value, axis, [(i, i ^ 1 << distance) for i in range(lax.axis...  3.6 us
    dot_general x4, matrix products, local_stiffness(): jnp.einsum('pn,prj->nrj', mirror_onehot, mirror, precision=lax.Precision....  3.19 us
    dot_general x4, matrix products, apply_operator(): jnp.einsum('sn,nrk->srk', far_onehot, other, precision=lax.Precision.HIGH...  3.17 us
  transfers between devices with their start and end apart: 22, of which 16 were waited for; matrix products, arithmetic and copies ran while one was open for 8% of the time, Pallas kernels for 0%

profile of v17, /device:TPU:0, one launch (start us, length us, event | category | flops | bytes accessed | tf_op | source)
XLA Modules:
  0.0 115.1 jit_solution(4958765631506618803)
XLA Ops:
  3.7 2.4 %collective-permute-start.6 = (bf16[8,128,128]{2,0,1:T(8,128)(2,1)S(1)}, bf16[8,128,128]{2,0,1:T(8,128)(2,1)S(1)}, u32[]{:S(2)}, u32[]{:S(2)}) collective-permute-start(bf16[8,128,128]{2,0,1:T(8,128)(2,1)S(1)} %select_bitcast_fusion), channel_id=1, source_target_pairs={{0,3},{1,0},{2,1},{3,2},{4,7},{5,4},{6,5},{7,6},{8,11},{9,8},{10,9... | collective-permute-start | bytes 786440 | tf_op jit(solution)/shard_map/ppermute | solution.py:14
  7.3 1.7 %collective-permute-start.1 = (s32[8,2]{0,1:T(2,128)S(1)}, s32[8,2]{0,1:T(2,128)S(1)}, u32[]{:S(2)}, u32[]{:S(2)}) collective-permute-start(s32[8,2]{0,1:T(2,128)S(1)} %bitcast.330), channel_id=1, source_target_pairs={{0,2},{1,3},{2,0},{3,1},{4,6},{5,7},{6,4},{7,5},{8,10},{9,11},{10,... | collective-permute-start | bytes 200 | tf_op jit(solution)/shard_map/ppermute | solution.py:14
  9.2 1.6 %collective-permute-start.3 = (bf16[8,32,128]{2,0,1:T(8,128)(2,1)S(1)}, bf16[8,32,128]{2,0,1:T(8,128)(2,1)S(1)}, u32[]{:S(2)}, u32[]{:S(2)}) collective-permute-start(bf16[8,32,128]{2,0,1:T(8,128)(2,1)S(1)} %multiply_convert_fusion), channel_id=1, source_target_pairs={{0,4},{4,0},{8,12},{12,8},{16,20},{20,16},{24,28},{28,24},{1,5},{5... | collective-permute-start | bytes 196616 | tf_op jit(solution)/shard_map/ppermute | solution.py:18
  11.1 4.6 %collective-permute-done.2 = s32[8,2]{0,1:T(2,128)S(1)} collective-permute-done((s32[8,2]{0,1:T(2,128)S(1)}, s32[8,2]{0,1:T(2,128)S(1)}, u32[]{:S(2)}, u32[]{:S(2)}) %collective-permute-start.2) | collective-permute-done | bytes 96 | tf_op jit(solution)/shard_map/ppermute | solution.py:14
  15.7 1.1 collective-permute-start
  16.8 2.3 %collective-permute-done = s32[8,2]{0,1:T(2,128)S(1)} collective-permute-done((s32[8,2]{0,1:T(2,128)S(1)}, s32[8,2]{0,1:T(2,128)S(1)}, u32[]{:S(2)}, u32[]{:S(2)}) %collective-permute-start) | collective-permute-done | bytes 96 | tf_op jit(solution)/shard_map/ppermute | solution.py:14
  19.6 3.0 %collective-permute-done.7 = bf16[32,128]{1,0:T(8,128)(2,1)S(1)} collective-permute-done((bf16[32,128]{1,0:T(8,128)(2,1)S(1)}, bf16[32,128]{1,0:T(8,128)(2,1)S(1)}, u32[]{:S(2)}, u32[]{:S(2)}) %collective-permute-start.7) | collective-permute-done | bytes 8224 | tf_op jit(solution)/shard_map/ppermute | solution.py:14
  25.0 1.6 %collective-permute-start.9 = (bf16[8,32,128]{2,0,1:T(8,128)(2,1)S(1)}, bf16[8,32,128]{2,0,1:T(8,128)(2,1)S(1)}, u32[]{:S(2)}, u32[]{:S(2)}) collective-permute-start(bf16[8,32,128]{2,0,1:T(8,128)(2,1)S(1)} %convolution_convert_fusion.12), channel_id=1, source_target_pairs={{0,4},{4,0},{8,12},{12,8},{16,20},{20,16},{24,28},{28,24},{1,5},{5... | collective-permute-start | bytes 196616 | tf_op jit(solution)/shard_map/ppermute | solution.py:18
  30.3 12.7 %all_to_all.20 = f32[32,1,128]{2,1,0:T(1,128)S(1)} all-to-all(f32[32,1,128]{2,1,0:T(1,128)S(1)} %reshape.371), channel_id=1, replica_groups=mesh['dom'=8,'rep'=4] {'rep','dom'}, dimensions={0} | all-to-all | bytes 32768 | tf_op jit(solution)/shard_map/all_to_all | solution.py:24
  45.8 2.7 %collective-permute-done.11 = bf16[32,128]{1,0:T(8,128)(2,1)S(1)} collective-permute-done((bf16[32,128]{1,0:T(8,128)(2,1)S(1)}, bf16[32,128]{1,0:T(8,128)(2,1)S(1)}, u32[]{:S(2)}, u32[]{:S(2)}) %collective-permute-start.11) | collective-permute-done | bytes 8224 | tf_op jit(solution)/shard_map/ppermute | solution.py:14
  48.9 1.0 fusion.2
  49.9 1.9 %fusion.6 = f32[32,32,128]{2,1,0:T(8,128)S(1)} fusion(bf16[32,128,128]{2,1,0:T(8,128)(2,1)S(1)} %bitcast.283, bf16[32,32,128]{2,0,1:T(8,128)(2,1)} %fusion.2), kind=kOutput, calls=%fused_computation.15 | convolution fusion | flops 67239936 | bytes 1835008 | tf_op jit(solution)/shard_map/srj,skj->srk/dot_general | solution.py:54
  52.8 1.1 collective-permute-start.13
  56.1 1.0 collective-permute-done.13
  58.1 8.8 %all_to_all.21 = f32[32,1,128]{2,1,0:T(1,128)S(1)} all-to-all(f32[32,1,128]{2,1,0:T(1,128)S(1)} %reshape.373), channel_id=1, replica_groups=mesh['dom'=8,'rep'=4] {'rep','dom'}, dimensions={0} | all-to-all | bytes 32768 | tf_op jit(solution)/shard_map/all_to_all | solution.py:24
  69.3 2.6 %collective-permute-done.15 = bf16[32,128]{1,0:T(8,128)(2,1)S(1)} collective-permute-done((bf16[32,128]{1,0:T(8,128)(2,1)S(1)}, bf16[32,128]{1,0:T(8,128)(2,1)S(1)}, u32[]{:S(2)}, u32[]{:S(2)}) %collective-permute-start.15) | collective-permute-done | bytes 8224 | tf_op jit(solution)/shard_map/ppermute | solution.py:14
  73.2 1.9 %fusion.7 = f32[32,32,128]{2,1,0:T(8,128)S(1)} fusion(bf16[32,128,128]{2,1,0:T(8,128)(2,1)S(1)} %bitcast.284, bf16[32,32,128]{2,0,1:T(8,128)(2,1)} %fusion.3), kind=kOutput, calls=%fused_computation.16 | convolution fusion | flops 67239936 | bytes 1835008 | tf_op jit(solution)/shard_map/srj,skj->srk/dot_general | solution.py:54
  76.1 1.3 %collective-permute-start.17 = (bf16[8,32,128]{2,0,1:T(8,128)(2,1)S(1)}, bf16[8,32,128]{2,0,1:T(8,128)(2,1)S(1)}, u32[]{:S(2)}, u32[]{:S(2)}) collective-permute-start(bf16[8,32,128]{2,0,1:T(8,128)(2,1)S(1)} %convolution_convert_fusion.10), channel_id=1, source_target_pairs={{0,4},{4,0},{8,12},{12,8},{16,20},{20,16},{24,28},{28,24},{1,5},{5... | collective-permute-start | bytes 196616 | tf_op jit(solution)/shard_map/ppermute | solution.py:18
  81.4 8.8 %all_to_all.22 = f32[32,1,128]{2,1,0:T(1,128)S(1)} all-to-all(f32[32,1,128]{2,1,0:T(1,128)S(1)} %reshape.375), channel_id=1, replica_groups=mesh['dom'=8,'rep'=4] {'rep','dom'}, dimensions={0} | all-to-all | bytes 32768 | tf_op jit(solution)/shard_map/all_to_all | solution.py:24
  93.2 2.2 %collective-permute-done.19 = bf16[32,128]{1,0:T(8,128)(2,1)S(1)} collective-permute-done((bf16[32,128]{1,0:T(8,128)(2,1)S(1)}, bf16[32,128]{1,0:T(8,128)(2,1)S(1)}, u32[]{:S(2)}, u32[]{:S(2)}) %collective-permute-start.19) | collective-permute-done | bytes 8224 | tf_op jit(solution)/shard_map/ppermute | solution.py:14
  95.6 1.0 fusion.4
  96.5 1.9 %fusion.8 = f32[32,32,128]{2,1,0:T(8,128)S(1)} fusion(bf16[32,128,128]{2,1,0:T(8,128)(2,1)S(1)} %bitcast.285, bf16[32,32,128]{2,0,1:T(8,128)(2,1)} %fusion.4), kind=kOutput, calls=%fused_computation.17 | convolution fusion | flops 67239936 | bytes 1835008 | tf_op jit(solution)/shard_map/srj,skj->srk/dot_general | solution.py:54
  99.4 1.5 %collective-permute-start.21 = (bf16[8,32,128]{2,0,1:T(8,128)(2,1)S(1)}, bf16[8,32,128]{2,0,1:T(8,128)(2,1)S(1)}, u32[]{:S(2)}, u32[]{:S(2)}) collective-permute-start(bf16[8,32,128]{2,0,1:T(8,128)(2,1)S(1)} %convolution_convert_fusion.9), channel_id=1, source_target_pairs={{0,4},{4,0},{8,12},{12,8},{16,20},{20,16},{24,28},{28,24},{1,5},{5... | collective-permute-start | bytes 196616 | tf_op jit(solution)/shard_map/ppermute | solution.py:18
  104.6 8.9 %all_to_all.23 = f32[32,2,32]{2,1,0:T(2,128)S(1)} all-to-all(f32[32,2,32]{2,1,0:T(2,128)S(1)} %broadcast_in_dim.115), channel_id=1, replica_groups=mesh['dom'=8,'rep'=4] {'rep','dom'}, dimensions={0} | all-to-all | bytes 16384 | tf_op jit(solution)/shard_map/all_to_all | solution.py:24
  (164 shorter events, 36.2 us)
Async XLA Ops:
  3.7 19.4 %collective-permute-start.6 = (bf16[8,128,128]{2,0,1:T(8,128)(2,1)S(1)}, bf16[8,128,128]{2,0,1:T(8,128)(2,1)S(1)}, u32[]{:S(2)}, u32[]{:S(2)}) collective-permute-start(bf16[8,128,128]{2,0,1:T(8,128)(2,1)S(1)} %select_bitcast_fusion), channel_id=1, source_target_pairs={{0,3},{1,0},{2,1},{3,2},{4,7},{5,4},{6,5},{7,6},{8,11},{9,8},{10,9... | collective-permute-start | bytes 786440 | tf_op jit(solution)/shard_map/ppermute | solution.py:14
  6.1 16.5 %copy-start.4 = (bf16[1,128,128]{2,1,0:T(8,128)(2,1)S(1)}, bf16[1,128,128]{2,1,0:T(8,128)(2,1)}, u32[]{:S(2)}) copy-start(bf16[1,128,128]{2,1,0:T(8,128)(2,1)} %param.19) | copy-start | bytes 98308
  6.2 16.9 %collective-permute-start.5 = (bf16[8,128,128]{2,0,1:T(8,128)(2,1)S(1)}, bf16[8,128,128]{2,0,1:T(8,128)(2,1)S(1)}, u32[]{:S(2)}, u32[]{:S(2)}) collective-permute-start(bf16[8,128,128]{2,0,1:T(8,128)(2,1)S(1)} %get-tuple-element.86), channel_id=1, source_target_pairs={{0,2},{1,3},{2,0},{3,1},{4,6},{5,7},{6,4},{7,5},{8,10},{9,11},{10,... | collective-permute-start | bytes 786440 | tf_op jit(solution)/shard_map/ppermute | solution.py:14
  7.2 8.4 %collective-permute-start.2 = (s32[8,2]{0,1:T(2,128)S(1)}, s32[8,2]{0,1:T(2,128)S(1)}, u32[]{:S(2)}, u32[]{:S(2)}) collective-permute-start(s32[8,2]{0,1:T(2,128)S(1)} %bitcast.331), channel_id=1, source_target_pairs={{0,3},{1,0},{2,1},{3,2},{4,7},{5,4},{6,5},{7,6},{8,11},{9,8},{10,9... | collective-permute-start | bytes 200 | tf_op jit(solution)/shard_map/ppermute | solution.py:14
  7.3 9.5 %collective-permute-start.1 = (s32[8,2]{0,1:T(2,128)S(1)}, s32[8,2]{0,1:T(2,128)S(1)}, u32[]{:S(2)}, u32[]{:S(2)}) collective-permute-start(s32[8,2]{0,1:T(2,128)S(1)} %bitcast.330), channel_id=1, source_target_pairs={{0,2},{1,3},{2,0},{3,1},{4,6},{5,7},{6,4},{7,5},{8,10},{9,11},{10,... | collective-permute-start | bytes 200 | tf_op jit(solution)/shard_map/ppermute | solution.py:14
  9.2 13.6 %collective-permute-start.3 = (bf16[8,32,128]{2,0,1:T(8,128)(2,1)S(1)}, bf16[8,32,128]{2,0,1:T(8,128)(2,1)S(1)}, u32[]{:S(2)}, u32[]{:S(2)}) collective-permute-start(bf16[8,32,128]{2,0,1:T(8,128)(2,1)S(1)} %multiply_convert_fusion), channel_id=1, source_target_pairs={{0,4},{4,0},{8,12},{12,8},{16,20},{20,16},{24,28},{28,24},{1,5},{5... | collective-permute-start | bytes 196616 | tf_op jit(solution)/shard_map/ppermute | solution.py:18
  15.7 3.4 %collective-permute-start = (s32[8,2]{0,1:T(2,128)S(1)}, s32[8,2]{0,1:T(2,128)S(1)}, u32[]{:S(2)}, u32[]{:S(2)}) collective-permute-start(s32[8,2]{0,1:T(2,128)S(1)} %bitcast.329), channel_id=1, source_target_pairs={{0,1},{1,2},{2,3},{3,0},{4,5},{5,6},{6,7},{7,4},{8,9},{9,10},{10,1... | collective-permute-start | bytes 200 | tf_op jit(solution)/shard_map/ppermute | solution.py:14
  16.8 6.3 %collective-permute-start.4 = (bf16[8,128,128]{2,0,1:T(8,128)(2,1)S(1)}, bf16[8,128,128]{2,0,1:T(8,128)(2,1)S(1)}, u32[]{:S(2)}, u32[]{:S(2)}) collective-permute-start(bf16[8,128,128]{2,0,1:T(8,128)(2,1)S(1)} %get-tuple-element.85), channel_id=1, source_target_pairs={{0,1},{1,2},{2,3},{3,0},{4,5},{5,6},{6,7},{7,4},{8,9},{9,10},{10,1... | collective-permute-start | bytes 786440 | tf_op jit(solution)/shard_map/ppermute | solution.py:14
  19.1 3.6 %collective-permute-start.7 = (bf16[32,128]{1,0:T(8,128)(2,1)S(1)}, bf16[32,128]{1,0:T(8,128)(2,1)S(1)}, u32[]{:S(2)}, u32[]{:S(2)}) collective-permute-start(bf16[32,128]{1,0:T(8,128)(2,1)S(1)} %bitcast.309), channel_id=1, source_target_pairs={{0,1},{1,2},{2,3},{3,0},{4,5},{5,6},{6,7},{7,4},{8,9},{9,10},{10,1... | collective-permute-start | bytes 24584 | tf_op jit(solution)/shard_map/ppermute | solution.py:14
  25.0 4.3 %collective-permute-start.9 = (bf16[8,32,128]{2,0,1:T(8,128)(2,1)S(1)}, bf16[8,32,128]{2,0,1:T(8,128)(2,1)S(1)}, u32[]{:S(2)}, u32[]{:S(2)}) collective-permute-start(bf16[8,32,128]{2,0,1:T(8,128)(2,1)S(1)} %convolution_convert_fusion.12), channel_id=1, source_target_pairs={{0,4},{4,0},{8,12},{12,8},{16,20},{20,16},{24,28},{28,24},{1,5},{5... | collective-permute-start | bytes 196616 | tf_op jit(solution)/shard_map/ppermute | solution.py:18
  27.4 1.5 %collective-permute-start.8 = (f32[32,128]{1,0:T(8,128)S(1)}, f32[32,128]{1,0:T(8,128)S(1)}, u32[]{:S(2)}, u32[]{:S(2)}) collective-permute-start(f32[32,128]{1,0:T(8,128)S(1)} %fusion.93), channel_id=1, source_target_pairs={{0,3},{1,0},{2,1},{3,2},{4,7},{5,4},{6,5},{7,6},{8,11},{9,8},{10,9... | collective-permute-start | bytes 49160 | tf_op jit(solution)/shard_map/ppermute | solution.py:14
  44.6 4.3 %collective-permute-start.10 = (bf16[8,32,128]{2,0,1:T(8,128)(2,1)S(1)}, bf16[8,32,128]{2,0,1:T(8,128)(2,1)S(1)}, u32[]{:S(2)}, u32[]{:S(2)}) collective-permute-start(bf16[8,32,128]{2,0,1:T(8,128)(2,1)S(1)} %get-tuple-element.19), channel_id=1, source_target_pairs={{0,4},{4,0},{8,12},{12,8},{16,20},{20,16},{24,28},{28,24},{1,5},{5... | collective-permute-start | bytes 196616 | tf_op jit(solution)/shard_map/ppermute | solution.py:18
  45.3 3.1 %collective-permute-start.11 = (bf16[32,128]{1,0:T(8,128)(2,1)S(1)}, bf16[32,128]{1,0:T(8,128)(2,1)S(1)}, u32[]{:S(2)}, u32[]{:S(2)}) collective-permute-start(bf16[32,128]{1,0:T(8,128)(2,1)S(1)} %bitcast.311), channel_id=1, source_target_pairs={{0,1},{1,2},{2,3},{3,0},{4,5},{5,6},{6,7},{7,4},{8,9},{9,10},{10,1... | collective-permute-start | bytes 24584 | tf_op jit(solution)/shard_map/ppermute | solution.py:14
  52.8 4.3 %collective-permute-start.13 = (bf16[8,32,128]{2,0,1:T(8,128)(2,1)S(1)}, bf16[8,32,128]{2,0,1:T(8,128)(2,1)S(1)}, u32[]{:S(2)}, u32[]{:S(2)}) collective-permute-start(bf16[8,32,128]{2,0,1:T(8,128)(2,1)S(1)} %convolution_convert_fusion.11), channel_id=1, source_target_pairs={{0,4},{4,0},{8,12},{12,8},{16,20},{20,16},{24,28},{28,24},{1,5},{5... | collective-permute-start | bytes 196616 | tf_op jit(solution)/shard_map/ppermute | solution.py:18
  54.6 1.5 %collective-permute-start.12 = (f32[32,128]{1,0:T(8,128)S(1)}, f32[32,128]{1,0:T(8,128)S(1)}, u32[]{:S(2)}, u32[]{:S(2)}) collective-permute-start(f32[32,128]{1,0:T(8,128)S(1)} %fusion.89), channel_id=1, source_target_pairs={{0,3},{1,0},{2,1},{3,2},{4,7},{5,4},{6,5},{7,6},{8,11},{9,8},{10,9... | collective-permute-start | bytes 49160 | tf_op jit(solution)/shard_map/ppermute | solution.py:14
  67.9 4.3 %collective-permute-start.14 = (bf16[8,32,128]{2,0,1:T(8,128)(2,1)S(1)}, bf16[8,32,128]{2,0,1:T(8,128)(2,1)S(1)}, u32[]{:S(2)}, u32[]{:S(2)}) collective-permute-start(bf16[8,32,128]{2,0,1:T(8,128)(2,1)S(1)} %get-tuple-element.22), channel_id=1, source_target_pairs={{0,4},{4,0},{8,12},{12,8},{16,20},{20,16},{24,28},{28,24},{1,5},{5... | collective-permute-start | bytes 196616 | tf_op jit(solution)/shard_map/ppermute | solution.py:18
  68.6 3.3 %collective-permute-start.15 = (bf16[32,128]{1,0:T(8,128)(2,1)S(1)}, bf16[32,128]{1,0:T(8,128)(2,1)S(1)}, u32[]{:S(2)}, u32[]{:S(2)}) collective-permute-start(bf16[32,128]{1,0:T(8,128)(2,1)S(1)} %bitcast.312), channel_id=1, source_target_pairs={{0,1},{1,2},{2,3},{3,0},{4,5},{5,6},{6,7},{7,4},{8,9},{9,10},{10,1... | collective-permute-start | bytes 24584 | tf_op jit(solution)/shard_map/ppermute | solution.py:14
  76.1 4.3 %collective-permute-start.17 = (bf16[8,32,128]{2,0,1:T(8,128)(2,1)S(1)}, bf16[8,32,128]{2,0,1:T(8,128)(2,1)S(1)}, u32[]{:S(2)}, u32[]{:S(2)}) collective-permute-start(bf16[8,32,128]{2,0,1:T(8,128)(2,1)S(1)} %convolution_convert_fusion.10), channel_id=1, source_target_pairs={{0,4},{4,0},{8,12},{12,8},{16,20},{20,16},{24,28},{28,24},{1,5},{5... | collective-permute-start | bytes 196616 | tf_op jit(solution)/shard_map/ppermute | solution.py:18
  78.1 1.5 %collective-permute-start.16 = (f32[32,128]{1,0:T(8,128)S(1)}, f32[32,128]{1,0:T(8,128)S(1)}, u32[]{:S(2)}, u32[]{:S(2)}) collective-permute-start(f32[32,128]{1,0:T(8,128)S(1)} %fusion.85), channel_id=1, source_target_pairs={{0,3},{1,0},{2,1},{3,2},{4,7},{5,4},{6,5},{7,6},{8,11},{9,8},{10,9... | collective-permute-start | bytes 49160 | tf_op jit(solution)/shard_map/ppermute | solution.py:14
  91.2 4.4 %collective-permute-start.18 = (bf16[8,32,128]{2,0,1:T(8,128)(2,1)S(1)}, bf16[8,32,128]{2,0,1:T(8,128)(2,1)S(1)}, u32[]{:S(2)}, u32[]{:S(2)}) collective-permute-start(bf16[8,32,128]{2,0,1:T(8,128)(2,1)S(1)} %get-tuple-element.25), channel_id=1, source_target_pairs={{0,4},{4,0},{8,12},{12,8},{16,20},{20,16},{24,28},{28,24},{1,5},{5... | collective-permute-start | bytes 196616 | tf_op jit(solution)/shard_map/ppermute | solution.py:18
  92.3 3.1 %collective-permute-start.19 = (bf16[32,128]{1,0:T(8,128)(2,1)S(1)}, bf16[32,128]{1,0:T(8,128)(2,1)S(1)}, u32[]{:S(2)}, u32[]{:S(2)}) collective-permute-start(bf16[32,128]{1,0:T(8,128)(2,1)S(1)} %bitcast.310), channel_id=1, source_target_pairs={{0,1},{1,2},{2,3},{3,0},{4,5},{5,6},{6,7},{7,4},{8,9},{9,10},{10,1... | collective-permute-start | bytes 24584 | tf_op jit(solution)/shard_map/ppermute | solution.py:14
  99.4 4.3 %collective-permute-start.21 = (bf16[8,32,128]{2,0,1:T(8,128)(2,1)S(1)}, bf16[8,32,128]{2,0,1:T(8,128)(2,1)S(1)}, u32[]{:S(2)}, u32[]{:S(2)}) collective-permute-start(bf16[8,32,128]{2,0,1:T(8,128)(2,1)S(1)} %convolution_convert_fusion.9), channel_id=1, source_target_pairs={{0,4},{4,0},{8,12},{12,8},{16,20},{20,16},{24,28},{28,24},{1,5},{5... | collective-permute-start | bytes 196616 | tf_op jit(solution)/shard_map/ppermute | solution.py:18
  101.6 1.5 %collective-permute-start.20 = (f32[32,128]{1,0:T(8,128)S(1)}, f32[32,128]{1,0:T(8,128)S(1)}, u32[]{:S(2)}, u32[]{:S(2)}) collective-permute-start(f32[32,128]{1,0:T(8,128)S(1)} %fusion.81), channel_id=1, source_target_pairs={{0,3},{1,0},{2,1},{3,2},{4,7},{5,4},{6,5},{7,6},{8,11},{9,8},{10,9... | collective-permute-start | bytes 49160 | tf_op jit(solution)/shard_map/ppermute | solution.py:14
  101.9 11.6 %copy-start.6 = (f32[8,32,128]{2,0,1:T(8,128)S(1)}, f32[8,32,128]{2,0,1:T(8,128)}, u32[]{:S(2)}) copy-start(f32[8,32,128]{2,0,1:T(8,128)} %copy-done.5) | copy-start | bytes 393220
  (10 other events, 40.8 us)

commit v18 on v12

--- a/solution.py
+++ b/solution.py
@@ -43,7 +43,6 @@
     cols_onehot, mirror_onehot, near_onehot, far_onehot, near_collect, far_collect = tables
     nodes = vector.shape[0]
     rounded = vector.astype(jnp.bfloat16)
-    before = from_behind(rounded[nodes - 1], "rep", 1)
     other = partner(rounded, "dom", 0).astype(vector.dtype)
     near = jnp.einsum("sn,nrk->srk", near_onehot, vector, precision=lax.Precision.HIGHEST)
     far = jnp.einsum("sn,nrk->srk", far_onehot, other, precision=lax.Precision.HIGHEST)
@@ -61,6 +60,7 @@
         rounded[0], link_tile, (((1,), (1,)), ((), ())), preferred_element_type=jnp.float32
     )
     after = from_behind(back_term, "rep", -1)
+    before = from_behind(rounded[nodes - 1], "rep", 1)
     result = local_stiffness(rounded, diag_tiles, off_tiles, cols_onehot, mirror_onehot)
     first_add = jnp.dot(before, link_tile, preferred_element_type=jnp.float32)
     ends = jnp.concatenate(

time: 116 us -> 118 us (1.017)
  waiting for transfers between devices: 24.6 us -> 28.2 us
    ppermute x8, waiting for transfers between devices: 3.69 us -> 11.7 us  [partner(): lax.ppermute(value, axis, [(i, i ^ 1 << distance) for i in range(lax.axis...]
    ppermute x14, waiting for transfers between devices: 20.9 us -> 16.5 us  [from_behind(): return lax.ppermute(value, axis, pairs)]
    ppermute x14, starting transfers between devices: 6.46 us -> 9.77 us  [from_behind(): return lax.ppermute(value, axis, pairs)]
    ppermute x8, starting transfers between devices: 8.92 us -> 6.21 us  [partner(): lax.ppermute(value, axis, [(i, i ^ 1 << distance) for i in range(lax.axis...]
  transfers between devices with their start and end apart: 22 -> 22, of which waited for: 16 -> 10; matrix products, arithmetic and copies ran while one was open for 8% -> 7% of each run, Pallas kernels for 0% -> 0%
where the time goes in v18:
time: 118 us
  blocking collectives  38.4 us (33%)
  waiting for transfers between devices  28.2 us (24%)
  matrix products  24.4 us (21%)
  starting transfers between devices  16 us (14%)
  other arithmetic  6.15 us (5%)
  local copies, waits for them, and re-layouts  3.4 us (3%)
  between operations  1.25 us (1%)
    all_to_all x4, blocking collectives, total(): gathered = lax.all_to_all(spread, ('dom', 'rep'), 0, 0, tiled=True)  38.4 us
    ppermute x14, waiting for transfers between devices, from_behind(): return lax.ppermute(value, axis, pairs)  16.5 us
    ppermute x8, waiting for transfers between devices, partner(): lax.ppermute(value, axis, [(i, i ^ 1 << distance) for i in range(lax.axis...  11.7 us
    ppermute x14, starting transfers between devices, from_behind(): return lax.ppermute(value, axis, pairs)  9.77 us
    dot_general x4, matrix products, apply_operator(): jnp.einsum('srj,skj->srk', multiplier, contact_set, preferred_element_typ...  6.53 us
    ppermute x8, starting transfers between devices, partner(): lax.ppermute(value, axis, [(i, i ^ 1 << distance) for i in range(lax.axis...  6.21 us
    dot_general x4, matrix products, local_stiffness(): jnp.einsum('pn,prj->nrj', mirror_onehot, mirror, precision=lax.Precision....  3.23 us
    dot_general x4, matrix products, apply_operator(): jnp.einsum('sn,nrk->srk', far_onehot, other, precision=lax.Precision.HIGH...  3.16 us
  transfers between devices with their start and end apart: 22, of which 10 were waited for; matrix products, arithmetic and copies ran while one was open for 7% of the time, Pallas kernels for 0%

profile of v18, /device:TPU:0, one launch (start us, length us, event | category | flops | bytes accessed | tf_op | source)
XLA Modules:
  0.0 117.7 jit_solution(9437164599382781444)
XLA Ops:
  3.7 2.4 %collective-permute-start.6 = (bf16[8,128,128]{2,0,1:T(8,128)(2,1)S(1)}, bf16[8,128,128]{2,0,1:T(8,128)(2,1)S(1)}, u32[]{:S(2)}, u32[]{:S(2)}) collective-permute-start(bf16[8,128,128]{2,0,1:T(8,128)(2,1)S(1)} %select_bitcast_fusion), channel_id=1, source_target_pairs={{0,3},{1,0},{2,1},{3,2},{4,7},{5,4},{6,5},{7,6},{8,11},{9,8},{10,9... | collective-permute-start | bytes 786440 | tf_op jit(solution)/shard_map/ppermute | solution.py:14
  7.4 1.6 %collective-permute-start.2 = (s32[8,2]{0,1:T(2,128)S(1)}, s32[8,2]{0,1:T(2,128)S(1)}, u32[]{:S(2)}, u32[]{:S(2)}) collective-permute-start(s32[8,2]{0,1:T(2,128)S(1)} %bitcast.331), channel_id=1, source_target_pairs={{0,3},{1,0},{2,1},{3,2},{4,7},{5,4},{6,5},{7,6},{8,11},{9,8},{10,9... | collective-permute-start | bytes 200 | tf_op jit(solution)/shard_map/ppermute | solution.py:14
  9.0 1.4 %collective-permute-start.1 = (s32[8,2]{0,1:T(2,128)S(1)}, s32[8,2]{0,1:T(2,128)S(1)}, u32[]{:S(2)}, u32[]{:S(2)}) collective-permute-start(s32[8,2]{0,1:T(2,128)S(1)} %bitcast.330), channel_id=1, source_target_pairs={{0,2},{1,3},{2,0},{3,1},{4,6},{5,7},{6,4},{7,5},{8,10},{9,11},{10,... | collective-permute-start | bytes 200 | tf_op jit(solution)/shard_map/ppermute | solution.py:14
  10.8 7.4 %collective-permute-done.2 = s32[8,2]{0,1:T(2,128)S(1)} collective-permute-done((s32[8,2]{0,1:T(2,128)S(1)}, s32[8,2]{0,1:T(2,128)S(1)}, u32[]{:S(2)}, u32[]{:S(2)}) %collective-permute-start.2) | collective-permute-done | bytes 96 | tf_op jit(solution)/shard_map/ppermute | solution.py:14
  18.2 1.4 %collective-permute-start = (s32[8,2]{0,1:T(2,128)S(1)}, s32[8,2]{0,1:T(2,128)S(1)}, u32[]{:S(2)}, u32[]{:S(2)}) collective-permute-start(s32[8,2]{0,1:T(2,128)S(1)} %bitcast.329), channel_id=1, source_target_pairs={{0,1},{1,2},{2,3},{3,0},{4,5},{5,6},{6,7},{7,4},{8,9},{9,10},{10,1... | collective-permute-start | bytes 200 | tf_op jit(solution)/shard_map/ppermute | solution.py:14
  19.6 1.3 %collective-permute-start.3 = (bf16[8,32,128]{2,0,1:T(8,128)(2,1)S(1)}, bf16[8,32,128]{2,0,1:T(8,128)(2,1)S(1)}, u32[]{:S(2)}, u32[]{:S(2)}) collective-permute-start(bf16[8,32,128]{2,0,1:T(8,128)(2,1)S(1)} %multiply_convert_fusion), channel_id=1, source_target_pairs={{0,4},{4,0},{8,12},{12,8},{16,20},{20,16},{24,28},{28,24},{1,5},{5... | collective-permute-start | bytes 196616 | tf_op jit(solution)/shard_map/ppermute | solution.py:18
  22.2 1.7 %collective-permute-done.3 = bf16[8,32,128]{2,0,1:T(8,128)(2,1)S(1)} collective-permute-done((bf16[8,32,128]{2,0,1:T(8,128)(2,1)S(1)}, bf16[8,32,128]{2,0,1:T(8,128)(2,1)S(1)}, u32[]{:S(2)}, u32[]{:S(2)}) %collective-permute-start.3) | collective-permute-done | bytes 65568 | tf_op jit(solution)/shard_map/ppermute | solution.py:18
  26.1 1.4 %collective-permute-start.9 = (bf16[8,32,128]{2,0,1:T(8,128)(2,1)S(1)}, bf16[8,32,128]{2,0,1:T(8,128)(2,1)S(1)}, u32[]{:S(2)}, u32[]{:S(2)}) collective-permute-start(bf16[8,32,128]{2,0,1:T(8,128)(2,1)S(1)} %convolution_convert_fusion.12), channel_id=1, source_target_pairs={{0,4},{4,0},{8,12},{12,8},{16,20},{20,16},{24,28},{28,24},{1,5},{5... | collective-permute-start | bytes 196616 | tf_op jit(solution)/shard_map/ppermute | solution.py:18
  29.7 1.9 %collective-permute-done.7 = bf16[32,128]{1,0:T(8,128)(2,1)S(1)} collective-permute-done((bf16[32,128]{1,0:T(8,128)(2,1)S(1)}, bf16[32,128]{1,0:T(8,128)(2,1)S(1)}, u32[]{:S(2)}, u32[]{:S(2)}) %collective-permute-start.7) | collective-permute-done | bytes 8224 | tf_op jit(solution)/shard_map/ppermute | solution.py:14
  32.6 11.6 %all_to_all.20 = f32[32,1,128]{2,1,0:T(1,128)S(1)} all-to-all(f32[32,1,128]{2,1,0:T(1,128)S(1)} %reshape.371), channel_id=1, replica_groups=mesh['dom'=8,'rep'=4] {'dom','rep'}, dimensions={0} | all-to-all | bytes 32768 | tf_op jit(solution)/shard_map/all_to_all | solution.py:24
  46.8 3.3 %collective-permute-done.10 = bf16[8,32,128]{2,0,1:T(8,128)(2,1)S(1)} collective-permute-done((bf16[8,32,128]{2,0,1:T(8,128)(2,1)S(1)}, bf16[8,32,128]{2,0,1:T(8,128)(2,1)S(1)}, u32[]{:S(2)}, u32[]{:S(2)}) %collective-permute-start.10) | collective-permute-done | bytes 65568 | tf_op jit(solution)/shard_map/ppermute | solution.py:18
  50.1 1.0 fusion.2
  51.1 1.9 %fusion.6 = f32[32,32,128]{2,1,0:T(8,128)S(1)} fusion(bf16[32,128,128]{2,1,0:T(8,128)(2,1)S(1)} %bitcast.283, bf16[32,32,128]{2,0,1:T(8,128)(2,1)} %fusion.2), kind=kOutput, calls=%fused_computation.15 | convolution fusion | flops 67239936 | bytes 1835008 | tf_op jit(solution)/shard_map/srj,skj->srk/dot_general | solution.py:53
  56.3 2.1 %collective-permute-done.11 = bf16[32,128]{1,0:T(8,128)(2,1)S(1)} collective-permute-done((bf16[32,128]{1,0:T(8,128)(2,1)S(1)}, bf16[32,128]{1,0:T(8,128)(2,1)S(1)}, u32[]{:S(2)}, u32[]{:S(2)}) %collective-permute-start.11) | collective-permute-done | bytes 8224 | tf_op jit(solution)/shard_map/ppermute | solution.py:14
  59.6 8.9 %all_to_all.21 = f32[32,1,128]{2,1,0:T(1,128)S(1)} all-to-all(f32[32,1,128]{2,1,0:T(1,128)S(1)} %reshape.373), channel_id=1, replica_groups=mesh['dom'=8,'rep'=4] {'dom','rep'}, dimensions={0} | all-to-all | bytes 32768 | tf_op jit(solution)/shard_map/all_to_all | solution.py:24
  70.5 3.3 %collective-permute-done.14 = bf16[8,32,128]{2,0,1:T(8,128)(2,1)S(1)} collective-permute-done((bf16[8,32,128]{2,0,1:T(8,128)(2,1)S(1)}, bf16[8,32,128]{2,0,1:T(8,128)(2,1)S(1)}, u32[]{:S(2)}, u32[]{:S(2)}) %collective-permute-start.14) | collective-permute-done | bytes 65568 | tf_op jit(solution)/shard_map/ppermute | solution.py:18
  73.8 1.0 fusion.3
  74.7 1.9 %fusion.7 = f32[32,32,128]{2,1,0:T(8,128)S(1)} fusion(bf16[32,128,128]{2,1,0:T(8,128)(2,1)S(1)} %bitcast.284, bf16[32,32,128]{2,0,1:T(8,128)(2,1)} %fusion.3), kind=kOutput, calls=%fused_computation.16 | convolution fusion | flops 67239936 | bytes 1835008 | tf_op jit(solution)/shard_map/srj,skj->srk/dot_general | solution.py:53
  80.0 2.1 %collective-permute-done.15 = bf16[32,128]{1,0:T(8,128)(2,1)S(1)} collective-permute-done((bf16[32,128]{1,0:T(8,128)(2,1)S(1)}, bf16[32,128]{1,0:T(8,128)(2,1)S(1)}, u32[]{:S(2)}, u32[]{:S(2)}) %collective-permute-start.15) | collective-permute-done | bytes 8224 | tf_op jit(solution)/shard_map/ppermute | solution.py:14
  83.2 8.9 %all_to_all.22 = f32[32,1,128]{2,1,0:T(1,128)S(1)} all-to-all(f32[32,1,128]{2,1,0:T(1,128)S(1)} %reshape.375), channel_id=1, replica_groups=mesh['dom'=8,'rep'=4] {'dom','rep'}, dimensions={0} | all-to-all | bytes 32768 | tf_op jit(solution)/shard_map/all_to_all | solution.py:24
  94.4 3.4 %collective-permute-done.18 = bf16[8,32,128]{2,0,1:T(8,128)(2,1)S(1)} collective-permute-done((bf16[8,32,128]{2,0,1:T(8,128)(2,1)S(1)}, bf16[8,32,128]{2,0,1:T(8,128)(2,1)S(1)}, u32[]{:S(2)}, u32[]{:S(2)}) %collective-permute-start.18) | collective-permute-done | bytes 65568 | tf_op jit(solution)/shard_map/ppermute | solution.py:18
  98.8 1.9 %fusion.8 = f32[32,32,128]{2,1,0:T(8,128)S(1)} fusion(bf16[32,128,128]{2,1,0:T(8,128)(2,1)S(1)} %bitcast.285, bf16[32,32,128]{2,0,1:T(8,128)(2,1)} %fusion.4), kind=kOutput, calls=%fused_computation.17 | convolution fusion | flops 67239936 | bytes 1835008 | tf_op jit(solution)/shard_map/srj,skj->srk/dot_general | solution.py:53
  104.1 2.1 %collective-permute-done.19 = bf16[32,128]{1,0:T(8,128)(2,1)S(1)} collective-permute-done((bf16[32,128]{1,0:T(8,128)(2,1)S(1)}, bf16[32,128]{1,0:T(8,128)(2,1)S(1)}, u32[]{:S(2)}, u32[]{:S(2)}) %collective-permute-start.19) | collective-permute-done | bytes 8224 | tf_op jit(solution)/shard_map/ppermute | solution.py:14
  107.1 9.0 %all_to_all.23 = f32[32,2,32]{2,1,0:T(2,128)S(1)} all-to-all(f32[32,2,32]{2,1,0:T(2,128)S(1)} %broadcast_in_dim.115), channel_id=1, replica_groups=mesh['dom'=8,'rep'=4] {'dom','rep'}, dimensions={0} | all-to-all | bytes 16384 | tf_op jit(solution)/shard_map/all_to_all | solution.py:24
  (158 shorter events, 33.7 us)
Async XLA Ops:
  3.6 7.0 %copy-start.3 = (f32[8,32,128]{2,1,0:T(8,128)S(1)}, f32[8,32,128]{2,1,0:T(8,128)}, u32[]{:S(2)}) copy-start(f32[8,32,128]{2,1,0:T(8,128)} %param.14) | copy-start | bytes 393220
  3.7 20.4 %collective-permute-start.6 = (bf16[8,128,128]{2,0,1:T(8,128)(2,1)S(1)}, bf16[8,128,128]{2,0,1:T(8,128)(2,1)S(1)}, u32[]{:S(2)}, u32[]{:S(2)}) collective-permute-start(bf16[8,128,128]{2,0,1:T(8,128)(2,1)S(1)} %select_bitcast_fusion), channel_id=1, source_target_pairs={{0,3},{1,0},{2,1},{3,2},{4,7},{5,4},{6,5},{7,6},{8,11},{9,8},{10,9... | collective-permute-start | bytes 786440 | tf_op jit(solution)/shard_map/ppermute | solution.py:14
  6.2 17.9 %collective-permute-start.5 = (bf16[8,128,128]{2,0,1:T(8,128)(2,1)S(1)}, bf16[8,128,128]{2,0,1:T(8,128)(2,1)S(1)}, u32[]{:S(2)}, u32[]{:S(2)}) collective-permute-start(bf16[8,128,128]{2,0,1:T(8,128)(2,1)S(1)} %get-tuple-element.86), channel_id=1, source_target_pairs={{0,2},{1,3},{2,0},{3,1},{4,6},{5,7},{6,4},{7,5},{8,10},{9,11},{10,... | collective-permute-start | bytes 786440 | tf_op jit(solution)/shard_map/ppermute | solution.py:14
  6.9 17.2 %collective-permute-start.4 = (bf16[8,128,128]{2,0,1:T(8,128)(2,1)S(1)}, bf16[8,128,128]{2,0,1:T(8,128)(2,1)S(1)}, u32[]{:S(2)}, u32[]{:S(2)}) collective-permute-start(bf16[8,128,128]{2,0,1:T(8,128)(2,1)S(1)} %get-tuple-element.85), channel_id=1, source_target_pairs={{0,1},{1,2},{2,3},{3,0},{4,5},{5,6},{6,7},{7,4},{8,9},{9,10},{10,1... | collective-permute-start | bytes 786440 | tf_op jit(solution)/shard_map/ppermute | solution.py:14
  7.4 10.8 %collective-permute-start.2 = (s32[8,2]{0,1:T(2,128)S(1)}, s32[8,2]{0,1:T(2,128)S(1)}, u32[]{:S(2)}, u32[]{:S(2)}) collective-permute-start(s32[8,2]{0,1:T(2,128)S(1)} %bitcast.331), channel_id=1, source_target_pairs={{0,3},{1,0},{2,1},{3,2},{4,7},{5,4},{6,5},{7,6},{8,11},{9,8},{10,9... | collective-permute-start | bytes 200 | tf_op jit(solution)/shard_map/ppermute | solution.py:14
  9.0 10.6 %collective-permute-start.1 = (s32[8,2]{0,1:T(2,128)S(1)}, s32[8,2]{0,1:T(2,128)S(1)}, u32[]{:S(2)}, u32[]{:S(2)}) collective-permute-start(s32[8,2]{0,1:T(2,128)S(1)} %bitcast.330), channel_id=1, source_target_pairs={{0,2},{1,3},{2,0},{3,1},{4,6},{5,7},{6,4},{7,5},{8,10},{9,11},{10,... | collective-permute-start | bytes 200 | tf_op jit(solution)/shard_map/ppermute | solution.py:14
  18.2 3.4 %collective-permute-start = (s32[8,2]{0,1:T(2,128)S(1)}, s32[8,2]{0,1:T(2,128)S(1)}, u32[]{:S(2)}, u32[]{:S(2)}) collective-permute-start(s32[8,2]{0,1:T(2,128)S(1)} %bitcast.329), channel_id=1, source_target_pairs={{0,1},{1,2},{2,3},{3,0},{4,5},{5,6},{6,7},{7,4},{8,9},{9,10},{10,1... | collective-permute-start | bytes 200 | tf_op jit(solution)/shard_map/ppermute | solution.py:14
  19.6 4.3 %collective-permute-start.3 = (bf16[8,32,128]{2,0,1:T(8,128)(2,1)S(1)}, bf16[8,32,128]{2,0,1:T(8,128)(2,1)S(1)}, u32[]{:S(2)}, u32[]{:S(2)}) collective-permute-start(bf16[8,32,128]{2,0,1:T(8,128)(2,1)S(1)} %multiply_convert_fusion), channel_id=1, source_target_pairs={{0,4},{4,0},{8,12},{12,8},{16,20},{20,16},{24,28},{28,24},{1,5},{5... | collective-permute-start | bytes 196616 | tf_op jit(solution)/shard_map/ppermute | solution.py:18
  26.1 5.6 %collective-permute-start.9 = (bf16[8,32,128]{2,0,1:T(8,128)(2,1)S(1)}, bf16[8,32,128]{2,0,1:T(8,128)(2,1)S(1)}, u32[]{:S(2)}, u32[]{:S(2)}) collective-permute-start(bf16[8,32,128]{2,0,1:T(8,128)(2,1)S(1)} %convolution_convert_fusion.12), channel_id=1, source_target_pairs={{0,4},{4,0},{8,12},{12,8},{16,20},{20,16},{24,28},{28,24},{1,5},{5... | collective-permute-start | bytes 196616 | tf_op jit(solution)/shard_map/ppermute | solution.py:18
  28.2 3.5 %collective-permute-start.8 = (f32[32,128]{1,0:T(8,128)S(1)}, f32[32,128]{1,0:T(8,128)S(1)}, u32[]{:S(2)}, u32[]{:S(2)}) collective-permute-start(f32[32,128]{1,0:T(8,128)S(1)} %fusion.93), channel_id=1, source_target_pairs={{0,3},{1,0},{2,1},{3,2},{4,7},{5,4},{6,5},{7,6},{8,11},{9,8},{10,9... | collective-permute-start | bytes 49160 | tf_op jit(solution)/shard_map/ppermute | solution.py:14
  28.5 3.1 %collective-permute-start.7 = (bf16[32,128]{1,0:T(8,128)(2,1)S(1)}, bf16[32,128]{1,0:T(8,128)(2,1)S(1)}, u32[]{:S(2)}, u32[]{:S(2)}) collective-permute-start(bf16[32,128]{1,0:T(8,128)(2,1)S(1)} %bitcast.309), channel_id=1, source_target_pairs={{0,1},{1,2},{2,3},{3,0},{4,5},{5,6},{6,7},{7,4},{8,9},{9,10},{10,1... | collective-permute-start | bytes 24584 | tf_op jit(solution)/shard_map/ppermute | solution.py:14
  45.8 4.3 %collective-permute-start.10 = (bf16[8,32,128]{2,0,1:T(8,128)(2,1)S(1)}, bf16[8,32,128]{2,0,1:T(8,128)(2,1)S(1)}, u32[]{:S(2)}, u32[]{:S(2)}) collective-permute-start(bf16[8,32,128]{2,0,1:T(8,128)(2,1)S(1)} %get-tuple-element.19), channel_id=1, source_target_pairs={{0,4},{4,0},{8,12},{12,8},{16,20},{20,16},{24,28},{28,24},{1,5},{5... | collective-permute-start | bytes 196616 | tf_op jit(solution)/shard_map/ppermute | solution.py:18
  54.0 4.6 %collective-permute-start.13 = (bf16[8,32,128]{2,0,1:T(8,128)(2,1)S(1)}, bf16[8,32,128]{2,0,1:T(8,128)(2,1)S(1)}, u32[]{:S(2)}, u32[]{:S(2)}) collective-permute-start(bf16[8,32,128]{2,0,1:T(8,128)(2,1)S(1)} %convolution_convert_fusion.11), channel_id=1, source_target_pairs={{0,4},{4,0},{8,12},{12,8},{16,20},{20,16},{24,28},{28,24},{1,5},{5... | collective-permute-start | bytes 196616 | tf_op jit(solution)/shard_map/ppermute | solution.py:18
  55.3 3.3 %collective-permute-start.12 = (f32[32,128]{1,0:T(8,128)S(1)}, f32[32,128]{1,0:T(8,128)S(1)}, u32[]{:S(2)}, u32[]{:S(2)}) collective-permute-start(f32[32,128]{1,0:T(8,128)S(1)} %fusion.89), channel_id=1, source_target_pairs={{0,3},{1,0},{2,1},{3,2},{4,7},{5,4},{6,5},{7,6},{8,11},{9,8},{10,9... | collective-permute-start | bytes 49160 | tf_op jit(solution)/shard_map/ppermute | solution.py:14
  55.3 3.1 %collective-permute-start.11 = (bf16[32,128]{1,0:T(8,128)(2,1)S(1)}, bf16[32,128]{1,0:T(8,128)(2,1)S(1)}, u32[]{:S(2)}, u32[]{:S(2)}) collective-permute-start(bf16[32,128]{1,0:T(8,128)(2,1)S(1)} %bitcast.310), channel_id=1, source_target_pairs={{0,1},{1,2},{2,3},{3,0},{4,5},{5,6},{6,7},{7,4},{8,9},{9,10},{10,1... | collective-permute-start | bytes 24584 | tf_op jit(solution)/shard_map/ppermute | solution.py:14
  69.4 4.3 %collective-permute-start.14 = (bf16[8,32,128]{2,0,1:T(8,128)(2,1)S(1)}, bf16[8,32,128]{2,0,1:T(8,128)(2,1)S(1)}, u32[]{:S(2)}, u32[]{:S(2)}) collective-permute-start(bf16[8,32,128]{2,0,1:T(8,128)(2,1)S(1)} %get-tuple-element.22), channel_id=1, source_target_pairs={{0,4},{4,0},{8,12},{12,8},{16,20},{20,16},{24,28},{28,24},{1,5},{5... | collective-permute-start | bytes 196616 | tf_op jit(solution)/shard_map/ppermute | solution.py:18
  77.6 4.6 %collective-permute-start.17 = (bf16[8,32,128]{2,0,1:T(8,128)(2,1)S(1)}, bf16[8,32,128]{2,0,1:T(8,128)(2,1)S(1)}, u32[]{:S(2)}, u32[]{:S(2)}) collective-permute-start(bf16[8,32,128]{2,0,1:T(8,128)(2,1)S(1)} %convolution_convert_fusion.10), channel_id=1, source_target_pairs={{0,4},{4,0},{8,12},{12,8},{16,20},{20,16},{24,28},{28,24},{1,5},{5... | collective-permute-start | bytes 196616 | tf_op jit(solution)/shard_map/ppermute | solution.py:18
  78.9 3.3 %collective-permute-start.16 = (f32[32,128]{1,0:T(8,128)S(1)}, f32[32,128]{1,0:T(8,128)S(1)}, u32[]{:S(2)}, u32[]{:S(2)}) collective-permute-start(f32[32,128]{1,0:T(8,128)S(1)} %fusion.85), channel_id=1, source_target_pairs={{0,3},{1,0},{2,1},{3,2},{4,7},{5,4},{6,5},{7,6},{8,11},{9,8},{10,9... | collective-permute-start | bytes 49160 | tf_op jit(solution)/shard_map/ppermute | solution.py:14
  79.0 3.1 %collective-permute-start.15 = (bf16[32,128]{1,0:T(8,128)(2,1)S(1)}, bf16[32,128]{1,0:T(8,128)(2,1)S(1)}, u32[]{:S(2)}, u32[]{:S(2)}) collective-permute-start(bf16[32,128]{1,0:T(8,128)(2,1)S(1)} %bitcast.311), channel_id=1, source_target_pairs={{0,1},{1,2},{2,3},{3,0},{4,5},{5,6},{6,7},{7,4},{8,9},{9,10},{10,1... | collective-permute-start | bytes 24584 | tf_op jit(solution)/shard_map/ppermute | solution.py:14
  93.5 4.3 %collective-permute-start.18 = (bf16[8,32,128]{2,0,1:T(8,128)(2,1)S(1)}, bf16[8,32,128]{2,0,1:T(8,128)(2,1)S(1)}, u32[]{:S(2)}, u32[]{:S(2)}) collective-permute-start(bf16[8,32,128]{2,0,1:T(8,128)(2,1)S(1)} %get-tuple-element.25), channel_id=1, source_target_pairs={{0,4},{4,0},{8,12},{12,8},{16,20},{20,16},{24,28},{28,24},{1,5},{5... | collective-permute-start | bytes 196616 | tf_op jit(solution)/shard_map/ppermute | solution.py:18
  101.8 4.6 %collective-permute-start.21 = (bf16[8,32,128]{2,0,1:T(8,128)(2,1)S(1)}, bf16[8,32,128]{2,0,1:T(8,128)(2,1)S(1)}, u32[]{:S(2)}, u32[]{:S(2)}) collective-permute-start(bf16[8,32,128]{2,0,1:T(8,128)(2,1)S(1)} %convolution_convert_fusion.9), channel_id=1, source_target_pairs={{0,4},{4,0},{8,12},{12,8},{16,20},{20,16},{24,28},{28,24},{1,5},{5... | collective-permute-start | bytes 196616 | tf_op jit(solution)/shard_map/ppermute | solution.py:18
  103.0 3.3 %collective-permute-start.20 = (f32[32,128]{1,0:T(8,128)S(1)}, f32[32,128]{1,0:T(8,128)S(1)}, u32[]{:S(2)}, u32[]{:S(2)}) collective-permute-start(f32[32,128]{1,0:T(8,128)S(1)} %fusion.81), channel_id=1, source_target_pairs={{0,3},{1,0},{2,1},{3,2},{4,7},{5,4},{6,5},{7,6},{8,11},{9,8},{10,9... | collective-permute-start | bytes 49160 | tf_op jit(solution)/shard_map/ppermute | solution.py:14
  103.1 3.1 %collective-permute-start.19 = (bf16[32,128]{1,0:T(8,128)(2,1)S(1)}, bf16[32,128]{1,0:T(8,128)(2,1)S(1)}, u32[]{:S(2)}, u32[]{:S(2)}) collective-permute-start(bf16[32,128]{1,0:T(8,128)(2,1)S(1)} %bitcast.312), channel_id=1, source_target_pairs={{0,1},{1,2},{2,3},{3,0},{4,5},{5,6},{6,7},{7,4},{8,9},{9,10},{10,1... | collective-permute-start | bytes 24584 | tf_op jit(solution)/shard_map/ppermute | solution.py:14
  103.8 12.3 %copy-start.6 = (f32[8,32,128]{2,0,1:T(8,128)S(1)}, f32[8,32,128]{2,0,1:T(8,128)}, u32[]{:S(2)}) copy-start(f32[8,32,128]{2,0,1:T(8,128)} %copy-done.5) | copy-start | bytes 393220
  (9 other events, 37.8 us)

commit v19 on v12

--- a/solution.py
+++ b/solution.py
@@ -85,8 +85,9 @@
 ):
     groups = lax.axis_size("rep")
     target = contact_owner[:, 0]
-    choose = (target[:, None] == jnp.arange(groups, dtype=jnp.int32)[None, :]).astype(jnp.int32)
-    rank = jnp.sum((jnp.cumsum(choose, axis=0) - choose) * choose, axis=1)
+    order = jnp.arange(target.shape[0], dtype=jnp.int32)
+    earlier = (target[None, :] == target[:, None]) & (order[None, :] < order[:, None])
+    rank = jnp.sum(earlier.astype(jnp.int32), axis=1)
     slot_of = target * CAP + rank
     pick = slot_of[None, :] == jnp.arange(groups * CAP, dtype=jnp.int32)[:, None]
     send_set = jnp.einsum(

time: 116 us -> 115 us (level)
  no operation moved by 1% of the time
where the time goes in v19:
time: 115 us; the launch traced here: 114 us
  blocking collectives  39.4 us (34%)
  waiting for transfers between devices  24.6 us (21%)
  matrix products  24.4 us (21%)
  starting transfers between devices  15.4 us (13%)
  other arithmetic  5.93 us (5%)
  local copies, waits for them, and re-layouts  3.38 us (3%)
  between operations  1.28 us (1%)
    all_to_all x4, blocking collectives, total(): gathered = lax.all_to_all(spread, ('dom', 'rep'), 0, 0, tiled=True)  39.4 us
    ppermute x14, waiting for transfers between devices, from_behind(): return lax.ppermute(value, axis, pairs)  20.9 us
    ppermute x8, starting transfers between devices, partner(): lax.ppermute(value, axis, [(i, i ^ 1 << distance) for i in range(lax.axis...  8.91 us
    dot_general x4, matrix products, apply_operator(): jnp.einsum('srj,skj->srk', multiplier, contact_set, preferred_element_typ...  6.53 us
    ppermute x14, starting transfers between devices, from_behind(): return lax.ppermute(value, axis, pairs)  6.46 us
    ppermute x8, waiting for transfers between devices, partner(): lax.ppermute(value, axis, [(i, i ^ 1 << distance) for i in range(lax.axis...  3.7 us
    dot_general x4, matrix products, local_stiffness(): jnp.einsum('pn,prj->nrj', mirror_onehot, mirror, precision=lax.Precision....  3.2 us
    dot_general x4, matrix products, apply_operator(): jnp.einsum('sn,nrk->srk', far_onehot, other, precision=lax.Precision.HIGH...  3.16 us
  transfers between devices with their start and end apart: 22, of which 16 were waited for; matrix products, arithmetic and copies ran while one was open for 8% of the time, Pallas kernels for 0%

profile of v19, /device:TPU:0, one launch (start us, length us, event | category | flops | bytes accessed | tf_op | source)
XLA Modules:
  0.0 114.4 jit_solution(14716237394681374943)
XLA Ops:
  3.0 2.4 %collective-permute-start.6 = (bf16[8,128,128]{2,0,1:T(8,128)(2,1)S(1)}, bf16[8,128,128]{2,0,1:T(8,128)(2,1)S(1)}, u32[]{:S(2)}, u32[]{:S(2)}) collective-permute-start(bf16[8,128,128]{2,0,1:T(8,128)(2,1)S(1)} %select_bitcast_fusion), channel_id=1, source_target_pairs={{0,3},{1,0},{2,1},{3,2},{4,7},{5,4},{6,5},{7,6},{8,11},{9,8},{10,9... | collective-permute-start | bytes 786440 | tf_op jit(solution)/shard_map/ppermute | solution.py:14
  6.6 1.7 %collective-permute-start.1 = (s32[8,2]{0,1:T(2,128)S(1)}, s32[8,2]{0,1:T(2,128)S(1)}, u32[]{:S(2)}, u32[]{:S(2)}) collective-permute-start(s32[8,2]{0,1:T(2,128)S(1)} %bitcast.328), channel_id=1, source_target_pairs={{0,2},{1,3},{2,0},{3,1},{4,6},{5,7},{6,4},{7,5},{8,10},{9,11},{10,... | collective-permute-start | bytes 200 | tf_op jit(solution)/shard_map/ppermute | solution.py:14
  8.4 1.6 %collective-permute-start.3 = (bf16[8,32,128]{2,0,1:T(8,128)(2,1)S(1)}, bf16[8,32,128]{2,0,1:T(8,128)(2,1)S(1)}, u32[]{:S(2)}, u32[]{:S(2)}) collective-permute-start(bf16[8,32,128]{2,0,1:T(8,128)(2,1)S(1)} %multiply_convert_fusion), channel_id=1, source_target_pairs={{0,4},{4,0},{8,12},{12,8},{16,20},{20,16},{24,28},{28,24},{1,5},{5... | collective-permute-start | bytes 196616 | tf_op jit(solution)/shard_map/ppermute | solution.py:18
  10.3 4.6 %collective-permute-done.2 = s32[8,2]{0,1:T(2,128)S(1)} collective-permute-done((s32[8,2]{0,1:T(2,128)S(1)}, s32[8,2]{0,1:T(2,128)S(1)}, u32[]{:S(2)}, u32[]{:S(2)}) %collective-permute-start.2) | collective-permute-done | bytes 96 | tf_op jit(solution)/shard_map/ppermute | solution.py:14
  14.9 1.1 collective-permute-start
  16.1 2.3 %collective-permute-done = s32[8,2]{0,1:T(2,128)S(1)} collective-permute-done((s32[8,2]{0,1:T(2,128)S(1)}, s32[8,2]{0,1:T(2,128)S(1)}, u32[]{:S(2)}, u32[]{:S(2)}) %collective-permute-start) | collective-permute-done | bytes 96 | tf_op jit(solution)/shard_map/ppermute | solution.py:14
  18.9 3.0 %collective-permute-done.7 = bf16[32,128]{1,0:T(8,128)(2,1)S(1)} collective-permute-done((bf16[32,128]{1,0:T(8,128)(2,1)S(1)}, bf16[32,128]{1,0:T(8,128)(2,1)S(1)}, u32[]{:S(2)}, u32[]{:S(2)}) %collective-permute-start.7) | collective-permute-done | bytes 8224 | tf_op jit(solution)/shard_map/ppermute | solution.py:14
  24.3 1.6 %collective-permute-start.9 = (bf16[8,32,128]{2,0,1:T(8,128)(2,1)S(1)}, bf16[8,32,128]{2,0,1:T(8,128)(2,1)S(1)}, u32[]{:S(2)}, u32[]{:S(2)}) collective-permute-start(bf16[8,32,128]{2,0,1:T(8,128)(2,1)S(1)} %convolution_convert_fusion.12), channel_id=1, source_target_pairs={{0,4},{4,0},{8,12},{12,8},{16,20},{20,16},{24,28},{28,24},{1,5},{5... | collective-permute-start | bytes 196616 | tf_op jit(solution)/shard_map/ppermute | solution.py:18
  29.6 12.8 %all_to_all.20 = f32[32,1,128]{2,1,0:T(1,128)S(1)} all-to-all(f32[32,1,128]{2,1,0:T(1,128)S(1)} %reshape.372), channel_id=1, replica_groups=mesh['dom'=8,'rep'=4] {'dom','rep'}, dimensions={0} | all-to-all | bytes 32768 | tf_op jit(solution)/shard_map/all_to_all | solution.py:24
  45.0 2.6 %collective-permute-done.11 = bf16[32,128]{1,0:T(8,128)(2,1)S(1)} collective-permute-done((bf16[32,128]{1,0:T(8,128)(2,1)S(1)}, bf16[32,128]{1,0:T(8,128)(2,1)S(1)}, u32[]{:S(2)}, u32[]{:S(2)}) %collective-permute-start.11) | collective-permute-done | bytes 8224 | tf_op jit(solution)/shard_map/ppermute | solution.py:14
  48.2 1.0 fusion.2
  49.2 1.9 %fusion.6 = f32[32,32,128]{2,1,0:T(8,128)S(1)} fusion(bf16[32,128,128]{2,1,0:T(8,128)(2,1)S(1)} %bitcast.283, bf16[32,32,128]{2,0,1:T(8,128)(2,1)} %fusion.2), kind=kOutput, calls=%fused_computation.15 | convolution fusion | flops 67239936 | bytes 1835008 | tf_op jit(solution)/shard_map/srj,skj->srk/dot_general | solution.py:54
  52.1 1.1 collective-permute-start.13
  55.4 1.0 collective-permute-done.13
  57.4 8.8 %all_to_all.21 = f32[32,1,128]{2,1,0:T(1,128)S(1)} all-to-all(f32[32,1,128]{2,1,0:T(1,128)S(1)} %reshape.374), channel_id=1, replica_groups=mesh['dom'=8,'rep'=4] {'dom','rep'}, dimensions={0} | all-to-all | bytes 32768 | tf_op jit(solution)/shard_map/all_to_all | solution.py:24
  68.5 2.6 %collective-permute-done.15 = bf16[32,128]{1,0:T(8,128)(2,1)S(1)} collective-permute-done((bf16[32,128]{1,0:T(8,128)(2,1)S(1)}, bf16[32,128]{1,0:T(8,128)(2,1)S(1)}, u32[]{:S(2)}, u32[]{:S(2)}) %collective-permute-start.15) | collective-permute-done | bytes 8224 | tf_op jit(solution)/shard_map/ppermute | solution.py:14
  72.5 1.9 %fusion.7 = f32[32,32,128]{2,1,0:T(8,128)S(1)} fusion(bf16[32,128,128]{2,1,0:T(8,128)(2,1)S(1)} %bitcast.284, bf16[32,32,128]{2,0,1:T(8,128)(2,1)} %fusion.3), kind=kOutput, calls=%fused_computation.16 | convolution fusion | flops 67239936 | bytes 1835008 | tf_op jit(solution)/shard_map/srj,skj->srk/dot_general | solution.py:54
  75.4 1.3 %collective-permute-start.17 = (bf16[8,32,128]{2,0,1:T(8,128)(2,1)S(1)}, bf16[8,32,128]{2,0,1:T(8,128)(2,1)S(1)}, u32[]{:S(2)}, u32[]{:S(2)}) collective-permute-start(bf16[8,32,128]{2,0,1:T(8,128)(2,1)S(1)} %convolution_convert_fusion.10), channel_id=1, source_target_pairs={{0,4},{4,0},{8,12},{12,8},{16,20},{20,16},{24,28},{28,24},{1,5},{5... | collective-permute-start | bytes 196616 | tf_op jit(solution)/shard_map/ppermute | solution.py:18
  80.7 8.8 %all_to_all.22 = f32[32,1,128]{2,1,0:T(1,128)S(1)} all-to-all(f32[32,1,128]{2,1,0:T(1,128)S(1)} %reshape.376), channel_id=1, replica_groups=mesh['dom'=8,'rep'=4] {'dom','rep'}, dimensions={0} | all-to-all | bytes 32768 | tf_op jit(solution)/shard_map/all_to_all | solution.py:24
  92.5 2.2 %collective-permute-done.19 = bf16[32,128]{1,0:T(8,128)(2,1)S(1)} collective-permute-done((bf16[32,128]{1,0:T(8,128)(2,1)S(1)}, bf16[32,128]{1,0:T(8,128)(2,1)S(1)}, u32[]{:S(2)}, u32[]{:S(2)}) %collective-permute-start.19) | collective-permute-done | bytes 8224 | tf_op jit(solution)/shard_map/ppermute | solution.py:14
  94.9 1.0 fusion.4
  95.8 1.9 %fusion.8 = f32[32,32,128]{2,1,0:T(8,128)S(1)} fusion(bf16[32,128,128]{2,1,0:T(8,128)(2,1)S(1)} %bitcast.285, bf16[32,32,128]{2,0,1:T(8,128)(2,1)} %fusion.4), kind=kOutput, calls=%fused_computation.17 | convolution fusion | flops 67239936 | bytes 1835008 | tf_op jit(solution)/shard_map/srj,skj->srk/dot_general | solution.py:54
  98.7 1.5 %collective-permute-start.21 = (bf16[8,32,128]{2,0,1:T(8,128)(2,1)S(1)}, bf16[8,32,128]{2,0,1:T(8,128)(2,1)S(1)}, u32[]{:S(2)}, u32[]{:S(2)}) collective-permute-start(bf16[8,32,128]{2,0,1:T(8,128)(2,1)S(1)} %convolution_convert_fusion.9), channel_id=1, source_target_pairs={{0,4},{4,0},{8,12},{12,8},{16,20},{20,16},{24,28},{28,24},{1,5},{5... | collective-permute-start | bytes 196616 | tf_op jit(solution)/shard_map/ppermute | solution.py:18
  103.8 8.9 %all_to_all.23 = f32[32,2,32]{2,1,0:T(2,128)S(1)} all-to-all(f32[32,2,32]{2,1,0:T(2,128)S(1)} %broadcast_in_dim.116), channel_id=1, replica_groups=mesh['dom'=8,'rep'=4] {'dom','rep'}, dimensions={0} | all-to-all | bytes 16384 | tf_op jit(solution)/shard_map/all_to_all | solution.py:24
  (162 shorter events, 35.3 us)
Async XLA Ops:
  3.0 19.4 %collective-permute-start.6 = (bf16[8,128,128]{2,0,1:T(8,128)(2,1)S(1)}, bf16[8,128,128]{2,0,1:T(8,128)(2,1)S(1)}, u32[]{:S(2)}, u32[]{:S(2)}) collective-permute-start(bf16[8,128,128]{2,0,1:T(8,128)(2,1)S(1)} %select_bitcast_fusion), channel_id=1, source_target_pairs={{0,3},{1,0},{2,1},{3,2},{4,7},{5,4},{6,5},{7,6},{8,11},{9,8},{10,9... | collective-permute-start | bytes 786440 | tf_op jit(solution)/shard_map/ppermute | solution.py:14
  5.4 16.5 %copy-start.4 = (bf16[1,128,128]{2,1,0:T(8,128)(2,1)S(1)}, bf16[1,128,128]{2,1,0:T(8,128)(2,1)}, u32[]{:S(2)}) copy-start(bf16[1,128,128]{2,1,0:T(8,128)(2,1)} %param.19) | copy-start | bytes 98308
  5.5 16.9 %collective-permute-start.5 = (bf16[8,128,128]{2,0,1:T(8,128)(2,1)S(1)}, bf16[8,128,128]{2,0,1:T(8,128)(2,1)S(1)}, u32[]{:S(2)}, u32[]{:S(2)}) collective-permute-start(bf16[8,128,128]{2,0,1:T(8,128)(2,1)S(1)} %get-tuple-element.86), channel_id=1, source_target_pairs={{0,2},{1,3},{2,0},{3,1},{4,6},{5,7},{6,4},{7,5},{8,10},{9,11},{10,... | collective-permute-start | bytes 786440 | tf_op jit(solution)/shard_map/ppermute | solution.py:14
  6.5 8.4 %collective-permute-start.2 = (s32[8,2]{0,1:T(2,128)S(1)}, s32[8,2]{0,1:T(2,128)S(1)}, u32[]{:S(2)}, u32[]{:S(2)}) collective-permute-start(s32[8,2]{0,1:T(2,128)S(1)} %bitcast.329), channel_id=1, source_target_pairs={{0,3},{1,0},{2,1},{3,2},{4,7},{5,4},{6,5},{7,6},{8,11},{9,8},{10,9... | collective-permute-start | bytes 200 | tf_op jit(solution)/shard_map/ppermute | solution.py:14
  6.6 9.5 %collective-permute-start.1 = (s32[8,2]{0,1:T(2,128)S(1)}, s32[8,2]{0,1:T(2,128)S(1)}, u32[]{:S(2)}, u32[]{:S(2)}) collective-permute-start(s32[8,2]{0,1:T(2,128)S(1)} %bitcast.328), channel_id=1, source_target_pairs={{0,2},{1,3},{2,0},{3,1},{4,6},{5,7},{6,4},{7,5},{8,10},{9,11},{10,... | collective-permute-start | bytes 200 | tf_op jit(solution)/shard_map/ppermute | solution.py:14
  8.4 13.6 %collective-permute-start.3 = (bf16[8,32,128]{2,0,1:T(8,128)(2,1)S(1)}, bf16[8,32,128]{2,0,1:T(8,128)(2,1)S(1)}, u32[]{:S(2)}, u32[]{:S(2)}) collective-permute-start(bf16[8,32,128]{2,0,1:T(8,128)(2,1)S(1)} %multiply_convert_fusion), channel_id=1, source_target_pairs={{0,4},{4,0},{8,12},{12,8},{16,20},{20,16},{24,28},{28,24},{1,5},{5... | collective-permute-start | bytes 196616 | tf_op jit(solution)/shard_map/ppermute | solution.py:18
  14.9 3.4 %collective-permute-start = (s32[8,2]{0,1:T(2,128)S(1)}, s32[8,2]{0,1:T(2,128)S(1)}, u32[]{:S(2)}, u32[]{:S(2)}) collective-permute-start(s32[8,2]{0,1:T(2,128)S(1)} %bitcast.327), channel_id=1, source_target_pairs={{0,1},{1,2},{2,3},{3,0},{4,5},{5,6},{6,7},{7,4},{8,9},{9,10},{10,1... | collective-permute-start | bytes 200 | tf_op jit(solution)/shard_map/ppermute | solution.py:14
  16.1 6.3 %collective-permute-start.4 = (bf16[8,128,128]{2,0,1:T(8,128)(2,1)S(1)}, bf16[8,128,128]{2,0,1:T(8,128)(2,1)S(1)}, u32[]{:S(2)}, u32[]{:S(2)}) collective-permute-start(bf16[8,128,128]{2,0,1:T(8,128)(2,1)S(1)} %get-tuple-element.85), channel_id=1, source_target_pairs={{0,1},{1,2},{2,3},{3,0},{4,5},{5,6},{6,7},{7,4},{8,9},{9,10},{10,1... | collective-permute-start | bytes 786440 | tf_op jit(solution)/shard_map/ppermute | solution.py:14
  18.4 3.6 %collective-permute-start.7 = (bf16[32,128]{1,0:T(8,128)(2,1)S(1)}, bf16[32,128]{1,0:T(8,128)(2,1)S(1)}, u32[]{:S(2)}, u32[]{:S(2)}) collective-permute-start(bf16[32,128]{1,0:T(8,128)(2,1)S(1)} %bitcast.309), channel_id=1, source_target_pairs={{0,1},{1,2},{2,3},{3,0},{4,5},{5,6},{6,7},{7,4},{8,9},{9,10},{10,1... | collective-permute-start | bytes 24584 | tf_op jit(solution)/shard_map/ppermute | solution.py:14
  24.3 4.3 %collective-permute-start.9 = (bf16[8,32,128]{2,0,1:T(8,128)(2,1)S(1)}, bf16[8,32,128]{2,0,1:T(8,128)(2,1)S(1)}, u32[]{:S(2)}, u32[]{:S(2)}) collective-permute-start(bf16[8,32,128]{2,0,1:T(8,128)(2,1)S(1)} %convolution_convert_fusion.12), channel_id=1, source_target_pairs={{0,4},{4,0},{8,12},{12,8},{16,20},{20,16},{24,28},{28,24},{1,5},{5... | collective-permute-start | bytes 196616 | tf_op jit(solution)/shard_map/ppermute | solution.py:18
  26.6 1.5 %collective-permute-start.8 = (f32[32,128]{1,0:T(8,128)S(1)}, f32[32,128]{1,0:T(8,128)S(1)}, u32[]{:S(2)}, u32[]{:S(2)}) collective-permute-start(f32[32,128]{1,0:T(8,128)S(1)} %fusion.93), channel_id=1, source_target_pairs={{0,3},{1,0},{2,1},{3,2},{4,7},{5,4},{6,5},{7,6},{8,11},{9,8},{10,9... | collective-permute-start | bytes 49160 | tf_op jit(solution)/shard_map/ppermute | solution.py:14
  43.9 4.3 %collective-permute-start.10 = (bf16[8,32,128]{2,0,1:T(8,128)(2,1)S(1)}, bf16[8,32,128]{2,0,1:T(8,128)(2,1)S(1)}, u32[]{:S(2)}, u32[]{:S(2)}) collective-permute-start(bf16[8,32,128]{2,0,1:T(8,128)(2,1)S(1)} %get-tuple-element.19), channel_id=1, source_target_pairs={{0,4},{4,0},{8,12},{12,8},{16,20},{20,16},{24,28},{28,24},{1,5},{5... | collective-permute-start | bytes 196616 | tf_op jit(solution)/shard_map/ppermute | solution.py:18
  44.5 3.1 %collective-permute-start.11 = (bf16[32,128]{1,0:T(8,128)(2,1)S(1)}, bf16[32,128]{1,0:T(8,128)(2,1)S(1)}, u32[]{:S(2)}, u32[]{:S(2)}) collective-permute-start(bf16[32,128]{1,0:T(8,128)(2,1)S(1)} %bitcast.311), channel_id=1, source_target_pairs={{0,1},{1,2},{2,3},{3,0},{4,5},{5,6},{6,7},{7,4},{8,9},{9,10},{10,1... | collective-permute-start | bytes 24584 | tf_op jit(solution)/shard_map/ppermute | solution.py:14
  52.1 4.3 %collective-permute-start.13 = (bf16[8,32,128]{2,0,1:T(8,128)(2,1)S(1)}, bf16[8,32,128]{2,0,1:T(8,128)(2,1)S(1)}, u32[]{:S(2)}, u32[]{:S(2)}) collective-permute-start(bf16[8,32,128]{2,0,1:T(8,128)(2,1)S(1)} %convolution_convert_fusion.11), channel_id=1, source_target_pairs={{0,4},{4,0},{8,12},{12,8},{16,20},{20,16},{24,28},{28,24},{1,5},{5... | collective-permute-start | bytes 196616 | tf_op jit(solution)/shard_map/ppermute | solution.py:18
  53.9 1.5 %collective-permute-start.12 = (f32[32,128]{1,0:T(8,128)S(1)}, f32[32,128]{1,0:T(8,128)S(1)}, u32[]{:S(2)}, u32[]{:S(2)}) collective-permute-start(f32[32,128]{1,0:T(8,128)S(1)} %fusion.89), channel_id=1, source_target_pairs={{0,3},{1,0},{2,1},{3,2},{4,7},{5,4},{6,5},{7,6},{8,11},{9,8},{10,9... | collective-permute-start | bytes 49160 | tf_op jit(solution)/shard_map/ppermute | solution.py:14
  67.2 4.3 %collective-permute-start.14 = (bf16[8,32,128]{2,0,1:T(8,128)(2,1)S(1)}, bf16[8,32,128]{2,0,1:T(8,128)(2,1)S(1)}, u32[]{:S(2)}, u32[]{:S(2)}) collective-permute-start(bf16[8,32,128]{2,0,1:T(8,128)(2,1)S(1)} %get-tuple-element.22), channel_id=1, source_target_pairs={{0,4},{4,0},{8,12},{12,8},{16,20},{20,16},{24,28},{28,24},{1,5},{5... | collective-permute-start | bytes 196616 | tf_op jit(solution)/shard_map/ppermute | solution.py:18
  67.9 3.3 %collective-permute-start.15 = (bf16[32,128]{1,0:T(8,128)(2,1)S(1)}, bf16[32,128]{1,0:T(8,128)(2,1)S(1)}, u32[]{:S(2)}, u32[]{:S(2)}) collective-permute-start(bf16[32,128]{1,0:T(8,128)(2,1)S(1)} %bitcast.312), channel_id=1, source_target_pairs={{0,1},{1,2},{2,3},{3,0},{4,5},{5,6},{6,7},{7,4},{8,9},{9,10},{10,1... | collective-permute-start | bytes 24584 | tf_op jit(solution)/shard_map/ppermute | solution.py:14
  75.4 4.3 %collective-permute-start.17 = (bf16[8,32,128]{2,0,1:T(8,128)(2,1)S(1)}, bf16[8,32,128]{2,0,1:T(8,128)(2,1)S(1)}, u32[]{:S(2)}, u32[]{:S(2)}) collective-permute-start(bf16[8,32,128]{2,0,1:T(8,128)(2,1)S(1)} %convolution_convert_fusion.10), channel_id=1, source_target_pairs={{0,4},{4,0},{8,12},{12,8},{16,20},{20,16},{24,28},{28,24},{1,5},{5... | collective-permute-start | bytes 196616 | tf_op jit(solution)/shard_map/ppermute | solution.py:18
  77.4 1.5 %collective-permute-start.16 = (f32[32,128]{1,0:T(8,128)S(1)}, f32[32,128]{1,0:T(8,128)S(1)}, u32[]{:S(2)}, u32[]{:S(2)}) collective-permute-start(f32[32,128]{1,0:T(8,128)S(1)} %fusion.85), channel_id=1, source_target_pairs={{0,3},{1,0},{2,1},{3,2},{4,7},{5,4},{6,5},{7,6},{8,11},{9,8},{10,9... | collective-permute-start | bytes 49160 | tf_op jit(solution)/shard_map/ppermute | solution.py:14
  90.5 4.3 %collective-permute-start.18 = (bf16[8,32,128]{2,0,1:T(8,128)(2,1)S(1)}, bf16[8,32,128]{2,0,1:T(8,128)(2,1)S(1)}, u32[]{:S(2)}, u32[]{:S(2)}) collective-permute-start(bf16[8,32,128]{2,0,1:T(8,128)(2,1)S(1)} %get-tuple-element.25), channel_id=1, source_target_pairs={{0,4},{4,0},{8,12},{12,8},{16,20},{20,16},{24,28},{28,24},{1,5},{5... | collective-permute-start | bytes 196616 | tf_op jit(solution)/shard_map/ppermute | solution.py:18
  91.6 3.1 %collective-permute-start.19 = (bf16[32,128]{1,0:T(8,128)(2,1)S(1)}, bf16[32,128]{1,0:T(8,128)(2,1)S(1)}, u32[]{:S(2)}, u32[]{:S(2)}) collective-permute-start(bf16[32,128]{1,0:T(8,128)(2,1)S(1)} %bitcast.310), channel_id=1, source_target_pairs={{0,1},{1,2},{2,3},{3,0},{4,5},{5,6},{6,7},{7,4},{8,9},{9,10},{10,1... | collective-permute-start | bytes 24584 | tf_op jit(solution)/shard_map/ppermute | solution.py:14
  98.7 4.3 %collective-permute-start.21 = (bf16[8,32,128]{2,0,1:T(8,128)(2,1)S(1)}, bf16[8,32,128]{2,0,1:T(8,128)(2,1)S(1)}, u32[]{:S(2)}, u32[]{:S(2)}) collective-permute-start(bf16[8,32,128]{2,0,1:T(8,128)(2,1)S(1)} %convolution_convert_fusion.9), channel_id=1, source_target_pairs={{0,4},{4,0},{8,12},{12,8},{16,20},{20,16},{24,28},{28,24},{1,5},{5... | collective-permute-start | bytes 196616 | tf_op jit(solution)/shard_map/ppermute | solution.py:18
  101.0 1.5 %collective-permute-start.20 = (f32[32,128]{1,0:T(8,128)S(1)}, f32[32,128]{1,0:T(8,128)S(1)}, u32[]{:S(2)}, u32[]{:S(2)}) collective-permute-start(f32[32,128]{1,0:T(8,128)S(1)} %fusion.81), channel_id=1, source_target_pairs={{0,3},{1,0},{2,1},{3,2},{4,7},{5,4},{6,5},{7,6},{8,11},{9,8},{10,9... | collective-permute-start | bytes 49160 | tf_op jit(solution)/shard_map/ppermute | solution.py:14
  101.3 11.6 %copy-start.6 = (f32[8,32,128]{2,0,1:T(8,128)S(1)}, f32[8,32,128]{2,0,1:T(8,128)}, u32[]{:S(2)}) copy-start(f32[8,32,128]{2,0,1:T(8,128)} %copy-done.5) | copy-start | bytes 393220
  (10 other events, 39.9 us)

commit v20 on v19

--- a/solution.py
+++ b/solution.py
@@ -87,8 +87,8 @@
     target = contact_owner[:, 0]
     order = jnp.arange(target.shape[0], dtype=jnp.int32)
     earlier = (target[None, :] == target[:, None]) & (order[None, :] < order[:, None])
-    rank = jnp.sum(earlier.astype(jnp.int32), axis=1)
-    slot_of = target * CAP + rank
+    itself = jnp.where(order[None, :] == order[:, None], target[:, None] * CAP, 0)
+    slot_of = jnp.sum(earlier.astype(jnp.int32) + itself, axis=1)
     pick = slot_of[None, :] == jnp.arange(groups * CAP, dtype=jnp.int32)[:, None]
     send_set = jnp.einsum(
         "sc,cij->sij", pick.astype(jnp.bfloat16), contact_tiles, preferred_element_type=jnp.float32

time: 115 us -> 115 us (level)
  no operation moved by 1% of the time
where the time goes in v20:
time: 115 us; the launch traced here: 114 us
  blocking collectives  39.4 us (34%)
  waiting for transfers between devices  24.6 us (21%)
  matrix products  24.4 us (21%)
  starting transfers between devices  15.4 us (13%)
  other arithmetic  5.98 us (5%)
  local copies, waits for them, and re-layouts  3.38 us (3%)
  between operations  1.28 us (1%)
    all_to_all x4, blocking collectives, total(): gathered = lax.all_to_all(spread, ('dom', 'rep'), 0, 0, tiled=True)  39.4 us
    ppermute x14, waiting for transfers between devices, from_behind(): return lax.ppermute(value, axis, pairs)  20.9 us
    ppermute x8, starting transfers between devices, partner(): lax.ppermute(value, axis, [(i, i ^ 1 << distance) for i in range(lax.axis...  8.92 us
    dot_general x4, matrix products, apply_operator(): jnp.einsum('srj,skj->srk', multiplier, contact_set, preferred_element_typ...  6.53 us
    ppermute x14, starting transfers between devices, from_behind(): return lax.ppermute(value, axis, pairs)  6.46 us
    ppermute x8, waiting for transfers between devices, partner(): lax.ppermute(value, axis, [(i, i ^ 1 << distance) for i in range(lax.axis...  3.69 us
    dot_general x4, matrix products, local_stiffness(): jnp.einsum('pn,prj->nrj', mirror_onehot, mirror, precision=lax.Precision....  3.19 us
    dot_general x4, matrix products, apply_operator(): jnp.einsum('sn,nrk->srk', far_onehot, other, precision=lax.Precision.HIGH...  3.16 us
  transfers between devices with their start and end apart: 22, of which 16 were waited for; matrix products, arithmetic and copies ran while one was open for 8% of the time, Pallas kernels for 0%

profile of v20, /device:TPU:0, one launch (start us, length us, event | category | flops | bytes accessed | tf_op | source)
XLA Modules:
  0.0 114.5 jit_solution(1427135477236808494)
XLA Ops:
  3.0 2.4 %collective-permute-start.6 = (bf16[8,128,128]{2,0,1:T(8,128)(2,1)S(1)}, bf16[8,128,128]{2,0,1:T(8,128)(2,1)S(1)}, u32[]{:S(2)}, u32[]{:S(2)}) collective-permute-start(bf16[8,128,128]{2,0,1:T(8,128)(2,1)S(1)} %select_bitcast_fusion), channel_id=1, source_target_pairs={{0,3},{1,0},{2,1},{3,2},{4,7},{5,4},{6,5},{7,6},{8,11},{9,8},{10,9... | collective-permute-start | bytes 786440 | tf_op jit(solution)/shard_map/ppermute | solution.py:14
  6.7 1.7 %collective-permute-start.1 = (s32[8,2]{0,1:T(2,128)S(1)}, s32[8,2]{0,1:T(2,128)S(1)}, u32[]{:S(2)}, u32[]{:S(2)}) collective-permute-start(s32[8,2]{0,1:T(2,128)S(1)} %bitcast.330), channel_id=1, source_target_pairs={{0,2},{1,3},{2,0},{3,1},{4,6},{5,7},{6,4},{7,5},{8,10},{9,11},{10,... | collective-permute-start | bytes 200 | tf_op jit(solution)/shard_map/ppermute | solution.py:14
  8.5 1.6 %collective-permute-start.3 = (bf16[8,32,128]{2,0,1:T(8,128)(2,1)S(1)}, bf16[8,32,128]{2,0,1:T(8,128)(2,1)S(1)}, u32[]{:S(2)}, u32[]{:S(2)}) collective-permute-start(bf16[8,32,128]{2,0,1:T(8,128)(2,1)S(1)} %multiply_convert_fusion), channel_id=1, source_target_pairs={{0,4},{4,0},{8,12},{12,8},{16,20},{20,16},{24,28},{28,24},{1,5},{5... | collective-permute-start | bytes 196616 | tf_op jit(solution)/shard_map/ppermute | solution.py:18
  10.4 4.6 %collective-permute-done.2 = s32[8,2]{0,1:T(2,128)S(1)} collective-permute-done((s32[8,2]{0,1:T(2,128)S(1)}, s32[8,2]{0,1:T(2,128)S(1)}, u32[]{:S(2)}, u32[]{:S(2)}) %collective-permute-start.2) | collective-permute-done | bytes 96 | tf_op jit(solution)/shard_map/ppermute | solution.py:14
  15.0 1.1 collective-permute-start
  16.1 2.3 %collective-permute-done = s32[8,2]{0,1:T(2,128)S(1)} collective-permute-done((s32[8,2]{0,1:T(2,128)S(1)}, s32[8,2]{0,1:T(2,128)S(1)}, u32[]{:S(2)}, u32[]{:S(2)}) %collective-permute-start) | collective-permute-done | bytes 96 | tf_op jit(solution)/shard_map/ppermute | solution.py:14
  19.0 3.0 %collective-permute-done.7 = bf16[32,128]{1,0:T(8,128)(2,1)S(1)} collective-permute-done((bf16[32,128]{1,0:T(8,128)(2,1)S(1)}, bf16[32,128]{1,0:T(8,128)(2,1)S(1)}, u32[]{:S(2)}, u32[]{:S(2)}) %collective-permute-start.7) | collective-permute-done | bytes 8224 | tf_op jit(solution)/shard_map/ppermute | solution.py:14
  24.4 1.6 %collective-permute-start.9 = (bf16[8,32,128]{2,0,1:T(8,128)(2,1)S(1)}, bf16[8,32,128]{2,0,1:T(8,128)(2,1)S(1)}, u32[]{:S(2)}, u32[]{:S(2)}) collective-permute-start(bf16[8,32,128]{2,0,1:T(8,128)(2,1)S(1)} %convolution_convert_fusion.12), channel_id=1, source_target_pairs={{0,4},{4,0},{8,12},{12,8},{16,20},{20,16},{24,28},{28,24},{1,5},{5... | collective-permute-start | bytes 196616 | tf_op jit(solution)/shard_map/ppermute | solution.py:18
  29.7 12.8 %all_to_all.20 = f32[32,1,128]{2,1,0:T(1,128)S(1)} all-to-all(f32[32,1,128]{2,1,0:T(1,128)S(1)} %reshape.363), channel_id=1, replica_groups=mesh['dom'=8,'rep'=4] {'dom','rep'}, dimensions={0} | all-to-all | bytes 32768 | tf_op jit(solution)/shard_map/all_to_all | solution.py:24
  45.1 2.6 %collective-permute-done.11 = bf16[32,128]{1,0:T(8,128)(2,1)S(1)} collective-permute-done((bf16[32,128]{1,0:T(8,128)(2,1)S(1)}, bf16[32,128]{1,0:T(8,128)(2,1)S(1)}, u32[]{:S(2)}, u32[]{:S(2)}) %collective-permute-start.11) | collective-permute-done | bytes 8224 | tf_op jit(solution)/shard_map/ppermute | solution.py:14
  48.3 1.0 fusion.2
  49.2 1.9 %fusion.6 = f32[32,32,128]{2,1,0:T(8,128)S(1)} fusion(bf16[32,128,128]{2,1,0:T(8,128)(2,1)S(1)} %bitcast.284, bf16[32,32,128]{2,0,1:T(8,128)(2,1)} %fusion.2), kind=kOutput, calls=%fused_computation.15 | convolution fusion | flops 67239936 | bytes 1835008 | tf_op jit(solution)/shard_map/srj,skj->srk/dot_general | solution.py:54
  52.1 1.1 collective-permute-start.13
  55.4 1.0 collective-permute-done.13
  57.4 8.8 %all_to_all.21 = f32[32,1,128]{2,1,0:T(1,128)S(1)} all-to-all(f32[32,1,128]{2,1,0:T(1,128)S(1)} %reshape.365), channel_id=1, replica_groups=mesh['dom'=8,'rep'=4] {'dom','rep'}, dimensions={0} | all-to-all | bytes 32768 | tf_op jit(solution)/shard_map/all_to_all | solution.py:24
  68.6 2.6 %collective-permute-done.15 = bf16[32,128]{1,0:T(8,128)(2,1)S(1)} collective-permute-done((bf16[32,128]{1,0:T(8,128)(2,1)S(1)}, bf16[32,128]{1,0:T(8,128)(2,1)S(1)}, u32[]{:S(2)}, u32[]{:S(2)}) %collective-permute-start.15) | collective-permute-done | bytes 8224 | tf_op jit(solution)/shard_map/ppermute | solution.py:14
  72.6 1.9 %fusion.7 = f32[32,32,128]{2,1,0:T(8,128)S(1)} fusion(bf16[32,128,128]{2,1,0:T(8,128)(2,1)S(1)} %bitcast.285, bf16[32,32,128]{2,0,1:T(8,128)(2,1)} %fusion.3), kind=kOutput, calls=%fused_computation.16 | convolution fusion | flops 67239936 | bytes 1835008 | tf_op jit(solution)/shard_map/srj,skj->srk/dot_general | solution.py:54
  75.5 1.3 %collective-permute-start.17 = (bf16[8,32,128]{2,0,1:T(8,128)(2,1)S(1)}, bf16[8,32,128]{2,0,1:T(8,128)(2,1)S(1)}, u32[]{:S(2)}, u32[]{:S(2)}) collective-permute-start(bf16[8,32,128]{2,0,1:T(8,128)(2,1)S(1)} %convolution_convert_fusion.10), channel_id=1, source_target_pairs={{0,4},{4,0},{8,12},{12,8},{16,20},{20,16},{24,28},{28,24},{1,5},{5... | collective-permute-start | bytes 196616 | tf_op jit(solution)/shard_map/ppermute | solution.py:18
  80.7 8.8 %all_to_all.22 = f32[32,1,128]{2,1,0:T(1,128)S(1)} all-to-all(f32[32,1,128]{2,1,0:T(1,128)S(1)} %reshape.367), channel_id=1, replica_groups=mesh['dom'=8,'rep'=4] {'dom','rep'}, dimensions={0} | all-to-all | bytes 32768 | tf_op jit(solution)/shard_map/all_to_all | solution.py:24
  92.5 2.2 %collective-permute-done.19 = bf16[32,128]{1,0:T(8,128)(2,1)S(1)} collective-permute-done((bf16[32,128]{1,0:T(8,128)(2,1)S(1)}, bf16[32,128]{1,0:T(8,128)(2,1)S(1)}, u32[]{:S(2)}, u32[]{:S(2)}) %collective-permute-start.19) | collective-permute-done | bytes 8224 | tf_op jit(solution)/shard_map/ppermute | solution.py:14
  94.9 1.0 fusion.4
  95.9 1.9 %fusion.8 = f32[32,32,128]{2,1,0:T(8,128)S(1)} fusion(bf16[32,128,128]{2,1,0:T(8,128)(2,1)S(1)} %bitcast.286, bf16[32,32,128]{2,0,1:T(8,128)(2,1)} %fusion.4), kind=kOutput, calls=%fused_computation.17 | convolution fusion | flops 67239936 | bytes 1835008 | tf_op jit(solution)/shard_map/srj,skj->srk/dot_general | solution.py:54
  98.8 1.5 %collective-permute-start.21 = (bf16[8,32,128]{2,0,1:T(8,128)(2,1)S(1)}, bf16[8,32,128]{2,0,1:T(8,128)(2,1)S(1)}, u32[]{:S(2)}, u32[]{:S(2)}) collective-permute-start(bf16[8,32,128]{2,0,1:T(8,128)(2,1)S(1)} %convolution_convert_fusion.9), channel_id=1, source_target_pairs={{0,4},{4,0},{8,12},{12,8},{16,20},{20,16},{24,28},{28,24},{1,5},{5... | collective-permute-start | bytes 196616 | tf_op jit(solution)/shard_map/ppermute | solution.py:18
  103.9 8.9 %all_to_all.23 = f32[32,2,32]{2,1,0:T(2,128)S(1)} all-to-all(f32[32,2,32]{2,1,0:T(2,128)S(1)} %broadcast_in_dim.135), channel_id=1, replica_groups=mesh['dom'=8,'rep'=4] {'dom','rep'}, dimensions={0} | all-to-all | bytes 16384 | tf_op jit(solution)/shard_map/all_to_all | solution.py:24
  (162 shorter events, 35.4 us)
Async XLA Ops:
  3.0 19.4 %collective-permute-start.6 = (bf16[8,128,128]{2,0,1:T(8,128)(2,1)S(1)}, bf16[8,128,128]{2,0,1:T(8,128)(2,1)S(1)}, u32[]{:S(2)}, u32[]{:S(2)}) collective-permute-start(bf16[8,128,128]{2,0,1:T(8,128)(2,1)S(1)} %select_bitcast_fusion), channel_id=1, source_target_pairs={{0,3},{1,0},{2,1},{3,2},{4,7},{5,4},{6,5},{7,6},{8,11},{9,8},{10,9... | collective-permute-start | bytes 786440 | tf_op jit(solution)/shard_map/ppermute | solution.py:14
  5.4 16.5 %copy-start.4 = (bf16[1,128,128]{2,1,0:T(8,128)(2,1)S(1)}, bf16[1,128,128]{2,1,0:T(8,128)(2,1)}, u32[]{:S(2)}) copy-start(bf16[1,128,128]{2,1,0:T(8,128)(2,1)} %param.19) | copy-start | bytes 98308
  5.6 16.9 %collective-permute-start.5 = (bf16[8,128,128]{2,0,1:T(8,128)(2,1)S(1)}, bf16[8,128,128]{2,0,1:T(8,128)(2,1)S(1)}, u32[]{:S(2)}, u32[]{:S(2)}) collective-permute-start(bf16[8,128,128]{2,0,1:T(8,128)(2,1)S(1)} %get-tuple-element.86), channel_id=1, source_target_pairs={{0,2},{1,3},{2,0},{3,1},{4,6},{5,7},{6,4},{7,5},{8,10},{9,11},{10,... | collective-permute-start | bytes 786440 | tf_op jit(solution)/shard_map/ppermute | solution.py:14
  6.6 8.4 %collective-permute-start.2 = (s32[8,2]{0,1:T(2,128)S(1)}, s32[8,2]{0,1:T(2,128)S(1)}, u32[]{:S(2)}, u32[]{:S(2)}) collective-permute-start(s32[8,2]{0,1:T(2,128)S(1)} %bitcast.331), channel_id=1, source_target_pairs={{0,3},{1,0},{2,1},{3,2},{4,7},{5,4},{6,5},{7,6},{8,11},{9,8},{10,9... | collective-permute-start | bytes 200 | tf_op jit(solution)/shard_map/ppermute | solution.py:14
  6.7 9.5 %collective-permute-start.1 = (s32[8,2]{0,1:T(2,128)S(1)}, s32[8,2]{0,1:T(2,128)S(1)}, u32[]{:S(2)}, u32[]{:S(2)}) collective-permute-start(s32[8,2]{0,1:T(2,128)S(1)} %bitcast.330), channel_id=1, source_target_pairs={{0,2},{1,3},{2,0},{3,1},{4,6},{5,7},{6,4},{7,5},{8,10},{9,11},{10,... | collective-permute-start | bytes 200 | tf_op jit(solution)/shard_map/ppermute | solution.py:14
  8.5 13.6 %collective-permute-start.3 = (bf16[8,32,128]{2,0,1:T(8,128)(2,1)S(1)}, bf16[8,32,128]{2,0,1:T(8,128)(2,1)S(1)}, u32[]{:S(2)}, u32[]{:S(2)}) collective-permute-start(bf16[8,32,128]{2,0,1:T(8,128)(2,1)S(1)} %multiply_convert_fusion), channel_id=1, source_target_pairs={{0,4},{4,0},{8,12},{12,8},{16,20},{20,16},{24,28},{28,24},{1,5},{5... | collective-permute-start | bytes 196616 | tf_op jit(solution)/shard_map/ppermute | solution.py:18
  15.0 3.4 %collective-permute-start = (s32[8,2]{0,1:T(2,128)S(1)}, s32[8,2]{0,1:T(2,128)S(1)}, u32[]{:S(2)}, u32[]{:S(2)}) collective-permute-start(s32[8,2]{0,1:T(2,128)S(1)} %bitcast.329), channel_id=1, source_target_pairs={{0,1},{1,2},{2,3},{3,0},{4,5},{5,6},{6,7},{7,4},{8,9},{9,10},{10,1... | collective-permute-start | bytes 200 | tf_op jit(solution)/shard_map/ppermute | solution.py:14
  16.1 6.3 %collective-permute-start.4 = (bf16[8,128,128]{2,0,1:T(8,128)(2,1)S(1)}, bf16[8,128,128]{2,0,1:T(8,128)(2,1)S(1)}, u32[]{:S(2)}, u32[]{:S(2)}) collective-permute-start(bf16[8,128,128]{2,0,1:T(8,128)(2,1)S(1)} %get-tuple-element.85), channel_id=1, source_target_pairs={{0,1},{1,2},{2,3},{3,0},{4,5},{5,6},{6,7},{7,4},{8,9},{9,10},{10,1... | collective-permute-start | bytes 786440 | tf_op jit(solution)/shard_map/ppermute | solution.py:14
  18.4 3.6 %collective-permute-start.7 = (bf16[32,128]{1,0:T(8,128)(2,1)S(1)}, bf16[32,128]{1,0:T(8,128)(2,1)S(1)}, u32[]{:S(2)}, u32[]{:S(2)}) collective-permute-start(bf16[32,128]{1,0:T(8,128)(2,1)S(1)} %bitcast.310), channel_id=1, source_target_pairs={{0,1},{1,2},{2,3},{3,0},{4,5},{5,6},{6,7},{7,4},{8,9},{9,10},{10,1... | collective-permute-start | bytes 24584 | tf_op jit(solution)/shard_map/ppermute | solution.py:14
  24.4 4.3 %collective-permute-start.9 = (bf16[8,32,128]{2,0,1:T(8,128)(2,1)S(1)}, bf16[8,32,128]{2,0,1:T(8,128)(2,1)S(1)}, u32[]{:S(2)}, u32[]{:S(2)}) collective-permute-start(bf16[8,32,128]{2,0,1:T(8,128)(2,1)S(1)} %convolution_convert_fusion.12), channel_id=1, source_target_pairs={{0,4},{4,0},{8,12},{12,8},{16,20},{20,16},{24,28},{28,24},{1,5},{5... | collective-permute-start | bytes 196616 | tf_op jit(solution)/shard_map/ppermute | solution.py:18
  26.7 1.5 %collective-permute-start.8 = (f32[32,128]{1,0:T(8,128)S(1)}, f32[32,128]{1,0:T(8,128)S(1)}, u32[]{:S(2)}, u32[]{:S(2)}) collective-permute-start(f32[32,128]{1,0:T(8,128)S(1)} %fusion.93), channel_id=1, source_target_pairs={{0,3},{1,0},{2,1},{3,2},{4,7},{5,4},{6,5},{7,6},{8,11},{9,8},{10,9... | collective-permute-start | bytes 49160 | tf_op jit(solution)/shard_map/ppermute | solution.py:14
  44.0 4.3 %collective-permute-start.10 = (bf16[8,32,128]{2,0,1:T(8,128)(2,1)S(1)}, bf16[8,32,128]{2,0,1:T(8,128)(2,1)S(1)}, u32[]{:S(2)}, u32[]{:S(2)}) collective-permute-start(bf16[8,32,128]{2,0,1:T(8,128)(2,1)S(1)} %get-tuple-element.19), channel_id=1, source_target_pairs={{0,4},{4,0},{8,12},{12,8},{16,20},{20,16},{24,28},{28,24},{1,5},{5... | collective-permute-start | bytes 196616 | tf_op jit(solution)/shard_map/ppermute | solution.py:18
  44.6 3.1 %collective-permute-start.11 = (bf16[32,128]{1,0:T(8,128)(2,1)S(1)}, bf16[32,128]{1,0:T(8,128)(2,1)S(1)}, u32[]{:S(2)}, u32[]{:S(2)}) collective-permute-start(bf16[32,128]{1,0:T(8,128)(2,1)S(1)} %bitcast.312), channel_id=1, source_target_pairs={{0,1},{1,2},{2,3},{3,0},{4,5},{5,6},{6,7},{7,4},{8,9},{9,10},{10,1... | collective-permute-start | bytes 24584 | tf_op jit(solution)/shard_map/ppermute | solution.py:14
  52.1 4.3 %collective-permute-start.13 = (bf16[8,32,128]{2,0,1:T(8,128)(2,1)S(1)}, bf16[8,32,128]{2,0,1:T(8,128)(2,1)S(1)}, u32[]{:S(2)}, u32[]{:S(2)}) collective-permute-start(bf16[8,32,128]{2,0,1:T(8,128)(2,1)S(1)} %convolution_convert_fusion.11), channel_id=1, source_target_pairs={{0,4},{4,0},{8,12},{12,8},{16,20},{20,16},{24,28},{28,24},{1,5},{5... | collective-permute-start | bytes 196616 | tf_op jit(solution)/shard_map/ppermute | solution.py:18
  54.0 1.5 %collective-permute-start.12 = (f32[32,128]{1,0:T(8,128)S(1)}, f32[32,128]{1,0:T(8,128)S(1)}, u32[]{:S(2)}, u32[]{:S(2)}) collective-permute-start(f32[32,128]{1,0:T(8,128)S(1)} %fusion.89), channel_id=1, source_target_pairs={{0,3},{1,0},{2,1},{3,2},{4,7},{5,4},{6,5},{7,6},{8,11},{9,8},{10,9... | collective-permute-start | bytes 49160 | tf_op jit(solution)/shard_map/ppermute | solution.py:14
  67.3 4.3 %collective-permute-start.14 = (bf16[8,32,128]{2,0,1:T(8,128)(2,1)S(1)}, bf16[8,32,128]{2,0,1:T(8,128)(2,1)S(1)}, u32[]{:S(2)}, u32[]{:S(2)}) collective-permute-start(bf16[8,32,128]{2,0,1:T(8,128)(2,1)S(1)} %get-tuple-element.22), channel_id=1, source_target_pairs={{0,4},{4,0},{8,12},{12,8},{16,20},{20,16},{24,28},{28,24},{1,5},{5... | collective-permute-start | bytes 196616 | tf_op jit(solution)/shard_map/ppermute | solution.py:18
  67.9 3.3 %collective-permute-start.15 = (bf16[32,128]{1,0:T(8,128)(2,1)S(1)}, bf16[32,128]{1,0:T(8,128)(2,1)S(1)}, u32[]{:S(2)}, u32[]{:S(2)}) collective-permute-start(bf16[32,128]{1,0:T(8,128)(2,1)S(1)} %bitcast.313), channel_id=1, source_target_pairs={{0,1},{1,2},{2,3},{3,0},{4,5},{5,6},{6,7},{7,4},{8,9},{9,10},{10,1... | collective-permute-start | bytes 24584 | tf_op jit(solution)/shard_map/ppermute | solution.py:14
  75.5 4.3 %collective-permute-start.17 = (bf16[8,32,128]{2,0,1:T(8,128)(2,1)S(1)}, bf16[8,32,128]{2,0,1:T(8,128)(2,1)S(1)}, u32[]{:S(2)}, u32[]{:S(2)}) collective-permute-start(bf16[8,32,128]{2,0,1:T(8,128)(2,1)S(1)} %convolution_convert_fusion.10), channel_id=1, source_target_pairs={{0,4},{4,0},{8,12},{12,8},{16,20},{20,16},{24,28},{28,24},{1,5},{5... | collective-permute-start | bytes 196616 | tf_op jit(solution)/shard_map/ppermute | solution.py:18
  77.5 1.5 %collective-permute-start.16 = (f32[32,128]{1,0:T(8,128)S(1)}, f32[32,128]{1,0:T(8,128)S(1)}, u32[]{:S(2)}, u32[]{:S(2)}) collective-permute-start(f32[32,128]{1,0:T(8,128)S(1)} %fusion.85), channel_id=1, source_target_pairs={{0,3},{1,0},{2,1},{3,2},{4,7},{5,4},{6,5},{7,6},{8,11},{9,8},{10,9... | collective-permute-start | bytes 49160 | tf_op jit(solution)/shard_map/ppermute | solution.py:14
  90.6 4.3 %collective-permute-start.18 = (bf16[8,32,128]{2,0,1:T(8,128)(2,1)S(1)}, bf16[8,32,128]{2,0,1:T(8,128)(2,1)S(1)}, u32[]{:S(2)}, u32[]{:S(2)}) collective-permute-start(bf16[8,32,128]{2,0,1:T(8,128)(2,1)S(1)} %get-tuple-element.25), channel_id=1, source_target_pairs={{0,4},{4,0},{8,12},{12,8},{16,20},{20,16},{24,28},{28,24},{1,5},{5... | collective-permute-start | bytes 196616 | tf_op jit(solution)/shard_map/ppermute | solution.py:18
  91.6 3.1 %collective-permute-start.19 = (bf16[32,128]{1,0:T(8,128)(2,1)S(1)}, bf16[32,128]{1,0:T(8,128)(2,1)S(1)}, u32[]{:S(2)}, u32[]{:S(2)}) collective-permute-start(bf16[32,128]{1,0:T(8,128)(2,1)S(1)} %bitcast.311), channel_id=1, source_target_pairs={{0,1},{1,2},{2,3},{3,0},{4,5},{5,6},{6,7},{7,4},{8,9},{9,10},{10,1... | collective-permute-start | bytes 24584 | tf_op jit(solution)/shard_map/ppermute | solution.py:14
  98.8 4.3 %collective-permute-start.21 = (bf16[8,32,128]{2,0,1:T(8,128)(2,1)S(1)}, bf16[8,32,128]{2,0,1:T(8,128)(2,1)S(1)}, u32[]{:S(2)}, u32[]{:S(2)}) collective-permute-start(bf16[8,32,128]{2,0,1:T(8,128)(2,1)S(1)} %convolution_convert_fusion.9), channel_id=1, source_target_pairs={{0,4},{4,0},{8,12},{12,8},{16,20},{20,16},{24,28},{28,24},{1,5},{5... | collective-permute-start | bytes 196616 | tf_op jit(solution)/shard_map/ppermute | solution.py:18
  101.0 1.5 %collective-permute-start.20 = (f32[32,128]{1,0:T(8,128)S(1)}, f32[32,128]{1,0:T(8,128)S(1)}, u32[]{:S(2)}, u32[]{:S(2)}) collective-permute-start(f32[32,128]{1,0:T(8,128)S(1)} %fusion.81), channel_id=1, source_target_pairs={{0,3},{1,0},{2,1},{3,2},{4,7},{5,4},{6,5},{7,6},{8,11},{9,8},{10,9... | collective-permute-start | bytes 49160 | tf_op jit(solution)/shard_map/ppermute | solution.py:14
  101.3 11.6 %copy-start.6 = (f32[8,32,128]{2,0,1:T(8,128)S(1)}, f32[8,32,128]{2,0,1:T(8,128)}, u32[]{:S(2)}) copy-start(f32[8,32,128]{2,0,1:T(8,128)} %copy-done.5) | copy-start | bytes 393220
  (10 other events, 40.0 us)

commit v21 on v20

--- a/solution.py
+++ b/solution.py
@@ -44,9 +44,9 @@
     nodes = vector.shape[0]
     rounded = vector.astype(jnp.bfloat16)
     before = from_behind(rounded[nodes - 1], "rep", 1)
-    other = partner(rounded, "dom", 0).astype(vector.dtype)
+    other = partner(rounded, "dom", 0)
     near = jnp.einsum("sn,nrk->srk", near_onehot, vector, precision=lax.Precision.HIGHEST)
-    far = jnp.einsum("sn,nrk->srk", far_onehot, other, precision=lax.Precision.HIGHEST)
+    far = jnp.einsum("sn,nrk->srk", far_onehot, other, preferred_element_type=jnp.float32)
     difference = (near - far).astype(jnp.bfloat16)
     multiplier = jnp.einsum(
         "srk,skj->srj", difference, contact_set, preferred_element_type=jnp.float32
@@ -120,7 +120,7 @@
         mirror_onehot.astype(jnp.bfloat16),
         mirror_onehot,
         near_collect,
-        far_collect,
+        far_collect.astype(jnp.bfloat16),
         near_collect,
         far_collect,
     )

time: 115 us -> 115 us (level)
  no operation moved by 1% of the time
where the time goes in v21:
time: 115 us; the launch traced here: 114 us
  blocking collectives  39.4 us (34%)
  waiting for transfers between devices  24.6 us (21%)
  matrix products  24.4 us (21%)
  starting transfers between devices  15.4 us (13%)
  other arithmetic  5.98 us (5%)
  local copies, waits for them, and re-layouts  3.38 us (3%)
  between operations  1.28 us (1%)
    all_to_all x4, blocking collectives, total(): gathered = lax.all_to_all(spread, ('dom', 'rep'), 0, 0, tiled=True)  39.4 us
    ppermute x14, waiting for transfers between devices, from_behind(): return lax.ppermute(value, axis, pairs)  20.9 us
    ppermute x8, starting transfers between devices, partner(): lax.ppermute(value, axis, [(i, i ^ 1 << distance) for i in range(lax.axis...  8.9 us
    dot_general x4, matrix products, apply_operator(): jnp.einsum('srj,skj->srk', multiplier, contact_set, preferred_element_typ...  6.53 us
    ppermute x14, starting transfers between devices, from_behind(): return lax.ppermute(value, axis, pairs)  6.46 us
    ppermute x8, waiting for transfers between devices, partner(): lax.ppermute(value, axis, [(i, i ^ 1 << distance) for i in range(lax.axis...  3.71 us
    dot_general x4, matrix products, local_stiffness(): jnp.einsum('pn,prj->nrj', mirror_onehot, mirror, precision=lax.Precision....  3.2 us
    dot_general x4, matrix products, apply_operator(): jnp.einsum('sn,nrk->srk', far_onehot, other, preferred_element_type=jnp.f...  3.16 us
  transfers between devices with their start and end apart: 22, of which 16 were waited for; matrix products, arithmetic and copies ran while one was open for 8% of the time, Pallas kernels for 0%

profile of v21, /device:TPU:0, one launch (start us, length us, event | category | flops | bytes accessed | tf_op | source)
XLA Modules:
  0.0 114.5 jit_solution(16214104456944019828)
XLA Ops:
  3.0 2.4 %collective-permute-start.6 = (bf16[8,128,128]{2,0,1:T(8,128)(2,1)S(1)}, bf16[8,128,128]{2,0,1:T(8,128)(2,1)S(1)}, u32[]{:S(2)}, u32[]{:S(2)}) collective-permute-start(bf16[8,128,128]{2,0,1:T(8,128)(2,1)S(1)} %select_bitcast_fusion), channel_id=1, source_target_pairs={{0,3},{1,0},{2,1},{3,2},{4,7},{5,4},{6,5},{7,6},{8,11},{9,8},{10,9... | collective-permute-start | bytes 786440 | tf_op jit(solution)/shard_map/ppermute | solution.py:14
  6.7 1.7 %collective-permute-start.1 = (s32[8,2]{0,1:T(2,128)S(1)}, s32[8,2]{0,1:T(2,128)S(1)}, u32[]{:S(2)}, u32[]{:S(2)}) collective-permute-start(s32[8,2]{0,1:T(2,128)S(1)} %bitcast.332), channel_id=1, source_target_pairs={{0,2},{1,3},{2,0},{3,1},{4,6},{5,7},{6,4},{7,5},{8,10},{9,11},{10,... | collective-permute-start | bytes 200 | tf_op jit(solution)/shard_map/ppermute | solution.py:14
  8.5 1.6 %collective-permute-start.3 = (bf16[8,32,128]{2,0,1:T(8,128)(2,1)S(1)}, bf16[8,32,128]{2,0,1:T(8,128)(2,1)S(1)}, u32[]{:S(2)}, u32[]{:S(2)}) collective-permute-start(bf16[8,32,128]{2,0,1:T(8,128)(2,1)S(1)} %multiply_convert_fusion), channel_id=1, source_target_pairs={{0,4},{4,0},{8,12},{12,8},{16,20},{20,16},{24,28},{28,24},{1,5},{5... | collective-permute-start | bytes 196616 | tf_op jit(solution)/shard_map/ppermute | solution.py:18
  10.4 4.6 %collective-permute-done.2 = s32[8,2]{0,1:T(2,128)S(1)} collective-permute-done((s32[8,2]{0,1:T(2,128)S(1)}, s32[8,2]{0,1:T(2,128)S(1)}, u32[]{:S(2)}, u32[]{:S(2)}) %collective-permute-start.2) | collective-permute-done | bytes 96 | tf_op jit(solution)/shard_map/ppermute | solution.py:14
  15.0 1.1 collective-permute-start
  16.1 2.3 %collective-permute-done = s32[8,2]{0,1:T(2,128)S(1)} collective-permute-done((s32[8,2]{0,1:T(2,128)S(1)}, s32[8,2]{0,1:T(2,128)S(1)}, u32[]{:S(2)}, u32[]{:S(2)}) %collective-permute-start) | collective-permute-done | bytes 96 | tf_op jit(solution)/shard_map/ppermute | solution.py:14
  19.0 3.0 %collective-permute-done.7 = bf16[32,128]{1,0:T(8,128)(2,1)S(1)} collective-permute-done((bf16[32,128]{1,0:T(8,128)(2,1)S(1)}, bf16[32,128]{1,0:T(8,128)(2,1)S(1)}, u32[]{:S(2)}, u32[]{:S(2)}) %collective-permute-start.7) | collective-permute-done | bytes 8224 | tf_op jit(solution)/shard_map/ppermute | solution.py:14
  24.4 1.6 %collective-permute-start.9 = (bf16[8,32,128]{2,0,1:T(8,128)(2,1)S(1)}, bf16[8,32,128]{2,0,1:T(8,128)(2,1)S(1)}, u32[]{:S(2)}, u32[]{:S(2)}) collective-permute-start(bf16[8,32,128]{2,0,1:T(8,128)(2,1)S(1)} %convolution_convert_fusion.12), channel_id=1, source_target_pairs={{0,4},{4,0},{8,12},{12,8},{16,20},{20,16},{24,28},{28,24},{1,5},{5... | collective-permute-start | bytes 196616 | tf_op jit(solution)/shard_map/ppermute | solution.py:18
  29.7 12.8 %all_to_all.20 = f32[32,1,128]{2,1,0:T(1,128)S(1)} all-to-all(f32[32,1,128]{2,1,0:T(1,128)S(1)} %reshape.364), channel_id=1, replica_groups=mesh['dom'=8,'rep'=4] {'dom','rep'}, dimensions={0} | all-to-all | bytes 32768 | tf_op jit(solution)/shard_map/all_to_all | solution.py:24
  45.1 2.6 %collective-permute-done.11 = bf16[32,128]{1,0:T(8,128)(2,1)S(1)} collective-permute-done((bf16[32,128]{1,0:T(8,128)(2,1)S(1)}, bf16[32,128]{1,0:T(8,128)(2,1)S(1)}, u32[]{:S(2)}, u32[]{:S(2)}) %collective-permute-start.11) | collective-permute-done | bytes 8224 | tf_op jit(solution)/shard_map/ppermute | solution.py:14
  48.3 1.0 fusion.2
  49.2 1.9 %fusion.6 = f32[32,32,128]{2,1,0:T(8,128)S(1)} fusion(bf16[32,128,128]{2,1,0:T(8,128)(2,1)S(1)} %bitcast.286, bf16[32,32,128]{2,0,1:T(8,128)(2,1)} %fusion.2), kind=kOutput, calls=%fused_computation.15 | convolution fusion | flops 67239936 | bytes 1835008 | tf_op jit(solution)/shard_map/srj,skj->srk/dot_general | solution.py:54
  52.1 1.1 collective-permute-start.13
  55.4 1.0 collective-permute-done.13
  57.4 8.8 %all_to_all.21 = f32[32,1,128]{2,1,0:T(1,128)S(1)} all-to-all(f32[32,1,128]{2,1,0:T(1,128)S(1)} %reshape.366), channel_id=1, replica_groups=mesh['dom'=8,'rep'=4] {'dom','rep'}, dimensions={0} | all-to-all | bytes 32768 | tf_op jit(solution)/shard_map/all_to_all | solution.py:24
  68.6 2.6 %collective-permute-done.15 = bf16[32,128]{1,0:T(8,128)(2,1)S(1)} collective-permute-done((bf16[32,128]{1,0:T(8,128)(2,1)S(1)}, bf16[32,128]{1,0:T(8,128)(2,1)S(1)}, u32[]{:S(2)}, u32[]{:S(2)}) %collective-permute-start.15) | collective-permute-done | bytes 8224 | tf_op jit(solution)/shard_map/ppermute | solution.py:14
  72.6 1.9 %fusion.7 = f32[32,32,128]{2,1,0:T(8,128)S(1)} fusion(bf16[32,128,128]{2,1,0:T(8,128)(2,1)S(1)} %bitcast.287, bf16[32,32,128]{2,0,1:T(8,128)(2,1)} %fusion.3), kind=kOutput, calls=%fused_computation.16 | convolution fusion | flops 67239936 | bytes 1835008 | tf_op jit(solution)/shard_map/srj,skj->srk/dot_general | solution.py:54
  75.5 1.3 %collective-permute-start.17 = (bf16[8,32,128]{2,0,1:T(8,128)(2,1)S(1)}, bf16[8,32,128]{2,0,1:T(8,128)(2,1)S(1)}, u32[]{:S(2)}, u32[]{:S(2)}) collective-permute-start(bf16[8,32,128]{2,0,1:T(8,128)(2,1)S(1)} %convolution_convert_fusion.10), channel_id=1, source_target_pairs={{0,4},{4,0},{8,12},{12,8},{16,20},{20,16},{24,28},{28,24},{1,5},{5... | collective-permute-start | bytes 196616 | tf_op jit(solution)/shard_map/ppermute | solution.py:18
  80.7 8.8 %all_to_all.22 = f32[32,1,128]{2,1,0:T(1,128)S(1)} all-to-all(f32[32,1,128]{2,1,0:T(1,128)S(1)} %reshape.368), channel_id=1, replica_groups=mesh['dom'=8,'rep'=4] {'dom','rep'}, dimensions={0} | all-to-all | bytes 32768 | tf_op jit(solution)/shard_map/all_to_all | solution.py:24
  92.5 2.2 %collective-permute-done.19 = bf16[32,128]{1,0:T(8,128)(2,1)S(1)} collective-permute-done((bf16[32,128]{1,0:T(8,128)(2,1)S(1)}, bf16[32,128]{1,0:T(8,128)(2,1)S(1)}, u32[]{:S(2)}, u32[]{:S(2)}) %collective-permute-start.19) | collective-permute-done | bytes 8224 | tf_op jit(solution)/shard_map/ppermute | solution.py:14
  94.9 1.0 fusion.4
  95.9 1.9 %fusion.8 = f32[32,32,128]{2,1,0:T(8,128)S(1)} fusion(bf16[32,128,128]{2,1,0:T(8,128)(2,1)S(1)} %bitcast.288, bf16[32,32,128]{2,0,1:T(8,128)(2,1)} %fusion.4), kind=kOutput, calls=%fused_computation.17 | convolution fusion | flops 67239936 | bytes 1835008 | tf_op jit(solution)/shard_map/srj,skj->srk/dot_general | solution.py:54
  98.8 1.5 %collective-permute-start.21 = (bf16[8,32,128]{2,0,1:T(8,128)(2,1)S(1)}, bf16[8,32,128]{2,0,1:T(8,128)(2,1)S(1)}, u32[]{:S(2)}, u32[]{:S(2)}) collective-permute-start(bf16[8,32,128]{2,0,1:T(8,128)(2,1)S(1)} %convolution_convert_fusion.9), channel_id=1, source_target_pairs={{0,4},{4,0},{8,12},{12,8},{16,20},{20,16},{24,28},{28,24},{1,5},{5... | collective-permute-start | bytes 196616 | tf_op jit(solution)/shard_map/ppermute | solution.py:18
  103.9 8.9 %all_to_all.23 = f32[32,2,32]{2,1,0:T(2,128)S(1)} all-to-all(f32[32,2,32]{2,1,0:T(2,128)S(1)} %broadcast_in_dim.135), channel_id=1, replica_groups=mesh['dom'=8,'rep'=4] {'dom','rep'}, dimensions={0} | all-to-all | bytes 16384 | tf_op jit(solution)/shard_map/all_to_all | solution.py:24
  (162 shorter events, 35.4 us)
Async XLA Ops:
  3.0 19.4 %collective-permute-start.6 = (bf16[8,128,128]{2,0,1:T(8,128)(2,1)S(1)}, bf16[8,128,128]{2,0,1:T(8,128)(2,1)S(1)}, u32[]{:S(2)}, u32[]{:S(2)}) collective-permute-start(bf16[8,128,128]{2,0,1:T(8,128)(2,1)S(1)} %select_bitcast_fusion), channel_id=1, source_target_pairs={{0,3},{1,0},{2,1},{3,2},{4,7},{5,4},{6,5},{7,6},{8,11},{9,8},{10,9... | collective-permute-start | bytes 786440 | tf_op jit(solution)/shard_map/ppermute | solution.py:14
  5.4 16.5 %copy-start.4 = (bf16[1,128,128]{2,1,0:T(8,128)(2,1)S(1)}, bf16[1,128,128]{2,1,0:T(8,128)(2,1)}, u32[]{:S(2)}) copy-start(bf16[1,128,128]{2,1,0:T(8,128)(2,1)} %param.19) | copy-start | bytes 98308
  5.6 16.9 %collective-permute-start.5 = (bf16[8,128,128]{2,0,1:T(8,128)(2,1)S(1)}, bf16[8,128,128]{2,0,1:T(8,128)(2,1)S(1)}, u32[]{:S(2)}, u32[]{:S(2)}) collective-permute-start(bf16[8,128,128]{2,0,1:T(8,128)(2,1)S(1)} %get-tuple-element.86), channel_id=1, source_target_pairs={{0,2},{1,3},{2,0},{3,1},{4,6},{5,7},{6,4},{7,5},{8,10},{9,11},{10,... | collective-permute-start | bytes 786440 | tf_op jit(solution)/shard_map/ppermute | solution.py:14
  6.6 8.4 %collective-permute-start.2 = (s32[8,2]{0,1:T(2,128)S(1)}, s32[8,2]{0,1:T(2,128)S(1)}, u32[]{:S(2)}, u32[]{:S(2)}) collective-permute-start(s32[8,2]{0,1:T(2,128)S(1)} %bitcast.333), channel_id=1, source_target_pairs={{0,3},{1,0},{2,1},{3,2},{4,7},{5,4},{6,5},{7,6},{8,11},{9,8},{10,9... | collective-permute-start | bytes 200 | tf_op jit(solution)/shard_map/ppermute | solution.py:14
  6.7 9.5 %collective-permute-start.1 = (s32[8,2]{0,1:T(2,128)S(1)}, s32[8,2]{0,1:T(2,128)S(1)}, u32[]{:S(2)}, u32[]{:S(2)}) collective-permute-start(s32[8,2]{0,1:T(2,128)S(1)} %bitcast.332), channel_id=1, source_target_pairs={{0,2},{1,3},{2,0},{3,1},{4,6},{5,7},{6,4},{7,5},{8,10},{9,11},{10,... | collective-permute-start | bytes 200 | tf_op jit(solution)/shard_map/ppermute | solution.py:14
  8.5 13.6 %collective-permute-start.3 = (bf16[8,32,128]{2,0,1:T(8,128)(2,1)S(1)}, bf16[8,32,128]{2,0,1:T(8,128)(2,1)S(1)}, u32[]{:S(2)}, u32[]{:S(2)}) collective-permute-start(bf16[8,32,128]{2,0,1:T(8,128)(2,1)S(1)} %multiply_convert_fusion), channel_id=1, source_target_pairs={{0,4},{4,0},{8,12},{12,8},{16,20},{20,16},{24,28},{28,24},{1,5},{5... | collective-permute-start | bytes 196616 | tf_op jit(solution)/shard_map/ppermute | solution.py:18
  15.0 3.4 %collective-permute-start = (s32[8,2]{0,1:T(2,128)S(1)}, s32[8,2]{0,1:T(2,128)S(1)}, u32[]{:S(2)}, u32[]{:S(2)}) collective-permute-start(s32[8,2]{0,1:T(2,128)S(1)} %bitcast.331), channel_id=1, source_target_pairs={{0,1},{1,2},{2,3},{3,0},{4,5},{5,6},{6,7},{7,4},{8,9},{9,10},{10,1... | collective-permute-start | bytes 200 | tf_op jit(solution)/shard_map/ppermute | solution.py:14
  16.1 6.3 %collective-permute-start.4 = (bf16[8,128,128]{2,0,1:T(8,128)(2,1)S(1)}, bf16[8,128,128]{2,0,1:T(8,128)(2,1)S(1)}, u32[]{:S(2)}, u32[]{:S(2)}) collective-permute-start(bf16[8,128,128]{2,0,1:T(8,128)(2,1)S(1)} %get-tuple-element.85), channel_id=1, source_target_pairs={{0,1},{1,2},{2,3},{3,0},{4,5},{5,6},{6,7},{7,4},{8,9},{9,10},{10,1... | collective-permute-start | bytes 786440 | tf_op jit(solution)/shard_map/ppermute | solution.py:14
  18.4 3.6 %collective-permute-start.7 = (bf16[32,128]{1,0:T(8,128)(2,1)S(1)}, bf16[32,128]{1,0:T(8,128)(2,1)S(1)}, u32[]{:S(2)}, u32[]{:S(2)}) collective-permute-start(bf16[32,128]{1,0:T(8,128)(2,1)S(1)} %bitcast.312), channel_id=1, source_target_pairs={{0,1},{1,2},{2,3},{3,0},{4,5},{5,6},{6,7},{7,4},{8,9},{9,10},{10,1... | collective-permute-start | bytes 24584 | tf_op jit(solution)/shard_map/ppermute | solution.py:14
  24.4 4.3 %collective-permute-start.9 = (bf16[8,32,128]{2,0,1:T(8,128)(2,1)S(1)}, bf16[8,32,128]{2,0,1:T(8,128)(2,1)S(1)}, u32[]{:S(2)}, u32[]{:S(2)}) collective-permute-start(bf16[8,32,128]{2,0,1:T(8,128)(2,1)S(1)} %convolution_convert_fusion.12), channel_id=1, source_target_pairs={{0,4},{4,0},{8,12},{12,8},{16,20},{20,16},{24,28},{28,24},{1,5},{5... | collective-permute-start | bytes 196616 | tf_op jit(solution)/shard_map/ppermute | solution.py:18
  26.7 1.5 %collective-permute-start.8 = (f32[32,128]{1,0:T(8,128)S(1)}, f32[32,128]{1,0:T(8,128)S(1)}, u32[]{:S(2)}, u32[]{:S(2)}) collective-permute-start(f32[32,128]{1,0:T(8,128)S(1)} %fusion.93), channel_id=1, source_target_pairs={{0,3},{1,0},{2,1},{3,2},{4,7},{5,4},{6,5},{7,6},{8,11},{9,8},{10,9... | collective-permute-start | bytes 49160 | tf_op jit(solution)/shard_map/ppermute | solution.py:14
  43.9 4.3 %collective-permute-start.10 = (bf16[8,32,128]{2,0,1:T(8,128)(2,1)S(1)}, bf16[8,32,128]{2,0,1:T(8,128)(2,1)S(1)}, u32[]{:S(2)}, u32[]{:S(2)}) collective-permute-start(bf16[8,32,128]{2,0,1:T(8,128)(2,1)S(1)} %get-tuple-element.19), channel_id=1, source_target_pairs={{0,4},{4,0},{8,12},{12,8},{16,20},{20,16},{24,28},{28,24},{1,5},{5... | collective-permute-start | bytes 196616 | tf_op jit(solution)/shard_map/ppermute | solution.py:18
  44.6 3.1 %collective-permute-start.11 = (bf16[32,128]{1,0:T(8,128)(2,1)S(1)}, bf16[32,128]{1,0:T(8,128)(2,1)S(1)}, u32[]{:S(2)}, u32[]{:S(2)}) collective-permute-start(bf16[32,128]{1,0:T(8,128)(2,1)S(1)} %bitcast.314), channel_id=1, source_target_pairs={{0,1},{1,2},{2,3},{3,0},{4,5},{5,6},{6,7},{7,4},{8,9},{9,10},{10,1... | collective-permute-start | bytes 24584 | tf_op jit(solution)/shard_map/ppermute | solution.py:14
  52.1 4.3 %collective-permute-start.13 = (bf16[8,32,128]{2,0,1:T(8,128)(2,1)S(1)}, bf16[8,32,128]{2,0,1:T(8,128)(2,1)S(1)}, u32[]{:S(2)}, u32[]{:S(2)}) collective-permute-start(bf16[8,32,128]{2,0,1:T(8,128)(2,1)S(1)} %convolution_convert_fusion.11), channel_id=1, source_target_pairs={{0,4},{4,0},{8,12},{12,8},{16,20},{20,16},{24,28},{28,24},{1,5},{5... | collective-permute-start | bytes 196616 | tf_op jit(solution)/shard_map/ppermute | solution.py:18
  54.0 1.5 %collective-permute-start.12 = (f32[32,128]{1,0:T(8,128)S(1)}, f32[32,128]{1,0:T(8,128)S(1)}, u32[]{:S(2)}, u32[]{:S(2)}) collective-permute-start(f32[32,128]{1,0:T(8,128)S(1)} %fusion.89), channel_id=1, source_target_pairs={{0,3},{1,0},{2,1},{3,2},{4,7},{5,4},{6,5},{7,6},{8,11},{9,8},{10,9... | collective-permute-start | bytes 49160 | tf_op jit(solution)/shard_map/ppermute | solution.py:14
  67.3 4.3 %collective-permute-start.14 = (bf16[8,32,128]{2,0,1:T(8,128)(2,1)S(1)}, bf16[8,32,128]{2,0,1:T(8,128)(2,1)S(1)}, u32[]{:S(2)}, u32[]{:S(2)}) collective-permute-start(bf16[8,32,128]{2,0,1:T(8,128)(2,1)S(1)} %get-tuple-element.22), channel_id=1, source_target_pairs={{0,4},{4,0},{8,12},{12,8},{16,20},{20,16},{24,28},{28,24},{1,5},{5... | collective-permute-start | bytes 196616 | tf_op jit(solution)/shard_map/ppermute | solution.py:18
  67.9 3.3 %collective-permute-start.15 = (bf16[32,128]{1,0:T(8,128)(2,1)S(1)}, bf16[32,128]{1,0:T(8,128)(2,1)S(1)}, u32[]{:S(2)}, u32[]{:S(2)}) collective-permute-start(bf16[32,128]{1,0:T(8,128)(2,1)S(1)} %bitcast.315), channel_id=1, source_target_pairs={{0,1},{1,2},{2,3},{3,0},{4,5},{5,6},{6,7},{7,4},{8,9},{9,10},{10,1... | collective-permute-start | bytes 24584 | tf_op jit(solution)/shard_map/ppermute | solution.py:14
  75.5 4.3 %collective-permute-start.17 = (bf16[8,32,128]{2,0,1:T(8,128)(2,1)S(1)}, bf16[8,32,128]{2,0,1:T(8,128)(2,1)S(1)}, u32[]{:S(2)}, u32[]{:S(2)}) collective-permute-start(bf16[8,32,128]{2,0,1:T(8,128)(2,1)S(1)} %convolution_convert_fusion.10), channel_id=1, source_target_pairs={{0,4},{4,0},{8,12},{12,8},{16,20},{20,16},{24,28},{28,24},{1,5},{5... | collective-permute-start | bytes 196616 | tf_op jit(solution)/shard_map/ppermute | solution.py:18
  77.5 1.5 %collective-permute-start.16 = (f32[32,128]{1,0:T(8,128)S(1)}, f32[32,128]{1,0:T(8,128)S(1)}, u32[]{:S(2)}, u32[]{:S(2)}) collective-permute-start(f32[32,128]{1,0:T(8,128)S(1)} %fusion.85), channel_id=1, source_target_pairs={{0,3},{1,0},{2,1},{3,2},{4,7},{5,4},{6,5},{7,6},{8,11},{9,8},{10,9... | collective-permute-start | bytes 49160 | tf_op jit(solution)/shard_map/ppermute | solution.py:14
  90.6 4.3 %collective-permute-start.18 = (bf16[8,32,128]{2,0,1:T(8,128)(2,1)S(1)}, bf16[8,32,128]{2,0,1:T(8,128)(2,1)S(1)}, u32[]{:S(2)}, u32[]{:S(2)}) collective-permute-start(bf16[8,32,128]{2,0,1:T(8,128)(2,1)S(1)} %get-tuple-element.25), channel_id=1, source_target_pairs={{0,4},{4,0},{8,12},{12,8},{16,20},{20,16},{24,28},{28,24},{1,5},{5... | collective-permute-start | bytes 196616 | tf_op jit(solution)/shard_map/ppermute | solution.py:18
  91.6 3.1 %collective-permute-start.19 = (bf16[32,128]{1,0:T(8,128)(2,1)S(1)}, bf16[32,128]{1,0:T(8,128)(2,1)S(1)}, u32[]{:S(2)}, u32[]{:S(2)}) collective-permute-start(bf16[32,128]{1,0:T(8,128)(2,1)S(1)} %bitcast.313), channel_id=1, source_target_pairs={{0,1},{1,2},{2,3},{3,0},{4,5},{5,6},{6,7},{7,4},{8,9},{9,10},{10,1... | collective-permute-start | bytes 24584 | tf_op jit(solution)/shard_map/ppermute | solution.py:14
  98.8 4.3 %collective-permute-start.21 = (bf16[8,32,128]{2,0,1:T(8,128)(2,1)S(1)}, bf16[8,32,128]{2,0,1:T(8,128)(2,1)S(1)}, u32[]{:S(2)}, u32[]{:S(2)}) collective-permute-start(bf16[8,32,128]{2,0,1:T(8,128)(2,1)S(1)} %convolution_convert_fusion.9), channel_id=1, source_target_pairs={{0,4},{4,0},{8,12},{12,8},{16,20},{20,16},{24,28},{28,24},{1,5},{5... | collective-permute-start | bytes 196616 | tf_op jit(solution)/shard_map/ppermute | solution.py:18
  101.0 1.5 %collective-permute-start.20 = (f32[32,128]{1,0:T(8,128)S(1)}, f32[32,128]{1,0:T(8,128)S(1)}, u32[]{:S(2)}, u32[]{:S(2)}) collective-permute-start(f32[32,128]{1,0:T(8,128)S(1)} %fusion.81), channel_id=1, source_target_pairs={{0,3},{1,0},{2,1},{3,2},{4,7},{5,4},{6,5},{7,6},{8,11},{9,8},{10,9... | collective-permute-start | bytes 49160 | tf_op jit(solution)/shard_map/ppermute | solution.py:14
  101.3 11.6 %copy-start.6 = (f32[8,32,128]{2,0,1:T(8,128)S(1)}, f32[8,32,128]{2,0,1:T(8,128)}, u32[]{:S(2)}) copy-start(f32[8,32,128]{2,0,1:T(8,128)} %copy-done.5) | copy-start | bytes 393220
  (10 other events, 40.0 us)

commit v22 on v20

--- a/solution.py
+++ b/solution.py
@@ -40,7 +40,7 @@
 
 
 def apply_operator(vector, diag_tiles, off_tiles, link_tile, contact_set, tables):
-    cols_onehot, mirror_onehot, near_onehot, far_onehot, near_collect, far_collect = tables
+    cols_onehot, mirror_onehot, near_onehot, far_onehot, near_collect, far_pick = tables
     nodes = vector.shape[0]
     rounded = vector.astype(jnp.bfloat16)
     before = from_behind(rounded[nodes - 1], "rep", 1)
@@ -51,11 +51,12 @@
     multiplier = jnp.einsum(
         "srk,skj->srj", difference, contact_set, preferred_element_type=jnp.float32
     ).astype(jnp.bfloat16)
+    spread = far_pick[:, :, None, None] * multiplier[:, None, :, :]
+    far_sum = jnp.einsum("snrj,skj->nrk", spread, contact_set, preferred_element_type=jnp.float32)
+    far_sum, rounded, multiplier = lax.optimization_barrier(
+        (far_sum.astype(jnp.bfloat16), rounded, multiplier)
+    )
     terms = jnp.einsum("srj,skj->srk", multiplier, contact_set, preferred_element_type=jnp.float32)
-    far_sum = jnp.einsum("sn,srk->nrk", far_collect, terms, precision=lax.Precision.HIGHEST)
-    far_sum, rounded, terms = lax.optimization_barrier(
-        (far_sum.astype(jnp.bfloat16), rounded, terms)
-    )
     far_terms = partner(far_sum, "dom", 0).astype(jnp.float32)
     back_term = lax.dot_general(
         rounded[0], link_tile, (((1,), (1,)), ((), ())), preferred_element_type=jnp.float32
@@ -122,7 +123,7 @@
         near_collect,
         far_collect,
         near_collect,
-        far_collect,
+        far_collect.astype(jnp.bfloat16),
     )
     link_tile = link_tiles[0]
     scale = precond[:, None, :]

time: 115 us -> 110 us (0.957)
  matrix products: 24.4 us -> 20.8 us
  waiting for transfers between devices: 24.6 us -> 22.6 us
    dot_general x4, matrix products: 6.53 us -> 2.58 us  [apply_operator(): jnp.einsum('srj,skj->srk', multiplier, contact_set, preferred_element_typ...]
    ppermute x8, waiting for transfers between devices: 3.69 us -> 1.24 us  [partner(): lax.ppermute(value, axis, [(i, i ^ 1 << distance) for i in range(lax.axis...]
    dot_general x4 -> x8, matrix products: 2.38 us -> 4.63 us  [the longest x4 3.09 us: apply_operator(): jnp.einsum('snrj,skj->nrk', spread, contact_set, preferred_element_type=j...]
    dot_general x4, matrix products: 3.16 us -> 1.08 us  [apply_operator(): jnp.einsum('sn,nrk->srk', far_onehot, other, precision=lax.Precision.HIGH...]
  transfers between devices with their start and end apart: 22 -> 22, of which waited for: 16 -> 14; matrix products, arithmetic and copies ran while one was open for 8% -> 10% of each run, Pallas kernels for 0% -> 0%
where the time goes in v22:
time: 110 us
  blocking collectives  40 us (36%)
  waiting for transfers between devices  22.6 us (21%)
  matrix products  20.8 us (19%)
  starting transfers between devices  15.4 us (14%)
  other arithmetic  6.41 us (6%)
  local copies, waits for them, and re-layouts  3.48 us (3%)
  between operations  1.32 us (1%)
    all_to_all x4, blocking collectives, total(): gathered = lax.all_to_all(spread, ('dom', 'rep'), 0, 0, tiled=True)  40 us
    ppermute x14, waiting for transfers between devices, from_behind(): return lax.ppermute(value, axis, pairs)  21.4 us
    ppermute x8, starting transfers between devices, partner(): lax.ppermute(value, axis, [(i, i ^ 1 << distance) for i in range(lax.axis...  8.91 us
    ppermute x14, starting transfers between devices, from_behind(): return lax.ppermute(value, axis, pairs)  6.46 us
    dot_general x4, matrix products, local_stiffness(): jnp.einsum('pn,prj->nrj', mirror_onehot, mirror, precision=lax.Precision....  3.2 us
    dot_general x4, matrix products, apply_operator(): jnp.einsum('snrj,skj->nrk', spread, contact_set, preferred_element_type=j...  3.09 us
    dot_general x4, matrix products, apply_operator(): jnp.einsum('srj,skj->srk', multiplier, contact_set, preferred_element_typ...  2.58 us
    dot_general x4, matrix products, apply_operator(): jnp.einsum('sn,srk->nrk', near_collect, terms, precision=lax.Precision.HI...  2.37 us
  transfers between devices with their start and end apart: 22, of which 14 were waited for; matrix products, arithmetic and copies ran while one was open for 10% of the time, Pallas kernels for 0%

profile of v22, /device:TPU:0, one launch (start us, length us, event | category | flops | bytes accessed | tf_op | source)
XLA Modules:
  0.0 110.0 jit_solution(2805030459229391282)
XLA Ops:
  1.4 0.9 add_reduce_fusion
  3.0 2.4 %collective-permute-start.6 = (bf16[8,128,128]{2,0,1:T(8,128)(2,1)S(1)}, bf16[8,128,128]{2,0,1:T(8,128)(2,1)}, u32[]{:S(2)}, u32[]{:S(2)}) collective-permute-start(bf16[8,128,128]{2,0,1:T(8,128)(2,1)S(1)} %select_bitcast_fusion), channel_id=1, source_target_pairs={{0,3},{1,0},{2,1},{3,2},{4,7},{5,4},{6,5},{7,6},{8,11},{9,8},{10,9... | collective-permute-start | bytes 786440 | tf_op jit(solution)/shard_map/ppermute | solution.py:14
  6.7 1.7 %collective-permute-start.1 = (s32[8,2]{0,1:T(2,128)S(1)}, s32[8,2]{0,1:T(2,128)S(1)}, u32[]{:S(2)}, u32[]{:S(2)}) collective-permute-start(s32[8,2]{0,1:T(2,128)S(1)} %bitcast.355), channel_id=1, source_target_pairs={{0,2},{1,3},{2,0},{3,1},{4,6},{5,7},{6,4},{7,5},{8,10},{9,11},{10,... | collective-permute-start | bytes 200 | tf_op jit(solution)/shard_map/ppermute | solution.py:14
  8.5 1.6 %collective-permute-start.3 = (bf16[8,32,128]{2,0,1:T(8,128)(2,1)S(1)}, bf16[8,32,128]{2,0,1:T(8,128)(2,1)S(1)}, u32[]{:S(2)}, u32[]{:S(2)}) collective-permute-start(bf16[8,32,128]{2,0,1:T(8,128)(2,1)S(1)} %multiply_convert_fusion), channel_id=1, source_target_pairs={{0,4},{4,0},{8,12},{12,8},{16,20},{20,16},{24,28},{28,24},{1,5},{5... | collective-permute-start | bytes 196616 | tf_op jit(solution)/shard_map/ppermute | solution.py:18
  10.4 4.6 %collective-permute-done.2 = s32[8,2]{0,1:T(2,128)S(1)} collective-permute-done((s32[8,2]{0,1:T(2,128)S(1)}, s32[8,2]{0,1:T(2,128)S(1)}, u32[]{:S(2)}, u32[]{:S(2)}) %collective-permute-start.2) | collective-permute-done | bytes 96 | tf_op jit(solution)/shard_map/ppermute | solution.py:14
  15.0 1.1 %collective-permute-start = (s32[8,2]{0,1:T(2,128)S(1)}, s32[8,2]{0,1:T(2,128)S(1)}, u32[]{:S(2)}, u32[]{:S(2)}) collective-permute-start(s32[8,2]{0,1:T(2,128)S(1)} %bitcast.354), channel_id=1, source_target_pairs={{0,1},{1,2},{2,3},{3,0},{4,5},{5,6},{6,7},{7,4},{8,9},{9,10},{10,1... | collective-permute-start | bytes 200 | tf_op jit(solution)/shard_map/ppermute | solution.py:14
  16.1 2.3 %collective-permute-done = s32[8,2]{0,1:T(2,128)S(1)} collective-permute-done((s32[8,2]{0,1:T(2,128)S(1)}, s32[8,2]{0,1:T(2,128)S(1)}, u32[]{:S(2)}, u32[]{:S(2)}) %collective-permute-start) | collective-permute-done | bytes 96 | tf_op jit(solution)/shard_map/ppermute | solution.py:14
  19.0 3.0 %collective-permute-done.7 = bf16[32,128]{1,0:T(8,128)(2,1)S(1)} collective-permute-done((bf16[32,128]{1,0:T(8,128)(2,1)S(1)}, bf16[32,128]{1,0:T(8,128)(2,1)S(1)}, u32[]{:S(2)}, u32[]{:S(2)}) %collective-permute-start.7) | collective-permute-done | bytes 8224 | tf_op jit(solution)/shard_map/ppermute | solution.py:14
  22.4 1.1 pad_maximum_fusion
  25.0 1.6 %collective-permute-start.9 = (bf16[8,32,128]{2,0,1:T(8,128)(2,1)S(1)}, bf16[8,32,128]{2,0,1:T(8,128)(2,1)S(1)}, u32[]{:S(2)}, u32[]{:S(2)}) collective-permute-start(bf16[8,32,128]{2,0,1:T(8,128)(2,1)S(1)} %copy.394), channel_id=1, source_target_pairs={{0,4},{4,0},{8,12},{12,8},{16,20},{20,16},{24,28},{28,24},{1,5},{5... | collective-permute-start | bytes 196616 | tf_op jit(solution)/shard_map/ppermute | solution.py:18
  30.4 12.7 %all_to_all.20 = f32[32,1,128]{2,1,0:T(1,128)S(1)} all-to-all(f32[32,1,128]{2,1,0:T(1,128)S(1)} %reshape.396), channel_id=1, replica_groups=mesh['dom'=8,'rep'=4] {'dom','rep'}, dimensions={0} | all-to-all | bytes 32768 | tf_op jit(solution)/shard_map/all_to_all | solution.py:24
  45.7 2.6 %collective-permute-done.11 = bf16[32,128]{1,0:T(8,128)(2,1)S(1)} collective-permute-done((bf16[32,128]{1,0:T(8,128)(2,1)S(1)}, bf16[32,128]{1,0:T(8,128)(2,1)S(1)}, u32[]{:S(2)}, u32[]{:S(2)}) %collective-permute-start.11) | collective-permute-done | bytes 8224 | tf_op jit(solution)/shard_map/ppermute | solution.py:14
  50.8 1.1 collective-permute-start.13
  53.8 1.0 collective-permute-done.12
  56.1 9.1 %all_to_all.21 = f32[32,1,128]{2,1,0:T(1,128)S(1)} all-to-all(f32[32,1,128]{2,1,0:T(1,128)S(1)} %reshape.398), channel_id=1, replica_groups=mesh['dom'=8,'rep'=4] {'dom','rep'}, dimensions={0} | all-to-all | bytes 32768 | tf_op jit(solution)/shard_map/all_to_all | solution.py:24
  67.5 2.6 %collective-permute-done.15 = bf16[32,128]{1,0:T(8,128)(2,1)S(1)} collective-permute-done((bf16[32,128]{1,0:T(8,128)(2,1)S(1)}, bf16[32,128]{1,0:T(8,128)(2,1)S(1)}, u32[]{:S(2)}, u32[]{:S(2)}) %collective-permute-start.15) | collective-permute-done | bytes 8224 | tf_op jit(solution)/shard_map/ppermute | solution.py:14
  72.4 1.3 %collective-permute-start.17 = (bf16[8,32,128]{2,0,1:T(8,128)(2,1)S(1)}, bf16[8,32,128]{2,0,1:T(8,128)(2,1)S(1)}, u32[]{:S(2)}, u32[]{:S(2)}) collective-permute-start(bf16[8,32,128]{2,0,1:T(8,128)(2,1)S(1)} %copy.392), channel_id=1, source_target_pairs={{0,4},{4,0},{8,12},{12,8},{16,20},{20,16},{24,28},{28,24},{1,5},{5... | collective-permute-start | bytes 196616 | tf_op jit(solution)/shard_map/ppermute | solution.py:18
  75.6 1.0 collective-permute-done.16
  76.7 0.8 fusion.61
  77.7 9.1 %all_to_all.22 = f32[32,1,128]{2,1,0:T(1,128)S(1)} all-to-all(f32[32,1,128]{2,1,0:T(1,128)S(1)} %reshape.400), channel_id=1, replica_groups=mesh['dom'=8,'rep'=4] {'dom','rep'}, dimensions={0} | all-to-all | bytes 32768 | tf_op jit(solution)/shard_map/all_to_all | solution.py:24
  89.3 2.7 %collective-permute-done.19 = bf16[32,128]{1,0:T(8,128)(2,1)S(1)} collective-permute-done((bf16[32,128]{1,0:T(8,128)(2,1)S(1)}, bf16[32,128]{1,0:T(8,128)(2,1)S(1)}, u32[]{:S(2)}, u32[]{:S(2)}) %collective-permute-start.19) | collective-permute-done | bytes 8224 | tf_op jit(solution)/shard_map/ppermute | solution.py:14
  94.1 1.5 %collective-permute-start.21 = (bf16[8,32,128]{2,0,1:T(8,128)(2,1)S(1)}, bf16[8,32,128]{2,0,1:T(8,128)(2,1)S(1)}, u32[]{:S(2)}, u32[]{:S(2)}) collective-permute-start(bf16[8,32,128]{2,0,1:T(8,128)(2,1)S(1)} %copy.391), channel_id=1, source_target_pairs={{0,4},{4,0},{8,12},{12,8},{16,20},{20,16},{24,28},{28,24},{1,5},{5... | collective-permute-start | bytes 196616 | tf_op jit(solution)/shard_map/ppermute | solution.py:18
  97.5 1.0 collective-permute-done.20
  99.2 9.2 %all_to_all.23 = f32[32,2,32]{2,1,0:T(2,128)S(1)} all-to-all(f32[32,2,32]{2,1,0:T(2,128)S(1)} %broadcast_in_dim.143), channel_id=1, replica_groups=mesh['dom'=8,'rep'=4] {'dom','rep'}, dimensions={0} | all-to-all | bytes 16384 | tf_op jit(solution)/shard_map/all_to_all | solution.py:24
  (165 shorter events, 32.6 us)
Async XLA Ops:
  3.0 7.1 %copy-start.6 = (s32[8,2]{0,1:T(2,128)S(1)}, s32[8,2]{0,1:T(2,128)}, u32[]{:S(2)}) copy-start(s32[8,2]{0,1:T(2,128)} %param.18) | copy-start | bytes 196
  3.0 19.4 %collective-permute-start.6 = (bf16[8,128,128]{2,0,1:T(8,128)(2,1)S(1)}, bf16[8,128,128]{2,0,1:T(8,128)(2,1)}, u32[]{:S(2)}, u32[]{:S(2)}) collective-permute-start(bf16[8,128,128]{2,0,1:T(8,128)(2,1)S(1)} %select_bitcast_fusion), channel_id=1, source_target_pairs={{0,3},{1,0},{2,1},{3,2},{4,7},{5,4},{6,5},{7,6},{8,11},{9,8},{10,9... | collective-permute-start | bytes 786440 | tf_op jit(solution)/shard_map/ppermute | solution.py:14
  5.4 16.5 %copy-start.4 = (bf16[1,128,128]{2,1,0:T(8,128)(2,1)S(1)}, bf16[1,128,128]{2,1,0:T(8,128)(2,1)}, u32[]{:S(2)}) copy-start(bf16[1,128,128]{2,1,0:T(8,128)(2,1)} %param.19) | copy-start | bytes 98308
  5.6 16.9 %collective-permute-start.5 = (bf16[8,128,128]{2,0,1:T(8,128)(2,1)S(1)}, bf16[8,128,128]{2,0,1:T(8,128)(2,1)S(1)}, u32[]{:S(2)}, u32[]{:S(2)}) collective-permute-start(bf16[8,128,128]{2,0,1:T(8,128)(2,1)S(1)} %get-tuple-element.84), channel_id=1, source_target_pairs={{0,2},{1,3},{2,0},{3,1},{4,6},{5,7},{6,4},{7,5},{8,10},{9,11},{10,... | collective-permute-start | bytes 786440 | tf_op jit(solution)/shard_map/ppermute | solution.py:14
  6.6 8.4 %collective-permute-start.2 = (s32[8,2]{0,1:T(2,128)S(1)}, s32[8,2]{0,1:T(2,128)S(1)}, u32[]{:S(2)}, u32[]{:S(2)}) collective-permute-start(s32[8,2]{0,1:T(2,128)S(1)} %bitcast.356), channel_id=1, source_target_pairs={{0,3},{1,0},{2,1},{3,2},{4,7},{5,4},{6,5},{7,6},{8,11},{9,8},{10,9... | collective-permute-start | bytes 200 | tf_op jit(solution)/shard_map/ppermute | solution.py:14
  6.7 9.5 %collective-permute-start.1 = (s32[8,2]{0,1:T(2,128)S(1)}, s32[8,2]{0,1:T(2,128)S(1)}, u32[]{:S(2)}, u32[]{:S(2)}) collective-permute-start(s32[8,2]{0,1:T(2,128)S(1)} %bitcast.355), channel_id=1, source_target_pairs={{0,2},{1,3},{2,0},{3,1},{4,6},{5,7},{6,4},{7,5},{8,10},{9,11},{10,... | collective-permute-start | bytes 200 | tf_op jit(solution)/shard_map/ppermute | solution.py:14
  8.5 13.6 %collective-permute-start.3 = (bf16[8,32,128]{2,0,1:T(8,128)(2,1)S(1)}, bf16[8,32,128]{2,0,1:T(8,128)(2,1)S(1)}, u32[]{:S(2)}, u32[]{:S(2)}) collective-permute-start(bf16[8,32,128]{2,0,1:T(8,128)(2,1)S(1)} %multiply_convert_fusion), channel_id=1, source_target_pairs={{0,4},{4,0},{8,12},{12,8},{16,20},{20,16},{24,28},{28,24},{1,5},{5... | collective-permute-start | bytes 196616 | tf_op jit(solution)/shard_map/ppermute | solution.py:18
  15.0 3.4 %collective-permute-start = (s32[8,2]{0,1:T(2,128)S(1)}, s32[8,2]{0,1:T(2,128)S(1)}, u32[]{:S(2)}, u32[]{:S(2)}) collective-permute-start(s32[8,2]{0,1:T(2,128)S(1)} %bitcast.354), channel_id=1, source_target_pairs={{0,1},{1,2},{2,3},{3,0},{4,5},{5,6},{6,7},{7,4},{8,9},{9,10},{10,1... | collective-permute-start | bytes 200 | tf_op jit(solution)/shard_map/ppermute | solution.py:14
  16.1 6.3 %collective-permute-start.4 = (bf16[8,128,128]{2,0,1:T(8,128)(2,1)S(1)}, bf16[8,128,128]{2,0,1:T(8,128)(2,1)S(1)}, u32[]{:S(2)}, u32[]{:S(2)}) collective-permute-start(bf16[8,128,128]{2,0,1:T(8,128)(2,1)S(1)} %get-tuple-element.83), channel_id=1, source_target_pairs={{0,1},{1,2},{2,3},{3,0},{4,5},{5,6},{6,7},{7,4},{8,9},{9,10},{10,1... | collective-permute-start | bytes 786440 | tf_op jit(solution)/shard_map/ppermute | solution.py:14
  18.4 3.6 %collective-permute-start.7 = (bf16[32,128]{1,0:T(8,128)(2,1)S(1)}, bf16[32,128]{1,0:T(8,128)(2,1)S(1)}, u32[]{:S(2)}, u32[]{:S(2)}) collective-permute-start(bf16[32,128]{1,0:T(8,128)(2,1)S(1)} %bitcast.335), channel_id=1, source_target_pairs={{0,1},{1,2},{2,3},{3,0},{4,5},{5,6},{6,7},{7,4},{8,9},{9,10},{10,1... | collective-permute-start | bytes 24584 | tf_op jit(solution)/shard_map/ppermute | solution.py:14
  25.0 4.5 %collective-permute-start.9 = (bf16[8,32,128]{2,0,1:T(8,128)(2,1)S(1)}, bf16[8,32,128]{2,0,1:T(8,128)(2,1)S(1)}, u32[]{:S(2)}, u32[]{:S(2)}) collective-permute-start(bf16[8,32,128]{2,0,1:T(8,128)(2,1)S(1)} %copy.394), channel_id=1, source_target_pairs={{0,4},{4,0},{8,12},{12,8},{16,20},{20,16},{24,28},{28,24},{1,5},{5... | collective-permute-start | bytes 196616 | tf_op jit(solution)/shard_map/ppermute | solution.py:18
  28.0 1.5 %collective-permute-start.8 = (f32[32,128]{1,0:T(8,128)S(1)}, f32[32,128]{1,0:T(8,128)S(1)}, u32[]{:S(2)}, u32[]{:S(2)}) collective-permute-start(f32[32,128]{1,0:T(8,128)S(1)} %fusion.109), channel_id=1, source_target_pairs={{0,3},{1,0},{2,1},{3,2},{4,7},{5,4},{6,5},{7,6},{8,11},{9,8},{10,9... | collective-permute-start | bytes 49160 | tf_op jit(solution)/shard_map/ppermute | solution.py:14
  44.6 4.3 %collective-permute-start.10 = (bf16[8,32,128]{2,0,1:T(8,128)(2,1)S(1)}, bf16[8,32,128]{2,0,1:T(8,128)(2,1)S(1)}, u32[]{:S(2)}, u32[]{:S(2)}) collective-permute-start(bf16[8,32,128]{2,0,1:T(8,128)(2,1)S(1)} %get-tuple-element.19), channel_id=1, source_target_pairs={{0,4},{4,0},{8,12},{12,8},{16,20},{20,16},{24,28},{28,24},{1,5},{5... | collective-permute-start | bytes 196616 | tf_op jit(solution)/shard_map/ppermute | solution.py:18
  45.2 3.1 %collective-permute-start.11 = (bf16[32,128]{1,0:T(8,128)(2,1)S(1)}, bf16[32,128]{1,0:T(8,128)(2,1)S(1)}, u32[]{:S(2)}, u32[]{:S(2)}) collective-permute-start(bf16[32,128]{1,0:T(8,128)(2,1)S(1)} %bitcast.337), channel_id=1, source_target_pairs={{0,1},{1,2},{2,3},{3,0},{4,5},{5,6},{6,7},{7,4},{8,9},{9,10},{10,1... | collective-permute-start | bytes 24584 | tf_op jit(solution)/shard_map/ppermute | solution.py:14
  50.8 4.3 %collective-permute-start.13 = (bf16[8,32,128]{2,0,1:T(8,128)(2,1)S(1)}, bf16[8,32,128]{2,0,1:T(8,128)(2,1)S(1)}, u32[]{:S(2)}, u32[]{:S(2)}) collective-permute-start(bf16[8,32,128]{2,0,1:T(8,128)(2,1)S(1)} %copy.393), channel_id=1, source_target_pairs={{0,4},{4,0},{8,12},{12,8},{16,20},{20,16},{24,28},{28,24},{1,5},{5... | collective-permute-start | bytes 196616 | tf_op jit(solution)/shard_map/ppermute | solution.py:18
  53.3 1.5 %collective-permute-start.12 = (f32[32,128]{1,0:T(8,128)S(1)}, f32[32,128]{1,0:T(8,128)S(1)}, u32[]{:S(2)}, u32[]{:S(2)}) collective-permute-start(f32[32,128]{1,0:T(8,128)S(1)} %fusion.105), channel_id=1, source_target_pairs={{0,3},{1,0},{2,1},{3,2},{4,7},{5,4},{6,5},{7,6},{8,11},{9,8},{10,9... | collective-permute-start | bytes 49160 | tf_op jit(solution)/shard_map/ppermute | solution.py:14
  66.2 4.3 %collective-permute-start.14 = (bf16[8,32,128]{2,0,1:T(8,128)(2,1)S(1)}, bf16[8,32,128]{2,0,1:T(8,128)(2,1)S(1)}, u32[]{:S(2)}, u32[]{:S(2)}) collective-permute-start(bf16[8,32,128]{2,0,1:T(8,128)(2,1)S(1)} %get-tuple-element.22), channel_id=1, source_target_pairs={{0,4},{4,0},{8,12},{12,8},{16,20},{20,16},{24,28},{28,24},{1,5},{5... | collective-permute-start | bytes 196616 | tf_op jit(solution)/shard_map/ppermute | solution.py:18
  66.8 3.3 %collective-permute-start.15 = (bf16[32,128]{1,0:T(8,128)(2,1)S(1)}, bf16[32,128]{1,0:T(8,128)(2,1)S(1)}, u32[]{:S(2)}, u32[]{:S(2)}) collective-permute-start(bf16[32,128]{1,0:T(8,128)(2,1)S(1)} %bitcast.338), channel_id=1, source_target_pairs={{0,1},{1,2},{2,3},{3,0},{4,5},{5,6},{6,7},{7,4},{8,9},{9,10},{10,1... | collective-permute-start | bytes 24584 | tf_op jit(solution)/shard_map/ppermute | solution.py:14
  72.4 4.3 %collective-permute-start.17 = (bf16[8,32,128]{2,0,1:T(8,128)(2,1)S(1)}, bf16[8,32,128]{2,0,1:T(8,128)(2,1)S(1)}, u32[]{:S(2)}, u32[]{:S(2)}) collective-permute-start(bf16[8,32,128]{2,0,1:T(8,128)(2,1)S(1)} %copy.392), channel_id=1, source_target_pairs={{0,4},{4,0},{8,12},{12,8},{16,20},{20,16},{24,28},{28,24},{1,5},{5... | collective-permute-start | bytes 196616 | tf_op jit(solution)/shard_map/ppermute | solution.py:18
  75.1 1.5 %collective-permute-start.16 = (f32[32,128]{1,0:T(8,128)S(1)}, f32[32,128]{1,0:T(8,128)S(1)}, u32[]{:S(2)}, u32[]{:S(2)}) collective-permute-start(f32[32,128]{1,0:T(8,128)S(1)} %fusion.101), channel_id=1, source_target_pairs={{0,3},{1,0},{2,1},{3,2},{4,7},{5,4},{6,5},{7,6},{8,11},{9,8},{10,9... | collective-permute-start | bytes 49160 | tf_op jit(solution)/shard_map/ppermute | solution.py:14
  87.8 4.3 %collective-permute-start.18 = (bf16[8,32,128]{2,0,1:T(8,128)(2,1)S(1)}, bf16[8,32,128]{2,0,1:T(8,128)(2,1)S(1)}, u32[]{:S(2)}, u32[]{:S(2)}) collective-permute-start(bf16[8,32,128]{2,0,1:T(8,128)(2,1)S(1)} %get-tuple-element.25), channel_id=1, source_target_pairs={{0,4},{4,0},{8,12},{12,8},{16,20},{20,16},{24,28},{28,24},{1,5},{5... | collective-permute-start | bytes 196616 | tf_op jit(solution)/shard_map/ppermute | solution.py:18
  88.9 3.1 %collective-permute-start.19 = (bf16[32,128]{1,0:T(8,128)(2,1)S(1)}, bf16[32,128]{1,0:T(8,128)(2,1)S(1)}, u32[]{:S(2)}, u32[]{:S(2)}) collective-permute-start(bf16[32,128]{1,0:T(8,128)(2,1)S(1)} %bitcast.336), channel_id=1, source_target_pairs={{0,1},{1,2},{2,3},{3,0},{4,5},{5,6},{6,7},{7,4},{8,9},{9,10},{10,1... | collective-permute-start | bytes 24584 | tf_op jit(solution)/shard_map/ppermute | solution.py:14
  94.1 4.4 %collective-permute-start.21 = (bf16[8,32,128]{2,0,1:T(8,128)(2,1)S(1)}, bf16[8,32,128]{2,0,1:T(8,128)(2,1)S(1)}, u32[]{:S(2)}, u32[]{:S(2)}) collective-permute-start(bf16[8,32,128]{2,0,1:T(8,128)(2,1)S(1)} %copy.391), channel_id=1, source_target_pairs={{0,4},{4,0},{8,12},{12,8},{16,20},{20,16},{24,28},{28,24},{1,5},{5... | collective-permute-start | bytes 196616 | tf_op jit(solution)/shard_map/ppermute | solution.py:18
  97.0 1.5 %collective-permute-start.20 = (f32[32,128]{1,0:T(8,128)S(1)}, f32[32,128]{1,0:T(8,128)S(1)}, u32[]{:S(2)}, u32[]{:S(2)}) collective-permute-start(f32[32,128]{1,0:T(8,128)S(1)} %fusion.97), channel_id=1, source_target_pairs={{0,3},{1,0},{2,1},{3,2},{4,7},{5,4},{6,5},{7,6},{8,11},{9,8},{10,9... | collective-permute-start | bytes 49160 | tf_op jit(solution)/shard_map/ppermute | solution.py:14
  (7 other events, 23.9 us)

commit v23 on v22

--- a/solution.py
+++ b/solution.py
@@ -40,7 +40,7 @@
 
 
 def apply_operator(vector, diag_tiles, off_tiles, link_tile, contact_set, tables):
-    cols_onehot, mirror_onehot, near_onehot, far_onehot, near_collect, far_pick = tables
+    cols_onehot, mirror_onehot, near_onehot, far_onehot, near_pick, far_pick = tables
     nodes = vector.shape[0]
     rounded = vector.astype(jnp.bfloat16)
     before = from_behind(rounded[nodes - 1], "rep", 1)
@@ -56,7 +56,6 @@
     far_sum, rounded, multiplier = lax.optimization_barrier(
         (far_sum.astype(jnp.bfloat16), rounded, multiplier)
     )
-    terms = jnp.einsum("srj,skj->srk", multiplier, contact_set, preferred_element_type=jnp.float32)
     far_terms = partner(far_sum, "dom", 0).astype(jnp.float32)
     back_term = lax.dot_general(
         rounded[0], link_tile, (((1,), (1,)), ((), ())), preferred_element_type=jnp.float32
@@ -68,7 +67,10 @@
         [first_add[None], jnp.zeros((nodes - 2,) + first_add.shape, jnp.float32), after[None]]
     )
     result = result + ends
-    result = result + jnp.einsum("sn,srk->nrk", near_collect, terms, precision=lax.Precision.HIGHEST)
+    near_spread = near_pick[:, :, None, None] * multiplier[:, None, :, :]
+    result = result + jnp.einsum(
+        "snrj,skj->nrk", near_spread, contact_set, preferred_element_type=jnp.float32
+    )
     return result - far_terms
 
 
@@ -122,7 +124,7 @@
         mirror_onehot,
         near_collect,
         far_collect,
-        near_collect,
+        near_collect.astype(jnp.bfloat16),
         far_collect.astype(jnp.bfloat16),
     )
     link_tile = link_tiles[0]

time: 110 us -> 110 us (level)
  matrix products: 20.8 us -> 19 us
  waiting for transfers between devices: 22.6 us -> 24.1 us
    ppermute x8, waiting for transfers between devices: 1.24 us -> 3.25 us  [partner(): lax.ppermute(value, axis, [(i, i ^ 1 << distance) for i in range(lax.axis...]
    dot_general x8 -> x4, matrix products: 4.95 us -> 2.99 us  [apply_operator(): jnp.einsum('snrj,skj->nrk', near_spread, contact_set, preferred_element_t...]
  transfers between devices with their start and end apart: 22 -> 22, of which waited for: 14 -> 15; matrix products, arithmetic and copies ran while one was open for 10% -> 9% of each run, Pallas kernels for 0% -> 0%
where the time goes in v23:
time: 110 us; the launch traced here: 109 us
  blocking collectives  39.4 us (36%)
  waiting for transfers between devices  24.1 us (22%)
  matrix products  19 us (17%)
  starting transfers between devices  15.4 us (14%)
  other arithmetic  6.42 us (6%)
  local copies, waits for them, and re-layouts  3.77 us (3%)
  between operations  1.34 us (1%)
    all_to_all x4, blocking collectives, total(): gathered = lax.all_to_all(spread, ('dom', 'rep'), 0, 0, tiled=True)  39.4 us
    ppermute x14, waiting for transfers between devices, from_behind(): return lax.ppermute(value, axis, pairs)  20.9 us
    ppermute x8, starting transfers between devices, partner(): lax.ppermute(value, axis, [(i, i ^ 1 << distance) for i in range(lax.axis...  8.89 us
    ppermute x14, starting transfers between devices, from_behind(): return lax.ppermute(value, axis, pairs)  6.46 us
    dot_general x4, matrix products, local_stiffness(): jnp.einsum('pn,prj->nrj', mirror_onehot, mirror, precision=lax.Precision....  3.43 us
    ppermute x8, waiting for transfers between devices, partner(): lax.ppermute(value, axis, [(i, i ^ 1 << distance) for i in range(lax.axis...  3.25 us
    dot_general x4, matrix products, apply_operator(): jnp.einsum('snrj,skj->nrk', spread, contact_set, preferred_element_type=j...  3.1 us
    dot_general x4, matrix products, apply_operator(): jnp.einsum('snrj,skj->nrk', near_spread, contact_set, preferred_element_t...  2.99 us
  transfers between devices with their start and end apart: 22, of which 15 were waited for; matrix products, arithmetic and copies ran while one was open for 9% of the time, Pallas kernels for 0%

profile of v23, /device:TPU:0, one launch (start us, length us, event | category | flops | bytes accessed | tf_op | source)
XLA Modules:
  0.0 109.4 jit_solution(18181563307756800518)
XLA Ops:
  1.4 0.9 add_reduce_fusion
  3.0 2.4 %collective-permute-start.6 = (bf16[8,128,128]{2,0,1:T(8,128)(2,1)S(1)}, bf16[8,128,128]{2,0,1:T(8,128)(2,1)}, u32[]{:S(2)}, u32[]{:S(2)}) collective-permute-start(bf16[8,128,128]{2,0,1:T(8,128)(2,1)S(1)} %select_bitcast_fusion), channel_id=1, source_target_pairs={{0,3},{1,0},{2,1},{3,2},{4,7},{5,4},{6,5},{7,6},{8,11},{9,8},{10,9... | collective-permute-start | bytes 786440 | tf_op jit(solution)/shard_map/ppermute | solution.py:14
  6.7 1.7 %collective-permute-start.1 = (s32[8,2]{0,1:T(2,128)S(1)}, s32[8,2]{0,1:T(2,128)S(1)}, u32[]{:S(2)}, u32[]{:S(2)}) collective-permute-start(s32[8,2]{0,1:T(2,128)S(1)} %bitcast.359), channel_id=1, source_target_pairs={{0,2},{1,3},{2,0},{3,1},{4,6},{5,7},{6,4},{7,5},{8,10},{9,11},{10,... | collective-permute-start | bytes 200 | tf_op jit(solution)/shard_map/ppermute | solution.py:14
  8.5 1.6 %collective-permute-start.3 = (bf16[8,32,128]{2,0,1:T(8,128)(2,1)S(1)}, bf16[8,32,128]{2,0,1:T(8,128)(2,1)S(1)}, u32[]{:S(2)}, u32[]{:S(2)}) collective-permute-start(bf16[8,32,128]{2,0,1:T(8,128)(2,1)S(1)} %multiply_convert_fusion), channel_id=1, source_target_pairs={{0,4},{4,0},{8,12},{12,8},{16,20},{20,16},{24,28},{28,24},{1,5},{5... | collective-permute-start | bytes 196616 | tf_op jit(solution)/shard_map/ppermute | solution.py:18
  10.4 4.6 %collective-permute-done.2 = s32[8,2]{0,1:T(2,128)S(1)} collective-permute-done((s32[8,2]{0,1:T(2,128)S(1)}, s32[8,2]{0,1:T(2,128)S(1)}, u32[]{:S(2)}, u32[]{:S(2)}) %collective-permute-start.2) | collective-permute-done | bytes 96 | tf_op jit(solution)/shard_map/ppermute | solution.py:14
  15.0 1.1 %collective-permute-start = (s32[8,2]{0,1:T(2,128)S(1)}, s32[8,2]{0,1:T(2,128)S(1)}, u32[]{:S(2)}, u32[]{:S(2)}) collective-permute-start(s32[8,2]{0,1:T(2,128)S(1)} %bitcast.358), channel_id=1, source_target_pairs={{0,1},{1,2},{2,3},{3,0},{4,5},{5,6},{6,7},{7,4},{8,9},{9,10},{10,1... | collective-permute-start | bytes 200 | tf_op jit(solution)/shard_map/ppermute | solution.py:14
  16.1 2.3 %collective-permute-done = s32[8,2]{0,1:T(2,128)S(1)} collective-permute-done((s32[8,2]{0,1:T(2,128)S(1)}, s32[8,2]{0,1:T(2,128)S(1)}, u32[]{:S(2)}, u32[]{:S(2)}) %collective-permute-start) | collective-permute-done | bytes 96 | tf_op jit(solution)/shard_map/ppermute | solution.py:14
  19.0 3.0 %collective-permute-done.7 = bf16[32,128]{1,0:T(8,128)(2,1)S(1)} collective-permute-done((bf16[32,128]{1,0:T(8,128)(2,1)S(1)}, bf16[32,128]{1,0:T(8,128)(2,1)S(1)}, u32[]{:S(2)}, u32[]{:S(2)}) %collective-permute-start.7) | collective-permute-done | bytes 8224 | tf_op jit(solution)/shard_map/ppermute | solution.py:14
  22.4 1.1 pad_maximum_fusion
  25.0 1.6 %collective-permute-start.9 = (bf16[8,32,128]{2,0,1:T(8,128)(2,1)S(1)}, bf16[8,32,128]{2,0,1:T(8,128)(2,1)S(1)}, u32[]{:S(2)}, u32[]{:S(2)}) collective-permute-start(bf16[8,32,128]{2,0,1:T(8,128)(2,1)S(1)} %copy.386), channel_id=1, source_target_pairs={{0,4},{4,0},{8,12},{12,8},{16,20},{20,16},{24,28},{28,24},{1,5},{5... | collective-permute-start | bytes 196616 | tf_op jit(solution)/shard_map/ppermute | solution.py:18
  29.3 0.9 fusion.75
  30.3 12.8 %all_to_all.20 = f32[32,1,128]{2,1,0:T(1,128)S(1)} all-to-all(f32[32,1,128]{2,1,0:T(1,128)S(1)} %reshape.428), channel_id=1, replica_groups=mesh['dom'=8,'rep'=4] {'dom','rep'}, dimensions={0} | all-to-all | bytes 32768 | tf_op jit(solution)/shard_map/all_to_all | solution.py:24
  45.7 2.6 %collective-permute-done.11 = bf16[32,128]{1,0:T(8,128)(2,1)S(1)} collective-permute-done((bf16[32,128]{1,0:T(8,128)(2,1)S(1)}, bf16[32,128]{1,0:T(8,128)(2,1)S(1)}, u32[]{:S(2)}, u32[]{:S(2)}) %collective-permute-start.11) | collective-permute-done | bytes 8224 | tf_op jit(solution)/shard_map/ppermute | solution.py:14
  50.9 1.1 %collective-permute-start.13 = (bf16[8,32,128]{2,0,1:T(8,128)(2,1)S(1)}, bf16[8,32,128]{2,0,1:T(8,128)(2,1)S(1)}, u32[]{:S(2)}, u32[]{:S(2)}) collective-permute-start(bf16[8,32,128]{2,0,1:T(8,128)(2,1)S(1)} %copy.385), channel_id=1, source_target_pairs={{0,4},{4,0},{8,12},{12,8},{16,20},{20,16},{24,28},{28,24},{1,5},{5... | collective-permute-start | bytes 196616 | tf_op jit(solution)/shard_map/ppermute | solution.py:18
  53.4 1.0 collective-permute-done.12
  56.2 8.8 %all_to_all.21 = f32[32,1,128]{2,1,0:T(1,128)S(1)} all-to-all(f32[32,1,128]{2,1,0:T(1,128)S(1)} %reshape.430), channel_id=1, replica_groups=mesh['dom'=8,'rep'=4] {'dom','rep'}, dimensions={0} | all-to-all | bytes 32768 | tf_op jit(solution)/shard_map/all_to_all | solution.py:24
  67.4 2.6 %collective-permute-done.15 = bf16[32,128]{1,0:T(8,128)(2,1)S(1)} collective-permute-done((bf16[32,128]{1,0:T(8,128)(2,1)S(1)}, bf16[32,128]{1,0:T(8,128)(2,1)S(1)}, u32[]{:S(2)}, u32[]{:S(2)}) %collective-permute-start.15) | collective-permute-done | bytes 8224 | tf_op jit(solution)/shard_map/ppermute | solution.py:14
  72.3 1.3 %collective-permute-start.17 = (bf16[8,32,128]{2,0,1:T(8,128)(2,1)S(1)}, bf16[8,32,128]{2,0,1:T(8,128)(2,1)S(1)}, u32[]{:S(2)}, u32[]{:S(2)}) collective-permute-start(bf16[8,32,128]{2,0,1:T(8,128)(2,1)S(1)} %copy.384), channel_id=1, source_target_pairs={{0,4},{4,0},{8,12},{12,8},{16,20},{20,16},{24,28},{28,24},{1,5},{5... | collective-permute-start | bytes 196616 | tf_op jit(solution)/shard_map/ppermute | solution.py:18
  74.9 1.0 collective-permute-done.16
  77.6 8.8 %all_to_all.22 = f32[32,1,128]{2,1,0:T(1,128)S(1)} all-to-all(f32[32,1,128]{2,1,0:T(1,128)S(1)} %reshape.432), channel_id=1, replica_groups=mesh['dom'=8,'rep'=4] {'dom','rep'}, dimensions={0} | all-to-all | bytes 32768 | tf_op jit(solution)/shard_map/all_to_all | solution.py:24
  88.9 2.7 %collective-permute-done.19 = bf16[32,128]{1,0:T(8,128)(2,1)S(1)} collective-permute-done((bf16[32,128]{1,0:T(8,128)(2,1)S(1)}, bf16[32,128]{1,0:T(8,128)(2,1)S(1)}, u32[]{:S(2)}, u32[]{:S(2)}) %collective-permute-start.19) | collective-permute-done | bytes 8224 | tf_op jit(solution)/shard_map/ppermute | solution.py:14
  93.7 1.5 %collective-permute-start.21 = (bf16[8,32,128]{2,0,1:T(8,128)(2,1)S(1)}, bf16[8,32,128]{2,0,1:T(8,128)(2,1)S(1)}, u32[]{:S(2)}, u32[]{:S(2)}) collective-permute-start(bf16[8,32,128]{2,0,1:T(8,128)(2,1)S(1)} %copy.383), channel_id=1, source_target_pairs={{0,4},{4,0},{8,12},{12,8},{16,20},{20,16},{24,28},{28,24},{1,5},{5... | collective-permute-start | bytes 196616 | tf_op jit(solution)/shard_map/ppermute | solution.py:18
  96.6 1.0 collective-permute-done.20
  98.9 8.9 %all_to_all.23 = f32[32,2,32]{2,1,0:T(2,128)S(1)} all-to-all(f32[32,2,32]{2,1,0:T(2,128)S(1)} %broadcast_in_dim.90), channel_id=1, replica_groups=mesh['dom'=8,'rep'=4] {'dom','rep'}, dimensions={0} | all-to-all | bytes 16384 | tf_op jit(solution)/shard_map/all_to_all | solution.py:24
  (162 shorter events, 32.6 us)
Async XLA Ops:
  3.0 7.1 %copy-start.6 = (s32[8,2]{0,1:T(2,128)S(1)}, s32[8,2]{0,1:T(2,128)}, u32[]{:S(2)}) copy-start(s32[8,2]{0,1:T(2,128)} %param.18) | copy-start | bytes 196
  3.0 19.4 %collective-permute-start.6 = (bf16[8,128,128]{2,0,1:T(8,128)(2,1)S(1)}, bf16[8,128,128]{2,0,1:T(8,128)(2,1)}, u32[]{:S(2)}, u32[]{:S(2)}) collective-permute-start(bf16[8,128,128]{2,0,1:T(8,128)(2,1)S(1)} %select_bitcast_fusion), channel_id=1, source_target_pairs={{0,3},{1,0},{2,1},{3,2},{4,7},{5,4},{6,5},{7,6},{8,11},{9,8},{10,9... | collective-permute-start | bytes 786440 | tf_op jit(solution)/shard_map/ppermute | solution.py:14
  5.4 16.5 %copy-start.4 = (bf16[1,128,128]{2,1,0:T(8,128)(2,1)S(1)}, bf16[1,128,128]{2,1,0:T(8,128)(2,1)}, u32[]{:S(2)}) copy-start(bf16[1,128,128]{2,1,0:T(8,128)(2,1)} %param.19) | copy-start | bytes 98308
  5.6 16.9 %collective-permute-start.5 = (bf16[8,128,128]{2,0,1:T(8,128)(2,1)S(1)}, bf16[8,128,128]{2,0,1:T(8,128)(2,1)S(1)}, u32[]{:S(2)}, u32[]{:S(2)}) collective-permute-start(bf16[8,128,128]{2,0,1:T(8,128)(2,1)S(1)} %get-tuple-element.84), channel_id=1, source_target_pairs={{0,2},{1,3},{2,0},{3,1},{4,6},{5,7},{6,4},{7,5},{8,10},{9,11},{10,... | collective-permute-start | bytes 786440 | tf_op jit(solution)/shard_map/ppermute | solution.py:14
  6.6 8.4 %collective-permute-start.2 = (s32[8,2]{0,1:T(2,128)S(1)}, s32[8,2]{0,1:T(2,128)S(1)}, u32[]{:S(2)}, u32[]{:S(2)}) collective-permute-start(s32[8,2]{0,1:T(2,128)S(1)} %bitcast.360), channel_id=1, source_target_pairs={{0,3},{1,0},{2,1},{3,2},{4,7},{5,4},{6,5},{7,6},{8,11},{9,8},{10,9... | collective-permute-start | bytes 200 | tf_op jit(solution)/shard_map/ppermute | solution.py:14
  6.7 9.5 %collective-permute-start.1 = (s32[8,2]{0,1:T(2,128)S(1)}, s32[8,2]{0,1:T(2,128)S(1)}, u32[]{:S(2)}, u32[]{:S(2)}) collective-permute-start(s32[8,2]{0,1:T(2,128)S(1)} %bitcast.359), channel_id=1, source_target_pairs={{0,2},{1,3},{2,0},{3,1},{4,6},{5,7},{6,4},{7,5},{8,10},{9,11},{10,... | collective-permute-start | bytes 200 | tf_op jit(solution)/shard_map/ppermute | solution.py:14
  8.5 13.6 %collective-permute-start.3 = (bf16[8,32,128]{2,0,1:T(8,128)(2,1)S(1)}, bf16[8,32,128]{2,0,1:T(8,128)(2,1)S(1)}, u32[]{:S(2)}, u32[]{:S(2)}) collective-permute-start(bf16[8,32,128]{2,0,1:T(8,128)(2,1)S(1)} %multiply_convert_fusion), channel_id=1, source_target_pairs={{0,4},{4,0},{8,12},{12,8},{16,20},{20,16},{24,28},{28,24},{1,5},{5... | collective-permute-start | bytes 196616 | tf_op jit(solution)/shard_map/ppermute | solution.py:18
  15.0 3.4 %collective-permute-start = (s32[8,2]{0,1:T(2,128)S(1)}, s32[8,2]{0,1:T(2,128)S(1)}, u32[]{:S(2)}, u32[]{:S(2)}) collective-permute-start(s32[8,2]{0,1:T(2,128)S(1)} %bitcast.358), channel_id=1, source_target_pairs={{0,1},{1,2},{2,3},{3,0},{4,5},{5,6},{6,7},{7,4},{8,9},{9,10},{10,1... | collective-permute-start | bytes 200 | tf_op jit(solution)/shard_map/ppermute | solution.py:14
  16.1 6.3 %collective-permute-start.4 = (bf16[8,128,128]{2,0,1:T(8,128)(2,1)S(1)}, bf16[8,128,128]{2,0,1:T(8,128)(2,1)S(1)}, u32[]{:S(2)}, u32[]{:S(2)}) collective-permute-start(bf16[8,128,128]{2,0,1:T(8,128)(2,1)S(1)} %get-tuple-element.83), channel_id=1, source_target_pairs={{0,1},{1,2},{2,3},{3,0},{4,5},{5,6},{6,7},{7,4},{8,9},{9,10},{10,1... | collective-permute-start | bytes 786440 | tf_op jit(solution)/shard_map/ppermute | solution.py:14
  18.4 3.6 %collective-permute-start.7 = (bf16[32,128]{1,0:T(8,128)(2,1)S(1)}, bf16[32,128]{1,0:T(8,128)(2,1)S(1)}, u32[]{:S(2)}, u32[]{:S(2)}) collective-permute-start(bf16[32,128]{1,0:T(8,128)(2,1)S(1)} %bitcast.339), channel_id=1, source_target_pairs={{0,1},{1,2},{2,3},{3,0},{4,5},{5,6},{6,7},{7,4},{8,9},{9,10},{10,1... | collective-permute-start | bytes 24584 | tf_op jit(solution)/shard_map/ppermute | solution.py:14
  25.0 4.3 %collective-permute-start.9 = (bf16[8,32,128]{2,0,1:T(8,128)(2,1)S(1)}, bf16[8,32,128]{2,0,1:T(8,128)(2,1)S(1)}, u32[]{:S(2)}, u32[]{:S(2)}) collective-permute-start(bf16[8,32,128]{2,0,1:T(8,128)(2,1)S(1)} %copy.386), channel_id=1, source_target_pairs={{0,4},{4,0},{8,12},{12,8},{16,20},{20,16},{24,28},{28,24},{1,5},{5... | collective-permute-start | bytes 196616 | tf_op jit(solution)/shard_map/ppermute | solution.py:18
  26.7 2.0 %collective-permute-start.8 = (f32[32,128]{1,0:T(8,128)S(1)}, f32[32,128]{1,0:T(8,128)S(1)}, u32[]{:S(2)}, u32[]{:S(2)}) collective-permute-start(f32[32,128]{1,0:T(8,128)S(1)} %fusion.129), channel_id=1, source_target_pairs={{0,3},{1,0},{2,1},{3,2},{4,7},{5,4},{6,5},{7,6},{8,11},{9,8},{10,9... | collective-permute-start | bytes 49160 | tf_op jit(solution)/shard_map/ppermute | solution.py:14
  44.6 4.3 %collective-permute-start.10 = (bf16[8,32,128]{2,0,1:T(8,128)(2,1)S(1)}, bf16[8,32,128]{2,0,1:T(8,128)(2,1)S(1)}, u32[]{:S(2)}, u32[]{:S(2)}) collective-permute-start(bf16[8,32,128]{2,0,1:T(8,128)(2,1)S(1)} %get-tuple-element.19), channel_id=1, source_target_pairs={{0,4},{4,0},{8,12},{12,8},{16,20},{20,16},{24,28},{28,24},{1,5},{5... | collective-permute-start | bytes 196616 | tf_op jit(solution)/shard_map/ppermute | solution.py:18
  45.3 3.1 %collective-permute-start.11 = (bf16[32,128]{1,0:T(8,128)(2,1)S(1)}, bf16[32,128]{1,0:T(8,128)(2,1)S(1)}, u32[]{:S(2)}, u32[]{:S(2)}) collective-permute-start(bf16[32,128]{1,0:T(8,128)(2,1)S(1)} %bitcast.341), channel_id=1, source_target_pairs={{0,1},{1,2},{2,3},{3,0},{4,5},{5,6},{6,7},{7,4},{8,9},{9,10},{10,1... | collective-permute-start | bytes 24584 | tf_op jit(solution)/shard_map/ppermute | solution.py:14
  50.9 4.3 %collective-permute-start.13 = (bf16[8,32,128]{2,0,1:T(8,128)(2,1)S(1)}, bf16[8,32,128]{2,0,1:T(8,128)(2,1)S(1)}, u32[]{:S(2)}, u32[]{:S(2)}) collective-permute-start(bf16[8,32,128]{2,0,1:T(8,128)(2,1)S(1)} %copy.385), channel_id=1, source_target_pairs={{0,4},{4,0},{8,12},{12,8},{16,20},{20,16},{24,28},{28,24},{1,5},{5... | collective-permute-start | bytes 196616 | tf_op jit(solution)/shard_map/ppermute | solution.py:18
  52.9 1.5 %collective-permute-start.12 = (f32[32,128]{1,0:T(8,128)S(1)}, f32[32,128]{1,0:T(8,128)S(1)}, u32[]{:S(2)}, u32[]{:S(2)}) collective-permute-start(f32[32,128]{1,0:T(8,128)S(1)} %fusion.125), channel_id=1, source_target_pairs={{0,3},{1,0},{2,1},{3,2},{4,7},{5,4},{6,5},{7,6},{8,11},{9,8},{10,9... | collective-permute-start | bytes 49160 | tf_op jit(solution)/shard_map/ppermute | solution.py:14
  66.0 4.3 %collective-permute-start.14 = (bf16[8,32,128]{2,0,1:T(8,128)(2,1)S(1)}, bf16[8,32,128]{2,0,1:T(8,128)(2,1)S(1)}, u32[]{:S(2)}, u32[]{:S(2)}) collective-permute-start(bf16[8,32,128]{2,0,1:T(8,128)(2,1)S(1)} %get-tuple-element.22), channel_id=1, source_target_pairs={{0,4},{4,0},{8,12},{12,8},{16,20},{20,16},{24,28},{28,24},{1,5},{5... | collective-permute-start | bytes 196616 | tf_op jit(solution)/shard_map/ppermute | solution.py:18
  66.7 3.3 %collective-permute-start.15 = (bf16[32,128]{1,0:T(8,128)(2,1)S(1)}, bf16[32,128]{1,0:T(8,128)(2,1)S(1)}, u32[]{:S(2)}, u32[]{:S(2)}) collective-permute-start(bf16[32,128]{1,0:T(8,128)(2,1)S(1)} %bitcast.342), channel_id=1, source_target_pairs={{0,1},{1,2},{2,3},{3,0},{4,5},{5,6},{6,7},{7,4},{8,9},{9,10},{10,1... | collective-permute-start | bytes 24584 | tf_op jit(solution)/shard_map/ppermute | solution.py:14
  72.3 4.3 %collective-permute-start.17 = (bf16[8,32,128]{2,0,1:T(8,128)(2,1)S(1)}, bf16[8,32,128]{2,0,1:T(8,128)(2,1)S(1)}, u32[]{:S(2)}, u32[]{:S(2)}) collective-permute-start(bf16[8,32,128]{2,0,1:T(8,128)(2,1)S(1)} %copy.384), channel_id=1, source_target_pairs={{0,4},{4,0},{8,12},{12,8},{16,20},{20,16},{24,28},{28,24},{1,5},{5... | collective-permute-start | bytes 196616 | tf_op jit(solution)/shard_map/ppermute | solution.py:18
  74.4 1.5 %collective-permute-start.16 = (f32[32,128]{1,0:T(8,128)S(1)}, f32[32,128]{1,0:T(8,128)S(1)}, u32[]{:S(2)}, u32[]{:S(2)}) collective-permute-start(f32[32,128]{1,0:T(8,128)S(1)} %fusion.121), channel_id=1, source_target_pairs={{0,3},{1,0},{2,1},{3,2},{4,7},{5,4},{6,5},{7,6},{8,11},{9,8},{10,9... | collective-permute-start | bytes 49160 | tf_op jit(solution)/shard_map/ppermute | solution.py:14
  87.4 4.3 %collective-permute-start.18 = (bf16[8,32,128]{2,0,1:T(8,128)(2,1)S(1)}, bf16[8,32,128]{2,0,1:T(8,128)(2,1)S(1)}, u32[]{:S(2)}, u32[]{:S(2)}) collective-permute-start(bf16[8,32,128]{2,0,1:T(8,128)(2,1)S(1)} %get-tuple-element.25), channel_id=1, source_target_pairs={{0,4},{4,0},{8,12},{12,8},{16,20},{20,16},{24,28},{28,24},{1,5},{5... | collective-permute-start | bytes 196616 | tf_op jit(solution)/shard_map/ppermute | solution.py:18
  88.5 3.1 %collective-permute-start.19 = (bf16[32,128]{1,0:T(8,128)(2,1)S(1)}, bf16[32,128]{1,0:T(8,128)(2,1)S(1)}, u32[]{:S(2)}, u32[]{:S(2)}) collective-permute-start(bf16[32,128]{1,0:T(8,128)(2,1)S(1)} %bitcast.340), channel_id=1, source_target_pairs={{0,1},{1,2},{2,3},{3,0},{4,5},{5,6},{6,7},{7,4},{8,9},{9,10},{10,1... | collective-permute-start | bytes 24584 | tf_op jit(solution)/shard_map/ppermute | solution.py:14
  93.7 4.3 %collective-permute-start.21 = (bf16[8,32,128]{2,0,1:T(8,128)(2,1)S(1)}, bf16[8,32,128]{2,0,1:T(8,128)(2,1)S(1)}, u32[]{:S(2)}, u32[]{:S(2)}) collective-permute-start(bf16[8,32,128]{2,0,1:T(8,128)(2,1)S(1)} %copy.383), channel_id=1, source_target_pairs={{0,4},{4,0},{8,12},{12,8},{16,20},{20,16},{24,28},{28,24},{1,5},{5... | collective-permute-start | bytes 196616 | tf_op jit(solution)/shard_map/ppermute | solution.py:18
  96.1 1.5 %collective-permute-start.20 = (f32[32,128]{1,0:T(8,128)S(1)}, f32[32,128]{1,0:T(8,128)S(1)}, u32[]{:S(2)}, u32[]{:S(2)}) collective-permute-start(f32[32,128]{1,0:T(8,128)S(1)} %fusion.117), channel_id=1, source_target_pairs={{0,3},{1,0},{2,1},{3,2},{4,7},{5,4},{6,5},{7,6},{8,11},{9,8},{10,9... | collective-permute-start | bytes 49160 | tf_op jit(solution)/shard_map/ppermute | solution.py:14
  (7 other events, 23.3 us)

commit v24 on v23

--- a/solution.py
+++ b/solution.py
@@ -34,9 +34,12 @@
     result = result + jnp.einsum(
         "nmrk,nmkj->nrj", picked, off_tiles, preferred_element_type=jnp.float32
     )
-    mirror = jnp.einsum("nrk,nmjk->nmrj", rounded, off_tiles, preferred_element_type=jnp.float32)
-    mirror = mirror.reshape(-1, rounded.shape[1], rounded.shape[2])
-    return result + jnp.einsum("pn,prj->nrj", mirror_onehot, mirror, precision=lax.Precision.HIGHEST)
+    nodes = rounded.shape[0]
+    chosen = mirror_onehot.reshape(nodes, off_tiles.shape[1], nodes)
+    spread = chosen[:, :, :, None, None] * rounded[:, None, None, :, :]
+    return result + jnp.einsum(
+        "nmirk,nmjk->irj", spread, off_tiles, preferred_element_type=jnp.float32
+    )
 
 
 def apply_operator(vector, diag_tiles, off_tiles, link_tile, contact_set, tables):
@@ -121,7 +124,7 @@
     mirror_onehot = (off_cols.reshape(-1)[:, None] == blocks).astype(jnp.float32)
     tables = (
         mirror_onehot.astype(jnp.bfloat16),
-        mirror_onehot,
+        mirror_onehot.astype(jnp.bfloat16),
         near_collect,
         far_collect,
         near_collect.astype(jnp.bfloat16),

time: 110 us -> 109 us (level)
  matrix products: 19 us -> 16.4 us
  other arithmetic: 6.42 us -> 8.87 us
    dot_general x8 -> x4, matrix products: 4.57 us -> 1.98 us  [local_stiffness(): jnp.einsum('nmirk,nmjk->irj', spread, off_tiles, preferred_element_type=j...]
    reduce_sum x1 -> x4, other arithmetic: 0.31 us -> 2.19 us  [body(): jnp.sum(residual * preconditioned, axis=(0, 2))]
  transfers between devices with their start and end apart: 22 -> 22, of which waited for: 15 -> 15; matrix products, arithmetic and copies ran while one was open for 9% -> 10% of each run, Pallas kernels for 0% -> 0%
where the time goes in v24:
time: 109 us
  blocking collectives  39.4 us (36%)
  waiting for transfers between devices  23.3 us (21%)
  matrix products  16.4 us (15%)
  starting transfers between devices  15.4 us (14%)
  other arithmetic  8.87 us (8%)
  local copies, waits for them, and re-layouts  3.82 us (4%)
  between operations  1.35 us (1%)
    all_to_all x4, blocking collectives, total(): gathered = lax.all_to_all(spread, ('dom', 'rep'), 0, 0, tiled=True)  39.4 us
    ppermute x14, waiting for transfers between devices, from_behind(): return lax.ppermute(value, axis, pairs)  20.3 us
    ppermute x8, starting transfers between devices, partner(): lax.ppermute(value, axis, [(i, i ^ 1 << distance) for i in range(lax.axis...  8.92 us
    ppermute x14, starting transfers between devices, from_behind(): return lax.ppermute(value, axis, pairs)  6.46 us
    dot_general x4, matrix products, apply_operator(): jnp.einsum('snrj,skj->nrk', spread, contact_set, preferred_element_type=j...  3.09 us
    ppermute x8, waiting for transfers between devices, partner(): lax.ppermute(value, axis, [(i, i ^ 1 << distance) for i in range(lax.axis...  3.04 us
    dot_general x4, matrix products, apply_operator(): jnp.einsum('snrj,skj->nrk', near_spread, contact_set, preferred_element_t...  3 us
    unnamed x31, local copies, waits for them, and re-layouts  2.39 us
  transfers between devices with their start and end apart: 22, of which 15 were waited for; matrix products, arithmetic and copies ran while one was open for 10% of the time, Pallas kernels for 0%

profile of v24, /device:TPU:0, one launch (start us, length us, event | category | flops | bytes accessed | tf_op | source)
XLA Modules:
  0.0 108.5 jit_solution(17228983901266508189)
XLA Ops:
  1.4 0.9 add_reduce_fusion
  3.0 2.4 %collective-permute-start.6 = (bf16[8,128,128]{2,0,1:T(8,128)(2,1)S(1)}, bf16[8,128,128]{2,0,1:T(8,128)(2,1)}, u32[]{:S(2)}, u32[]{:S(2)}) collective-permute-start(bf16[8,128,128]{2,0,1:T(8,128)(2,1)S(1)} %select_bitcast_fusion), channel_id=1, source_target_pairs={{0,3},{1,0},{2,1},{3,2},{4,7},{5,4},{6,5},{7,6},{8,11},{9,8},{10,9... | collective-permute-start | bytes 786440 | tf_op jit(solution)/shard_map/ppermute | solution.py:14
  6.7 1.7 %collective-permute-start.1 = (s32[8,2]{0,1:T(2,128)S(1)}, s32[8,2]{0,1:T(2,128)S(1)}, u32[]{:S(2)}, u32[]{:S(2)}) collective-permute-start(s32[8,2]{0,1:T(2,128)S(1)} %bitcast.341), channel_id=1, source_target_pairs={{0,2},{1,3},{2,0},{3,1},{4,6},{5,7},{6,4},{7,5},{8,10},{9,11},{10,... | collective-permute-start | bytes 200 | tf_op jit(solution)/shard_map/ppermute | solution.py:14
  8.5 1.6 %collective-permute-start.3 = (bf16[8,32,128]{2,0,1:T(8,128)(2,1)S(1)}, bf16[8,32,128]{2,0,1:T(8,128)(2,1)S(1)}, u32[]{:S(2)}, u32[]{:S(2)}) collective-permute-start(bf16[8,32,128]{2,0,1:T(8,128)(2,1)S(1)} %multiply_convert_fusion), channel_id=1, source_target_pairs={{0,4},{4,0},{8,12},{12,8},{16,20},{20,16},{24,28},{28,24},{1,5},{5... | collective-permute-start | bytes 196616 | tf_op jit(solution)/shard_map/ppermute | solution.py:18
  10.4 4.6 %collective-permute-done.2 = s32[8,2]{0,1:T(2,128)S(1)} collective-permute-done((s32[8,2]{0,1:T(2,128)S(1)}, s32[8,2]{0,1:T(2,128)S(1)}, u32[]{:S(2)}, u32[]{:S(2)}) %collective-permute-start.2) | collective-permute-done | bytes 96 | tf_op jit(solution)/shard_map/ppermute | solution.py:14
  15.0 1.1 %collective-permute-start = (s32[8,2]{0,1:T(2,128)S(1)}, s32[8,2]{0,1:T(2,128)S(1)}, u32[]{:S(2)}, u32[]{:S(2)}) collective-permute-start(s32[8,2]{0,1:T(2,128)S(1)} %bitcast.340), channel_id=1, source_target_pairs={{0,1},{1,2},{2,3},{3,0},{4,5},{5,6},{6,7},{7,4},{8,9},{9,10},{10,1... | collective-permute-start | bytes 200 | tf_op jit(solution)/shard_map/ppermute | solution.py:14
  16.1 2.3 %collective-permute-done = s32[8,2]{0,1:T(2,128)S(1)} collective-permute-done((s32[8,2]{0,1:T(2,128)S(1)}, s32[8,2]{0,1:T(2,128)S(1)}, u32[]{:S(2)}, u32[]{:S(2)}) %collective-permute-start) | collective-permute-done | bytes 96 | tf_op jit(solution)/shard_map/ppermute | solution.py:14
  19.0 3.0 %collective-permute-done.7 = bf16[32,128]{1,0:T(8,128)(2,1)S(1)} collective-permute-done((bf16[32,128]{1,0:T(8,128)(2,1)S(1)}, bf16[32,128]{1,0:T(8,128)(2,1)S(1)}, u32[]{:S(2)}, u32[]{:S(2)}) %collective-permute-start.7) | collective-permute-done | bytes 8224 | tf_op jit(solution)/shard_map/ppermute | solution.py:14
  22.4 1.1 pad_maximum_fusion
  25.0 1.6 %collective-permute-start.9 = (bf16[8,32,128]{2,0,1:T(8,128)(2,1)S(1)}, bf16[8,32,128]{2,0,1:T(8,128)(2,1)S(1)}, u32[]{:S(2)}, u32[]{:S(2)}) collective-permute-start(bf16[8,32,128]{2,0,1:T(8,128)(2,1)S(1)} %copy.374), channel_id=1, source_target_pairs={{0,4},{4,0},{8,12},{12,8},{16,20},{20,16},{24,28},{28,24},{1,5},{5... | collective-permute-start | bytes 196616 | tf_op jit(solution)/shard_map/ppermute | solution.py:18
  30.2 12.8 %all_to_all.20 = f32[32,1,128]{2,1,0:T(1,128)S(1)} all-to-all(f32[32,1,128]{2,1,0:T(1,128)S(1)} %reshape.433), channel_id=1, replica_groups=mesh['dom'=8,'rep'=4] {'dom','rep'}, dimensions={0} | all-to-all | bytes 32768 | tf_op jit(solution)/shard_map/all_to_all | solution.py:24
  45.6 2.6 %collective-permute-done.11 = bf16[32,128]{1,0:T(8,128)(2,1)S(1)} collective-permute-done((bf16[32,128]{1,0:T(8,128)(2,1)S(1)}, bf16[32,128]{1,0:T(8,128)(2,1)S(1)}, u32[]{:S(2)}, u32[]{:S(2)}) %collective-permute-start.11) | collective-permute-done | bytes 8224 | tf_op jit(solution)/shard_map/ppermute | solution.py:14
  49.5 0.8 fusion.27
  50.7 1.1 %collective-permute-start.13 = (bf16[8,32,128]{2,0,1:T(8,128)(2,1)S(1)}, bf16[8,32,128]{2,0,1:T(8,128)(2,1)S(1)}, u32[]{:S(2)}, u32[]{:S(2)}) collective-permute-start(bf16[8,32,128]{2,0,1:T(8,128)(2,1)S(1)} %copy.373), channel_id=1, source_target_pairs={{0,4},{4,0},{8,12},{12,8},{16,20},{20,16},{24,28},{28,24},{1,5},{5... | collective-permute-start | bytes 196616 | tf_op jit(solution)/shard_map/ppermute | solution.py:18
  54.2 0.9 collective-permute-done.13
  55.8 8.8 %all_to_all.21 = f32[32,1,128]{2,1,0:T(1,128)S(1)} all-to-all(f32[32,1,128]{2,1,0:T(1,128)S(1)} %reshape.435), channel_id=1, replica_groups=mesh['dom'=8,'rep'=4] {'dom','rep'}, dimensions={0} | all-to-all | bytes 32768 | tf_op jit(solution)/shard_map/all_to_all | solution.py:24
  66.9 2.6 %collective-permute-done.15 = bf16[32,128]{1,0:T(8,128)(2,1)S(1)} collective-permute-done((bf16[32,128]{1,0:T(8,128)(2,1)S(1)}, bf16[32,128]{1,0:T(8,128)(2,1)S(1)}, u32[]{:S(2)}, u32[]{:S(2)}) %collective-permute-start.15) | collective-permute-done | bytes 8224 | tf_op jit(solution)/shard_map/ppermute | solution.py:14
  70.6 0.8 fusion.33
  71.9 1.3 %collective-permute-start.17 = (bf16[8,32,128]{2,0,1:T(8,128)(2,1)S(1)}, bf16[8,32,128]{2,0,1:T(8,128)(2,1)S(1)}, u32[]{:S(2)}, u32[]{:S(2)}) collective-permute-start(bf16[8,32,128]{2,0,1:T(8,128)(2,1)S(1)} %copy.372), channel_id=1, source_target_pairs={{0,4},{4,0},{8,12},{12,8},{16,20},{20,16},{24,28},{28,24},{1,5},{5... | collective-permute-start | bytes 196616 | tf_op jit(solution)/shard_map/ppermute | solution.py:18
  76.9 8.8 %all_to_all.22 = f32[32,1,128]{2,1,0:T(1,128)S(1)} all-to-all(f32[32,1,128]{2,1,0:T(1,128)S(1)} %reshape.437), channel_id=1, replica_groups=mesh['dom'=8,'rep'=4] {'dom','rep'}, dimensions={0} | all-to-all | bytes 32768 | tf_op jit(solution)/shard_map/all_to_all | solution.py:24
  88.2 2.7 %collective-permute-done.19 = bf16[32,128]{1,0:T(8,128)(2,1)S(1)} collective-permute-done((bf16[32,128]{1,0:T(8,128)(2,1)S(1)}, bf16[32,128]{1,0:T(8,128)(2,1)S(1)}, u32[]{:S(2)}, u32[]{:S(2)}) %collective-permute-start.19) | collective-permute-done | bytes 8224 | tf_op jit(solution)/shard_map/ppermute | solution.py:14
  91.8 0.8 fusion.39
  93.0 1.5 %collective-permute-start.21 = (bf16[8,32,128]{2,0,1:T(8,128)(2,1)S(1)}, bf16[8,32,128]{2,0,1:T(8,128)(2,1)S(1)}, u32[]{:S(2)}, u32[]{:S(2)}) collective-permute-start(bf16[8,32,128]{2,0,1:T(8,128)(2,1)S(1)} %copy.371), channel_id=1, source_target_pairs={{0,4},{4,0},{8,12},{12,8},{16,20},{20,16},{24,28},{28,24},{1,5},{5... | collective-permute-start | bytes 196616 | tf_op jit(solution)/shard_map/ppermute | solution.py:18
  97.9 8.9 %all_to_all.23 = f32[32,2,32]{2,1,0:T(2,128)S(1)} all-to-all(f32[32,2,32]{2,1,0:T(2,128)S(1)} %broadcast_in_dim.90), channel_id=1, replica_groups=mesh['dom'=8,'rep'=4] {'dom','rep'}, dimensions={0} | all-to-all | bytes 16384 | tf_op jit(solution)/shard_map/all_to_all | solution.py:24
  (167 shorter events, 32.2 us)
Async XLA Ops:
  3.0 7.1 %copy-start.6 = (s32[8,2]{0,1:T(2,128)S(1)}, s32[8,2]{0,1:T(2,128)}, u32[]{:S(2)}) copy-start(s32[8,2]{0,1:T(2,128)} %param.18) | copy-start | bytes 196
  3.0 19.4 %collective-permute-start.6 = (bf16[8,128,128]{2,0,1:T(8,128)(2,1)S(1)}, bf16[8,128,128]{2,0,1:T(8,128)(2,1)}, u32[]{:S(2)}, u32[]{:S(2)}) collective-permute-start(bf16[8,128,128]{2,0,1:T(8,128)(2,1)S(1)} %select_bitcast_fusion), channel_id=1, source_target_pairs={{0,3},{1,0},{2,1},{3,2},{4,7},{5,4},{6,5},{7,6},{8,11},{9,8},{10,9... | collective-permute-start | bytes 786440 | tf_op jit(solution)/shard_map/ppermute | solution.py:14
  5.4 16.5 %copy-start.4 = (bf16[1,128,128]{2,1,0:T(8,128)(2,1)S(1)}, bf16[1,128,128]{2,1,0:T(8,128)(2,1)}, u32[]{:S(2)}) copy-start(bf16[1,128,128]{2,1,0:T(8,128)(2,1)} %param.19) | copy-start | bytes 98308
  5.6 16.9 %collective-permute-start.5 = (bf16[8,128,128]{2,0,1:T(8,128)(2,1)S(1)}, bf16[8,128,128]{2,0,1:T(8,128)(2,1)S(1)}, u32[]{:S(2)}, u32[]{:S(2)}) collective-permute-start(bf16[8,128,128]{2,0,1:T(8,128)(2,1)S(1)} %get-tuple-element.89), channel_id=1, source_target_pairs={{0,2},{1,3},{2,0},{3,1},{4,6},{5,7},{6,4},{7,5},{8,10},{9,11},{10,... | collective-permute-start | bytes 786440 | tf_op jit(solution)/shard_map/ppermute | solution.py:14
  6.6 8.4 %collective-permute-start.2 = (s32[8,2]{0,1:T(2,128)S(1)}, s32[8,2]{0,1:T(2,128)S(1)}, u32[]{:S(2)}, u32[]{:S(2)}) collective-permute-start(s32[8,2]{0,1:T(2,128)S(1)} %bitcast.342), channel_id=1, source_target_pairs={{0,3},{1,0},{2,1},{3,2},{4,7},{5,4},{6,5},{7,6},{8,11},{9,8},{10,9... | collective-permute-start | bytes 200 | tf_op jit(solution)/shard_map/ppermute | solution.py:14
  6.7 9.5 %collective-permute-start.1 = (s32[8,2]{0,1:T(2,128)S(1)}, s32[8,2]{0,1:T(2,128)S(1)}, u32[]{:S(2)}, u32[]{:S(2)}) collective-permute-start(s32[8,2]{0,1:T(2,128)S(1)} %bitcast.341), channel_id=1, source_target_pairs={{0,2},{1,3},{2,0},{3,1},{4,6},{5,7},{6,4},{7,5},{8,10},{9,11},{10,... | collective-permute-start | bytes 200 | tf_op jit(solution)/shard_map/ppermute | solution.py:14
  8.5 13.6 %collective-permute-start.3 = (bf16[8,32,128]{2,0,1:T(8,128)(2,1)S(1)}, bf16[8,32,128]{2,0,1:T(8,128)(2,1)S(1)}, u32[]{:S(2)}, u32[]{:S(2)}) collective-permute-start(bf16[8,32,128]{2,0,1:T(8,128)(2,1)S(1)} %multiply_convert_fusion), channel_id=1, source_target_pairs={{0,4},{4,0},{8,12},{12,8},{16,20},{20,16},{24,28},{28,24},{1,5},{5... | collective-permute-start | bytes 196616 | tf_op jit(solution)/shard_map/ppermute | solution.py:18
  15.0 3.4 %collective-permute-start = (s32[8,2]{0,1:T(2,128)S(1)}, s32[8,2]{0,1:T(2,128)S(1)}, u32[]{:S(2)}, u32[]{:S(2)}) collective-permute-start(s32[8,2]{0,1:T(2,128)S(1)} %bitcast.340), channel_id=1, source_target_pairs={{0,1},{1,2},{2,3},{3,0},{4,5},{5,6},{6,7},{7,4},{8,9},{9,10},{10,1... | collective-permute-start | bytes 200 | tf_op jit(solution)/shard_map/ppermute | solution.py:14
  16.1 6.3 %collective-permute-start.4 = (bf16[8,128,128]{2,0,1:T(8,128)(2,1)S(1)}, bf16[8,128,128]{2,0,1:T(8,128)(2,1)S(1)}, u32[]{:S(2)}, u32[]{:S(2)}) collective-permute-start(bf16[8,128,128]{2,0,1:T(8,128)(2,1)S(1)} %get-tuple-element.88), channel_id=1, source_target_pairs={{0,1},{1,2},{2,3},{3,0},{4,5},{5,6},{6,7},{7,4},{8,9},{9,10},{10,1... | collective-permute-start | bytes 786440 | tf_op jit(solution)/shard_map/ppermute | solution.py:14
  18.4 3.6 %collective-permute-start.7 = (bf16[32,128]{1,0:T(8,128)(2,1)S(1)}, bf16[32,128]{1,0:T(8,128)(2,1)S(1)}, u32[]{:S(2)}, u32[]{:S(2)}) collective-permute-start(bf16[32,128]{1,0:T(8,128)(2,1)S(1)} %bitcast.321), channel_id=1, source_target_pairs={{0,1},{1,2},{2,3},{3,0},{4,5},{5,6},{6,7},{7,4},{8,9},{9,10},{10,1... | collective-permute-start | bytes 24584 | tf_op jit(solution)/shard_map/ppermute | solution.py:14
  25.0 4.3 %collective-permute-start.9 = (bf16[8,32,128]{2,0,1:T(8,128)(2,1)S(1)}, bf16[8,32,128]{2,0,1:T(8,128)(2,1)S(1)}, u32[]{:S(2)}, u32[]{:S(2)}) collective-permute-start(bf16[8,32,128]{2,0,1:T(8,128)(2,1)S(1)} %copy.374), channel_id=1, source_target_pairs={{0,4},{4,0},{8,12},{12,8},{16,20},{20,16},{24,28},{28,24},{1,5},{5... | collective-permute-start | bytes 196616 | tf_op jit(solution)/shard_map/ppermute | solution.py:18
  26.7 2.2 %collective-permute-start.8 = (f32[32,128]{1,0:T(8,128)S(1)}, f32[32,128]{1,0:T(8,128)S(1)}, u32[]{:S(2)}, u32[]{:S(2)}) collective-permute-start(f32[32,128]{1,0:T(8,128)S(1)} %fusion.125), channel_id=1, source_target_pairs={{0,3},{1,0},{2,1},{3,2},{4,7},{5,4},{6,5},{7,6},{8,11},{9,8},{10,9... | collective-permute-start | bytes 49160 | tf_op jit(solution)/shard_map/ppermute | solution.py:14
  44.5 4.3 %collective-permute-start.10 = (bf16[8,32,128]{2,0,1:T(8,128)(2,1)S(1)}, bf16[8,32,128]{2,0,1:T(8,128)(2,1)S(1)}, u32[]{:S(2)}, u32[]{:S(2)}) collective-permute-start(bf16[8,32,128]{2,0,1:T(8,128)(2,1)S(1)} %get-tuple-element.19), channel_id=1, source_target_pairs={{0,4},{4,0},{8,12},{12,8},{16,20},{20,16},{24,28},{28,24},{1,5},{5... | collective-permute-start | bytes 196616 | tf_op jit(solution)/shard_map/ppermute | solution.py:18
  45.1 3.1 %collective-permute-start.11 = (bf16[32,128]{1,0:T(8,128)(2,1)S(1)}, bf16[32,128]{1,0:T(8,128)(2,1)S(1)}, u32[]{:S(2)}, u32[]{:S(2)}) collective-permute-start(bf16[32,128]{1,0:T(8,128)(2,1)S(1)} %bitcast.323), channel_id=1, source_target_pairs={{0,1},{1,2},{2,3},{3,0},{4,5},{5,6},{6,7},{7,4},{8,9},{9,10},{10,1... | collective-permute-start | bytes 24584 | tf_op jit(solution)/shard_map/ppermute | solution.py:14
  50.7 4.3 %collective-permute-start.13 = (bf16[8,32,128]{2,0,1:T(8,128)(2,1)S(1)}, bf16[8,32,128]{2,0,1:T(8,128)(2,1)S(1)}, u32[]{:S(2)}, u32[]{:S(2)}) collective-permute-start(bf16[8,32,128]{2,0,1:T(8,128)(2,1)S(1)} %copy.373), channel_id=1, source_target_pairs={{0,4},{4,0},{8,12},{12,8},{16,20},{20,16},{24,28},{28,24},{1,5},{5... | collective-permute-start | bytes 196616 | tf_op jit(solution)/shard_map/ppermute | solution.py:18
  52.7 1.5 %collective-permute-start.12 = (f32[32,128]{1,0:T(8,128)S(1)}, f32[32,128]{1,0:T(8,128)S(1)}, u32[]{:S(2)}, u32[]{:S(2)}) collective-permute-start(f32[32,128]{1,0:T(8,128)S(1)} %fusion.121), channel_id=1, source_target_pairs={{0,3},{1,0},{2,1},{3,2},{4,7},{5,4},{6,5},{7,6},{8,11},{9,8},{10,9... | collective-permute-start | bytes 49160 | tf_op jit(solution)/shard_map/ppermute | solution.py:14
  65.6 4.3 %collective-permute-start.14 = (bf16[8,32,128]{2,0,1:T(8,128)(2,1)S(1)}, bf16[8,32,128]{2,0,1:T(8,128)(2,1)S(1)}, u32[]{:S(2)}, u32[]{:S(2)}) collective-permute-start(bf16[8,32,128]{2,0,1:T(8,128)(2,1)S(1)} %get-tuple-element.22), channel_id=1, source_target_pairs={{0,4},{4,0},{8,12},{12,8},{16,20},{20,16},{24,28},{28,24},{1,5},{5... | collective-permute-start | bytes 196616 | tf_op jit(solution)/shard_map/ppermute | solution.py:18
  66.3 3.3 %collective-permute-start.15 = (bf16[32,128]{1,0:T(8,128)(2,1)S(1)}, bf16[32,128]{1,0:T(8,128)(2,1)S(1)}, u32[]{:S(2)}, u32[]{:S(2)}) collective-permute-start(bf16[32,128]{1,0:T(8,128)(2,1)S(1)} %bitcast.324), channel_id=1, source_target_pairs={{0,1},{1,2},{2,3},{3,0},{4,5},{5,6},{6,7},{7,4},{8,9},{9,10},{10,1... | collective-permute-start | bytes 24584 | tf_op jit(solution)/shard_map/ppermute | solution.py:14
  71.9 4.3 %collective-permute-start.17 = (bf16[8,32,128]{2,0,1:T(8,128)(2,1)S(1)}, bf16[8,32,128]{2,0,1:T(8,128)(2,1)S(1)}, u32[]{:S(2)}, u32[]{:S(2)}) collective-permute-start(bf16[8,32,128]{2,0,1:T(8,128)(2,1)S(1)} %copy.372), channel_id=1, source_target_pairs={{0,4},{4,0},{8,12},{12,8},{16,20},{20,16},{24,28},{28,24},{1,5},{5... | collective-permute-start | bytes 196616 | tf_op jit(solution)/shard_map/ppermute | solution.py:18
  74.1 1.5 %collective-permute-start.16 = (f32[32,128]{1,0:T(8,128)S(1)}, f32[32,128]{1,0:T(8,128)S(1)}, u32[]{:S(2)}, u32[]{:S(2)}) collective-permute-start(f32[32,128]{1,0:T(8,128)S(1)} %fusion.117), channel_id=1, source_target_pairs={{0,3},{1,0},{2,1},{3,2},{4,7},{5,4},{6,5},{7,6},{8,11},{9,8},{10,9... | collective-permute-start | bytes 49160 | tf_op jit(solution)/shard_map/ppermute | solution.py:14
  86.8 4.3 %collective-permute-start.18 = (bf16[8,32,128]{2,0,1:T(8,128)(2,1)S(1)}, bf16[8,32,128]{2,0,1:T(8,128)(2,1)S(1)}, u32[]{:S(2)}, u32[]{:S(2)}) collective-permute-start(bf16[8,32,128]{2,0,1:T(8,128)(2,1)S(1)} %get-tuple-element.25), channel_id=1, source_target_pairs={{0,4},{4,0},{8,12},{12,8},{16,20},{20,16},{24,28},{28,24},{1,5},{5... | collective-permute-start | bytes 196616 | tf_op jit(solution)/shard_map/ppermute | solution.py:18
  87.8 3.1 %collective-permute-start.19 = (bf16[32,128]{1,0:T(8,128)(2,1)S(1)}, bf16[32,128]{1,0:T(8,128)(2,1)S(1)}, u32[]{:S(2)}, u32[]{:S(2)}) collective-permute-start(bf16[32,128]{1,0:T(8,128)(2,1)S(1)} %bitcast.322), channel_id=1, source_target_pairs={{0,1},{1,2},{2,3},{3,0},{4,5},{5,6},{6,7},{7,4},{8,9},{9,10},{10,1... | collective-permute-start | bytes 24584 | tf_op jit(solution)/shard_map/ppermute | solution.py:14
  93.0 4.3 %collective-permute-start.21 = (bf16[8,32,128]{2,0,1:T(8,128)(2,1)S(1)}, bf16[8,32,128]{2,0,1:T(8,128)(2,1)S(1)}, u32[]{:S(2)}, u32[]{:S(2)}) collective-permute-start(bf16[8,32,128]{2,0,1:T(8,128)(2,1)S(1)} %copy.371), channel_id=1, source_target_pairs={{0,4},{4,0},{8,12},{12,8},{16,20},{20,16},{24,28},{28,24},{1,5},{5... | collective-permute-start | bytes 196616 | tf_op jit(solution)/shard_map/ppermute | solution.py:18
  95.5 1.5 %collective-permute-start.20 = (f32[32,128]{1,0:T(8,128)S(1)}, f32[32,128]{1,0:T(8,128)S(1)}, u32[]{:S(2)}, u32[]{:S(2)}) collective-permute-start(f32[32,128]{1,0:T(8,128)S(1)} %fusion.113), channel_id=1, source_target_pairs={{0,3},{1,0},{2,1},{3,2},{4,7},{5,4},{6,5},{7,6},{8,11},{9,8},{10,9... | collective-permute-start | bytes 49160 | tf_op jit(solution)/shard_map/ppermute | solution.py:14
  (7 other events, 23.4 us)

commit v25 on v24

--- a/solution.py
+++ b/solution.py
@@ -74,6 +74,7 @@
     result = result + jnp.einsum(
         "snrj,skj->nrk", near_spread, contact_set, preferred_element_type=jnp.float32
     )
+    result = lax.optimization_barrier(result)
     return result - far_terms
 
 

time: 109 us -> 114 us (1.046)
  waiting for transfers between devices: 23.3 us -> 29 us
    ppermute x8, waiting for transfers between devices: 3.04 us -> 11 us  [partner(): lax.ppermute(value, axis, [(i, i ^ 1 << distance) for i in range(lax.axis...]
    ppermute x14, waiting for transfers between devices: 20.3 us -> 18 us  [from_behind(): return lax.ppermute(value, axis, pairs)]
    reduce_sum x4 -> x1, other arithmetic: 2.19 us -> 0.31 us  [body(): jnp.sum(residual * preconditioned, axis=(0, 2))]
    add x0 -> x4, other arithmetic: none -> 1.28 us  [apply_operator(): result + jnp.einsum('snrj,skj->nrk', near_spread, contact_set, preferred_...]
  transfers between devices with their start and end apart: 22 -> 22, of which waited for: 15 -> 12; matrix products, arithmetic and copies ran while one was open for 10% -> 10% of each run, Pallas kernels for 0% -> 0%
where the time goes in v25:
time: 114 us
  blocking collectives  39.4 us (35%)
  waiting for transfers between devices  29 us (25%)
  matrix products  16.4 us (14%)
  starting transfers between devices  15.2 us (13%)
  other arithmetic  9.02 us (8%)
  local copies, waits for them, and re-layouts  3.53 us (3%)
  between operations  1.4 us (1%)
    all_to_all x4, blocking collectives, total(): gathered = lax.all_to_all(spread, ('dom', 'rep'), 0, 0, tiled=True)  39.4 us
    ppermute x14, waiting for transfers between devices, from_behind(): return lax.ppermute(value, axis, pairs)  18 us
    ppermute x8, waiting for transfers between devices, partner(): lax.ppermute(value, axis, [(i, i ^ 1 << distance) for i in range(lax.axis...  11 us
    ppermute x8, starting transfers between devices, partner(): lax.ppermute(value, axis, [(i, i ^ 1 << distance) for i in range(lax.axis...  8.79 us
    ppermute x14, starting transfers between devices, from_behind(): return lax.ppermute(value, axis, pairs)  6.41 us
    dot_general x4, matrix products, apply_operator(): jnp.einsum('snrj,skj->nrk', spread, contact_set, preferred_element_type=j...  3.1 us
    dot_general x4, matrix products, apply_operator(): jnp.einsum('snrj,skj->nrk', near_spread, contact_set, preferred_element_t...  3.05 us
  transfers between devices with their start and end apart: 22, of which 12 were waited for; matrix products, arithmetic and copies ran while one was open for 10% of the time, Pallas kernels for 0%

profile of v25, /device:TPU:0, one launch (start us, length us, event | category | flops | bytes accessed | tf_op | source)
XLA Modules:
  0.0 113.9 jit_solution(15643932727247475266)
XLA Ops:
  1.4 0.9 add_reduce_fusion
  3.0 2.4 %collective-permute-start.6 = (bf16[8,128,128]{2,0,1:T(8,128)(2,1)S(1)}, bf16[8,128,128]{2,0,1:T(8,128)(2,1)}, u32[]{:S(2)}, u32[]{:S(2)}) collective-permute-start(bf16[8,128,128]{2,0,1:T(8,128)(2,1)S(1)} %select_bitcast_fusion), channel_id=1, source_target_pairs={{0,3},{1,0},{2,1},{3,2},{4,7},{5,4},{6,5},{7,6},{8,11},{9,8},{10,9... | collective-permute-start | bytes 786440 | tf_op jit(solution)/shard_map/ppermute | solution.py:14
  6.7 1.7 %collective-permute-start.1 = (s32[8,2]{0,1:T(2,128)S(1)}, s32[8,2]{0,1:T(2,128)S(1)}, u32[]{:S(2)}, u32[]{:S(2)}) collective-permute-start(s32[8,2]{0,1:T(2,128)S(1)} %bitcast.341), channel_id=1, source_target_pairs={{0,2},{1,3},{2,0},{3,1},{4,6},{5,7},{6,4},{7,5},{8,10},{9,11},{10,... | collective-permute-start | bytes 200 | tf_op jit(solution)/shard_map/ppermute | solution.py:14
  8.5 1.6 %collective-permute-start.3 = (bf16[8,32,128]{2,0,1:T(8,128)(2,1)S(1)}, bf16[8,32,128]{2,0,1:T(8,128)(2,1)S(1)}, u32[]{:S(2)}, u32[]{:S(2)}) collective-permute-start(bf16[8,32,128]{2,0,1:T(8,128)(2,1)S(1)} %multiply_convert_fusion), channel_id=1, source_target_pairs={{0,4},{4,0},{8,12},{12,8},{16,20},{20,16},{24,28},{28,24},{1,5},{5... | collective-permute-start | bytes 196616 | tf_op jit(solution)/shard_map/ppermute | solution.py:18
  10.4 4.6 %collective-permute-done.2 = s32[8,2]{0,1:T(2,128)S(1)} collective-permute-done((s32[8,2]{0,1:T(2,128)S(1)}, s32[8,2]{0,1:T(2,128)S(1)}, u32[]{:S(2)}, u32[]{:S(2)}) %collective-permute-start.2) | collective-permute-done | bytes 96 | tf_op jit(solution)/shard_map/ppermute | solution.py:14
  15.0 1.1 collective-permute-start
  16.1 2.3 %collective-permute-done = s32[8,2]{0,1:T(2,128)S(1)} collective-permute-done((s32[8,2]{0,1:T(2,128)S(1)}, s32[8,2]{0,1:T(2,128)S(1)}, u32[]{:S(2)}, u32[]{:S(2)}) %collective-permute-start) | collective-permute-done | bytes 96 | tf_op jit(solution)/shard_map/ppermute | solution.py:14
  19.0 3.0 %collective-permute-done.7 = bf16[32,128]{1,0:T(8,128)(2,1)S(1)} collective-permute-done((bf16[32,128]{1,0:T(8,128)(2,1)S(1)}, bf16[32,128]{1,0:T(8,128)(2,1)S(1)}, u32[]{:S(2)}, u32[]{:S(2)}) %collective-permute-start.7) | collective-permute-done | bytes 8224 | tf_op jit(solution)/shard_map/ppermute | solution.py:14
  22.4 1.1 pad_maximum_fusion
  25.6 1.6 %collective-permute-start.9 = (bf16[8,32,128]{2,0,1:T(8,128)(2,1)S(1)}, bf16[8,32,128]{2,0,1:T(8,128)(2,1)S(1)}, u32[]{:S(2)}, u32[]{:S(2)}) collective-permute-start(bf16[8,32,128]{2,0,1:T(8,128)(2,1)S(1)} %copy.374), channel_id=1, source_target_pairs={{0,4},{4,0},{8,12},{12,8},{16,20},{20,16},{24,28},{28,24},{1,5},{5... | collective-permute-start | bytes 196616 | tf_op jit(solution)/shard_map/ppermute | solution.py:18
  29.0 1.2 %collective-permute-done.9 = bf16[8,32,128]{2,0,1:T(8,128)(2,1)S(1)} collective-permute-done((bf16[8,32,128]{2,0,1:T(8,128)(2,1)S(1)}, bf16[8,32,128]{2,0,1:T(8,128)(2,1)S(1)}, u32[]{:S(2)}, u32[]{:S(2)}) %collective-permute-start.9) | collective-permute-done | bytes 65568 | tf_op jit(solution)/shard_map/ppermute | solution.py:18
  30.6 12.8 %all_to_all.20 = f32[32,1,128]{2,1,0:T(1,128)S(1)} all-to-all(f32[32,1,128]{2,1,0:T(1,128)S(1)} %reshape.433), channel_id=1, replica_groups=mesh['dom'=8,'rep'=4] {'dom','rep'}, dimensions={0} | all-to-all | bytes 32768 | tf_op jit(solution)/shard_map/all_to_all | solution.py:24
  46.1 2.6 %collective-permute-done.11 = bf16[32,128]{1,0:T(8,128)(2,1)S(1)} collective-permute-done((bf16[32,128]{1,0:T(8,128)(2,1)S(1)}, bf16[32,128]{1,0:T(8,128)(2,1)S(1)}, u32[]{:S(2)}, u32[]{:S(2)}) %collective-permute-start.11) | collective-permute-done | bytes 8224 | tf_op jit(solution)/shard_map/ppermute | solution.py:14
  52.8 1.1 collective-permute-start.13
  54.2 3.1 %collective-permute-done.13 = bf16[8,32,128]{2,0,1:T(8,128)(2,1)S(1)} collective-permute-done((bf16[8,32,128]{2,0,1:T(8,128)(2,1)S(1)}, bf16[8,32,128]{2,0,1:T(8,128)(2,1)S(1)}, u32[]{:S(2)}, u32[]{:S(2)}) %collective-permute-start.13) | collective-permute-done | bytes 65568 | tf_op jit(solution)/shard_map/ppermute | solution.py:18
  57.8 8.8 %all_to_all.21 = f32[32,1,128]{2,1,0:T(1,128)S(1)} all-to-all(f32[32,1,128]{2,1,0:T(1,128)S(1)} %reshape.435), channel_id=1, replica_groups=mesh['dom'=8,'rep'=4] {'dom','rep'}, dimensions={0} | all-to-all | bytes 32768 | tf_op jit(solution)/shard_map/all_to_all | solution.py:24
  68.8 2.6 %collective-permute-done.15 = bf16[32,128]{1,0:T(8,128)(2,1)S(1)} collective-permute-done((bf16[32,128]{1,0:T(8,128)(2,1)S(1)}, bf16[32,128]{1,0:T(8,128)(2,1)S(1)}, u32[]{:S(2)}, u32[]{:S(2)}) %collective-permute-start.15) | collective-permute-done | bytes 8224 | tf_op jit(solution)/shard_map/ppermute | solution.py:14
  75.6 1.1 collective-permute-start.17
  77.1 3.1 %collective-permute-done.17 = bf16[8,32,128]{2,0,1:T(8,128)(2,1)S(1)} collective-permute-done((bf16[8,32,128]{2,0,1:T(8,128)(2,1)S(1)}, bf16[8,32,128]{2,0,1:T(8,128)(2,1)S(1)}, u32[]{:S(2)}, u32[]{:S(2)}) %collective-permute-start.17) | collective-permute-done | bytes 65568 | tf_op jit(solution)/shard_map/ppermute | solution.py:18
  80.7 8.8 %all_to_all.22 = f32[32,1,128]{2,1,0:T(1,128)S(1)} all-to-all(f32[32,1,128]{2,1,0:T(1,128)S(1)} %reshape.437), channel_id=1, replica_groups=mesh['dom'=8,'rep'=4] {'dom','rep'}, dimensions={0} | all-to-all | bytes 32768 | tf_op jit(solution)/shard_map/all_to_all | solution.py:24
  92.0 2.7 %collective-permute-done.19 = bf16[32,128]{1,0:T(8,128)(2,1)S(1)} collective-permute-done((bf16[32,128]{1,0:T(8,128)(2,1)S(1)}, bf16[32,128]{1,0:T(8,128)(2,1)S(1)}, u32[]{:S(2)}, u32[]{:S(2)}) %collective-permute-start.19) | collective-permute-done | bytes 8224 | tf_op jit(solution)/shard_map/ppermute | solution.py:14
  98.4 1.5 %collective-permute-start.21 = (bf16[8,32,128]{2,0,1:T(8,128)(2,1)S(1)}, bf16[8,32,128]{2,0,1:T(8,128)(2,1)S(1)}, u32[]{:S(2)}, u32[]{:S(2)}) collective-permute-start(bf16[8,32,128]{2,0,1:T(8,128)(2,1)S(1)} %copy.371), channel_id=1, source_target_pairs={{0,4},{4,0},{8,12},{12,8},{16,20},{20,16},{24,28},{28,24},{1,5},{5... | collective-permute-start | bytes 196616 | tf_op jit(solution)/shard_map/ppermute | solution.py:18
  100.3 2.7 %collective-permute-done.21 = bf16[8,32,128]{2,0,1:T(8,128)(2,1)S(1)} collective-permute-done((bf16[8,32,128]{2,0,1:T(8,128)(2,1)S(1)}, bf16[8,32,128]{2,0,1:T(8,128)(2,1)S(1)}, u32[]{:S(2)}, u32[]{:S(2)}) %collective-permute-start.21) | collective-permute-done | bytes 65568 | tf_op jit(solution)/shard_map/ppermute | solution.py:18
  103.3 8.9 %all_to_all.23 = f32[32,2,32]{2,1,0:T(2,128)S(1)} all-to-all(f32[32,2,32]{2,1,0:T(2,128)S(1)} %broadcast_in_dim.90), channel_id=1, replica_groups=mesh['dom'=8,'rep'=4] {'dom','rep'}, dimensions={0} | all-to-all | bytes 16384 | tf_op jit(solution)/shard_map/all_to_all | solution.py:24
  (171 shorter events, 30.8 us)
Async XLA Ops:
  3.0 7.1 %copy-start.6 = (s32[8,2]{0,1:T(2,128)S(1)}, s32[8,2]{0,1:T(2,128)}, u32[]{:S(2)}) copy-start(s32[8,2]{0,1:T(2,128)} %param.18) | copy-start | bytes 196
  3.0 19.4 %collective-permute-start.6 = (bf16[8,128,128]{2,0,1:T(8,128)(2,1)S(1)}, bf16[8,128,128]{2,0,1:T(8,128)(2,1)}, u32[]{:S(2)}, u32[]{:S(2)}) collective-permute-start(bf16[8,128,128]{2,0,1:T(8,128)(2,1)S(1)} %select_bitcast_fusion), channel_id=1, source_target_pairs={{0,3},{1,0},{2,1},{3,2},{4,7},{5,4},{6,5},{7,6},{8,11},{9,8},{10,9... | collective-permute-start | bytes 786440 | tf_op jit(solution)/shard_map/ppermute | solution.py:14
  5.4 16.5 %copy-start.4 = (bf16[1,128,128]{2,1,0:T(8,128)(2,1)S(1)}, bf16[1,128,128]{2,1,0:T(8,128)(2,1)}, u32[]{:S(2)}) copy-start(bf16[1,128,128]{2,1,0:T(8,128)(2,1)} %param.19) | copy-start | bytes 98308
  5.6 16.9 %collective-permute-start.5 = (bf16[8,128,128]{2,0,1:T(8,128)(2,1)S(1)}, bf16[8,128,128]{2,0,1:T(8,128)(2,1)S(1)}, u32[]{:S(2)}, u32[]{:S(2)}) collective-permute-start(bf16[8,128,128]{2,0,1:T(8,128)(2,1)S(1)} %get-tuple-element.84), channel_id=1, source_target_pairs={{0,2},{1,3},{2,0},{3,1},{4,6},{5,7},{6,4},{7,5},{8,10},{9,11},{10,... | collective-permute-start | bytes 786440 | tf_op jit(solution)/shard_map/ppermute | solution.py:14
  6.6 8.4 %collective-permute-start.2 = (s32[8,2]{0,1:T(2,128)S(1)}, s32[8,2]{0,1:T(2,128)S(1)}, u32[]{:S(2)}, u32[]{:S(2)}) collective-permute-start(s32[8,2]{0,1:T(2,128)S(1)} %bitcast.342), channel_id=1, source_target_pairs={{0,3},{1,0},{2,1},{3,2},{4,7},{5,4},{6,5},{7,6},{8,11},{9,8},{10,9... | collective-permute-start | bytes 200 | tf_op jit(solution)/shard_map/ppermute | solution.py:14
  6.7 9.5 %collective-permute-start.1 = (s32[8,2]{0,1:T(2,128)S(1)}, s32[8,2]{0,1:T(2,128)S(1)}, u32[]{:S(2)}, u32[]{:S(2)}) collective-permute-start(s32[8,2]{0,1:T(2,128)S(1)} %bitcast.341), channel_id=1, source_target_pairs={{0,2},{1,3},{2,0},{3,1},{4,6},{5,7},{6,4},{7,5},{8,10},{9,11},{10,... | collective-permute-start | bytes 200 | tf_op jit(solution)/shard_map/ppermute | solution.py:14
  8.5 13.6 %collective-permute-start.3 = (bf16[8,32,128]{2,0,1:T(8,128)(2,1)S(1)}, bf16[8,32,128]{2,0,1:T(8,128)(2,1)S(1)}, u32[]{:S(2)}, u32[]{:S(2)}) collective-permute-start(bf16[8,32,128]{2,0,1:T(8,128)(2,1)S(1)} %multiply_convert_fusion), channel_id=1, source_target_pairs={{0,4},{4,0},{8,12},{12,8},{16,20},{20,16},{24,28},{28,24},{1,5},{5... | collective-permute-start | bytes 196616 | tf_op jit(solution)/shard_map/ppermute | solution.py:18
  15.0 3.4 %collective-permute-start = (s32[8,2]{0,1:T(2,128)S(1)}, s32[8,2]{0,1:T(2,128)S(1)}, u32[]{:S(2)}, u32[]{:S(2)}) collective-permute-start(s32[8,2]{0,1:T(2,128)S(1)} %bitcast.340), channel_id=1, source_target_pairs={{0,1},{1,2},{2,3},{3,0},{4,5},{5,6},{6,7},{7,4},{8,9},{9,10},{10,1... | collective-permute-start | bytes 200 | tf_op jit(solution)/shard_map/ppermute | solution.py:14
  16.1 6.3 %collective-permute-start.4 = (bf16[8,128,128]{2,0,1:T(8,128)(2,1)S(1)}, bf16[8,128,128]{2,0,1:T(8,128)(2,1)S(1)}, u32[]{:S(2)}, u32[]{:S(2)}) collective-permute-start(bf16[8,128,128]{2,0,1:T(8,128)(2,1)S(1)} %get-tuple-element.83), channel_id=1, source_target_pairs={{0,1},{1,2},{2,3},{3,0},{4,5},{5,6},{6,7},{7,4},{8,9},{9,10},{10,1... | collective-permute-start | bytes 786440 | tf_op jit(solution)/shard_map/ppermute | solution.py:14
  18.4 3.6 %collective-permute-start.7 = (bf16[32,128]{1,0:T(8,128)(2,1)S(1)}, bf16[32,128]{1,0:T(8,128)(2,1)S(1)}, u32[]{:S(2)}, u32[]{:S(2)}) collective-permute-start(bf16[32,128]{1,0:T(8,128)(2,1)S(1)} %bitcast.321), channel_id=1, source_target_pairs={{0,1},{1,2},{2,3},{3,0},{4,5},{5,6},{6,7},{7,4},{8,9},{9,10},{10,1... | collective-permute-start | bytes 24584 | tf_op jit(solution)/shard_map/ppermute | solution.py:14
  25.1 3.5 %collective-permute-start.8 = (f32[32,128]{1,0:T(8,128)S(1)}, f32[32,128]{1,0:T(8,128)S(1)}, u32[]{:S(2)}, u32[]{:S(2)}) collective-permute-start(f32[32,128]{1,0:T(8,128)S(1)} %fusion.121), channel_id=1, source_target_pairs={{0,3},{1,0},{2,1},{3,2},{4,7},{5,4},{6,5},{7,6},{8,11},{9,8},{10,9... | collective-permute-start | bytes 49160 | tf_op jit(solution)/shard_map/ppermute | solution.py:14
  25.6 4.6 %collective-permute-start.9 = (bf16[8,32,128]{2,0,1:T(8,128)(2,1)S(1)}, bf16[8,32,128]{2,0,1:T(8,128)(2,1)S(1)}, u32[]{:S(2)}, u32[]{:S(2)}) collective-permute-start(bf16[8,32,128]{2,0,1:T(8,128)(2,1)S(1)} %copy.374), channel_id=1, source_target_pairs={{0,4},{4,0},{8,12},{12,8},{16,20},{20,16},{24,28},{28,24},{1,5},{5... | collective-permute-start | bytes 196616 | tf_op jit(solution)/shard_map/ppermute | solution.py:18
  44.9 4.3 %collective-permute-start.10 = (bf16[8,32,128]{2,0,1:T(8,128)(2,1)S(1)}, bf16[8,32,128]{2,0,1:T(8,128)(2,1)S(1)}, u32[]{:S(2)}, u32[]{:S(2)}) collective-permute-start(bf16[8,32,128]{2,0,1:T(8,128)(2,1)S(1)} %get-tuple-element.19), channel_id=1, source_target_pairs={{0,4},{4,0},{8,12},{12,8},{16,20},{20,16},{24,28},{28,24},{1,5},{5... | collective-permute-start | bytes 196616 | tf_op jit(solution)/shard_map/ppermute | solution.py:18
  45.6 3.1 %collective-permute-start.11 = (bf16[32,128]{1,0:T(8,128)(2,1)S(1)}, bf16[32,128]{1,0:T(8,128)(2,1)S(1)}, u32[]{:S(2)}, u32[]{:S(2)}) collective-permute-start(bf16[32,128]{1,0:T(8,128)(2,1)S(1)} %bitcast.323), channel_id=1, source_target_pairs={{0,1},{1,2},{2,3},{3,0},{4,5},{5,6},{6,7},{7,4},{8,9},{9,10},{10,1... | collective-permute-start | bytes 24584 | tf_op jit(solution)/shard_map/ppermute | solution.py:14
  51.3 2.6 %collective-permute-start.12 = (f32[32,128]{1,0:T(8,128)S(1)}, f32[32,128]{1,0:T(8,128)S(1)}, u32[]{:S(2)}, u32[]{:S(2)}) collective-permute-start(f32[32,128]{1,0:T(8,128)S(1)} %fusion.117), channel_id=1, source_target_pairs={{0,3},{1,0},{2,1},{3,2},{4,7},{5,4},{6,5},{7,6},{8,11},{9,8},{10,9... | collective-permute-start | bytes 49160 | tf_op jit(solution)/shard_map/ppermute | solution.py:14
  52.8 4.6 %collective-permute-start.13 = (bf16[8,32,128]{2,0,1:T(8,128)(2,1)S(1)}, bf16[8,32,128]{2,0,1:T(8,128)(2,1)S(1)}, u32[]{:S(2)}, u32[]{:S(2)}) collective-permute-start(bf16[8,32,128]{2,0,1:T(8,128)(2,1)S(1)} %copy.373), channel_id=1, source_target_pairs={{0,4},{4,0},{8,12},{12,8},{16,20},{20,16},{24,28},{28,24},{1,5},{5... | collective-permute-start | bytes 196616 | tf_op jit(solution)/shard_map/ppermute | solution.py:18
  67.7 4.3 %collective-permute-start.14 = (bf16[8,32,128]{2,0,1:T(8,128)(2,1)S(1)}, bf16[8,32,128]{2,0,1:T(8,128)(2,1)S(1)}, u32[]{:S(2)}, u32[]{:S(2)}) collective-permute-start(bf16[8,32,128]{2,0,1:T(8,128)(2,1)S(1)} %get-tuple-element.22), channel_id=1, source_target_pairs={{0,4},{4,0},{8,12},{12,8},{16,20},{20,16},{24,28},{28,24},{1,5},{5... | collective-permute-start | bytes 196616 | tf_op jit(solution)/shard_map/ppermute | solution.py:18
  68.3 3.1 %collective-permute-start.15 = (bf16[32,128]{1,0:T(8,128)(2,1)S(1)}, bf16[32,128]{1,0:T(8,128)(2,1)S(1)}, u32[]{:S(2)}, u32[]{:S(2)}) collective-permute-start(bf16[32,128]{1,0:T(8,128)(2,1)S(1)} %bitcast.324), channel_id=1, source_target_pairs={{0,1},{1,2},{2,3},{3,0},{4,5},{5,6},{6,7},{7,4},{8,9},{9,10},{10,1... | collective-permute-start | bytes 24584 | tf_op jit(solution)/shard_map/ppermute | solution.py:14
  74.1 2.7 %collective-permute-start.16 = (f32[32,128]{1,0:T(8,128)S(1)}, f32[32,128]{1,0:T(8,128)S(1)}, u32[]{:S(2)}, u32[]{:S(2)}) collective-permute-start(f32[32,128]{1,0:T(8,128)S(1)} %fusion.113), channel_id=1, source_target_pairs={{0,3},{1,0},{2,1},{3,2},{4,7},{5,4},{6,5},{7,6},{8,11},{9,8},{10,9... | collective-permute-start | bytes 49160 | tf_op jit(solution)/shard_map/ppermute | solution.py:14
  75.6 4.6 %collective-permute-start.17 = (bf16[8,32,128]{2,0,1:T(8,128)(2,1)S(1)}, bf16[8,32,128]{2,0,1:T(8,128)(2,1)S(1)}, u32[]{:S(2)}, u32[]{:S(2)}) collective-permute-start(bf16[8,32,128]{2,0,1:T(8,128)(2,1)S(1)} %copy.372), channel_id=1, source_target_pairs={{0,4},{4,0},{8,12},{12,8},{16,20},{20,16},{24,28},{28,24},{1,5},{5... | collective-permute-start | bytes 196616 | tf_op jit(solution)/shard_map/ppermute | solution.py:18
  90.5 4.3 %collective-permute-start.18 = (bf16[8,32,128]{2,0,1:T(8,128)(2,1)S(1)}, bf16[8,32,128]{2,0,1:T(8,128)(2,1)S(1)}, u32[]{:S(2)}, u32[]{:S(2)}) collective-permute-start(bf16[8,32,128]{2,0,1:T(8,128)(2,1)S(1)} %get-tuple-element.25), channel_id=1, source_target_pairs={{0,4},{4,0},{8,12},{12,8},{16,20},{20,16},{24,28},{28,24},{1,5},{5... | collective-permute-start | bytes 196616 | tf_op jit(solution)/shard_map/ppermute | solution.py:18
  91.6 3.1 %collective-permute-start.19 = (bf16[32,128]{1,0:T(8,128)(2,1)S(1)}, bf16[32,128]{1,0:T(8,128)(2,1)S(1)}, u32[]{:S(2)}, u32[]{:S(2)}) collective-permute-start(bf16[32,128]{1,0:T(8,128)(2,1)S(1)} %bitcast.322), channel_id=1, source_target_pairs={{0,1},{1,2},{2,3},{3,0},{4,5},{5,6},{6,7},{7,4},{8,9},{9,10},{10,1... | collective-permute-start | bytes 24584 | tf_op jit(solution)/shard_map/ppermute | solution.py:14
  96.9 3.0 %collective-permute-start.20 = (f32[32,128]{1,0:T(8,128)S(1)}, f32[32,128]{1,0:T(8,128)S(1)}, u32[]{:S(2)}, u32[]{:S(2)}) collective-permute-start(f32[32,128]{1,0:T(8,128)S(1)} %fusion.109), channel_id=1, source_target_pairs={{0,3},{1,0},{2,1},{3,2},{4,7},{5,4},{6,5},{7,6},{8,11},{9,8},{10,9... | collective-permute-start | bytes 49160 | tf_op jit(solution)/shard_map/ppermute | solution.py:14
  98.4 4.6 %collective-permute-start.21 = (bf16[8,32,128]{2,0,1:T(8,128)(2,1)S(1)}, bf16[8,32,128]{2,0,1:T(8,128)(2,1)S(1)}, u32[]{:S(2)}, u32[]{:S(2)}) collective-permute-start(bf16[8,32,128]{2,0,1:T(8,128)(2,1)S(1)} %copy.371), channel_id=1, source_target_pairs={{0,4},{4,0},{8,12},{12,8},{16,20},{20,16},{24,28},{28,24},{1,5},{5... | collective-permute-start | bytes 196616 | tf_op jit(solution)/shard_map/ppermute | solution.py:18
  (7 other events, 23.0 us)

commit v26 on v24

--- a/solution.py
+++ b/solution.py
@@ -25,21 +25,22 @@
     return jnp.sum(gathered, axis=0)
 
 
-def local_stiffness(rounded, diag_tiles, off_tiles, cols_onehot, mirror_onehot):
+def early_stiffness(rounded, diag_tiles, off_tiles, cols_onehot):
     result = jnp.einsum("nrk,nkj->nrj", rounded, diag_tiles, preferred_element_type=jnp.float32)
     picked = jnp.einsum(
         "pn,nrk->prk", cols_onehot, rounded, preferred_element_type=jnp.float32
     ).astype(jnp.bfloat16)
     picked = picked.reshape(off_tiles.shape[0], off_tiles.shape[1], rounded.shape[1], rounded.shape[2])
-    result = result + jnp.einsum(
+    return result + jnp.einsum(
         "nmrk,nmkj->nrj", picked, off_tiles, preferred_element_type=jnp.float32
     )
+
+
+def mirror_stiffness(rounded, off_tiles, mirror_onehot):
     nodes = rounded.shape[0]
     chosen = mirror_onehot.reshape(nodes, off_tiles.shape[1], nodes)
     spread = chosen[:, :, :, None, None] * rounded[:, None, None, :, :]
-    return result + jnp.einsum(
-        "nmirk,nmjk->irj", spread, off_tiles, preferred_element_type=jnp.float32
-    )
+    return jnp.einsum("nmirk,nmjk->irj", spread, off_tiles, preferred_element_type=jnp.float32)
 
 
 def apply_operator(vector, diag_tiles, off_tiles, link_tile, contact_set, tables):
@@ -56,6 +57,7 @@
     ).astype(jnp.bfloat16)
     spread = far_pick[:, :, None, None] * multiplier[:, None, :, :]
     far_sum = jnp.einsum("snrj,skj->nrk", spread, contact_set, preferred_element_type=jnp.float32)
+    early = early_stiffness(rounded, diag_tiles, off_tiles, cols_onehot)
     far_sum, rounded, multiplier = lax.optimization_barrier(
         (far_sum.astype(jnp.bfloat16), rounded, multiplier)
     )
@@ -64,7 +66,7 @@
         rounded[0], link_tile, (((1,), (1,)), ((), ())), preferred_element_type=jnp.float32
     )
     after = from_behind(back_term, "rep", -1)
-    result = local_stiffness(rounded, diag_tiles, off_tiles, cols_onehot, mirror_onehot)
+    result = early + mirror_stiffness(rounded, off_tiles, mirror_onehot)
     first_add = jnp.dot(before, link_tile, preferred_element_type=jnp.float32)
     ends = jnp.concatenate(
         [first_add[None], jnp.zeros((nodes - 2,) + first_add.shape, jnp.float32), after[None]]

time: 109 us -> 111 us (1.018)
  waiting for transfers between devices: 23.3 us -> 28.5 us
  blocking collectives: 39.4 us -> 37.7 us
  local copies, waits for them, and re-layouts: 3.82 us -> 2.26 us
  matrix products: 16.4 us -> 17.7 us
    ppermute x8, waiting for transfers between devices: 3.04 us -> 6.19 us  [partner(): lax.ppermute(value, axis, [(i, i ^ 1 << distance) for i in range(lax.axis...]
    reduce_sum x4 -> x1, other arithmetic: 2.19 us -> 0.13 us  [body(): jnp.sum(residual * preconditioned, axis=(0, 2))]
    ppermute x14, waiting for transfers between devices: 20.3 us -> 22.3 us  [from_behind(): return lax.ppermute(value, axis, pairs)]
    all_to_all x4, blocking collectives: 39.4 us -> 37.7 us  [total(): gathered = lax.all_to_all(spread, ('dom', 'rep'), 0, 0, tiled=True)]
    unnamed x31 -> x21, local copies, waits for them, and re-layouts: 2.39 us -> 1.13 us
  transfers between devices with their start and end apart: 22 -> 22, of which waited for: 15 -> 12; matrix products, arithmetic and copies ran while one was open for 10% -> 8% of each run, Pallas kernels for 0% -> 0%
where the time goes in v26:
time: 111 us; the launch traced here: 110 us
  blocking collectives  37.7 us (34%)
  waiting for transfers between devices  28.5 us (26%)
  matrix products  17.7 us (16%)
  starting transfers between devices  14.8 us (13%)
  other arithmetic  8.3 us (7%)
  local copies, waits for them, and re-layouts  2.26 us (2%)
  between operations  1.23 us (1%)
    all_to_all x4, blocking collectives, total(): gathered = lax.all_to_all(spread, ('dom', 'rep'), 0, 0, tiled=True)  37.7 us
    ppermute x14, waiting for transfers between devices, from_behind(): return lax.ppermute(value, axis, pairs)  22.3 us
    ppermute x8, starting transfers between devices, partner(): lax.ppermute(value, axis, [(i, i ^ 1 << distance) for i in range(lax.axis...  8.5 us
    ppermute x14, starting transfers between devices, from_behind(): return lax.ppermute(value, axis, pairs)  6.3 us
    ppermute x8, waiting for transfers between devices, partner(): lax.ppermute(value, axis, [(i, i ^ 1 << distance) for i in range(lax.axis...  6.19 us
    dot_general x4, matrix products, apply_operator(): jnp.einsum('snrj,skj->nrk', near_spread, contact_set, preferred_element_t...  3.52 us
    dot_general x4, matrix products, apply_operator(): jnp.einsum('snrj,skj->nrk', spread, contact_set, preferred_element_type=j...  3.1 us
  transfers between devices with their start and end apart: 22, of which 12 were waited for; matrix products, arithmetic and copies ran while one was open for 8% of the time, Pallas kernels for 0%

profile of v26, /device:TPU:0, one launch (start us, length us, event | category | flops | bytes accessed | tf_op | source)
XLA Modules:
  0.0 110.5 jit_solution(1601553789211053395)
XLA Ops:
  3.8 2.6 %collective-permute-start.1 = (s32[8,2]{0,1:T(2,128)S(1)}, s32[8,2]{0,1:T(2,128)S(1)}, u32[]{:S(2)}, u32[]{:S(2)}) collective-permute-start(s32[8,2]{0,1:T(2,128)S(1)} %bitcast.336), channel_id=1, source_target_pairs={{0,2},{1,3},{2,0},{3,1},{4,6},{5,7},{6,4},{7,5},{8,10},{9,11},{10,... | collective-permute-start | bytes 200 | tf_op jit(solution)/shard_map/ppermute | solution.py:14
  6.3 1.4 %collective-permute-start.2 = (s32[8,2]{0,1:T(2,128)S(1)}, s32[8,2]{0,1:T(2,128)S(1)}, u32[]{:S(2)}, u32[]{:S(2)}) collective-permute-start(s32[8,2]{0,1:T(2,128)S(1)} %bitcast.335), channel_id=1, source_target_pairs={{0,3},{1,0},{2,1},{3,2},{4,7},{5,4},{6,5},{7,6},{8,11},{9,8},{10,9... | collective-permute-start | bytes 200 | tf_op jit(solution)/shard_map/ppermute | solution.py:14
  8.7 1.6 %collective-permute-start.3 = (bf16[8,32,128]{2,1,0:T(8,128)(2,1)S(1)}, bf16[8,32,128]{2,1,0:T(8,128)(2,1)}, u32[]{:S(2)}, u32[]{:S(2)}) collective-permute-start(bf16[8,32,128]{2,1,0:T(8,128)(2,1)S(1)} %get-tuple-element.16), channel_id=1, source_target_pairs={{0,4},{4,0},{8,12},{12,8},{16,20},{20,16},{24,28},{28,24},{1,5},{5... | collective-permute-start | bytes 196616 | tf_op jit(solution)/shard_map/ppermute | solution.py:18
  12.8 1.1 collective-permute-start.6
  14.4 9.3 %collective-permute-done.7 = bf16[32,128]{1,0:T(8,128)(2,1)S(1)} collective-permute-done((bf16[32,128]{1,0:T(8,128)(2,1)S(1)}, bf16[32,128]{1,0:T(8,128)(2,1)S(1)}, u32[]{:S(2)}, u32[]{:S(2)}) %collective-permute-start.7) | collective-permute-done | bytes 8224 | tf_op jit(solution)/shard_map/ppermute | solution.py:14
  23.8 1.1 %fusion.17 = bf16[32,32,128]{2,0,1:T(8,128)(2,1)S(1)} fusion(f32[32,32,128]{2,0,1:T(8,128)S(1)} %fusion.129, bf16[8,32,128]{2,1,0:T(8,128)(2,1)} %collective-permute-done.3, s32[32]{0:T(128)S(1)} %get-tuple-element.88), kind=kOutput, calls=%fused_computation.22 | convolution fusion | flops 2359552 | bytes 852096 | tf_op jit(solution)/shard_map/sn,nrk->srk/dot_general | solution.py:53
  24.9 1.1 pad_maximum_fusion
  29.6 2.2 %collective-permute-done.9 = bf16[8,32,128]{2,1,0:T(8,128)(2,1)S(1)} collective-permute-done((bf16[8,32,128]{2,1,0:T(8,128)(2,1)S(1)}, bf16[8,32,128]{2,1,0:T(8,128)(2,1)S(1)}, u32[]{:S(2)}, u32[]{:S(2)}) %collective-permute-start.9) | collective-permute-done | bytes 65568 | tf_op jit(solution)/shard_map/ppermute | solution.py:18
  32.8 11.0 %all_to_all.20 = f32[32,1,128]{2,1,0:T(1,128)S(1)} all-to-all(f32[32,1,128]{2,1,0:T(1,128)S(1)} %reshape.433), channel_id=1, replica_groups=mesh['dom'=8,'rep'=4] {'dom','rep'}, dimensions={0} | all-to-all | bytes 32768 | tf_op jit(solution)/shard_map/all_to_all | solution.py:24
  46.8 2.8 %collective-permute-done.11 = bf16[32,128]{1,0:T(8,128)(2,1)S(1)} collective-permute-done((bf16[32,128]{1,0:T(8,128)(2,1)S(1)}, bf16[32,128]{1,0:T(8,128)(2,1)S(1)}, u32[]{:S(2)}, u32[]{:S(2)}) %collective-permute-start.11) | collective-permute-done | bytes 8224 | tf_op jit(solution)/shard_map/ppermute | solution.py:14
  51.8 1.5 %collective-permute-start.13 = (bf16[8,32,128]{2,1,0:T(8,128)(2,1)S(1)}, bf16[8,32,128]{2,1,0:T(8,128)(2,1)S(1)}, u32[]{:S(2)}, u32[]{:S(2)}) collective-permute-start(bf16[8,32,128]{2,1,0:T(8,128)(2,1)S(1)} %fusion.59), channel_id=1, source_target_pairs={{0,4},{4,0},{8,12},{12,8},{16,20},{20,16},{24,28},{28,24},{1,5},{5... | collective-permute-start | bytes 196616 | tf_op jit(solution)/shard_map/ppermute | solution.py:18
  53.5 1.2 %collective-permute-done.12 = f32[32,128]{1,0:T(8,128)S(1)} collective-permute-done((f32[32,128]{1,0:T(8,128)S(1)}, f32[32,128]{1,0:T(8,128)S(1)}, u32[]{:S(2)}, u32[]{:S(2)}) %collective-permute-start.12) | collective-permute-done | bytes 16416 | tf_op jit(solution)/shard_map/ppermute | solution.py:14
  54.8 1.3 %collective-permute-done.13 = bf16[8,32,128]{2,1,0:T(8,128)(2,1)S(1)} collective-permute-done((bf16[8,32,128]{2,1,0:T(8,128)(2,1)S(1)}, bf16[8,32,128]{2,1,0:T(8,128)(2,1)S(1)}, u32[]{:S(2)}, u32[]{:S(2)}) %collective-permute-start.13) | collective-permute-done | bytes 65568 | tf_op jit(solution)/shard_map/ppermute | solution.py:18
  57.2 8.8 %all_to_all.21 = f32[32,1,128]{2,1,0:T(1,128)S(1)} all-to-all(f32[32,1,128]{2,1,0:T(1,128)S(1)} %reshape.435), channel_id=1, replica_groups=mesh['dom'=8,'rep'=4] {'dom','rep'}, dimensions={0} | all-to-all | bytes 32768 | tf_op jit(solution)/shard_map/all_to_all | solution.py:24
  68.5 2.8 %collective-permute-done.15 = bf16[32,128]{1,0:T(8,128)(2,1)S(1)} collective-permute-done((bf16[32,128]{1,0:T(8,128)(2,1)S(1)}, bf16[32,128]{1,0:T(8,128)(2,1)S(1)}, u32[]{:S(2)}, u32[]{:S(2)}) %collective-permute-start.15) | collective-permute-done | bytes 8224 | tf_op jit(solution)/shard_map/ppermute | solution.py:14
  73.5 1.5 %collective-permute-start.17 = (bf16[8,32,128]{2,1,0:T(8,128)(2,1)S(1)}, bf16[8,32,128]{2,1,0:T(8,128)(2,1)S(1)}, u32[]{:S(2)}, u32[]{:S(2)}) collective-permute-start(bf16[8,32,128]{2,1,0:T(8,128)(2,1)S(1)} %fusion.56), channel_id=1, source_target_pairs={{0,4},{4,0},{8,12},{12,8},{16,20},{20,16},{24,28},{28,24},{1,5},{5... | collective-permute-start | bytes 196616 | tf_op jit(solution)/shard_map/ppermute | solution.py:18
  75.2 1.2 %collective-permute-done.16 = f32[32,128]{1,0:T(8,128)S(1)} collective-permute-done((f32[32,128]{1,0:T(8,128)S(1)}, f32[32,128]{1,0:T(8,128)S(1)}, u32[]{:S(2)}, u32[]{:S(2)}) %collective-permute-start.16) | collective-permute-done | bytes 16416 | tf_op jit(solution)/shard_map/ppermute | solution.py:14
  76.5 1.3 %collective-permute-done.17 = bf16[8,32,128]{2,1,0:T(8,128)(2,1)S(1)} collective-permute-done((bf16[8,32,128]{2,1,0:T(8,128)(2,1)S(1)}, bf16[8,32,128]{2,1,0:T(8,128)(2,1)S(1)}, u32[]{:S(2)}, u32[]{:S(2)}) %collective-permute-start.17) | collective-permute-done | bytes 65568 | tf_op jit(solution)/shard_map/ppermute | solution.py:18
  78.9 8.8 %all_to_all.22 = f32[32,1,128]{2,1,0:T(1,128)S(1)} all-to-all(f32[32,1,128]{2,1,0:T(1,128)S(1)} %reshape.437), channel_id=1, replica_groups=mesh['dom'=8,'rep'=4] {'dom','rep'}, dimensions={0} | all-to-all | bytes 32768 | tf_op jit(solution)/shard_map/all_to_all | solution.py:24
  90.3 2.9 %collective-permute-done.19 = bf16[32,128]{1,0:T(8,128)(2,1)S(1)} collective-permute-done((bf16[32,128]{1,0:T(8,128)(2,1)S(1)}, bf16[32,128]{1,0:T(8,128)(2,1)S(1)}, u32[]{:S(2)}, u32[]{:S(2)}) %collective-permute-start.19) | collective-permute-done | bytes 8224 | tf_op jit(solution)/shard_map/ppermute | solution.py:14
  95.4 1.5 %collective-permute-start.21 = (bf16[8,32,128]{2,1,0:T(8,128)(2,1)S(1)}, bf16[8,32,128]{2,1,0:T(8,128)(2,1)S(1)}, u32[]{:S(2)}, u32[]{:S(2)}) collective-permute-start(bf16[8,32,128]{2,1,0:T(8,128)(2,1)S(1)} %fusion.53), channel_id=1, source_target_pairs={{0,4},{4,0},{8,12},{12,8},{16,20},{20,16},{24,28},{28,24},{1,5},{5... | collective-permute-start | bytes 196616 | tf_op jit(solution)/shard_map/ppermute | solution.py:18
  97.2 1.2 %collective-permute-done.20 = f32[32,128]{1,0:T(8,128)S(1)} collective-permute-done((f32[32,128]{1,0:T(8,128)S(1)}, f32[32,128]{1,0:T(8,128)S(1)}, u32[]{:S(2)}, u32[]{:S(2)}) %collective-permute-start.20) | collective-permute-done | bytes 16416 | tf_op jit(solution)/shard_map/ppermute | solution.py:14
  98.4 1.3 %collective-permute-done.21 = bf16[8,32,128]{2,1,0:T(8,128)(2,1)S(1)} collective-permute-done((bf16[8,32,128]{2,1,0:T(8,128)(2,1)S(1)}, bf16[8,32,128]{2,1,0:T(8,128)(2,1)S(1)}, u32[]{:S(2)}, u32[]{:S(2)}) %collective-permute-start.21) | collective-permute-done | bytes 65568 | tf_op jit(solution)/shard_map/ppermute | solution.py:18
  100.6 8.9 %all_to_all.23 = f32[32,2,32]{2,1,0:T(2,128)S(1)} all-to-all(f32[32,2,32]{2,1,0:T(2,128)S(1)} %broadcast_in_dim.90), channel_id=1, replica_groups=mesh['dom'=8,'rep'=4] {'dom','rep'}, dimensions={0} | all-to-all | bytes 16384 | tf_op jit(solution)/shard_map/all_to_all | solution.py:24
  (141 shorter events, 30.5 us)
Async XLA Ops:
  0.6 9.6 %copy-start = (bf16[16,128,128]{2,1,0:T(8,128)(2,1)S(1)}, bf16[16,128,128]{2,1,0:T(8,128)(2,1)}, u32[]{:S(2)}) copy-start(bf16[16,128,128]{2,1,0:T(8,128)(2,1)} %param.20) | copy-start | bytes 1572868
  3.3 8.9 %collective-permute-start = (s32[8,2]{0,1:T(2,128)S(1)}, s32[8,2]{0,1:T(2,128)S(1)}, u32[]{:S(2)}, u32[]{:S(2)}) collective-permute-start(s32[8,2]{0,1:T(2,128)S(1)} %bitcast.337), channel_id=1, source_target_pairs={{0,1},{1,2},{2,3},{3,0},{4,5},{5,6},{6,7},{7,4},{8,9},{9,10},{10,1... | collective-permute-start | bytes 200 | tf_op jit(solution)/shard_map/ppermute | solution.py:14
  3.8 9.0 %collective-permute-start.1 = (s32[8,2]{0,1:T(2,128)S(1)}, s32[8,2]{0,1:T(2,128)S(1)}, u32[]{:S(2)}, u32[]{:S(2)}) collective-permute-start(s32[8,2]{0,1:T(2,128)S(1)} %bitcast.336), channel_id=1, source_target_pairs={{0,2},{1,3},{2,0},{3,1},{4,6},{5,7},{6,4},{7,5},{8,10},{9,11},{10,... | collective-permute-start | bytes 200 | tf_op jit(solution)/shard_map/ppermute | solution.py:14
  6.3 7.5 %collective-permute-start.2 = (s32[8,2]{0,1:T(2,128)S(1)}, s32[8,2]{0,1:T(2,128)S(1)}, u32[]{:S(2)}, u32[]{:S(2)}) collective-permute-start(s32[8,2]{0,1:T(2,128)S(1)} %bitcast.335), channel_id=1, source_target_pairs={{0,3},{1,0},{2,1},{3,2},{4,7},{5,4},{6,5},{7,6},{8,11},{9,8},{10,9... | collective-permute-start | bytes 200 | tf_op jit(solution)/shard_map/ppermute | solution.py:14
  8.7 15.1 %collective-permute-start.3 = (bf16[8,32,128]{2,1,0:T(8,128)(2,1)S(1)}, bf16[8,32,128]{2,1,0:T(8,128)(2,1)}, u32[]{:S(2)}, u32[]{:S(2)}) collective-permute-start(bf16[8,32,128]{2,1,0:T(8,128)(2,1)S(1)} %get-tuple-element.16), channel_id=1, source_target_pairs={{0,4},{4,0},{8,12},{12,8},{16,20},{20,16},{24,28},{28,24},{1,5},{5... | collective-permute-start | bytes 196616 | tf_op jit(solution)/shard_map/ppermute | solution.py:18
  11.0 12.7 %copy-start.3 = (bf16[1,128,128]{2,1,0:T(8,128)(2,1)S(1)}, bf16[1,128,128]{2,1,0:T(8,128)(2,1)}, u32[]{:S(2)}) copy-start(bf16[1,128,128]{2,1,0:T(8,128)(2,1)} %param.19) | copy-start | bytes 98308
  11.0 13.9 %collective-permute-start.4 = (bf16[8,128,128]{2,0,1:T(8,128)(2,1)S(1)}, bf16[8,128,128]{2,0,1:T(8,128)(2,1)}, u32[]{:S(2)}, u32[]{:S(2)}) collective-permute-start(bf16[8,128,128]{2,0,1:T(8,128)(2,1)S(1)} %get-tuple-element.80), channel_id=1, source_target_pairs={{0,1},{1,2},{2,3},{3,0},{4,5},{5,6},{6,7},{7,4},{8,9},{9,10},{10,1... | collective-permute-start | bytes 786440 | tf_op jit(solution)/shard_map/ppermute | solution.py:14
  12.2 12.7 %collective-permute-start.5 = (bf16[8,128,128]{2,0,1:T(8,128)(2,1)S(1)}, bf16[8,128,128]{2,0,1:T(8,128)(2,1)S(1)}, u32[]{:S(2)}, u32[]{:S(2)}) collective-permute-start(bf16[8,128,128]{2,0,1:T(8,128)(2,1)S(1)} %get-tuple-element.81), channel_id=1, source_target_pairs={{0,2},{1,3},{2,0},{3,1},{4,6},{5,7},{6,4},{7,5},{8,10},{9,11},{10,... | collective-permute-start | bytes 786440 | tf_op jit(solution)/shard_map/ppermute | solution.py:14
  12.8 12.2 %collective-permute-start.6 = (bf16[8,128,128]{2,0,1:T(8,128)(2,1)S(1)}, bf16[8,128,128]{2,0,1:T(8,128)(2,1)S(1)}, u32[]{:S(2)}, u32[]{:S(2)}) collective-permute-start(bf16[8,128,128]{2,0,1:T(8,128)(2,1)S(1)} %select_bitcast_fusion), channel_id=1, source_target_pairs={{0,3},{1,0},{2,1},{3,2},{4,7},{5,4},{6,5},{7,6},{8,11},{9,8},{10,9... | collective-permute-start | bytes 786440 | tf_op jit(solution)/shard_map/ppermute | solution.py:14
  13.8 9.8 %collective-permute-start.7 = (bf16[32,128]{1,0:T(8,128)(2,1)S(1)}, bf16[32,128]{1,0:T(8,128)(2,1)S(1)}, u32[]{:S(2)}, u32[]{:S(2)}) collective-permute-start(bf16[32,128]{1,0:T(8,128)(2,1)S(1)} %slice_bitcast_fusion.3), channel_id=1, source_target_pairs={{0,1},{1,2},{2,3},{3,0},{4,5},{5,6},{6,7},{7,4},{8,9},{9,10},{10,1... | collective-permute-start | bytes 24584 | tf_op jit(solution)/shard_map/ppermute | solution.py:14
  27.4 4.3 %collective-permute-start.9 = (bf16[8,32,128]{2,1,0:T(8,128)(2,1)S(1)}, bf16[8,32,128]{2,1,0:T(8,128)(2,1)S(1)}, u32[]{:S(2)}, u32[]{:S(2)}) collective-permute-start(bf16[8,32,128]{2,1,0:T(8,128)(2,1)S(1)} %fusion.62), channel_id=1, source_target_pairs={{0,4},{4,0},{8,12},{12,8},{16,20},{20,16},{24,28},{28,24},{1,5},{5... | collective-permute-start | bytes 196616 | tf_op jit(solution)/shard_map/ppermute | solution.py:18
  28.1 1.5 %collective-permute-start.8 = (f32[32,128]{1,0:T(8,128)S(1)}, f32[32,128]{1,0:T(8,128)S(1)}, u32[]{:S(2)}, u32[]{:S(2)}) collective-permute-start(f32[32,128]{1,0:T(8,128)S(1)} %fusion.149), channel_id=1, source_target_pairs={{0,3},{1,0},{2,1},{3,2},{4,7},{5,4},{6,5},{7,6},{8,11},{9,8},{10,9... | collective-permute-start | bytes 49160 | tf_op jit(solution)/shard_map/ppermute | solution.py:14
  45.3 4.5 %collective-permute-start.10 = (bf16[8,32,128]{2,1,0:T(8,128)(2,1)S(1)}, bf16[8,32,128]{2,1,0:T(8,128)(2,1)S(1)}, u32[]{:S(2)}, u32[]{:S(2)}) collective-permute-start(bf16[8,32,128]{2,1,0:T(8,128)(2,1)S(1)} %get-tuple-element.19), channel_id=1, source_target_pairs={{0,4},{4,0},{8,12},{12,8},{16,20},{20,16},{24,28},{28,24},{1,5},{5... | collective-permute-start | bytes 196616 | tf_op jit(solution)/shard_map/ppermute | solution.py:18
  46.5 3.1 %collective-permute-start.11 = (bf16[32,128]{1,0:T(8,128)(2,1)S(1)}, bf16[32,128]{1,0:T(8,128)(2,1)S(1)}, u32[]{:S(2)}, u32[]{:S(2)}) collective-permute-start(bf16[32,128]{1,0:T(8,128)(2,1)S(1)} %slice_bitcast_fusion.2), channel_id=1, source_target_pairs={{0,1},{1,2},{2,3},{3,0},{4,5},{5,6},{6,7},{7,4},{8,9},{9,10},{10,1... | collective-permute-start | bytes 24584 | tf_op jit(solution)/shard_map/ppermute | solution.py:14
  51.8 4.3 %collective-permute-start.13 = (bf16[8,32,128]{2,1,0:T(8,128)(2,1)S(1)}, bf16[8,32,128]{2,1,0:T(8,128)(2,1)S(1)}, u32[]{:S(2)}, u32[]{:S(2)}) collective-permute-start(bf16[8,32,128]{2,1,0:T(8,128)(2,1)S(1)} %fusion.59), channel_id=1, source_target_pairs={{0,4},{4,0},{8,12},{12,8},{16,20},{20,16},{24,28},{28,24},{1,5},{5... | collective-permute-start | bytes 196616 | tf_op jit(solution)/shard_map/ppermute | solution.py:18
  53.3 1.4 %collective-permute-start.12 = (f32[32,128]{1,0:T(8,128)S(1)}, f32[32,128]{1,0:T(8,128)S(1)}, u32[]{:S(2)}, u32[]{:S(2)}) collective-permute-start(f32[32,128]{1,0:T(8,128)S(1)} %fusion.146), channel_id=1, source_target_pairs={{0,3},{1,0},{2,1},{3,2},{4,7},{5,4},{6,5},{7,6},{8,11},{9,8},{10,9... | collective-permute-start | bytes 49160 | tf_op jit(solution)/shard_map/ppermute | solution.py:14
  67.0 4.5 %collective-permute-start.14 = (bf16[8,32,128]{2,1,0:T(8,128)(2,1)S(1)}, bf16[8,32,128]{2,1,0:T(8,128)(2,1)S(1)}, u32[]{:S(2)}, u32[]{:S(2)}) collective-permute-start(bf16[8,32,128]{2,1,0:T(8,128)(2,1)S(1)} %get-tuple-element.22), channel_id=1, source_target_pairs={{0,4},{4,0},{8,12},{12,8},{16,20},{20,16},{24,28},{28,24},{1,5},{5... | collective-permute-start | bytes 196616 | tf_op jit(solution)/shard_map/ppermute | solution.py:18
  68.2 3.1 %collective-permute-start.15 = (bf16[32,128]{1,0:T(8,128)(2,1)S(1)}, bf16[32,128]{1,0:T(8,128)(2,1)S(1)}, u32[]{:S(2)}, u32[]{:S(2)}) collective-permute-start(bf16[32,128]{1,0:T(8,128)(2,1)S(1)} %slice_bitcast_fusion.1), channel_id=1, source_target_pairs={{0,1},{1,2},{2,3},{3,0},{4,5},{5,6},{6,7},{7,4},{8,9},{9,10},{10,1... | collective-permute-start | bytes 24584 | tf_op jit(solution)/shard_map/ppermute | solution.py:14
  73.5 4.3 %collective-permute-start.17 = (bf16[8,32,128]{2,1,0:T(8,128)(2,1)S(1)}, bf16[8,32,128]{2,1,0:T(8,128)(2,1)S(1)}, u32[]{:S(2)}, u32[]{:S(2)}) collective-permute-start(bf16[8,32,128]{2,1,0:T(8,128)(2,1)S(1)} %fusion.56), channel_id=1, source_target_pairs={{0,4},{4,0},{8,12},{12,8},{16,20},{20,16},{24,28},{28,24},{1,5},{5... | collective-permute-start | bytes 196616 | tf_op jit(solution)/shard_map/ppermute | solution.py:18
  75.0 1.4 %collective-permute-start.16 = (f32[32,128]{1,0:T(8,128)S(1)}, f32[32,128]{1,0:T(8,128)S(1)}, u32[]{:S(2)}, u32[]{:S(2)}) collective-permute-start(f32[32,128]{1,0:T(8,128)S(1)} %fusion.143), channel_id=1, source_target_pairs={{0,3},{1,0},{2,1},{3,2},{4,7},{5,4},{6,5},{7,6},{8,11},{9,8},{10,9... | collective-permute-start | bytes 49160 | tf_op jit(solution)/shard_map/ppermute | solution.py:14
  88.7 4.7 %collective-permute-start.18 = (bf16[8,32,128]{2,1,0:T(8,128)(2,1)S(1)}, bf16[8,32,128]{2,1,0:T(8,128)(2,1)S(1)}, u32[]{:S(2)}, u32[]{:S(2)}) collective-permute-start(bf16[8,32,128]{2,1,0:T(8,128)(2,1)S(1)} %get-tuple-element.25), channel_id=1, source_target_pairs={{0,4},{4,0},{8,12},{12,8},{16,20},{20,16},{24,28},{28,24},{1,5},{5... | collective-permute-start | bytes 196616 | tf_op jit(solution)/shard_map/ppermute | solution.py:18
  90.1 3.1 %collective-permute-start.19 = (bf16[32,128]{1,0:T(8,128)(2,1)S(1)}, bf16[32,128]{1,0:T(8,128)(2,1)S(1)}, u32[]{:S(2)}, u32[]{:S(2)}) collective-permute-start(bf16[32,128]{1,0:T(8,128)(2,1)S(1)} %slice_bitcast_fusion), channel_id=1, source_target_pairs={{0,1},{1,2},{2,3},{3,0},{4,5},{5,6},{6,7},{7,4},{8,9},{9,10},{10,1... | collective-permute-start | bytes 24584 | tf_op jit(solution)/shard_map/ppermute | solution.py:14
  95.4 4.3 %collective-permute-start.21 = (bf16[8,32,128]{2,1,0:T(8,128)(2,1)S(1)}, bf16[8,32,128]{2,1,0:T(8,128)(2,1)S(1)}, u32[]{:S(2)}, u32[]{:S(2)}) collective-permute-start(bf16[8,32,128]{2,1,0:T(8,128)(2,1)S(1)} %fusion.53), channel_id=1, source_target_pairs={{0,4},{4,0},{8,12},{12,8},{16,20},{20,16},{24,28},{28,24},{1,5},{5... | collective-permute-start | bytes 196616 | tf_op jit(solution)/shard_map/ppermute | solution.py:18
  97.0 1.4 %collective-permute-start.20 = (f32[32,128]{1,0:T(8,128)S(1)}, f32[32,128]{1,0:T(8,128)S(1)}, u32[]{:S(2)}, u32[]{:S(2)}) collective-permute-start(f32[32,128]{1,0:T(8,128)S(1)} %fusion.140), channel_id=1, source_target_pairs={{0,3},{1,0},{2,1},{3,2},{4,7},{5,4},{6,5},{7,6},{8,11},{9,8},{10,9... | collective-permute-start | bytes 49160 | tf_op jit(solution)/shard_map/ppermute | solution.py:14
  (5 other events, 9.5 us)

commit v27 on v24

--- a/solution.py
+++ b/solution.py
@@ -27,12 +27,11 @@
 
 def local_stiffness(rounded, diag_tiles, off_tiles, cols_onehot, mirror_onehot):
     result = jnp.einsum("nrk,nkj->nrj", rounded, diag_tiles, preferred_element_type=jnp.float32)
-    picked = jnp.einsum(
-        "pn,nrk->prk", cols_onehot, rounded, preferred_element_type=jnp.float32
-    ).astype(jnp.bfloat16)
-    picked = picked.reshape(off_tiles.shape[0], off_tiles.shape[1], rounded.shape[1], rounded.shape[2])
+    count = rounded.shape[0]
+    chosen = cols_onehot.reshape(count, off_tiles.shape[1], count)
+    picked = chosen[:, :, :, None, None] * rounded[None, None, :, :, :]
     result = result + jnp.einsum(
-        "nmrk,nmkj->nrj", picked, off_tiles, preferred_element_type=jnp.float32
+        "nmirk,nmkj->nrj", picked, off_tiles, preferred_element_type=jnp.float32
     )
     nodes = rounded.shape[0]
     chosen = mirror_onehot.reshape(nodes, off_tiles.shape[1], nodes)

time: 109 us -> 110 us (level)
  waiting for transfers between devices: 23.3 us -> 24.7 us
    ppermute x14, waiting for transfers between devices: 20.3 us -> 21.8 us  [from_behind(): return lax.ppermute(value, axis, pairs)]
    unnamed x31 -> x30, local copies, waits for them, and re-layouts: 2.39 us -> 2.49 us
  transfers between devices with their start and end apart: 22 -> 22, of which waited for: 15 -> 15; matrix products, arithmetic and copies ran while one was open for 10% -> 8% of each run, Pallas kernels for 0% -> 0%
where the time goes in v27:
time: 110 us
  blocking collectives  39.4 us (36%)
  waiting for transfers between devices  24.7 us (22%)
  matrix products  15.5 us (14%)
  starting transfers between devices  15.4 us (14%)
  other arithmetic  9.74 us (9%)
  local copies, waits for them, and re-layouts  3.83 us (3%)
  between operations  1.36 us (1%)
    all_to_all x4, blocking collectives, total(): gathered = lax.all_to_all(spread, ('dom', 'rep'), 0, 0, tiled=True)  39.4 us
    ppermute x14, waiting for transfers between devices, from_behind(): return lax.ppermute(value, axis, pairs)  21.8 us
    ppermute x8, starting transfers between devices, partner(): lax.ppermute(value, axis, [(i, i ^ 1 << distance) for i in range(lax.axis...  8.92 us
    ppermute x14, starting transfers between devices, from_behind(): return lax.ppermute(value, axis, pairs)  6.46 us
    dot_general x4, matrix products, apply_operator(): jnp.einsum('snrj,skj->nrk', spread, contact_set, preferred_element_type=j...  3.09 us
    dot_general x4, matrix products, apply_operator(): jnp.einsum('snrj,skj->nrk', near_spread, contact_set, preferred_element_t...  2.99 us
    ppermute x8, waiting for transfers between devices, partner(): lax.ppermute(value, axis, [(i, i ^ 1 << distance) for i in range(lax.axis...  2.87 us
    unnamed x30, local copies, waits for them, and re-layouts  2.49 us
  transfers between devices with their start and end apart: 22, of which 15 were waited for; matrix products, arithmetic and copies ran while one was open for 8% of the time, Pallas kernels for 0%

profile of v27, /device:TPU:0, one launch (start us, length us, event | category | flops | bytes accessed | tf_op | source)
XLA Modules:
  0.0 109.9 jit_solution(9765968675211163640)
XLA Ops:
  1.4 0.9 add_reduce_fusion
  3.0 2.4 %collective-permute-start.6 = (bf16[8,128,128]{2,0,1:T(8,128)(2,1)S(1)}, bf16[8,128,128]{2,0,1:T(8,128)(2,1)}, u32[]{:S(2)}, u32[]{:S(2)}) collective-permute-start(bf16[8,128,128]{2,0,1:T(8,128)(2,1)S(1)} %select_bitcast_fusion), channel_id=1, source_target_pairs={{0,3},{1,0},{2,1},{3,2},{4,7},{5,4},{6,5},{7,6},{8,11},{9,8},{10,9... | collective-permute-start | bytes 786440 | tf_op jit(solution)/shard_map/ppermute | solution.py:14
  6.7 1.7 %collective-permute-start.1 = (s32[8,2]{0,1:T(2,128)S(1)}, s32[8,2]{0,1:T(2,128)S(1)}, u32[]{:S(2)}, u32[]{:S(2)}) collective-permute-start(s32[8,2]{0,1:T(2,128)S(1)} %bitcast.339), channel_id=1, source_target_pairs={{0,2},{1,3},{2,0},{3,1},{4,6},{5,7},{6,4},{7,5},{8,10},{9,11},{10,... | collective-permute-start | bytes 200 | tf_op jit(solution)/shard_map/ppermute | solution.py:14
  8.5 1.6 %collective-permute-start.3 = (bf16[8,32,128]{2,0,1:T(8,128)(2,1)S(1)}, bf16[8,32,128]{2,0,1:T(8,128)(2,1)S(1)}, u32[]{:S(2)}, u32[]{:S(2)}) collective-permute-start(bf16[8,32,128]{2,0,1:T(8,128)(2,1)S(1)} %multiply_convert_fusion), channel_id=1, source_target_pairs={{0,4},{4,0},{8,12},{12,8},{16,20},{20,16},{24,28},{28,24},{1,5},{5... | collective-permute-start | bytes 196616 | tf_op jit(solution)/shard_map/ppermute | solution.py:18
  10.2 4.8 %collective-permute-done.2 = s32[8,2]{0,1:T(2,128)S(1)} collective-permute-done((s32[8,2]{0,1:T(2,128)S(1)}, s32[8,2]{0,1:T(2,128)S(1)}, u32[]{:S(2)}, u32[]{:S(2)}) %collective-permute-start.2) | collective-permute-done | bytes 96 | tf_op jit(solution)/shard_map/ppermute | solution.py:14
  15.0 1.1 %collective-permute-start = (s32[8,2]{0,1:T(2,128)S(1)}, s32[8,2]{0,1:T(2,128)S(1)}, u32[]{:S(2)}, u32[]{:S(2)}) collective-permute-start(s32[8,2]{0,1:T(2,128)S(1)} %bitcast.338), channel_id=1, source_target_pairs={{0,1},{1,2},{2,3},{3,0},{4,5},{5,6},{6,7},{7,4},{8,9},{9,10},{10,1... | collective-permute-start | bytes 200 | tf_op jit(solution)/shard_map/ppermute | solution.py:14
  16.1 2.3 %collective-permute-done = s32[8,2]{0,1:T(2,128)S(1)} collective-permute-done((s32[8,2]{0,1:T(2,128)S(1)}, s32[8,2]{0,1:T(2,128)S(1)}, u32[]{:S(2)}, u32[]{:S(2)}) %collective-permute-start) | collective-permute-done | bytes 96 | tf_op jit(solution)/shard_map/ppermute | solution.py:14
  19.0 3.0 %collective-permute-done.7 = bf16[32,128]{1,0:T(8,128)(2,1)S(1)} collective-permute-done((bf16[32,128]{1,0:T(8,128)(2,1)S(1)}, bf16[32,128]{1,0:T(8,128)(2,1)S(1)}, u32[]{:S(2)}, u32[]{:S(2)}) %collective-permute-start.7) | collective-permute-done | bytes 8224 | tf_op jit(solution)/shard_map/ppermute | solution.py:14
  22.4 1.1 pad_maximum_fusion
  25.0 1.6 %collective-permute-start.9 = (bf16[8,32,128]{2,0,1:T(8,128)(2,1)S(1)}, bf16[8,32,128]{2,0,1:T(8,128)(2,1)S(1)}, u32[]{:S(2)}, u32[]{:S(2)}) collective-permute-start(bf16[8,32,128]{2,0,1:T(8,128)(2,1)S(1)} %copy.385), channel_id=1, source_target_pairs={{0,4},{4,0},{8,12},{12,8},{16,20},{20,16},{24,28},{28,24},{1,5},{5... | collective-permute-start | bytes 196616 | tf_op jit(solution)/shard_map/ppermute | solution.py:18
  30.2 12.8 %all_to_all.20 = f32[32,1,128]{2,1,0:T(1,128)S(1)} all-to-all(f32[32,1,128]{2,1,0:T(1,128)S(1)} %reshape.420), channel_id=1, replica_groups=mesh['dom'=8,'rep'=4] {'dom','rep'}, dimensions={0} | all-to-all | bytes 32768 | tf_op jit(solution)/shard_map/all_to_all | solution.py:24
  45.6 2.6 %collective-permute-done.11 = bf16[32,128]{1,0:T(8,128)(2,1)S(1)} collective-permute-done((bf16[32,128]{1,0:T(8,128)(2,1)S(1)}, bf16[32,128]{1,0:T(8,128)(2,1)S(1)}, u32[]{:S(2)}, u32[]{:S(2)}) %collective-permute-start.11) | collective-permute-done | bytes 8224 | tf_op jit(solution)/shard_map/ppermute | solution.py:14
  51.2 1.1 %collective-permute-start.13 = (bf16[8,32,128]{2,0,1:T(8,128)(2,1)S(1)}, bf16[8,32,128]{2,0,1:T(8,128)(2,1)S(1)}, u32[]{:S(2)}, u32[]{:S(2)}) collective-permute-start(bf16[8,32,128]{2,0,1:T(8,128)(2,1)S(1)} %copy.384), channel_id=1, source_target_pairs={{0,4},{4,0},{8,12},{12,8},{16,20},{20,16},{24,28},{28,24},{1,5},{5... | collective-permute-start | bytes 196616 | tf_op jit(solution)/shard_map/ppermute | solution.py:18
  53.4 1.2 %collective-permute-done.12 = f32[32,128]{1,0:T(8,128)S(1)} collective-permute-done((f32[32,128]{1,0:T(8,128)S(1)}, f32[32,128]{1,0:T(8,128)S(1)}, u32[]{:S(2)}, u32[]{:S(2)}) %collective-permute-start.12) | collective-permute-done | bytes 16416 | tf_op jit(solution)/shard_map/ppermute | solution.py:14
  54.7 0.8 collective-permute-done.13
  56.3 8.8 %all_to_all.21 = f32[32,1,128]{2,1,0:T(1,128)S(1)} all-to-all(f32[32,1,128]{2,1,0:T(1,128)S(1)} %reshape.422), channel_id=1, replica_groups=mesh['dom'=8,'rep'=4] {'dom','rep'}, dimensions={0} | all-to-all | bytes 32768 | tf_op jit(solution)/shard_map/all_to_all | solution.py:24
  67.4 2.6 %collective-permute-done.15 = bf16[32,128]{1,0:T(8,128)(2,1)S(1)} collective-permute-done((bf16[32,128]{1,0:T(8,128)(2,1)S(1)}, bf16[32,128]{1,0:T(8,128)(2,1)S(1)}, u32[]{:S(2)}, u32[]{:S(2)}) %collective-permute-start.15) | collective-permute-done | bytes 8224 | tf_op jit(solution)/shard_map/ppermute | solution.py:14
  72.8 1.3 %collective-permute-start.17 = (bf16[8,32,128]{2,0,1:T(8,128)(2,1)S(1)}, bf16[8,32,128]{2,0,1:T(8,128)(2,1)S(1)}, u32[]{:S(2)}, u32[]{:S(2)}) collective-permute-start(bf16[8,32,128]{2,0,1:T(8,128)(2,1)S(1)} %copy.383), channel_id=1, source_target_pairs={{0,4},{4,0},{8,12},{12,8},{16,20},{20,16},{24,28},{28,24},{1,5},{5... | collective-permute-start | bytes 196616 | tf_op jit(solution)/shard_map/ppermute | solution.py:18
  75.2 1.2 %collective-permute-done.16 = f32[32,128]{1,0:T(8,128)S(1)} collective-permute-done((f32[32,128]{1,0:T(8,128)S(1)}, f32[32,128]{1,0:T(8,128)S(1)}, u32[]{:S(2)}, u32[]{:S(2)}) %collective-permute-start.16) | collective-permute-done | bytes 16416 | tf_op jit(solution)/shard_map/ppermute | solution.py:14
  77.9 8.8 %all_to_all.22 = f32[32,1,128]{2,1,0:T(1,128)S(1)} all-to-all(f32[32,1,128]{2,1,0:T(1,128)S(1)} %reshape.424), channel_id=1, replica_groups=mesh['dom'=8,'rep'=4] {'dom','rep'}, dimensions={0} | all-to-all | bytes 32768 | tf_op jit(solution)/shard_map/all_to_all | solution.py:24
  89.2 2.7 %collective-permute-done.19 = bf16[32,128]{1,0:T(8,128)(2,1)S(1)} collective-permute-done((bf16[32,128]{1,0:T(8,128)(2,1)S(1)}, bf16[32,128]{1,0:T(8,128)(2,1)S(1)}, u32[]{:S(2)}, u32[]{:S(2)}) %collective-permute-start.19) | collective-permute-done | bytes 8224 | tf_op jit(solution)/shard_map/ppermute | solution.py:14
  94.4 1.5 %collective-permute-start.21 = (bf16[8,32,128]{2,0,1:T(8,128)(2,1)S(1)}, bf16[8,32,128]{2,0,1:T(8,128)(2,1)S(1)}, u32[]{:S(2)}, u32[]{:S(2)}) collective-permute-start(bf16[8,32,128]{2,0,1:T(8,128)(2,1)S(1)} %copy.382), channel_id=1, source_target_pairs={{0,4},{4,0},{8,12},{12,8},{16,20},{20,16},{24,28},{28,24},{1,5},{5... | collective-permute-start | bytes 196616 | tf_op jit(solution)/shard_map/ppermute | solution.py:18
  97.1 1.2 %collective-permute-done.20 = f32[32,128]{1,0:T(8,128)S(1)} collective-permute-done((f32[32,128]{1,0:T(8,128)S(1)}, f32[32,128]{1,0:T(8,128)S(1)}, u32[]{:S(2)}, u32[]{:S(2)}) %collective-permute-start.20) | collective-permute-done | bytes 16416 | tf_op jit(solution)/shard_map/ppermute | solution.py:14
  99.3 8.9 %all_to_all.23 = f32[32,2,32]{2,1,0:T(2,128)S(1)} all-to-all(f32[32,2,32]{2,1,0:T(2,128)S(1)} %broadcast_in_dim.90), channel_id=1, replica_groups=mesh['dom'=8,'rep'=4] {'dom','rep'}, dimensions={0} | all-to-all | bytes 16384 | tf_op jit(solution)/shard_map/all_to_all | solution.py:24
  (165 shorter events, 32.1 us)
Async XLA Ops:
  3.0 7.1 %copy-start.6 = (s32[8,2]{0,1:T(2,128)S(1)}, s32[8,2]{0,1:T(2,128)}, u32[]{:S(2)}) copy-start(s32[8,2]{0,1:T(2,128)} %param.18) | copy-start | bytes 196
  3.0 19.4 %collective-permute-start.6 = (bf16[8,128,128]{2,0,1:T(8,128)(2,1)S(1)}, bf16[8,128,128]{2,0,1:T(8,128)(2,1)}, u32[]{:S(2)}, u32[]{:S(2)}) collective-permute-start(bf16[8,128,128]{2,0,1:T(8,128)(2,1)S(1)} %select_bitcast_fusion), channel_id=1, source_target_pairs={{0,3},{1,0},{2,1},{3,2},{4,7},{5,4},{6,5},{7,6},{8,11},{9,8},{10,9... | collective-permute-start | bytes 786440 | tf_op jit(solution)/shard_map/ppermute | solution.py:14
  5.4 16.5 %copy-start.4 = (bf16[1,128,128]{2,1,0:T(8,128)(2,1)S(1)}, bf16[1,128,128]{2,1,0:T(8,128)(2,1)}, u32[]{:S(2)}) copy-start(bf16[1,128,128]{2,1,0:T(8,128)(2,1)} %param.19) | copy-start | bytes 98308
  5.6 16.9 %collective-permute-start.5 = (bf16[8,128,128]{2,0,1:T(8,128)(2,1)S(1)}, bf16[8,128,128]{2,0,1:T(8,128)(2,1)S(1)}, u32[]{:S(2)}, u32[]{:S(2)}) collective-permute-start(bf16[8,128,128]{2,0,1:T(8,128)(2,1)S(1)} %get-tuple-element.89), channel_id=1, source_target_pairs={{0,2},{1,3},{2,0},{3,1},{4,6},{5,7},{6,4},{7,5},{8,10},{9,11},{10,... | collective-permute-start | bytes 786440 | tf_op jit(solution)/shard_map/ppermute | solution.py:14
  6.6 8.4 %collective-permute-start.2 = (s32[8,2]{0,1:T(2,128)S(1)}, s32[8,2]{0,1:T(2,128)S(1)}, u32[]{:S(2)}, u32[]{:S(2)}) collective-permute-start(s32[8,2]{0,1:T(2,128)S(1)} %bitcast.340), channel_id=1, source_target_pairs={{0,3},{1,0},{2,1},{3,2},{4,7},{5,4},{6,5},{7,6},{8,11},{9,8},{10,9... | collective-permute-start | bytes 200 | tf_op jit(solution)/shard_map/ppermute | solution.py:14
  6.7 9.5 %collective-permute-start.1 = (s32[8,2]{0,1:T(2,128)S(1)}, s32[8,2]{0,1:T(2,128)S(1)}, u32[]{:S(2)}, u32[]{:S(2)}) collective-permute-start(s32[8,2]{0,1:T(2,128)S(1)} %bitcast.339), channel_id=1, source_target_pairs={{0,2},{1,3},{2,0},{3,1},{4,6},{5,7},{6,4},{7,5},{8,10},{9,11},{10,... | collective-permute-start | bytes 200 | tf_op jit(solution)/shard_map/ppermute | solution.py:14
  8.5 13.6 %collective-permute-start.3 = (bf16[8,32,128]{2,0,1:T(8,128)(2,1)S(1)}, bf16[8,32,128]{2,0,1:T(8,128)(2,1)S(1)}, u32[]{:S(2)}, u32[]{:S(2)}) collective-permute-start(bf16[8,32,128]{2,0,1:T(8,128)(2,1)S(1)} %multiply_convert_fusion), channel_id=1, source_target_pairs={{0,4},{4,0},{8,12},{12,8},{16,20},{20,16},{24,28},{28,24},{1,5},{5... | collective-permute-start | bytes 196616 | tf_op jit(solution)/shard_map/ppermute | solution.py:18
  15.0 3.4 %collective-permute-start = (s32[8,2]{0,1:T(2,128)S(1)}, s32[8,2]{0,1:T(2,128)S(1)}, u32[]{:S(2)}, u32[]{:S(2)}) collective-permute-start(s32[8,2]{0,1:T(2,128)S(1)} %bitcast.338), channel_id=1, source_target_pairs={{0,1},{1,2},{2,3},{3,0},{4,5},{5,6},{6,7},{7,4},{8,9},{9,10},{10,1... | collective-permute-start | bytes 200 | tf_op jit(solution)/shard_map/ppermute | solution.py:14
  16.1 6.3 %collective-permute-start.4 = (bf16[8,128,128]{2,0,1:T(8,128)(2,1)S(1)}, bf16[8,128,128]{2,0,1:T(8,128)(2,1)S(1)}, u32[]{:S(2)}, u32[]{:S(2)}) collective-permute-start(bf16[8,128,128]{2,0,1:T(8,128)(2,1)S(1)} %get-tuple-element.88), channel_id=1, source_target_pairs={{0,1},{1,2},{2,3},{3,0},{4,5},{5,6},{6,7},{7,4},{8,9},{9,10},{10,1... | collective-permute-start | bytes 786440 | tf_op jit(solution)/shard_map/ppermute | solution.py:14
  18.4 3.6 %collective-permute-start.7 = (bf16[32,128]{1,0:T(8,128)(2,1)S(1)}, bf16[32,128]{1,0:T(8,128)(2,1)S(1)}, u32[]{:S(2)}, u32[]{:S(2)}) collective-permute-start(bf16[32,128]{1,0:T(8,128)(2,1)S(1)} %bitcast.319), channel_id=1, source_target_pairs={{0,1},{1,2},{2,3},{3,0},{4,5},{5,6},{6,7},{7,4},{8,9},{9,10},{10,1... | collective-permute-start | bytes 24584 | tf_op jit(solution)/shard_map/ppermute | solution.py:14
  25.0 4.3 %collective-permute-start.9 = (bf16[8,32,128]{2,0,1:T(8,128)(2,1)S(1)}, bf16[8,32,128]{2,0,1:T(8,128)(2,1)S(1)}, u32[]{:S(2)}, u32[]{:S(2)}) collective-permute-start(bf16[8,32,128]{2,0,1:T(8,128)(2,1)S(1)} %copy.385), channel_id=1, source_target_pairs={{0,4},{4,0},{8,12},{12,8},{16,20},{20,16},{24,28},{28,24},{1,5},{5... | collective-permute-start | bytes 196616 | tf_op jit(solution)/shard_map/ppermute | solution.py:18
  26.7 2.4 %collective-permute-start.8 = (f32[32,128]{1,0:T(8,128)S(1)}, f32[32,128]{1,0:T(8,128)S(1)}, u32[]{:S(2)}, u32[]{:S(2)}) collective-permute-start(f32[32,128]{1,0:T(8,128)S(1)} %fusion.129), channel_id=1, source_target_pairs={{0,3},{1,0},{2,1},{3,2},{4,7},{5,4},{6,5},{7,6},{8,11},{9,8},{10,9... | collective-permute-start | bytes 49160 | tf_op jit(solution)/shard_map/ppermute | solution.py:14
  44.5 4.3 %collective-permute-start.10 = (bf16[8,32,128]{2,0,1:T(8,128)(2,1)S(1)}, bf16[8,32,128]{2,0,1:T(8,128)(2,1)S(1)}, u32[]{:S(2)}, u32[]{:S(2)}) collective-permute-start(bf16[8,32,128]{2,0,1:T(8,128)(2,1)S(1)} %get-tuple-element.19), channel_id=1, source_target_pairs={{0,4},{4,0},{8,12},{12,8},{16,20},{20,16},{24,28},{28,24},{1,5},{5... | collective-permute-start | bytes 196616 | tf_op jit(solution)/shard_map/ppermute | solution.py:18
  45.1 3.1 %collective-permute-start.11 = (bf16[32,128]{1,0:T(8,128)(2,1)S(1)}, bf16[32,128]{1,0:T(8,128)(2,1)S(1)}, u32[]{:S(2)}, u32[]{:S(2)}) collective-permute-start(bf16[32,128]{1,0:T(8,128)(2,1)S(1)} %bitcast.321), channel_id=1, source_target_pairs={{0,1},{1,2},{2,3},{3,0},{4,5},{5,6},{6,7},{7,4},{8,9},{9,10},{10,1... | collective-permute-start | bytes 24584 | tf_op jit(solution)/shard_map/ppermute | solution.py:14
  51.2 4.3 %collective-permute-start.13 = (bf16[8,32,128]{2,0,1:T(8,128)(2,1)S(1)}, bf16[8,32,128]{2,0,1:T(8,128)(2,1)S(1)}, u32[]{:S(2)}, u32[]{:S(2)}) collective-permute-start(bf16[8,32,128]{2,0,1:T(8,128)(2,1)S(1)} %copy.384), channel_id=1, source_target_pairs={{0,4},{4,0},{8,12},{12,8},{16,20},{20,16},{24,28},{28,24},{1,5},{5... | collective-permute-start | bytes 196616 | tf_op jit(solution)/shard_map/ppermute | solution.py:18
  53.2 1.5 %collective-permute-start.12 = (f32[32,128]{1,0:T(8,128)S(1)}, f32[32,128]{1,0:T(8,128)S(1)}, u32[]{:S(2)}, u32[]{:S(2)}) collective-permute-start(f32[32,128]{1,0:T(8,128)S(1)} %fusion.125), channel_id=1, source_target_pairs={{0,3},{1,0},{2,1},{3,2},{4,7},{5,4},{6,5},{7,6},{8,11},{9,8},{10,9... | collective-permute-start | bytes 49160 | tf_op jit(solution)/shard_map/ppermute | solution.py:14
  66.1 4.3 %collective-permute-start.14 = (bf16[8,32,128]{2,0,1:T(8,128)(2,1)S(1)}, bf16[8,32,128]{2,0,1:T(8,128)(2,1)S(1)}, u32[]{:S(2)}, u32[]{:S(2)}) collective-permute-start(bf16[8,32,128]{2,0,1:T(8,128)(2,1)S(1)} %get-tuple-element.22), channel_id=1, source_target_pairs={{0,4},{4,0},{8,12},{12,8},{16,20},{20,16},{24,28},{28,24},{1,5},{5... | collective-permute-start | bytes 196616 | tf_op jit(solution)/shard_map/ppermute | solution.py:18
  66.7 3.3 %collective-permute-start.15 = (bf16[32,128]{1,0:T(8,128)(2,1)S(1)}, bf16[32,128]{1,0:T(8,128)(2,1)S(1)}, u32[]{:S(2)}, u32[]{:S(2)}) collective-permute-start(bf16[32,128]{1,0:T(8,128)(2,1)S(1)} %bitcast.322), channel_id=1, source_target_pairs={{0,1},{1,2},{2,3},{3,0},{4,5},{5,6},{6,7},{7,4},{8,9},{9,10},{10,1... | collective-permute-start | bytes 24584 | tf_op jit(solution)/shard_map/ppermute | solution.py:14
  72.8 4.3 %collective-permute-start.17 = (bf16[8,32,128]{2,0,1:T(8,128)(2,1)S(1)}, bf16[8,32,128]{2,0,1:T(8,128)(2,1)S(1)}, u32[]{:S(2)}, u32[]{:S(2)}) collective-permute-start(bf16[8,32,128]{2,0,1:T(8,128)(2,1)S(1)} %copy.383), channel_id=1, source_target_pairs={{0,4},{4,0},{8,12},{12,8},{16,20},{20,16},{24,28},{28,24},{1,5},{5... | collective-permute-start | bytes 196616 | tf_op jit(solution)/shard_map/ppermute | solution.py:18
  75.0 1.5 %collective-permute-start.16 = (f32[32,128]{1,0:T(8,128)S(1)}, f32[32,128]{1,0:T(8,128)S(1)}, u32[]{:S(2)}, u32[]{:S(2)}) collective-permute-start(f32[32,128]{1,0:T(8,128)S(1)} %fusion.121), channel_id=1, source_target_pairs={{0,3},{1,0},{2,1},{3,2},{4,7},{5,4},{6,5},{7,6},{8,11},{9,8},{10,9... | collective-permute-start | bytes 49160 | tf_op jit(solution)/shard_map/ppermute | solution.py:14
  87.7 4.3 %collective-permute-start.18 = (bf16[8,32,128]{2,0,1:T(8,128)(2,1)S(1)}, bf16[8,32,128]{2,0,1:T(8,128)(2,1)S(1)}, u32[]{:S(2)}, u32[]{:S(2)}) collective-permute-start(bf16[8,32,128]{2,0,1:T(8,128)(2,1)S(1)} %get-tuple-element.25), channel_id=1, source_target_pairs={{0,4},{4,0},{8,12},{12,8},{16,20},{20,16},{24,28},{28,24},{1,5},{5... | collective-permute-start | bytes 196616 | tf_op jit(solution)/shard_map/ppermute | solution.py:18
  88.8 3.1 %collective-permute-start.19 = (bf16[32,128]{1,0:T(8,128)(2,1)S(1)}, bf16[32,128]{1,0:T(8,128)(2,1)S(1)}, u32[]{:S(2)}, u32[]{:S(2)}) collective-permute-start(bf16[32,128]{1,0:T(8,128)(2,1)S(1)} %bitcast.320), channel_id=1, source_target_pairs={{0,1},{1,2},{2,3},{3,0},{4,5},{5,6},{6,7},{7,4},{8,9},{9,10},{10,1... | collective-permute-start | bytes 24584 | tf_op jit(solution)/shard_map/ppermute | solution.py:14
  94.4 4.3 %collective-permute-start.21 = (bf16[8,32,128]{2,0,1:T(8,128)(2,1)S(1)}, bf16[8,32,128]{2,0,1:T(8,128)(2,1)S(1)}, u32[]{:S(2)}, u32[]{:S(2)}) collective-permute-start(bf16[8,32,128]{2,0,1:T(8,128)(2,1)S(1)} %copy.382), channel_id=1, source_target_pairs={{0,4},{4,0},{8,12},{12,8},{16,20},{20,16},{24,28},{28,24},{1,5},{5... | collective-permute-start | bytes 196616 | tf_op jit(solution)/shard_map/ppermute | solution.py:18
  96.9 1.5 %collective-permute-start.20 = (f32[32,128]{1,0:T(8,128)S(1)}, f32[32,128]{1,0:T(8,128)S(1)}, u32[]{:S(2)}, u32[]{:S(2)}) collective-permute-start(f32[32,128]{1,0:T(8,128)S(1)} %fusion.117), channel_id=1, source_target_pairs={{0,3},{1,0},{2,1},{3,2},{4,7},{5,4},{6,5},{7,6},{8,11},{9,8},{10,9... | collective-permute-start | bytes 49160 | tf_op jit(solution)/shard_map/ppermute | solution.py:14
  (7 other events, 23.2 us)
